TPU v7x, 32 devices: a whole 2x2x4 slice. The times are simulated.
32 devices in a mesh: row: 8 (over z, y), col: 4 (over x, core).
Axes of the slice: x: 2, y: 2, z: 4, core: 2. Of those that a mesh axis runs over, the one named last changes fastest.
Arguments:
- tokens: bfloat16 [1024, 4096], P('row'), may hold values from -6 to 6
- in_weight: bfloat16 [4096, 8192], P('row', 'col'), may hold values from -0.09375 to 0.09375
- gate_branch: bfloat16 [1024, 8192], P('row', 'col'), may hold values from -6 to 6
- conv_weight: float32 [4, 8192], P(None, 'col'), may hold values from -3 to 3
- out_weight: bfloat16 [8192, 4096], P('col'), may hold values from -0.0625 to 0.0625
- target: bfloat16 [1024, 4096], P('row'), may hold values from -6 to 6
- lang_ids: int32 [1024], P('row'), may hold values from 0 to 31
- lang_weight: float32 [32], replicated, may hold values from 0.25 to 4
- doc_pos: int32 [1024], P('row'), may hold values from 0 to 127, as said below
Outputs:
- block_out: bfloat16 [1024, 4096], P('row', 'col')
- grad_tokens: bfloat16 [1024, 4096], P('row', 'col')
- grad_gate: bfloat16 [1024, 8192], P('row', 'col')
Inputs may be any that keep to these rules, and one draw needn't show every extreme that they name: doc_pos is 0 at the first token and at every document's first token, and otherwise one more than the previous token's; no document is longer than 128 tokens and one is exactly 128 tokens long; apart from token 0, no document begins within the first 4 tokens of an aligned block of 128 tokens.
All inputs are finite; a program needn't handle non-finite values.
Results may differ from a plain program's by a relative error of at most 0.022.
Values may be sent and summed in bfloat16 or wider, within the bound.
No kernel may reach another device: no remote copies, remote signals or barrier semaphores. Data moves between devices by JAX's collectives and lax.ppermute only.
A program may use at most 128 MiB of HBM per device.

v0:
```python
import jax
import jax.numpy as jnp
from jax import lax
from jax.sharding import PartitionSpec as P

CONV = 4
LANGS = 32


def passed_along(value, axis, steps):
    count = lax.axis_size(axis)
    first, last = (max(0, -steps), min(count, count - steps))
    return lax.ppermute(value, axis, [(source, source + steps) for source in range(first, last)])


def silu_grad(argument):
    sigmoid_v = jax.nn.sigmoid(argument)
    return sigmoid_v * (1.0 + argument * (1.0 - sigmoid_v))


def shards(
    tokens, in_weight, gate_branch, conv_weight, out_weight, target, lang_ids, lang_weight, doc_pos
):
    row_count = tokens.shape[0]
    inner_width = gate_branch.shape[1]
    margin = CONV - 1
    full_in = lax.all_gather(in_weight, "row", axis=0, tiled=True)
    inner_x = jnp.dot(tokens, full_in, preferred_element_type=jnp.float32).astype(jnp.bfloat16)
    from_prev = passed_along(inner_x[row_count - margin :], "row", 1)
    extended = jnp.concatenate([from_prev, inner_x], axis=0).astype(jnp.float32)
    conv_sum = jnp.zeros((row_count, inner_width), jnp.float32)
    for offset in range(CONV):
        keep_mask = (doc_pos >= offset).astype(jnp.float32)[:, None]
        conv_sum = (
            conv_sum
            + conv_weight[offset][None, :]
            * extended[margin - offset : margin - offset + row_count]
            * keep_mask
        )
    gate_value = gate_branch.astype(jnp.float32)
    gate_act = jax.nn.silu(gate_value)
    conv_act = jax.nn.silu(conv_sum)
    mixed = (conv_act * gate_act).astype(jnp.bfloat16)
    partial_value = jnp.dot(mixed, out_weight, preferred_element_type=jnp.float32)
    columns = tokens.shape[1] // lax.axis_size("col")
    col_start = lax.axis_index("col") * columns
    lang_table = (lang_ids[:, None] == jnp.arange(LANGS, dtype=jnp.int32)[None, :]).astype(
        jnp.float32
    )
    token_weight = jnp.sum(lang_table * lang_weight[None, :], axis=1)[:, None]
    out_total = lax.psum(partial_value.astype(jnp.bfloat16), "col").astype(jnp.float32)
    out_block = lax.dynamic_slice_in_dim(out_total, col_start, columns, 1)
    residual_grad = (token_weight * (out_total - target.astype(jnp.float32))).astype(jnp.bfloat16)
    grad_mixed = lax.dot_general(
        residual_grad, out_weight, (((1,), (1,)), ((), ())), preferred_element_type=jnp.float32
    )
    grad_conv = grad_mixed * gate_act * silu_grad(conv_sum)
    grad_gate = (grad_mixed * conv_act * silu_grad(gate_value)).astype(jnp.bfloat16)
    local_grad = conv_weight[0][None, :] * grad_conv
    spill_over = jnp.zeros((margin, inner_width), jnp.float32)
    for offset in range(1, CONV):
        masked = (
            conv_weight[offset][None, :]
            * grad_conv
            * (doc_pos >= offset).astype(jnp.float32)[:, None]
        )
        local_grad = local_grad + jnp.concatenate(
            [masked[offset:], jnp.zeros((offset, inner_width), jnp.float32)], axis=0
        )
        spill_over = spill_over + jnp.concatenate(
            [jnp.zeros((margin - offset, inner_width), jnp.float32), masked[:offset]], axis=0
        )
    from_next = passed_along(spill_over, "row", -1)
    grad_x = (
        local_grad
        + jnp.concatenate(
            [jnp.zeros((row_count - margin, inner_width), jnp.float32), from_next], axis=0
        )
    ).astype(jnp.bfloat16)
    partial_grad = lax.dot_general(
        grad_x, full_in, (((1,), (1,)), ((), ())), preferred_element_type=jnp.float32
    )
    grad_tokens = lax.psum_scatter(
        partial_grad.astype(jnp.bfloat16), "col", scatter_dimension=1, tiled=True
    )
    return (out_block.astype(jnp.bfloat16), grad_tokens, grad_gate)


def solution(mesh):
    in_specs = (
        P("row", None),
        P("row", "col"),
        P("row", "col"),
        P(None, "col"),
        P("col", None),
        P("row", None),
        P("row"),
        P(),
        P("row"),
    )
    out_specs = (P("row", "col"), P("row", "col"), P("row", "col"))
    return jax.shard_map(shards, mesh=mesh, in_specs=in_specs, out_specs=out_specs, check_vma=False)
```

profile of v0, /device:TPU:2, one launch (start us, length us, event | category | flops | bytes accessed | tf_op | source)
XLA Modules:
  0.0 359.0 jit_solution(7084845556274055566)
XLA Ops:
  7.2 0.0 copy-start
  7.2 0.0 copy-start.3
  7.2 0.0 copy-start.5
  7.2 0.0 all-gather.2.cloned.1.call-start
  7.2 0.7 all-gather.2.cloned.1.call-update
  7.9 0.0 all-reduce.8.cloned.1.call-start
  8.0 0.9 fusion.22
  8.9 230.1 %all-gather.2.cloned.1.call-done = bf16[4096,2048]{1,0:T(8,128)(2,1)} async-done(((bf16[512,2048]{1,0:T(8,128)(2,1)}), bf16[4096,2048]{1,0:T(8,128)(2,1)}) %all-gather.2.cloned.1.call-update) | async-done | bytes 16777232 | tf_op jit(solution)/shard_map/all_gather | solution.py:27
  239.0 0.0 copy-done
  239.0 0.0 copy-start.4
  239.0 8.3 %convolution_convert_fusion.2 = bf16[128,2048]{1,0:T(8,128)(2,1)S(1)} fusion(bf16[128,4096]{1,0:T(8,128)(2,1)S(1)} %copy-done, bf16[4096,2048]{1,0:T(8,128)(2,1)} %all-gather.2.cloned.1.call-done), kind=kOutput, calls=%fused_computation.2 | convolution fusion | flops 2147745792 | bytes 18350080 | tf_op jit(solution)/shard_map/dot_general | solution.py:28
  247.3 2.7 collective-permute-start
  250.0 0.0 copy-done.3
  250.1 1.4 collective-permute-done
  251.5 0.1 maximum_convert_fusion
  251.6 0.7 fusion.9
  252.4 0.0 copy-start.2
  252.4 1.0 copy-done.2
  253.4 0.0 copy-done.5
  253.4 0.0 copy-done.4
  253.4 0.0 copy-start.6
  253.4 0.0 copy-start.7
  253.4 3.8 %convolution_convert_fusion.1 = bf16[128,4096]{1,0:T(8,128)(2,1)} fusion(bf16[2048,4096]{1,0:T(8,128)(2,1)S(1)} %copy-done.4, bf16[128,2048]{1,0:T(8,128)(2,1)S(1)} %copy-done.5, f32[128,2048]{1,0:T(8,128)S(1)} %fusion.9), kind=kOutput, calls=%fused_computation.1 | convolution fusion | flops 2150891520 | bytes 19398656 | tf_op jit(solution)/shard_map/dot_general | solution.py:44
  257.1 0.0 all-reduce.8.cloned.1.call-update
  257.2 0.0 reduce-scatter.2.cloned.1.call-start
  257.2 0.0 copy-done.6
  257.2 0.0 copy-done.7
  257.2 0.1 select_reduce_fusion
  257.3 36.4 %all-reduce.8.cloned.1.call-done = bf16[128,4096]{1,0:T(8,128)(2,1)} async-done(((bf16[128,4096]{1,0:T(8,128)(2,1)}), bf16[128,4096]{1,0:T(8,128)(2,1)}) %all-reduce.8.cloned.1.call-update) | async-done | bytes 1048592 | tf_op jit(solution)/shard_map/psum | solution.py:51
  293.7 13.7 %multiply_multiply_fusion.2 = (f32[128,2048]{1,0:T(8,128)S(1)}, f32[128,2048]{1,0:T(8,128)S(1)}, bf16[128,2048]{1,0:T(8,128)(2,1)}) fusion(f32[128]{0:T(128)S(1)} %get-tuple-element.13, f32[2048]{0:T(1024)S(1)} %bitcast.16, f32[128,2048]{1,0:T(8,128)} %copy-done.2, bf16[128,2048]{1,0:T(8,128)(2,1)} %param.11, bf16[2048,4096]{1,0:T(8,128)(2,1)} %param.13, ...), kind=kOutput, calls=%fused_computation.29 | convolution fusion | flops 2156396544 | bytes 23077888 | tf_op jit(solution)/shard_map/dot_general | solution.py:54
  307.4 0.0 copy-start.1
  307.4 0.3 multiply_multiply_fusion.1
  307.8 0.7 copy-done.1
  308.4 1.5 collective-permute-start.1
  309.9 1.3 slice.69
  311.2 1.1 slice.70
  312.3 1.1 slice.71
  313.4 0.8 collective-permute-done.1
  314.2 13.1 %convolution_convert_fusion = bf16[128,4096]{1,0:T(8,128)(2,1)} fusion(bf16[4096,2048]{1,0:T(8,128)(2,1)} %all-gather.2.cloned.1.call-done, f32[3,2048]{1,0:T(4,128)S(1)} %collective-permute-done.1, f32[125,2048]{1,0:T(8,128)} %slice.71, f32[126,2048]{1,0:T(8,128)} %slice.70, f32[127,2048]{1,0:T(8,128)S(1)} %slice.69, f32[128,2048]{1,0:T(8,128)S(1)} %get-tuple-element.4, ...), kind=kOutput, calls=%fused_computation | convolution fusion | flops 2149580800 | bytes 22003712 | tf_op jit(solution)/shard_map/dot_general | solution.py:80
  327.3 0.0 reduce-scatter.2.cloned.1.call-update
  327.3 1.7 dynamic-slice_convert_fusion
  329.0 23.5 %reduce-scatter.2.cloned.1.call-done = bf16[128,1024]{1,0:T(8,128)(2,1)} async-done(((bf16[128,4096]{1,0:T(8,128)(2,1)}), bf16[128,1024]{1,0:T(8,128)(2,1)}) %reduce-scatter.2.cloned.1.call-update) | async-done | bytes 262160 | tf_op jit(solution)/shard_map/reduce_scatter | solution.py:83
  (5 shorter events, 0.1 us)
Async XLA Ops:
  7.2 231.9 %copy-start = (bf16[128,4096]{1,0:T(8,128)(2,1)S(1)}, bf16[128,4096]{1,0:T(8,128)(2,1)}, u32[]{:S(2)}) copy-start(bf16[128,4096]{1,0:T(8,128)(2,1)} %param.9) | copy-start | bytes 3145732
  7.2 242.9 %copy-start.3 = (s32[128]{0:T(128)S(1)}, s32[128]{0:T(128)}, u32[]{:S(2)}) copy-start(s32[128]{0:T(128)} %param.17) | copy-start | bytes 1540
  7.2 246.2 %copy-start.5 = (bf16[128,2048]{1,0:T(8,128)(2,1)S(1)}, bf16[128,2048]{1,0:T(8,128)(2,1)}, u32[]{:S(2)}) copy-start(bf16[128,2048]{1,0:T(8,128)(2,1)} %param.11) | copy-start | bytes 1572868
  7.2 231.8 %all-gather.2.cloned.1.call-start = ((), (), s32[]{:S(2)}) async-start(), calls=%async_computation.1 | async-start | bytes 18874368 | tf_op jit(solution)/shard_map/all_gather | solution.py:27
  7.9 285.8 %all-reduce.8.cloned.1.call-start = ((), (), s32[]{:S(2)}) async-start(), calls=%async_computation.2 | async-start | bytes 2097152 | tf_op jit(solution)/shard_map/psum | solution.py:51
  239.0 14.3 %copy-start.4 = (bf16[2048,4096]{1,0:T(8,128)(2,1)S(1)}, bf16[2048,4096]{1,0:T(8,128)(2,1)}, u32[]{:S(2)}) copy-start(bf16[2048,4096]{1,0:T(8,128)(2,1)} %param.13) | copy-start | bytes 50331652
  247.3 4.2 %collective-permute-start = (bf16[3,2048]{1,0:T(4,128)(2,1)S(1)}, bf16[3,2048]{1,0:T(4,128)(2,1)S(1)}, u32[]{:S(2)}, u32[]{:S(2)}) collective-permute-start(bf16[3,2048]{1,0:T(4,128)(2,1)S(1)} %slice.64), channel_id=1, source_target_pairs={{0,4},{4,8},{8,12},{12,16},{16,20},{20,24},{24,28},{1,5},{5,9},{9,... | collective-permute-start | bytes 36872 | tf_op jit(solution)/shard_map/ppermute | solution.py:13
  252.4 1.0 copy-start.2
  253.4 3.8 %copy-start.6 = (f32[32]{0:T(128)S(1)}, f32[32]{0:T(128)}, u32[]{:S(2)}) copy-start(f32[32]{0:T(128)} %param.16) | copy-start | bytes 388
  253.4 3.9 %copy-start.7 = (s32[128]{0:T(128)S(1)}, s32[128]{0:T(128)}, u32[]{:S(2)}) copy-start(s32[128]{0:T(128)} %param.15) | copy-start | bytes 1540
  257.2 95.3 %reduce-scatter.2.cloned.1.call-start = ((), (), s32[]{:S(2)}) async-start(), calls=%async_computation.3 | async-start | bytes 1310720 | tf_op jit(solution)/shard_map/reduce_scatter | solution.py:83
  307.4 1.0 copy-start.1
  308.4 5.8 %collective-permute-start.1 = (f32[3,2048]{1,0:T(4,128)S(1)}, f32[3,2048]{1,0:T(4,128)S(1)}, u32[]{:S(2)}, u32[]{:S(2)}) collective-permute-start(f32[3,2048]{1,0:T(4,128)S(1)} %slice_add_fusion), channel_id=1, source_target_pairs={{4,0},{8,4},{12,8},{16,12},{20,16},{24,20},{28,24},{5,1},{9,5},{13... | collective-permute-start | bytes 73736 | tf_op jit(solution)/shard_map/ppermute | solution.py:13
Sparse Core Ops, SparseCore 0:
  10.2 228.8 all-gather.1
  257.3 36.3 all-reduce.7
  327.4 25.0 reduce-scatter.1
where the time goes:
time: 362 us; the launch traced here: 359 us
  waiting for transfers between devices  293 us (81%)
  matrix products  38.8 us (11%)
  between operations  13.9 us (4%)
  local copies, waits for them, and re-layouts  7.83 us (2%)
  starting transfers between devices  4.3 us (1%)
    all_gather x1, waiting for transfers between devices, shards(): full_in = lax.all_gather(in_weight, 'row', axis=0, tiled=True)  230 us
    psum x1, waiting for transfers between devices, shards(): lax.psum(partial_value.astype(jnp.bfloat16), 'col').astype(jnp.float32)  36.4 us
    reduce_scatter x1, waiting for transfers between devices, shards(): lax.psum_scatter(partial_grad.astype(jnp.bfloat16), 'col', scatter_dimens...  23.5 us
    dot_general x1, matrix products, shards(): lax.dot_general(residual_grad, out_weight, (((1,), (1,)), ((), ())), pref...  13.7 us
    dot_general x1, matrix products, shards(): lax.dot_general(grad_x, full_in, (((1,), (1,)), ((), ())), preferred_elem...  13.1 us
    dot_general x1, matrix products, shards(): jnp.dot(tokens, full_in, preferred_element_type=jnp.float32)  8.25 us
  transfers between devices with their start and end apart: 5, of which 5 were waited for; matrix products, arithmetic and copies ran while one was open for 2% of the time, Pallas kernels for 0%

commit v1 on v0

--- a/solution.py
+++ b/solution.py
@@ -24,8 +24,14 @@
     row_count = tokens.shape[0]
     inner_width = gate_branch.shape[1]
     margin = CONV - 1
-    full_in = lax.all_gather(in_weight, "row", axis=0, tiled=True)
-    inner_x = jnp.dot(tokens, full_in, preferred_element_type=jnp.float32).astype(jnp.bfloat16)
+    moves_tokens = row_count * lax.axis_size("row") < tokens.shape[1]
+    if moves_tokens:
+        token_cols = lax.all_to_all(tokens, "row", 1, 0, tiled=True)
+        part_x = jnp.dot(token_cols, in_weight, preferred_element_type=jnp.float32)
+        inner_x = lax.psum_scatter(part_x.astype(jnp.bfloat16), "row", scatter_dimension=0, tiled=True)
+    else:
+        full_in = lax.all_gather(in_weight, "row", axis=0, tiled=True)
+        inner_x = jnp.dot(tokens, full_in, preferred_element_type=jnp.float32).astype(jnp.bfloat16)
     from_prev = passed_along(inner_x[row_count - margin :], "row", 1)
     extended = jnp.concatenate([from_prev, inner_x], axis=0).astype(jnp.float32)
     conv_sum = jnp.zeros((row_count, inner_width), jnp.float32)
@@ -77,9 +83,16 @@
             [jnp.zeros((row_count - margin, inner_width), jnp.float32), from_next], axis=0
         )
     ).astype(jnp.bfloat16)
-    partial_grad = lax.dot_general(
-        grad_x, full_in, (((1,), (1,)), ((), ())), preferred_element_type=jnp.float32
-    )
+    if moves_tokens:
+        grad_x_all = lax.all_gather(grad_x, "row", axis=0, tiled=True)
+        grad_cols = lax.dot_general(
+            grad_x_all, in_weight, (((1,), (1,)), ((), ())), preferred_element_type=jnp.float32
+        )
+        partial_grad = lax.all_to_all(grad_cols.astype(jnp.bfloat16), "row", 0, 1, tiled=True)
+    else:
+        partial_grad = lax.dot_general(
+            grad_x, full_in, (((1,), (1,)), ((), ())), preferred_element_type=jnp.float32
+        )
     grad_tokens = lax.psum_scatter(
         partial_grad.astype(jnp.bfloat16), "col", scatter_dimension=1, tiled=True
     )

time: 362 us -> 353 us (0.975)
  waiting for transfers between devices: 293 us -> 224 us
  blocking collectives: 0 us -> 60.1 us
  matrix products: 38.8 us -> 33.6 us
    all_gather x1, waiting for transfers between devices: 230 us -> 74.4 us  [shards(): grad_x_all = lax.all_gather(grad_x, 'row', axis=0, tiled=True)]
    reduce_scatter x0 -> x1, waiting for transfers between devices: none -> 86.5 us  [shards(): lax.psum_scatter(part_x.astype(jnp.bfloat16), 'row', scatter_dimension=0,...]
    all_to_all x0 -> x2, blocking collectives: none -> 60.1 us  [the longest x1 31.6 us: shards(): token_cols = lax.all_to_all(tokens, 'row', 1, 0, tiled=True)]
    dot_general x2, matrix products: 21.3 us -> 10.1 us  [the longest x1 5.51 us: shards(): part_x = jnp.dot(token_cols, in_weight, preferred_element_type=jnp.float32)]
    dot_general x1, matrix products: 3.76 us -> 9.46 us  [shards(): jnp.dot(mixed, out_weight, preferred_element_type=jnp.float32)]
  transfers between devices with their start and end apart: 5 -> 6, of which waited for: 5 -> 6; matrix products, arithmetic and copies ran while one was open for 2% -> 1% of each run, Pallas kernels for 0% -> 0%
where the time goes in v1:
time: 353 us; the launch traced here: 350 us
  waiting for transfers between devices  224 us (63%)
  blocking collectives  60.1 us (17%)
  matrix products  33.6 us (10%)
  between operations  13.9 us (4%)
  local copies, waits for them, and re-layouts  10.2 us (3%)
  starting transfers between devices  5.03 us (1%)
    reduce_scatter x1, waiting for transfers between devices, shards(): lax.psum_scatter(part_x.astype(jnp.bfloat16), 'row', scatter_dimension=0,...  86.5 us
    all_gather x1, waiting for transfers between devices, shards(): grad_x_all = lax.all_gather(grad_x, 'row', axis=0, tiled=True)  74.4 us
    psum x1, waiting for transfers between devices, shards(): lax.psum(partial_value.astype(jnp.bfloat16), 'col').astype(jnp.float32)  36.1 us
    all_to_all x1, blocking collectives, shards(): token_cols = lax.all_to_all(tokens, 'row', 1, 0, tiled=True)  31.6 us
    all_to_all x1, blocking collectives, shards(): lax.all_to_all(grad_cols.astype(jnp.bfloat16), 'row', 0, 1, tiled=True)  28.5 us
    reduce_scatter x1, waiting for transfers between devices, shards(): lax.psum_scatter(partial_grad.astype(jnp.bfloat16), 'col', scatter_dimens...  21.2 us
    dot_general x1, matrix products, shards(): lax.dot_general(residual_grad, out_weight, (((1,), (1,)), ((), ())), pref...  14.1 us
    dot_general x1, matrix products, shards(): jnp.dot(mixed, out_weight, preferred_element_type=jnp.float32)  9.46 us
  transfers between devices with their start and end apart: 6, of which 6 were waited for; matrix products, arithmetic and copies ran while one was open for 1% of the time, Pallas kernels for 0%

profile of v1, /device:TPU:2, one launch (start us, length us, event | category | flops | bytes accessed | tf_op | source)
XLA Modules:
  0.0 350.1 jit_solution(13760163877622993587)
XLA Ops:
  7.2 0.0 copy-start
  7.2 0.0 reduce-scatter.3.cloned.1.call-start
  7.2 2.4 copy.17
  9.6 31.6 %all_to_all.38 = bf16[128,8,512]{0,2,1:T(8,128)(2,1)S(1)} all-to-all(bf16[128,8,512]{0,2,1:T(8,128)(2,1)} %bitcast.20), channel_id=1, replica_groups=mesh['row'=8,'col'=4] {'row'}, dimensions={1} | all-to-all | bytes 2097152 | tf_op jit(solution)/shard_map/all_to_all | solution.py:29
  41.2 1.3 copy.18
  42.5 0.0 copy-done
  42.5 5.5 %convolution_convert_fusion.1 = bf16[1024,2048]{1,0:T(8,128)(2,1)} fusion(bf16[1024,512]{1,0:T(8,128)(2,1)} %bitcast.21, bf16[512,2048]{1,0:T(8,128)(2,1)S(1)} %copy-done), kind=kOutput, calls=%fused_computation.1 | convolution fusion | flops 2149580800 | bytes 7340032 | tf_op jit(solution)/shard_map/dot_general | solution.py:30
  48.1 0.0 copy-start.3
  48.1 0.0 copy-start.4
  48.1 0.0 reduce-scatter.3.cloned.1.call-update
  48.1 0.0 all-reduce.8.cloned.1.call-start
  48.1 0.7 copy-done.3
  48.8 86.5 %reduce-scatter.3.cloned.1.call-done = bf16[128,2048]{1,0:T(8,128)(2,1)} async-done(((bf16[1024,2048]{1,0:T(8,128)(2,1)}), bf16[128,2048]{1,0:T(8,128)(2,1)}) %reduce-scatter.3.cloned.1.call-update) | async-done | bytes 524304 | tf_op jit(solution)/shard_map/reduce_scatter | solution.py:31
  135.3 0.8 slice.64
  136.1 3.4 collective-permute-start
  139.5 0.0 copy-done.4
  139.5 1.4 collective-permute-done
  140.9 1.2 maximum_convert_fusion
  142.1 0.0 copy-start.5
  142.1 0.7 fusion.9
  142.8 0.0 copy-start.2
  142.9 1.0 copy-done.2
  143.8 0.0 copy-done.5
  143.8 0.0 copy-start.6
  143.8 0.0 copy-start.7
  143.8 9.5 %convolution_convert_fusion = bf16[128,4096]{1,0:T(8,128)(2,1)} fusion(bf16[2048,4096]{1,0:T(8,128)(2,1)} %param.13, bf16[128,2048]{1,0:T(8,128)(2,1)S(1)} %copy-done.5, f32[128,2048]{1,0:T(8,128)S(1)} %fusion.9), kind=kOutput, calls=%fused_computation | convolution fusion | flops 2150891520 | bytes 19398656 | tf_op jit(solution)/shard_map/dot_general | solution.py:50
  153.3 0.0 all-reduce.8.cloned.1.call-update
  153.3 0.0 all-gather.2.cloned.1.call-start
  153.4 0.0 copy-done.6
  153.4 0.0 copy-done.7
  153.4 0.1 select_reduce_fusion
  153.5 36.1 %all-reduce.8.cloned.1.call-done = bf16[128,4096]{1,0:T(8,128)(2,1)} async-done(((bf16[128,4096]{1,0:T(8,128)(2,1)}), bf16[128,4096]{1,0:T(8,128)(2,1)}) %all-reduce.8.cloned.1.call-update) | async-done | bytes 1048592 | tf_op jit(solution)/shard_map/psum | solution.py:57
  189.6 14.1 %multiply_multiply_fusion.2 = (f32[128,2048]{1,0:T(8,128)}, f32[128,2048]{1,0:T(8,128)S(1)}, bf16[128,2048]{1,0:T(8,128)(2,1)}) fusion(f32[128]{0:T(128)S(1)} %get-tuple-element.13, f32[2048]{0:T(1024)S(1)} %bitcast.30, f32[128,2048]{1,0:T(8,128)} %copy-done.2, bf16[128,2048]{1,0:T(8,128)(2,1)} %param.11, bf16[2048,4096]{1,0:T(8,128)(2,1)} %param.13, ...), kind=kOutput, calls=%fused_computation.29 | convolution fusion | flops 2156396544 | bytes 23077888 | tf_op jit(solution)/shard_map/dot_general | solution.py:60
  203.7 0.0 copy-start.1
  203.7 0.9 slice.72
  204.6 0.3 multiply_multiply_fusion.1
  204.9 1.5 collective-permute-start.1
  206.4 0.0 copy-done.1
  206.4 0.1 slice.69
  206.5 0.1 slice.70
  206.6 0.1 slice.71
  206.7 4.0 %collective-permute-done.1 = f32[3,2048]{1,0:T(4,128)S(1)} collective-permute-done((f32[3,2048]{1,0:T(4,128)S(1)}, f32[3,2048]{1,0:T(4,128)S(1)}, u32[]{:S(2)}, u32[]{:S(2)}) %collective-permute-start.1) | collective-permute-done | bytes 24608 | tf_op jit(solution)/shard_map/ppermute | solution.py:13
  210.7 1.2 add_convert_fusion
  211.9 0.0 all-gather.2.cloned.1.call-update
  212.0 0.0 reduce-scatter.5.cloned.1.call-start
  212.0 74.4 %all-gather.2.cloned.1.call-done = bf16[1024,2048]{1,0:T(8,128)(2,1)} async-done(((bf16[128,2048]{1,0:T(8,128)(2,1)}), bf16[1024,2048]{1,0:T(8,128)(2,1)}) %all-gather.2.cloned.1.call-update) | async-done | bytes 4194320 | tf_op jit(solution)/shard_map/all_gather | solution.py:87
  286.4 4.5 %convolution_convert_fusion.2 = bf16[1024,512]{1,0:T(8,128)(2,1)S(1)} fusion(bf16[1024,2048]{1,0:T(8,128)(2,1)} %all-gather.2.cloned.1.call-done, bf16[512,2048]{1,0:T(8,128)(2,1)S(1)} %copy-done), kind=kOutput, calls=%fused_computation.6 | convolution fusion | flops 2148007936 | bytes 7340032 | tf_op jit(solution)/shard_map/dot_general | solution.py:88
  290.9 28.5 %all_to_all.39 = bf16[8,128,512]{2,1,0:T(8,128)(2,1)S(1)} all-to-all(bf16[8,128,512]{2,1,0:T(8,128)(2,1)S(1)} %bitcast.22), channel_id=1, replica_groups=mesh['row'=8,'col'=4] {'row'}, dimensions={0} | all-to-all | bytes 2097152 | tf_op jit(solution)/shard_map/all_to_all | solution.py:91
  319.5 1.1 copy.20
  320.6 0.0 reduce-scatter.5.cloned.1.call-update
  320.6 1.7 dynamic-slice_convert_fusion
  322.3 21.2 %reduce-scatter.5.cloned.1.call-done = bf16[128,1024]{1,0:T(8,128)(2,1)} async-done(((bf16[128,4096]{1,0:T(8,128)(2,1)}), bf16[128,1024]{1,0:T(8,128)(2,1)}) %reduce-scatter.5.cloned.1.call-update) | async-done | bytes 262160 | tf_op jit(solution)/shard_map/reduce_scatter | solution.py:96
  (4 shorter events, 0.1 us)
Async XLA Ops:
  7.2 35.4 %copy-start = (bf16[512,2048]{1,0:T(8,128)(2,1)S(1)}, bf16[512,2048]{1,0:T(8,128)(2,1)}, u32[]{:S(2)}) copy-start(bf16[512,2048]{1,0:T(8,128)(2,1)} %param.10) | copy-start | bytes 6291460
  7.2 128.1 %reduce-scatter.3.cloned.1.call-start = ((), (), s32[]{:S(2)}) async-start(), calls=%async_computation.4 | async-start | bytes 4718592 | tf_op jit(solution)/shard_map/reduce_scatter | solution.py:31
  48.1 0.8 copy-start.3
  48.1 91.4 %copy-start.4 = (s32[128]{0:T(128)S(1)}, s32[128]{0:T(128)}, u32[]{:S(2)}) copy-start(s32[128]{0:T(128)} %param.17) | copy-start | bytes 1540
  48.1 141.5 %all-reduce.8.cloned.1.call-start = ((), (), s32[]{:S(2)}) async-start(), calls=%async_computation.5 | async-start | bytes 2097152 | tf_op jit(solution)/shard_map/psum | solution.py:57
  136.1 4.8 %collective-permute-start = (bf16[3,2048]{1,0:T(4,128)(2,1)S(1)}, bf16[3,2048]{1,0:T(4,128)(2,1)S(1)}, u32[]{:S(2)}, u32[]{:S(2)}) collective-permute-start(bf16[3,2048]{1,0:T(4,128)(2,1)S(1)} %slice.64), channel_id=1, source_target_pairs={{0,4},{4,8},{8,12},{12,16},{16,20},{20,24},{24,28},{1,5},{5,9},{9,... | collective-permute-start | bytes 36872 | tf_op jit(solution)/shard_map/ppermute | solution.py:13
  142.1 1.7 copy-start.5
  142.8 1.0 copy-start.2
  143.8 9.5 %copy-start.6 = (f32[32]{0:T(128)S(1)}, f32[32]{0:T(128)}, u32[]{:S(2)}) copy-start(f32[32]{0:T(128)} %param.16) | copy-start | bytes 388
  143.8 9.5 %copy-start.7 = (s32[128]{0:T(128)S(1)}, s32[128]{0:T(128)}, u32[]{:S(2)}) copy-start(s32[128]{0:T(128)} %param.15) | copy-start | bytes 1540
  153.3 133.1 %all-gather.2.cloned.1.call-start = ((), (), s32[]{:S(2)}) async-start(), calls=%async_computation.6 | async-start | bytes 4718592 | tf_op jit(solution)/shard_map/all_gather | solution.py:87
  203.7 2.7 copy-start.1
  204.9 5.8 %collective-permute-start.1 = (f32[3,2048]{1,0:T(4,128)S(1)}, f32[3,2048]{1,0:T(4,128)S(1)}, u32[]{:S(2)}, u32[]{:S(2)}) collective-permute-start(f32[3,2048]{1,0:T(4,128)S(1)} %slice_add_fusion), channel_id=1, source_target_pairs={{4,0},{8,4},{12,8},{16,12},{20,16},{24,20},{28,24},{5,1},{9,5},{13... | collective-permute-start | bytes 73736 | tf_op jit(solution)/shard_map/ppermute | solution.py:13
  212.0 131.6 %reduce-scatter.5.cloned.1.call-start = ((), (), s32[]{:S(2)}) async-start(), calls=%async_computation.7 | async-start | bytes 1310720 | tf_op jit(solution)/shard_map/reduce_scatter | solution.py:96
Sparse Core Ops, SparseCore 0:
  48.2 87.0 reduce-scatter.2
  153.4 36.1 all-reduce.7
  212.1 74.2 all-gather.1
  320.7 22.7 reduce-scatter.4

commit v2 on v1

--- a/solution.py
+++ b/solution.py
@@ -13,6 +13,43 @@
     return lax.ppermute(value, axis, [(source, source + steps) for source in range(first, last)])
 
 
+def fetched_columns(tokens):
+    n_row, n_col = lax.axis_size("row"), lax.axis_size("col")
+    width = tokens.shape[1] // n_row
+    if n_col % 2:
+        return lax.all_to_all(tokens, "row", 1, 0, tiled=True)
+    core = lax.axis_index("col") % 2
+    halves = tokens.reshape(tokens.shape[0], n_row, 2, width // 2)
+    mine = jnp.take(halves, core, axis=2).reshape(tokens.shape[0], n_row * (width // 2))
+    mine = lax.all_to_all(mine, "row", 1, 0, tiled=True)
+    other = lax.ppermute(mine, "col", [(c, c ^ 1) for c in range(n_col)])
+    return jnp.where(
+        core == 0, jnp.concatenate([mine, other], axis=1), jnp.concatenate([other, mine], axis=1)
+    )
+
+
+def placed_blocks(grad_sum, row_count):
+    n_row, n_col = lax.axis_size("row"), lax.axis_size("col")
+    share = n_row // n_col
+    row, col = lax.axis_index("row"), lax.axis_index("col")
+    pieces = []
+    for j in range(share):
+        got = []
+        for k in range(share):
+            pairs = [
+                (r * n_col + c, (c * share + k) * n_col + r // share)
+                for r in range(n_row)
+                if r % share == j
+                for c in range(n_col)
+            ]
+            got.append(lax.ppermute(grad_sum[k * row_count : (k + 1) * row_count], ("row", "col"), pairs))
+        piece = got[0]
+        for k in range(1, share):
+            piece = jnp.where(row % share == k, got[k], piece)
+        pieces.append(piece)
+    return jnp.concatenate(pieces, axis=1)
+
+
 def silu_grad(argument):
     sigmoid_v = jax.nn.sigmoid(argument)
     return sigmoid_v * (1.0 + argument * (1.0 - sigmoid_v))
@@ -24,9 +61,12 @@
     row_count = tokens.shape[0]
     inner_width = gate_branch.shape[1]
     margin = CONV - 1
-    moves_tokens = row_count * lax.axis_size("row") < tokens.shape[1]
+    moves_tokens = (
+        row_count * lax.axis_size("row") < tokens.shape[1]
+        and lax.axis_size("row") % lax.axis_size("col") == 0
+    )
     if moves_tokens:
-        token_cols = lax.all_to_all(tokens, "row", 1, 0, tiled=True)
+        token_cols = fetched_columns(tokens)
         part_x = jnp.dot(token_cols, in_weight, preferred_element_type=jnp.float32)
         inner_x = lax.psum_scatter(part_x.astype(jnp.bfloat16), "row", scatter_dimension=0, tiled=True)
     else:
@@ -88,14 +128,17 @@
         grad_cols = lax.dot_general(
             grad_x_all, in_weight, (((1,), (1,)), ((), ())), preferred_element_type=jnp.float32
         )
-        partial_grad = lax.all_to_all(grad_cols.astype(jnp.bfloat16), "row", 0, 1, tiled=True)
+        grad_sum = lax.psum_scatter(
+            grad_cols.astype(jnp.bfloat16), "col", scatter_dimension=0, tiled=True
+        )
+        grad_tokens = placed_blocks(grad_sum, row_count)
     else:
         partial_grad = lax.dot_general(
             grad_x, full_in, (((1,), (1,)), ((), ())), preferred_element_type=jnp.float32
         )
-    grad_tokens = lax.psum_scatter(
-        partial_grad.astype(jnp.bfloat16), "col", scatter_dimension=1, tiled=True
-    )
+        grad_tokens = lax.psum_scatter(
+            partial_grad.astype(jnp.bfloat16), "col", scatter_dimension=1, tiled=True
+        )
     return (out_block.astype(jnp.bfloat16), grad_tokens, grad_gate)
 
 

time: 353 us -> 335 us (0.949)
  blocking collectives: 60.1 us -> 20.2 us
  starting transfers between devices: 5.03 us -> 19.7 us
  waiting for transfers between devices: 224 us -> 229 us
    all_to_all x2 -> x1, blocking collectives: 60.1 us -> 20.2 us  [fetched_columns(): mine = lax.all_to_all(mine, 'row', 1, 0, tiled=True)]
    ppermute x0 -> x5, starting transfers between devices: none -> 14.7 us  [the longest x4 14.7 us: placed_blocks(): lax.ppermute(grad_sum[k * row_count:(k + 1) * row_count], ('row', 'col'),...]
    ppermute x0 -> x5, waiting for transfers between devices: none -> 4.81 us  [the longest x4 2.9 us: placed_blocks(): lax.ppermute(grad_sum[k * row_count:(k + 1) * row_count], ('row', 'col'),...]
  transfers between devices with their start and end apart: 6 -> 11, of which waited for: 6 -> 8; matrix products, arithmetic and copies ran while one was open for 1% -> 1% of each run, Pallas kernels for 0% -> 0%
where the time goes in v2:
time: 335 us; the launch traced here: 331 us
  waiting for transfers between devices  229 us (68%)
  matrix products  33.3 us (10%)
  blocking collectives  20.2 us (6%)
  starting transfers between devices  19.7 us (6%)
  between operations  14 us (4%)
  local copies, waits for them, and re-layouts  9.33 us (3%)
  other arithmetic  5.08 us (2%)
    reduce_scatter x1, waiting for transfers between devices, shards(): lax.psum_scatter(part_x.astype(jnp.bfloat16), 'row', scatter_dimension=0,...  86.4 us
    all_gather x1, waiting for transfers between devices, shards(): grad_x_all = lax.all_gather(grad_x, 'row', axis=0, tiled=True)  74.4 us
    psum x1, waiting for transfers between devices, shards(): lax.psum(partial_value.astype(jnp.bfloat16), 'col').astype(jnp.float32)  36.1 us
    reduce_scatter x1, waiting for transfers between devices, shards(): lax.psum_scatter(grad_cols.astype(jnp.bfloat16), 'col', scatter_dimension...  22.1 us
    all_to_all x1, blocking collectives, fetched_columns(): mine = lax.all_to_all(mine, 'row', 1, 0, tiled=True)  20.2 us
    ppermute x4, starting transfers between devices, placed_blocks(): lax.ppermute(grad_sum[k * row_count:(k + 1) * row_count], ('row', 'col'),...  14.7 us
    dot_general x1, matrix products, shards(): lax.dot_general(residual_grad, out_weight, (((1,), (1,)), ((), ())), pref...  14.1 us
    dot_general x1, matrix products, shards(): jnp.dot(mixed, out_weight, preferred_element_type=jnp.float32)  9.44 us
  transfers between devices with their start and end apart: 11, of which 8 were waited for; matrix products, arithmetic and copies ran while one was open for 1% of the time, Pallas kernels for 0%

profile of v2, /device:TPU:2, one launch (start us, length us, event | category | flops | bytes accessed | tf_op | source)
XLA Modules:
  0.0 331.0 jit_solution(12576042622889315957)
XLA Ops:
  7.2 0.0 copy-start
  7.2 0.0 reduce-scatter.3.cloned.1.call-start
  7.2 1.8 copy.19
  9.0 0.8 select_bitcast_fusion
  9.9 1.2 copy.21
  11.1 20.2 %all_to_all.16 = bf16[128,8,256]{2,0,1:T(8,128)(2,1)S(1)} all-to-all(bf16[128,8,256]{2,0,1:T(8,128)(2,1)S(1)} %copy.21), channel_id=1, replica_groups=mesh['row'=8,'col'=4] {'row'}, dimensions={1} | all-to-all | bytes 1048576 | tf_op jit(solution)/shard_map/all_to_all | solution.py:24
  31.3 0.0 collective-permute-start
  31.3 1.9 collective-permute-done
  33.2 0.0 copy-done
  33.2 4.3 %convolution_convert_fusion.1 = bf16[1024,2048]{1,0:T(8,128)(2,1)} fusion(bf16[512,2048]{1,0:T(8,128)(2,1)S(1)} %copy-done, bf16[1024,256]{1,0:T(8,128)(2,1)S(1)} %collective-permute-done, bf16[1024,256]{1,0:T(8,128)(2,1)S(1)} %bitcast.17, pred[]{:T(512)S(6)} %eq.24), kind=kOutput, calls=%fused_computation.1 | convolution fusion | flops 2154299392 | bytes 7340033 | tf_op jit(solution)/shard_map/dot_general | solution.py:70
  37.5 0.0 copy-start.3
  37.5 0.0 copy-start.4
  37.5 0.0 reduce-scatter.3.cloned.1.call-update
  37.5 0.0 all-reduce.8.cloned.1.call-start
  37.6 0.7 copy-done.3
  38.3 86.4 %reduce-scatter.3.cloned.1.call-done = bf16[128,2048]{1,0:T(8,128)(2,1)} async-done(((bf16[1024,2048]{1,0:T(8,128)(2,1)}), bf16[128,2048]{1,0:T(8,128)(2,1)}) %reduce-scatter.3.cloned.1.call-update) | async-done | bytes 524304 | tf_op jit(solution)/shard_map/reduce_scatter | solution.py:71
  124.7 0.8 slice.85
  125.5 3.4 %collective-permute-start.1 = (bf16[3,2048]{1,0:T(4,128)(2,1)S(1)}, bf16[3,2048]{1,0:T(4,128)(2,1)S(1)}, u32[]{:S(2)}, u32[]{:S(2)}) collective-permute-start(bf16[3,2048]{1,0:T(4,128)(2,1)S(1)} %slice.85), channel_id=1, source_target_pairs={{0,4},{4,8},{8,12},{12,16},{16,20},{20,24},{24,28},{1,5},{5,9},{9,... | collective-permute-start | bytes 36872 | tf_op jit(solution)/shard_map/ppermute | solution.py:13
  128.9 0.0 copy-done.4
  128.9 1.4 collective-permute-done.1
  130.3 1.2 maximum_convert_fusion
  131.5 0.0 copy-start.5
  131.5 0.7 fusion.9
  132.2 0.0 copy-start.2
  132.2 1.0 copy-done.2
  133.2 0.0 copy-done.5
  133.2 0.0 copy-start.6
  133.2 0.0 copy-start.7
  133.2 9.4 %convolution_convert_fusion = bf16[128,4096]{1,0:T(8,128)(2,1)} fusion(bf16[2048,4096]{1,0:T(8,128)(2,1)} %param.13, bf16[128,2048]{1,0:T(8,128)(2,1)S(1)} %copy-done.5, f32[128,2048]{1,0:T(8,128)S(1)} %fusion.9), kind=kOutput, calls=%fused_computation | convolution fusion | flops 2150891520 | bytes 19398656 | tf_op jit(solution)/shard_map/dot_general | solution.py:90
  142.7 0.0 all-reduce.8.cloned.1.call-update
  142.7 0.0 all-gather.2.cloned.1.call-start
  142.8 0.0 copy-done.6
  142.8 0.0 copy-done.7
  142.8 0.1 select_reduce_fusion
  142.9 36.1 %all-reduce.8.cloned.1.call-done = bf16[128,4096]{1,0:T(8,128)(2,1)} async-done(((bf16[128,4096]{1,0:T(8,128)(2,1)}), bf16[128,4096]{1,0:T(8,128)(2,1)}) %all-reduce.8.cloned.1.call-update) | async-done | bytes 1048592 | tf_op jit(solution)/shard_map/psum | solution.py:97
  179.0 14.1 %multiply_multiply_fusion.2 = (f32[128,2048]{1,0:T(8,128)}, f32[128,2048]{1,0:T(8,128)S(1)}, bf16[128,2048]{1,0:T(8,128)(2,1)}) fusion(f32[128]{0:T(128)S(1)} %get-tuple-element.26, f32[2048]{0:T(1024)S(1)} %bitcast.25, f32[128,2048]{1,0:T(8,128)} %copy-done.2, bf16[128,2048]{1,0:T(8,128)(2,1)} %param.11, bf16[2048,4096]{1,0:T(8,128)(2,1)} %param.13, ...), kind=kOutput, calls=%fused_computation.35 | convolution fusion | flops 2156396544 | bytes 23077888 | tf_op jit(solution)/shard_map/dot_general | solution.py:100
  193.0 0.0 copy-start.1
  193.0 0.9 slice.93
  193.9 0.3 multiply_multiply_fusion.1
  194.3 1.5 collective-permute-start.2
  195.8 0.0 copy-done.1
  195.8 0.1 slice.90
  195.9 0.1 slice.91
  195.9 0.1 slice.92
  196.0 4.0 %collective-permute-done.2 = f32[3,2048]{1,0:T(4,128)S(1)} collective-permute-done((f32[3,2048]{1,0:T(4,128)S(1)}, f32[3,2048]{1,0:T(4,128)S(1)}, u32[]{:S(2)}, u32[]{:S(2)}) %collective-permute-start.2) | collective-permute-done | bytes 24608 | tf_op jit(solution)/shard_map/ppermute | solution.py:13
  200.1 1.2 add_convert_fusion
  201.2 0.0 all-gather.2.cloned.1.call-update
  201.3 0.0 reduce-scatter.5.cloned.1.call-start
  201.3 74.4 %all-gather.2.cloned.1.call-done = bf16[1024,2048]{1,0:T(8,128)(2,1)} async-done(((bf16[128,2048]{1,0:T(8,128)(2,1)}), bf16[1024,2048]{1,0:T(8,128)(2,1)}) %all-gather.2.cloned.1.call-update) | async-done | bytes 4194320 | tf_op jit(solution)/shard_map/all_gather | solution.py:127
  275.7 5.6 %convolution_convert_fusion.2 = bf16[1024,512]{1,0:T(8,128)(2,1)} fusion(bf16[1024,2048]{1,0:T(8,128)(2,1)} %all-gather.2.cloned.1.call-done, bf16[512,2048]{1,0:T(8,128)(2,1)S(1)} %copy-done), kind=kOutput, calls=%fused_computation.6 | convolution fusion | flops 2148007936 | bytes 7340032 | tf_op jit(solution)/shard_map/dot_general | solution.py:128
  281.3 0.0 reduce-scatter.5.cloned.1.call-update
  281.3 22.1 %reduce-scatter.5.cloned.1.call-done = bf16[256,512]{1,0:T(8,128)(2,1)} async-done(((bf16[1024,512]{1,0:T(8,128)(2,1)}), bf16[256,512]{1,0:T(8,128)(2,1)}) %reduce-scatter.5.cloned.1.call-update) | async-done | bytes 262160 | tf_op jit(solution)/shard_map/reduce_scatter | solution.py:131
  303.4 1.0 fusion.27
  304.4 1.3 collective-permute-start.6
  305.7 0.7 collective-permute-start.5
  306.4 1.7 dynamic-slice_convert_fusion
  308.1 5.4 %collective-permute-start.4 = (bf16[128,512]{1,0:T(8,128)(2,1)S(1)}, bf16[128,512]{1,0:T(8,128)(2,1)S(1)}, u32[]{:S(2)}, u32[]{:S(2)}) collective-permute-start(bf16[128,512]{1,0:T(8,128)(2,1)S(1)} %get-tuple-element.19), channel_id=1, source_target_pairs={{0,0},{1,8},{2,16},{3,24},{8,1},{9,9},{10,17},{11,25},{16,2},{17,1... | collective-permute-start | bytes 393224 | tf_op jit(solution)/shard_map/ppermute | solution.py:45
  313.5 7.3 %collective-permute-start.3 = (bf16[128,512]{1,0:T(8,128)(2,1)S(1)}, bf16[128,512]{1,0:T(8,128)(2,1)S(1)}, u32[]{:S(2)}, u32[]{:S(2)}) collective-permute-start(bf16[128,512]{1,0:T(8,128)(2,1)S(1)} %get-tuple-element.20), channel_id=1, source_target_pairs={{0,4},{1,12},{2,20},{3,28},{8,5},{9,13},{10,21},{11,29},{16,6},{17... | collective-permute-start | bytes 393224 | tf_op jit(solution)/shard_map/ppermute | solution.py:45
  320.8 0.0 collective-permute-done.6
  320.8 0.0 collective-permute-done.5
  320.8 0.0 collective-permute-done.4
  320.9 2.9 collective-permute-done.3
  323.8 0.7 pad_maximum_fusion
  (6 shorter events, 0.1 us)
Async XLA Ops:
  7.2 26.0 %copy-start = (bf16[512,2048]{1,0:T(8,128)(2,1)S(1)}, bf16[512,2048]{1,0:T(8,128)(2,1)}, u32[]{:S(2)}) copy-start(bf16[512,2048]{1,0:T(8,128)(2,1)} %param.10) | copy-start | bytes 6291460
  7.2 117.5 %reduce-scatter.3.cloned.1.call-start = ((), (), s32[]{:S(2)}) async-start(), calls=%async_computation.3 | async-start | bytes 4718592 | tf_op jit(solution)/shard_map/reduce_scatter | solution.py:71
  31.3 1.9 collective-permute-start
  37.5 0.8 copy-start.3
  37.5 91.4 %copy-start.4 = (s32[128]{0:T(128)S(1)}, s32[128]{0:T(128)}, u32[]{:S(2)}) copy-start(s32[128]{0:T(128)} %param.17) | copy-start | bytes 1540
  37.5 141.4 %all-reduce.8.cloned.1.call-start = ((), (), s32[]{:S(2)}) async-start(), calls=%async_computation.4 | async-start | bytes 2097152 | tf_op jit(solution)/shard_map/psum | solution.py:97
  125.5 4.8 %collective-permute-start.1 = (bf16[3,2048]{1,0:T(4,128)(2,1)S(1)}, bf16[3,2048]{1,0:T(4,128)(2,1)S(1)}, u32[]{:S(2)}, u32[]{:S(2)}) collective-permute-start(bf16[3,2048]{1,0:T(4,128)(2,1)S(1)} %slice.85), channel_id=1, source_target_pairs={{0,4},{4,8},{8,12},{12,16},{16,20},{20,24},{24,28},{1,5},{5,9},{9,... | collective-permute-start | bytes 36872 | tf_op jit(solution)/shard_map/ppermute | solution.py:13
  131.5 1.7 copy-start.5
  132.2 1.0 copy-start.2
  133.2 9.5 %copy-start.6 = (f32[32]{0:T(128)S(1)}, f32[32]{0:T(128)}, u32[]{:S(2)}) copy-start(f32[32]{0:T(128)} %param.16) | copy-start | bytes 388
  133.2 9.5 %copy-start.7 = (s32[128]{0:T(128)S(1)}, s32[128]{0:T(128)}, u32[]{:S(2)}) copy-start(s32[128]{0:T(128)} %param.15) | copy-start | bytes 1540
  142.7 133.0 %all-gather.2.cloned.1.call-start = ((), (), s32[]{:S(2)}) async-start(), calls=%async_computation.5 | async-start | bytes 4718592 | tf_op jit(solution)/shard_map/all_gather | solution.py:127
  193.0 2.7 copy-start.1
  194.3 5.8 %collective-permute-start.2 = (f32[3,2048]{1,0:T(4,128)S(1)}, f32[3,2048]{1,0:T(4,128)S(1)}, u32[]{:S(2)}, u32[]{:S(2)}) collective-permute-start(f32[3,2048]{1,0:T(4,128)S(1)} %slice_add_fusion), channel_id=1, source_target_pairs={{4,0},{8,4},{12,8},{16,12},{20,16},{24,20},{28,24},{5,1},{9,5},{13... | collective-permute-start | bytes 73736 | tf_op jit(solution)/shard_map/ppermute | solution.py:13
  201.3 102.2 %reduce-scatter.5.cloned.1.call-start = ((), (), s32[]{:S(2)}) async-start(), calls=%async_computation.6 | async-start | bytes 1310720 | tf_op jit(solution)/shard_map/reduce_scatter | solution.py:131
  304.4 16.4 %collective-permute-start.6 = (bf16[128,512]{1,0:T(8,128)(2,1)S(1)}, bf16[128,512]{1,0:T(8,128)(2,1)S(1)}, u32[]{:S(2)}, u32[]{:S(2)}) collective-permute-start(bf16[128,512]{1,0:T(8,128)(2,1)S(1)} %get-tuple-element.19), channel_id=1, source_target_pairs={{4,0},{5,8},{6,16},{7,24},{12,1},{13,9},{14,17},{15,25},{20,2},{21... | collective-permute-start | bytes 393224 | tf_op jit(solution)/shard_map/ppermute | solution.py:45
  305.7 15.1 %collective-permute-start.5 = (bf16[128,512]{1,0:T(8,128)(2,1)S(1)}, bf16[128,512]{1,0:T(8,128)(2,1)S(1)}, u32[]{:S(2)}, u32[]{:S(2)}) collective-permute-start(bf16[128,512]{1,0:T(8,128)(2,1)S(1)} %get-tuple-element.20), channel_id=1, source_target_pairs={{4,4},{5,12},{6,20},{7,28},{12,5},{13,13},{14,21},{15,29},{20,6},{... | collective-permute-start | bytes 393224 | tf_op jit(solution)/shard_map/ppermute | solution.py:45
  308.1 12.8 %collective-permute-start.4 = (bf16[128,512]{1,0:T(8,128)(2,1)S(1)}, bf16[128,512]{1,0:T(8,128)(2,1)S(1)}, u32[]{:S(2)}, u32[]{:S(2)}) collective-permute-start(bf16[128,512]{1,0:T(8,128)(2,1)S(1)} %get-tuple-element.19), channel_id=1, source_target_pairs={{0,0},{1,8},{2,16},{3,24},{8,1},{9,9},{10,17},{11,25},{16,2},{17,1... | collective-permute-start | bytes 393224 | tf_op jit(solution)/shard_map/ppermute | solution.py:45
  313.5 10.2 %collective-permute-start.3 = (bf16[128,512]{1,0:T(8,128)(2,1)S(1)}, bf16[128,512]{1,0:T(8,128)(2,1)S(1)}, u32[]{:S(2)}, u32[]{:S(2)}) collective-permute-start(bf16[128,512]{1,0:T(8,128)(2,1)S(1)} %get-tuple-element.20), channel_id=1, source_target_pairs={{0,4},{1,12},{2,20},{3,28},{8,5},{9,13},{10,21},{11,29},{16,6},{17... | collective-permute-start | bytes 393224 | tf_op jit(solution)/shard_map/ppermute | solution.py:45
Sparse Core Ops, SparseCore 0:
  37.6 87.0 reduce-scatter.2
  142.8 36.0 all-reduce.7
  201.4 74.2 all-gather.1
  281.4 21.9 reduce-scatter.4

commit v3 on v2

--- a/solution.py
+++ b/solution.py
@@ -48,6 +48,37 @@
             piece = jnp.where(row % share == k, got[k], piece)
         pieces.append(piece)
     return jnp.concatenate(pieces, axis=1)
+
+
+def ring_order(count):
+    if count % 2:
+        return list(range(count))
+    return list(range(0, count, 2)) + list(range(count - 1, 0, -2))
+
+
+def ring_gather(value, axis):
+    count = lax.axis_size(axis)
+    order = ring_order(count)
+    place = jnp.array([order.index(i) for i in range(count)], jnp.int32)[lax.axis_index(axis)]
+    ahead = [(order[i], order[(i + 1) % count]) for i in range(count)]
+    behind = [(order[(i + 1) % count], order[i]) for i in range(count)]
+    half = value.shape[1] // 2
+    sent_a, sent_b = value[:, :half], value[:, half:]
+    got_a, got_b = [sent_a], [sent_b]
+    for _ in range(1, count):
+        sent_a = lax.ppermute(sent_a, axis, ahead)
+        sent_b = lax.ppermute(sent_b, axis, behind)
+        got_a.append(sent_a)
+        got_b.append(sent_b)
+    steps = jnp.arange(count)
+    order_arr = jnp.array(order, jnp.int32)
+    from_a = jnp.argsort(order_arr[(place - steps) % count])
+    from_b = jnp.argsort(order_arr[(place + steps) % count])
+    gathered_a = jnp.take(jnp.stack(got_a), from_a, axis=0)
+    gathered_b = jnp.take(jnp.stack(got_b), from_b, axis=0)
+    return jnp.concatenate([gathered_a, gathered_b], axis=2).reshape(
+        count * value.shape[0], value.shape[1]
+    )
 
 
 def silu_grad(argument):
@@ -124,7 +155,7 @@
         )
     ).astype(jnp.bfloat16)
     if moves_tokens:
-        grad_x_all = lax.all_gather(grad_x, "row", axis=0, tiled=True)
+        grad_x_all = ring_gather(grad_x, "row")
         grad_cols = lax.dot_general(
             grad_x_all, in_weight, (((1,), (1,)), ((), ())), preferred_element_type=jnp.float32
         )

time: 335 us -> 331 us (0.988); the launches traced: 331 us -> 331 us
  waiting for transfers between devices: 229 us -> 185 us
  local copies, waits for them, and re-layouts: 9.33 us -> 29.4 us
  starting transfers between devices: 19.7 us -> 37.7 us
  other arithmetic: 5.08 us -> 13.2 us
    all_gather x1 -> x0, waiting for transfers between devices: 74.4 us -> none  [shards(): grad_x_all = lax.all_gather(grad_x, 'row', axis=0, tiled=True)]
    ppermute x0 -> x14, waiting for transfers between devices: none -> 26.9 us  [the longest x7 26.8 us: ring_gather(): sent_b = lax.ppermute(sent_b, axis, behind)]
    ppermute x0 -> x14, starting transfers between devices: none -> 17.3 us  [the longest x7 17.2 us: ring_gather(): sent_b = lax.ppermute(sent_b, axis, behind)]
    unnamed x17 -> x36, local copies, waits for them, and re-layouts: 3.45 us -> 13.9 us
    gather x0 -> x4, local copies, waits for them, and re-layouts: none -> 8.48 us  [the longest x1 3.62 us: ring_gather(): gathered_b = jnp.take(jnp.stack(got_b), from_b, axis=0)]
    select_n x0 -> x6, other arithmetic: none -> 6.52 us  [the longest x2 3.21 us: ring_gather(): gathered_b = jnp.take(jnp.stack(got_b), from_b, axis=0)]
    ppermute x4, waiting for transfers between devices: 2.9 us -> 8.9 us  [placed_blocks(): lax.ppermute(grad_sum[k * row_count:(k + 1) * row_count], ('row', 'col'),...]
    reduce_scatter x1, waiting for transfers between devices: 86.4 us -> 83 us  [shards(): lax.psum_scatter(part_x.astype(jnp.bfloat16), 'row', scatter_dimension=0,...]
  transfers between devices with their start and end apart: 11 -> 24, of which waited for: 8 -> 14; matrix products, arithmetic and copies ran while one was open for 1% -> 7% of each run, Pallas kernels for 0% -> 0%
where the time goes in v3:
time: 331 us
  waiting for transfers between devices  185 us (56%)
  starting transfers between devices  37.7 us (11%)
  matrix products  31.1 us (9%)
  local copies, waits for them, and re-layouts  29.4 us (9%)
  blocking collectives  20.2 us (6%)
  between operations  14.1 us (4%)
  other arithmetic  13.2 us (4%)
    reduce_scatter x1, waiting for transfers between devices, shards(): lax.psum_scatter(part_x.astype(jnp.bfloat16), 'row', scatter_dimension=0,...  83 us
    psum x1, waiting for transfers between devices, shards(): lax.psum(partial_value.astype(jnp.bfloat16), 'col').astype(jnp.float32)  35.8 us
    ppermute x7, waiting for transfers between devices, ring_gather(): sent_b = lax.ppermute(sent_b, axis, behind)  26.8 us
    reduce_scatter x1, waiting for transfers between devices, shards(): lax.psum_scatter(grad_cols.astype(jnp.bfloat16), 'col', scatter_dimension...  24.1 us
    all_to_all x1, blocking collectives, fetched_columns(): mine = lax.all_to_all(mine, 'row', 1, 0, tiled=True)  20.2 us
    ppermute x7, starting transfers between devices, ring_gather(): sent_b = lax.ppermute(sent_b, axis, behind)  17.2 us
    ppermute x4, starting transfers between devices, placed_blocks(): lax.ppermute(grad_sum[k * row_count:(k + 1) * row_count], ('row', 'col'),...  15.3 us
    dot_general x1, matrix products, shards(): lax.dot_general(residual_grad, out_weight, (((1,), (1,)), ((), ())), pref...  14 us
  transfers between devices with their start and end apart: 24, of which 14 were waited for; matrix products, arithmetic and copies ran while one was open for 7% of the time, Pallas kernels for 0%

profile of v3, /device:TPU:2, one launch (start us, length us, event | category | flops | bytes accessed | tf_op | source)
XLA Modules:
  0.0 330.5 jit_solution(3866224230449279530)
XLA Ops:
  7.2 1.8 copy.21
  9.0 0.8 select_bitcast_fusion
  9.9 1.2 copy.23
  11.1 20.2 %all_to_all.16 = bf16[128,8,256]{2,0,1:T(8,128)(2,1)S(1)} all-to-all(bf16[128,8,256]{2,0,1:T(8,128)(2,1)S(1)} %copy.23), channel_id=1, replica_groups=mesh['row'=8,'col'=4] {'row'}, dimensions={1} | all-to-all | bytes 1048576 | tf_op jit(solution)/shard_map/all_to_all | solution.py:24
  31.3 1.9 collective-permute-done
  33.2 4.3 %convolution_convert_fusion.1 = bf16[1024,2048]{1,0:T(8,128)(2,1)} fusion(bf16[512,2048]{1,0:T(8,128)(2,1)S(1)} %copy-done, bf16[1024,256]{1,0:T(8,128)(2,1)S(1)} %collective-permute-done, bf16[1024,256]{1,0:T(8,128)(2,1)S(1)} %bitcast.56, pred[]{:T(512)S(6)} %eq.27), kind=kOutput, calls=%fused_computation.6 | convolution fusion | flops 2154299392 | bytes 7340033 | tf_op jit(solution)/shard_map/dot_general | solution.py:101
  40.0 1.0 sort.32
  41.8 83.0 %reduce-scatter.3.cloned.1.call-done = bf16[128,2048]{1,0:T(8,128)(2,1)} async-done(((bf16[1024,2048]{1,0:T(8,128)(2,1)}), bf16[128,2048]{1,0:T(8,128)(2,1)}) %reduce-scatter.3.cloned.1.call-update) | async-done | bytes 524304 | tf_op jit(solution)/shard_map/reduce_scatter | solution.py:102
  124.7 0.8 slice.101
  125.5 3.4 %collective-permute-start.1 = (bf16[3,2048]{1,0:T(4,128)(2,1)S(1)}, bf16[3,2048]{1,0:T(4,128)(2,1)S(1)}, u32[]{:S(2)}, u32[]{:S(2)}) collective-permute-start(bf16[3,2048]{1,0:T(4,128)(2,1)S(1)} %slice.101), channel_id=1, source_target_pairs={{0,4},{4,8},{8,12},{12,16},{16,20},{20,24},{24,28},{1,5},{5,9},{9,... | collective-permute-start | bytes 36872 | tf_op jit(solution)/shard_map/ppermute | solution.py:13
  129.5 1.0 sort.31
  130.5 1.2 maximum_convert_fusion
  131.7 0.7 fusion.9
  132.5 1.0 copy-done.4
  133.4 9.4 %convolution_convert_fusion = bf16[128,4096]{1,0:T(8,128)(2,1)} fusion(bf16[2048,4096]{1,0:T(8,128)(2,1)} %param.17, bf16[128,2048]{1,0:T(8,128)(2,1)S(1)} %copy-done.7, f32[128,2048]{1,0:T(8,128)S(1)} %fusion.9), kind=kOutput, calls=%fused_computation.4 | convolution fusion | flops 2150891520 | bytes 19398656 | tf_op jit(solution)/shard_map/dot_general | solution.py:121
  143.3 35.8 %all-reduce.8.cloned.1.call-done = bf16[128,4096]{1,0:T(8,128)(2,1)} async-done(((bf16[128,4096]{1,0:T(8,128)(2,1)}), bf16[128,4096]{1,0:T(8,128)(2,1)}) %all-reduce.8.cloned.1.call-update) | async-done | bytes 1048592 | tf_op jit(solution)/shard_map/psum | solution.py:128
  179.1 14.0 %multiply_multiply_fusion.2 = (f32[128,2048]{1,0:T(8,128)}, f32[128,2048]{1,0:T(8,128)S(1)}, bf16[128,2048]{1,0:T(8,128)(2,1)}) fusion(f32[128]{0:T(128)S(1)} %get-tuple-element.35, f32[2048]{0:T(1024)S(1)} %bitcast.64, f32[128,2048]{1,0:T(8,128)} %copy-done.4, bf16[128,2048]{1,0:T(8,128)(2,1)} %param.15, bf16[2048,4096]{1,0:T(8,128)(2,1)} %param.17, ...), kind=kOutput, calls=%fused_computation.42 | convolution fusion | flops 2156396544 | bytes 23077888 | tf_op jit(solution)/shard_map/dot_general | solution.py:131
  193.4 0.9 copy-done.3
  194.4 1.3 collective-permute-start.2
  196.0 4.2 %collective-permute-done.2 = f32[3,2048]{1,0:T(4,128)S(1)} collective-permute-done((f32[3,2048]{1,0:T(4,128)S(1)}, f32[3,2048]{1,0:T(4,128)S(1)}, u32[]{:S(2)}, u32[]{:S(2)}) %collective-permute-start.2) | collective-permute-done | bytes 24608 | tf_op jit(solution)/shard_map/ppermute | solution.py:13
  200.6 2.4 collective-permute-start.10
  203.1 0.8 bitcast_dynamic-update-slice_fusion.15
  203.9 3.5 %collective-permute-done.10 = bf16[128,1024]{1,0:T(8,128)(2,1)S(1)} collective-permute-done((bf16[128,1024]{1,0:T(8,128)(2,1)S(1)}, bf16[128,1024]{1,0:T(8,128)(2,1)S(1)}, u32[]{:S(2)}, u32[]{:S(2)}) %collective-permute-start.10) | collective-permute-done | bytes 262176 | tf_op jit(solution)/shard_map/ppermute | solution.py:70
  207.4 2.4 collective-permute-start.11
  209.8 0.7 bitcast_dynamic-update-slice_fusion.6
  210.5 0.7 bitcast_dynamic-update-slice_fusion.14
  211.2 3.3 %collective-permute-done.11 = bf16[128,1024]{1,0:T(8,128)(2,1)S(1)} collective-permute-done((bf16[128,1024]{1,0:T(8,128)(2,1)S(1)}, bf16[128,1024]{1,0:T(8,128)(2,1)S(1)}, u32[]{:S(2)}, u32[]{:S(2)}) %collective-permute-start.11) | collective-permute-done | bytes 262176 | tf_op jit(solution)/shard_map/ppermute | solution.py:70
  214.6 2.5 collective-permute-start.12
  217.0 0.7 bitcast_dynamic-update-slice_fusion.5
  217.8 0.7 bitcast_dynamic-update-slice_fusion.13
  218.5 4.1 %collective-permute-done.12 = bf16[128,1024]{1,0:T(8,128)(2,1)S(1)} collective-permute-done((bf16[128,1024]{1,0:T(8,128)(2,1)S(1)}, bf16[128,1024]{1,0:T(8,128)(2,1)S(1)}, u32[]{:S(2)}, u32[]{:S(2)}) %collective-permute-start.12) | collective-permute-done | bytes 262176 | tf_op jit(solution)/shard_map/ppermute | solution.py:70
  222.6 2.5 collective-permute-start.13
  225.1 0.7 bitcast_dynamic-update-slice_fusion.4
  225.8 0.7 bitcast_dynamic-update-slice_fusion.12
  226.6 5.0 %collective-permute-done.13 = bf16[128,1024]{1,0:T(8,128)(2,1)S(1)} collective-permute-done((bf16[128,1024]{1,0:T(8,128)(2,1)S(1)}, bf16[128,1024]{1,0:T(8,128)(2,1)S(1)}, u32[]{:S(2)}, u32[]{:S(2)}) %collective-permute-start.13) | collective-permute-done | bytes 262176 | tf_op jit(solution)/shard_map/ppermute | solution.py:70
  231.5 2.5 collective-permute-start.14
  234.0 0.7 bitcast_dynamic-update-slice_fusion.3
  234.8 0.7 bitcast_dynamic-update-slice_fusion.11
  235.5 4.7 %collective-permute-done.14 = bf16[128,1024]{1,0:T(8,128)(2,1)S(1)} collective-permute-done((bf16[128,1024]{1,0:T(8,128)(2,1)S(1)}, bf16[128,1024]{1,0:T(8,128)(2,1)S(1)}, u32[]{:S(2)}, u32[]{:S(2)}) %collective-permute-start.14) | collective-permute-done | bytes 262176 | tf_op jit(solution)/shard_map/ppermute | solution.py:70
  240.2 2.5 collective-permute-start.15
  242.6 0.7 bitcast_dynamic-update-slice_fusion.2
  243.4 0.7 bitcast_dynamic-update-slice_fusion.10
  244.1 3.8 %collective-permute-done.15 = bf16[128,1024]{1,0:T(8,128)(2,1)S(1)} collective-permute-done((bf16[128,1024]{1,0:T(8,128)(2,1)S(1)}, bf16[128,1024]{1,0:T(8,128)(2,1)S(1)}, u32[]{:S(2)}, u32[]{:S(2)}) %collective-permute-start.15) | collective-permute-done | bytes 262176 | tf_op jit(solution)/shard_map/ppermute | solution.py:70
  247.9 2.5 collective-permute-start.16
  250.4 0.7 bitcast_dynamic-update-slice_fusion.1
  251.2 0.7 bitcast_dynamic-update-slice_fusion.9
  251.9 2.4 collective-permute-done.16
  254.3 0.7 bitcast_dynamic-update-slice_fusion
  255.0 3.6 %gather_fusion.3 = bf16[8,128,1024]{2,1,0:T(8,128)(2,1)} fusion(bf16[8,128,1024]{2,1,0:T(8,128)(2,1)} %bitcast_dynamic-update-slice_fusion, s32[1024]{0:T(1024)S(1)} %pad_clamp_fusion), kind=kCustom, calls=%fused_computation.1.clone | custom fusion | bytes 4194336 | tf_op jit(solution)/shard_map/jit(_take)/gather | solution.py:78
  258.6 3.2 broadcast_select_fusion
  261.8 0.7 bitcast_dynamic-update-slice_fusion.8
  262.5 3.6 %gather_fusion.2 = bf16[8,128,1024]{2,1,0:T(8,128)(2,1)} fusion(bf16[8,128,1024]{2,1,0:T(8,128)(2,1)} %bitcast_dynamic-update-slice_fusion.8, s32[1024]{0:T(1024)S(1)} %pad_clamp_fusion.2), kind=kCustom, calls=%fused_computation.clone | custom fusion | bytes 4194336 | tf_op jit(solution)/shard_map/jit(_take)/gather | solution.py:77
  266.1 2.0 broadcast_select_fusion.1
  268.8 3.4 %convolution_convert_fusion.2 = bf16[1024,512]{1,0:T(8,128)(2,1)} fusion(bf16[1024,2048]{1,0:T(8,128)(2,1)S(1)} %bitcast.53, bf16[512,2048]{1,0:T(8,128)(2,1)S(1)} %copy-done), kind=kOutput, calls=%fused_computation.13 | convolution fusion | flops 2148007936 | bytes 7340032 | tf_op jit(solution)/shard_map/dot_general | solution.py:159
  272.2 24.1 %reduce-scatter.5.cloned.1.call-done = bf16[256,512]{1,0:T(8,128)(2,1)} async-done(((bf16[1024,512]{1,0:T(8,128)(2,1)}), bf16[256,512]{1,0:T(8,128)(2,1)}) %reduce-scatter.5.cloned.1.call-update) | async-done | bytes 262160 | tf_op jit(solution)/shard_map/reduce_scatter | solution.py:162
  296.3 1.0 fusion.32
  297.3 0.7 collective-permute-start.19
  298.0 1.3 collective-permute-start.20
  299.3 1.7 dynamic-slice_convert_fusion
  300.9 8.1 %collective-permute-start.17 = (bf16[128,512]{1,0:T(8,128)(2,1)S(1)}, bf16[128,512]{1,0:T(8,128)(2,1)S(1)}, u32[]{:S(2)}, u32[]{:S(2)}) collective-permute-start(bf16[128,512]{1,0:T(8,128)(2,1)S(1)} %get-tuple-element.29), channel_id=1, source_target_pairs={{0,4},{1,12},{2,20},{3,28},{8,5},{9,13},{10,21},{11,29},{16,6},{17... | collective-permute-start | bytes 393224 | tf_op jit(solution)/shard_map/ppermute | solution.py:45
  309.1 5.2 %collective-permute-start.18 = (bf16[128,512]{1,0:T(8,128)(2,1)S(1)}, bf16[128,512]{1,0:T(8,128)(2,1)S(1)}, u32[]{:S(2)}, u32[]{:S(2)}) collective-permute-start(bf16[128,512]{1,0:T(8,128)(2,1)S(1)} %get-tuple-element.28), channel_id=1, source_target_pairs={{0,0},{1,8},{2,16},{3,24},{8,1},{9,9},{10,17},{11,25},{16,2},{17,1... | collective-permute-start | bytes 393224 | tf_op jit(solution)/shard_map/ppermute | solution.py:45
  314.3 2.0 collective-permute-done.20
  316.4 6.9 %collective-permute-done.18 = bf16[128,512]{1,0:T(8,128)(2,1)S(1)} collective-permute-done((bf16[128,512]{1,0:T(8,128)(2,1)S(1)}, bf16[128,512]{1,0:T(8,128)(2,1)S(1)}, u32[]{:S(2)}, u32[]{:S(2)}) %collective-permute-start.18) | collective-permute-done | bytes 131104 | tf_op jit(solution)/shard_map/ppermute | solution.py:45
  323.3 0.7 pad_maximum_fusion.1
  (73 shorter events, 6.2 us)
Async XLA Ops:
  7.2 26.0 %copy-start = (bf16[512,2048]{1,0:T(8,128)(2,1)S(1)}, bf16[512,2048]{1,0:T(8,128)(2,1)}, u32[]{:S(2)}) copy-start(bf16[512,2048]{1,0:T(8,128)(2,1)} %param.14) | copy-start | bytes 6291460
  7.2 117.5 %reduce-scatter.3.cloned.1.call-start = ((), (), s32[]{:S(2)}) async-start(), calls=%async_computation.3 | async-start | bytes 4718592 | tf_op jit(solution)/shard_map/reduce_scatter | solution.py:102
  31.3 1.9 collective-permute-start
  37.5 0.7 copy-start.10
  37.5 1.9 copy-start.1
  37.5 4.2 %copy-start.6 = (s32[128]{0:T(128)S(1)}, s32[128]{0:T(128)}, u32[]{:S(2)}) copy-start(s32[128]{0:T(128)} %param.21) | copy-start | bytes 1540
  37.5 4.2 %copy-start.5 = (f32[4,2048]{1,0:T(4,128)S(1)}, f32[4,2048]{1,0:T(4,128)}, u32[]{:S(2)}) copy-start(f32[4,2048]{1,0:T(4,128)} %param.16) | copy-start | bytes 98308
  37.5 141.6 %all-reduce.8.cloned.1.call-start = ((), (), s32[]{:S(2)}) async-start(), calls=%async_computation.4 | async-start | bytes 2097152 | tf_op jit(solution)/shard_map/psum | solution.py:128
  125.5 5.0 %collective-permute-start.1 = (bf16[3,2048]{1,0:T(4,128)(2,1)S(1)}, bf16[3,2048]{1,0:T(4,128)(2,1)S(1)}, u32[]{:S(2)}, u32[]{:S(2)}) collective-permute-start(bf16[3,2048]{1,0:T(4,128)(2,1)S(1)} %slice.101), channel_id=1, source_target_pairs={{0,4},{4,8},{8,12},{12,16},{16,20},{20,24},{24,28},{1,5},{5,9},{9,... | collective-permute-start | bytes 36872 | tf_op jit(solution)/shard_map/ppermute | solution.py:13
  131.7 1.7 copy-start.7
  132.4 1.0 copy-start.4
  133.4 9.7 %copy-start.8 = (f32[32]{0:T(128)S(1)}, f32[32]{0:T(128)}, u32[]{:S(2)}) copy-start(f32[32]{0:T(128)} %param.20) | copy-start | bytes 388
  133.4 9.7 %copy-start.9 = (s32[128]{0:T(128)S(1)}, s32[128]{0:T(128)}, u32[]{:S(2)}) copy-start(s32[128]{0:T(128)} %param.19) | copy-start | bytes 1540
  142.9 153.4 %reduce-scatter.5.cloned.1.call-start = ((), (), s32[]{:S(2)}) async-start(), calls=%async_computation.5 | async-start | bytes 1310720 | tf_op jit(solution)/shard_map/reduce_scatter | solution.py:162
  193.1 1.2 copy-start.3
  194.4 5.8 %collective-permute-start.2 = (f32[3,2048]{1,0:T(4,128)S(1)}, f32[3,2048]{1,0:T(4,128)S(1)}, u32[]{:S(2)}, u32[]{:S(2)}) collective-permute-start(f32[3,2048]{1,0:T(4,128)S(1)} %slice_add_fusion), channel_id=1, source_target_pairs={{4,0},{8,4},{12,8},{16,12},{20,16},{24,20},{28,24},{5,1},{9,5},{13... | collective-permute-start | bytes 73736 | tf_op jit(solution)/shard_map/ppermute | solution.py:13
  200.6 6.8 %collective-permute-start.10 = (bf16[128,1024]{1,0:T(8,128)(2,1)S(1)}, bf16[128,1024]{1,0:T(8,128)(2,1)S(1)}, u32[]{:S(2)}, u32[]{:S(2)}) collective-permute-start(bf16[128,1024]{1,0:T(8,128)(2,1)S(1)} %get-tuple-element.25), channel_id=1, source_target_pairs={{8,0},{16,8},{24,16},{28,24},{20,28},{12,20},{4,12},{0,4},{9,1},{1... | collective-permute-start | bytes 786440 | tf_op jit(solution)/shard_map/ppermute | solution.py:70
  203.1 7.5 %collective-permute-start.3 = (bf16[128,1024]{1,0:T(8,128)(2,1)S(1)}, bf16[128,1024]{1,0:T(8,128)(2,1)S(1)}, u32[]{:S(2)}, u32[]{:S(2)}) collective-permute-start(bf16[128,1024]{1,0:T(8,128)(2,1)S(1)} %get-tuple-element.24), channel_id=1, source_target_pairs={{0,8},{8,16},{16,24},{24,28},{28,20},{20,12},{12,4},{4,0},{1,9},{9... | collective-permute-start | bytes 786440 | tf_op jit(solution)/shard_map/ppermute | solution.py:69
  207.4 7.1 %collective-permute-start.11 = (bf16[128,1024]{1,0:T(8,128)(2,1)S(1)}, bf16[128,1024]{1,0:T(8,128)(2,1)S(1)}, u32[]{:S(2)}, u32[]{:S(2)}) collective-permute-start(bf16[128,1024]{1,0:T(8,128)(2,1)S(1)} %collective-permute-done.10), channel_id=1, source_target_pairs={{8,0},{16,8},{24,16},{28,24},{20,28},{12,20},{4,12},{0,4},{9,1},{1... | collective-permute-start | bytes 786440 | tf_op jit(solution)/shard_map/ppermute | solution.py:70
  210.5 7.2 %collective-permute-start.4 = (bf16[128,1024]{1,0:T(8,128)(2,1)S(1)}, bf16[128,1024]{1,0:T(8,128)(2,1)S(1)}, u32[]{:S(2)}, u32[]{:S(2)}) collective-permute-start(bf16[128,1024]{1,0:T(8,128)(2,1)S(1)} %collective-permute-done.3), channel_id=1, source_target_pairs={{0,8},{8,16},{16,24},{24,28},{28,20},{20,12},{12,4},{4,0},{1,9},{9... | collective-permute-start | bytes 786440 | tf_op jit(solution)/shard_map/ppermute | solution.py:69
  214.6 8.1 %collective-permute-start.12 = (bf16[128,1024]{1,0:T(8,128)(2,1)S(1)}, bf16[128,1024]{1,0:T(8,128)(2,1)S(1)}, u32[]{:S(2)}, u32[]{:S(2)}) collective-permute-start(bf16[128,1024]{1,0:T(8,128)(2,1)S(1)} %collective-permute-done.11), channel_id=1, source_target_pairs={{8,0},{16,8},{24,16},{28,24},{20,28},{12,20},{4,12},{0,4},{9,1},{1... | collective-permute-start | bytes 786440 | tf_op jit(solution)/shard_map/ppermute | solution.py:70
  217.8 8.1 %collective-permute-start.5 = (bf16[128,1024]{1,0:T(8,128)(2,1)S(1)}, bf16[128,1024]{1,0:T(8,128)(2,1)S(1)}, u32[]{:S(2)}, u32[]{:S(2)}) collective-permute-start(bf16[128,1024]{1,0:T(8,128)(2,1)S(1)} %collective-permute-done.4), channel_id=1, source_target_pairs={{0,8},{8,16},{16,24},{24,28},{28,20},{20,12},{12,4},{4,0},{1,9},{9... | collective-permute-start | bytes 786440 | tf_op jit(solution)/shard_map/ppermute | solution.py:69
  222.6 8.9 %collective-permute-start.13 = (bf16[128,1024]{1,0:T(8,128)(2,1)S(1)}, bf16[128,1024]{1,0:T(8,128)(2,1)S(1)}, u32[]{:S(2)}, u32[]{:S(2)}) collective-permute-start(bf16[128,1024]{1,0:T(8,128)(2,1)S(1)} %collective-permute-done.12), channel_id=1, source_target_pairs={{8,0},{16,8},{24,16},{28,24},{20,28},{12,20},{4,12},{0,4},{9,1},{1... | collective-permute-start | bytes 786440 | tf_op jit(solution)/shard_map/ppermute | solution.py:70
  225.8 8.9 %collective-permute-start.6 = (bf16[128,1024]{1,0:T(8,128)(2,1)S(1)}, bf16[128,1024]{1,0:T(8,128)(2,1)S(1)}, u32[]{:S(2)}, u32[]{:S(2)}) collective-permute-start(bf16[128,1024]{1,0:T(8,128)(2,1)S(1)} %collective-permute-done.5), channel_id=1, source_target_pairs={{0,8},{8,16},{16,24},{24,28},{28,20},{20,12},{12,4},{4,0},{1,9},{9... | collective-permute-start | bytes 786440 | tf_op jit(solution)/shard_map/ppermute | solution.py:69
  231.5 8.6 %collective-permute-start.14 = (bf16[128,1024]{1,0:T(8,128)(2,1)S(1)}, bf16[128,1024]{1,0:T(8,128)(2,1)S(1)}, u32[]{:S(2)}, u32[]{:S(2)}) collective-permute-start(bf16[128,1024]{1,0:T(8,128)(2,1)S(1)} %collective-permute-done.13), channel_id=1, source_target_pairs={{8,0},{16,8},{24,16},{28,24},{20,28},{12,20},{4,12},{0,4},{9,1},{1... | collective-permute-start | bytes 786440 | tf_op jit(solution)/shard_map/ppermute | solution.py:70
  234.8 8.6 %collective-permute-start.7 = (bf16[128,1024]{1,0:T(8,128)(2,1)S(1)}, bf16[128,1024]{1,0:T(8,128)(2,1)S(1)}, u32[]{:S(2)}, u32[]{:S(2)}) collective-permute-start(bf16[128,1024]{1,0:T(8,128)(2,1)S(1)} %collective-permute-done.6), channel_id=1, source_target_pairs={{0,8},{8,16},{16,24},{24,28},{28,20},{20,12},{12,4},{4,0},{1,9},{9... | collective-permute-start | bytes 786440 | tf_op jit(solution)/shard_map/ppermute | solution.py:69
  240.2 7.7 %collective-permute-start.15 = (bf16[128,1024]{1,0:T(8,128)(2,1)S(1)}, bf16[128,1024]{1,0:T(8,128)(2,1)S(1)}, u32[]{:S(2)}, u32[]{:S(2)}) collective-permute-start(bf16[128,1024]{1,0:T(8,128)(2,1)S(1)} %collective-permute-done.14), channel_id=1, source_target_pairs={{8,0},{16,8},{24,16},{28,24},{20,28},{12,20},{4,12},{0,4},{9,1},{1... | collective-permute-start | bytes 786440 | tf_op jit(solution)/shard_map/ppermute | solution.py:70
  243.3 7.8 %collective-permute-start.8 = (bf16[128,1024]{1,0:T(8,128)(2,1)S(1)}, bf16[128,1024]{1,0:T(8,128)(2,1)S(1)}, u32[]{:S(2)}, u32[]{:S(2)}) collective-permute-start(bf16[128,1024]{1,0:T(8,128)(2,1)S(1)} %collective-permute-done.7), channel_id=1, source_target_pairs={{0,8},{8,16},{16,24},{24,28},{28,20},{20,12},{12,4},{4,0},{1,9},{9... | collective-permute-start | bytes 786440 | tf_op jit(solution)/shard_map/ppermute | solution.py:69
  247.9 6.4 %collective-permute-start.16 = (bf16[128,1024]{1,0:T(8,128)(2,1)S(1)}, bf16[128,1024]{1,0:T(8,128)(2,1)S(1)}, u32[]{:S(2)}, u32[]{:S(2)}) collective-permute-start(bf16[128,1024]{1,0:T(8,128)(2,1)S(1)} %collective-permute-done.15), channel_id=1, source_target_pairs={{8,0},{16,8},{24,16},{28,24},{20,28},{12,20},{4,12},{0,4},{9,1},{1... | collective-permute-start | bytes 786440 | tf_op jit(solution)/shard_map/ppermute | solution.py:70
  251.1 10.7 %collective-permute-start.9 = (bf16[128,1024]{1,0:T(8,128)(2,1)S(1)}, bf16[128,1024]{1,0:T(8,128)(2,1)S(1)}, u32[]{:S(2)}, u32[]{:S(2)}) collective-permute-start(bf16[128,1024]{1,0:T(8,128)(2,1)S(1)} %collective-permute-done.8), channel_id=1, source_target_pairs={{0,8},{8,16},{16,24},{24,28},{28,20},{20,12},{12,4},{4,0},{1,9},{9... | collective-permute-start | bytes 786440 | tf_op jit(solution)/shard_map/ppermute | solution.py:69
  266.1 2.2 copy-start.2
  297.3 17.0 %collective-permute-start.19 = (bf16[128,512]{1,0:T(8,128)(2,1)S(1)}, bf16[128,512]{1,0:T(8,128)(2,1)S(1)}, u32[]{:S(2)}, u32[]{:S(2)}) collective-permute-start(bf16[128,512]{1,0:T(8,128)(2,1)S(1)} %get-tuple-element.29), channel_id=1, source_target_pairs={{4,4},{5,12},{6,20},{7,28},{12,5},{13,13},{14,21},{15,29},{20,6},{... | collective-permute-start | bytes 393224 | tf_op jit(solution)/shard_map/ppermute | solution.py:45
  298.0 18.4 %collective-permute-start.20 = (bf16[128,512]{1,0:T(8,128)(2,1)S(1)}, bf16[128,512]{1,0:T(8,128)(2,1)S(1)}, u32[]{:S(2)}, u32[]{:S(2)}) collective-permute-start(bf16[128,512]{1,0:T(8,128)(2,1)S(1)} %get-tuple-element.28), channel_id=1, source_target_pairs={{4,0},{5,8},{6,16},{7,24},{12,1},{13,9},{14,17},{15,25},{20,2},{21... | collective-permute-start | bytes 393224 | tf_op jit(solution)/shard_map/ppermute | solution.py:45
  300.9 15.4 %collective-permute-start.17 = (bf16[128,512]{1,0:T(8,128)(2,1)S(1)}, bf16[128,512]{1,0:T(8,128)(2,1)S(1)}, u32[]{:S(2)}, u32[]{:S(2)}) collective-permute-start(bf16[128,512]{1,0:T(8,128)(2,1)S(1)} %get-tuple-element.29), channel_id=1, source_target_pairs={{0,4},{1,12},{2,20},{3,28},{8,5},{9,13},{10,21},{11,29},{16,6},{17... | collective-permute-start | bytes 393224 | tf_op jit(solution)/shard_map/ppermute | solution.py:45
  309.1 14.2 %collective-permute-start.18 = (bf16[128,512]{1,0:T(8,128)(2,1)S(1)}, bf16[128,512]{1,0:T(8,128)(2,1)S(1)}, u32[]{:S(2)}, u32[]{:S(2)}) collective-permute-start(bf16[128,512]{1,0:T(8,128)(2,1)S(1)} %get-tuple-element.28), channel_id=1, source_target_pairs={{0,0},{1,8},{2,16},{3,24},{8,1},{9,9},{10,17},{11,25},{16,2},{17,1... | collective-permute-start | bytes 393224 | tf_op jit(solution)/shard_map/ppermute | solution.py:45
Sparse Core Ops, SparseCore 0:
  37.6 87.0 reduce-scatter.2
  143.0 36.0 all-reduce.7
  272.3 23.9 reduce-scatter.4

commit v4 on v3

--- a/solution.py
+++ b/solution.py
@@ -56,12 +56,17 @@
     return list(range(0, count, 2)) + list(range(count - 1, 0, -2))
 
 
-def ring_gather(value, axis):
+def ring_place(axis):
     count = lax.axis_size(axis)
     order = ring_order(count)
     place = jnp.array([order.index(i) for i in range(count)], jnp.int32)[lax.axis_index(axis)]
     ahead = [(order[i], order[(i + 1) % count]) for i in range(count)]
     behind = [(order[(i + 1) % count], order[i]) for i in range(count)]
+    return count, jnp.array(order, jnp.int32), place, ahead, behind
+
+
+def ring_gather(value, axis):
+    count, order, place, ahead, behind = ring_place(axis)
     half = value.shape[1] // 2
     sent_a, sent_b = value[:, :half], value[:, half:]
     got_a, got_b = [sent_a], [sent_b]
@@ -70,16 +75,30 @@
         sent_b = lax.ppermute(sent_b, axis, behind)
         got_a.append(sent_a)
         got_b.append(sent_b)
+    got_b = [got_b[(count - s) % count] for s in range(count)]
+    sources = order[(place - jnp.arange(count)) % count]
+    return jnp.stack(got_a), jnp.stack(got_b), sources
+
+
+def ring_reduce_scatter(token_cols, weight, axis):
+    count, order, place, ahead, behind = ring_place(axis)
+    rows = token_cols.shape[0] // count
+    blocks = token_cols.reshape(count, rows, token_cols.shape[1])
+    half = weight.shape[1] // 2
     steps = jnp.arange(count)
-    order_arr = jnp.array(order, jnp.int32)
-    from_a = jnp.argsort(order_arr[(place - steps) % count])
-    from_b = jnp.argsort(order_arr[(place + steps) % count])
-    gathered_a = jnp.take(jnp.stack(got_a), from_a, axis=0)
-    gathered_b = jnp.take(jnp.stack(got_b), from_b, axis=0)
-    return jnp.concatenate([gathered_a, gathered_b], axis=2).reshape(
-        count * value.shape[0], value.shape[1]
-    )
-
+    first = jnp.take(blocks, order[(place - 1 - steps) % count], axis=0).reshape(token_cols.shape)
+    second = jnp.take(blocks, order[(place + 1 + steps) % count], axis=0).reshape(token_cols.shape)
+    own_a = jnp.dot(first, weight[:, :half], preferred_element_type=jnp.float32)
+    own_b = jnp.dot(second, weight[:, half:], preferred_element_type=jnp.float32)
+    own_a = own_a.reshape(count, rows, half)
+    own_b = own_b.reshape(count, rows, weight.shape[1] - half)
+    sum_a, sum_b = own_a[0].astype(jnp.bfloat16), own_b[0].astype(jnp.bfloat16)
+    for s in range(1, count):
+        sum_a = lax.ppermute(sum_a, axis, ahead)
+        sum_b = lax.ppermute(sum_b, axis, behind)
+        sum_a = (sum_a.astype(jnp.float32) + own_a[s]).astype(jnp.bfloat16)
+        sum_b = (sum_b.astype(jnp.float32) + own_b[s]).astype(jnp.bfloat16)
+    return jnp.concatenate([sum_a, sum_b], axis=1)
 
 def silu_grad(argument):
     sigmoid_v = jax.nn.sigmoid(argument)
@@ -97,9 +116,7 @@
         and lax.axis_size("row") % lax.axis_size("col") == 0
     )
     if moves_tokens:
-        token_cols = fetched_columns(tokens)
-        part_x = jnp.dot(token_cols, in_weight, preferred_element_type=jnp.float32)
-        inner_x = lax.psum_scatter(part_x.astype(jnp.bfloat16), "row", scatter_dimension=0, tiled=True)
+        inner_x = ring_reduce_scatter(fetched_columns(tokens), in_weight, "row")
     else:
         full_in = lax.all_gather(in_weight, "row", axis=0, tiled=True)
         inner_x = jnp.dot(tokens, full_in, preferred_element_type=jnp.float32).astype(jnp.bfloat16)
@@ -155,12 +172,15 @@
         )
     ).astype(jnp.bfloat16)
     if moves_tokens:
-        grad_x_all = ring_gather(grad_x, "row")
+        got_a, got_b, sources = ring_gather(grad_x, "row")
+        half = grad_x.shape[1] // 2
+        contract = (((2,), (1,)), ((), ()))
         grad_cols = lax.dot_general(
-            grad_x_all, in_weight, (((1,), (1,)), ((), ())), preferred_element_type=jnp.float32
-        )
+            got_a, in_weight[:, :half], contract, preferred_element_type=jnp.float32
+        ) + lax.dot_general(got_b, in_weight[:, half:], contract, preferred_element_type=jnp.float32)
+        grad_cols = jnp.take(grad_cols.astype(jnp.bfloat16), jnp.argsort(sources), axis=0)
         grad_sum = lax.psum_scatter(
-            grad_cols.astype(jnp.bfloat16), "col", scatter_dimension=0, tiled=True
+            grad_cols.reshape(-1, grad_cols.shape[2]), "col", scatter_dimension=0, tiled=True
         )
         grad_tokens = placed_blocks(grad_sum, row_count)
     else:

time: 331 us -> 301 us (0.909)
  blocking collectives: 20.2 us -> 0 us
  waiting for transfers between devices: 185 us -> 167 us
  starting transfers between devices: 37.7 us -> 54.1 us
  local copies, waits for them, and re-layouts: 29.4 us -> 22.6 us
  matrix products: 31.1 us -> 27 us
    reduce_scatter x2 -> x1, waiting for transfers between devices: 107 us -> 24.2 us  [shards(): lax.psum_scatter(grad_cols.reshape(-1, grad_cols.shape[2]), 'col', scatte...]
    ppermute x0 -> x14, waiting for transfers between devices: none -> 39.6 us  [the longest x7 27 us: ring_reduce_scatter(): sum_a = lax.ppermute(sum_a, axis, ahead)]
    all_to_all x1 -> x0, blocking collectives: 20.2 us -> none  [fetched_columns(): mine = lax.all_to_all(mine, 'row', 1, 0, tiled=True)]
    ppermute x0 -> x14, starting transfers between devices: none -> 14.7 us  [the longest x7 10.5 us: ring_reduce_scatter(): sum_b = lax.ppermute(sum_b, axis, behind)]
    ppermute x7, waiting for transfers between devices: 26.8 us -> 37.3 us  [ring_gather(): sent_b = lax.ppermute(sent_b, axis, behind)]
    all_to_all x0 -> x1, waiting for transfers between devices: none -> 8.87 us  [fetched_columns(): mine = lax.all_to_all(mine, 'row', 1, 0, tiled=True)]
    all_to_all x0 -> x1, starting transfers between devices: none -> 5.83 us  [fetched_columns(): mine = lax.all_to_all(mine, 'row', 1, 0, tiled=True)]
    ppermute x7, starting transfers between devices: 17.2 us -> 11.6 us  [ring_gather(): sent_b = lax.ppermute(sent_b, axis, behind)]
  transfers between devices with their start and end apart: 24 -> 38, of which waited for: 14 -> 32; matrix products, arithmetic and copies ran while one was open for 7% -> 5% of each run, Pallas kernels for 0% -> 0%
where the time goes in v4:
time: 301 us; the launch traced here: 300 us
  waiting for transfers between devices  167 us (55%)
  starting transfers between devices  54.1 us (18%)
  matrix products  27 us (9%)
  local copies, waits for them, and re-layouts  22.6 us (8%)
  between operations  16 us (5%)
  other arithmetic  12.9 us (4%)
    ppermute x7, waiting for transfers between devices, ring_gather(): sent_b = lax.ppermute(sent_b, axis, behind)  37.3 us
    psum x1, waiting for transfers between devices, shards(): lax.psum(partial_value.astype(jnp.bfloat16), 'col').astype(jnp.float32)  37.2 us
    ppermute x7, waiting for transfers between devices, ring_reduce_scatter(): sum_a = lax.ppermute(sum_a, axis, ahead)  27 us
    reduce_scatter x1, waiting for transfers between devices, shards(): lax.psum_scatter(grad_cols.reshape(-1, grad_cols.shape[2]), 'col', scatte...  24.2 us
    ppermute x4, starting transfers between devices, placed_blocks(): lax.ppermute(grad_sum[k * row_count:(k + 1) * row_count], ('row', 'col'),...  15.3 us
    ppermute x7, waiting for transfers between devices, ring_reduce_scatter(): sum_b = lax.ppermute(sum_b, axis, behind)  12.7 us
    dot_general x1, matrix products, shards(): lax.dot_general(residual_grad, out_weight, (((1,), (1,)), ((), ())), pref...  12.6 us
    ppermute x7, starting transfers between devices, ring_gather(): sent_b = lax.ppermute(sent_b, axis, behind)  11.6 us
  transfers between devices with their start and end apart: 38, of which 32 were waited for; matrix products, arithmetic and copies ran while one was open for 5% of the time, Pallas kernels for 0%

profile of v4, /device:TPU:2, one launch (start us, length us, event | category | flops | bytes accessed | tf_op | source)
XLA Modules:
  0.0 300.1 jit_solution(13545205715410552707)
XLA Ops:
  7.2 1.6 copy.49
  10.0 5.8 %all-to-all-start = ((bf16[128,8,256]{2,0,1:T(8,128)(2,1)}), bf16[128,8,256]{2,0,1:T(8,128)(2,1)S(1)}, u32[]{:S(2)}, u32[]{:S(2)}) async-start(bf16[128,8,256]{2,0,1:T(8,128)(2,1)} %copy.51), calls=%async_computation | async-start | bytes 1048576 | tf_op jit(solution)/shard_map/all_to_all | solution.py:24
  21.4 8.9 %all-to-all-done = bf16[128,8,256]{2,0,1:T(8,128)(2,1)S(1)} async-done(((bf16[128,8,256]{2,0,1:T(8,128)(2,1)}), bf16[128,8,256]{2,0,1:T(8,128)(2,1)S(1)}, u32[]{:S(2)}, u32[]{:S(2)}) %all-to-all-start) | async-done | bytes 524320 | tf_op jit(solution)/shard_map/all_to_all | solution.py:24
  30.3 1.9 collective-permute-done
  33.3 1.4 copy-done.10
  34.7 1.3 fusion.21
  36.1 1.9 copy-done.4
  38.0 1.5 collective-permute-start.8
  40.3 1.4 copy-done.11
  41.7 1.3 fusion.24
  43.7 2.6 collective-permute-done.8
  46.4 1.5 collective-permute-start.9
  47.9 3.2 %collective-permute-done.1 = bf16[128,1024]{0,1:T(8,128)(2,1)S(1)} collective-permute-done((bf16[128,1024]{0,1:T(8,128)(2,1)S(1)}, bf16[128,1024]{0,1:T(8,128)(2,1)S(1)}, u32[]{:S(2)}, u32[]{:S(2)}) %collective-permute-start.1) | collective-permute-done | bytes 262176 | tf_op jit(solution)/shard_map/ppermute | solution.py:97
  51.9 2.1 collective-permute-done.9
  54.1 1.5 collective-permute-start.10
  55.6 2.9 collective-permute-done.2
  59.2 1.5 collective-permute-done.10
  60.8 1.5 collective-permute-start.11
  62.3 3.0 collective-permute-done.3
  66.0 1.8 collective-permute-done.11
  67.9 1.5 collective-permute-start.12
  69.4 3.5 %collective-permute-done.4 = bf16[128,1024]{0,1:T(8,128)(2,1)S(1)} collective-permute-done((bf16[128,1024]{0,1:T(8,128)(2,1)S(1)}, bf16[128,1024]{0,1:T(8,128)(2,1)S(1)}, u32[]{:S(2)}, u32[]{:S(2)}) %collective-permute-start.4) | collective-permute-done | bytes 262176 | tf_op jit(solution)/shard_map/ppermute | solution.py:97
  73.6 2.1 collective-permute-done.12
  75.8 1.5 collective-permute-start.13
  77.3 4.1 %collective-permute-done.5 = bf16[128,1024]{0,1:T(8,128)(2,1)S(1)} collective-permute-done((bf16[128,1024]{0,1:T(8,128)(2,1)S(1)}, bf16[128,1024]{0,1:T(8,128)(2,1)S(1)}, u32[]{:S(2)}, u32[]{:S(2)}) %collective-permute-start.5) | collective-permute-done | bytes 262176 | tf_op jit(solution)/shard_map/ppermute | solution.py:97
  82.1 2.5 collective-permute-done.13
  84.6 1.5 collective-permute-start.14
  86.2 4.6 %collective-permute-done.6 = bf16[128,1024]{0,1:T(8,128)(2,1)S(1)} collective-permute-done((bf16[128,1024]{0,1:T(8,128)(2,1)S(1)}, bf16[128,1024]{0,1:T(8,128)(2,1)S(1)}, u32[]{:S(2)}, u32[]{:S(2)}) %collective-permute-start.6) | collective-permute-done | bytes 262176 | tf_op jit(solution)/shard_map/ppermute | solution.py:97
  91.5 5.7 %collective-permute-done.7 = bf16[128,1024]{0,1:T(8,128)(2,1)S(1)} collective-permute-done((bf16[128,1024]{0,1:T(8,128)(2,1)S(1)}, bf16[128,1024]{0,1:T(8,128)(2,1)S(1)}, u32[]{:S(2)}, u32[]{:S(2)}) %collective-permute-start.7) | collective-permute-done | bytes 262176 | tf_op jit(solution)/shard_map/ppermute | solution.py:97
  97.5 1.5 collective-permute-start.15
  99.3 6.3 %collective-permute-done.15 = bf16[3,2048]{0,1:T(8,128)(2,1)S(1)} collective-permute-done((bf16[3,2048]{0,1:T(8,128)(2,1)S(1)}, bf16[3,2048]{0,1:T(8,128)(2,1)S(1)}, u32[]{:S(2)}, u32[]{:S(2)}) %collective-permute-start.15) | collective-permute-done | bytes 12320 | tf_op jit(solution)/shard_map/ppermute | solution.py:13
  106.1 2.2 fusion.9
  108.4 9.2 %convolution_convert_fusion = bf16[128,4096]{1,0:T(8,128)(2,1)} fusion(bf16[2048,4096]{1,0:T(8,128)(2,1)} %param.19, bf16[128,2048]{0,1:T(8,128)(2,1)S(1)} %copy.52, f32[128,2048]{0,1:T(8,128)S(1)} %fusion.9), kind=kOutput, calls=%fused_computation.6 | convolution fusion | flops 2150891520 | bytes 19398656 | tf_op jit(solution)/shard_map/dot_general | solution.py:138
  118.0 37.2 %all-reduce.8.cloned.1.call-done = bf16[128,4096]{1,0:T(8,128)(2,1)} async-done(((bf16[128,4096]{1,0:T(8,128)(2,1)}), bf16[128,4096]{1,0:T(8,128)(2,1)}) %all-reduce.8.cloned.1.call-update) | async-done | bytes 1048592 | tf_op jit(solution)/shard_map/psum | solution.py:145
  155.2 12.6 %multiply_multiply_fusion.2 = (f32[128,2048]{0,1:T(8,128)S(1)}, f32[128,2048]{0,1:T(8,128)S(1)}, bf16[128,2048]{0,1:T(8,128)(2,1)}) fusion(f32[128]{0:T(128)S(1)} %get-tuple-element.48, f32[2048]{0:T(1024)S(1)} %bitcast.85, f32[128,2048]{0,1:T(8,128)S(1)} %fusion.9, bf16[128,2048]{0,1:T(8,128)(2,1)S(1)} %copy.52, bf16[2048,4096]{1,0:T(8,128)(2,1)} %param.19, ...), kind=kOutput, calls=%fused_computation.40 | convolution fusion | flops 2156396544 | bytes 23077888 | tf_op jit(solution)/shard_map/dot_general | solution.py:148
  168.7 1.6 slice_add_fusion
  170.3 1.6 copy.54
  171.9 1.4 collective-permute-start.16
  173.3 1.3 slice.219
  175.0 1.3 slice.217
  176.3 1.5 collective-permute-done.16
  177.8 1.3 copy.55
  179.2 2.1 add_convert_fusion.1
  181.4 2.4 collective-permute-start.24
  183.8 5.6 %collective-permute-done.24 = bf16[128,1024]{0,1:T(8,128)(2,1)S(1)} collective-permute-done((bf16[128,1024]{0,1:T(8,128)(2,1)S(1)}, bf16[128,1024]{0,1:T(8,128)(2,1)S(1)}, u32[]{:S(2)}, u32[]{:S(2)}) %collective-permute-start.24) | collective-permute-done | bytes 262176 | tf_op jit(solution)/shard_map/ppermute | solution.py:75
  191.4 5.0 %collective-permute-done.25 = bf16[128,1024]{0,1:T(8,128)(2,1)S(1)} collective-permute-done((bf16[128,1024]{0,1:T(8,128)(2,1)S(1)}, bf16[128,1024]{0,1:T(8,128)(2,1)S(1)}, u32[]{:S(2)}, u32[]{:S(2)}) %collective-permute-start.25) | collective-permute-done | bytes 262176 | tf_op jit(solution)/shard_map/ppermute | solution.py:75
  196.9 1.5 collective-permute-start.19
  198.4 4.9 %collective-permute-done.26 = bf16[128,1024]{0,1:T(8,128)(2,1)S(1)} collective-permute-done((bf16[128,1024]{0,1:T(8,128)(2,1)S(1)}, bf16[128,1024]{0,1:T(8,128)(2,1)S(1)}, u32[]{:S(2)}, u32[]{:S(2)}) %collective-permute-start.26) | collective-permute-done | bytes 262176 | tf_op jit(solution)/shard_map/ppermute | solution.py:75
  203.3 1.9 collective-permute-start.27
  205.5 6.4 %collective-permute-done.27 = bf16[128,1024]{0,1:T(8,128)(2,1)S(1)} collective-permute-done((bf16[128,1024]{0,1:T(8,128)(2,1)S(1)}, bf16[128,1024]{0,1:T(8,128)(2,1)S(1)}, u32[]{:S(2)}, u32[]{:S(2)}) %collective-permute-start.27) | collective-permute-done | bytes 262176 | tf_op jit(solution)/shard_map/ppermute | solution.py:75
  211.8 2.5 collective-permute-start.28
  214.9 5.9 %collective-permute-done.28 = bf16[128,1024]{0,1:T(8,128)(2,1)S(1)} collective-permute-done((bf16[128,1024]{0,1:T(8,128)(2,1)S(1)}, bf16[128,1024]{0,1:T(8,128)(2,1)S(1)}, u32[]{:S(2)}, u32[]{:S(2)}) %collective-permute-start.28) | collective-permute-done | bytes 262176 | tf_op jit(solution)/shard_map/ppermute | solution.py:75
  220.8 1.9 collective-permute-start.29
  223.4 5.5 %collective-permute-done.29 = bf16[128,1024]{0,1:T(8,128)(2,1)S(1)} collective-permute-done((bf16[128,1024]{0,1:T(8,128)(2,1)S(1)}, bf16[128,1024]{0,1:T(8,128)(2,1)S(1)}, u32[]{:S(2)}, u32[]{:S(2)}) %collective-permute-start.29) | collective-permute-done | bytes 262176 | tf_op jit(solution)/shard_map/ppermute | solution.py:75
  229.0 1.3 collective-permute-start.30
  231.4 4.0 %collective-permute-done.30 = bf16[128,1024]{0,1:T(8,128)(2,1)S(1)} collective-permute-done((bf16[128,1024]{0,1:T(8,128)(2,1)S(1)}, bf16[128,1024]{0,1:T(8,128)(2,1)S(1)}, u32[]{:S(2)}, u32[]{:S(2)}) %collective-permute-start.30) | collective-permute-done | bytes 262176 | tf_op jit(solution)/shard_map/ppermute | solution.py:75
  235.7 1.3 fusion.15
  237.1 1.3 add_convert_fusion
  240.2 24.2 %reduce-scatter.2.cloned.1.call-done = bf16[256,512]{1,0:T(8,128)(2,1)} async-done(((bf16[1024,512]{1,0:T(8,128)(2,1)}), bf16[256,512]{1,0:T(8,128)(2,1)}) %reduce-scatter.2.cloned.1.call-update) | async-done | bytes 262160 | tf_op jit(solution)/shard_map/reduce_scatter | solution.py:182
  266.2 1.3 collective-permute-start.34
  268.5 1.7 dynamic-slice_convert_fusion
  270.2 8.1 %collective-permute-start.31 = (bf16[128,512]{1,0:T(8,128)(2,1)S(1)}, bf16[128,512]{1,0:T(8,128)(2,1)S(1)}, u32[]{:S(2)}, u32[]{:S(2)}) collective-permute-start(bf16[128,512]{1,0:T(8,128)(2,1)S(1)} %get-tuple-element.42), channel_id=1, source_target_pairs={{0,4},{1,12},{2,20},{3,28},{8,5},{9,13},{10,21},{11,29},{16,6},{17... | collective-permute-start | bytes 393224 | tf_op jit(solution)/shard_map/ppermute | solution.py:45
  278.3 5.2 %collective-permute-start.32 = (bf16[128,512]{1,0:T(8,128)(2,1)S(1)}, bf16[128,512]{1,0:T(8,128)(2,1)S(1)}, u32[]{:S(2)}, u32[]{:S(2)}) collective-permute-start(bf16[128,512]{1,0:T(8,128)(2,1)S(1)} %get-tuple-element.41), channel_id=1, source_target_pairs={{0,0},{1,8},{2,16},{3,24},{8,1},{9,9},{10,17},{11,25},{16,2},{17,1... | collective-permute-start | bytes 393224 | tf_op jit(solution)/shard_map/ppermute | solution.py:45
  284.6 7.9 %collective-permute-done.32 = bf16[128,512]{1,0:T(8,128)(2,1)S(1)} collective-permute-done((bf16[128,512]{1,0:T(8,128)(2,1)S(1)}, bf16[128,512]{1,0:T(8,128)(2,1)S(1)}, u32[]{:S(2)}, u32[]{:S(2)}) %collective-permute-start.32) | collective-permute-done | bytes 131104 | tf_op jit(solution)/shard_map/ppermute | solution.py:45
  (134 shorter events, 27.3 us)
Async XLA Ops:
  8.8 7.0 %copy-start.15 = (s32[8]{0:T(128)S(1)}, s32[8]{0:T(128)}, u32[]{:S(2)}) copy-start(s32[8]{0:T(128)} %constant.110.clone) | copy-start | bytes 100
  8.9 8.9 %copy-start = (s32[8]{0:T(128)S(1)}, s32[8]{0:T(128)}, u32[]{:S(2)}) copy-start(s32[8]{0:T(128)} %constant.111.clone) | copy-start | bytes 100
  10.0 20.3 %all-to-all-start = ((bf16[128,8,256]{2,0,1:T(8,128)(2,1)}), bf16[128,8,256]{2,0,1:T(8,128)(2,1)S(1)}, u32[]{:S(2)}, u32[]{:S(2)}) async-start(bf16[128,8,256]{2,0,1:T(8,128)(2,1)} %copy.51), calls=%async_computation | async-start | bytes 1048576 | tf_op jit(solution)/shard_map/all_to_all | solution.py:24
  15.8 139.4 %all-reduce.8.cloned.1.call-start = ((), (), s32[]{:S(2)}) async-start(), calls=%async_computation.2 | async-start | bytes 2097152 | tf_op jit(solution)/shard_map/psum | solution.py:145
  30.3 1.9 collective-permute-start
  33.1 1.6 copy-start.10
  36.0 2.0 copy-start.4
  38.0 8.3 %collective-permute-start.8 = (bf16[128,1024]{0,1:T(8,128)(2,1)S(1)}, bf16[128,1024]{0,1:T(8,128)(2,1)S(1)}, u32[]{:S(2)}, u32[]{:S(2)}) collective-permute-start(bf16[128,1024]{0,1:T(8,128)(2,1)S(1)} %slice.310), channel_id=1, source_target_pairs={{8,0},{16,8},{24,16},{28,24},{20,28},{12,20},{4,12},{0,4},{9,1},{1... | collective-permute-start | bytes 786440 | tf_op jit(solution)/shard_map/ppermute | solution.py:98
  40.1 1.6 copy-start.11
  41.7 4.7 %copy-start.5 = (f32[1024,1024]{0,1:T(8,128)S(1)}, f32[1024,1024]{0,1:T(8,128)}, u32[]{:S(2)}) copy-start(f32[1024,1024]{0,1:T(8,128)} %copy-done.4) | copy-start | bytes 12582916
  43.1 8.1 %collective-permute-start.1 = (bf16[128,1024]{0,1:T(8,128)(2,1)S(1)}, bf16[128,1024]{0,1:T(8,128)(2,1)S(1)}, u32[]{:S(2)}, u32[]{:S(2)}) collective-permute-start(bf16[128,1024]{0,1:T(8,128)(2,1)S(1)} %slice.311), channel_id=1, source_target_pairs={{0,8},{8,16},{16,24},{24,28},{28,20},{20,12},{12,4},{4,0},{1,9},{9... | collective-permute-start | bytes 786440 | tf_op jit(solution)/shard_map/ppermute | solution.py:97
  46.4 7.6 %collective-permute-start.9 = (bf16[128,1024]{0,1:T(8,128)(2,1)S(1)}, bf16[128,1024]{0,1:T(8,128)(2,1)S(1)}, u32[]{:S(2)}, u32[]{:S(2)}) collective-permute-start(bf16[128,1024]{0,1:T(8,128)(2,1)S(1)} %fusion.32), channel_id=1, source_target_pairs={{8,0},{16,8},{24,16},{28,24},{20,28},{12,20},{4,12},{0,4},{9,1},{1... | collective-permute-start | bytes 786440 | tf_op jit(solution)/shard_map/ppermute | solution.py:98
  51.3 7.2 %collective-permute-start.2 = (bf16[128,1024]{0,1:T(8,128)(2,1)S(1)}, bf16[128,1024]{0,1:T(8,128)(2,1)S(1)}, u32[]{:S(2)}, u32[]{:S(2)}) collective-permute-start(bf16[128,1024]{0,1:T(8,128)(2,1)S(1)} %fusion.39), channel_id=1, source_target_pairs={{0,8},{8,16},{16,24},{24,28},{28,20},{20,12},{12,4},{4,0},{1,9},{9... | collective-permute-start | bytes 786440 | tf_op jit(solution)/shard_map/ppermute | solution.py:97
  54.1 6.7 %collective-permute-start.10 = (bf16[128,1024]{0,1:T(8,128)(2,1)S(1)}, bf16[128,1024]{0,1:T(8,128)(2,1)S(1)}, u32[]{:S(2)}, u32[]{:S(2)}) collective-permute-start(bf16[128,1024]{0,1:T(8,128)(2,1)S(1)} %fusion.31), channel_id=1, source_target_pairs={{8,0},{16,8},{24,16},{28,24},{20,28},{12,20},{4,12},{0,4},{9,1},{1... | collective-permute-start | bytes 786440 | tf_op jit(solution)/shard_map/ppermute | solution.py:98
  58.6 6.7 %collective-permute-start.3 = (bf16[128,1024]{0,1:T(8,128)(2,1)S(1)}, bf16[128,1024]{0,1:T(8,128)(2,1)S(1)}, u32[]{:S(2)}, u32[]{:S(2)}) collective-permute-start(bf16[128,1024]{0,1:T(8,128)(2,1)S(1)} %fusion.38), channel_id=1, source_target_pairs={{0,8},{8,16},{16,24},{24,28},{28,20},{20,12},{12,4},{4,0},{1,9},{9... | collective-permute-start | bytes 786440 | tf_op jit(solution)/shard_map/ppermute | solution.py:97
  60.8 7.0 %collective-permute-start.11 = (bf16[128,1024]{0,1:T(8,128)(2,1)S(1)}, bf16[128,1024]{0,1:T(8,128)(2,1)S(1)}, u32[]{:S(2)}, u32[]{:S(2)}) collective-permute-start(bf16[128,1024]{0,1:T(8,128)(2,1)S(1)} %fusion.30), channel_id=1, source_target_pairs={{8,0},{16,8},{24,16},{28,24},{20,28},{12,20},{4,12},{0,4},{9,1},{1... | collective-permute-start | bytes 786440 | tf_op jit(solution)/shard_map/ppermute | solution.py:98
  65.4 7.5 %collective-permute-start.4 = (bf16[128,1024]{0,1:T(8,128)(2,1)S(1)}, bf16[128,1024]{0,1:T(8,128)(2,1)S(1)}, u32[]{:S(2)}, u32[]{:S(2)}) collective-permute-start(bf16[128,1024]{0,1:T(8,128)(2,1)S(1)} %fusion.37), channel_id=1, source_target_pairs={{0,8},{8,16},{16,24},{24,28},{28,20},{20,12},{12,4},{4,0},{1,9},{9... | collective-permute-start | bytes 786440 | tf_op jit(solution)/shard_map/ppermute | solution.py:97
  67.9 7.8 %collective-permute-start.12 = (bf16[128,1024]{0,1:T(8,128)(2,1)S(1)}, bf16[128,1024]{0,1:T(8,128)(2,1)S(1)}, u32[]{:S(2)}, u32[]{:S(2)}) collective-permute-start(bf16[128,1024]{0,1:T(8,128)(2,1)S(1)} %fusion.29), channel_id=1, source_target_pairs={{8,0},{16,8},{24,16},{28,24},{20,28},{12,20},{4,12},{0,4},{9,1},{1... | collective-permute-start | bytes 786440 | tf_op jit(solution)/shard_map/ppermute | solution.py:98
  73.0 18.4 %copy-start.8 = (f32[4,2048]{1,0:T(4,128)S(1)}, f32[4,2048]{1,0:T(4,128)}, u32[]{:S(2)}) copy-start(f32[4,2048]{1,0:T(4,128)} %param.18) | copy-start | bytes 98308
  73.0 8.4 %collective-permute-start.5 = (bf16[128,1024]{0,1:T(8,128)(2,1)S(1)}, bf16[128,1024]{0,1:T(8,128)(2,1)S(1)}, u32[]{:S(2)}, u32[]{:S(2)}) collective-permute-start(bf16[128,1024]{0,1:T(8,128)(2,1)S(1)} %fusion.36), channel_id=1, source_target_pairs={{0,8},{8,16},{16,24},{24,28},{28,20},{20,12},{12,4},{4,0},{1,9},{9... | collective-permute-start | bytes 786440 | tf_op jit(solution)/shard_map/ppermute | solution.py:97
  75.8 8.7 %collective-permute-start.13 = (bf16[128,1024]{0,1:T(8,128)(2,1)S(1)}, bf16[128,1024]{0,1:T(8,128)(2,1)S(1)}, u32[]{:S(2)}, u32[]{:S(2)}) collective-permute-start(bf16[128,1024]{0,1:T(8,128)(2,1)S(1)} %fusion.28), channel_id=1, source_target_pairs={{8,0},{16,8},{24,16},{28,24},{20,28},{12,20},{4,12},{0,4},{9,1},{1... | collective-permute-start | bytes 786440 | tf_op jit(solution)/shard_map/ppermute | solution.py:98
  81.5 9.2 %collective-permute-start.6 = (bf16[128,1024]{0,1:T(8,128)(2,1)S(1)}, bf16[128,1024]{0,1:T(8,128)(2,1)S(1)}, u32[]{:S(2)}, u32[]{:S(2)}) collective-permute-start(bf16[128,1024]{0,1:T(8,128)(2,1)S(1)} %fusion.35), channel_id=1, source_target_pairs={{0,8},{8,16},{16,24},{24,28},{28,20},{20,12},{12,4},{4,0},{1,9},{9... | collective-permute-start | bytes 786440 | tf_op jit(solution)/shard_map/ppermute | solution.py:97
  84.6 14.4 %copy-start.9 = (s32[128]{0:T(128)S(1)}, s32[128]{0:T(128)}, u32[]{:S(2)}) copy-start(s32[128]{0:T(128)} %param.23) | copy-start | bytes 1540
  84.6 14.4 %copy-start.6 = (bf16[128,2048]{1,0:T(8,128)(2,1)S(1)}, bf16[128,2048]{1,0:T(8,128)(2,1)}, u32[]{:S(2)}) copy-start(bf16[128,2048]{1,0:T(8,128)(2,1)} %param.17) | copy-start | bytes 1572868
  84.6 6.8 %collective-permute-start.14 = (bf16[128,1024]{0,1:T(8,128)(2,1)S(1)}, bf16[128,1024]{0,1:T(8,128)(2,1)S(1)}, u32[]{:S(2)}, u32[]{:S(2)}) collective-permute-start(bf16[128,1024]{0,1:T(8,128)(2,1)S(1)} %fusion.27), channel_id=1, source_target_pairs={{8,0},{16,8},{24,16},{28,24},{20,28},{12,20},{4,12},{0,4},{9,1},{1... | collective-permute-start | bytes 786440 | tf_op jit(solution)/shard_map/ppermute | solution.py:98
  90.8 6.4 %collective-permute-start.7 = (bf16[128,1024]{0,1:T(8,128)(2,1)S(1)}, bf16[128,1024]{0,1:T(8,128)(2,1)S(1)}, u32[]{:S(2)}, u32[]{:S(2)}) collective-permute-start(bf16[128,1024]{0,1:T(8,128)(2,1)S(1)} %fusion.34), channel_id=1, source_target_pairs={{0,8},{8,16},{16,24},{24,28},{28,20},{20,12},{12,4},{4,0},{1,9},{9... | collective-permute-start | bytes 786440 | tf_op jit(solution)/shard_map/ppermute | solution.py:97
  97.5 8.1 %collective-permute-start.15 = (bf16[3,2048]{0,1:T(8,128)(2,1)S(1)}, bf16[3,2048]{0,1:T(8,128)(2,1)S(1)}, u32[]{:S(2)}, u32[]{:S(2)}) collective-permute-start(bf16[3,2048]{0,1:T(8,128)(2,1)S(1)} %pad_maximum_fusion), channel_id=1, source_target_pairs={{0,4},{4,8},{8,12},{12,16},{16,20},{20,24},{24,28},{1,5},{5,9},{9,... | collective-permute-start | bytes 36872 | tf_op jit(solution)/shard_map/ppermute | solution.py:13
  108.4 9.5 %copy-start.13 = (f32[32]{0:T(128)S(1)}, f32[32]{0:T(128)}, u32[]{:S(2)}) copy-start(f32[32]{0:T(128)} %param.22) | copy-start | bytes 388
  108.4 9.5 %copy-start.14 = (s32[128]{0:T(128)S(1)}, s32[128]{0:T(128)}, u32[]{:S(2)}) copy-start(s32[128]{0:T(128)} %param.21) | copy-start | bytes 1540
  117.6 146.9 %reduce-scatter.2.cloned.1.call-start = ((), (), s32[]{:S(2)}) async-start(), calls=%async_computation.3 | async-start | bytes 1310720 | tf_op jit(solution)/shard_map/reduce_scatter | solution.py:182
  167.8 1.0 copy-start.1
  171.9 3.1 %copy-start.2 = (f32[128,2048]{0,1:T(8,128)S(1)}, f32[128,2048]{0,1:T(8,128)}, u32[]{:S(2)}) copy-start(f32[128,2048]{0,1:T(8,128)} %copy-done.1) | copy-start | bytes 3145732
  171.9 5.9 %collective-permute-start.16 = (f32[3,2048]{1,0:T(4,128)S(1)}, f32[3,2048]{1,0:T(4,128)S(1)}, u32[]{:S(2)}, u32[]{:S(2)}) collective-permute-start(f32[3,2048]{1,0:T(4,128)S(1)} %copy.54), channel_id=1, source_target_pairs={{4,0},{8,4},{12,8},{16,12},{20,16},{24,20},{28,24},{5,1},{9,5},{13... | collective-permute-start | bytes 73736 | tf_op jit(solution)/shard_map/ppermute | solution.py:13
  175.0 4.2 %copy-start.3 = (f32[125,2048]{0,1:T(8,128)S(1)}, f32[125,2048]{0,1:T(8,128)}, u32[]{:S(2)}) copy-start(f32[125,2048]{0,1:T(8,128)} %slice.219) | copy-start | bytes 3072004
  181.4 8.0 %collective-permute-start.24 = (bf16[128,1024]{0,1:T(8,128)(2,1)S(1)}, bf16[128,1024]{0,1:T(8,128)(2,1)S(1)}, u32[]{:S(2)}, u32[]{:S(2)}) collective-permute-start(bf16[128,1024]{0,1:T(8,128)(2,1)S(1)} %get-tuple-element.38), channel_id=1, source_target_pairs={{8,0},{16,8},{24,16},{28,24},{20,28},{12,20},{4,12},{0,4},{9,1},{1... | collective-permute-start | bytes 786440 | tf_op jit(solution)/shard_map/ppermute | solution.py:75
  183.8 6.8 %collective-permute-start.17 = (bf16[128,1024]{0,1:T(8,128)(2,1)S(1)}, bf16[128,1024]{0,1:T(8,128)(2,1)S(1)}, u32[]{:S(2)}, u32[]{:S(2)}) collective-permute-start(bf16[128,1024]{0,1:T(8,128)(2,1)S(1)} %get-tuple-element.37), channel_id=1, source_target_pairs={{0,8},{8,16},{16,24},{24,28},{28,20},{20,12},{12,4},{4,0},{1,9},{9... | collective-permute-start | bytes 786440 | tf_op jit(solution)/shard_map/ppermute | solution.py:74
  189.3 7.0 %collective-permute-start.25 = (bf16[128,1024]{0,1:T(8,128)(2,1)S(1)}, bf16[128,1024]{0,1:T(8,128)(2,1)S(1)}, u32[]{:S(2)}, u32[]{:S(2)}) collective-permute-start(bf16[128,1024]{0,1:T(8,128)(2,1)S(1)} %collective-permute-done.24), channel_id=1, source_target_pairs={{8,0},{16,8},{24,16},{28,24},{20,28},{12,20},{4,12},{0,4},{9,1},{1... | collective-permute-start | bytes 786440 | tf_op jit(solution)/shard_map/ppermute | solution.py:75
  190.5 6.4 %collective-permute-start.18 = (bf16[128,1024]{0,1:T(8,128)(2,1)S(1)}, bf16[128,1024]{0,1:T(8,128)(2,1)S(1)}, u32[]{:S(2)}, u32[]{:S(2)}) collective-permute-start(bf16[128,1024]{0,1:T(8,128)(2,1)S(1)} %collective-permute-done.17), channel_id=1, source_target_pairs={{0,8},{8,16},{16,24},{24,28},{28,20},{20,12},{12,4},{4,0},{1,9},{9... | collective-permute-start | bytes 786440 | tf_op jit(solution)/shard_map/ppermute | solution.py:74
  196.4 7.0 %collective-permute-start.26 = (bf16[128,1024]{0,1:T(8,128)(2,1)S(1)}, bf16[128,1024]{0,1:T(8,128)(2,1)S(1)}, u32[]{:S(2)}, u32[]{:S(2)}) collective-permute-start(bf16[128,1024]{0,1:T(8,128)(2,1)S(1)} %collective-permute-done.25), channel_id=1, source_target_pairs={{8,0},{16,8},{24,16},{28,24},{20,28},{12,20},{4,12},{0,4},{9,1},{1... | collective-permute-start | bytes 786440 | tf_op jit(solution)/shard_map/ppermute | solution.py:75
  196.9 8.3 %collective-permute-start.19 = (bf16[128,1024]{0,1:T(8,128)(2,1)S(1)}, bf16[128,1024]{0,1:T(8,128)(2,1)S(1)}, u32[]{:S(2)}, u32[]{:S(2)}) collective-permute-start(bf16[128,1024]{0,1:T(8,128)(2,1)S(1)} %collective-permute-done.18), channel_id=1, source_target_pairs={{0,8},{8,16},{16,24},{24,28},{28,20},{20,12},{12,4},{4,0},{1,9},{9... | collective-permute-start | bytes 786440 | tf_op jit(solution)/shard_map/ppermute | solution.py:74
  203.3 8.5 %collective-permute-start.27 = (bf16[128,1024]{0,1:T(8,128)(2,1)S(1)}, bf16[128,1024]{0,1:T(8,128)(2,1)S(1)}, u32[]{:S(2)}, u32[]{:S(2)}) collective-permute-start(bf16[128,1024]{0,1:T(8,128)(2,1)S(1)} %collective-permute-done.26), channel_id=1, source_target_pairs={{8,0},{16,8},{24,16},{28,24},{20,28},{12,20},{4,12},{0,4},{9,1},{1... | collective-permute-start | bytes 786440 | tf_op jit(solution)/shard_map/ppermute | solution.py:75
  205.2 9.6 %collective-permute-start.20 = (bf16[128,1024]{0,1:T(8,128)(2,1)S(1)}, bf16[128,1024]{0,1:T(8,128)(2,1)S(1)}, u32[]{:S(2)}, u32[]{:S(2)}) collective-permute-start(bf16[128,1024]{0,1:T(8,128)(2,1)S(1)} %collective-permute-done.19), channel_id=1, source_target_pairs={{0,8},{8,16},{16,24},{24,28},{28,20},{20,12},{12,4},{4,0},{1,9},{9... | collective-permute-start | bytes 786440 | tf_op jit(solution)/shard_map/ppermute | solution.py:74
  211.8 9.0 %collective-permute-start.28 = (bf16[128,1024]{0,1:T(8,128)(2,1)S(1)}, bf16[128,1024]{0,1:T(8,128)(2,1)S(1)}, u32[]{:S(2)}, u32[]{:S(2)}) collective-permute-start(bf16[128,1024]{0,1:T(8,128)(2,1)S(1)} %collective-permute-done.27), channel_id=1, source_target_pairs={{8,0},{16,8},{24,16},{28,24},{20,28},{12,20},{4,12},{0,4},{9,1},{1... | collective-permute-start | bytes 786440 | tf_op jit(solution)/shard_map/ppermute | solution.py:75
  214.9 8.3 %collective-permute-start.21 = (bf16[128,1024]{0,1:T(8,128)(2,1)S(1)}, bf16[128,1024]{0,1:T(8,128)(2,1)S(1)}, u32[]{:S(2)}, u32[]{:S(2)}) collective-permute-start(bf16[128,1024]{0,1:T(8,128)(2,1)S(1)} %collective-permute-done.20), channel_id=1, source_target_pairs={{0,8},{8,16},{16,24},{24,28},{28,20},{20,12},{12,4},{4,0},{1,9},{9... | collective-permute-start | bytes 786440 | tf_op jit(solution)/shard_map/ppermute | solution.py:74
  220.8 8.1 %collective-permute-start.29 = (bf16[128,1024]{0,1:T(8,128)(2,1)S(1)}, bf16[128,1024]{0,1:T(8,128)(2,1)S(1)}, u32[]{:S(2)}, u32[]{:S(2)}) collective-permute-start(bf16[128,1024]{0,1:T(8,128)(2,1)S(1)} %collective-permute-done.28), channel_id=1, source_target_pairs={{8,0},{16,8},{24,16},{28,24},{20,28},{12,20},{4,12},{0,4},{9,1},{1... | collective-permute-start | bytes 786440 | tf_op jit(solution)/shard_map/ppermute | solution.py:75
  223.1 7.6 %collective-permute-start.22 = (bf16[128,1024]{0,1:T(8,128)(2,1)S(1)}, bf16[128,1024]{0,1:T(8,128)(2,1)S(1)}, u32[]{:S(2)}, u32[]{:S(2)}) collective-permute-start(bf16[128,1024]{0,1:T(8,128)(2,1)S(1)} %collective-permute-done.21), channel_id=1, source_target_pairs={{0,8},{8,16},{16,24},{24,28},{28,20},{20,12},{12,4},{4,0},{1,9},{9... | collective-permute-start | bytes 786440 | tf_op jit(solution)/shard_map/ppermute | solution.py:74
  229.0 6.4 %collective-permute-start.30 = (bf16[128,1024]{0,1:T(8,128)(2,1)S(1)}, bf16[128,1024]{0,1:T(8,128)(2,1)S(1)}, u32[]{:S(2)}, u32[]{:S(2)}) collective-permute-start(bf16[128,1024]{0,1:T(8,128)(2,1)S(1)} %collective-permute-done.29), channel_id=1, source_target_pairs={{8,0},{16,8},{24,16},{28,24},{20,28},{12,20},{4,12},{0,4},{9,1},{1... | collective-permute-start | bytes 786440 | tf_op jit(solution)/shard_map/ppermute | solution.py:75
  230.3 5.4 %copy-start.12 = (bf16[512,2048]{1,0:T(8,128)(2,1)S(1)}, bf16[512,2048]{1,0:T(8,128)(2,1)}, u32[]{:S(2)}) copy-start(bf16[512,2048]{1,0:T(8,128)(2,1)} %param.16) | copy-start | bytes 6291460
  230.7 6.4 %collective-permute-start.23 = (bf16[128,1024]{0,1:T(8,128)(2,1)S(1)}, bf16[128,1024]{0,1:T(8,128)(2,1)S(1)}, u32[]{:S(2)}, u32[]{:S(2)}) collective-permute-start(bf16[128,1024]{0,1:T(8,128)(2,1)S(1)} %collective-permute-done.22), channel_id=1, source_target_pairs={{0,8},{8,16},{16,24},{24,28},{28,20},{20,12},{12,4},{4,0},{1,9},{9... | collective-permute-start | bytes 786440 | tf_op jit(solution)/shard_map/ppermute | solution.py:74
  239.1 28.4 %copy-start.7 = (bf16[128,2048]{0,1:T(8,128)(2,1)S(1)}, bf16[128,2048]{0,1:T(8,128)(2,1)}, u32[]{:S(2)}) copy-start(bf16[128,2048]{0,1:T(8,128)(2,1)} %get-tuple-element.34) | copy-start | bytes 1572868
  265.5 18.0 %collective-permute-start.33 = (bf16[128,512]{1,0:T(8,128)(2,1)S(1)}, bf16[128,512]{1,0:T(8,128)(2,1)S(1)}, u32[]{:S(2)}, u32[]{:S(2)}) collective-permute-start(bf16[128,512]{1,0:T(8,128)(2,1)S(1)} %get-tuple-element.42), channel_id=1, source_target_pairs={{4,4},{5,12},{6,20},{7,28},{12,5},{13,13},{14,21},{15,29},{20,6},{... | collective-permute-start | bytes 393224 | tf_op jit(solution)/shard_map/ppermute | solution.py:45
  266.2 18.4 %collective-permute-start.34 = (bf16[128,512]{1,0:T(8,128)(2,1)S(1)}, bf16[128,512]{1,0:T(8,128)(2,1)S(1)}, u32[]{:S(2)}, u32[]{:S(2)}) collective-permute-start(bf16[128,512]{1,0:T(8,128)(2,1)S(1)} %get-tuple-element.41), channel_id=1, source_target_pairs={{4,0},{5,8},{6,16},{7,24},{12,1},{13,9},{14,17},{15,25},{20,2},{21... | collective-permute-start | bytes 393224 | tf_op jit(solution)/shard_map/ppermute | solution.py:45
  270.2 14.4 %collective-permute-start.31 = (bf16[128,512]{1,0:T(8,128)(2,1)S(1)}, bf16[128,512]{1,0:T(8,128)(2,1)S(1)}, u32[]{:S(2)}, u32[]{:S(2)}) collective-permute-start(bf16[128,512]{1,0:T(8,128)(2,1)S(1)} %get-tuple-element.42), channel_id=1, source_target_pairs={{0,4},{1,12},{2,20},{3,28},{8,5},{9,13},{10,21},{11,29},{16,6},{17... | collective-permute-start | bytes 393224 | tf_op jit(solution)/shard_map/ppermute | solution.py:45
  278.3 14.2 %collective-permute-start.32 = (bf16[128,512]{1,0:T(8,128)(2,1)S(1)}, bf16[128,512]{1,0:T(8,128)(2,1)S(1)}, u32[]{:S(2)}, u32[]{:S(2)}) collective-permute-start(bf16[128,512]{1,0:T(8,128)(2,1)S(1)} %get-tuple-element.41), channel_id=1, source_target_pairs={{0,0},{1,8},{2,16},{3,24},{8,1},{9,9},{10,17},{11,25},{16,2},{17,1... | collective-permute-start | bytes 393224 | tf_op jit(solution)/shard_map/ppermute | solution.py:45
Sparse Core Ops, SparseCore 0:
  117.8 37.4 all-reduce.7
  240.4 24.0 reduce-scatter.1

commit v5 on v4

--- a/solution.py
+++ b/solution.py
@@ -100,6 +100,40 @@
         sum_b = (sum_b.astype(jnp.float32) + own_b[s]).astype(jnp.bfloat16)
     return jnp.concatenate([sum_a, sum_b], axis=1)
 
+def halves_of(value, dim, upper):
+    low, high = jnp.split(value, 2, axis=dim)
+    return jnp.where(upper, high, low), jnp.where(upper, low, high)
+
+
+def col_psum(value):
+    core = lax.axis_index("col") % 2 == 1
+    keep, give = halves_of(value, 1, core)
+    count = lax.axis_size("col")
+    got = lax.ppermute(give, "col", [(c, c ^ 1) for c in range(count)])
+    pair = keep.astype(jnp.float32) + got.astype(jnp.float32)
+    total = pair + lax.ppermute(
+        pair.astype(jnp.bfloat16), "col", [(c, c ^ 2) for c in range(count)]
+    ).astype(jnp.float32)
+    other = lax.ppermute(total, "col", [(c, c ^ 1) for c in range(count)])
+    return jnp.where(
+        core, jnp.concatenate([other, total], axis=1), jnp.concatenate([total, other], axis=1)
+    )
+
+
+def col_psum_scatter(value):
+    col = lax.axis_index("col")
+    count = lax.axis_size("col")
+    quarters = value.reshape(2, 2, value.shape[0] // 4, value.shape[1])
+    keep = jnp.take(quarters, col % 2, axis=1)
+    give = jnp.take(quarters, 1 - col % 2, axis=1)
+    got = lax.ppermute(give, "col", [(c, c ^ 1) for c in range(count)])
+    pair = keep.astype(jnp.float32) + got.astype(jnp.float32)
+    mine = jnp.take(pair, col // 2, axis=0)
+    theirs = jnp.take(pair, 1 - col // 2, axis=0)
+    got = lax.ppermute(theirs.astype(jnp.bfloat16), "col", [(c, c ^ 2) for c in range(count)])
+    return (mine + got.astype(jnp.float32)).astype(jnp.bfloat16)
+
+
 def silu_grad(argument):
     sigmoid_v = jax.nn.sigmoid(argument)
     return sigmoid_v * (1.0 + argument * (1.0 - sigmoid_v))
@@ -142,7 +176,10 @@
         jnp.float32
     )
     token_weight = jnp.sum(lang_table * lang_weight[None, :], axis=1)[:, None]
-    out_total = lax.psum(partial_value.astype(jnp.bfloat16), "col").astype(jnp.float32)
+    if moves_tokens and lax.axis_size("col") == 4:
+        out_total = col_psum(partial_value.astype(jnp.bfloat16))
+    else:
+        out_total = lax.psum(partial_value.astype(jnp.bfloat16), "col").astype(jnp.float32)
     out_block = lax.dynamic_slice_in_dim(out_total, col_start, columns, 1)
     residual_grad = (token_weight * (out_total - target.astype(jnp.float32))).astype(jnp.bfloat16)
     grad_mixed = lax.dot_general(
@@ -179,9 +216,11 @@
             got_a, in_weight[:, :half], contract, preferred_element_type=jnp.float32
         ) + lax.dot_general(got_b, in_weight[:, half:], contract, preferred_element_type=jnp.float32)
         grad_cols = jnp.take(grad_cols.astype(jnp.bfloat16), jnp.argsort(sources), axis=0)
-        grad_sum = lax.psum_scatter(
-            grad_cols.reshape(-1, grad_cols.shape[2]), "col", scatter_dimension=0, tiled=True
-        )
+        grad_cols = grad_cols.reshape(-1, grad_cols.shape[2])
+        if lax.axis_size("col") == 4:
+            grad_sum = col_psum_scatter(grad_cols)
+        else:
+            grad_sum = lax.psum_scatter(grad_cols, "col", scatter_dimension=0, tiled=True)
         grad_tokens = placed_blocks(grad_sum, row_count)
     else:
         partial_grad = lax.dot_general(

time: 301 us -> 255 us (0.85)
  waiting for transfers between devices: 167 us -> 134 us
  between operations: 16 us -> 2.75 us
    psum x1 -> x0, waiting for transfers between devices: 37.2 us -> none  [shards(): lax.psum(partial_value.astype(jnp.bfloat16), 'col').astype(jnp.float32)]
    ppermute x0 -> x5, waiting for transfers between devices: none -> 27.5 us  [the longest x1 13.4 us: col_psum(): lax.ppermute(pair.astype(jnp.bfloat16), 'col', [(c, c ^ 2) for c in range...]
    reduce_scatter x1 -> x0, waiting for transfers between devices: 24.2 us -> none  [shards(): lax.psum_scatter(grad_cols.reshape(-1, grad_cols.shape[2]), 'col', scatte...]
    unnamed x48 -> x52, local copies, waits for them, and re-layouts: 8.44 us -> 8.49 us
  transfers between devices with their start and end apart: 38 -> 41, of which waited for: 32 -> 36; matrix products, arithmetic and copies ran while one was open for 5% -> 6% of each run, Pallas kernels for 0% -> 0%
where the time goes in v5:
time: 255 us; the launch traced here: 254 us
  waiting for transfers between devices  134 us (53%)
  starting transfers between devices  54.7 us (21%)
  matrix products  26.3 us (10%)
  local copies, waits for them, and re-layouts  22.8 us (9%)
  other arithmetic  13.5 us (5%)
  between operations  2.75 us (1%)
    ppermute x7, waiting for transfers between devices, ring_gather(): sent_b = lax.ppermute(sent_b, axis, behind)  39.3 us
    ppermute x7, waiting for transfers between devices, ring_reduce_scatter(): sum_a = lax.ppermute(sum_a, axis, ahead)  26.9 us
    ppermute x4, starting transfers between devices, placed_blocks(): lax.ppermute(grad_sum[k * row_count:(k + 1) * row_count], ('row', 'col'),...  14.4 us
    ppermute x1, waiting for transfers between devices, col_psum(): lax.ppermute(pair.astype(jnp.bfloat16), 'col', [(c, c ^ 2) for c in range...  13.4 us
    dot_general x1, matrix products, shards(): lax.dot_general(residual_grad, out_weight, (((1,), (1,)), ((), ())), pref...  12.8 us
    ppermute x7, waiting for transfers between devices, ring_reduce_scatter(): sum_b = lax.ppermute(sum_b, axis, behind)  12.7 us
    ppermute x7, starting transfers between devices, ring_reduce_scatter(): sum_b = lax.ppermute(sum_b, axis, behind)  10.5 us
    ppermute x7, starting transfers between devices, ring_gather(): sent_b = lax.ppermute(sent_b, axis, behind)  9.13 us
  transfers between devices with their start and end apart: 41, of which 36 were waited for; matrix products, arithmetic and copies ran while one was open for 6% of the time, Pallas kernels for 0%

profile of v5, /device:TPU:2, one launch (start us, length us, event | category | flops | bytes accessed | tf_op | source)
XLA Modules:
  0.0 254.4 jit_solution(13062609354642942995)
XLA Ops:
  0.7 1.6 copy.57
  3.4 5.8 %all-to-all-start = ((bf16[128,8,256]{2,0,1:T(8,128)(2,1)}), bf16[128,8,256]{2,0,1:T(8,128)(2,1)S(1)}, u32[]{:S(2)}, u32[]{:S(2)}) async-start(bf16[128,8,256]{2,0,1:T(8,128)(2,1)} %copy.59), calls=%async_computation | async-start | bytes 1048576 | tf_op jit(solution)/shard_map/all_to_all | solution.py:24
  14.8 8.9 %all-to-all-done = bf16[128,8,256]{2,0,1:T(8,128)(2,1)S(1)} async-done(((bf16[128,8,256]{2,0,1:T(8,128)(2,1)}), bf16[128,8,256]{2,0,1:T(8,128)(2,1)S(1)}, u32[]{:S(2)}, u32[]{:S(2)}) %all-to-all-start) | async-done | bytes 524320 | tf_op jit(solution)/shard_map/all_to_all | solution.py:24
  23.8 1.9 collective-permute-done
  26.8 1.4 copy-done.11
  28.2 1.3 fusion.22
  29.6 1.9 copy-done.4
  31.5 1.5 collective-permute-start.8
  33.7 1.4 copy-done.12
  35.2 1.3 fusion.25
  37.2 2.6 %collective-permute-done.8 = bf16[128,1024]{0,1:T(8,128)(2,1)S(1)} collective-permute-done((bf16[128,1024]{0,1:T(8,128)(2,1)S(1)}, bf16[128,1024]{0,1:T(8,128)(2,1)S(1)}, u32[]{:S(2)}, u32[]{:S(2)}) %collective-permute-start.8) | collective-permute-done | bytes 262176 | tf_op jit(solution)/shard_map/ppermute | solution.py:98
  39.9 1.5 collective-permute-start.9
  41.4 3.2 %collective-permute-done.1 = bf16[128,1024]{0,1:T(8,128)(2,1)S(1)} collective-permute-done((bf16[128,1024]{0,1:T(8,128)(2,1)S(1)}, bf16[128,1024]{0,1:T(8,128)(2,1)S(1)}, u32[]{:S(2)}, u32[]{:S(2)}) %collective-permute-start.1) | collective-permute-done | bytes 262176 | tf_op jit(solution)/shard_map/ppermute | solution.py:97
  45.4 2.1 collective-permute-done.9
  47.6 1.5 collective-permute-start.10
  49.1 2.9 %collective-permute-done.2 = bf16[128,1024]{0,1:T(8,128)(2,1)S(1)} collective-permute-done((bf16[128,1024]{0,1:T(8,128)(2,1)S(1)}, bf16[128,1024]{0,1:T(8,128)(2,1)S(1)}, u32[]{:S(2)}, u32[]{:S(2)}) %collective-permute-start.2) | collective-permute-done | bytes 262176 | tf_op jit(solution)/shard_map/ppermute | solution.py:97
  52.7 1.5 collective-permute-done.10
  54.3 1.5 collective-permute-start.11
  55.8 3.0 %collective-permute-done.3 = bf16[128,1024]{0,1:T(8,128)(2,1)S(1)} collective-permute-done((bf16[128,1024]{0,1:T(8,128)(2,1)S(1)}, bf16[128,1024]{0,1:T(8,128)(2,1)S(1)}, u32[]{:S(2)}, u32[]{:S(2)}) %collective-permute-start.3) | collective-permute-done | bytes 262176 | tf_op jit(solution)/shard_map/ppermute | solution.py:97
  59.5 1.8 collective-permute-done.11
  61.4 1.5 collective-permute-start.12
  62.9 3.5 %collective-permute-done.4 = bf16[128,1024]{0,1:T(8,128)(2,1)S(1)} collective-permute-done((bf16[128,1024]{0,1:T(8,128)(2,1)S(1)}, bf16[128,1024]{0,1:T(8,128)(2,1)S(1)}, u32[]{:S(2)}, u32[]{:S(2)}) %collective-permute-start.4) | collective-permute-done | bytes 262176 | tf_op jit(solution)/shard_map/ppermute | solution.py:97
  67.1 2.1 collective-permute-done.12
  69.3 1.5 collective-permute-start.13
  70.8 4.0 %collective-permute-done.5 = bf16[128,1024]{0,1:T(8,128)(2,1)S(1)} collective-permute-done((bf16[128,1024]{0,1:T(8,128)(2,1)S(1)}, bf16[128,1024]{0,1:T(8,128)(2,1)S(1)}, u32[]{:S(2)}, u32[]{:S(2)}) %collective-permute-start.5) | collective-permute-done | bytes 262176 | tf_op jit(solution)/shard_map/ppermute | solution.py:97
  75.5 2.5 collective-permute-done.13
  78.1 1.5 collective-permute-start.14
  79.7 4.5 %collective-permute-done.6 = bf16[128,1024]{0,1:T(8,128)(2,1)S(1)} collective-permute-done((bf16[128,1024]{0,1:T(8,128)(2,1)S(1)}, bf16[128,1024]{0,1:T(8,128)(2,1)S(1)}, u32[]{:S(2)}, u32[]{:S(2)}) %collective-permute-start.6) | collective-permute-done | bytes 262176 | tf_op jit(solution)/shard_map/ppermute | solution.py:97
  85.0 5.7 %collective-permute-done.7 = bf16[128,1024]{0,1:T(8,128)(2,1)S(1)} collective-permute-done((bf16[128,1024]{0,1:T(8,128)(2,1)S(1)}, bf16[128,1024]{0,1:T(8,128)(2,1)S(1)}, u32[]{:S(2)}, u32[]{:S(2)}) %collective-permute-start.7) | collective-permute-done | bytes 262176 | tf_op jit(solution)/shard_map/ppermute | solution.py:97
  91.0 1.7 collective-permute-start.15
  93.0 6.2 %collective-permute-done.15 = bf16[3,2048]{0,1:T(8,128)(2,1)S(1)} collective-permute-done((bf16[3,2048]{0,1:T(8,128)(2,1)S(1)}, bf16[3,2048]{0,1:T(8,128)(2,1)S(1)}, u32[]{:S(2)}, u32[]{:S(2)}) %collective-permute-start.15) | collective-permute-done | bytes 12320 | tf_op jit(solution)/shard_map/ppermute | solution.py:13
  99.6 2.2 fusion.9
  101.8 8.3 %convolution_convert_fusion = bf16[128,4096]{1,0:T(8,128)(2,1)S(1)} fusion(bf16[2048,4096]{1,0:T(8,128)(2,1)} %param.23, bf16[128,2048]{0,1:T(8,128)(2,1)S(1)} %copy.60, f32[128,2048]{0,1:T(8,128)S(1)} %fusion.9), kind=kOutput, calls=%fused_computation.6 | convolution fusion | flops 2150891520 | bytes 19398656 | tf_op jit(solution)/shard_map/dot_general | solution.py:172
  110.2 1.9 collective-permute-done.16
  113.0 13.4 %collective-permute-done.17 = bf16[128,2048]{1,0:T(8,128)(2,1)S(1)} collective-permute-done((bf16[128,2048]{1,0:T(8,128)(2,1)S(1)}, bf16[128,2048]{1,0:T(8,128)(2,1)S(1)}, u32[]{:S(2)}, u32[]{:S(2)}) %collective-permute-start.17) | collective-permute-done | bytes 524320 | tf_op jit(solution)/shard_map/ppermute | solution.py:114
  127.0 2.5 collective-permute-done.18
  129.7 12.8 %multiply_multiply_fusion.2 = (f32[128,2048]{0,1:T(8,128)S(1)}, f32[128,2048]{0,1:T(8,128)S(1)}, bf16[128,2048]{0,1:T(8,128)(2,1)}) fusion(f32[128]{0:T(128)S(1)} %get-tuple-element.72, f32[2048]{0:T(1024)S(1)} %bitcast.108, f32[128,2048]{0,1:T(8,128)S(1)} %fusion.9, bf16[128,2048]{0,1:T(8,128)(2,1)S(1)} %copy.60, bf16[2048,4096]{1,0:T(8,128)(2,1)} %param.23, ...), kind=kOutput, calls=%fused_computation.42 | convolution fusion | flops 2155872256 | bytes 24126464 | tf_op jit(solution)/shard_map/dot_general | solution.py:185
  143.6 1.6 slice_add_fusion
  145.1 1.6 copy.62
  146.7 1.6 collective-permute-start.19
  148.3 1.3 slice.239
  149.7 1.3 slice.238
  151.0 1.3 slice.237
  153.1 1.4 copy.63
  154.5 2.5 add_convert_fusion.1
  157.0 3.4 %collective-permute-start.27 = (bf16[128,1024]{0,1:T(8,128)(2,1)S(1)}, bf16[128,1024]{0,1:T(8,128)(2,1)S(1)}, u32[]{:S(2)}, u32[]{:S(2)}) collective-permute-start(bf16[128,1024]{0,1:T(8,128)(2,1)S(1)} %get-tuple-element.62), channel_id=1, source_target_pairs={{8,0},{16,8},{24,16},{28,24},{20,28},{12,20},{4,12},{0,4},{9,1},{1... | collective-permute-start | bytes 786440 | tf_op jit(solution)/shard_map/ppermute | solution.py:75
  161.3 6.5 %collective-permute-done.27 = bf16[128,1024]{0,1:T(8,128)(2,1)S(1)} collective-permute-done((bf16[128,1024]{0,1:T(8,128)(2,1)S(1)}, bf16[128,1024]{0,1:T(8,128)(2,1)S(1)}, u32[]{:S(2)}, u32[]{:S(2)}) %collective-permute-start.27) | collective-permute-done | bytes 262176 | tf_op jit(solution)/shard_map/ppermute | solution.py:75
  169.9 5.8 %collective-permute-done.28 = bf16[128,1024]{0,1:T(8,128)(2,1)S(1)} collective-permute-done((bf16[128,1024]{0,1:T(8,128)(2,1)S(1)}, bf16[128,1024]{0,1:T(8,128)(2,1)S(1)}, u32[]{:S(2)}, u32[]{:S(2)}) %collective-permute-start.28) | collective-permute-done | bytes 262176 | tf_op jit(solution)/shard_map/ppermute | solution.py:75
  177.7 4.9 %collective-permute-done.29 = bf16[128,1024]{0,1:T(8,128)(2,1)S(1)} collective-permute-done((bf16[128,1024]{0,1:T(8,128)(2,1)S(1)}, bf16[128,1024]{0,1:T(8,128)(2,1)S(1)}, u32[]{:S(2)}, u32[]{:S(2)}) %collective-permute-start.29) | collective-permute-done | bytes 262176 | tf_op jit(solution)/shard_map/ppermute | solution.py:75
  182.9 1.8 collective-permute-start.23
  184.7 4.9 %collective-permute-done.30 = bf16[128,1024]{0,1:T(8,128)(2,1)S(1)} collective-permute-done((bf16[128,1024]{0,1:T(8,128)(2,1)S(1)}, bf16[128,1024]{0,1:T(8,128)(2,1)S(1)}, u32[]{:S(2)}, u32[]{:S(2)}) %collective-permute-start.30) | collective-permute-done | bytes 262176 | tf_op jit(solution)/shard_map/ppermute | solution.py:75
  191.8 6.0 %collective-permute-done.31 = bf16[128,1024]{0,1:T(8,128)(2,1)S(1)} collective-permute-done((bf16[128,1024]{0,1:T(8,128)(2,1)S(1)}, bf16[128,1024]{0,1:T(8,128)(2,1)S(1)}, u32[]{:S(2)}, u32[]{:S(2)}) %collective-permute-start.31) | collective-permute-done | bytes 262176 | tf_op jit(solution)/shard_map/ppermute | solution.py:75
  197.9 1.7 collective-permute-start.32
  200.1 6.9 %collective-permute-done.32 = bf16[128,1024]{0,1:T(8,128)(2,1)S(1)} collective-permute-done((bf16[128,1024]{0,1:T(8,128)(2,1)S(1)}, bf16[128,1024]{0,1:T(8,128)(2,1)S(1)}, u32[]{:S(2)}, u32[]{:S(2)}) %collective-permute-start.32) | collective-permute-done | bytes 262176 | tf_op jit(solution)/shard_map/ppermute | solution.py:75
  206.9 1.3 collective-permute-start.33
  209.1 4.2 %collective-permute-done.33 = bf16[128,1024]{0,1:T(8,128)(2,1)S(1)} collective-permute-done((bf16[128,1024]{0,1:T(8,128)(2,1)S(1)}, bf16[128,1024]{0,1:T(8,128)(2,1)S(1)}, u32[]{:S(2)}, u32[]{:S(2)}) %collective-permute-start.33) | collective-permute-done | bytes 262176 | tf_op jit(solution)/shard_map/ppermute | solution.py:75
  213.6 1.3 fusion.15
  217.5 1.9 collective-permute-done.34
  220.2 7.8 %collective-permute-done.35 = bf16[256,512]{1,0:T(8,128)(2,1)S(1)} collective-permute-done((bf16[256,512]{1,0:T(8,128)(2,1)S(1)}, bf16[256,512]{1,0:T(8,128)(2,1)S(1)}, u32[]{:S(2)}, u32[]{:S(2)}) %collective-permute-start.35) | collective-permute-done | bytes 262176 | tf_op jit(solution)/shard_map/ppermute | solution.py:133
  231.1 1.8 dynamic-slice_convert_fusion
  232.9 8.4 %collective-permute-start.36 = (bf16[128,512]{1,0:T(8,128)(2,1)S(1)}, bf16[128,512]{1,0:T(8,128)(2,1)S(1)}, u32[]{:S(2)}, u32[]{:S(2)}) collective-permute-start(bf16[128,512]{1,0:T(8,128)(2,1)S(1)} %get-tuple-element.66), channel_id=1, source_target_pairs={{0,4},{1,12},{2,20},{3,28},{8,5},{9,13},{10,21},{11,29},{16,6},{17... | collective-permute-start | bytes 393224 | tf_op jit(solution)/shard_map/ppermute | solution.py:45
  241.4 4.0 %collective-permute-start.37 = (bf16[128,512]{1,0:T(8,128)(2,1)S(1)}, bf16[128,512]{1,0:T(8,128)(2,1)S(1)}, u32[]{:S(2)}, u32[]{:S(2)}) collective-permute-start(bf16[128,512]{1,0:T(8,128)(2,1)S(1)} %get-tuple-element.65), channel_id=1, source_target_pairs={{0,0},{1,8},{2,16},{3,24},{8,1},{9,9},{10,17},{11,25},{16,2},{17,1... | collective-permute-start | bytes 393224 | tf_op jit(solution)/shard_map/ppermute | solution.py:45
  245.3 2.0 collective-permute-done.39
  247.4 6.2 %collective-permute-done.37 = bf16[128,512]{1,0:T(8,128)(2,1)S(1)} collective-permute-done((bf16[128,512]{1,0:T(8,128)(2,1)S(1)}, bf16[128,512]{1,0:T(8,128)(2,1)S(1)}, u32[]{:S(2)}, u32[]{:S(2)}) %collective-permute-start.37) | collective-permute-done | bytes 131104 | tf_op jit(solution)/shard_map/ppermute | solution.py:45
  (150 shorter events, 33.5 us)
Async XLA Ops:
  2.3 7.0 %copy-start.17 = (s32[8]{0:T(128)S(1)}, s32[8]{0:T(128)}, u32[]{:S(2)}) copy-start(s32[8]{0:T(128)} %constant.151.clone) | copy-start | bytes 100
  2.3 8.9 %copy-start = (s32[8]{0:T(128)S(1)}, s32[8]{0:T(128)}, u32[]{:S(2)}) copy-start(s32[8]{0:T(128)} %constant.152.clone) | copy-start | bytes 100
  3.4 20.3 %all-to-all-start = ((bf16[128,8,256]{2,0,1:T(8,128)(2,1)}), bf16[128,8,256]{2,0,1:T(8,128)(2,1)S(1)}, u32[]{:S(2)}, u32[]{:S(2)}) async-start(bf16[128,8,256]{2,0,1:T(8,128)(2,1)} %copy.59), calls=%async_computation | async-start | bytes 1048576 | tf_op jit(solution)/shard_map/all_to_all | solution.py:24
  23.7 1.9 collective-permute-start
  26.6 1.6 copy-start.11
  29.5 2.0 copy-start.4
  31.5 8.3 %collective-permute-start.8 = (bf16[128,1024]{0,1:T(8,128)(2,1)S(1)}, bf16[128,1024]{0,1:T(8,128)(2,1)S(1)}, u32[]{:S(2)}, u32[]{:S(2)}) collective-permute-start(bf16[128,1024]{0,1:T(8,128)(2,1)S(1)} %slice.330), channel_id=1, source_target_pairs={{8,0},{16,8},{24,16},{28,24},{20,28},{12,20},{4,12},{0,4},{9,1},{1... | collective-permute-start | bytes 786440 | tf_op jit(solution)/shard_map/ppermute | solution.py:98
  33.6 1.6 copy-start.12
  35.2 4.7 %copy-start.5 = (f32[1024,1024]{0,1:T(8,128)S(1)}, f32[1024,1024]{0,1:T(8,128)}, u32[]{:S(2)}) copy-start(f32[1024,1024]{0,1:T(8,128)} %copy-done.4) | copy-start | bytes 12582916
  36.6 8.1 %collective-permute-start.1 = (bf16[128,1024]{0,1:T(8,128)(2,1)S(1)}, bf16[128,1024]{0,1:T(8,128)(2,1)S(1)}, u32[]{:S(2)}, u32[]{:S(2)}) collective-permute-start(bf16[128,1024]{0,1:T(8,128)(2,1)S(1)} %slice.331), channel_id=1, source_target_pairs={{0,8},{8,16},{16,24},{24,28},{28,20},{20,12},{12,4},{4,0},{1,9},{9... | collective-permute-start | bytes 786440 | tf_op jit(solution)/shard_map/ppermute | solution.py:97
  39.9 7.6 %collective-permute-start.9 = (bf16[128,1024]{0,1:T(8,128)(2,1)S(1)}, bf16[128,1024]{0,1:T(8,128)(2,1)S(1)}, u32[]{:S(2)}, u32[]{:S(2)}) collective-permute-start(bf16[128,1024]{0,1:T(8,128)(2,1)S(1)} %fusion.33), channel_id=1, source_target_pairs={{8,0},{16,8},{24,16},{28,24},{20,28},{12,20},{4,12},{0,4},{9,1},{1... | collective-permute-start | bytes 786440 | tf_op jit(solution)/shard_map/ppermute | solution.py:98
  44.8 7.2 %collective-permute-start.2 = (bf16[128,1024]{0,1:T(8,128)(2,1)S(1)}, bf16[128,1024]{0,1:T(8,128)(2,1)S(1)}, u32[]{:S(2)}, u32[]{:S(2)}) collective-permute-start(bf16[128,1024]{0,1:T(8,128)(2,1)S(1)} %fusion.40), channel_id=1, source_target_pairs={{0,8},{8,16},{16,24},{24,28},{28,20},{20,12},{12,4},{4,0},{1,9},{9... | collective-permute-start | bytes 786440 | tf_op jit(solution)/shard_map/ppermute | solution.py:97
  47.6 6.7 %collective-permute-start.10 = (bf16[128,1024]{0,1:T(8,128)(2,1)S(1)}, bf16[128,1024]{0,1:T(8,128)(2,1)S(1)}, u32[]{:S(2)}, u32[]{:S(2)}) collective-permute-start(bf16[128,1024]{0,1:T(8,128)(2,1)S(1)} %fusion.32), channel_id=1, source_target_pairs={{8,0},{16,8},{24,16},{28,24},{20,28},{12,20},{4,12},{0,4},{9,1},{1... | collective-permute-start | bytes 786440 | tf_op jit(solution)/shard_map/ppermute | solution.py:98
  52.1 6.7 %collective-permute-start.3 = (bf16[128,1024]{0,1:T(8,128)(2,1)S(1)}, bf16[128,1024]{0,1:T(8,128)(2,1)S(1)}, u32[]{:S(2)}, u32[]{:S(2)}) collective-permute-start(bf16[128,1024]{0,1:T(8,128)(2,1)S(1)} %fusion.39), channel_id=1, source_target_pairs={{0,8},{8,16},{16,24},{24,28},{28,20},{20,12},{12,4},{4,0},{1,9},{9... | collective-permute-start | bytes 786440 | tf_op jit(solution)/shard_map/ppermute | solution.py:97
  54.3 7.0 %collective-permute-start.11 = (bf16[128,1024]{0,1:T(8,128)(2,1)S(1)}, bf16[128,1024]{0,1:T(8,128)(2,1)S(1)}, u32[]{:S(2)}, u32[]{:S(2)}) collective-permute-start(bf16[128,1024]{0,1:T(8,128)(2,1)S(1)} %fusion.31), channel_id=1, source_target_pairs={{8,0},{16,8},{24,16},{28,24},{20,28},{12,20},{4,12},{0,4},{9,1},{1... | collective-permute-start | bytes 786440 | tf_op jit(solution)/shard_map/ppermute | solution.py:98
  58.9 7.5 %collective-permute-start.4 = (bf16[128,1024]{0,1:T(8,128)(2,1)S(1)}, bf16[128,1024]{0,1:T(8,128)(2,1)S(1)}, u32[]{:S(2)}, u32[]{:S(2)}) collective-permute-start(bf16[128,1024]{0,1:T(8,128)(2,1)S(1)} %fusion.38), channel_id=1, source_target_pairs={{0,8},{8,16},{16,24},{24,28},{28,20},{20,12},{12,4},{4,0},{1,9},{9... | collective-permute-start | bytes 786440 | tf_op jit(solution)/shard_map/ppermute | solution.py:97
  61.4 7.8 %collective-permute-start.12 = (bf16[128,1024]{0,1:T(8,128)(2,1)S(1)}, bf16[128,1024]{0,1:T(8,128)(2,1)S(1)}, u32[]{:S(2)}, u32[]{:S(2)}) collective-permute-start(bf16[128,1024]{0,1:T(8,128)(2,1)S(1)} %fusion.30), channel_id=1, source_target_pairs={{8,0},{16,8},{24,16},{28,24},{20,28},{12,20},{4,12},{0,4},{9,1},{1... | collective-permute-start | bytes 786440 | tf_op jit(solution)/shard_map/ppermute | solution.py:98
  66.5 18.4 %copy-start.9 = (f32[4,2048]{1,0:T(4,128)S(1)}, f32[4,2048]{1,0:T(4,128)}, u32[]{:S(2)}) copy-start(f32[4,2048]{1,0:T(4,128)} %param.22) | copy-start | bytes 98308
  66.5 8.4 %collective-permute-start.5 = (bf16[128,1024]{0,1:T(8,128)(2,1)S(1)}, bf16[128,1024]{0,1:T(8,128)(2,1)S(1)}, u32[]{:S(2)}, u32[]{:S(2)}) collective-permute-start(bf16[128,1024]{0,1:T(8,128)(2,1)S(1)} %fusion.37), channel_id=1, source_target_pairs={{0,8},{8,16},{16,24},{24,28},{28,20},{20,12},{12,4},{4,0},{1,9},{9... | collective-permute-start | bytes 786440 | tf_op jit(solution)/shard_map/ppermute | solution.py:97
  69.3 8.7 %collective-permute-start.13 = (bf16[128,1024]{0,1:T(8,128)(2,1)S(1)}, bf16[128,1024]{0,1:T(8,128)(2,1)S(1)}, u32[]{:S(2)}, u32[]{:S(2)}) collective-permute-start(bf16[128,1024]{0,1:T(8,128)(2,1)S(1)} %fusion.29), channel_id=1, source_target_pairs={{8,0},{16,8},{24,16},{28,24},{20,28},{12,20},{4,12},{0,4},{9,1},{1... | collective-permute-start | bytes 786440 | tf_op jit(solution)/shard_map/ppermute | solution.py:98
  75.0 9.2 %collective-permute-start.6 = (bf16[128,1024]{0,1:T(8,128)(2,1)S(1)}, bf16[128,1024]{0,1:T(8,128)(2,1)S(1)}, u32[]{:S(2)}, u32[]{:S(2)}) collective-permute-start(bf16[128,1024]{0,1:T(8,128)(2,1)S(1)} %fusion.36), channel_id=1, source_target_pairs={{0,8},{8,16},{16,24},{24,28},{28,20},{20,12},{12,4},{4,0},{1,9},{9... | collective-permute-start | bytes 786440 | tf_op jit(solution)/shard_map/ppermute | solution.py:97
  78.1 14.6 %copy-start.10 = (s32[128]{0:T(128)S(1)}, s32[128]{0:T(128)}, u32[]{:S(2)}) copy-start(s32[128]{0:T(128)} %param.27) | copy-start | bytes 1540
  78.1 14.6 %copy-start.7 = (bf16[128,2048]{1,0:T(8,128)(2,1)S(1)}, bf16[128,2048]{1,0:T(8,128)(2,1)}, u32[]{:S(2)}) copy-start(bf16[128,2048]{1,0:T(8,128)(2,1)} %param.21) | copy-start | bytes 1572868
  78.1 6.7 %collective-permute-start.14 = (bf16[128,1024]{0,1:T(8,128)(2,1)S(1)}, bf16[128,1024]{0,1:T(8,128)(2,1)S(1)}, u32[]{:S(2)}, u32[]{:S(2)}) collective-permute-start(bf16[128,1024]{0,1:T(8,128)(2,1)S(1)} %fusion.28), channel_id=1, source_target_pairs={{8,0},{16,8},{24,16},{28,24},{20,28},{12,20},{4,12},{0,4},{9,1},{1... | collective-permute-start | bytes 786440 | tf_op jit(solution)/shard_map/ppermute | solution.py:98
  84.3 6.4 %collective-permute-start.7 = (bf16[128,1024]{0,1:T(8,128)(2,1)S(1)}, bf16[128,1024]{0,1:T(8,128)(2,1)S(1)}, u32[]{:S(2)}, u32[]{:S(2)}) collective-permute-start(bf16[128,1024]{0,1:T(8,128)(2,1)S(1)} %fusion.35), channel_id=1, source_target_pairs={{0,8},{8,16},{16,24},{24,28},{28,20},{20,12},{12,4},{4,0},{1,9},{9... | collective-permute-start | bytes 786440 | tf_op jit(solution)/shard_map/ppermute | solution.py:97
  91.0 8.1 %collective-permute-start.15 = (bf16[3,2048]{0,1:T(8,128)(2,1)S(1)}, bf16[3,2048]{0,1:T(8,128)(2,1)S(1)}, u32[]{:S(2)}, u32[]{:S(2)}) collective-permute-start(bf16[3,2048]{0,1:T(8,128)(2,1)S(1)} %pad_maximum_fusion), channel_id=1, source_target_pairs={{0,4},{4,8},{8,12},{12,16},{16,20},{20,24},{24,28},{1,5},{5,9},{9,... | collective-permute-start | bytes 36872 | tf_op jit(solution)/shard_map/ppermute | solution.py:13
  110.2 2.0 collective-permute-start.16
  112.4 14.5 %copy-start.15 = (f32[32]{0:T(128)S(1)}, f32[32]{0:T(128)}, u32[]{:S(2)}) copy-start(f32[32]{0:T(128)} %param.26) | copy-start | bytes 388
  112.4 14.4 %copy-start.16 = (s32[128]{0:T(128)S(1)}, s32[128]{0:T(128)}, u32[]{:S(2)}) copy-start(s32[128]{0:T(128)} %param.25) | copy-start | bytes 1540
  112.4 14.0 %collective-permute-start.17 = (bf16[128,2048]{1,0:T(8,128)(2,1)S(1)}, bf16[128,2048]{1,0:T(8,128)(2,1)S(1)}, u32[]{:S(2)}, u32[]{:S(2)}) collective-permute-start(bf16[128,2048]{1,0:T(8,128)(2,1)S(1)} %fusion.20), channel_id=1, source_target_pairs={{0,2},{1,3},{2,0},{3,1},{4,6},{5,7},{6,4},{7,5},{8,10},{9,11},{10,... | collective-permute-start | bytes 1572872 | tf_op jit(solution)/shard_map/ppermute | solution.py:114
  126.8 2.7 %collective-permute-start.18 = (f32[128,2048]{1,0:T(8,128)S(1)}, f32[128,2048]{1,0:T(8,128)S(1)}, u32[]{:S(2)}, u32[]{:S(2)}) collective-permute-start(f32[128,2048]{1,0:T(8,128)S(1)} %convert_add_fusion.1), channel_id=1, source_target_pairs={{0,1},{1,0},{2,3},{3,2},{4,5},{5,4},{6,7},{7,6},{8,9},{9,8},{10,11... | collective-permute-start | bytes 3145736 | tf_op jit(solution)/shard_map/ppermute | solution.py:117
  127.0 2.8 %copy-start.14 = (bf16[128,4096]{1,0:T(8,128)(2,1)S(1)}, bf16[128,4096]{1,0:T(8,128)(2,1)}, u32[]{:S(2)}) copy-start(bf16[128,4096]{1,0:T(8,128)(2,1)} %param.24) | copy-start | bytes 3145732
  129.7 12.8 %copy-start.6 = (f32[128,4096]{1,0:T(8,128)}, f32[128,4096]{1,0:T(8,128)S(1)}, u32[]{:S(2)}) copy-start(f32[128,4096]{1,0:T(8,128)S(1)} %maximum_select_fusion) | copy-start | bytes 6291460
  142.6 1.0 copy-start.1
  146.7 4.3 %copy-start.2 = (f32[128,2048]{0,1:T(8,128)S(1)}, f32[128,2048]{0,1:T(8,128)}, u32[]{:S(2)}) copy-start(f32[128,2048]{0,1:T(8,128)} %copy-done.1) | copy-start | bytes 3145732
  146.7 6.4 %collective-permute-start.19 = (f32[3,2048]{1,0:T(4,128)S(1)}, f32[3,2048]{1,0:T(4,128)S(1)}, u32[]{:S(2)}, u32[]{:S(2)}) collective-permute-start(f32[3,2048]{1,0:T(4,128)S(1)} %copy.62), channel_id=1, source_target_pairs={{4,0},{8,4},{12,8},{16,12},{20,16},{24,20},{28,24},{5,1},{9,5},{13... | collective-permute-start | bytes 73736 | tf_op jit(solution)/shard_map/ppermute | solution.py:13
  151.0 3.5 %copy-start.3 = (f32[125,2048]{0,1:T(8,128)S(1)}, f32[125,2048]{0,1:T(8,128)}, u32[]{:S(2)}) copy-start(f32[125,2048]{0,1:T(8,128)} %slice.239) | copy-start | bytes 3072004
  157.0 10.8 %collective-permute-start.27 = (bf16[128,1024]{0,1:T(8,128)(2,1)S(1)}, bf16[128,1024]{0,1:T(8,128)(2,1)S(1)}, u32[]{:S(2)}, u32[]{:S(2)}) collective-permute-start(bf16[128,1024]{0,1:T(8,128)(2,1)S(1)} %get-tuple-element.62), channel_id=1, source_target_pairs={{8,0},{16,8},{24,16},{28,24},{20,28},{12,20},{4,12},{0,4},{9,1},{1... | collective-permute-start | bytes 786440 | tf_op jit(solution)/shard_map/ppermute | solution.py:75
  160.4 8.9 %collective-permute-start.20 = (bf16[128,1024]{0,1:T(8,128)(2,1)S(1)}, bf16[128,1024]{0,1:T(8,128)(2,1)S(1)}, u32[]{:S(2)}, u32[]{:S(2)}) collective-permute-start(bf16[128,1024]{0,1:T(8,128)(2,1)S(1)} %get-tuple-element.61), channel_id=1, source_target_pairs={{0,8},{8,16},{16,24},{24,28},{28,20},{20,12},{12,4},{4,0},{1,9},{9... | collective-permute-start | bytes 786440 | tf_op jit(solution)/shard_map/ppermute | solution.py:74
  167.8 7.8 %collective-permute-start.28 = (bf16[128,1024]{0,1:T(8,128)(2,1)S(1)}, bf16[128,1024]{0,1:T(8,128)(2,1)S(1)}, u32[]{:S(2)}, u32[]{:S(2)}) collective-permute-start(bf16[128,1024]{0,1:T(8,128)(2,1)S(1)} %collective-permute-done.27), channel_id=1, source_target_pairs={{8,0},{16,8},{24,16},{28,24},{20,28},{12,20},{4,12},{0,4},{9,1},{1... | collective-permute-start | bytes 786440 | tf_op jit(solution)/shard_map/ppermute | solution.py:75
  169.3 7.2 %collective-permute-start.21 = (bf16[128,1024]{0,1:T(8,128)(2,1)S(1)}, bf16[128,1024]{0,1:T(8,128)(2,1)S(1)}, u32[]{:S(2)}, u32[]{:S(2)}) collective-permute-start(bf16[128,1024]{0,1:T(8,128)(2,1)S(1)} %collective-permute-done.20), channel_id=1, source_target_pairs={{0,8},{8,16},{16,24},{24,28},{28,20},{20,12},{12,4},{4,0},{1,9},{9... | collective-permute-start | bytes 786440 | tf_op jit(solution)/shard_map/ppermute | solution.py:74
  175.7 6.9 %collective-permute-start.29 = (bf16[128,1024]{0,1:T(8,128)(2,1)S(1)}, bf16[128,1024]{0,1:T(8,128)(2,1)S(1)}, u32[]{:S(2)}, u32[]{:S(2)}) collective-permute-start(bf16[128,1024]{0,1:T(8,128)(2,1)S(1)} %collective-permute-done.28), channel_id=1, source_target_pairs={{8,0},{16,8},{24,16},{28,24},{20,28},{12,20},{4,12},{0,4},{9,1},{1... | collective-permute-start | bytes 786440 | tf_op jit(solution)/shard_map/ppermute | solution.py:75
  176.5 6.4 %collective-permute-start.22 = (bf16[128,1024]{0,1:T(8,128)(2,1)S(1)}, bf16[128,1024]{0,1:T(8,128)(2,1)S(1)}, u32[]{:S(2)}, u32[]{:S(2)}) collective-permute-start(bf16[128,1024]{0,1:T(8,128)(2,1)S(1)} %collective-permute-done.21), channel_id=1, source_target_pairs={{0,8},{8,16},{16,24},{24,28},{28,20},{20,12},{12,4},{4,0},{1,9},{9... | collective-permute-start | bytes 786440 | tf_op jit(solution)/shard_map/ppermute | solution.py:74
  182.6 7.1 %collective-permute-start.30 = (bf16[128,1024]{0,1:T(8,128)(2,1)S(1)}, bf16[128,1024]{0,1:T(8,128)(2,1)S(1)}, u32[]{:S(2)}, u32[]{:S(2)}) collective-permute-start(bf16[128,1024]{0,1:T(8,128)(2,1)S(1)} %collective-permute-done.29), channel_id=1, source_target_pairs={{8,0},{16,8},{24,16},{28,24},{20,28},{12,20},{4,12},{0,4},{9,1},{1... | collective-permute-start | bytes 786440 | tf_op jit(solution)/shard_map/ppermute | solution.py:75
  182.9 7.9 %collective-permute-start.23 = (bf16[128,1024]{0,1:T(8,128)(2,1)S(1)}, bf16[128,1024]{0,1:T(8,128)(2,1)S(1)}, u32[]{:S(2)}, u32[]{:S(2)}) collective-permute-start(bf16[128,1024]{0,1:T(8,128)(2,1)S(1)} %collective-permute-done.22), channel_id=1, source_target_pairs={{0,8},{8,16},{16,24},{24,28},{28,20},{20,12},{12,4},{4,0},{1,9},{9... | collective-permute-start | bytes 786440 | tf_op jit(solution)/shard_map/ppermute | solution.py:74
  189.7 8.2 %collective-permute-start.31 = (bf16[128,1024]{0,1:T(8,128)(2,1)S(1)}, bf16[128,1024]{0,1:T(8,128)(2,1)S(1)}, u32[]{:S(2)}, u32[]{:S(2)}) collective-permute-start(bf16[128,1024]{0,1:T(8,128)(2,1)S(1)} %collective-permute-done.30), channel_id=1, source_target_pairs={{8,0},{16,8},{24,16},{28,24},{20,28},{12,20},{4,12},{0,4},{9,1},{1... | collective-permute-start | bytes 786440 | tf_op jit(solution)/shard_map/ppermute | solution.py:75
  190.8 9.1 %collective-permute-start.24 = (bf16[128,1024]{0,1:T(8,128)(2,1)S(1)}, bf16[128,1024]{0,1:T(8,128)(2,1)S(1)}, u32[]{:S(2)}, u32[]{:S(2)}) collective-permute-start(bf16[128,1024]{0,1:T(8,128)(2,1)S(1)} %collective-permute-done.23), channel_id=1, source_target_pairs={{0,8},{8,16},{16,24},{24,28},{28,20},{20,12},{12,4},{4,0},{1,9},{9... | collective-permute-start | bytes 786440 | tf_op jit(solution)/shard_map/ppermute | solution.py:74
  197.9 9.1 %collective-permute-start.32 = (bf16[128,1024]{0,1:T(8,128)(2,1)S(1)}, bf16[128,1024]{0,1:T(8,128)(2,1)S(1)}, u32[]{:S(2)}, u32[]{:S(2)}) collective-permute-start(bf16[128,1024]{0,1:T(8,128)(2,1)S(1)} %collective-permute-done.31), channel_id=1, source_target_pairs={{8,0},{16,8},{24,16},{28,24},{20,28},{12,20},{4,12},{0,4},{9,1},{1... | collective-permute-start | bytes 786440 | tf_op jit(solution)/shard_map/ppermute | solution.py:75
  199.9 8.9 %collective-permute-start.25 = (bf16[128,1024]{0,1:T(8,128)(2,1)S(1)}, bf16[128,1024]{0,1:T(8,128)(2,1)S(1)}, u32[]{:S(2)}, u32[]{:S(2)}) collective-permute-start(bf16[128,1024]{0,1:T(8,128)(2,1)S(1)} %collective-permute-done.24), channel_id=1, source_target_pairs={{0,8},{8,16},{16,24},{24,28},{28,20},{20,12},{12,4},{4,0},{1,9},{9... | collective-permute-start | bytes 786440 | tf_op jit(solution)/shard_map/ppermute | solution.py:74
  206.9 6.4 %collective-permute-start.33 = (bf16[128,1024]{0,1:T(8,128)(2,1)S(1)}, bf16[128,1024]{0,1:T(8,128)(2,1)S(1)}, u32[]{:S(2)}, u32[]{:S(2)}) collective-permute-start(bf16[128,1024]{0,1:T(8,128)(2,1)S(1)} %collective-permute-done.32), channel_id=1, source_target_pairs={{8,0},{16,8},{24,16},{28,24},{20,28},{12,20},{4,12},{0,4},{9,1},{1... | collective-permute-start | bytes 786440 | tf_op jit(solution)/shard_map/ppermute | solution.py:75
  208.3 5.3 %copy-start.13 = (bf16[512,2048]{1,0:T(8,128)(2,1)S(1)}, bf16[512,2048]{1,0:T(8,128)(2,1)}, u32[]{:S(2)}) copy-start(bf16[512,2048]{1,0:T(8,128)(2,1)} %param.20) | copy-start | bytes 6291460
  208.8 6.4 %collective-permute-start.26 = (bf16[128,1024]{0,1:T(8,128)(2,1)S(1)}, bf16[128,1024]{0,1:T(8,128)(2,1)S(1)}, u32[]{:S(2)}, u32[]{:S(2)}) collective-permute-start(bf16[128,1024]{0,1:T(8,128)(2,1)S(1)} %collective-permute-done.25), channel_id=1, source_target_pairs={{0,8},{8,16},{16,24},{24,28},{28,20},{20,12},{12,4},{4,0},{1,9},{9... | collective-permute-start | bytes 786440 | tf_op jit(solution)/shard_map/ppermute | solution.py:74
  217.4 2.0 collective-permute-start.34
  217.5 12.6 %copy-start.8 = (bf16[128,2048]{0,1:T(8,128)(2,1)S(1)}, bf16[128,2048]{0,1:T(8,128)(2,1)}, u32[]{:S(2)}) copy-start(bf16[128,2048]{0,1:T(8,128)(2,1)} %get-tuple-element.58) | copy-start | bytes 1572868
  219.6 8.4 %collective-permute-start.35 = (bf16[256,512]{1,0:T(8,128)(2,1)S(1)}, bf16[256,512]{1,0:T(8,128)(2,1)S(1)}, u32[]{:S(2)}, u32[]{:S(2)}) collective-permute-start(bf16[256,512]{1,0:T(8,128)(2,1)S(1)} %bitcast_convert_fusion), channel_id=1, source_target_pairs={{0,2},{1,3},{2,0},{3,1},{4,6},{5,7},{6,4},{7,5},{8,10},{9,11},{10,... | collective-permute-start | bytes 786440 | tf_op jit(solution)/shard_map/ppermute | solution.py:133
  228.1 17.2 %collective-permute-start.38 = (bf16[128,512]{1,0:T(8,128)(2,1)S(1)}, bf16[128,512]{1,0:T(8,128)(2,1)S(1)}, u32[]{:S(2)}, u32[]{:S(2)}) collective-permute-start(bf16[128,512]{1,0:T(8,128)(2,1)S(1)} %get-tuple-element.66), channel_id=1, source_target_pairs={{4,4},{5,12},{6,20},{7,28},{12,5},{13,13},{14,21},{15,29},{20,6},{... | collective-permute-start | bytes 393224 | tf_op jit(solution)/shard_map/ppermute | solution.py:45
  228.8 18.6 %collective-permute-start.39 = (bf16[128,512]{1,0:T(8,128)(2,1)S(1)}, bf16[128,512]{1,0:T(8,128)(2,1)S(1)}, u32[]{:S(2)}, u32[]{:S(2)}) collective-permute-start(bf16[128,512]{1,0:T(8,128)(2,1)S(1)} %get-tuple-element.65), channel_id=1, source_target_pairs={{4,0},{5,8},{6,16},{7,24},{12,1},{13,9},{14,17},{15,25},{20,2},{21... | collective-permute-start | bytes 393224 | tf_op jit(solution)/shard_map/ppermute | solution.py:45
  232.9 14.5 %collective-permute-start.36 = (bf16[128,512]{1,0:T(8,128)(2,1)S(1)}, bf16[128,512]{1,0:T(8,128)(2,1)S(1)}, u32[]{:S(2)}, u32[]{:S(2)}) collective-permute-start(bf16[128,512]{1,0:T(8,128)(2,1)S(1)} %get-tuple-element.66), channel_id=1, source_target_pairs={{0,4},{1,12},{2,20},{3,28},{8,5},{9,13},{10,21},{11,29},{16,6},{17... | collective-permute-start | bytes 393224 | tf_op jit(solution)/shard_map/ppermute | solution.py:45
  241.4 12.3 %collective-permute-start.37 = (bf16[128,512]{1,0:T(8,128)(2,1)S(1)}, bf16[128,512]{1,0:T(8,128)(2,1)S(1)}, u32[]{:S(2)}, u32[]{:S(2)}) collective-permute-start(bf16[128,512]{1,0:T(8,128)(2,1)S(1)} %get-tuple-element.65), channel_id=1, source_target_pairs={{0,0},{1,8},{2,16},{3,24},{8,1},{9,9},{10,17},{11,25},{16,2},{17,1... | collective-permute-start | bytes 393224 | tf_op jit(solution)/shard_map/ppermute | solution.py:45

commit v6 on v5

--- a/solution.py
+++ b/solution.py
@@ -65,22 +65,24 @@
     return count, jnp.array(order, jnp.int32), place, ahead, behind
 
 
-def ring_gather(value, axis):
+def ring_gather(value, axis, chains=2):
     count, order, place, ahead, behind = ring_place(axis)
-    half = value.shape[1] // 2
-    sent_a, sent_b = value[:, :half], value[:, half:]
-    got_a, got_b = [sent_a], [sent_b]
-    for _ in range(1, count):
-        sent_a = lax.ppermute(sent_a, axis, ahead)
-        sent_b = lax.ppermute(sent_b, axis, behind)
-        got_a.append(sent_a)
-        got_b.append(sent_b)
-    got_b = [got_b[(count - s) % count] for s in range(count)]
+    parts = jnp.split(value, 2 * chains, axis=1)
+    stacks = []
+    for number, part in enumerate(parts):
+        pairs = ahead if number < chains else behind
+        got = [part]
+        for _ in range(1, count):
+            part = lax.ppermute(part, axis, pairs)
+            got.append(part)
+        if number >= chains:
+            got = [got[(count - s) % count] for s in range(count)]
+        stacks.append(jnp.stack(got))
     sources = order[(place - jnp.arange(count)) % count]
-    return jnp.stack(got_a), jnp.stack(got_b), sources
-
-
-def ring_reduce_scatter(token_cols, weight, axis):
+    return stacks, sources
+
+
+def ring_reduce_scatter(token_cols, weight, axis, chains=2):
     count, order, place, ahead, behind = ring_place(axis)
     rows = token_cols.shape[0] // count
     blocks = token_cols.reshape(count, rows, token_cols.shape[1])
@@ -90,15 +92,18 @@
     second = jnp.take(blocks, order[(place + 1 + steps) % count], axis=0).reshape(token_cols.shape)
     own_a = jnp.dot(first, weight[:, :half], preferred_element_type=jnp.float32)
     own_b = jnp.dot(second, weight[:, half:], preferred_element_type=jnp.float32)
-    own_a = own_a.reshape(count, rows, half)
-    own_b = own_b.reshape(count, rows, weight.shape[1] - half)
-    sum_a, sum_b = own_a[0].astype(jnp.bfloat16), own_b[0].astype(jnp.bfloat16)
-    for s in range(1, count):
-        sum_a = lax.ppermute(sum_a, axis, ahead)
-        sum_b = lax.ppermute(sum_b, axis, behind)
-        sum_a = (sum_a.astype(jnp.float32) + own_a[s]).astype(jnp.bfloat16)
-        sum_b = (sum_b.astype(jnp.float32) + own_b[s]).astype(jnp.bfloat16)
-    return jnp.concatenate([sum_a, sum_b], axis=1)
+    owns = jnp.split(own_a.reshape(count, rows, half), chains, axis=2) + jnp.split(
+        own_b.reshape(count, rows, weight.shape[1] - half), chains, axis=2
+    )
+    sums = []
+    for number, own in enumerate(owns):
+        pairs = ahead if number < chains else behind
+        total = own[0].astype(jnp.bfloat16)
+        for s in range(1, count):
+            total = lax.ppermute(total, axis, pairs)
+            total = (total.astype(jnp.float32) + own[s]).astype(jnp.bfloat16)
+        sums.append(total)
+    return jnp.concatenate(sums, axis=1)
 
 def halves_of(value, dim, upper):
     low, high = jnp.split(value, 2, axis=dim)
@@ -209,12 +214,16 @@
         )
     ).astype(jnp.bfloat16)
     if moves_tokens:
-        got_a, got_b, sources = ring_gather(grad_x, "row")
-        half = grad_x.shape[1] // 2
+        stacks, sources = ring_gather(grad_x, "row")
         contract = (((2,), (1,)), ((), ()))
+        weight_parts = jnp.split(in_weight, len(stacks), axis=1)
         grad_cols = lax.dot_general(
-            got_a, in_weight[:, :half], contract, preferred_element_type=jnp.float32
-        ) + lax.dot_general(got_b, in_weight[:, half:], contract, preferred_element_type=jnp.float32)
+            stacks[0], weight_parts[0], contract, preferred_element_type=jnp.float32
+        )
+        for stack, weight_part in zip(stacks[1:], weight_parts[1:]):
+            grad_cols = grad_cols + lax.dot_general(
+                stack, weight_part, contract, preferred_element_type=jnp.float32
+            )
         grad_cols = jnp.take(grad_cols.astype(jnp.bfloat16), jnp.argsort(sources), axis=0)
         grad_cols = grad_cols.reshape(-1, grad_cols.shape[2])
         if lax.axis_size("col") == 4:

time: 255 us -> 241 us (0.945)
  waiting for transfers between devices: 134 us -> 91.7 us
  starting transfers between devices: 54.7 us -> 83.1 us
  local copies, waits for them, and re-layouts: 22.8 us -> 15.8 us
  matrix products: 26.3 us -> 33 us
    ppermute x28 -> x56, waiting for transfers between devices: 80.7 us -> 42.8 us  [the longest x28 25.7 us: ring_reduce_scatter(): total = lax.ppermute(total, axis, pairs)]
    ppermute x28 -> x56, starting transfers between devices: 29.8 us -> 59.7 us  [the longest x28 30.7 us: ring_gather(): part = lax.ppermute(part, axis, pairs)]
    unnamed x52 -> x64, local copies, waits for them, and re-layouts: 8.49 us -> 4.67 us
    slice x3, local copies, waits for them, and re-layouts: 3.95 us -> 0.26 us  [shards(): masked[offset:]]
    dot_general x1, matrix products: 1.32 us -> 4.51 us  [ring_reduce_scatter(): jnp.dot(second, weight[:, half:], preferred_element_type=jnp.float32)]
  transfers between devices with their start and end apart: 41 -> 69, of which waited for: 36 -> 48; matrix products, arithmetic and copies ran while one was open for 6% -> 7% of each run, Pallas kernels for 0% -> 0%
where the time goes in v6:
time: 241 us; the launch traced here: 240 us
  waiting for transfers between devices  91.7 us (38%)
  starting transfers between devices  83.1 us (34%)
  matrix products  33 us (14%)
  local copies, waits for them, and re-layouts  15.8 us (7%)
  other arithmetic  13.6 us (6%)
  between operations  2.85 us (1%)
    ppermute x28, starting transfers between devices, ring_gather(): part = lax.ppermute(part, axis, pairs)  30.7 us
    ppermute x28, starting transfers between devices, ring_reduce_scatter(): total = lax.ppermute(total, axis, pairs)  29 us
    ppermute x28, waiting for transfers between devices, ring_reduce_scatter(): total = lax.ppermute(total, axis, pairs)  25.7 us
    ppermute x28, waiting for transfers between devices, ring_gather(): part = lax.ppermute(part, axis, pairs)  17.1 us
    dot_general x1, matrix products, shards(): lax.dot_general(residual_grad, out_weight, (((1,), (1,)), ((), ())), pref...  14.4 us
    ppermute x1, waiting for transfers between devices, col_psum(): lax.ppermute(pair.astype(jnp.bfloat16), 'col', [(c, c ^ 2) for c in range...  13.4 us
    ppermute x4, starting transfers between devices, placed_blocks(): lax.ppermute(grad_sum[k * row_count:(k + 1) * row_count], ('row', 'col'),...  12.5 us
    ppermute x4, waiting for transfers between devices, placed_blocks(): lax.ppermute(grad_sum[k * row_count:(k + 1) * row_count], ('row', 'col'),...  8.49 us
  transfers between devices with their start and end apart: 69, of which 48 were waited for; matrix products, arithmetic and copies ran while one was open for 7% of the time, Pallas kernels for 0%

profile of v6, /device:TPU:2, one launch (start us, length us, event | category | flops | bytes accessed | tf_op | source)
XLA Modules:
  0.0 240.1 jit_solution(16755377926742624912)
XLA Ops:
  0.7 1.6 copy.26
  3.4 5.8 %all-to-all-start = ((bf16[128,8,256]{2,0,1:T(8,128)(2,1)}), bf16[128,8,256]{2,0,1:T(8,128)(2,1)S(1)}, u32[]{:S(2)}, u32[]{:S(2)}) async-start(bf16[128,8,256]{2,0,1:T(8,128)(2,1)} %copy.28), calls=%async_computation | async-start | bytes 1048576 | tf_op jit(solution)/shard_map/all_to_all | solution.py:24
  16.0 7.7 %all-to-all-done = bf16[128,8,256]{2,0,1:T(8,128)(2,1)S(1)} async-done(((bf16[128,8,256]{2,0,1:T(8,128)(2,1)}), bf16[128,8,256]{2,0,1:T(8,128)(2,1)S(1)}, u32[]{:S(2)}, u32[]{:S(2)}) %all-to-all-start) | async-done | bytes 524320 | tf_op jit(solution)/shard_map/all_to_all | solution.py:24
  25.7 1.6 maximum_select_fusion.1
  27.3 1.6 gather_fusion.4
  28.9 4.5 %fusion.113 = (bf16[8,128,1024]{2,1,0:T(8,128)(2,1)S(1)}, f32[8,128,1024]{2,1,0:T(8,128)}) fusion(bf16[512,2048]{1,0:T(8,128)(2,1)S(1)} %copy-done.2, bf16[8,128,512]{2,1,0:T(8,128)(2,1)} %gather_fusion.4, pred[8]{0:T(512)(128)(4,1)S(1)} %get-tuple-element.103), kind=kOutput, calls=%fused_computation.251 | convolution fusion | flops 1075314688 | bytes 8389120 | tf_op jit(solution)/shard_map/dot_general | solution.py:94
  33.5 1.5 collective-permute-start.15
  35.0 1.7 gather_fusion.3
  36.8 2.7 %fusion.114 = (bf16[8,128,1024]{2,1,0:T(8,128)(2,1)S(1)}, f32[8,128,1024]{2,1,0:T(8,128)S(1)}) fusion(bf16[512,2048]{1,0:T(8,128)(2,1)S(1)} %copy-done.2, bf16[8,128,512]{2,1,0:T(8,128)(2,1)} %gather_fusion.3, pred[8]{0:T(512)(128)(4,1)} %compare_and_fusion.2), kind=kOutput, calls=%fused_computation.252 | convolution fusion | flops 1075314688 | bytes 8388616 | tf_op jit(solution)/shard_map/dot_general | solution.py:93
  39.5 2.0 collective-permute-start.1
  43.1 1.5 collective-permute-start.16
  45.9 1.7 collective-permute-done.8
  47.7 1.7 collective-permute-start.2
  50.6 1.5 collective-permute-start.17
  53.5 1.4 collective-permute-done.9
  55.0 1.4 collective-permute-start.3
  57.3 1.5 collective-permute-start.18
  60.1 1.7 collective-permute-done.10
  61.8 1.7 collective-permute-start.4
  64.7 1.3 collective-permute-start.19
  66.8 3.1 %collective-permute-done.11 = bf16[128,512]{1,0:T(8,128)(2,1)S(1)} collective-permute-done((bf16[128,512]{1,0:T(8,128)(2,1)S(1)}, bf16[128,512]{1,0:T(8,128)(2,1)S(1)}, u32[]{:S(2)}, u32[]{:S(2)}) %collective-permute-start.11) | collective-permute-done | bytes 131104 | tf_op jit(solution)/shard_map/ppermute | solution.py:103
  70.0 1.8 collective-permute-start.5
  74.3 1.7 collective-permute-done.5
  75.9 2.8 %collective-permute-done.12 = bf16[128,512]{1,0:T(8,128)(2,1)S(1)} collective-permute-done((bf16[128,512]{1,0:T(8,128)(2,1)S(1)}, bf16[128,512]{1,0:T(8,128)(2,1)S(1)}, u32[]{:S(2)}, u32[]{:S(2)}) %collective-permute-start.12) | collective-permute-done | bytes 131104 | tf_op jit(solution)/shard_map/ppermute | solution.py:103
  78.8 2.1 collective-permute-start.6
  83.2 2.0 collective-permute-done.6
  85.2 2.5 %collective-permute-done.13 = bf16[128,512]{1,0:T(8,128)(2,1)S(1)} collective-permute-done((bf16[128,512]{1,0:T(8,128)(2,1)S(1)}, bf16[128,512]{1,0:T(8,128)(2,1)S(1)}, u32[]{:S(2)}, u32[]{:S(2)}) %collective-permute-start.13) | collective-permute-done | bytes 131104 | tf_op jit(solution)/shard_map/ppermute | solution.py:103
  87.8 1.8 collective-permute-start.7
  90.2 2.6 %collective-permute-done.7 = bf16[128,512]{1,0:T(8,128)(2,1)S(1)} collective-permute-done((bf16[128,512]{1,0:T(8,128)(2,1)S(1)}, bf16[128,512]{1,0:T(8,128)(2,1)S(1)}, u32[]{:S(2)}, u32[]{:S(2)}) %collective-permute-start.7) | collective-permute-done | bytes 131104 | tf_op jit(solution)/shard_map/ppermute | solution.py:103
  92.8 1.8 collective-permute-done.14
  94.7 2.4 collective-permute-start.29
  99.5 8.4 %convolution_convert_fusion = bf16[128,4096]{1,0:T(8,128)(2,1)S(1)} fusion(bf16[2048,4096]{1,0:T(8,128)(2,1)} %param.23, bf16[128,2048]{1,0:T(8,128)(2,1)S(1)} %copy-done.15, f32[128,2048]{1,0:T(8,128)S(1)} %fusion.9), kind=kOutput, calls=%fused_computation.6 | convolution fusion | flops 2150891520 | bytes 19398656 | tf_op jit(solution)/shard_map/dot_general | solution.py:177
  108.1 1.9 collective-permute-done.30
  110.8 13.4 %collective-permute-done.31 = bf16[128,2048]{1,0:T(8,128)(2,1)S(1)} collective-permute-done((bf16[128,2048]{1,0:T(8,128)(2,1)S(1)}, bf16[128,2048]{1,0:T(8,128)(2,1)S(1)}, u32[]{:S(2)}, u32[]{:S(2)}) %collective-permute-start.31) | collective-permute-done | bytes 524320 | tf_op jit(solution)/shard_map/ppermute | solution.py:119
  124.8 2.5 %collective-permute-done.32 = f32[128,2048]{1,0:T(8,128)S(1)} collective-permute-done((f32[128,2048]{1,0:T(8,128)S(1)}, f32[128,2048]{1,0:T(8,128)S(1)}, u32[]{:S(2)}, u32[]{:S(2)}) %collective-permute-start.32) | collective-permute-done | bytes 1048608 | tf_op jit(solution)/shard_map/ppermute | solution.py:122
  127.3 1.5 maximum_select_fusion
  128.8 14.4 %multiply_multiply_fusion.2 = (f32[128,2048]{1,0:T(8,128)}, f32[128,2048]{1,0:T(8,128)}, bf16[128,2048]{1,0:T(8,128)(2,1)}) fusion(f32[128]{0:T(128)S(1)} %get-tuple-element.93, f32[2048]{0:T(1024)S(1)} %bitcast.324, f32[128,2048]{1,0:T(8,128)S(1)} %fusion.9, bf16[128,2048]{1,0:T(8,128)(2,1)} %param.21, bf16[2048,4096]{1,0:T(8,128)(2,1)} %param.23, ...), kind=kOutput, calls=%fused_computation.43 | convolution fusion | flops 2155872256 | bytes 24126464 | tf_op jit(solution)/shard_map/dot_general | solution.py:190
  143.3 1.5 multiply_multiply_fusion.1
  146.6 1.3 collective-permute-start.33
  149.6 3.4 %collective-permute-done.33 = f32[3,2048]{1,0:T(4,128)S(1)} collective-permute-done((f32[3,2048]{1,0:T(4,128)S(1)}, f32[3,2048]{1,0:T(4,128)S(1)}, u32[]{:S(2)}, u32[]{:S(2)}) %collective-permute-start.33) | collective-permute-done | bytes 24608 | tf_op jit(solution)/shard_map/ppermute | solution.py:13
  153.5 3.2 %collective-permute-start.55 = (bf16[128,512]{1,0:T(8,128)(2,1)S(1)}, bf16[128,512]{1,0:T(8,128)(2,1)S(1)}, u32[]{:S(2)}, u32[]{:S(2)}) collective-permute-start(bf16[128,512]{1,0:T(8,128)(2,1)S(1)} %get-tuple-element.79), channel_id=1, source_target_pairs={{8,0},{16,8},{24,16},{28,24},{20,28},{12,20},{4,12},{0,4},{9,1},{1... | collective-permute-start | bytes 393224 | tf_op jit(solution)/shard_map/ppermute | solution.py:76
  159.4 2.3 collective-permute-done.55
  161.7 1.4 collective-permute-start.56
  163.1 1.4 collective-permute-done.48
  164.5 1.4 collective-permute-start.49
  166.5 1.8 collective-permute-start.35
  168.7 2.2 collective-permute-done.49
  170.9 1.4 collective-permute-start.50
  173.7 1.7 collective-permute-start.36
  175.8 1.4 collective-permute-done.50
  177.2 1.4 collective-permute-start.51
  179.3 1.7 collective-permute-done.36
  185.8 1.7 collective-permute-done.37
  188.4 1.2 collective-permute-start.60
  193.1 1.7 collective-permute-start.39
  196.2 1.2 collective-permute-start.54
  205.8 1.9 collective-permute-done.62
  208.6 7.7 %collective-permute-done.63 = bf16[256,512]{1,0:T(8,128)(2,1)S(1)} collective-permute-done((bf16[256,512]{1,0:T(8,128)(2,1)S(1)}, bf16[256,512]{1,0:T(8,128)(2,1)S(1)}, u32[]{:S(2)}, u32[]{:S(2)}) %collective-permute-start.63) | collective-permute-done | bytes 262176 | tf_op jit(solution)/shard_map/ppermute | solution.py:138
  217.2 1.3 collective-permute-start.67
  218.5 1.8 dynamic-slice_convert_fusion
  220.3 7.7 %collective-permute-start.64 = (bf16[128,512]{1,0:T(8,128)(2,1)S(1)}, bf16[128,512]{1,0:T(8,128)(2,1)S(1)}, u32[]{:S(2)}, u32[]{:S(2)}) collective-permute-start(bf16[128,512]{1,0:T(8,128)(2,1)S(1)} %get-tuple-element.87), channel_id=1, source_target_pairs={{0,4},{1,12},{2,20},{3,28},{8,5},{9,13},{10,21},{11,29},{16,6},{17... | collective-permute-start | bytes 393224 | tf_op jit(solution)/shard_map/ppermute | solution.py:45
  227.9 2.9 %collective-permute-start.65 = (bf16[128,512]{1,0:T(8,128)(2,1)S(1)}, bf16[128,512]{1,0:T(8,128)(2,1)S(1)}, u32[]{:S(2)}, u32[]{:S(2)}) collective-permute-start(bf16[128,512]{1,0:T(8,128)(2,1)S(1)} %get-tuple-element.86), channel_id=1, source_target_pairs={{0,0},{1,8},{2,16},{3,24},{8,1},{9,9},{10,17},{11,25},{16,2},{17,1... | collective-permute-start | bytes 393224 | tf_op jit(solution)/shard_map/ppermute | solution.py:45
  230.8 3.3 %collective-permute-done.67 = bf16[128,512]{1,0:T(8,128)(2,1)S(1)} collective-permute-done((bf16[128,512]{1,0:T(8,128)(2,1)S(1)}, bf16[128,512]{1,0:T(8,128)(2,1)S(1)}, u32[]{:S(2)}, u32[]{:S(2)}) %collective-permute-start.67) | collective-permute-done | bytes 131104 | tf_op jit(solution)/shard_map/ppermute | solution.py:45
  234.2 5.2 %collective-permute-done.65 = bf16[128,512]{1,0:T(8,128)(2,1)S(1)} collective-permute-done((bf16[128,512]{1,0:T(8,128)(2,1)S(1)}, bf16[128,512]{1,0:T(8,128)(2,1)S(1)}, u32[]{:S(2)}, u32[]{:S(2)}) %collective-permute-start.65) | collective-permute-done | bytes 131104 | tf_op jit(solution)/shard_map/ppermute | solution.py:45
  (220 shorter events, 58.9 us)
Async XLA Ops:
  3.4 20.3 %all-to-all-start = ((bf16[128,8,256]{2,0,1:T(8,128)(2,1)}), bf16[128,8,256]{2,0,1:T(8,128)(2,1)S(1)}, u32[]{:S(2)}, u32[]{:S(2)}) async-start(bf16[128,8,256]{2,0,1:T(8,128)(2,1)} %copy.28), calls=%async_computation | async-start | bytes 1048576 | tf_op jit(solution)/shard_map/all_to_all | solution.py:24
  33.5 8.6 %collective-permute-start.15 = (bf16[128,512]{1,0:T(8,128)(2,1)S(1)}, bf16[128,512]{1,0:T(8,128)(2,1)S(1)}, u32[]{:S(2)}, u32[]{:S(2)}) collective-permute-start(bf16[128,512]{1,0:T(8,128)(2,1)S(1)} %get-tuple-element.74), channel_id=1, source_target_pairs={{8,0},{16,8},{24,16},{28,24},{20,28},{12,20},{4,12},{0,4},{9,1},{1... | collective-permute-start | bytes 393224 | tf_op jit(solution)/shard_map/ppermute | solution.py:103
  35.0 7.1 %collective-permute-start.22 = (bf16[128,512]{1,0:T(8,128)(2,1)S(1)}, bf16[128,512]{1,0:T(8,128)(2,1)}, u32[]{:S(2)}, u32[]{:S(2)}) collective-permute-start(bf16[128,512]{1,0:T(8,128)(2,1)S(1)} %get-tuple-element.75), channel_id=1, source_target_pairs={{8,0},{16,8},{24,16},{28,24},{20,28},{12,20},{4,12},{0,4},{9,1},{1... | collective-permute-start | bytes 393224 | tf_op jit(solution)/shard_map/ppermute | solution.py:103
  39.5 6.4 %collective-permute-start.1 = (bf16[128,512]{1,0:T(8,128)(2,1)S(1)}, bf16[128,512]{1,0:T(8,128)(2,1)S(1)}, u32[]{:S(2)}, u32[]{:S(2)}) collective-permute-start(bf16[128,512]{1,0:T(8,128)(2,1)S(1)} %get-tuple-element.72), channel_id=1, source_target_pairs={{0,8},{8,16},{16,24},{24,28},{28,20},{20,12},{12,4},{4,0},{1,9},{9... | collective-permute-start | bytes 393224 | tf_op jit(solution)/shard_map/ppermute | solution.py:103
  41.5 6.1 %collective-permute-start.8 = (bf16[128,512]{1,0:T(8,128)(2,1)S(1)}, bf16[128,512]{1,0:T(8,128)(2,1)S(1)}, u32[]{:S(2)}, u32[]{:S(2)}) collective-permute-start(bf16[128,512]{1,0:T(8,128)(2,1)S(1)} %get-tuple-element.73), channel_id=1, source_target_pairs={{0,8},{8,16},{16,24},{24,28},{28,20},{20,12},{12,4},{4,0},{1,9},{9... | collective-permute-start | bytes 393224 | tf_op jit(solution)/shard_map/ppermute | solution.py:103
  43.1 6.9 %collective-permute-start.16 = (bf16[128,512]{1,0:T(8,128)(2,1)S(1)}, bf16[128,512]{1,0:T(8,128)(2,1)S(1)}, u32[]{:S(2)}, u32[]{:S(2)}) collective-permute-start(bf16[128,512]{1,0:T(8,128)(2,1)S(1)} %get-tuple-element.69), channel_id=1, source_target_pairs={{8,0},{16,8},{24,16},{28,24},{20,28},{12,20},{4,12},{0,4},{9,1},{1... | collective-permute-start | bytes 393224 | tf_op jit(solution)/shard_map/ppermute | solution.py:103
  44.6 6.0 %collective-permute-start.23 = (bf16[128,512]{1,0:T(8,128)(2,1)S(1)}, bf16[128,512]{1,0:T(8,128)(2,1)S(1)}, u32[]{:S(2)}, u32[]{:S(2)}) collective-permute-start(bf16[128,512]{1,0:T(8,128)(2,1)S(1)} %get-tuple-element.70), channel_id=1, source_target_pairs={{8,0},{16,8},{24,16},{28,24},{20,28},{12,20},{4,12},{0,4},{9,1},{1... | collective-permute-start | bytes 393224 | tf_op jit(solution)/shard_map/ppermute | solution.py:103
  47.7 5.9 %collective-permute-start.2 = (bf16[128,512]{1,0:T(8,128)(2,1)S(1)}, bf16[128,512]{1,0:T(8,128)(2,1)S(1)}, u32[]{:S(2)}, u32[]{:S(2)}) collective-permute-start(bf16[128,512]{1,0:T(8,128)(2,1)S(1)} %get-tuple-element.55), channel_id=1, source_target_pairs={{0,8},{8,16},{16,24},{24,28},{28,20},{20,12},{12,4},{4,0},{1,9},{9... | collective-permute-start | bytes 393224 | tf_op jit(solution)/shard_map/ppermute | solution.py:103
  49.4 5.5 %collective-permute-start.9 = (bf16[128,512]{1,0:T(8,128)(2,1)S(1)}, bf16[128,512]{1,0:T(8,128)(2,1)S(1)}, u32[]{:S(2)}, u32[]{:S(2)}) collective-permute-start(bf16[128,512]{1,0:T(8,128)(2,1)S(1)} %get-tuple-element.56), channel_id=1, source_target_pairs={{0,8},{8,16},{16,24},{24,28},{28,20},{20,12},{12,4},{4,0},{1,9},{9... | collective-permute-start | bytes 393224 | tf_op jit(solution)/shard_map/ppermute | solution.py:103
  50.6 6.4 %collective-permute-start.17 = (bf16[128,512]{1,0:T(8,128)(2,1)S(1)}, bf16[128,512]{1,0:T(8,128)(2,1)S(1)}, u32[]{:S(2)}, u32[]{:S(2)}) collective-permute-start(bf16[128,512]{1,0:T(8,128)(2,1)S(1)} %get-tuple-element.67), channel_id=1, source_target_pairs={{8,0},{16,8},{24,16},{28,24},{20,28},{12,20},{4,12},{0,4},{9,1},{1... | collective-permute-start | bytes 393224 | tf_op jit(solution)/shard_map/ppermute | solution.py:103
  52.1 5.1 %collective-permute-start.24 = (bf16[128,512]{1,0:T(8,128)(2,1)S(1)}, bf16[128,512]{1,0:T(8,128)(2,1)S(1)}, u32[]{:S(2)}, u32[]{:S(2)}) collective-permute-start(bf16[128,512]{1,0:T(8,128)(2,1)S(1)} %get-tuple-element.68), channel_id=1, source_target_pairs={{8,0},{16,8},{24,16},{28,24},{20,28},{12,20},{4,12},{0,4},{9,1},{1... | collective-permute-start | bytes 393224 | tf_op jit(solution)/shard_map/ppermute | solution.py:103
  55.0 5.0 %collective-permute-start.3 = (bf16[128,512]{1,0:T(8,128)(2,1)S(1)}, bf16[128,512]{1,0:T(8,128)(2,1)S(1)}, u32[]{:S(2)}, u32[]{:S(2)}) collective-permute-start(bf16[128,512]{1,0:T(8,128)(2,1)S(1)} %get-tuple-element.53), channel_id=1, source_target_pairs={{0,8},{8,16},{16,24},{24,28},{28,20},{20,12},{12,4},{4,0},{1,9},{9... | collective-permute-start | bytes 393224 | tf_op jit(solution)/shard_map/ppermute | solution.py:103
  56.4 5.3 %collective-permute-start.10 = (bf16[128,512]{1,0:T(8,128)(2,1)S(1)}, bf16[128,512]{1,0:T(8,128)(2,1)S(1)}, u32[]{:S(2)}, u32[]{:S(2)}) collective-permute-start(bf16[128,512]{1,0:T(8,128)(2,1)S(1)} %get-tuple-element.54), channel_id=1, source_target_pairs={{0,8},{8,16},{16,24},{24,28},{28,20},{20,12},{12,4},{4,0},{1,9},{9... | collective-permute-start | bytes 393224 | tf_op jit(solution)/shard_map/ppermute | solution.py:103
  57.3 6.8 %collective-permute-start.18 = (bf16[128,512]{1,0:T(8,128)(2,1)S(1)}, bf16[128,512]{1,0:T(8,128)(2,1)S(1)}, u32[]{:S(2)}, u32[]{:S(2)}) collective-permute-start(bf16[128,512]{1,0:T(8,128)(2,1)S(1)} %get-tuple-element.65), channel_id=1, source_target_pairs={{8,0},{16,8},{24,16},{28,24},{20,28},{12,20},{4,12},{0,4},{9,1},{1... | collective-permute-start | bytes 393224 | tf_op jit(solution)/shard_map/ppermute | solution.py:103
  58.8 5.8 %collective-permute-start.25 = (bf16[128,512]{1,0:T(8,128)(2,1)S(1)}, bf16[128,512]{1,0:T(8,128)(2,1)S(1)}, u32[]{:S(2)}, u32[]{:S(2)}) collective-permute-start(bf16[128,512]{1,0:T(8,128)(2,1)S(1)} %get-tuple-element.66), channel_id=1, source_target_pairs={{8,0},{16,8},{24,16},{28,24},{20,28},{12,20},{4,12},{0,4},{9,1},{1... | collective-permute-start | bytes 393224 | tf_op jit(solution)/shard_map/ppermute | solution.py:103
  61.8 5.0 %collective-permute-start.4 = (bf16[128,512]{1,0:T(8,128)(2,1)S(1)}, bf16[128,512]{1,0:T(8,128)(2,1)S(1)}, u32[]{:S(2)}, u32[]{:S(2)}) collective-permute-start(bf16[128,512]{1,0:T(8,128)(2,1)S(1)} %get-tuple-element.51), channel_id=1, source_target_pairs={{0,8},{8,16},{16,24},{24,28},{28,20},{20,12},{12,4},{4,0},{1,9},{9... | collective-permute-start | bytes 393224 | tf_op jit(solution)/shard_map/ppermute | solution.py:103
  63.6 6.4 %collective-permute-start.11 = (bf16[128,512]{1,0:T(8,128)(2,1)S(1)}, bf16[128,512]{1,0:T(8,128)(2,1)S(1)}, u32[]{:S(2)}, u32[]{:S(2)}) collective-permute-start(bf16[128,512]{1,0:T(8,128)(2,1)S(1)} %get-tuple-element.52), channel_id=1, source_target_pairs={{0,8},{8,16},{16,24},{24,28},{28,20},{20,12},{12,4},{4,0},{1,9},{9... | collective-permute-start | bytes 393224 | tf_op jit(solution)/shard_map/ppermute | solution.py:103
  64.7 7.7 %collective-permute-start.19 = (bf16[128,512]{1,0:T(8,128)(2,1)S(1)}, bf16[128,512]{1,0:T(8,128)(2,1)S(1)}, u32[]{:S(2)}, u32[]{:S(2)}) collective-permute-start(bf16[128,512]{1,0:T(8,128)(2,1)S(1)} %get-tuple-element.63), channel_id=1, source_target_pairs={{8,0},{16,8},{24,16},{28,24},{20,28},{12,20},{4,12},{0,4},{9,1},{1... | collective-permute-start | bytes 393224 | tf_op jit(solution)/shard_map/ppermute | solution.py:103
  66.0 6.8 %collective-permute-start.26 = (bf16[128,512]{1,0:T(8,128)(2,1)S(1)}, bf16[128,512]{1,0:T(8,128)(2,1)S(1)}, u32[]{:S(2)}, u32[]{:S(2)}) collective-permute-start(bf16[128,512]{1,0:T(8,128)(2,1)S(1)} %get-tuple-element.64), channel_id=1, source_target_pairs={{8,0},{16,8},{24,16},{28,24},{20,28},{12,20},{4,12},{0,4},{9,1},{1... | collective-permute-start | bytes 393224 | tf_op jit(solution)/shard_map/ppermute | solution.py:103
  70.0 5.9 %collective-permute-start.5 = (bf16[128,512]{1,0:T(8,128)(2,1)S(1)}, bf16[128,512]{1,0:T(8,128)(2,1)S(1)}, u32[]{:S(2)}, u32[]{:S(2)}) collective-permute-start(bf16[128,512]{1,0:T(8,128)(2,1)S(1)} %get-tuple-element.49), channel_id=1, source_target_pairs={{0,8},{8,16},{16,24},{24,28},{28,20},{20,12},{12,4},{4,0},{1,9},{9... | collective-permute-start | bytes 393224 | tf_op jit(solution)/shard_map/ppermute | solution.py:103
  71.8 6.9 %collective-permute-start.12 = (bf16[128,512]{1,0:T(8,128)(2,1)S(1)}, bf16[128,512]{1,0:T(8,128)(2,1)S(1)}, u32[]{:S(2)}, u32[]{:S(2)}) collective-permute-start(bf16[128,512]{1,0:T(8,128)(2,1)S(1)} %get-tuple-element.50), channel_id=1, source_target_pairs={{0,8},{8,16},{16,24},{24,28},{28,20},{20,12},{12,4},{4,0},{1,9},{9... | collective-permute-start | bytes 393224 | tf_op jit(solution)/shard_map/ppermute | solution.py:103
  72.9 8.6 %collective-permute-start.20 = (bf16[128,512]{1,0:T(8,128)(2,1)S(1)}, bf16[128,512]{1,0:T(8,128)(2,1)S(1)}, u32[]{:S(2)}, u32[]{:S(2)}) collective-permute-start(bf16[128,512]{1,0:T(8,128)(2,1)S(1)} %get-tuple-element.61), channel_id=1, source_target_pairs={{8,0},{16,8},{24,16},{28,24},{20,28},{12,20},{4,12},{0,4},{9,1},{1... | collective-permute-start | bytes 393224 | tf_op jit(solution)/shard_map/ppermute | solution.py:103
  74.0 7.8 %collective-permute-start.27 = (bf16[128,512]{1,0:T(8,128)(2,1)S(1)}, bf16[128,512]{1,0:T(8,128)(2,1)S(1)}, u32[]{:S(2)}, u32[]{:S(2)}) collective-permute-start(bf16[128,512]{1,0:T(8,128)(2,1)S(1)} %get-tuple-element.62), channel_id=1, source_target_pairs={{8,0},{16,8},{24,16},{28,24},{20,28},{12,20},{4,12},{0,4},{9,1},{1... | collective-permute-start | bytes 393224 | tf_op jit(solution)/shard_map/ppermute | solution.py:103
  78.8 6.3 %collective-permute-start.6 = (bf16[128,512]{1,0:T(8,128)(2,1)S(1)}, bf16[128,512]{1,0:T(8,128)(2,1)S(1)}, u32[]{:S(2)}, u32[]{:S(2)}) collective-permute-start(bf16[128,512]{1,0:T(8,128)(2,1)S(1)} %get-tuple-element.47), channel_id=1, source_target_pairs={{0,8},{8,16},{16,24},{24,28},{28,20},{20,12},{12,4},{4,0},{1,9},{9... | collective-permute-start | bytes 393224 | tf_op jit(solution)/shard_map/ppermute | solution.py:103
  80.9 6.8 %collective-permute-start.13 = (bf16[128,512]{1,0:T(8,128)(2,1)S(1)}, bf16[128,512]{1,0:T(8,128)(2,1)S(1)}, u32[]{:S(2)}, u32[]{:S(2)}) collective-permute-start(bf16[128,512]{1,0:T(8,128)(2,1)S(1)} %get-tuple-element.48), channel_id=1, source_target_pairs={{0,8},{8,16},{16,24},{24,28},{28,20},{20,12},{12,4},{4,0},{1,9},{9... | collective-permute-start | bytes 393224 | tf_op jit(solution)/shard_map/ppermute | solution.py:103
  81.9 8.2 %collective-permute-start.21 = (bf16[128,512]{1,0:T(8,128)(2,1)S(1)}, bf16[128,512]{1,0:T(8,128)(2,1)S(1)}, u32[]{:S(2)}, u32[]{:S(2)}) collective-permute-start(bf16[128,512]{1,0:T(8,128)(2,1)S(1)} %get-tuple-element.59), channel_id=1, source_target_pairs={{8,0},{16,8},{24,16},{28,24},{20,28},{12,20},{4,12},{0,4},{9,1},{1... | collective-permute-start | bytes 393224 | tf_op jit(solution)/shard_map/ppermute | solution.py:103
  83.1 7.0 %collective-permute-start.28 = (bf16[128,512]{1,0:T(8,128)(2,1)S(1)}, bf16[128,512]{1,0:T(8,128)(2,1)S(1)}, u32[]{:S(2)}, u32[]{:S(2)}) collective-permute-start(bf16[128,512]{1,0:T(8,128)(2,1)S(1)} %get-tuple-element.60), channel_id=1, source_target_pairs={{8,0},{16,8},{24,16},{28,24},{20,28},{12,20},{4,12},{0,4},{9,1},{1... | collective-permute-start | bytes 393224 | tf_op jit(solution)/shard_map/ppermute | solution.py:103
  87.8 5.0 %collective-permute-start.7 = (bf16[128,512]{1,0:T(8,128)(2,1)S(1)}, bf16[128,512]{1,0:T(8,128)(2,1)S(1)}, u32[]{:S(2)}, u32[]{:S(2)}) collective-permute-start(bf16[128,512]{1,0:T(8,128)(2,1)S(1)} %get-tuple-element.45), channel_id=1, source_target_pairs={{0,8},{8,16},{16,24},{24,28},{28,20},{20,12},{12,4},{4,0},{1,9},{9... | collective-permute-start | bytes 393224 | tf_op jit(solution)/shard_map/ppermute | solution.py:103
  89.6 5.0 %collective-permute-start.14 = (bf16[128,512]{1,0:T(8,128)(2,1)S(1)}, bf16[128,512]{1,0:T(8,128)(2,1)S(1)}, u32[]{:S(2)}, u32[]{:S(2)}) collective-permute-start(bf16[128,512]{1,0:T(8,128)(2,1)S(1)} %get-tuple-element.46), channel_id=1, source_target_pairs={{0,8},{8,16},{16,24},{24,28},{28,20},{20,12},{12,4},{4,0},{1,9},{9... | collective-permute-start | bytes 393224 | tf_op jit(solution)/shard_map/ppermute | solution.py:103
  110.2 14.0 %collective-permute-start.31 = (bf16[128,2048]{1,0:T(8,128)(2,1)S(1)}, bf16[128,2048]{1,0:T(8,128)(2,1)S(1)}, u32[]{:S(2)}, u32[]{:S(2)}) collective-permute-start(bf16[128,2048]{1,0:T(8,128)(2,1)S(1)} %fusion.27), channel_id=1, source_target_pairs={{0,2},{1,3},{2,0},{3,1},{4,6},{5,7},{6,4},{7,5},{8,10},{9,11},{10,... | collective-permute-start | bytes 1572872 | tf_op jit(solution)/shard_map/ppermute | solution.py:119
  146.6 6.4 %collective-permute-start.33 = (f32[3,2048]{1,0:T(4,128)S(1)}, f32[3,2048]{1,0:T(4,128)S(1)}, u32[]{:S(2)}, u32[]{:S(2)}) collective-permute-start(f32[3,2048]{1,0:T(4,128)S(1)} %slice_add_fusion), channel_id=1, source_target_pairs={{4,0},{8,4},{12,8},{16,12},{20,16},{24,20},{28,24},{5,1},{9,5},{13... | collective-permute-start | bytes 73736 | tf_op jit(solution)/shard_map/ppermute | solution.py:13
  153.5 8.2 %collective-permute-start.55 = (bf16[128,512]{1,0:T(8,128)(2,1)S(1)}, bf16[128,512]{1,0:T(8,128)(2,1)S(1)}, u32[]{:S(2)}, u32[]{:S(2)}) collective-permute-start(bf16[128,512]{1,0:T(8,128)(2,1)S(1)} %get-tuple-element.79), channel_id=1, source_target_pairs={{8,0},{16,8},{24,16},{28,24},{20,28},{12,20},{4,12},{0,4},{9,1},{1... | collective-permute-start | bytes 393224 | tf_op jit(solution)/shard_map/ppermute | solution.py:76
  156.7 7.8 %collective-permute-start.48 = (bf16[128,512]{1,0:T(8,128)(2,1)S(1)}, bf16[128,512]{1,0:T(8,128)(2,1)S(1)}, u32[]{:S(2)}, u32[]{:S(2)}) collective-permute-start(bf16[128,512]{1,0:T(8,128)(2,1)S(1)} %get-tuple-element.80), channel_id=1, source_target_pairs={{8,0},{16,8},{24,16},{28,24},{20,28},{12,20},{4,12},{0,4},{9,1},{1... | collective-permute-start | bytes 393224 | tf_op jit(solution)/shard_map/ppermute | solution.py:76
  157.9 7.9 %collective-permute-start.41 = (bf16[128,512]{1,0:T(8,128)(2,1)S(1)}, bf16[128,512]{1,0:T(8,128)(2,1)S(1)}, u32[]{:S(2)}, u32[]{:S(2)}) collective-permute-start(bf16[128,512]{1,0:T(8,128)(2,1)S(1)} %get-tuple-element.81), channel_id=1, source_target_pairs={{0,8},{8,16},{16,24},{24,28},{28,20},{20,12},{12,4},{4,0},{1,9},{9... | collective-permute-start | bytes 393224 | tf_op jit(solution)/shard_map/ppermute | solution.py:76
  158.7 7.8 %collective-permute-start.34 = (bf16[128,512]{1,0:T(8,128)(2,1)S(1)}, bf16[128,512]{1,0:T(8,128)(2,1)S(1)}, u32[]{:S(2)}, u32[]{:S(2)}) collective-permute-start(bf16[128,512]{1,0:T(8,128)(2,1)S(1)} %get-tuple-element.78), channel_id=1, source_target_pairs={{0,8},{8,16},{16,24},{24,28},{28,20},{20,12},{12,4},{4,0},{1,9},{9... | collective-permute-start | bytes 393224 | tf_op jit(solution)/shard_map/ppermute | solution.py:76
  161.7 6.6 %collective-permute-start.56 = (bf16[128,512]{1,0:T(8,128)(2,1)S(1)}, bf16[128,512]{1,0:T(8,128)(2,1)S(1)}, u32[]{:S(2)}, u32[]{:S(2)}) collective-permute-start(bf16[128,512]{1,0:T(8,128)(2,1)S(1)} %collective-permute-done.55), channel_id=1, source_target_pairs={{8,0},{16,8},{24,16},{28,24},{20,28},{12,20},{4,12},{0,4},{9,1},{1... | collective-permute-start | bytes 393224 | tf_op jit(solution)/shard_map/ppermute | solution.py:76
  164.5 6.4 %collective-permute-start.49 = (bf16[128,512]{1,0:T(8,128)(2,1)S(1)}, bf16[128,512]{1,0:T(8,128)(2,1)S(1)}, u32[]{:S(2)}, u32[]{:S(2)}) collective-permute-start(bf16[128,512]{1,0:T(8,128)(2,1)S(1)} %collective-permute-done.48), channel_id=1, source_target_pairs={{8,0},{16,8},{24,16},{28,24},{20,28},{12,20},{4,12},{0,4},{9,1},{1... | collective-permute-start | bytes 393224 | tf_op jit(solution)/shard_map/ppermute | solution.py:76
  165.9 6.4 %collective-permute-start.42 = (bf16[128,512]{1,0:T(8,128)(2,1)S(1)}, bf16[128,512]{1,0:T(8,128)(2,1)S(1)}, u32[]{:S(2)}, u32[]{:S(2)}) collective-permute-start(bf16[128,512]{1,0:T(8,128)(2,1)S(1)} %collective-permute-done.41), channel_id=1, source_target_pairs={{0,8},{8,16},{16,24},{24,28},{28,20},{20,12},{12,4},{4,0},{1,9},{9... | collective-permute-start | bytes 393224 | tf_op jit(solution)/shard_map/ppermute | solution.py:76
  166.5 7.1 %collective-permute-start.35 = (bf16[128,512]{1,0:T(8,128)(2,1)S(1)}, bf16[128,512]{1,0:T(8,128)(2,1)S(1)}, u32[]{:S(2)}, u32[]{:S(2)}) collective-permute-start(bf16[128,512]{1,0:T(8,128)(2,1)S(1)} %collective-permute-done.34), channel_id=1, source_target_pairs={{0,8},{8,16},{16,24},{24,28},{28,20},{20,12},{12,4},{4,0},{1,9},{9... | collective-permute-start | bytes 393224 | tf_op jit(solution)/shard_map/ppermute | solution.py:76
  168.3 7.1 %collective-permute-start.57 = (bf16[128,512]{1,0:T(8,128)(2,1)S(1)}, bf16[128,512]{1,0:T(8,128)(2,1)S(1)}, u32[]{:S(2)}, u32[]{:S(2)}) collective-permute-start(bf16[128,512]{1,0:T(8,128)(2,1)S(1)} %collective-permute-done.56), channel_id=1, source_target_pairs={{8,0},{16,8},{24,16},{28,24},{20,28},{12,20},{4,12},{0,4},{9,1},{1... | collective-permute-start | bytes 393224 | tf_op jit(solution)/shard_map/ppermute | solution.py:76
  170.9 6.3 %collective-permute-start.50 = (bf16[128,512]{1,0:T(8,128)(2,1)S(1)}, bf16[128,512]{1,0:T(8,128)(2,1)S(1)}, u32[]{:S(2)}, u32[]{:S(2)}) collective-permute-start(bf16[128,512]{1,0:T(8,128)(2,1)S(1)} %collective-permute-done.49), channel_id=1, source_target_pairs={{8,0},{16,8},{24,16},{28,24},{20,28},{12,20},{4,12},{0,4},{9,1},{1... | collective-permute-start | bytes 393224 | tf_op jit(solution)/shard_map/ppermute | solution.py:76
  172.3 6.3 %collective-permute-start.43 = (bf16[128,512]{1,0:T(8,128)(2,1)S(1)}, bf16[128,512]{1,0:T(8,128)(2,1)S(1)}, u32[]{:S(2)}, u32[]{:S(2)}) collective-permute-start(bf16[128,512]{1,0:T(8,128)(2,1)S(1)} %collective-permute-done.42), channel_id=1, source_target_pairs={{0,8},{8,16},{16,24},{24,28},{28,20},{20,12},{12,4},{4,0},{1,9},{9... | collective-permute-start | bytes 393224 | tf_op jit(solution)/shard_map/ppermute | solution.py:76
  173.7 7.3 %collective-permute-start.36 = (bf16[128,512]{1,0:T(8,128)(2,1)S(1)}, bf16[128,512]{1,0:T(8,128)(2,1)S(1)}, u32[]{:S(2)}, u32[]{:S(2)}) collective-permute-start(bf16[128,512]{1,0:T(8,128)(2,1)S(1)} %collective-permute-done.35), channel_id=1, source_target_pairs={{0,8},{8,16},{16,24},{24,28},{28,20},{20,12},{12,4},{4,0},{1,9},{9... | collective-permute-start | bytes 393224 | tf_op jit(solution)/shard_map/ppermute | solution.py:76
  175.4 6.6 %collective-permute-start.58 = (bf16[128,512]{1,0:T(8,128)(2,1)S(1)}, bf16[128,512]{1,0:T(8,128)(2,1)S(1)}, u32[]{:S(2)}, u32[]{:S(2)}) collective-permute-start(bf16[128,512]{1,0:T(8,128)(2,1)S(1)} %collective-permute-done.57), channel_id=1, source_target_pairs={{8,0},{16,8},{24,16},{28,24},{20,28},{12,20},{4,12},{0,4},{9,1},{1... | collective-permute-start | bytes 393224 | tf_op jit(solution)/shard_map/ppermute | solution.py:76
  177.2 6.6 %collective-permute-start.51 = (bf16[128,512]{1,0:T(8,128)(2,1)S(1)}, bf16[128,512]{1,0:T(8,128)(2,1)S(1)}, u32[]{:S(2)}, u32[]{:S(2)}) collective-permute-start(bf16[128,512]{1,0:T(8,128)(2,1)S(1)} %collective-permute-done.50), channel_id=1, source_target_pairs={{8,0},{16,8},{24,16},{28,24},{20,28},{12,20},{4,12},{0,4},{9,1},{1... | collective-permute-start | bytes 393224 | tf_op jit(solution)/shard_map/ppermute | solution.py:76
  178.6 6.3 %collective-permute-start.44 = (bf16[128,512]{1,0:T(8,128)(2,1)S(1)}, bf16[128,512]{1,0:T(8,128)(2,1)S(1)}, u32[]{:S(2)}, u32[]{:S(2)}) collective-permute-start(bf16[128,512]{1,0:T(8,128)(2,1)S(1)} %collective-permute-done.43), channel_id=1, source_target_pairs={{0,8},{8,16},{16,24},{24,28},{28,20},{20,12},{12,4},{4,0},{1,9},{9... | collective-permute-start | bytes 393224 | tf_op jit(solution)/shard_map/ppermute | solution.py:76
  181.0 6.6 %collective-permute-start.37 = (bf16[128,512]{1,0:T(8,128)(2,1)S(1)}, bf16[128,512]{1,0:T(8,128)(2,1)S(1)}, u32[]{:S(2)}, u32[]{:S(2)}) collective-permute-start(bf16[128,512]{1,0:T(8,128)(2,1)S(1)} %collective-permute-done.36), channel_id=1, source_target_pairs={{0,8},{8,16},{16,24},{24,28},{28,20},{20,12},{12,4},{4,0},{1,9},{9... | collective-permute-start | bytes 393224 | tf_op jit(solution)/shard_map/ppermute | solution.py:76
  182.0 6.4 %collective-permute-start.59 = (bf16[128,512]{1,0:T(8,128)(2,1)S(1)}, bf16[128,512]{1,0:T(8,128)(2,1)S(1)}, u32[]{:S(2)}, u32[]{:S(2)}) collective-permute-start(bf16[128,512]{1,0:T(8,128)(2,1)S(1)} %collective-permute-done.58), channel_id=1, source_target_pairs={{8,0},{16,8},{24,16},{28,24},{20,28},{12,20},{4,12},{0,4},{9,1},{1... | collective-permute-start | bytes 393224 | tf_op jit(solution)/shard_map/ppermute | solution.py:76
  183.8 6.7 %collective-permute-start.52 = (bf16[128,512]{1,0:T(8,128)(2,1)S(1)}, bf16[128,512]{1,0:T(8,128)(2,1)S(1)}, u32[]{:S(2)}, u32[]{:S(2)}) collective-permute-start(bf16[128,512]{1,0:T(8,128)(2,1)S(1)} %collective-permute-done.51), channel_id=1, source_target_pairs={{8,0},{16,8},{24,16},{28,24},{20,28},{12,20},{4,12},{0,4},{9,1},{1... | collective-permute-start | bytes 393224 | tf_op jit(solution)/shard_map/ppermute | solution.py:76
  184.9 6.7 %collective-permute-start.45 = (bf16[128,512]{1,0:T(8,128)(2,1)S(1)}, bf16[128,512]{1,0:T(8,128)(2,1)S(1)}, u32[]{:S(2)}, u32[]{:S(2)}) collective-permute-start(bf16[128,512]{1,0:T(8,128)(2,1)S(1)} %collective-permute-done.44), channel_id=1, source_target_pairs={{0,8},{8,16},{16,24},{24,28},{28,20},{20,12},{12,4},{4,0},{1,9},{9... | collective-permute-start | bytes 393224 | tf_op jit(solution)/shard_map/ppermute | solution.py:76
  187.6 5.5 %collective-permute-start.38 = (bf16[128,512]{1,0:T(8,128)(2,1)S(1)}, bf16[128,512]{1,0:T(8,128)(2,1)S(1)}, u32[]{:S(2)}, u32[]{:S(2)}) collective-permute-start(bf16[128,512]{1,0:T(8,128)(2,1)S(1)} %collective-permute-done.37), channel_id=1, source_target_pairs={{0,8},{8,16},{16,24},{24,28},{28,20},{20,12},{12,4},{4,0},{1,9},{9... | collective-permute-start | bytes 393224 | tf_op jit(solution)/shard_map/ppermute | solution.py:76
  188.4 6.4 %collective-permute-start.60 = (bf16[128,512]{1,0:T(8,128)(2,1)S(1)}, bf16[128,512]{1,0:T(8,128)(2,1)S(1)}, u32[]{:S(2)}, u32[]{:S(2)}) collective-permute-start(bf16[128,512]{1,0:T(8,128)(2,1)S(1)} %collective-permute-done.59), channel_id=1, source_target_pairs={{8,0},{16,8},{24,16},{28,24},{20,28},{12,20},{4,12},{0,4},{9,1},{1... | collective-permute-start | bytes 393224 | tf_op jit(solution)/shard_map/ppermute | solution.py:76
  190.5 5.7 %collective-permute-start.53 = (bf16[128,512]{1,0:T(8,128)(2,1)S(1)}, bf16[128,512]{1,0:T(8,128)(2,1)S(1)}, u32[]{:S(2)}, u32[]{:S(2)}) collective-permute-start(bf16[128,512]{1,0:T(8,128)(2,1)S(1)} %collective-permute-done.52), channel_id=1, source_target_pairs={{8,0},{16,8},{24,16},{28,24},{20,28},{12,20},{4,12},{0,4},{9,1},{1... | collective-permute-start | bytes 393224 | tf_op jit(solution)/shard_map/ppermute | solution.py:76
  191.6 6.1 %collective-permute-start.46 = (bf16[128,512]{1,0:T(8,128)(2,1)S(1)}, bf16[128,512]{1,0:T(8,128)(2,1)S(1)}, u32[]{:S(2)}, u32[]{:S(2)}) collective-permute-start(bf16[128,512]{1,0:T(8,128)(2,1)S(1)} %collective-permute-done.45), channel_id=1, source_target_pairs={{0,8},{8,16},{16,24},{24,28},{28,20},{20,12},{12,4},{4,0},{1,9},{9... | collective-permute-start | bytes 393224 | tf_op jit(solution)/shard_map/ppermute | solution.py:76
  193.1 6.0 %collective-permute-start.39 = (bf16[128,512]{1,0:T(8,128)(2,1)S(1)}, bf16[128,512]{1,0:T(8,128)(2,1)S(1)}, u32[]{:S(2)}, u32[]{:S(2)}) collective-permute-start(bf16[128,512]{1,0:T(8,128)(2,1)S(1)} %collective-permute-done.38), channel_id=1, source_target_pairs={{0,8},{8,16},{16,24},{24,28},{28,20},{20,12},{12,4},{4,0},{1,9},{9... | collective-permute-start | bytes 393224 | tf_op jit(solution)/shard_map/ppermute | solution.py:76
  194.8 5.0 %collective-permute-start.61 = (bf16[128,512]{1,0:T(8,128)(2,1)S(1)}, bf16[128,512]{1,0:T(8,128)(2,1)S(1)}, u32[]{:S(2)}, u32[]{:S(2)}) collective-permute-start(bf16[128,512]{1,0:T(8,128)(2,1)S(1)} %collective-permute-done.60), channel_id=1, source_target_pairs={{8,0},{16,8},{24,16},{28,24},{20,28},{12,20},{4,12},{0,4},{9,1},{1... | collective-permute-start | bytes 393224 | tf_op jit(solution)/shard_map/ppermute | solution.py:76
  196.2 5.0 %collective-permute-start.54 = (bf16[128,512]{1,0:T(8,128)(2,1)S(1)}, bf16[128,512]{1,0:T(8,128)(2,1)S(1)}, u32[]{:S(2)}, u32[]{:S(2)}) collective-permute-start(bf16[128,512]{1,0:T(8,128)(2,1)S(1)} %collective-permute-done.53), channel_id=1, source_target_pairs={{8,0},{16,8},{24,16},{28,24},{20,28},{12,20},{4,12},{0,4},{9,1},{1... | collective-permute-start | bytes 393224 | tf_op jit(solution)/shard_map/ppermute | solution.py:76
  197.7 5.0 %collective-permute-start.47 = (bf16[128,512]{1,0:T(8,128)(2,1)S(1)}, bf16[128,512]{1,0:T(8,128)(2,1)S(1)}, u32[]{:S(2)}, u32[]{:S(2)}) collective-permute-start(bf16[128,512]{1,0:T(8,128)(2,1)S(1)} %collective-permute-done.46), channel_id=1, source_target_pairs={{0,8},{8,16},{16,24},{24,28},{28,20},{20,12},{12,4},{4,0},{1,9},{9... | collective-permute-start | bytes 393224 | tf_op jit(solution)/shard_map/ppermute | solution.py:76
  199.1 5.0 %collective-permute-start.40 = (bf16[128,512]{1,0:T(8,128)(2,1)S(1)}, bf16[128,512]{1,0:T(8,128)(2,1)S(1)}, u32[]{:S(2)}, u32[]{:S(2)}) collective-permute-start(bf16[128,512]{1,0:T(8,128)(2,1)S(1)} %collective-permute-done.39), channel_id=1, source_target_pairs={{0,8},{8,16},{16,24},{24,28},{28,20},{20,12},{12,4},{4,0},{1,9},{9... | collective-permute-start | bytes 393224 | tf_op jit(solution)/shard_map/ppermute | solution.py:76
  208.0 8.4 %collective-permute-start.63 = (bf16[256,512]{1,0:T(8,128)(2,1)S(1)}, bf16[256,512]{1,0:T(8,128)(2,1)S(1)}, u32[]{:S(2)}, u32[]{:S(2)}) collective-permute-start(bf16[256,512]{1,0:T(8,128)(2,1)S(1)} %bitcast_convert_fusion), channel_id=1, source_target_pairs={{0,2},{1,3},{2,0},{3,1},{4,6},{5,7},{6,4},{7,5},{8,10},{9,11},{10,... | collective-permute-start | bytes 786440 | tf_op jit(solution)/shard_map/ppermute | solution.py:138
  216.5 14.3 %collective-permute-start.66 = (bf16[128,512]{1,0:T(8,128)(2,1)S(1)}, bf16[128,512]{1,0:T(8,128)(2,1)S(1)}, u32[]{:S(2)}, u32[]{:S(2)}) collective-permute-start(bf16[128,512]{1,0:T(8,128)(2,1)S(1)} %get-tuple-element.87), channel_id=1, source_target_pairs={{4,4},{5,12},{6,20},{7,28},{12,5},{13,13},{14,21},{15,29},{20,6},{... | collective-permute-start | bytes 393224 | tf_op jit(solution)/shard_map/ppermute | solution.py:45
  217.2 17.0 %collective-permute-start.67 = (bf16[128,512]{1,0:T(8,128)(2,1)S(1)}, bf16[128,512]{1,0:T(8,128)(2,1)S(1)}, u32[]{:S(2)}, u32[]{:S(2)}) collective-permute-start(bf16[128,512]{1,0:T(8,128)(2,1)S(1)} %get-tuple-element.86), channel_id=1, source_target_pairs={{4,0},{5,8},{6,16},{7,24},{12,1},{13,9},{14,17},{15,25},{20,2},{21... | collective-permute-start | bytes 393224 | tf_op jit(solution)/shard_map/ppermute | solution.py:45
  220.3 13.9 %collective-permute-start.64 = (bf16[128,512]{1,0:T(8,128)(2,1)S(1)}, bf16[128,512]{1,0:T(8,128)(2,1)S(1)}, u32[]{:S(2)}, u32[]{:S(2)}) collective-permute-start(bf16[128,512]{1,0:T(8,128)(2,1)S(1)} %get-tuple-element.87), channel_id=1, source_target_pairs={{0,4},{1,12},{2,20},{3,28},{8,5},{9,13},{10,21},{11,29},{16,6},{17... | collective-permute-start | bytes 393224 | tf_op jit(solution)/shard_map/ppermute | solution.py:45
  227.9 11.4 %collective-permute-start.65 = (bf16[128,512]{1,0:T(8,128)(2,1)S(1)}, bf16[128,512]{1,0:T(8,128)(2,1)S(1)}, u32[]{:S(2)}, u32[]{:S(2)}) collective-permute-start(bf16[128,512]{1,0:T(8,128)(2,1)S(1)} %get-tuple-element.86), channel_id=1, source_target_pairs={{0,0},{1,8},{2,16},{3,24},{8,1},{9,9},{10,17},{11,25},{16,2},{17,1... | collective-permute-start | bytes 393224 | tf_op jit(solution)/shard_map/ppermute | solution.py:45
  (24 other events, 157.6 us)

commit v7 on v6

--- a/solution.py
+++ b/solution.py
@@ -82,26 +82,34 @@
     return stacks, sources
 
 
-def ring_reduce_scatter(token_cols, weight, axis, chains=2):
+def ring_reduce_scatter(tokens, weight, axis, chains=2):
     count, order, place, ahead, behind = ring_place(axis)
-    rows = token_cols.shape[0] // count
-    blocks = token_cols.reshape(count, rows, token_cols.shape[1])
+    rows = tokens.shape[0]
+    width = tokens.shape[1] // count
+    columns = tokens.reshape(rows, count, width)
+    fetched = {0: jnp.take(columns, order[place], axis=1)}
+    for distance in sorted(range(1, count), key=lambda k: min(k, count - k)):
+        sent = jnp.take(columns, order[(place + distance) % count], axis=1)
+        cycle = ring_order(count)
+        fetched[distance] = lax.ppermute(
+            sent, axis, [(cycle[i], cycle[(i + distance) % count]) for i in range(count)]
+        )
     half = weight.shape[1] // 2
-    steps = jnp.arange(count)
-    first = jnp.take(blocks, order[(place - 1 - steps) % count], axis=0).reshape(token_cols.shape)
-    second = jnp.take(blocks, order[(place + 1 + steps) % count], axis=0).reshape(token_cols.shape)
-    own_a = jnp.dot(first, weight[:, :half], preferred_element_type=jnp.float32)
-    own_b = jnp.dot(second, weight[:, half:], preferred_element_type=jnp.float32)
-    owns = jnp.split(own_a.reshape(count, rows, half), chains, axis=2) + jnp.split(
-        own_b.reshape(count, rows, weight.shape[1] - half), chains, axis=2
-    )
+    part = half // chains
     sums = []
-    for number, own in enumerate(owns):
-        pairs = ahead if number < chains else behind
-        total = own[0].astype(jnp.bfloat16)
-        for s in range(1, count):
-            total = lax.ppermute(total, axis, pairs)
-            total = (total.astype(jnp.float32) + own[s]).astype(jnp.bfloat16)
+    for number in range(2 * chains):
+        forward = number < chains
+        pairs = ahead if forward else behind
+        cols = slice(number * part, (number + 1) * part)
+        total = None
+        for s in range(count):
+            distance = (s + 1) % count if forward else (count - 1 - s) % count
+            own = jnp.dot(fetched[distance], weight[:, cols], preferred_element_type=jnp.float32)
+            if total is None:
+                total = own.astype(jnp.bfloat16)
+            else:
+                total = lax.ppermute(total, axis, pairs)
+                total = (total.astype(jnp.float32) + own).astype(jnp.bfloat16)
         sums.append(total)
     return jnp.concatenate(sums, axis=1)
 
@@ -155,7 +163,7 @@
         and lax.axis_size("row") % lax.axis_size("col") == 0
     )
     if moves_tokens:
-        inner_x = ring_reduce_scatter(fetched_columns(tokens), in_weight, "row")
+        inner_x = ring_reduce_scatter(tokens, in_weight, "row")
     else:
         full_in = lax.all_gather(in_weight, "row", axis=0, tiled=True)
         inner_x = jnp.dot(tokens, full_in, preferred_element_type=jnp.float32).astype(jnp.bfloat16)

time: 241 us -> 273 us (1.13)
  between operations: 2.85 us -> 23.9 us
  waiting for transfers between devices: 91.7 us -> 70.8 us
  matrix products: 33 us -> 53.6 us
  starting transfers between devices: 83.1 us -> 90.8 us
  local copies, waits for them, and re-layouts: 15.8 us -> 21.8 us
  other arithmetic: 13.6 us -> 10.5 us
    dot_general x2 -> x32, matrix products: 7.17 us -> 27.1 us  [ring_reduce_scatter(): jnp.dot(fetched[distance], weight[:, cols], preferred_element_type=jnp.fl...]
    ppermute x28, waiting for transfers between devices: 25.7 us -> 13.1 us  [ring_reduce_scatter(): total = lax.ppermute(total, axis, pairs)]
    ppermute x1 -> x7, starting transfers between devices: 0.01 us -> 12.5 us  [ring_reduce_scatter(): lax.ppermute(sent, axis, [(cycle[i], cycle[(i + distance) % count]) for i...]
    select_n x1 -> x7, local copies, waits for them, and re-layouts: 1.02 us -> 8.92 us  [ring_reduce_scatter(): sent = jnp.take(columns, order[(place + distance) % count], axis=1)]
    all_to_all x1 -> x0, waiting for transfers between devices: 7.73 us -> none  [fetched_columns(): mine = lax.all_to_all(mine, 'row', 1, 0, tiled=True)]
    all_to_all x1 -> x0, starting transfers between devices: 5.83 us -> none  [fetched_columns(): mine = lax.all_to_all(mine, 'row', 1, 0, tiled=True)]
    gather x4 -> x0, local copies, waits for them, and re-layouts: 4.63 us -> none  [the longest x1 1.73 us: ring_reduce_scatter(): jnp.take(blocks, order[(place - 1 - steps) % count], axis=0)]
  transfers between devices with their start and end apart: 69 -> 74, of which waited for: 48 -> 39; matrix products, arithmetic and copies ran while one was open for 7% -> 16% of each run, Pallas kernels for 0% -> 0%
where the time goes in v7:
time: 273 us; the launch traced here: 271 us
  starting transfers between devices  90.8 us (33%)
  waiting for transfers between devices  70.8 us (26%)
  matrix products  53.6 us (20%)
  between operations  23.9 us (9%)
  local copies, waits for them, and re-layouts  21.8 us (8%)
  other arithmetic  10.5 us (4%)
    ppermute x28, starting transfers between devices, ring_gather(): part = lax.ppermute(part, axis, pairs)  29.7 us
    ppermute x28, starting transfers between devices, ring_reduce_scatter(): total = lax.ppermute(total, axis, pairs)  29.4 us
    dot_general x32, matrix products, ring_reduce_scatter(): jnp.dot(fetched[distance], weight[:, cols], preferred_element_type=jnp.fl...  27.1 us
    ppermute x28, waiting for transfers between devices, ring_gather(): part = lax.ppermute(part, axis, pairs)  17.9 us
    dot_general x1, matrix products, shards(): lax.dot_general(residual_grad, out_weight, (((1,), (1,)), ((), ())), pref...  14.7 us
    ppermute x28, waiting for transfers between devices, ring_reduce_scatter(): total = lax.ppermute(total, axis, pairs)  13.1 us
    ppermute x4, starting transfers between devices, placed_blocks(): lax.ppermute(grad_sum[k * row_count:(k + 1) * row_count], ('row', 'col'),...  13 us
    ppermute x1, waiting for transfers between devices, col_psum(): lax.ppermute(pair.astype(jnp.bfloat16), 'col', [(c, c ^ 2) for c in range...  12.9 us
  transfers between devices with their start and end apart: 74, of which 39 were waited for; matrix products, arithmetic and copies ran while one was open for 16% of the time, Pallas kernels for 0%

profile of v7, /device:TPU:2, one launch (start us, length us, event | category | flops | bytes accessed | tf_op | source)
XLA Modules:
  0.0 271.4 jit_solution(9893160067717449967)
XLA Ops:
  0.6 1.3 dynamic_slice.33
  8.8 1.7 fusion.157
  23.7 1.6 copy.31
  26.2 1.6 copy.38
  27.9 1.5 collective-permute-start.12
  29.4 1.7 copy.37
  31.0 2.6 collective-permute-start.10
  33.6 1.7 copy.36
  35.3 1.4 collective-permute-start.8
  37.5 2.3 collective-permute-start.6
  40.5 1.4 collective-permute-start.4
  46.2 1.7 copy.33
  49.8 1.6 collective-permute-start
  53.7 2.2 collective-permute-done
  57.0 1.7 collective-permute-start.2
  58.6 2.2 collective-permute-done.28
  62.8 3.0 %collective-permute-done.21 = bf16[128,512]{1,0:T(8,128)(2,1)S(1)} collective-permute-done((bf16[128,512]{1,0:T(8,128)(2,1)S(1)}, bf16[128,512]{1,0:T(8,128)(2,1)S(1)}, u32[]{:S(2)}, u32[]{:S(2)}) %collective-permute-start.21) | collective-permute-done | bytes 131104 | tf_op jit(solution)/shard_map/ppermute | solution.py:111
  67.7 1.8 collective-permute-start.1
  72.7 1.3 collective-permute-start.22
  80.9 1.3 collective-permute-start.23
  85.3 1.3 collective-permute-start.5
  89.8 1.3 collective-permute-start.24
  94.2 1.3 collective-permute-start.7
  98.6 1.3 collective-permute-start.25
  103.1 1.4 collective-permute-start.9
  105.7 1.3 collective-permute-start.26
  110.6 1.4 collective-permute-start.11
  113.2 1.4 collective-permute-start.27
  119.2 1.6 collective-permute-done.20
  120.9 2.0 collective-permute-done.13
  122.9 3.2 %collective-permute-start.35 = (bf16[3,2048]{1,0:T(4,128)(2,1)S(1)}, bf16[3,2048]{1,0:T(4,128)(2,1)S(1)}, u32[]{:S(2)}, u32[]{:S(2)}) collective-permute-start(bf16[3,2048]{1,0:T(4,128)(2,1)S(1)} %pad_maximum_fusion.1), channel_id=1, source_target_pairs={{0,4},{4,8},{8,12},{12,16},{16,20},{20,24},{24,28},{1,5},{5,9},{9,... | collective-permute-start | bytes 36872 | tf_op jit(solution)/shard_map/ppermute | solution.py:13
  128.6 8.8 %convolution_convert_fusion = bf16[128,4096]{1,0:T(8,128)(2,1)S(1)} fusion(bf16[2048,4096]{1,0:T(8,128)(2,1)} %param.23, bf16[128,2048]{1,0:T(8,128)(2,1)S(1)} %copy-done.11, f32[128,2048]{1,0:T(8,128)S(1)} %fusion.9), kind=kOutput, calls=%fused_computation.2 | convolution fusion | flops 2150891520 | bytes 19398656 | tf_op jit(solution)/shard_map/dot_general | solution.py:185
  137.6 1.9 collective-permute-done.36
  140.9 12.9 %collective-permute-done.37 = bf16[128,2048]{1,0:T(8,128)(2,1)S(1)} collective-permute-done((bf16[128,2048]{1,0:T(8,128)(2,1)S(1)}, bf16[128,2048]{1,0:T(8,128)(2,1)S(1)}, u32[]{:S(2)}, u32[]{:S(2)}) %collective-permute-start.37) | collective-permute-done | bytes 524320 | tf_op jit(solution)/shard_map/ppermute | solution.py:127
  157.0 3.1 %maximum_select_fusion = f32[128,4096]{1,0:T(8,128)} fusion(f32[128,2048]{1,0:T(8,128)S(1)} %convert_add_fusion.1, f32[128,2048]{1,0:T(8,128)} %collective-permute-done.38, pred[]{:T(512)S(6)} %eq.35), kind=kLoop, calls=%fused_computation.3 | loop fusion | flops 1572864 | bytes 4194305 | tf_op jit(solution)/shard_map/jit(_where)/select_n | solution.py:131
  160.0 14.7 %multiply_multiply_fusion.2 = (f32[128,2048]{1,0:T(8,128)}, f32[128,2048]{1,0:T(8,128)}, bf16[128,2048]{1,0:T(8,128)(2,1)}) fusion(f32[128]{0:T(128)S(1)} %get-tuple-element.68, f32[2048]{0:T(1024)S(1)} %bitcast.178, f32[128,2048]{1,0:T(8,128)} %copy-done.6, bf16[128,2048]{1,0:T(8,128)(2,1)} %param.21, bf16[2048,4096]{1,0:T(8,128)(2,1)} %param.23, ...), kind=kOutput, calls=%fused_computation.37 | convolution fusion | flops 2155872256 | bytes 24126464 | tf_op jit(solution)/shard_map/dot_general | solution.py:198
  174.8 1.5 multiply_multiply_fusion.1
  178.1 1.3 collective-permute-start.39
  181.3 2.9 %collective-permute-done.39 = f32[3,2048]{1,0:T(4,128)S(1)} collective-permute-done((f32[3,2048]{1,0:T(4,128)S(1)}, f32[3,2048]{1,0:T(4,128)S(1)}, u32[]{:S(2)}, u32[]{:S(2)}) %collective-permute-start.39) | collective-permute-done | bytes 24608 | tf_op jit(solution)/shard_map/ppermute | solution.py:13
  184.7 3.0 %collective-permute-start.61 = (bf16[128,512]{1,0:T(8,128)(2,1)S(1)}, bf16[128,512]{1,0:T(8,128)(2,1)S(1)}, u32[]{:S(2)}, u32[]{:S(2)}) collective-permute-start(bf16[128,512]{1,0:T(8,128)(2,1)S(1)} %get-tuple-element.54), channel_id=1, source_target_pairs={{8,0},{16,8},{24,16},{28,24},{20,28},{12,20},{4,12},{0,4},{9,1},{1... | collective-permute-start | bytes 393224 | tf_op jit(solution)/shard_map/ppermute | solution.py:76
  189.8 2.3 collective-permute-done.61
  192.0 1.9 collective-permute-start.62
  194.8 1.9 collective-permute-start.55
  196.9 2.1 collective-permute-start.41
  199.4 1.8 collective-permute-done.55
  201.2 1.8 collective-permute-start.56
  203.3 1.5 collective-permute-done.41
  205.4 1.7 collective-permute-start.64
  210.1 1.8 collective-permute-done.42
  212.4 1.6 collective-permute-start.65
  214.3 1.7 collective-permute-start.58
  216.4 1.6 collective-permute-done.43
  218.8 1.5 collective-permute-start.66
  220.7 1.8 collective-permute-start.59
  225.1 1.3 collective-permute-start.67
  226.5 1.6 collective-permute-start.60
  236.9 1.9 collective-permute-done.68
  239.3 8.1 %collective-permute-done.69 = bf16[256,512]{1,0:T(8,128)(2,1)S(1)} collective-permute-done((bf16[256,512]{1,0:T(8,128)(2,1)S(1)}, bf16[256,512]{1,0:T(8,128)(2,1)S(1)}, u32[]{:S(2)}, u32[]{:S(2)}) %collective-permute-start.69) | collective-permute-done | bytes 262176 | tf_op jit(solution)/shard_map/ppermute | solution.py:146
  248.2 1.3 collective-permute-start.73
  249.5 1.8 dynamic-slice_convert_fusion
  251.3 7.2 %collective-permute-start.70 = (bf16[128,512]{1,0:T(8,128)(2,1)S(1)}, bf16[128,512]{1,0:T(8,128)(2,1)S(1)}, u32[]{:S(2)}, u32[]{:S(2)}) collective-permute-start(bf16[128,512]{1,0:T(8,128)(2,1)S(1)} %get-tuple-element.62), channel_id=1, source_target_pairs={{0,4},{1,12},{2,20},{3,28},{8,5},{9,13},{10,21},{11,29},{16,6},{17... | collective-permute-start | bytes 393224 | tf_op jit(solution)/shard_map/ppermute | solution.py:45
  258.5 3.8 %collective-permute-start.71 = (bf16[128,512]{1,0:T(8,128)(2,1)S(1)}, bf16[128,512]{1,0:T(8,128)(2,1)S(1)}, u32[]{:S(2)}, u32[]{:S(2)}) collective-permute-start(bf16[128,512]{1,0:T(8,128)(2,1)S(1)} %get-tuple-element.61), channel_id=1, source_target_pairs={{0,0},{1,8},{2,16},{3,24},{8,1},{9,9},{10,17},{11,25},{16,2},{17,1... | collective-permute-start | bytes 393224 | tf_op jit(solution)/shard_map/ppermute | solution.py:45
  262.4 3.0 %collective-permute-done.73 = bf16[128,512]{1,0:T(8,128)(2,1)S(1)} collective-permute-done((bf16[128,512]{1,0:T(8,128)(2,1)S(1)}, bf16[128,512]{1,0:T(8,128)(2,1)S(1)}, u32[]{:S(2)}, u32[]{:S(2)}) %collective-permute-start.73) | collective-permute-done | bytes 131104 | tf_op jit(solution)/shard_map/ppermute | solution.py:45
  265.4 5.2 %collective-permute-done.71 = bf16[128,512]{1,0:T(8,128)(2,1)S(1)} collective-permute-done((bf16[128,512]{1,0:T(8,128)(2,1)S(1)}, bf16[128,512]{1,0:T(8,128)(2,1)S(1)}, u32[]{:S(2)}, u32[]{:S(2)}) %collective-permute-start.71) | collective-permute-done | bytes 131104 | tf_op jit(solution)/shard_map/ppermute | solution.py:45
  (235 shorter events, 83.5 us)
Async XLA Ops:
  27.9 21.9 %collective-permute-start.12 = (bf16[128,512]{1,0:T(8,128)(2,1)}, bf16[128,512]{1,0:T(8,128)(2,1)}, u32[]{:S(2)}, u32[]{:S(2)}) collective-permute-start(bf16[128,512]{1,0:T(8,128)(2,1)} %bitcast.169), channel_id=1, source_target_pairs={{0,4},{8,0},{16,8},{24,16},{28,24},{20,28},{12,20},{4,12},{1,5},{9... | collective-permute-start | bytes 393224 | tf_op jit(solution)/shard_map/ppermute | solution.py:94
  31.0 25.9 %collective-permute-start.10 = (bf16[128,512]{1,0:T(8,128)(2,1)}, bf16[128,512]{1,0:T(8,128)(2,1)}, u32[]{:S(2)}, u32[]{:S(2)}) collective-permute-start(bf16[128,512]{1,0:T(8,128)(2,1)} %bitcast.167), channel_id=1, source_target_pairs={{0,12},{8,4},{16,0},{24,8},{28,16},{20,24},{12,28},{4,20},{1,13},{... | collective-permute-start | bytes 393224 | tf_op jit(solution)/shard_map/ppermute | solution.py:94
  35.3 39.0 %collective-permute-start.8 = (bf16[128,512]{1,0:T(8,128)(2,1)}, bf16[128,512]{1,0:T(8,128)(2,1)}, u32[]{:S(2)}, u32[]{:S(2)}) collective-permute-start(bf16[128,512]{1,0:T(8,128)(2,1)} %bitcast.166), channel_id=1, source_target_pairs={{0,20},{8,12},{16,4},{24,0},{28,8},{20,16},{12,24},{4,28},{1,21},{... | collective-permute-start | bytes 393224 | tf_op jit(solution)/shard_map/ppermute | solution.py:94
  37.5 49.2 %collective-permute-start.6 = (bf16[128,512]{1,0:T(8,128)(2,1)}, bf16[128,512]{1,0:T(8,128)(2,1)}, u32[]{:S(2)}, u32[]{:S(2)}) collective-permute-start(bf16[128,512]{1,0:T(8,128)(2,1)} %bitcast.165), channel_id=1, source_target_pairs={{0,28},{8,20},{16,12},{24,4},{28,0},{20,8},{12,16},{4,24},{1,29},{... | collective-permute-start | bytes 393224 | tf_op jit(solution)/shard_map/ppermute | solution.py:94
  40.5 40.4 %collective-permute-start.4 = (bf16[128,512]{1,0:T(8,128)(2,1)}, bf16[128,512]{1,0:T(8,128)(2,1)}, u32[]{:S(2)}, u32[]{:S(2)}) collective-permute-start(bf16[128,512]{1,0:T(8,128)(2,1)} %bitcast.8), channel_id=1, source_target_pairs={{0,24},{8,28},{16,20},{24,12},{28,4},{20,0},{12,8},{4,16},{1,25},{... | collective-permute-start | bytes 393224 | tf_op jit(solution)/shard_map/ppermute | solution.py:94
  49.8 6.1 %collective-permute-start = (bf16[128,512]{1,0:T(8,128)(2,1)}, bf16[128,512]{1,0:T(8,128)(2,1)S(1)}, u32[]{:S(2)}, u32[]{:S(2)}) collective-permute-start(bf16[128,512]{1,0:T(8,128)(2,1)} %bitcast.170), channel_id=1, source_target_pairs={{0,8},{8,16},{16,24},{24,28},{28,20},{20,12},{12,4},{4,0},{1,9},{9... | collective-permute-start | bytes 393224 | tf_op jit(solution)/shard_map/ppermute | solution.py:94
  55.9 5.0 %collective-permute-start.28 = (bf16[128,512]{1,0:T(8,128)(2,1)S(1)}, bf16[128,512]{1,0:T(8,128)(2,1)S(1)}, u32[]{:S(2)}, u32[]{:S(2)}) collective-permute-start(bf16[128,512]{1,0:T(8,128)(2,1)S(1)} %convolution_convert_fusion.1), channel_id=1, source_target_pairs={{8,0},{16,8},{24,16},{28,24},{20,28},{12,20},{4,12},{0,4},{9,1},{1... | collective-permute-start | bytes 393224 | tf_op jit(solution)/shard_map/ppermute | solution.py:111
  57.0 10.7 %collective-permute-start.2 = (bf16[128,512]{1,0:T(8,128)(2,1)S(1)}, bf16[128,512]{1,0:T(8,128)(2,1)S(1)}, u32[]{:S(2)}, u32[]{:S(2)}) collective-permute-start(bf16[128,512]{1,0:T(8,128)(2,1)S(1)} %bitcast.168), channel_id=1, source_target_pairs={{0,16},{8,24},{16,28},{24,20},{28,12},{20,4},{12,0},{4,8},{1,17},{... | collective-permute-start | bytes 393224 | tf_op jit(solution)/shard_map/ppermute | solution.py:94
  67.7 5.0 %collective-permute-start.1 = (bf16[128,512]{1,0:T(8,128)(2,1)S(1)}, bf16[128,512]{1,0:T(8,128)(2,1)S(1)}, u32[]{:S(2)}, u32[]{:S(2)}) collective-permute-start(bf16[128,512]{1,0:T(8,128)(2,1)S(1)} %convolution_convert_fusion.4), channel_id=1, source_target_pairs={{0,8},{8,16},{16,24},{24,28},{28,20},{20,12},{12,4},{4,0},{1,9},{9... | collective-permute-start | bytes 393224 | tf_op jit(solution)/shard_map/ppermute | solution.py:111
  72.7 6.1 %collective-permute-start.22 = (bf16[128,512]{1,0:T(8,128)(2,1)S(1)}, bf16[128,512]{1,0:T(8,128)(2,1)S(1)}, u32[]{:S(2)}, u32[]{:S(2)}) collective-permute-start(bf16[128,512]{1,0:T(8,128)(2,1)S(1)} %add_convert_fusion.15), channel_id=1, source_target_pairs={{8,0},{16,8},{24,16},{28,24},{20,28},{12,20},{4,12},{0,4},{9,1},{1... | collective-permute-start | bytes 393224 | tf_op jit(solution)/shard_map/ppermute | solution.py:111
  74.3 8.0 %collective-permute-start.15 = (bf16[128,512]{1,0:T(8,128)(2,1)S(1)}, bf16[128,512]{1,0:T(8,128)(2,1)S(1)}, u32[]{:S(2)}, u32[]{:S(2)}) collective-permute-start(bf16[128,512]{1,0:T(8,128)(2,1)S(1)} %add_convert_fusion.22), channel_id=1, source_target_pairs={{0,8},{8,16},{16,24},{24,28},{28,20},{20,12},{12,4},{4,0},{1,9},{9... | collective-permute-start | bytes 393224 | tf_op jit(solution)/shard_map/ppermute | solution.py:111
  75.8 8.4 %collective-permute-start.3 = (bf16[128,512]{1,0:T(8,128)(2,1)S(1)}, bf16[128,512]{1,0:T(8,128)(2,1)S(1)}, u32[]{:S(2)}, u32[]{:S(2)}) collective-permute-start(bf16[128,512]{1,0:T(8,128)(2,1)S(1)} %add_convert_fusion.29), channel_id=1, source_target_pairs={{0,8},{8,16},{16,24},{24,28},{28,20},{20,12},{12,4},{4,0},{1,9},{9... | collective-permute-start | bytes 393224 | tf_op jit(solution)/shard_map/ppermute | solution.py:111
  78.8 7.9 %collective-permute-start.30 = (bf16[128,512]{1,0:T(8,128)(2,1)S(1)}, bf16[128,512]{1,0:T(8,128)(2,1)S(1)}, u32[]{:S(2)}, u32[]{:S(2)}) collective-permute-start(bf16[128,512]{1,0:T(8,128)(2,1)S(1)} %add_convert_fusion.7), channel_id=1, source_target_pairs={{8,0},{16,8},{24,16},{28,24},{20,28},{12,20},{4,12},{0,4},{9,1},{1... | collective-permute-start | bytes 393224 | tf_op jit(solution)/shard_map/ppermute | solution.py:111
  80.9 7.7 %collective-permute-start.23 = (bf16[128,512]{1,0:T(8,128)(2,1)S(1)}, bf16[128,512]{1,0:T(8,128)(2,1)S(1)}, u32[]{:S(2)}, u32[]{:S(2)}) collective-permute-start(bf16[128,512]{1,0:T(8,128)(2,1)S(1)} %add_convert_fusion.14), channel_id=1, source_target_pairs={{8,0},{16,8},{24,16},{28,24},{20,28},{12,20},{4,12},{0,4},{9,1},{1... | collective-permute-start | bytes 393224 | tf_op jit(solution)/shard_map/ppermute | solution.py:111
  83.4 7.7 %collective-permute-start.16 = (bf16[128,512]{1,0:T(8,128)(2,1)S(1)}, bf16[128,512]{1,0:T(8,128)(2,1)S(1)}, u32[]{:S(2)}, u32[]{:S(2)}) collective-permute-start(bf16[128,512]{1,0:T(8,128)(2,1)S(1)} %add_convert_fusion.21), channel_id=1, source_target_pairs={{0,8},{8,16},{16,24},{24,28},{28,20},{20,12},{12,4},{4,0},{1,9},{9... | collective-permute-start | bytes 393224 | tf_op jit(solution)/shard_map/ppermute | solution.py:111
  85.3 7.7 %collective-permute-start.5 = (bf16[128,512]{1,0:T(8,128)(2,1)S(1)}, bf16[128,512]{1,0:T(8,128)(2,1)S(1)}, u32[]{:S(2)}, u32[]{:S(2)}) collective-permute-start(bf16[128,512]{1,0:T(8,128)(2,1)S(1)} %add_convert_fusion.28), channel_id=1, source_target_pairs={{0,8},{8,16},{16,24},{24,28},{28,20},{20,12},{12,4},{4,0},{1,9},{9... | collective-permute-start | bytes 393224 | tf_op jit(solution)/shard_map/ppermute | solution.py:111
  87.8 7.7 %collective-permute-start.31 = (bf16[128,512]{1,0:T(8,128)(2,1)S(1)}, bf16[128,512]{1,0:T(8,128)(2,1)S(1)}, u32[]{:S(2)}, u32[]{:S(2)}) collective-permute-start(bf16[128,512]{1,0:T(8,128)(2,1)S(1)} %add_convert_fusion.6), channel_id=1, source_target_pairs={{8,0},{16,8},{24,16},{28,24},{20,28},{12,20},{4,12},{0,4},{9,1},{1... | collective-permute-start | bytes 393224 | tf_op jit(solution)/shard_map/ppermute | solution.py:111
  89.8 7.7 %collective-permute-start.24 = (bf16[128,512]{1,0:T(8,128)(2,1)S(1)}, bf16[128,512]{1,0:T(8,128)(2,1)S(1)}, u32[]{:S(2)}, u32[]{:S(2)}) collective-permute-start(bf16[128,512]{1,0:T(8,128)(2,1)S(1)} %add_convert_fusion.13), channel_id=1, source_target_pairs={{8,0},{16,8},{24,16},{28,24},{20,28},{12,20},{4,12},{0,4},{9,1},{1... | collective-permute-start | bytes 393224 | tf_op jit(solution)/shard_map/ppermute | solution.py:111
  92.3 7.7 %collective-permute-start.17 = (bf16[128,512]{1,0:T(8,128)(2,1)S(1)}, bf16[128,512]{1,0:T(8,128)(2,1)S(1)}, u32[]{:S(2)}, u32[]{:S(2)}) collective-permute-start(bf16[128,512]{1,0:T(8,128)(2,1)S(1)} %add_convert_fusion.20), channel_id=1, source_target_pairs={{0,8},{8,16},{16,24},{24,28},{28,20},{20,12},{12,4},{4,0},{1,9},{9... | collective-permute-start | bytes 393224 | tf_op jit(solution)/shard_map/ppermute | solution.py:111
  94.2 7.7 %collective-permute-start.7 = (bf16[128,512]{1,0:T(8,128)(2,1)S(1)}, bf16[128,512]{1,0:T(8,128)(2,1)S(1)}, u32[]{:S(2)}, u32[]{:S(2)}) collective-permute-start(bf16[128,512]{1,0:T(8,128)(2,1)S(1)} %add_convert_fusion.27), channel_id=1, source_target_pairs={{0,8},{8,16},{16,24},{24,28},{28,20},{20,12},{12,4},{4,0},{1,9},{9... | collective-permute-start | bytes 393224 | tf_op jit(solution)/shard_map/ppermute | solution.py:111
  96.7 7.8 %collective-permute-start.32 = (bf16[128,512]{1,0:T(8,128)(2,1)S(1)}, bf16[128,512]{1,0:T(8,128)(2,1)S(1)}, u32[]{:S(2)}, u32[]{:S(2)}) collective-permute-start(bf16[128,512]{1,0:T(8,128)(2,1)S(1)} %add_convert_fusion.5), channel_id=1, source_target_pairs={{8,0},{16,8},{24,16},{28,24},{20,28},{12,20},{4,12},{0,4},{9,1},{1... | collective-permute-start | bytes 393224 | tf_op jit(solution)/shard_map/ppermute | solution.py:111
  98.6 6.8 %collective-permute-start.25 = (bf16[128,512]{1,0:T(8,128)(2,1)S(1)}, bf16[128,512]{1,0:T(8,128)(2,1)S(1)}, u32[]{:S(2)}, u32[]{:S(2)}) collective-permute-start(bf16[128,512]{1,0:T(8,128)(2,1)S(1)} %add_convert_fusion.12), channel_id=1, source_target_pairs={{8,0},{16,8},{24,16},{28,24},{20,28},{12,20},{4,12},{0,4},{9,1},{1... | collective-permute-start | bytes 393224 | tf_op jit(solution)/shard_map/ppermute | solution.py:111
  101.1 6.4 %collective-permute-start.18 = (bf16[128,512]{1,0:T(8,128)(2,1)S(1)}, bf16[128,512]{1,0:T(8,128)(2,1)S(1)}, u32[]{:S(2)}, u32[]{:S(2)}) collective-permute-start(bf16[128,512]{1,0:T(8,128)(2,1)S(1)} %add_convert_fusion.19), channel_id=1, source_target_pairs={{0,8},{8,16},{16,24},{24,28},{28,20},{20,12},{12,4},{4,0},{1,9},{9... | collective-permute-start | bytes 393224 | tf_op jit(solution)/shard_map/ppermute | solution.py:111
  103.1 6.4 %collective-permute-start.9 = (bf16[128,512]{1,0:T(8,128)(2,1)S(1)}, bf16[128,512]{1,0:T(8,128)(2,1)S(1)}, u32[]{:S(2)}, u32[]{:S(2)}) collective-permute-start(bf16[128,512]{1,0:T(8,128)(2,1)S(1)} %add_convert_fusion.26), channel_id=1, source_target_pairs={{0,8},{8,16},{16,24},{24,28},{28,20},{20,12},{12,4},{4,0},{1,9},{9... | collective-permute-start | bytes 393224 | tf_op jit(solution)/shard_map/ppermute | solution.py:111
  104.8 7.2 %collective-permute-start.33 = (bf16[128,512]{1,0:T(8,128)(2,1)S(1)}, bf16[128,512]{1,0:T(8,128)(2,1)S(1)}, u32[]{:S(2)}, u32[]{:S(2)}) collective-permute-start(bf16[128,512]{1,0:T(8,128)(2,1)S(1)} %add_convert_fusion.4), channel_id=1, source_target_pairs={{8,0},{16,8},{24,16},{28,24},{20,28},{12,20},{4,12},{0,4},{9,1},{1... | collective-permute-start | bytes 393224 | tf_op jit(solution)/shard_map/ppermute | solution.py:111
  105.7 7.3 %collective-permute-start.26 = (bf16[128,512]{1,0:T(8,128)(2,1)S(1)}, bf16[128,512]{1,0:T(8,128)(2,1)S(1)}, u32[]{:S(2)}, u32[]{:S(2)}) collective-permute-start(bf16[128,512]{1,0:T(8,128)(2,1)S(1)} %add_convert_fusion.11), channel_id=1, source_target_pairs={{8,0},{16,8},{24,16},{28,24},{20,28},{12,20},{4,12},{0,4},{9,1},{1... | collective-permute-start | bytes 393224 | tf_op jit(solution)/shard_map/ppermute | solution.py:111
  108.7 5.9 %collective-permute-start.19 = (bf16[128,512]{1,0:T(8,128)(2,1)S(1)}, bf16[128,512]{1,0:T(8,128)(2,1)S(1)}, u32[]{:S(2)}, u32[]{:S(2)}) collective-permute-start(bf16[128,512]{1,0:T(8,128)(2,1)S(1)} %add_convert_fusion.18), channel_id=1, source_target_pairs={{0,8},{8,16},{16,24},{24,28},{28,20},{20,12},{12,4},{4,0},{1,9},{9... | collective-permute-start | bytes 393224 | tf_op jit(solution)/shard_map/ppermute | solution.py:111
  110.6 6.1 %collective-permute-start.11 = (bf16[128,512]{1,0:T(8,128)(2,1)S(1)}, bf16[128,512]{1,0:T(8,128)(2,1)S(1)}, u32[]{:S(2)}, u32[]{:S(2)}) collective-permute-start(bf16[128,512]{1,0:T(8,128)(2,1)S(1)} %add_convert_fusion.25), channel_id=1, source_target_pairs={{0,8},{8,16},{16,24},{24,28},{28,20},{20,12},{12,4},{4,0},{1,9},{9... | collective-permute-start | bytes 393224 | tf_op jit(solution)/shard_map/ppermute | solution.py:111
  112.3 6.8 %collective-permute-start.34 = (bf16[128,512]{1,0:T(8,128)(2,1)S(1)}, bf16[128,512]{1,0:T(8,128)(2,1)S(1)}, u32[]{:S(2)}, u32[]{:S(2)}) collective-permute-start(bf16[128,512]{1,0:T(8,128)(2,1)S(1)} %add_convert_fusion.3), channel_id=1, source_target_pairs={{8,0},{16,8},{24,16},{28,24},{20,28},{12,20},{4,12},{0,4},{9,1},{1... | collective-permute-start | bytes 393224 | tf_op jit(solution)/shard_map/ppermute | solution.py:111
  113.2 5.9 %collective-permute-start.27 = (bf16[128,512]{1,0:T(8,128)(2,1)S(1)}, bf16[128,512]{1,0:T(8,128)(2,1)S(1)}, u32[]{:S(2)}, u32[]{:S(2)}) collective-permute-start(bf16[128,512]{1,0:T(8,128)(2,1)S(1)} %add_convert_fusion.10), channel_id=1, source_target_pairs={{8,0},{16,8},{24,16},{28,24},{20,28},{12,20},{4,12},{0,4},{9,1},{1... | collective-permute-start | bytes 393224 | tf_op jit(solution)/shard_map/ppermute | solution.py:111
  115.8 5.0 %collective-permute-start.20 = (bf16[128,512]{1,0:T(8,128)(2,1)S(1)}, bf16[128,512]{1,0:T(8,128)(2,1)S(1)}, u32[]{:S(2)}, u32[]{:S(2)}) collective-permute-start(bf16[128,512]{1,0:T(8,128)(2,1)S(1)} %add_convert_fusion.17), channel_id=1, source_target_pairs={{0,8},{8,16},{16,24},{24,28},{28,20},{20,12},{12,4},{4,0},{1,9},{9... | collective-permute-start | bytes 393224 | tf_op jit(solution)/shard_map/ppermute | solution.py:111
  117.9 5.0 %collective-permute-start.13 = (bf16[128,512]{1,0:T(8,128)(2,1)S(1)}, bf16[128,512]{1,0:T(8,128)(2,1)S(1)}, u32[]{:S(2)}, u32[]{:S(2)}) collective-permute-start(bf16[128,512]{1,0:T(8,128)(2,1)S(1)} %add_convert_fusion.24), channel_id=1, source_target_pairs={{0,8},{8,16},{16,24},{24,28},{28,20},{20,12},{12,4},{4,0},{1,9},{9... | collective-permute-start | bytes 393224 | tf_op jit(solution)/shard_map/ppermute | solution.py:111
  139.8 14.0 %collective-permute-start.37 = (bf16[128,2048]{1,0:T(8,128)(2,1)S(1)}, bf16[128,2048]{1,0:T(8,128)(2,1)S(1)}, u32[]{:S(2)}, u32[]{:S(2)}) collective-permute-start(bf16[128,2048]{1,0:T(8,128)(2,1)S(1)} %fusion.17), channel_id=1, source_target_pairs={{0,2},{1,3},{2,0},{3,1},{4,6},{5,7},{6,4},{7,5},{8,10},{9,11},{10,... | collective-permute-start | bytes 1572872 | tf_op jit(solution)/shard_map/ppermute | solution.py:127
  178.1 6.1 %collective-permute-start.39 = (f32[3,2048]{1,0:T(4,128)S(1)}, f32[3,2048]{1,0:T(4,128)S(1)}, u32[]{:S(2)}, u32[]{:S(2)}) collective-permute-start(f32[3,2048]{1,0:T(4,128)S(1)} %slice_add_fusion), channel_id=1, source_target_pairs={{4,0},{8,4},{12,8},{16,12},{20,16},{24,20},{28,24},{5,1},{9,5},{13... | collective-permute-start | bytes 73736 | tf_op jit(solution)/shard_map/ppermute | solution.py:13
  184.7 7.4 %collective-permute-start.61 = (bf16[128,512]{1,0:T(8,128)(2,1)S(1)}, bf16[128,512]{1,0:T(8,128)(2,1)S(1)}, u32[]{:S(2)}, u32[]{:S(2)}) collective-permute-start(bf16[128,512]{1,0:T(8,128)(2,1)S(1)} %get-tuple-element.54), channel_id=1, source_target_pairs={{8,0},{16,8},{24,16},{28,24},{20,28},{12,20},{4,12},{0,4},{9,1},{1... | collective-permute-start | bytes 393224 | tf_op jit(solution)/shard_map/ppermute | solution.py:76
  187.6 7.2 %collective-permute-start.54 = (bf16[128,512]{1,0:T(8,128)(2,1)S(1)}, bf16[128,512]{1,0:T(8,128)(2,1)S(1)}, u32[]{:S(2)}, u32[]{:S(2)}) collective-permute-start(bf16[128,512]{1,0:T(8,128)(2,1)S(1)} %get-tuple-element.55), channel_id=1, source_target_pairs={{8,0},{16,8},{24,16},{28,24},{20,28},{12,20},{4,12},{0,4},{9,1},{1... | collective-permute-start | bytes 393224 | tf_op jit(solution)/shard_map/ppermute | solution.py:76
  188.6 8.2 %collective-permute-start.47 = (bf16[128,512]{1,0:T(8,128)(2,1)S(1)}, bf16[128,512]{1,0:T(8,128)(2,1)S(1)}, u32[]{:S(2)}, u32[]{:S(2)}) collective-permute-start(bf16[128,512]{1,0:T(8,128)(2,1)S(1)} %get-tuple-element.56), channel_id=1, source_target_pairs={{0,8},{8,16},{16,24},{24,28},{28,20},{20,12},{12,4},{4,0},{1,9},{9... | collective-permute-start | bytes 393224 | tf_op jit(solution)/shard_map/ppermute | solution.py:76
  189.6 7.2 %collective-permute-start.40 = (bf16[128,512]{1,0:T(8,128)(2,1)S(1)}, bf16[128,512]{1,0:T(8,128)(2,1)S(1)}, u32[]{:S(2)}, u32[]{:S(2)}) collective-permute-start(bf16[128,512]{1,0:T(8,128)(2,1)S(1)} %get-tuple-element.53), channel_id=1, source_target_pairs={{0,8},{8,16},{16,24},{24,28},{28,20},{20,12},{12,4},{4,0},{1,9},{9... | collective-permute-start | bytes 393224 | tf_op jit(solution)/shard_map/ppermute | solution.py:76
  192.0 7.0 %collective-permute-start.62 = (bf16[128,512]{1,0:T(8,128)(2,1)S(1)}, bf16[128,512]{1,0:T(8,128)(2,1)S(1)}, u32[]{:S(2)}, u32[]{:S(2)}) collective-permute-start(bf16[128,512]{1,0:T(8,128)(2,1)S(1)} %collective-permute-done.61), channel_id=1, source_target_pairs={{8,0},{16,8},{24,16},{28,24},{20,28},{12,20},{4,12},{0,4},{9,1},{1... | collective-permute-start | bytes 393224 | tf_op jit(solution)/shard_map/ppermute | solution.py:76
  194.8 6.4 %collective-permute-start.55 = (bf16[128,512]{1,0:T(8,128)(2,1)S(1)}, bf16[128,512]{1,0:T(8,128)(2,1)S(1)}, u32[]{:S(2)}, u32[]{:S(2)}) collective-permute-start(bf16[128,512]{1,0:T(8,128)(2,1)S(1)} %collective-permute-done.54), channel_id=1, source_target_pairs={{8,0},{16,8},{24,16},{28,24},{20,28},{12,20},{4,12},{0,4},{9,1},{1... | collective-permute-start | bytes 393224 | tf_op jit(solution)/shard_map/ppermute | solution.py:76
  196.7 6.3 %collective-permute-start.48 = (bf16[128,512]{1,0:T(8,128)(2,1)S(1)}, bf16[128,512]{1,0:T(8,128)(2,1)S(1)}, u32[]{:S(2)}, u32[]{:S(2)}) collective-permute-start(bf16[128,512]{1,0:T(8,128)(2,1)S(1)} %collective-permute-done.47), channel_id=1, source_target_pairs={{0,8},{8,16},{16,24},{24,28},{28,20},{20,12},{12,4},{4,0},{1,9},{9... | collective-permute-start | bytes 393224 | tf_op jit(solution)/shard_map/ppermute | solution.py:76
  196.9 8.0 %collective-permute-start.41 = (bf16[128,512]{1,0:T(8,128)(2,1)S(1)}, bf16[128,512]{1,0:T(8,128)(2,1)S(1)}, u32[]{:S(2)}, u32[]{:S(2)}) collective-permute-start(bf16[128,512]{1,0:T(8,128)(2,1)S(1)} %collective-permute-done.40), channel_id=1, source_target_pairs={{0,8},{8,16},{16,24},{24,28},{28,20},{20,12},{12,4},{4,0},{1,9},{9... | collective-permute-start | bytes 393224 | tf_op jit(solution)/shard_map/ppermute | solution.py:76
  199.0 6.4 %collective-permute-start.63 = (bf16[128,512]{1,0:T(8,128)(2,1)S(1)}, bf16[128,512]{1,0:T(8,128)(2,1)S(1)}, u32[]{:S(2)}, u32[]{:S(2)}) collective-permute-start(bf16[128,512]{1,0:T(8,128)(2,1)S(1)} %collective-permute-done.62), channel_id=1, source_target_pairs={{8,0},{16,8},{24,16},{28,24},{20,28},{12,20},{4,12},{0,4},{9,1},{1... | collective-permute-start | bytes 393224 | tf_op jit(solution)/shard_map/ppermute | solution.py:76
  201.2 6.9 %collective-permute-start.56 = (bf16[128,512]{1,0:T(8,128)(2,1)S(1)}, bf16[128,512]{1,0:T(8,128)(2,1)S(1)}, u32[]{:S(2)}, u32[]{:S(2)}) collective-permute-start(bf16[128,512]{1,0:T(8,128)(2,1)S(1)} %collective-permute-done.55), channel_id=1, source_target_pairs={{8,0},{16,8},{24,16},{28,24},{20,28},{12,20},{4,12},{0,4},{9,1},{1... | collective-permute-start | bytes 393224 | tf_op jit(solution)/shard_map/ppermute | solution.py:76
  203.0 6.2 %collective-permute-start.49 = (bf16[128,512]{1,0:T(8,128)(2,1)S(1)}, bf16[128,512]{1,0:T(8,128)(2,1)S(1)}, u32[]{:S(2)}, u32[]{:S(2)}) collective-permute-start(bf16[128,512]{1,0:T(8,128)(2,1)S(1)} %collective-permute-done.48), channel_id=1, source_target_pairs={{0,8},{8,16},{16,24},{24,28},{28,20},{20,12},{12,4},{4,0},{1,9},{9... | collective-permute-start | bytes 393224 | tf_op jit(solution)/shard_map/ppermute | solution.py:76
  204.9 7.0 %collective-permute-start.42 = (bf16[128,512]{1,0:T(8,128)(2,1)S(1)}, bf16[128,512]{1,0:T(8,128)(2,1)S(1)}, u32[]{:S(2)}, u32[]{:S(2)}) collective-permute-start(bf16[128,512]{1,0:T(8,128)(2,1)S(1)} %collective-permute-done.41), channel_id=1, source_target_pairs={{0,8},{8,16},{16,24},{24,28},{28,20},{20,12},{12,4},{4,0},{1,9},{9... | collective-permute-start | bytes 393224 | tf_op jit(solution)/shard_map/ppermute | solution.py:76
  205.4 6.9 %collective-permute-start.64 = (bf16[128,512]{1,0:T(8,128)(2,1)S(1)}, bf16[128,512]{1,0:T(8,128)(2,1)S(1)}, u32[]{:S(2)}, u32[]{:S(2)}) collective-permute-start(bf16[128,512]{1,0:T(8,128)(2,1)S(1)} %collective-permute-done.63), channel_id=1, source_target_pairs={{8,0},{16,8},{24,16},{28,24},{20,28},{12,20},{4,12},{0,4},{9,1},{1... | collective-permute-start | bytes 393224 | tf_op jit(solution)/shard_map/ppermute | solution.py:76
  208.1 6.2 %collective-permute-start.57 = (bf16[128,512]{1,0:T(8,128)(2,1)S(1)}, bf16[128,512]{1,0:T(8,128)(2,1)S(1)}, u32[]{:S(2)}, u32[]{:S(2)}) collective-permute-start(bf16[128,512]{1,0:T(8,128)(2,1)S(1)} %collective-permute-done.56), channel_id=1, source_target_pairs={{8,0},{16,8},{24,16},{28,24},{20,28},{12,20},{4,12},{0,4},{9,1},{1... | collective-permute-start | bytes 393224 | tf_op jit(solution)/shard_map/ppermute | solution.py:76
  209.2 6.9 %collective-permute-start.50 = (bf16[128,512]{1,0:T(8,128)(2,1)S(1)}, bf16[128,512]{1,0:T(8,128)(2,1)S(1)}, u32[]{:S(2)}, u32[]{:S(2)}) collective-permute-start(bf16[128,512]{1,0:T(8,128)(2,1)S(1)} %collective-permute-done.49), channel_id=1, source_target_pairs={{0,8},{8,16},{16,24},{24,28},{28,20},{20,12},{12,4},{4,0},{1,9},{9... | collective-permute-start | bytes 393224 | tf_op jit(solution)/shard_map/ppermute | solution.py:76
  211.9 6.1 %collective-permute-start.43 = (bf16[128,512]{1,0:T(8,128)(2,1)S(1)}, bf16[128,512]{1,0:T(8,128)(2,1)S(1)}, u32[]{:S(2)}, u32[]{:S(2)}) collective-permute-start(bf16[128,512]{1,0:T(8,128)(2,1)S(1)} %collective-permute-done.42), channel_id=1, source_target_pairs={{0,8},{8,16},{16,24},{24,28},{28,20},{20,12},{12,4},{4,0},{1,9},{9... | collective-permute-start | bytes 393224 | tf_op jit(solution)/shard_map/ppermute | solution.py:76
  212.4 6.5 %collective-permute-start.65 = (bf16[128,512]{1,0:T(8,128)(2,1)S(1)}, bf16[128,512]{1,0:T(8,128)(2,1)S(1)}, u32[]{:S(2)}, u32[]{:S(2)}) collective-permute-start(bf16[128,512]{1,0:T(8,128)(2,1)S(1)} %collective-permute-done.64), channel_id=1, source_target_pairs={{8,0},{16,8},{24,16},{28,24},{20,28},{12,20},{4,12},{0,4},{9,1},{1... | collective-permute-start | bytes 393224 | tf_op jit(solution)/shard_map/ppermute | solution.py:76
  214.3 6.4 %collective-permute-start.58 = (bf16[128,512]{1,0:T(8,128)(2,1)S(1)}, bf16[128,512]{1,0:T(8,128)(2,1)S(1)}, u32[]{:S(2)}, u32[]{:S(2)}) collective-permute-start(bf16[128,512]{1,0:T(8,128)(2,1)S(1)} %collective-permute-done.57), channel_id=1, source_target_pairs={{8,0},{16,8},{24,16},{28,24},{20,28},{12,20},{4,12},{0,4},{9,1},{1... | collective-permute-start | bytes 393224 | tf_op jit(solution)/shard_map/ppermute | solution.py:76
  216.1 6.4 %collective-permute-start.51 = (bf16[128,512]{1,0:T(8,128)(2,1)S(1)}, bf16[128,512]{1,0:T(8,128)(2,1)S(1)}, u32[]{:S(2)}, u32[]{:S(2)}) collective-permute-start(bf16[128,512]{1,0:T(8,128)(2,1)S(1)} %collective-permute-done.50), channel_id=1, source_target_pairs={{0,8},{8,16},{16,24},{24,28},{28,20},{20,12},{12,4},{4,0},{1,9},{9... | collective-permute-start | bytes 393224 | tf_op jit(solution)/shard_map/ppermute | solution.py:76
  218.0 5.8 %collective-permute-start.44 = (bf16[128,512]{1,0:T(8,128)(2,1)S(1)}, bf16[128,512]{1,0:T(8,128)(2,1)S(1)}, u32[]{:S(2)}, u32[]{:S(2)}) collective-permute-start(bf16[128,512]{1,0:T(8,128)(2,1)S(1)} %collective-permute-done.43), channel_id=1, source_target_pairs={{0,8},{8,16},{16,24},{24,28},{28,20},{20,12},{12,4},{4,0},{1,9},{9... | collective-permute-start | bytes 393224 | tf_op jit(solution)/shard_map/ppermute | solution.py:76
  218.8 6.3 %collective-permute-start.66 = (bf16[128,512]{1,0:T(8,128)(2,1)S(1)}, bf16[128,512]{1,0:T(8,128)(2,1)S(1)}, u32[]{:S(2)}, u32[]{:S(2)}) collective-permute-start(bf16[128,512]{1,0:T(8,128)(2,1)S(1)} %collective-permute-done.65), channel_id=1, source_target_pairs={{8,0},{16,8},{24,16},{28,24},{20,28},{12,20},{4,12},{0,4},{9,1},{1... | collective-permute-start | bytes 393224 | tf_op jit(solution)/shard_map/ppermute | solution.py:76
  220.7 5.8 %collective-permute-start.59 = (bf16[128,512]{1,0:T(8,128)(2,1)S(1)}, bf16[128,512]{1,0:T(8,128)(2,1)S(1)}, u32[]{:S(2)}, u32[]{:S(2)}) collective-permute-start(bf16[128,512]{1,0:T(8,128)(2,1)S(1)} %collective-permute-done.58), channel_id=1, source_target_pairs={{8,0},{16,8},{24,16},{28,24},{20,28},{12,20},{4,12},{0,4},{9,1},{1... | collective-permute-start | bytes 393224 | tf_op jit(solution)/shard_map/ppermute | solution.py:76
  222.4 6.3 %collective-permute-start.52 = (bf16[128,512]{1,0:T(8,128)(2,1)S(1)}, bf16[128,512]{1,0:T(8,128)(2,1)S(1)}, u32[]{:S(2)}, u32[]{:S(2)}) collective-permute-start(bf16[128,512]{1,0:T(8,128)(2,1)S(1)} %collective-permute-done.51), channel_id=1, source_target_pairs={{0,8},{8,16},{16,24},{24,28},{28,20},{20,12},{12,4},{4,0},{1,9},{9... | collective-permute-start | bytes 393224 | tf_op jit(solution)/shard_map/ppermute | solution.py:76
  223.8 6.3 %collective-permute-start.45 = (bf16[128,512]{1,0:T(8,128)(2,1)S(1)}, bf16[128,512]{1,0:T(8,128)(2,1)S(1)}, u32[]{:S(2)}, u32[]{:S(2)}) collective-permute-start(bf16[128,512]{1,0:T(8,128)(2,1)S(1)} %collective-permute-done.44), channel_id=1, source_target_pairs={{0,8},{8,16},{16,24},{24,28},{28,20},{20,12},{12,4},{4,0},{1,9},{9... | collective-permute-start | bytes 393224 | tf_op jit(solution)/shard_map/ppermute | solution.py:76
  225.1 5.3 %collective-permute-start.67 = (bf16[128,512]{1,0:T(8,128)(2,1)S(1)}, bf16[128,512]{1,0:T(8,128)(2,1)S(1)}, u32[]{:S(2)}, u32[]{:S(2)}) collective-permute-start(bf16[128,512]{1,0:T(8,128)(2,1)S(1)} %collective-permute-done.66), channel_id=1, source_target_pairs={{8,0},{16,8},{24,16},{28,24},{20,28},{12,20},{4,12},{0,4},{9,1},{1... | collective-permute-start | bytes 393224 | tf_op jit(solution)/shard_map/ppermute | solution.py:76
  239.0 8.4 %collective-permute-start.69 = (bf16[256,512]{1,0:T(8,128)(2,1)S(1)}, bf16[256,512]{1,0:T(8,128)(2,1)S(1)}, u32[]{:S(2)}, u32[]{:S(2)}) collective-permute-start(bf16[256,512]{1,0:T(8,128)(2,1)S(1)} %bitcast_convert_fusion), channel_id=1, source_target_pairs={{0,2},{1,3},{2,0},{3,1},{4,6},{5,7},{6,4},{7,5},{8,10},{9,11},{10,... | collective-permute-start | bytes 786440 | tf_op jit(solution)/shard_map/ppermute | solution.py:146
  247.5 14.9 %collective-permute-start.72 = (bf16[128,512]{1,0:T(8,128)(2,1)S(1)}, bf16[128,512]{1,0:T(8,128)(2,1)S(1)}, u32[]{:S(2)}, u32[]{:S(2)}) collective-permute-start(bf16[128,512]{1,0:T(8,128)(2,1)S(1)} %get-tuple-element.62), channel_id=1, source_target_pairs={{4,4},{5,12},{6,20},{7,28},{12,5},{13,13},{14,21},{15,29},{20,6},{... | collective-permute-start | bytes 393224 | tf_op jit(solution)/shard_map/ppermute | solution.py:45
  248.2 17.2 %collective-permute-start.73 = (bf16[128,512]{1,0:T(8,128)(2,1)S(1)}, bf16[128,512]{1,0:T(8,128)(2,1)S(1)}, u32[]{:S(2)}, u32[]{:S(2)}) collective-permute-start(bf16[128,512]{1,0:T(8,128)(2,1)S(1)} %get-tuple-element.61), channel_id=1, source_target_pairs={{4,0},{5,8},{6,16},{7,24},{12,1},{13,9},{14,17},{15,25},{20,2},{21... | collective-permute-start | bytes 393224 | tf_op jit(solution)/shard_map/ppermute | solution.py:45
  251.3 14.2 %collective-permute-start.70 = (bf16[128,512]{1,0:T(8,128)(2,1)S(1)}, bf16[128,512]{1,0:T(8,128)(2,1)S(1)}, u32[]{:S(2)}, u32[]{:S(2)}) collective-permute-start(bf16[128,512]{1,0:T(8,128)(2,1)S(1)} %get-tuple-element.62), channel_id=1, source_target_pairs={{0,4},{1,12},{2,20},{3,28},{8,5},{9,13},{10,21},{11,29},{16,6},{17... | collective-permute-start | bytes 393224 | tf_op jit(solution)/shard_map/ppermute | solution.py:45
  258.5 12.1 %collective-permute-start.71 = (bf16[128,512]{1,0:T(8,128)(2,1)S(1)}, bf16[128,512]{1,0:T(8,128)(2,1)S(1)}, u32[]{:S(2)}, u32[]{:S(2)}) collective-permute-start(bf16[128,512]{1,0:T(8,128)(2,1)S(1)} %get-tuple-element.61), channel_id=1, source_target_pairs={{0,0},{1,8},{2,16},{3,24},{8,1},{9,9},{10,17},{11,25},{16,2},{17,1... | collective-permute-start | bytes 393224 | tf_op jit(solution)/shard_map/ppermute | solution.py:45
  (24 other events, 165.6 us)

commit v8 on v6

--- a/solution.py
+++ b/solution.py
@@ -65,9 +65,10 @@
     return count, jnp.array(order, jnp.int32), place, ahead, behind
 
 
-def ring_gather(value, axis, chains=2):
+def ring_gather(value, axis):
     count, order, place, ahead, behind = ring_place(axis)
-    parts = jnp.split(value, 2 * chains, axis=1)
+    parts = value
+    chains = len(parts) // 2
     stacks = []
     for number, part in enumerate(parts):
         pairs = ahead if number < chains else behind
@@ -187,34 +188,44 @@
         out_total = lax.psum(partial_value.astype(jnp.bfloat16), "col").astype(jnp.float32)
     out_block = lax.dynamic_slice_in_dim(out_total, col_start, columns, 1)
     residual_grad = (token_weight * (out_total - target.astype(jnp.float32))).astype(jnp.bfloat16)
-    grad_mixed = lax.dot_general(
-        residual_grad, out_weight, (((1,), (1,)), ((), ())), preferred_element_type=jnp.float32
-    )
-    grad_conv = grad_mixed * gate_act * silu_grad(conv_sum)
-    grad_gate = (grad_mixed * conv_act * silu_grad(gate_value)).astype(jnp.bfloat16)
-    local_grad = conv_weight[0][None, :] * grad_conv
-    spill_over = jnp.zeros((margin, inner_width), jnp.float32)
-    for offset in range(1, CONV):
-        masked = (
-            conv_weight[offset][None, :]
-            * grad_conv
-            * (doc_pos >= offset).astype(jnp.float32)[:, None]
-        )
-        local_grad = local_grad + jnp.concatenate(
-            [masked[offset:], jnp.zeros((offset, inner_width), jnp.float32)], axis=0
-        )
-        spill_over = spill_over + jnp.concatenate(
-            [jnp.zeros((margin - offset, inner_width), jnp.float32), masked[:offset]], axis=0
-        )
-    from_next = passed_along(spill_over, "row", -1)
-    grad_x = (
-        local_grad
-        + jnp.concatenate(
-            [jnp.zeros((row_count - margin, inner_width), jnp.float32), from_next], axis=0
-        )
-    ).astype(jnp.bfloat16)
+    def backward_part(cols):
+        width = cols.stop - cols.start
+        mixed_grad = lax.dot_general(
+            residual_grad, out_weight[cols], (((1,), (1,)), ((), ())), preferred_element_type=jnp.float32
+        )
+        grad_conv = mixed_grad * gate_act[:, cols] * silu_grad(conv_sum[:, cols])
+        gate_grad = (mixed_grad * conv_act[:, cols] * silu_grad(gate_value[:, cols])).astype(jnp.bfloat16)
+        local_grad = conv_weight[0][None, cols] * grad_conv
+        spill_over = jnp.zeros((margin, width), jnp.float32)
+        for offset in range(1, CONV):
+            masked = (
+                conv_weight[offset][None, cols]
+                * grad_conv
+                * (doc_pos >= offset).astype(jnp.float32)[:, None]
+            )
+            local_grad = local_grad + jnp.concatenate(
+                [masked[offset:], jnp.zeros((offset, width), jnp.float32)], axis=0
+            )
+            spill_over = spill_over + jnp.concatenate(
+                [jnp.zeros((margin - offset, width), jnp.float32), masked[:offset]], axis=0
+            )
+        from_next = passed_along(spill_over, "row", -1)
+        x_grad = (
+            local_grad
+            + jnp.concatenate([jnp.zeros((row_count - margin, width), jnp.float32), from_next], axis=0)
+        ).astype(jnp.bfloat16)
+        return x_grad, gate_grad
+
+    part_count = 4 if moves_tokens else 1
+    part_width = inner_width // part_count
+    outcomes = [
+        backward_part(slice(k * part_width, (k + 1) * part_width)) for k in range(part_count)
+    ]
+    grad_x_parts = [x for x, _ in outcomes]
+    grad_gate = jnp.concatenate([g for _, g in outcomes], axis=1)
+    grad_x = jnp.concatenate(grad_x_parts, axis=1)
     if moves_tokens:
-        stacks, sources = ring_gather(grad_x, "row")
+        stacks, sources = ring_gather(grad_x_parts, "row")
         contract = (((2,), (1,)), ((), ()))
         weight_parts = jnp.split(in_weight, len(stacks), axis=1)
         grad_cols = lax.dot_general(

time: 241 us -> 249 us (1.033)
  starting transfers between devices: 83.1 us -> 98.8 us
  waiting for transfers between devices: 91.7 us -> 81.9 us
  other arithmetic: 13.6 us -> 18.1 us
  local copies, waits for them, and re-layouts: 15.8 us -> 11.5 us
    ppermute x28, starting transfers between devices: 30.7 us -> 41 us  [ring_gather(): part = lax.ppermute(part, axis, pairs)]
    ppermute x2 -> x5, starting transfers between devices: 3.65 us -> 8.83 us  [passed_along(): lax.ppermute(value, axis, [(source, source + steps) for source in range(f...]
    ppermute x28, waiting for transfers between devices: 17.1 us -> 12.1 us  [ring_gather(): part = lax.ppermute(part, axis, pairs)]
    ppermute x28, waiting for transfers between devices: 25.7 us -> 21.1 us  [ring_reduce_scatter(): total = lax.ppermute(total, axis, pairs)]
    ppermute x28, starting transfers between devices: 29 us -> 32.4 us  [ring_reduce_scatter(): total = lax.ppermute(total, axis, pairs)]
    ppermute x4, starting transfers between devices: 12.5 us -> 9.15 us  [placed_blocks(): lax.ppermute(grad_sum[k * row_count:(k + 1) * row_count], ('row', 'col'),...]
    convert_element_type x1 -> x3, other arithmetic: 0.37 us -> 3.66 us  [the longest x1 3.04 us: shards(): (token_weight * (out_total - target.astype(jnp.float32))).astype(jnp.bflo...]
    ppermute x2 -> x5, waiting for transfers between devices: 4.64 us -> 1.71 us  [passed_along(): lax.ppermute(value, axis, [(source, source + steps) for source in range(f...]
  transfers between devices with their start and end apart: 69 -> 72, of which waited for: 48 -> 40; matrix products, arithmetic and copies ran while one was open for 7% -> 7% of each run, Pallas kernels for 0% -> 0%
where the time goes in v8:
time: 249 us
  starting transfers between devices  98.8 us (40%)
  waiting for transfers between devices  81.9 us (33%)
  matrix products  35.2 us (14%)
  other arithmetic  18.1 us (7%)
  local copies, waits for them, and re-layouts  11.5 us (5%)
  between operations  3.13 us (1%)
    ppermute x28, starting transfers between devices, ring_gather(): part = lax.ppermute(part, axis, pairs)  41 us
    ppermute x28, starting transfers between devices, ring_reduce_scatter(): total = lax.ppermute(total, axis, pairs)  32.4 us
    ppermute x28, waiting for transfers between devices, ring_reduce_scatter(): total = lax.ppermute(total, axis, pairs)  21.1 us
    dot_general x4, matrix products, backward_part(): lax.dot_general(residual_grad, out_weight[cols], (((1,), (1,)), ((), ()))...  16.3 us
    ppermute x1, waiting for transfers between devices, col_psum(): lax.ppermute(pair.astype(jnp.bfloat16), 'col', [(c, c ^ 2) for c in range...  13.4 us
    ppermute x28, waiting for transfers between devices, ring_gather(): part = lax.ppermute(part, axis, pairs)  12.1 us
    ppermute x4, waiting for transfers between devices, placed_blocks(): lax.ppermute(grad_sum[k * row_count:(k + 1) * row_count], ('row', 'col'),...  10.6 us
    ppermute x4, starting transfers between devices, placed_blocks(): lax.ppermute(grad_sum[k * row_count:(k + 1) * row_count], ('row', 'col'),...  9.15 us
  transfers between devices with their start and end apart: 72, of which 40 were waited for; matrix products, arithmetic and copies ran while one was open for 7% of the time, Pallas kernels for 0%

profile of v8, /device:TPU:2, one launch (start us, length us, event | category | flops | bytes accessed | tf_op | source)
XLA Modules:
  0.0 248.6 jit_solution(6073010666108671034)
XLA Ops:
  0.7 1.6 copy.26
  3.4 5.8 %all-to-all-start = ((bf16[128,8,256]{2,0,1:T(8,128)(2,1)}), bf16[128,8,256]{2,0,1:T(8,128)(2,1)S(1)}, u32[]{:S(2)}, u32[]{:S(2)}) async-start(bf16[128,8,256]{2,0,1:T(8,128)(2,1)} %copy.28), calls=%async_computation | async-start | bytes 1048576 | tf_op jit(solution)/shard_map/all_to_all | solution.py:24
  14.9 8.9 %all-to-all-done = bf16[128,8,256]{2,0,1:T(8,128)(2,1)S(1)} async-done(((bf16[128,8,256]{2,0,1:T(8,128)(2,1)}), bf16[128,8,256]{2,0,1:T(8,128)(2,1)S(1)}, u32[]{:S(2)}, u32[]{:S(2)}) %all-to-all-start) | async-done | bytes 524320 | tf_op jit(solution)/shard_map/all_to_all | solution.py:24
  23.8 1.9 collective-permute-done
  25.7 1.6 maximum_select_fusion.1
  27.3 1.6 gather_fusion.3
  28.9 4.5 %fusion.127 = (bf16[8,128,1024]{2,1,0:T(8,128)(2,1)S(1)}, f32[8,128,1024]{2,1,0:T(8,128)}) fusion(bf16[512,2048]{1,0:T(8,128)(2,1)S(1)} %copy-done.2, bf16[8,128,512]{2,1,0:T(8,128)(2,1)} %gather_fusion.3, pred[8]{0:T(512)(128)(4,1)S(1)} %compare_and_fusion.2), kind=kOutput, calls=%fused_computation.282 | convolution fusion | flops 1075314688 | bytes 8389120 | tf_op jit(solution)/shard_map/dot_general | solution.py:94
  34.4 1.6 gather_fusion.4
  36.0 2.7 %fusion.126 = (bf16[8,128,1024]{2,1,0:T(8,128)(2,1)S(1)}, f32[8,128,1024]{2,1,0:T(8,128)S(1)}) fusion(bf16[512,2048]{1,0:T(8,128)(2,1)S(1)} %copy-done.2, bf16[8,128,512]{2,1,0:T(8,128)(2,1)} %gather_fusion.4, pred[8]{0:T(512)(128)(4,1)S(1)} %get-tuple-element.151), kind=kOutput, calls=%fused_computation.281 | convolution fusion | flops 1075314688 | bytes 8389120 | tf_op jit(solution)/shard_map/dot_general | solution.py:95
  38.7 2.0 collective-permute-start.15
  45.1 1.7 collective-permute-done.22
  46.9 1.7 collective-permute-start.16
  52.7 1.4 collective-permute-done.23
  54.2 1.4 collective-permute-start.17
  59.2 1.7 collective-permute-done.24
  61.0 1.4 collective-permute-start.18
  62.4 1.7 collective-permute-start.25
  66.0 2.5 collective-permute-done.25
  68.6 2.1 collective-permute-start.19
  70.7 1.6 collective-permute-start.26
  74.2 2.9 %collective-permute-done.26 = bf16[128,512]{1,0:T(8,128)(2,1)S(1)} collective-permute-done((bf16[128,512]{1,0:T(8,128)(2,1)S(1)}, bf16[128,512]{1,0:T(8,128)(2,1)S(1)}, u32[]{:S(2)}, u32[]{:S(2)}) %collective-permute-start.26) | collective-permute-done | bytes 131104 | tf_op jit(solution)/shard_map/ppermute | solution.py:104
  77.2 2.5 collective-permute-start.20
  79.6 1.6 collective-permute-start.27
  83.6 2.7 %collective-permute-done.27 = bf16[128,512]{1,0:T(8,128)(2,1)S(1)} collective-permute-done((bf16[128,512]{1,0:T(8,128)(2,1)S(1)}, bf16[128,512]{1,0:T(8,128)(2,1)S(1)}, u32[]{:S(2)}, u32[]{:S(2)}) %collective-permute-start.27) | collective-permute-done | bytes 131104 | tf_op jit(solution)/shard_map/ppermute | solution.py:104
  86.4 2.1 collective-permute-start.21
  88.5 1.6 collective-permute-start.28
  91.4 2.1 collective-permute-done.28
  93.6 3.7 %collective-permute-start.29 = (bf16[3,2048]{1,0:T(4,128)(2,1)S(1)}, bf16[3,2048]{1,0:T(4,128)(2,1)S(1)}, u32[]{:S(2)}, u32[]{:S(2)}) collective-permute-start(bf16[3,2048]{1,0:T(4,128)(2,1)S(1)} %pad_maximum_fusion.2), channel_id=1, source_target_pairs={{0,4},{4,8},{8,12},{12,16},{16,20},{20,24},{24,28},{1,5},{5,9},{9,... | collective-permute-start | bytes 36872 | tf_op jit(solution)/shard_map/ppermute | solution.py:13
  98.6 1.9 divide_multiply_fusion.1
  100.6 8.8 %convolution_convert_fusion = bf16[128,4096]{1,0:T(8,128)(2,1)S(1)} fusion(bf16[2048,4096]{1,0:T(8,128)(2,1)} %param.23, bf16[128,2048]{1,0:T(8,128)(2,1)S(1)} %copy-done.4, f32[128,2048]{1,0:T(8,128)S(1)} %get-tuple-element.42), kind=kOutput, calls=%fused_computation.6 | convolution fusion | flops 2150891520 | bytes 19398656 | tf_op jit(solution)/shard_map/dot_general | solution.py:178
  109.5 1.9 collective-permute-done.30
  112.4 13.4 %collective-permute-done.31 = bf16[128,2048]{1,0:T(8,128)(2,1)S(1)} collective-permute-done((bf16[128,2048]{1,0:T(8,128)(2,1)S(1)}, bf16[128,2048]{1,0:T(8,128)(2,1)S(1)}, u32[]{:S(2)}, u32[]{:S(2)}) %collective-permute-start.31) | collective-permute-done | bytes 524320 | tf_op jit(solution)/shard_map/ppermute | solution.py:120
  126.3 1.4 divide_multiply_fusion
  128.9 3.0 %multiply_convert_fusion = (bf16[128,4096]{1,0:T(8,128)(2,1)S(1)}, bf16[128,4096]{1,0:T(8,128)(2,1)}) fusion(bf16[128,4096]{1,0:T(8,128)(2,1)S(1)} %copy-done.7, f32[128]{0:T(128)S(1)} %select_reduce_fusion, f32[128,2048]{1,0:T(8,128)} %collective-permute-done.32, f32[128,2048]{1,0:T(8,128)S(1)} %convert_add_fusion.1, pred[]{:T(512)S(6)} %eq.34), kind=kLoop, calls=%fused_computation.17 | loop fusion | flops 4194304 | bytes 5243393 | tf_op jit(solution)/shard_map/convert_element_type | solution.py:190
  131.9 3.7 %fusion = f32[128,512]{1,0:T(8,128)S(1)} fusion(bf16[128,4096]{1,0:T(8,128)(2,1)S(1)} %get-tuple-element.59, bf16[2048,4096]{1,0:T(8,128)(2,1)} %param.23), kind=kOutput, calls=%fused_computation.7 | convolution fusion | flops 536870912 | bytes 5505024 | tf_op jit(solution)/shard_map/dot_general | solution.py:193
  135.7 3.7 %fusion.2 = f32[128,512]{1,0:T(8,128)S(1)} fusion(bf16[128,4096]{1,0:T(8,128)(2,1)S(1)} %get-tuple-element.59, bf16[2048,4096]{1,0:T(8,128)(2,1)} %param.23), kind=kOutput, calls=%fused_computation.9 | convolution fusion | flops 536870912 | bytes 5505024 | tf_op jit(solution)/shard_map/dot_general | solution.py:193
  139.4 3.8 %fusion.4 = f32[128,512]{1,0:T(8,128)S(1)} fusion(bf16[128,4096]{1,0:T(8,128)(2,1)S(1)} %get-tuple-element.59, bf16[2048,4096]{1,0:T(8,128)(2,1)} %param.23), kind=kOutput, calls=%fused_computation.11 | convolution fusion | flops 536870912 | bytes 5505024 | tf_op jit(solution)/shard_map/dot_general | solution.py:193
  143.2 5.0 %multiply_multiply_fusion.11 = (f32[128,512]{1,0:T(8,128)S(1)}, f32[128,512]{1,0:T(8,128)S(1)}, f32[128,512]{1,0:T(8,128)S(1)}, f32[128,512]{1,0:T(8,128)S(1)}, ...) fusion(f32[128]{0:T(128)S(1)} %get-tuple-element.140, ...), kind=kOutput, calls=%fused_computation.194 | convolution fusion | flops 539754496 | bytes 10494464 | tf_op jit(solution)/shard_map/dot_general | solution.py:193
  154.8 5.8 %collective-permute-start.34 = (bf16[128,512]{1,0:T(8,128)(2,1)S(1)}, bf16[128,512]{1,0:T(8,128)(2,1)S(1)}, u32[]{:S(2)}, u32[]{:S(2)}) collective-permute-start(bf16[128,512]{1,0:T(8,128)(2,1)S(1)} %get-tuple-element.44), channel_id=1, source_target_pairs={{0,8},{8,16},{16,24},{24,28},{28,20},{20,12},{12,4},{4,0},{1,9},{9... | collective-permute-start | bytes 393224 | tf_op jit(solution)/shard_map/ppermute | solution.py:77
  160.8 3.5 %collective-permute-start.42 = (bf16[128,512]{1,0:T(8,128)(2,1)S(1)}, bf16[128,512]{1,0:T(8,128)(2,1)S(1)}, u32[]{:S(2)}, u32[]{:S(2)}) collective-permute-start(bf16[128,512]{1,0:T(8,128)(2,1)S(1)} %get-tuple-element.48), channel_id=1, source_target_pairs={{0,8},{8,16},{16,24},{24,28},{28,20},{20,12},{12,4},{4,0},{1,9},{9... | collective-permute-start | bytes 393224 | tf_op jit(solution)/shard_map/ppermute | solution.py:77
  165.4 2.3 collective-permute-start.35
  167.9 2.9 %collective-permute-start.43 = (bf16[128,512]{1,0:T(8,128)(2,1)S(1)}, bf16[128,512]{1,0:T(8,128)(2,1)S(1)}, u32[]{:S(2)}, u32[]{:S(2)}) collective-permute-start(bf16[128,512]{1,0:T(8,128)(2,1)S(1)} %collective-permute-done.42), channel_id=1, source_target_pairs={{0,8},{8,16},{16,24},{24,28},{28,20},{20,12},{12,4},{4,0},{1,9},{9... | collective-permute-start | bytes 393224 | tf_op jit(solution)/shard_map/ppermute | solution.py:77
  170.8 1.6 collective-permute-done.58
  173.2 1.3 collective-permute-start.36
  174.7 2.5 collective-permute-start.44
  177.4 1.4 collective-permute-done.59
  179.6 2.3 collective-permute-start.37
  182.0 2.7 %collective-permute-start.45 = (bf16[128,512]{1,0:T(8,128)(2,1)S(1)}, bf16[128,512]{1,0:T(8,128)(2,1)S(1)}, u32[]{:S(2)}, u32[]{:S(2)}) collective-permute-start(bf16[128,512]{1,0:T(8,128)(2,1)S(1)} %collective-permute-done.44), channel_id=1, source_target_pairs={{0,8},{8,16},{16,24},{24,28},{28,20},{20,12},{12,4},{4,0},{1,9},{9... | collective-permute-start | bytes 393224 | tf_op jit(solution)/shard_map/ppermute | solution.py:77
  184.7 1.5 collective-permute-done.60
  186.4 2.9 %collective-permute-start.38 = (bf16[128,512]{1,0:T(8,128)(2,1)S(1)}, bf16[128,512]{1,0:T(8,128)(2,1)S(1)}, u32[]{:S(2)}, u32[]{:S(2)}) collective-permute-start(bf16[128,512]{1,0:T(8,128)(2,1)S(1)} %collective-permute-done.37), channel_id=1, source_target_pairs={{0,8},{8,16},{16,24},{24,28},{28,20},{20,12},{12,4},{4,0},{1,9},{9... | collective-permute-start | bytes 393224 | tf_op jit(solution)/shard_map/ppermute | solution.py:77
  189.2 2.0 collective-permute-start.46
  191.3 1.8 collective-permute-done.61
  193.1 2.5 collective-permute-start.39
  195.6 2.4 collective-permute-start.47
  199.4 2.2 collective-permute-start.40
  201.6 2.2 collective-permute-start.48
  207.3 1.4 collective-permute-done.56
  213.7 2.1 collective-permute-done.65
  218.2 7.2 %collective-permute-done.66 = bf16[256,512]{1,0:T(8,128)(2,1)S(1)} collective-permute-done((bf16[256,512]{1,0:T(8,128)(2,1)S(1)}, bf16[256,512]{1,0:T(8,128)(2,1)S(1)}, u32[]{:S(2)}, u32[]{:S(2)}) %collective-permute-start.66) | collective-permute-done | bytes 262176 | tf_op jit(solution)/shard_map/ppermute | solution.py:139
  225.5 4.1 %collective-permute-start.67 = (bf16[128,512]{1,0:T(8,128)(2,1)S(1)}, bf16[128,512]{1,0:T(8,128)(2,1)S(1)}, u32[]{:S(2)}, u32[]{:S(2)}) collective-permute-start(bf16[128,512]{1,0:T(8,128)(2,1)S(1)} %get-tuple-element.104), channel_id=1, source_target_pairs={{0,4},{1,12},{2,20},{3,28},{8,5},{9,13},{10,21},{11,29},{16,6},{17... | collective-permute-start | bytes 393224 | tf_op jit(solution)/shard_map/ppermute | solution.py:45
  229.6 3.1 %collective-permute-start.68 = (bf16[128,512]{1,0:T(8,128)(2,1)S(1)}, bf16[128,512]{1,0:T(8,128)(2,1)S(1)}, u32[]{:S(2)}, u32[]{:S(2)}) collective-permute-start(bf16[128,512]{1,0:T(8,128)(2,1)S(1)} %get-tuple-element.103), channel_id=1, source_target_pairs={{0,0},{1,8},{2,16},{3,24},{8,1},{9,9},{10,17},{11,25},{16,2},{17,1... | collective-permute-start | bytes 393224 | tf_op jit(solution)/shard_map/ppermute | solution.py:45
  233.6 1.7 dynamic-slice_convert_fusion
  237.2 5.5 %collective-permute-done.68 = bf16[128,512]{1,0:T(8,128)(2,1)S(1)} collective-permute-done((bf16[128,512]{1,0:T(8,128)(2,1)S(1)}, bf16[128,512]{1,0:T(8,128)(2,1)S(1)}, u32[]{:S(2)}, u32[]{:S(2)}) %collective-permute-start.68) | collective-permute-done | bytes 131104 | tf_op jit(solution)/shard_map/ppermute | solution.py:45
  242.8 5.1 %collective-permute-done.70 = bf16[128,512]{1,0:T(8,128)(2,1)S(1)} collective-permute-done((bf16[128,512]{1,0:T(8,128)(2,1)S(1)}, bf16[128,512]{1,0:T(8,128)(2,1)S(1)}, u32[]{:S(2)}, u32[]{:S(2)}) %collective-permute-start.70) | collective-permute-done | bytes 131104 | tf_op jit(solution)/shard_map/ppermute | solution.py:45
  (253 shorter events, 56.4 us)
Async XLA Ops:
  3.4 20.3 %all-to-all-start = ((bf16[128,8,256]{2,0,1:T(8,128)(2,1)}), bf16[128,8,256]{2,0,1:T(8,128)(2,1)S(1)}, u32[]{:S(2)}, u32[]{:S(2)}) async-start(bf16[128,8,256]{2,0,1:T(8,128)(2,1)} %copy.28), calls=%async_computation | async-start | bytes 1048576 | tf_op jit(solution)/shard_map/all_to_all | solution.py:24
  33.5 8.5 %collective-permute-start.1 = (bf16[128,512]{1,0:T(8,128)(2,1)S(1)}, bf16[128,512]{1,0:T(8,128)(2,1)}, u32[]{:S(2)}, u32[]{:S(2)}) collective-permute-start(bf16[128,512]{1,0:T(8,128)(2,1)S(1)} %get-tuple-element.99), channel_id=1, source_target_pairs={{0,8},{8,16},{16,24},{24,28},{28,20},{20,12},{12,4},{4,0},{1,9},{9... | collective-permute-start | bytes 393224 | tf_op jit(solution)/shard_map/ppermute | solution.py:104
  34.3 7.7 %collective-permute-start.8 = (bf16[128,512]{1,0:T(8,128)(2,1)S(1)}, bf16[128,512]{1,0:T(8,128)(2,1)}, u32[]{:S(2)}, u32[]{:S(2)}) collective-permute-start(bf16[128,512]{1,0:T(8,128)(2,1)S(1)} %get-tuple-element.100), channel_id=1, source_target_pairs={{0,8},{8,16},{16,24},{24,28},{28,20},{20,12},{12,4},{4,0},{1,9},{9... | collective-permute-start | bytes 393224 | tf_op jit(solution)/shard_map/ppermute | solution.py:104
  38.7 6.4 %collective-permute-start.15 = (bf16[128,512]{1,0:T(8,128)(2,1)S(1)}, bf16[128,512]{1,0:T(8,128)(2,1)S(1)}, u32[]{:S(2)}, u32[]{:S(2)}) collective-permute-start(bf16[128,512]{1,0:T(8,128)(2,1)S(1)} %get-tuple-element.101), channel_id=1, source_target_pairs={{8,0},{16,8},{24,16},{28,24},{20,28},{12,20},{4,12},{0,4},{9,1},{1... | collective-permute-start | bytes 393224 | tf_op jit(solution)/shard_map/ppermute | solution.py:104
  40.7 6.1 %collective-permute-start.22 = (bf16[128,512]{1,0:T(8,128)(2,1)S(1)}, bf16[128,512]{1,0:T(8,128)(2,1)S(1)}, u32[]{:S(2)}, u32[]{:S(2)}) collective-permute-start(bf16[128,512]{1,0:T(8,128)(2,1)S(1)} %get-tuple-element.102), channel_id=1, source_target_pairs={{8,0},{16,8},{24,16},{28,24},{20,28},{12,20},{4,12},{0,4},{9,1},{1... | collective-permute-start | bytes 393224 | tf_op jit(solution)/shard_map/ppermute | solution.py:104
  43.0 6.8 %collective-permute-start.2 = (bf16[128,512]{1,0:T(8,128)(2,1)S(1)}, bf16[128,512]{1,0:T(8,128)(2,1)S(1)}, u32[]{:S(2)}, u32[]{:S(2)}) collective-permute-start(bf16[128,512]{1,0:T(8,128)(2,1)S(1)} %get-tuple-element.73), channel_id=1, source_target_pairs={{0,8},{8,16},{16,24},{24,28},{28,20},{20,12},{12,4},{4,0},{1,9},{9... | collective-permute-start | bytes 393224 | tf_op jit(solution)/shard_map/ppermute | solution.py:104
  43.9 6.7 %collective-permute-start.9 = (bf16[128,512]{1,0:T(8,128)(2,1)S(1)}, bf16[128,512]{1,0:T(8,128)(2,1)S(1)}, u32[]{:S(2)}, u32[]{:S(2)}) collective-permute-start(bf16[128,512]{1,0:T(8,128)(2,1)S(1)} %get-tuple-element.74), channel_id=1, source_target_pairs={{0,8},{8,16},{16,24},{24,28},{28,20},{20,12},{12,4},{4,0},{1,9},{9... | collective-permute-start | bytes 393224 | tf_op jit(solution)/shard_map/ppermute | solution.py:104
  46.9 5.8 %collective-permute-start.16 = (bf16[128,512]{1,0:T(8,128)(2,1)S(1)}, bf16[128,512]{1,0:T(8,128)(2,1)S(1)}, u32[]{:S(2)}, u32[]{:S(2)}) collective-permute-start(bf16[128,512]{1,0:T(8,128)(2,1)S(1)} %get-tuple-element.87), channel_id=1, source_target_pairs={{8,0},{16,8},{24,16},{28,24},{20,28},{12,20},{4,12},{0,4},{9,1},{1... | collective-permute-start | bytes 393224 | tf_op jit(solution)/shard_map/ppermute | solution.py:104
  48.6 5.5 %collective-permute-start.23 = (bf16[128,512]{1,0:T(8,128)(2,1)S(1)}, bf16[128,512]{1,0:T(8,128)(2,1)S(1)}, u32[]{:S(2)}, u32[]{:S(2)}) collective-permute-start(bf16[128,512]{1,0:T(8,128)(2,1)S(1)} %get-tuple-element.88), channel_id=1, source_target_pairs={{8,0},{16,8},{24,16},{28,24},{20,28},{12,20},{4,12},{0,4},{9,1},{1... | collective-permute-start | bytes 393224 | tf_op jit(solution)/shard_map/ppermute | solution.py:104
  50.7 6.2 %collective-permute-start.10 = (bf16[128,512]{1,0:T(8,128)(2,1)S(1)}, bf16[128,512]{1,0:T(8,128)(2,1)S(1)}, u32[]{:S(2)}, u32[]{:S(2)}) collective-permute-start(bf16[128,512]{1,0:T(8,128)(2,1)S(1)} %get-tuple-element.72), channel_id=1, source_target_pairs={{0,8},{8,16},{16,24},{24,28},{28,20},{20,12},{12,4},{4,0},{1,9},{9... | collective-permute-start | bytes 393224 | tf_op jit(solution)/shard_map/ppermute | solution.py:104
  51.5 5.8 %collective-permute-start.3 = (bf16[128,512]{1,0:T(8,128)(2,1)S(1)}, bf16[128,512]{1,0:T(8,128)(2,1)S(1)}, u32[]{:S(2)}, u32[]{:S(2)}) collective-permute-start(bf16[128,512]{1,0:T(8,128)(2,1)S(1)} %get-tuple-element.71), channel_id=1, source_target_pairs={{0,8},{8,16},{16,24},{24,28},{28,20},{20,12},{12,4},{4,0},{1,9},{9... | collective-permute-start | bytes 393224 | tf_op jit(solution)/shard_map/ppermute | solution.py:104
  54.2 5.0 %collective-permute-start.17 = (bf16[128,512]{1,0:T(8,128)(2,1)S(1)}, bf16[128,512]{1,0:T(8,128)(2,1)S(1)}, u32[]{:S(2)}, u32[]{:S(2)}) collective-permute-start(bf16[128,512]{1,0:T(8,128)(2,1)S(1)} %get-tuple-element.85), channel_id=1, source_target_pairs={{8,0},{16,8},{24,16},{28,24},{20,28},{12,20},{4,12},{0,4},{9,1},{1... | collective-permute-start | bytes 393224 | tf_op jit(solution)/shard_map/ppermute | solution.py:104
  55.6 5.3 %collective-permute-start.24 = (bf16[128,512]{1,0:T(8,128)(2,1)S(1)}, bf16[128,512]{1,0:T(8,128)(2,1)S(1)}, u32[]{:S(2)}, u32[]{:S(2)}) collective-permute-start(bf16[128,512]{1,0:T(8,128)(2,1)S(1)} %get-tuple-element.86), channel_id=1, source_target_pairs={{8,0},{16,8},{24,16},{28,24},{20,28},{12,20},{4,12},{0,4},{9,1},{1... | collective-permute-start | bytes 393224 | tf_op jit(solution)/shard_map/ppermute | solution.py:104
  57.4 6.8 %collective-permute-start.11 = (bf16[128,512]{1,0:T(8,128)(2,1)S(1)}, bf16[128,512]{1,0:T(8,128)(2,1)S(1)}, u32[]{:S(2)}, u32[]{:S(2)}) collective-permute-start(bf16[128,512]{1,0:T(8,128)(2,1)S(1)} %get-tuple-element.70), channel_id=1, source_target_pairs={{0,8},{8,16},{16,24},{24,28},{28,20},{20,12},{12,4},{4,0},{1,9},{9... | collective-permute-start | bytes 393224 | tf_op jit(solution)/shard_map/ppermute | solution.py:104
  58.3 6.2 %collective-permute-start.4 = (bf16[128,512]{1,0:T(8,128)(2,1)S(1)}, bf16[128,512]{1,0:T(8,128)(2,1)S(1)}, u32[]{:S(2)}, u32[]{:S(2)}) collective-permute-start(bf16[128,512]{1,0:T(8,128)(2,1)S(1)} %get-tuple-element.69), channel_id=1, source_target_pairs={{0,8},{8,16},{16,24},{24,28},{28,20},{20,12},{12,4},{4,0},{1,9},{9... | collective-permute-start | bytes 393224 | tf_op jit(solution)/shard_map/ppermute | solution.py:104
  61.0 5.0 %collective-permute-start.18 = (bf16[128,512]{1,0:T(8,128)(2,1)S(1)}, bf16[128,512]{1,0:T(8,128)(2,1)S(1)}, u32[]{:S(2)}, u32[]{:S(2)}) collective-permute-start(bf16[128,512]{1,0:T(8,128)(2,1)S(1)} %get-tuple-element.83), channel_id=1, source_target_pairs={{8,0},{16,8},{24,16},{28,24},{20,28},{12,20},{4,12},{0,4},{9,1},{1... | collective-permute-start | bytes 393224 | tf_op jit(solution)/shard_map/ppermute | solution.py:104
  62.4 6.1 %collective-permute-start.25 = (bf16[128,512]{1,0:T(8,128)(2,1)S(1)}, bf16[128,512]{1,0:T(8,128)(2,1)S(1)}, u32[]{:S(2)}, u32[]{:S(2)}) collective-permute-start(bf16[128,512]{1,0:T(8,128)(2,1)S(1)} %get-tuple-element.84), channel_id=1, source_target_pairs={{8,0},{16,8},{24,16},{28,24},{20,28},{12,20},{4,12},{0,4},{9,1},{1... | collective-permute-start | bytes 393224 | tf_op jit(solution)/shard_map/ppermute | solution.py:104
  64.5 7.7 %collective-permute-start.12 = (bf16[128,512]{1,0:T(8,128)(2,1)S(1)}, bf16[128,512]{1,0:T(8,128)(2,1)S(1)}, u32[]{:S(2)}, u32[]{:S(2)}) collective-permute-start(bf16[128,512]{1,0:T(8,128)(2,1)S(1)} %get-tuple-element.68), channel_id=1, source_target_pairs={{0,8},{8,16},{16,24},{24,28},{28,20},{20,12},{12,4},{4,0},{1,9},{9... | collective-permute-start | bytes 393224 | tf_op jit(solution)/shard_map/ppermute | solution.py:104
  65.4 7.0 %collective-permute-start.5 = (bf16[128,512]{1,0:T(8,128)(2,1)S(1)}, bf16[128,512]{1,0:T(8,128)(2,1)S(1)}, u32[]{:S(2)}, u32[]{:S(2)}) collective-permute-start(bf16[128,512]{1,0:T(8,128)(2,1)S(1)} %get-tuple-element.67), channel_id=1, source_target_pairs={{0,8},{8,16},{16,24},{24,28},{28,20},{20,12},{12,4},{4,0},{1,9},{9... | collective-permute-start | bytes 393224 | tf_op jit(solution)/shard_map/ppermute | solution.py:104
  68.6 5.6 %collective-permute-start.19 = (bf16[128,512]{1,0:T(8,128)(2,1)S(1)}, bf16[128,512]{1,0:T(8,128)(2,1)S(1)}, u32[]{:S(2)}, u32[]{:S(2)}) collective-permute-start(bf16[128,512]{1,0:T(8,128)(2,1)S(1)} %get-tuple-element.81), channel_id=1, source_target_pairs={{8,0},{16,8},{24,16},{28,24},{20,28},{12,20},{4,12},{0,4},{9,1},{1... | collective-permute-start | bytes 393224 | tf_op jit(solution)/shard_map/ppermute | solution.py:104
  70.7 6.4 %collective-permute-start.26 = (bf16[128,512]{1,0:T(8,128)(2,1)S(1)}, bf16[128,512]{1,0:T(8,128)(2,1)S(1)}, u32[]{:S(2)}, u32[]{:S(2)}) collective-permute-start(bf16[128,512]{1,0:T(8,128)(2,1)S(1)} %get-tuple-element.82), channel_id=1, source_target_pairs={{8,0},{16,8},{24,16},{28,24},{20,28},{12,20},{4,12},{0,4},{9,1},{1... | collective-permute-start | bytes 393224 | tf_op jit(solution)/shard_map/ppermute | solution.py:104
  72.4 8.8 %collective-permute-start.13 = (bf16[128,512]{1,0:T(8,128)(2,1)S(1)}, bf16[128,512]{1,0:T(8,128)(2,1)S(1)}, u32[]{:S(2)}, u32[]{:S(2)}) collective-permute-start(bf16[128,512]{1,0:T(8,128)(2,1)S(1)} %get-tuple-element.66), channel_id=1, source_target_pairs={{0,8},{8,16},{16,24},{24,28},{28,20},{20,12},{12,4},{4,0},{1,9},{9... | collective-permute-start | bytes 393224 | tf_op jit(solution)/shard_map/ppermute | solution.py:104
  73.3 8.0 %collective-permute-start.6 = (bf16[128,512]{1,0:T(8,128)(2,1)S(1)}, bf16[128,512]{1,0:T(8,128)(2,1)S(1)}, u32[]{:S(2)}, u32[]{:S(2)}) collective-permute-start(bf16[128,512]{1,0:T(8,128)(2,1)S(1)} %get-tuple-element.65), channel_id=1, source_target_pairs={{0,8},{8,16},{16,24},{24,28},{28,20},{20,12},{12,4},{4,0},{1,9},{9... | collective-permute-start | bytes 393224 | tf_op jit(solution)/shard_map/ppermute | solution.py:104
  77.2 6.4 %collective-permute-start.20 = (bf16[128,512]{1,0:T(8,128)(2,1)S(1)}, bf16[128,512]{1,0:T(8,128)(2,1)S(1)}, u32[]{:S(2)}, u32[]{:S(2)}) collective-permute-start(bf16[128,512]{1,0:T(8,128)(2,1)S(1)} %get-tuple-element.79), channel_id=1, source_target_pairs={{8,0},{16,8},{24,16},{28,24},{20,28},{12,20},{4,12},{0,4},{9,1},{1... | collective-permute-start | bytes 393224 | tf_op jit(solution)/shard_map/ppermute | solution.py:104
  79.6 6.7 %collective-permute-start.27 = (bf16[128,512]{1,0:T(8,128)(2,1)S(1)}, bf16[128,512]{1,0:T(8,128)(2,1)S(1)}, u32[]{:S(2)}, u32[]{:S(2)}) collective-permute-start(bf16[128,512]{1,0:T(8,128)(2,1)S(1)} %get-tuple-element.80), channel_id=1, source_target_pairs={{8,0},{16,8},{24,16},{28,24},{20,28},{12,20},{4,12},{0,4},{9,1},{1... | collective-permute-start | bytes 393224 | tf_op jit(solution)/shard_map/ppermute | solution.py:104
  81.4 8.7 %collective-permute-start.14 = (bf16[128,512]{1,0:T(8,128)(2,1)S(1)}, bf16[128,512]{1,0:T(8,128)(2,1)S(1)}, u32[]{:S(2)}, u32[]{:S(2)}) collective-permute-start(bf16[128,512]{1,0:T(8,128)(2,1)S(1)} %get-tuple-element.64), channel_id=1, source_target_pairs={{0,8},{8,16},{16,24},{24,28},{28,20},{20,12},{12,4},{4,0},{1,9},{9... | collective-permute-start | bytes 393224 | tf_op jit(solution)/shard_map/ppermute | solution.py:104
  82.1 8.0 %collective-permute-start.7 = (bf16[128,512]{1,0:T(8,128)(2,1)S(1)}, bf16[128,512]{1,0:T(8,128)(2,1)S(1)}, u32[]{:S(2)}, u32[]{:S(2)}) collective-permute-start(bf16[128,512]{1,0:T(8,128)(2,1)S(1)} %get-tuple-element.63), channel_id=1, source_target_pairs={{0,8},{8,16},{16,24},{24,28},{28,20},{20,12},{12,4},{4,0},{1,9},{9... | collective-permute-start | bytes 393224 | tf_op jit(solution)/shard_map/ppermute | solution.py:104
  86.4 5.0 %collective-permute-start.21 = (bf16[128,512]{1,0:T(8,128)(2,1)S(1)}, bf16[128,512]{1,0:T(8,128)(2,1)S(1)}, u32[]{:S(2)}, u32[]{:S(2)}) collective-permute-start(bf16[128,512]{1,0:T(8,128)(2,1)S(1)} %get-tuple-element.77), channel_id=1, source_target_pairs={{8,0},{16,8},{24,16},{28,24},{20,28},{12,20},{4,12},{0,4},{9,1},{1... | collective-permute-start | bytes 393224 | tf_op jit(solution)/shard_map/ppermute | solution.py:104
  111.7 14.0 %collective-permute-start.31 = (bf16[128,2048]{1,0:T(8,128)(2,1)S(1)}, bf16[128,2048]{1,0:T(8,128)(2,1)S(1)}, u32[]{:S(2)}, u32[]{:S(2)}) collective-permute-start(bf16[128,2048]{1,0:T(8,128)(2,1)S(1)} %fusion.25), channel_id=1, source_target_pairs={{0,2},{1,3},{2,0},{3,1},{4,6},{5,7},{6,4},{7,5},{8,10},{9,11},{10,... | collective-permute-start | bytes 1572872 | tf_op jit(solution)/shard_map/ppermute | solution.py:120
  148.9 5.8 %collective-permute-start.33 = (f32[3,512]{1,0:T(4,128)S(1)}, f32[3,512]{1,0:T(4,128)S(1)}, u32[]{:S(2)}, u32[]{:S(2)}) collective-permute-start(f32[3,512]{1,0:T(4,128)S(1)} %slice_add_fusion.3), channel_id=1, source_target_pairs={{4,0},{8,4},{12,8},{16,12},{20,16},{24,20},{28,24},{5,1},{9,5},{13... | collective-permute-start | bytes 18440 | tf_op jit(solution)/shard_map/ppermute | solution.py:13
  150.3 10.4 %collective-permute-start.41 = (f32[3,512]{1,0:T(4,128)S(1)}, f32[3,512]{1,0:T(4,128)S(1)}, u32[]{:S(2)}, u32[]{:S(2)}) collective-permute-start(f32[3,512]{1,0:T(4,128)S(1)} %slice_add_fusion.2), channel_id=1, source_target_pairs={{4,0},{8,4},{12,8},{16,12},{20,16},{24,20},{28,24},{5,1},{9,5},{13... | collective-permute-start | bytes 18440 | tf_op jit(solution)/shard_map/ppermute | solution.py:13
  151.6 12.7 %collective-permute-start.49 = (f32[3,512]{1,0:T(4,128)S(1)}, f32[3,512]{1,0:T(4,128)S(1)}, u32[]{:S(2)}, u32[]{:S(2)}) collective-permute-start(f32[3,512]{1,0:T(4,128)S(1)} %slice_add_fusion.1), channel_id=1, source_target_pairs={{4,0},{8,4},{12,8},{16,12},{20,16},{24,20},{28,24},{5,1},{9,5},{13... | collective-permute-start | bytes 18440 | tf_op jit(solution)/shard_map/ppermute | solution.py:13
  153.0 11.5 %collective-permute-start.57 = (f32[3,512]{1,0:T(4,128)S(1)}, f32[3,512]{1,0:T(4,128)S(1)}, u32[]{:S(2)}, u32[]{:S(2)}) collective-permute-start(f32[3,512]{1,0:T(4,128)S(1)} %slice_add_fusion), channel_id=1, source_target_pairs={{4,0},{8,4},{12,8},{16,12},{20,16},{24,20},{28,24},{5,1},{9,5},{13... | collective-permute-start | bytes 18440 | tf_op jit(solution)/shard_map/ppermute | solution.py:13
  154.8 10.5 %collective-permute-start.34 = (bf16[128,512]{1,0:T(8,128)(2,1)S(1)}, bf16[128,512]{1,0:T(8,128)(2,1)S(1)}, u32[]{:S(2)}, u32[]{:S(2)}) collective-permute-start(bf16[128,512]{1,0:T(8,128)(2,1)S(1)} %get-tuple-element.44), channel_id=1, source_target_pairs={{0,8},{8,16},{16,24},{24,28},{28,20},{20,12},{12,4},{4,0},{1,9},{9... | collective-permute-start | bytes 393224 | tf_op jit(solution)/shard_map/ppermute | solution.py:77
  160.8 7.1 %collective-permute-start.42 = (bf16[128,512]{1,0:T(8,128)(2,1)S(1)}, bf16[128,512]{1,0:T(8,128)(2,1)S(1)}, u32[]{:S(2)}, u32[]{:S(2)}) collective-permute-start(bf16[128,512]{1,0:T(8,128)(2,1)S(1)} %get-tuple-element.48), channel_id=1, source_target_pairs={{0,8},{8,16},{16,24},{24,28},{28,20},{20,12},{12,4},{4,0},{1,9},{9... | collective-permute-start | bytes 393224 | tf_op jit(solution)/shard_map/ppermute | solution.py:77
  164.4 6.3 %collective-permute-start.50 = (bf16[128,512]{1,0:T(8,128)(2,1)S(1)}, bf16[128,512]{1,0:T(8,128)(2,1)S(1)}, u32[]{:S(2)}, u32[]{:S(2)}) collective-permute-start(bf16[128,512]{1,0:T(8,128)(2,1)S(1)} %get-tuple-element.52), channel_id=1, source_target_pairs={{8,0},{16,8},{24,16},{28,24},{20,28},{12,20},{4,12},{0,4},{9,1},{1... | collective-permute-start | bytes 393224 | tf_op jit(solution)/shard_map/ppermute | solution.py:77
  164.6 7.8 %collective-permute-start.58 = (bf16[128,512]{1,0:T(8,128)(2,1)S(1)}, bf16[128,512]{1,0:T(8,128)(2,1)S(1)}, u32[]{:S(2)}, u32[]{:S(2)}) collective-permute-start(bf16[128,512]{1,0:T(8,128)(2,1)S(1)} %get-tuple-element.56), channel_id=1, source_target_pairs={{8,0},{16,8},{24,16},{28,24},{20,28},{12,20},{4,12},{0,4},{9,1},{1... | collective-permute-start | bytes 393224 | tf_op jit(solution)/shard_map/ppermute | solution.py:77
  165.4 7.8 %collective-permute-start.35 = (bf16[128,512]{1,0:T(8,128)(2,1)S(1)}, bf16[128,512]{1,0:T(8,128)(2,1)S(1)}, u32[]{:S(2)}, u32[]{:S(2)}) collective-permute-start(bf16[128,512]{1,0:T(8,128)(2,1)S(1)} %collective-permute-done.34), channel_id=1, source_target_pairs={{0,8},{8,16},{16,24},{24,28},{28,20},{20,12},{12,4},{4,0},{1,9},{9... | collective-permute-start | bytes 393224 | tf_op jit(solution)/shard_map/ppermute | solution.py:77
  167.9 6.8 %collective-permute-start.43 = (bf16[128,512]{1,0:T(8,128)(2,1)S(1)}, bf16[128,512]{1,0:T(8,128)(2,1)S(1)}, u32[]{:S(2)}, u32[]{:S(2)}) collective-permute-start(bf16[128,512]{1,0:T(8,128)(2,1)S(1)} %collective-permute-done.42), channel_id=1, source_target_pairs={{0,8},{8,16},{16,24},{24,28},{28,20},{20,12},{12,4},{4,0},{1,9},{9... | collective-permute-start | bytes 393224 | tf_op jit(solution)/shard_map/ppermute | solution.py:77
  170.8 6.4 %collective-permute-start.51 = (bf16[128,512]{1,0:T(8,128)(2,1)S(1)}, bf16[128,512]{1,0:T(8,128)(2,1)S(1)}, u32[]{:S(2)}, u32[]{:S(2)}) collective-permute-start(bf16[128,512]{1,0:T(8,128)(2,1)S(1)} %collective-permute-done.50), channel_id=1, source_target_pairs={{8,0},{16,8},{24,16},{28,24},{20,28},{12,20},{4,12},{0,4},{9,1},{1... | collective-permute-start | bytes 393224 | tf_op jit(solution)/shard_map/ppermute | solution.py:77
  172.4 6.4 %collective-permute-start.59 = (bf16[128,512]{1,0:T(8,128)(2,1)S(1)}, bf16[128,512]{1,0:T(8,128)(2,1)S(1)}, u32[]{:S(2)}, u32[]{:S(2)}) collective-permute-start(bf16[128,512]{1,0:T(8,128)(2,1)S(1)} %collective-permute-done.58), channel_id=1, source_target_pairs={{8,0},{16,8},{24,16},{28,24},{20,28},{12,20},{4,12},{0,4},{9,1},{1... | collective-permute-start | bytes 393224 | tf_op jit(solution)/shard_map/ppermute | solution.py:77
  173.2 6.3 %collective-permute-start.36 = (bf16[128,512]{1,0:T(8,128)(2,1)S(1)}, bf16[128,512]{1,0:T(8,128)(2,1)S(1)}, u32[]{:S(2)}, u32[]{:S(2)}) collective-permute-start(bf16[128,512]{1,0:T(8,128)(2,1)S(1)} %collective-permute-done.35), channel_id=1, source_target_pairs={{0,8},{8,16},{16,24},{24,28},{28,20},{20,12},{12,4},{4,0},{1,9},{9... | collective-permute-start | bytes 393224 | tf_op jit(solution)/shard_map/ppermute | solution.py:77
  174.7 7.3 %collective-permute-start.44 = (bf16[128,512]{1,0:T(8,128)(2,1)S(1)}, bf16[128,512]{1,0:T(8,128)(2,1)S(1)}, u32[]{:S(2)}, u32[]{:S(2)}) collective-permute-start(bf16[128,512]{1,0:T(8,128)(2,1)S(1)} %collective-permute-done.43), channel_id=1, source_target_pairs={{0,8},{8,16},{16,24},{24,28},{28,20},{20,12},{12,4},{4,0},{1,9},{9... | collective-permute-start | bytes 393224 | tf_op jit(solution)/shard_map/ppermute | solution.py:77
  177.1 7.5 %collective-permute-start.52 = (bf16[128,512]{1,0:T(8,128)(2,1)S(1)}, bf16[128,512]{1,0:T(8,128)(2,1)S(1)}, u32[]{:S(2)}, u32[]{:S(2)}) collective-permute-start(bf16[128,512]{1,0:T(8,128)(2,1)S(1)} %collective-permute-done.51), channel_id=1, source_target_pairs={{8,0},{16,8},{24,16},{28,24},{20,28},{12,20},{4,12},{0,4},{9,1},{1... | collective-permute-start | bytes 393224 | tf_op jit(solution)/shard_map/ppermute | solution.py:77
  178.8 7.4 %collective-permute-start.60 = (bf16[128,512]{1,0:T(8,128)(2,1)S(1)}, bf16[128,512]{1,0:T(8,128)(2,1)S(1)}, u32[]{:S(2)}, u32[]{:S(2)}) collective-permute-start(bf16[128,512]{1,0:T(8,128)(2,1)S(1)} %collective-permute-done.59), channel_id=1, source_target_pairs={{8,0},{16,8},{24,16},{28,24},{20,28},{12,20},{4,12},{0,4},{9,1},{1... | collective-permute-start | bytes 393224 | tf_op jit(solution)/shard_map/ppermute | solution.py:77
  179.6 6.8 %collective-permute-start.37 = (bf16[128,512]{1,0:T(8,128)(2,1)S(1)}, bf16[128,512]{1,0:T(8,128)(2,1)S(1)}, u32[]{:S(2)}, u32[]{:S(2)}) collective-permute-start(bf16[128,512]{1,0:T(8,128)(2,1)S(1)} %collective-permute-done.36), channel_id=1, source_target_pairs={{0,8},{8,16},{16,24},{24,28},{28,20},{20,12},{12,4},{4,0},{1,9},{9... | collective-permute-start | bytes 393224 | tf_op jit(solution)/shard_map/ppermute | solution.py:77
  182.0 7.2 %collective-permute-start.45 = (bf16[128,512]{1,0:T(8,128)(2,1)S(1)}, bf16[128,512]{1,0:T(8,128)(2,1)S(1)}, u32[]{:S(2)}, u32[]{:S(2)}) collective-permute-start(bf16[128,512]{1,0:T(8,128)(2,1)S(1)} %collective-permute-done.44), channel_id=1, source_target_pairs={{0,8},{8,16},{16,24},{24,28},{28,20},{20,12},{12,4},{4,0},{1,9},{9... | collective-permute-start | bytes 393224 | tf_op jit(solution)/shard_map/ppermute | solution.py:77
  184.7 6.6 %collective-permute-start.53 = (bf16[128,512]{1,0:T(8,128)(2,1)S(1)}, bf16[128,512]{1,0:T(8,128)(2,1)S(1)}, u32[]{:S(2)}, u32[]{:S(2)}) collective-permute-start(bf16[128,512]{1,0:T(8,128)(2,1)S(1)} %collective-permute-done.52), channel_id=1, source_target_pairs={{8,0},{16,8},{24,16},{28,24},{20,28},{12,20},{4,12},{0,4},{9,1},{1... | collective-permute-start | bytes 393224 | tf_op jit(solution)/shard_map/ppermute | solution.py:77
  186.2 6.8 %collective-permute-start.61 = (bf16[128,512]{1,0:T(8,128)(2,1)S(1)}, bf16[128,512]{1,0:T(8,128)(2,1)S(1)}, u32[]{:S(2)}, u32[]{:S(2)}) collective-permute-start(bf16[128,512]{1,0:T(8,128)(2,1)S(1)} %collective-permute-done.60), channel_id=1, source_target_pairs={{8,0},{16,8},{24,16},{28,24},{20,28},{12,20},{4,12},{0,4},{9,1},{1... | collective-permute-start | bytes 393224 | tf_op jit(solution)/shard_map/ppermute | solution.py:77
  186.4 6.7 %collective-permute-start.38 = (bf16[128,512]{1,0:T(8,128)(2,1)S(1)}, bf16[128,512]{1,0:T(8,128)(2,1)S(1)}, u32[]{:S(2)}, u32[]{:S(2)}) collective-permute-start(bf16[128,512]{1,0:T(8,128)(2,1)S(1)} %collective-permute-done.37), channel_id=1, source_target_pairs={{0,8},{8,16},{16,24},{24,28},{28,20},{20,12},{12,4},{4,0},{1,9},{9... | collective-permute-start | bytes 393224 | tf_op jit(solution)/shard_map/ppermute | solution.py:77
  189.2 6.3 %collective-permute-start.46 = (bf16[128,512]{1,0:T(8,128)(2,1)S(1)}, bf16[128,512]{1,0:T(8,128)(2,1)S(1)}, u32[]{:S(2)}, u32[]{:S(2)}) collective-permute-start(bf16[128,512]{1,0:T(8,128)(2,1)S(1)} %collective-permute-done.45), channel_id=1, source_target_pairs={{0,8},{8,16},{16,24},{24,28},{28,20},{20,12},{12,4},{4,0},{1,9},{9... | collective-permute-start | bytes 393224 | tf_op jit(solution)/shard_map/ppermute | solution.py:77
  191.3 6.7 %collective-permute-start.54 = (bf16[128,512]{1,0:T(8,128)(2,1)S(1)}, bf16[128,512]{1,0:T(8,128)(2,1)S(1)}, u32[]{:S(2)}, u32[]{:S(2)}) collective-permute-start(bf16[128,512]{1,0:T(8,128)(2,1)S(1)} %collective-permute-done.53), channel_id=1, source_target_pairs={{8,0},{16,8},{24,16},{28,24},{20,28},{12,20},{4,12},{0,4},{9,1},{1... | collective-permute-start | bytes 393224 | tf_op jit(solution)/shard_map/ppermute | solution.py:77
  193.0 6.0 %collective-permute-start.62 = (bf16[128,512]{1,0:T(8,128)(2,1)S(1)}, bf16[128,512]{1,0:T(8,128)(2,1)S(1)}, u32[]{:S(2)}, u32[]{:S(2)}) collective-permute-start(bf16[128,512]{1,0:T(8,128)(2,1)S(1)} %collective-permute-done.61), channel_id=1, source_target_pairs={{8,0},{16,8},{24,16},{28,24},{20,28},{12,20},{4,12},{0,4},{9,1},{1... | collective-permute-start | bytes 393224 | tf_op jit(solution)/shard_map/ppermute | solution.py:77
  193.1 6.3 %collective-permute-start.39 = (bf16[128,512]{1,0:T(8,128)(2,1)S(1)}, bf16[128,512]{1,0:T(8,128)(2,1)S(1)}, u32[]{:S(2)}, u32[]{:S(2)}) collective-permute-start(bf16[128,512]{1,0:T(8,128)(2,1)S(1)} %collective-permute-done.38), channel_id=1, source_target_pairs={{0,8},{8,16},{16,24},{24,28},{28,20},{20,12},{12,4},{4,0},{1,9},{9... | collective-permute-start | bytes 393224 | tf_op jit(solution)/shard_map/ppermute | solution.py:77
  195.6 6.0 %collective-permute-start.47 = (bf16[128,512]{1,0:T(8,128)(2,1)S(1)}, bf16[128,512]{1,0:T(8,128)(2,1)S(1)}, u32[]{:S(2)}, u32[]{:S(2)}) collective-permute-start(bf16[128,512]{1,0:T(8,128)(2,1)S(1)} %collective-permute-done.46), channel_id=1, source_target_pairs={{0,8},{8,16},{16,24},{24,28},{28,20},{20,12},{12,4},{4,0},{1,9},{9... | collective-permute-start | bytes 393224 | tf_op jit(solution)/shard_map/ppermute | solution.py:77
  198.0 5.8 %collective-permute-start.55 = (bf16[128,512]{1,0:T(8,128)(2,1)S(1)}, bf16[128,512]{1,0:T(8,128)(2,1)S(1)}, u32[]{:S(2)}, u32[]{:S(2)}) collective-permute-start(bf16[128,512]{1,0:T(8,128)(2,1)S(1)} %collective-permute-done.54), channel_id=1, source_target_pairs={{8,0},{16,8},{24,16},{28,24},{20,28},{12,20},{4,12},{0,4},{9,1},{1... | collective-permute-start | bytes 393224 | tf_op jit(solution)/shard_map/ppermute | solution.py:77
  199.1 5.9 %collective-permute-start.63 = (bf16[128,512]{1,0:T(8,128)(2,1)S(1)}, bf16[128,512]{1,0:T(8,128)(2,1)S(1)}, u32[]{:S(2)}, u32[]{:S(2)}) collective-permute-start(bf16[128,512]{1,0:T(8,128)(2,1)S(1)} %collective-permute-done.62), channel_id=1, source_target_pairs={{8,0},{16,8},{24,16},{28,24},{20,28},{12,20},{4,12},{0,4},{9,1},{1... | collective-permute-start | bytes 393224 | tf_op jit(solution)/shard_map/ppermute | solution.py:77
  199.4 11.6 %collective-permute-start.40 = (bf16[128,512]{1,0:T(8,128)(2,1)S(1)}, bf16[128,512]{1,0:T(8,128)(2,1)S(1)}, u32[]{:S(2)}, u32[]{:S(2)}) collective-permute-start(bf16[128,512]{1,0:T(8,128)(2,1)S(1)} %collective-permute-done.39), channel_id=1, source_target_pairs={{0,8},{8,16},{16,24},{24,28},{28,20},{20,12},{12,4},{4,0},{1,9},{9... | collective-permute-start | bytes 393224 | tf_op jit(solution)/shard_map/ppermute | solution.py:77
  205.0 5.2 %collective-permute-start.64 = (bf16[128,512]{1,0:T(8,128)(2,1)S(1)}, bf16[128,512]{1,0:T(8,128)(2,1)S(1)}, u32[]{:S(2)}, u32[]{:S(2)}) collective-permute-start(bf16[128,512]{1,0:T(8,128)(2,1)S(1)} %collective-permute-done.63), channel_id=1, source_target_pairs={{8,0},{16,8},{24,16},{28,24},{20,28},{12,20},{4,12},{0,4},{9,1},{1... | collective-permute-start | bytes 393224 | tf_op jit(solution)/shard_map/ppermute | solution.py:77
  217.0 8.4 %collective-permute-start.66 = (bf16[256,512]{1,0:T(8,128)(2,1)S(1)}, bf16[256,512]{1,0:T(8,128)(2,1)S(1)}, u32[]{:S(2)}, u32[]{:S(2)}) collective-permute-start(bf16[256,512]{1,0:T(8,128)(2,1)S(1)} %bitcast_convert_fusion), channel_id=1, source_target_pairs={{0,2},{1,3},{2,0},{3,1},{4,6},{5,7},{6,4},{7,5},{8,10},{9,11},{10,... | collective-permute-start | bytes 786440 | tf_op jit(solution)/shard_map/ppermute | solution.py:139
  225.5 11.7 %collective-permute-start.67 = (bf16[128,512]{1,0:T(8,128)(2,1)S(1)}, bf16[128,512]{1,0:T(8,128)(2,1)S(1)}, u32[]{:S(2)}, u32[]{:S(2)}) collective-permute-start(bf16[128,512]{1,0:T(8,128)(2,1)S(1)} %get-tuple-element.104), channel_id=1, source_target_pairs={{0,4},{1,12},{2,20},{3,28},{8,5},{9,13},{10,21},{11,29},{16,6},{17... | collective-permute-start | bytes 393224 | tf_op jit(solution)/shard_map/ppermute | solution.py:45
  229.6 13.1 %collective-permute-start.68 = (bf16[128,512]{1,0:T(8,128)(2,1)S(1)}, bf16[128,512]{1,0:T(8,128)(2,1)S(1)}, u32[]{:S(2)}, u32[]{:S(2)}) collective-permute-start(bf16[128,512]{1,0:T(8,128)(2,1)S(1)} %get-tuple-element.103), channel_id=1, source_target_pairs={{0,0},{1,8},{2,16},{3,24},{8,1},{9,9},{10,17},{11,25},{16,2},{17,1... | collective-permute-start | bytes 393224 | tf_op jit(solution)/shard_map/ppermute | solution.py:45
  235.2 7.5 %collective-permute-start.69 = (bf16[128,512]{1,0:T(8,128)(2,1)S(1)}, bf16[128,512]{1,0:T(8,128)(2,1)S(1)}, u32[]{:S(2)}, u32[]{:S(2)}) collective-permute-start(bf16[128,512]{1,0:T(8,128)(2,1)S(1)} %get-tuple-element.104), channel_id=1, source_target_pairs={{4,4},{5,12},{6,20},{7,28},{12,5},{13,13},{14,21},{15,29},{20,6},{... | collective-permute-start | bytes 393224 | tf_op jit(solution)/shard_map/ppermute | solution.py:45
  235.9 12.0 %collective-permute-start.70 = (bf16[128,512]{1,0:T(8,128)(2,1)S(1)}, bf16[128,512]{1,0:T(8,128)(2,1)S(1)}, u32[]{:S(2)}, u32[]{:S(2)}) collective-permute-start(bf16[128,512]{1,0:T(8,128)(2,1)S(1)} %get-tuple-element.103), channel_id=1, source_target_pairs={{4,0},{5,8},{6,16},{7,24},{12,1},{13,9},{14,17},{15,25},{20,2},{21... | collective-permute-start | bytes 393224 | tf_op jit(solution)/shard_map/ppermute | solution.py:45
  (27 other events, 162.6 us)

commit v9 on v6

--- a/solution.py
+++ b/solution.py
@@ -31,24 +31,25 @@
 def placed_blocks(grad_sum, row_count):
     n_row, n_col = lax.axis_size("row"), lax.axis_size("col")
     share = n_row // n_col
-    row, col = lax.axis_index("row"), lax.axis_index("col")
+    row = lax.axis_index("row")
+    got = []
+    for m in range(share):
+        pairs = [
+            (r * n_col + c, (c * share + (r % share + m) % share) * n_col + r // share)
+            for r in range(n_row)
+            for c in range(n_col)
+        ]
+        start = ((row % share + m) % share) * row_count
+        piece = lax.dynamic_slice_in_dim(grad_sum, start, row_count, axis=0)
+        got.append(lax.ppermute(piece, ("row", "col"), pairs))
     pieces = []
     for j in range(share):
-        got = []
-        for k in range(share):
-            pairs = [
-                (r * n_col + c, (c * share + k) * n_col + r // share)
-                for r in range(n_row)
-                if r % share == j
-                for c in range(n_col)
-            ]
-            got.append(lax.ppermute(grad_sum[k * row_count : (k + 1) * row_count], ("row", "col"), pairs))
+        want = (row % share - j) % share
         piece = got[0]
-        for k in range(1, share):
-            piece = jnp.where(row % share == k, got[k], piece)
+        for m in range(1, share):
+            piece = jnp.where(want == m, got[m], piece)
         pieces.append(piece)
     return jnp.concatenate(pieces, axis=1)
-
 
 def ring_order(count):
     if count % 2:

time: 241 us -> 234 us (0.971)
  starting transfers between devices: 83.1 us -> 76.7 us
    ppermute x4 -> x2, starting transfers between devices: 12.5 us -> 6.46 us  [placed_blocks(): got.append(lax.ppermute(piece, ('row', 'col'), pairs))]
    ppermute x4 -> x2, waiting for transfers between devices: 8.49 us -> 7.57 us  [placed_blocks(): got.append(lax.ppermute(piece, ('row', 'col'), pairs))]
  transfers between devices with their start and end apart: 69 -> 67, of which waited for: 48 -> 48; matrix products, arithmetic and copies ran while one was open for 7% -> 8% of each run, Pallas kernels for 0% -> 0%
where the time goes in v9:
time: 234 us; the launch traced here: 233 us
  waiting for transfers between devices  91.3 us (39%)
  starting transfers between devices  76.7 us (33%)
  matrix products  33 us (14%)
  local copies, waits for them, and re-layouts  15.9 us (7%)
  other arithmetic  13.5 us (6%)
  between operations  2.83 us (1%)
    ppermute x28, starting transfers between devices, ring_gather(): part = lax.ppermute(part, axis, pairs)  30.7 us
    ppermute x28, starting transfers between devices, ring_reduce_scatter(): total = lax.ppermute(total, axis, pairs)  28.6 us
    ppermute x28, waiting for transfers between devices, ring_reduce_scatter(): total = lax.ppermute(total, axis, pairs)  26 us
    ppermute x28, waiting for transfers between devices, ring_gather(): part = lax.ppermute(part, axis, pairs)  17.1 us
    dot_general x1, matrix products, shards(): lax.dot_general(residual_grad, out_weight, (((1,), (1,)), ((), ())), pref...  14.4 us
    ppermute x1, waiting for transfers between devices, col_psum(): lax.ppermute(pair.astype(jnp.bfloat16), 'col', [(c, c ^ 2) for c in range...  13.4 us
    dot_general x1, matrix products, shards(): jnp.dot(mixed, out_weight, preferred_element_type=jnp.float32)  8.41 us
    ppermute x1, waiting for transfers between devices, col_psum_scatter(): lax.ppermute(theirs.astype(jnp.bfloat16), 'col', [(c, c ^ 2) for c in ran...  7.81 us
  transfers between devices with their start and end apart: 67, of which 48 were waited for; matrix products, arithmetic and copies ran while one was open for 8% of the time, Pallas kernels for 0%

profile of v9, /device:TPU:2, one launch (start us, length us, event | category | flops | bytes accessed | tf_op | source)
XLA Modules:
  0.0 233.1 jit_solution(11440594105341429981)
XLA Ops:
  0.7 1.7 copy.26
  3.5 5.8 %all-to-all-start = ((bf16[128,8,256]{2,0,1:T(8,128)(2,1)}), bf16[128,8,256]{2,0,1:T(8,128)(2,1)S(1)}, u32[]{:S(2)}, u32[]{:S(2)}) async-start(bf16[128,8,256]{2,0,1:T(8,128)(2,1)} %copy.28), calls=%async_computation | async-start | bytes 1048576 | tf_op jit(solution)/shard_map/all_to_all | solution.py:24
  16.0 7.8 %all-to-all-done = bf16[128,8,256]{2,0,1:T(8,128)(2,1)S(1)} async-done(((bf16[128,8,256]{2,0,1:T(8,128)(2,1)}), bf16[128,8,256]{2,0,1:T(8,128)(2,1)S(1)}, u32[]{:S(2)}, u32[]{:S(2)}) %all-to-all-start) | async-done | bytes 524320 | tf_op jit(solution)/shard_map/all_to_all | solution.py:24
  25.7 1.6 maximum_select_fusion.1
  27.4 1.6 gather_fusion.4
  29.0 4.5 %fusion.112 = (bf16[8,128,1024]{2,1,0:T(8,128)(2,1)S(1)}, f32[8,128,1024]{2,1,0:T(8,128)}) fusion(bf16[512,2048]{1,0:T(8,128)(2,1)S(1)} %copy-done.2, bf16[8,128,512]{2,1,0:T(8,128)(2,1)} %gather_fusion.4, pred[8]{0:T(512)(128)(4,1)S(1)} %get-tuple-element.105), kind=kOutput, calls=%fused_computation.252 | convolution fusion | flops 1075314688 | bytes 8389120 | tf_op jit(solution)/shard_map/dot_general | solution.py:95
  33.5 1.5 collective-permute-start.15
  35.1 1.7 gather_fusion.3
  36.9 2.7 %fusion.113 = (bf16[8,128,1024]{2,1,0:T(8,128)(2,1)S(1)}, f32[8,128,1024]{2,1,0:T(8,128)S(1)}) fusion(bf16[512,2048]{1,0:T(8,128)(2,1)S(1)} %copy-done.2, bf16[8,128,512]{2,1,0:T(8,128)(2,1)} %gather_fusion.3, pred[8]{0:T(512)(128)(4,1)} %compare_and_fusion.2), kind=kOutput, calls=%fused_computation.253 | convolution fusion | flops 1075314688 | bytes 8388616 | tf_op jit(solution)/shard_map/dot_general | solution.py:94
  39.6 2.0 collective-permute-start.1
  43.1 1.5 collective-permute-start.16
  46.0 1.7 collective-permute-done.8
  47.8 1.7 collective-permute-start.2
  50.7 1.5 collective-permute-start.17
  53.6 1.4 collective-permute-done.9
  55.1 1.4 collective-permute-start.3
  57.3 1.5 collective-permute-start.18
  60.1 1.7 collective-permute-done.10
  61.9 1.7 collective-permute-start.4
  64.8 1.2 collective-permute-start.19
  66.9 3.1 %collective-permute-done.11 = bf16[128,512]{1,0:T(8,128)(2,1)S(1)} collective-permute-done((bf16[128,512]{1,0:T(8,128)(2,1)S(1)}, bf16[128,512]{1,0:T(8,128)(2,1)S(1)}, u32[]{:S(2)}, u32[]{:S(2)}) %collective-permute-start.11) | collective-permute-done | bytes 131104 | tf_op jit(solution)/shard_map/ppermute | solution.py:104
  70.1 1.8 collective-permute-start.5
  74.3 1.7 collective-permute-done.5
  76.0 2.8 %collective-permute-done.12 = bf16[128,512]{1,0:T(8,128)(2,1)S(1)} collective-permute-done((bf16[128,512]{1,0:T(8,128)(2,1)S(1)}, bf16[128,512]{1,0:T(8,128)(2,1)S(1)}, u32[]{:S(2)}, u32[]{:S(2)}) %collective-permute-start.12) | collective-permute-done | bytes 131104 | tf_op jit(solution)/shard_map/ppermute | solution.py:104
  78.9 2.1 collective-permute-start.6
  83.2 2.0 collective-permute-done.6
  85.3 2.5 %collective-permute-done.13 = bf16[128,512]{1,0:T(8,128)(2,1)S(1)} collective-permute-done((bf16[128,512]{1,0:T(8,128)(2,1)S(1)}, bf16[128,512]{1,0:T(8,128)(2,1)S(1)}, u32[]{:S(2)}, u32[]{:S(2)}) %collective-permute-start.13) | collective-permute-done | bytes 131104 | tf_op jit(solution)/shard_map/ppermute | solution.py:104
  87.9 1.8 collective-permute-start.7
  90.3 2.6 %collective-permute-done.7 = bf16[128,512]{1,0:T(8,128)(2,1)S(1)} collective-permute-done((bf16[128,512]{1,0:T(8,128)(2,1)S(1)}, bf16[128,512]{1,0:T(8,128)(2,1)S(1)}, u32[]{:S(2)}, u32[]{:S(2)}) %collective-permute-start.7) | collective-permute-done | bytes 131104 | tf_op jit(solution)/shard_map/ppermute | solution.py:104
  92.9 1.8 collective-permute-done.14
  94.7 2.4 %collective-permute-start.29 = (bf16[3,2048]{1,0:T(4,128)(2,1)S(1)}, bf16[3,2048]{1,0:T(4,128)(2,1)S(1)}, u32[]{:S(2)}, u32[]{:S(2)}) collective-permute-start(bf16[3,2048]{1,0:T(4,128)(2,1)S(1)} %pad_maximum_fusion.1), channel_id=1, source_target_pairs={{0,4},{4,8},{8,12},{12,16},{16,20},{20,24},{24,28},{1,5},{5,9},{9,... | collective-permute-start | bytes 36872 | tf_op jit(solution)/shard_map/ppermute | solution.py:13
  99.6 8.4 %convolution_convert_fusion = bf16[128,4096]{1,0:T(8,128)(2,1)S(1)} fusion(bf16[2048,4096]{1,0:T(8,128)(2,1)} %param.23, bf16[128,2048]{1,0:T(8,128)(2,1)S(1)} %copy-done.15, f32[128,2048]{1,0:T(8,128)S(1)} %fusion.9), kind=kOutput, calls=%fused_computation.6 | convolution fusion | flops 2150891520 | bytes 19398656 | tf_op jit(solution)/shard_map/dot_general | solution.py:178
  108.1 1.9 collective-permute-done.30
  110.9 13.4 %collective-permute-done.31 = bf16[128,2048]{1,0:T(8,128)(2,1)S(1)} collective-permute-done((bf16[128,2048]{1,0:T(8,128)(2,1)S(1)}, bf16[128,2048]{1,0:T(8,128)(2,1)S(1)}, u32[]{:S(2)}, u32[]{:S(2)}) %collective-permute-start.31) | collective-permute-done | bytes 524320 | tf_op jit(solution)/shard_map/ppermute | solution.py:120
  124.9 2.5 %collective-permute-done.32 = f32[128,2048]{1,0:T(8,128)S(1)} collective-permute-done((f32[128,2048]{1,0:T(8,128)S(1)}, f32[128,2048]{1,0:T(8,128)S(1)}, u32[]{:S(2)}, u32[]{:S(2)}) %collective-permute-start.32) | collective-permute-done | bytes 1048608 | tf_op jit(solution)/shard_map/ppermute | solution.py:123
  127.4 1.5 maximum_select_fusion
  128.9 14.4 %multiply_multiply_fusion.2 = (f32[128,2048]{1,0:T(8,128)}, f32[128,2048]{1,0:T(8,128)}, bf16[128,2048]{1,0:T(8,128)(2,1)}) fusion(f32[128]{0:T(128)S(1)} %get-tuple-element.95, f32[2048]{0:T(1024)S(1)} %bitcast.324, f32[128,2048]{1,0:T(8,128)S(1)} %fusion.9, bf16[128,2048]{1,0:T(8,128)(2,1)} %param.21, bf16[2048,4096]{1,0:T(8,128)(2,1)} %param.23, ...), kind=kOutput, calls=%fused_computation.43 | convolution fusion | flops 2155872256 | bytes 24126464 | tf_op jit(solution)/shard_map/dot_general | solution.py:191
  143.3 1.5 multiply_multiply_fusion.1
  146.7 1.3 collective-permute-start.33
  149.7 3.4 %collective-permute-done.33 = f32[3,2048]{1,0:T(4,128)S(1)} collective-permute-done((f32[3,2048]{1,0:T(4,128)S(1)}, f32[3,2048]{1,0:T(4,128)S(1)}, u32[]{:S(2)}, u32[]{:S(2)}) %collective-permute-start.33) | collective-permute-done | bytes 24608 | tf_op jit(solution)/shard_map/ppermute | solution.py:13
  153.5 3.2 %collective-permute-start.55 = (bf16[128,512]{1,0:T(8,128)(2,1)S(1)}, bf16[128,512]{1,0:T(8,128)(2,1)S(1)}, u32[]{:S(2)}, u32[]{:S(2)}) collective-permute-start(bf16[128,512]{1,0:T(8,128)(2,1)S(1)} %get-tuple-element.79), channel_id=1, source_target_pairs={{8,0},{16,8},{24,16},{28,24},{20,28},{12,20},{4,12},{0,4},{9,1},{1... | collective-permute-start | bytes 393224 | tf_op jit(solution)/shard_map/ppermute | solution.py:77
  156.8 1.2 collective-permute-start.48
  159.5 2.3 collective-permute-done.55
  161.7 1.4 collective-permute-start.56
  163.1 1.4 collective-permute-done.48
  164.5 1.4 collective-permute-start.49
  166.6 1.8 collective-permute-start.35
  168.8 2.2 collective-permute-done.49
  171.0 1.4 collective-permute-start.50
  173.7 1.7 collective-permute-start.36
  175.8 1.4 collective-permute-done.50
  177.3 1.4 collective-permute-start.51
  179.3 1.7 collective-permute-done.36
  185.9 1.7 collective-permute-done.37
  188.5 1.2 collective-permute-start.60
  193.1 1.7 collective-permute-start.39
  196.3 1.2 collective-permute-start.54
  205.9 1.9 collective-permute-done.62
  208.6 7.8 %collective-permute-done.63 = bf16[256,512]{1,0:T(8,128)(2,1)S(1)} collective-permute-done((bf16[256,512]{1,0:T(8,128)(2,1)S(1)}, bf16[256,512]{1,0:T(8,128)(2,1)S(1)}, u32[]{:S(2)}, u32[]{:S(2)}) %collective-permute-start.63) | collective-permute-done | bytes 262176 | tf_op jit(solution)/shard_map/ppermute | solution.py:139
  216.5 1.8 collective-permute-start.64
  218.3 4.7 %collective-permute-start.65 = (bf16[128,512]{1,0:T(8,128)(2,1)S(1)}, bf16[128,512]{1,0:T(8,128)(2,1)S(1)}, u32[]{:S(2)}, u32[]{:S(2)}) collective-permute-start(bf16[128,512]{1,0:T(8,128)(2,1)S(1)} %get-tuple-element.88), channel_id=1, source_target_pairs={{0,0},{1,8},{2,16},{3,24},{4,4},{5,12},{6,20},{7,28},{8,1},{9,9},{... | collective-permute-start | bytes 393224 | tf_op jit(solution)/shard_map/ppermute | solution.py:44
  223.0 1.8 dynamic-slice_convert_fusion
  224.8 5.0 %collective-permute-done.64 = bf16[128,512]{1,0:T(8,128)(2,1)S(1)} collective-permute-done((bf16[128,512]{1,0:T(8,128)(2,1)S(1)}, bf16[128,512]{1,0:T(8,128)(2,1)S(1)}, u32[]{:S(2)}, u32[]{:S(2)}) %collective-permute-start.64) | collective-permute-done | bytes 131104 | tf_op jit(solution)/shard_map/ppermute | solution.py:44
  229.8 2.6 %collective-permute-done.65 = bf16[128,512]{1,0:T(8,128)(2,1)S(1)} collective-permute-done((bf16[128,512]{1,0:T(8,128)(2,1)S(1)}, bf16[128,512]{1,0:T(8,128)(2,1)S(1)}, u32[]{:S(2)}, u32[]{:S(2)}) %collective-permute-start.65) | collective-permute-done | bytes 131104 | tf_op jit(solution)/shard_map/ppermute | solution.py:44
  (215 shorter events, 56.8 us)
Async XLA Ops:
  3.5 20.3 %all-to-all-start = ((bf16[128,8,256]{2,0,1:T(8,128)(2,1)}), bf16[128,8,256]{2,0,1:T(8,128)(2,1)S(1)}, u32[]{:S(2)}, u32[]{:S(2)}) async-start(bf16[128,8,256]{2,0,1:T(8,128)(2,1)} %copy.28), calls=%async_computation | async-start | bytes 1048576 | tf_op jit(solution)/shard_map/all_to_all | solution.py:24
  33.5 8.6 %collective-permute-start.15 = (bf16[128,512]{1,0:T(8,128)(2,1)S(1)}, bf16[128,512]{1,0:T(8,128)(2,1)S(1)}, u32[]{:S(2)}, u32[]{:S(2)}) collective-permute-start(bf16[128,512]{1,0:T(8,128)(2,1)S(1)} %get-tuple-element.74), channel_id=1, source_target_pairs={{8,0},{16,8},{24,16},{28,24},{20,28},{12,20},{4,12},{0,4},{9,1},{1... | collective-permute-start | bytes 393224 | tf_op jit(solution)/shard_map/ppermute | solution.py:104
  35.1 7.1 %collective-permute-start.22 = (bf16[128,512]{1,0:T(8,128)(2,1)S(1)}, bf16[128,512]{1,0:T(8,128)(2,1)}, u32[]{:S(2)}, u32[]{:S(2)}) collective-permute-start(bf16[128,512]{1,0:T(8,128)(2,1)S(1)} %get-tuple-element.75), channel_id=1, source_target_pairs={{8,0},{16,8},{24,16},{28,24},{20,28},{12,20},{4,12},{0,4},{9,1},{1... | collective-permute-start | bytes 393224 | tf_op jit(solution)/shard_map/ppermute | solution.py:104
  39.6 6.4 %collective-permute-start.1 = (bf16[128,512]{1,0:T(8,128)(2,1)S(1)}, bf16[128,512]{1,0:T(8,128)(2,1)S(1)}, u32[]{:S(2)}, u32[]{:S(2)}) collective-permute-start(bf16[128,512]{1,0:T(8,128)(2,1)S(1)} %get-tuple-element.72), channel_id=1, source_target_pairs={{0,8},{8,16},{16,24},{24,28},{28,20},{20,12},{12,4},{4,0},{1,9},{9... | collective-permute-start | bytes 393224 | tf_op jit(solution)/shard_map/ppermute | solution.py:104
  41.6 6.1 %collective-permute-start.8 = (bf16[128,512]{1,0:T(8,128)(2,1)S(1)}, bf16[128,512]{1,0:T(8,128)(2,1)S(1)}, u32[]{:S(2)}, u32[]{:S(2)}) collective-permute-start(bf16[128,512]{1,0:T(8,128)(2,1)S(1)} %get-tuple-element.73), channel_id=1, source_target_pairs={{0,8},{8,16},{16,24},{24,28},{28,20},{20,12},{12,4},{4,0},{1,9},{9... | collective-permute-start | bytes 393224 | tf_op jit(solution)/shard_map/ppermute | solution.py:104
  43.1 6.9 %collective-permute-start.16 = (bf16[128,512]{1,0:T(8,128)(2,1)S(1)}, bf16[128,512]{1,0:T(8,128)(2,1)S(1)}, u32[]{:S(2)}, u32[]{:S(2)}) collective-permute-start(bf16[128,512]{1,0:T(8,128)(2,1)S(1)} %get-tuple-element.69), channel_id=1, source_target_pairs={{8,0},{16,8},{24,16},{28,24},{20,28},{12,20},{4,12},{0,4},{9,1},{1... | collective-permute-start | bytes 393224 | tf_op jit(solution)/shard_map/ppermute | solution.py:104
  44.7 5.9 %collective-permute-start.23 = (bf16[128,512]{1,0:T(8,128)(2,1)S(1)}, bf16[128,512]{1,0:T(8,128)(2,1)S(1)}, u32[]{:S(2)}, u32[]{:S(2)}) collective-permute-start(bf16[128,512]{1,0:T(8,128)(2,1)S(1)} %get-tuple-element.70), channel_id=1, source_target_pairs={{8,0},{16,8},{24,16},{28,24},{20,28},{12,20},{4,12},{0,4},{9,1},{1... | collective-permute-start | bytes 393224 | tf_op jit(solution)/shard_map/ppermute | solution.py:104
  47.8 5.8 %collective-permute-start.2 = (bf16[128,512]{1,0:T(8,128)(2,1)S(1)}, bf16[128,512]{1,0:T(8,128)(2,1)S(1)}, u32[]{:S(2)}, u32[]{:S(2)}) collective-permute-start(bf16[128,512]{1,0:T(8,128)(2,1)S(1)} %get-tuple-element.55), channel_id=1, source_target_pairs={{0,8},{8,16},{16,24},{24,28},{28,20},{20,12},{12,4},{4,0},{1,9},{9... | collective-permute-start | bytes 393224 | tf_op jit(solution)/shard_map/ppermute | solution.py:104
  49.5 5.5 %collective-permute-start.9 = (bf16[128,512]{1,0:T(8,128)(2,1)S(1)}, bf16[128,512]{1,0:T(8,128)(2,1)S(1)}, u32[]{:S(2)}, u32[]{:S(2)}) collective-permute-start(bf16[128,512]{1,0:T(8,128)(2,1)S(1)} %get-tuple-element.56), channel_id=1, source_target_pairs={{0,8},{8,16},{16,24},{24,28},{28,20},{20,12},{12,4},{4,0},{1,9},{9... | collective-permute-start | bytes 393224 | tf_op jit(solution)/shard_map/ppermute | solution.py:104
  50.7 6.4 %collective-permute-start.17 = (bf16[128,512]{1,0:T(8,128)(2,1)S(1)}, bf16[128,512]{1,0:T(8,128)(2,1)S(1)}, u32[]{:S(2)}, u32[]{:S(2)}) collective-permute-start(bf16[128,512]{1,0:T(8,128)(2,1)S(1)} %get-tuple-element.67), channel_id=1, source_target_pairs={{8,0},{16,8},{24,16},{28,24},{20,28},{12,20},{4,12},{0,4},{9,1},{1... | collective-permute-start | bytes 393224 | tf_op jit(solution)/shard_map/ppermute | solution.py:104
  52.2 5.0 %collective-permute-start.24 = (bf16[128,512]{1,0:T(8,128)(2,1)S(1)}, bf16[128,512]{1,0:T(8,128)(2,1)S(1)}, u32[]{:S(2)}, u32[]{:S(2)}) collective-permute-start(bf16[128,512]{1,0:T(8,128)(2,1)S(1)} %get-tuple-element.68), channel_id=1, source_target_pairs={{8,0},{16,8},{24,16},{28,24},{20,28},{12,20},{4,12},{0,4},{9,1},{1... | collective-permute-start | bytes 393224 | tf_op jit(solution)/shard_map/ppermute | solution.py:104
  55.1 5.0 %collective-permute-start.3 = (bf16[128,512]{1,0:T(8,128)(2,1)S(1)}, bf16[128,512]{1,0:T(8,128)(2,1)S(1)}, u32[]{:S(2)}, u32[]{:S(2)}) collective-permute-start(bf16[128,512]{1,0:T(8,128)(2,1)S(1)} %get-tuple-element.53), channel_id=1, source_target_pairs={{0,8},{8,16},{16,24},{24,28},{28,20},{20,12},{12,4},{4,0},{1,9},{9... | collective-permute-start | bytes 393224 | tf_op jit(solution)/shard_map/ppermute | solution.py:104
  56.5 5.3 %collective-permute-start.10 = (bf16[128,512]{1,0:T(8,128)(2,1)S(1)}, bf16[128,512]{1,0:T(8,128)(2,1)S(1)}, u32[]{:S(2)}, u32[]{:S(2)}) collective-permute-start(bf16[128,512]{1,0:T(8,128)(2,1)S(1)} %get-tuple-element.54), channel_id=1, source_target_pairs={{0,8},{8,16},{16,24},{24,28},{28,20},{20,12},{12,4},{4,0},{1,9},{9... | collective-permute-start | bytes 393224 | tf_op jit(solution)/shard_map/ppermute | solution.py:104
  57.3 6.9 %collective-permute-start.18 = (bf16[128,512]{1,0:T(8,128)(2,1)S(1)}, bf16[128,512]{1,0:T(8,128)(2,1)S(1)}, u32[]{:S(2)}, u32[]{:S(2)}) collective-permute-start(bf16[128,512]{1,0:T(8,128)(2,1)S(1)} %get-tuple-element.65), channel_id=1, source_target_pairs={{8,0},{16,8},{24,16},{28,24},{20,28},{12,20},{4,12},{0,4},{9,1},{1... | collective-permute-start | bytes 393224 | tf_op jit(solution)/shard_map/ppermute | solution.py:104
  58.8 5.9 %collective-permute-start.25 = (bf16[128,512]{1,0:T(8,128)(2,1)S(1)}, bf16[128,512]{1,0:T(8,128)(2,1)S(1)}, u32[]{:S(2)}, u32[]{:S(2)}) collective-permute-start(bf16[128,512]{1,0:T(8,128)(2,1)S(1)} %get-tuple-element.66), channel_id=1, source_target_pairs={{8,0},{16,8},{24,16},{28,24},{20,28},{12,20},{4,12},{0,4},{9,1},{1... | collective-permute-start | bytes 393224 | tf_op jit(solution)/shard_map/ppermute | solution.py:104
  61.9 5.0 %collective-permute-start.4 = (bf16[128,512]{1,0:T(8,128)(2,1)S(1)}, bf16[128,512]{1,0:T(8,128)(2,1)S(1)}, u32[]{:S(2)}, u32[]{:S(2)}) collective-permute-start(bf16[128,512]{1,0:T(8,128)(2,1)S(1)} %get-tuple-element.51), channel_id=1, source_target_pairs={{0,8},{8,16},{16,24},{24,28},{28,20},{20,12},{12,4},{4,0},{1,9},{9... | collective-permute-start | bytes 393224 | tf_op jit(solution)/shard_map/ppermute | solution.py:104
  63.6 6.4 %collective-permute-start.11 = (bf16[128,512]{1,0:T(8,128)(2,1)S(1)}, bf16[128,512]{1,0:T(8,128)(2,1)S(1)}, u32[]{:S(2)}, u32[]{:S(2)}) collective-permute-start(bf16[128,512]{1,0:T(8,128)(2,1)S(1)} %get-tuple-element.52), channel_id=1, source_target_pairs={{0,8},{8,16},{16,24},{24,28},{28,20},{20,12},{12,4},{4,0},{1,9},{9... | collective-permute-start | bytes 393224 | tf_op jit(solution)/shard_map/ppermute | solution.py:104
  64.8 7.6 %collective-permute-start.19 = (bf16[128,512]{1,0:T(8,128)(2,1)S(1)}, bf16[128,512]{1,0:T(8,128)(2,1)S(1)}, u32[]{:S(2)}, u32[]{:S(2)}) collective-permute-start(bf16[128,512]{1,0:T(8,128)(2,1)S(1)} %get-tuple-element.63), channel_id=1, source_target_pairs={{8,0},{16,8},{24,16},{28,24},{20,28},{12,20},{4,12},{0,4},{9,1},{1... | collective-permute-start | bytes 393224 | tf_op jit(solution)/shard_map/ppermute | solution.py:104
  66.0 6.9 %collective-permute-start.26 = (bf16[128,512]{1,0:T(8,128)(2,1)S(1)}, bf16[128,512]{1,0:T(8,128)(2,1)S(1)}, u32[]{:S(2)}, u32[]{:S(2)}) collective-permute-start(bf16[128,512]{1,0:T(8,128)(2,1)S(1)} %get-tuple-element.64), channel_id=1, source_target_pairs={{8,0},{16,8},{24,16},{28,24},{20,28},{12,20},{4,12},{0,4},{9,1},{1... | collective-permute-start | bytes 393224 | tf_op jit(solution)/shard_map/ppermute | solution.py:104
  70.1 5.9 %collective-permute-start.5 = (bf16[128,512]{1,0:T(8,128)(2,1)S(1)}, bf16[128,512]{1,0:T(8,128)(2,1)S(1)}, u32[]{:S(2)}, u32[]{:S(2)}) collective-permute-start(bf16[128,512]{1,0:T(8,128)(2,1)S(1)} %get-tuple-element.49), channel_id=1, source_target_pairs={{0,8},{8,16},{16,24},{24,28},{28,20},{20,12},{12,4},{4,0},{1,9},{9... | collective-permute-start | bytes 393224 | tf_op jit(solution)/shard_map/ppermute | solution.py:104
  71.9 6.9 %collective-permute-start.12 = (bf16[128,512]{1,0:T(8,128)(2,1)S(1)}, bf16[128,512]{1,0:T(8,128)(2,1)S(1)}, u32[]{:S(2)}, u32[]{:S(2)}) collective-permute-start(bf16[128,512]{1,0:T(8,128)(2,1)S(1)} %get-tuple-element.50), channel_id=1, source_target_pairs={{0,8},{8,16},{16,24},{24,28},{28,20},{20,12},{12,4},{4,0},{1,9},{9... | collective-permute-start | bytes 393224 | tf_op jit(solution)/shard_map/ppermute | solution.py:104
  73.1 8.5 %collective-permute-start.20 = (bf16[128,512]{1,0:T(8,128)(2,1)S(1)}, bf16[128,512]{1,0:T(8,128)(2,1)S(1)}, u32[]{:S(2)}, u32[]{:S(2)}) collective-permute-start(bf16[128,512]{1,0:T(8,128)(2,1)S(1)} %get-tuple-element.61), channel_id=1, source_target_pairs={{8,0},{16,8},{24,16},{28,24},{20,28},{12,20},{4,12},{0,4},{9,1},{1... | collective-permute-start | bytes 393224 | tf_op jit(solution)/shard_map/ppermute | solution.py:104
  74.1 8.0 %collective-permute-start.27 = (bf16[128,512]{1,0:T(8,128)(2,1)S(1)}, bf16[128,512]{1,0:T(8,128)(2,1)S(1)}, u32[]{:S(2)}, u32[]{:S(2)}) collective-permute-start(bf16[128,512]{1,0:T(8,128)(2,1)S(1)} %get-tuple-element.62), channel_id=1, source_target_pairs={{8,0},{16,8},{24,16},{28,24},{20,28},{12,20},{4,12},{0,4},{9,1},{1... | collective-permute-start | bytes 393224 | tf_op jit(solution)/shard_map/ppermute | solution.py:104
  78.9 6.3 %collective-permute-start.6 = (bf16[128,512]{1,0:T(8,128)(2,1)S(1)}, bf16[128,512]{1,0:T(8,128)(2,1)S(1)}, u32[]{:S(2)}, u32[]{:S(2)}) collective-permute-start(bf16[128,512]{1,0:T(8,128)(2,1)S(1)} %get-tuple-element.47), channel_id=1, source_target_pairs={{0,8},{8,16},{16,24},{24,28},{28,20},{20,12},{12,4},{4,0},{1,9},{9... | collective-permute-start | bytes 393224 | tf_op jit(solution)/shard_map/ppermute | solution.py:104
  81.0 6.8 %collective-permute-start.13 = (bf16[128,512]{1,0:T(8,128)(2,1)S(1)}, bf16[128,512]{1,0:T(8,128)(2,1)S(1)}, u32[]{:S(2)}, u32[]{:S(2)}) collective-permute-start(bf16[128,512]{1,0:T(8,128)(2,1)S(1)} %get-tuple-element.48), channel_id=1, source_target_pairs={{0,8},{8,16},{16,24},{24,28},{28,20},{20,12},{12,4},{4,0},{1,9},{9... | collective-permute-start | bytes 393224 | tf_op jit(solution)/shard_map/ppermute | solution.py:104
  82.2 8.1 %collective-permute-start.21 = (bf16[128,512]{1,0:T(8,128)(2,1)S(1)}, bf16[128,512]{1,0:T(8,128)(2,1)S(1)}, u32[]{:S(2)}, u32[]{:S(2)}) collective-permute-start(bf16[128,512]{1,0:T(8,128)(2,1)S(1)} %get-tuple-element.59), channel_id=1, source_target_pairs={{8,0},{16,8},{24,16},{28,24},{20,28},{12,20},{4,12},{0,4},{9,1},{1... | collective-permute-start | bytes 393224 | tf_op jit(solution)/shard_map/ppermute | solution.py:104
  83.2 7.0 %collective-permute-start.28 = (bf16[128,512]{1,0:T(8,128)(2,1)S(1)}, bf16[128,512]{1,0:T(8,128)(2,1)S(1)}, u32[]{:S(2)}, u32[]{:S(2)}) collective-permute-start(bf16[128,512]{1,0:T(8,128)(2,1)S(1)} %get-tuple-element.60), channel_id=1, source_target_pairs={{8,0},{16,8},{24,16},{28,24},{20,28},{12,20},{4,12},{0,4},{9,1},{1... | collective-permute-start | bytes 393224 | tf_op jit(solution)/shard_map/ppermute | solution.py:104
  87.9 5.0 %collective-permute-start.7 = (bf16[128,512]{1,0:T(8,128)(2,1)S(1)}, bf16[128,512]{1,0:T(8,128)(2,1)S(1)}, u32[]{:S(2)}, u32[]{:S(2)}) collective-permute-start(bf16[128,512]{1,0:T(8,128)(2,1)S(1)} %get-tuple-element.45), channel_id=1, source_target_pairs={{0,8},{8,16},{16,24},{24,28},{28,20},{20,12},{12,4},{4,0},{1,9},{9... | collective-permute-start | bytes 393224 | tf_op jit(solution)/shard_map/ppermute | solution.py:104
  89.7 5.0 %collective-permute-start.14 = (bf16[128,512]{1,0:T(8,128)(2,1)S(1)}, bf16[128,512]{1,0:T(8,128)(2,1)S(1)}, u32[]{:S(2)}, u32[]{:S(2)}) collective-permute-start(bf16[128,512]{1,0:T(8,128)(2,1)S(1)} %get-tuple-element.46), channel_id=1, source_target_pairs={{0,8},{8,16},{16,24},{24,28},{28,20},{20,12},{12,4},{4,0},{1,9},{9... | collective-permute-start | bytes 393224 | tf_op jit(solution)/shard_map/ppermute | solution.py:104
  94.7 3.6 %collective-permute-start.29 = (bf16[3,2048]{1,0:T(4,128)(2,1)S(1)}, bf16[3,2048]{1,0:T(4,128)(2,1)S(1)}, u32[]{:S(2)}, u32[]{:S(2)}) collective-permute-start(bf16[3,2048]{1,0:T(4,128)(2,1)S(1)} %pad_maximum_fusion.1), channel_id=1, source_target_pairs={{0,4},{4,8},{8,12},{12,16},{16,20},{20,24},{24,28},{1,5},{5,9},{9,... | collective-permute-start | bytes 36872 | tf_op jit(solution)/shard_map/ppermute | solution.py:13
  110.3 14.0 %collective-permute-start.31 = (bf16[128,2048]{1,0:T(8,128)(2,1)S(1)}, bf16[128,2048]{1,0:T(8,128)(2,1)S(1)}, u32[]{:S(2)}, u32[]{:S(2)}) collective-permute-start(bf16[128,2048]{1,0:T(8,128)(2,1)S(1)} %fusion.27), channel_id=1, source_target_pairs={{0,2},{1,3},{2,0},{3,1},{4,6},{5,7},{6,4},{7,5},{8,10},{9,11},{10,... | collective-permute-start | bytes 1572872 | tf_op jit(solution)/shard_map/ppermute | solution.py:120
  124.7 2.7 %collective-permute-start.32 = (f32[128,2048]{1,0:T(8,128)S(1)}, f32[128,2048]{1,0:T(8,128)S(1)}, u32[]{:S(2)}, u32[]{:S(2)}) collective-permute-start(f32[128,2048]{1,0:T(8,128)S(1)} %convert_add_fusion.1), channel_id=1, source_target_pairs={{0,1},{1,0},{2,3},{3,2},{4,5},{5,4},{6,7},{7,6},{8,9},{9,8},{10,11... | collective-permute-start | bytes 3145736 | tf_op jit(solution)/shard_map/ppermute | solution.py:123
  146.7 6.4 %collective-permute-start.33 = (f32[3,2048]{1,0:T(4,128)S(1)}, f32[3,2048]{1,0:T(4,128)S(1)}, u32[]{:S(2)}, u32[]{:S(2)}) collective-permute-start(f32[3,2048]{1,0:T(4,128)S(1)} %slice_add_fusion), channel_id=1, source_target_pairs={{4,0},{8,4},{12,8},{16,12},{20,16},{24,20},{28,24},{5,1},{9,5},{13... | collective-permute-start | bytes 73736 | tf_op jit(solution)/shard_map/ppermute | solution.py:13
  153.5 8.2 %collective-permute-start.55 = (bf16[128,512]{1,0:T(8,128)(2,1)S(1)}, bf16[128,512]{1,0:T(8,128)(2,1)S(1)}, u32[]{:S(2)}, u32[]{:S(2)}) collective-permute-start(bf16[128,512]{1,0:T(8,128)(2,1)S(1)} %get-tuple-element.79), channel_id=1, source_target_pairs={{8,0},{16,8},{24,16},{28,24},{20,28},{12,20},{4,12},{0,4},{9,1},{1... | collective-permute-start | bytes 393224 | tf_op jit(solution)/shard_map/ppermute | solution.py:77
  156.8 7.8 %collective-permute-start.48 = (bf16[128,512]{1,0:T(8,128)(2,1)S(1)}, bf16[128,512]{1,0:T(8,128)(2,1)S(1)}, u32[]{:S(2)}, u32[]{:S(2)}) collective-permute-start(bf16[128,512]{1,0:T(8,128)(2,1)S(1)} %get-tuple-element.80), channel_id=1, source_target_pairs={{8,0},{16,8},{24,16},{28,24},{20,28},{12,20},{4,12},{0,4},{9,1},{1... | collective-permute-start | bytes 393224 | tf_op jit(solution)/shard_map/ppermute | solution.py:77
  158.0 7.9 %collective-permute-start.41 = (bf16[128,512]{1,0:T(8,128)(2,1)S(1)}, bf16[128,512]{1,0:T(8,128)(2,1)S(1)}, u32[]{:S(2)}, u32[]{:S(2)}) collective-permute-start(bf16[128,512]{1,0:T(8,128)(2,1)S(1)} %get-tuple-element.81), channel_id=1, source_target_pairs={{0,8},{8,16},{16,24},{24,28},{28,20},{20,12},{12,4},{4,0},{1,9},{9... | collective-permute-start | bytes 393224 | tf_op jit(solution)/shard_map/ppermute | solution.py:77
  158.8 7.8 %collective-permute-start.34 = (bf16[128,512]{1,0:T(8,128)(2,1)S(1)}, bf16[128,512]{1,0:T(8,128)(2,1)S(1)}, u32[]{:S(2)}, u32[]{:S(2)}) collective-permute-start(bf16[128,512]{1,0:T(8,128)(2,1)S(1)} %get-tuple-element.78), channel_id=1, source_target_pairs={{0,8},{8,16},{16,24},{24,28},{28,20},{20,12},{12,4},{4,0},{1,9},{9... | collective-permute-start | bytes 393224 | tf_op jit(solution)/shard_map/ppermute | solution.py:77
  161.7 6.6 %collective-permute-start.56 = (bf16[128,512]{1,0:T(8,128)(2,1)S(1)}, bf16[128,512]{1,0:T(8,128)(2,1)S(1)}, u32[]{:S(2)}, u32[]{:S(2)}) collective-permute-start(bf16[128,512]{1,0:T(8,128)(2,1)S(1)} %collective-permute-done.55), channel_id=1, source_target_pairs={{8,0},{16,8},{24,16},{28,24},{20,28},{12,20},{4,12},{0,4},{9,1},{1... | collective-permute-start | bytes 393224 | tf_op jit(solution)/shard_map/ppermute | solution.py:77
  164.5 6.4 %collective-permute-start.49 = (bf16[128,512]{1,0:T(8,128)(2,1)S(1)}, bf16[128,512]{1,0:T(8,128)(2,1)S(1)}, u32[]{:S(2)}, u32[]{:S(2)}) collective-permute-start(bf16[128,512]{1,0:T(8,128)(2,1)S(1)} %collective-permute-done.48), channel_id=1, source_target_pairs={{8,0},{16,8},{24,16},{28,24},{20,28},{12,20},{4,12},{0,4},{9,1},{1... | collective-permute-start | bytes 393224 | tf_op jit(solution)/shard_map/ppermute | solution.py:77
  166.0 6.4 %collective-permute-start.42 = (bf16[128,512]{1,0:T(8,128)(2,1)S(1)}, bf16[128,512]{1,0:T(8,128)(2,1)S(1)}, u32[]{:S(2)}, u32[]{:S(2)}) collective-permute-start(bf16[128,512]{1,0:T(8,128)(2,1)S(1)} %collective-permute-done.41), channel_id=1, source_target_pairs={{0,8},{8,16},{16,24},{24,28},{28,20},{20,12},{12,4},{4,0},{1,9},{9... | collective-permute-start | bytes 393224 | tf_op jit(solution)/shard_map/ppermute | solution.py:77
  166.6 7.1 %collective-permute-start.35 = (bf16[128,512]{1,0:T(8,128)(2,1)S(1)}, bf16[128,512]{1,0:T(8,128)(2,1)S(1)}, u32[]{:S(2)}, u32[]{:S(2)}) collective-permute-start(bf16[128,512]{1,0:T(8,128)(2,1)S(1)} %collective-permute-done.34), channel_id=1, source_target_pairs={{0,8},{8,16},{16,24},{24,28},{28,20},{20,12},{12,4},{4,0},{1,9},{9... | collective-permute-start | bytes 393224 | tf_op jit(solution)/shard_map/ppermute | solution.py:77
  168.4 7.1 %collective-permute-start.57 = (bf16[128,512]{1,0:T(8,128)(2,1)S(1)}, bf16[128,512]{1,0:T(8,128)(2,1)S(1)}, u32[]{:S(2)}, u32[]{:S(2)}) collective-permute-start(bf16[128,512]{1,0:T(8,128)(2,1)S(1)} %collective-permute-done.56), channel_id=1, source_target_pairs={{8,0},{16,8},{24,16},{28,24},{20,28},{12,20},{4,12},{0,4},{9,1},{1... | collective-permute-start | bytes 393224 | tf_op jit(solution)/shard_map/ppermute | solution.py:77
  171.0 6.3 %collective-permute-start.50 = (bf16[128,512]{1,0:T(8,128)(2,1)S(1)}, bf16[128,512]{1,0:T(8,128)(2,1)S(1)}, u32[]{:S(2)}, u32[]{:S(2)}) collective-permute-start(bf16[128,512]{1,0:T(8,128)(2,1)S(1)} %collective-permute-done.49), channel_id=1, source_target_pairs={{8,0},{16,8},{24,16},{28,24},{20,28},{12,20},{4,12},{0,4},{9,1},{1... | collective-permute-start | bytes 393224 | tf_op jit(solution)/shard_map/ppermute | solution.py:77
  172.3 6.3 %collective-permute-start.43 = (bf16[128,512]{1,0:T(8,128)(2,1)S(1)}, bf16[128,512]{1,0:T(8,128)(2,1)S(1)}, u32[]{:S(2)}, u32[]{:S(2)}) collective-permute-start(bf16[128,512]{1,0:T(8,128)(2,1)S(1)} %collective-permute-done.42), channel_id=1, source_target_pairs={{0,8},{8,16},{16,24},{24,28},{28,20},{20,12},{12,4},{4,0},{1,9},{9... | collective-permute-start | bytes 393224 | tf_op jit(solution)/shard_map/ppermute | solution.py:77
  173.7 7.3 %collective-permute-start.36 = (bf16[128,512]{1,0:T(8,128)(2,1)S(1)}, bf16[128,512]{1,0:T(8,128)(2,1)S(1)}, u32[]{:S(2)}, u32[]{:S(2)}) collective-permute-start(bf16[128,512]{1,0:T(8,128)(2,1)S(1)} %collective-permute-done.35), channel_id=1, source_target_pairs={{0,8},{8,16},{16,24},{24,28},{28,20},{20,12},{12,4},{4,0},{1,9},{9... | collective-permute-start | bytes 393224 | tf_op jit(solution)/shard_map/ppermute | solution.py:77
  175.5 6.6 %collective-permute-start.58 = (bf16[128,512]{1,0:T(8,128)(2,1)S(1)}, bf16[128,512]{1,0:T(8,128)(2,1)S(1)}, u32[]{:S(2)}, u32[]{:S(2)}) collective-permute-start(bf16[128,512]{1,0:T(8,128)(2,1)S(1)} %collective-permute-done.57), channel_id=1, source_target_pairs={{8,0},{16,8},{24,16},{28,24},{20,28},{12,20},{4,12},{0,4},{9,1},{1... | collective-permute-start | bytes 393224 | tf_op jit(solution)/shard_map/ppermute | solution.py:77
  177.3 6.6 %collective-permute-start.51 = (bf16[128,512]{1,0:T(8,128)(2,1)S(1)}, bf16[128,512]{1,0:T(8,128)(2,1)S(1)}, u32[]{:S(2)}, u32[]{:S(2)}) collective-permute-start(bf16[128,512]{1,0:T(8,128)(2,1)S(1)} %collective-permute-done.50), channel_id=1, source_target_pairs={{8,0},{16,8},{24,16},{28,24},{20,28},{12,20},{4,12},{0,4},{9,1},{1... | collective-permute-start | bytes 393224 | tf_op jit(solution)/shard_map/ppermute | solution.py:77
  178.7 6.3 %collective-permute-start.44 = (bf16[128,512]{1,0:T(8,128)(2,1)S(1)}, bf16[128,512]{1,0:T(8,128)(2,1)S(1)}, u32[]{:S(2)}, u32[]{:S(2)}) collective-permute-start(bf16[128,512]{1,0:T(8,128)(2,1)S(1)} %collective-permute-done.43), channel_id=1, source_target_pairs={{0,8},{8,16},{16,24},{24,28},{28,20},{20,12},{12,4},{4,0},{1,9},{9... | collective-permute-start | bytes 393224 | tf_op jit(solution)/shard_map/ppermute | solution.py:77
  181.1 6.6 %collective-permute-start.37 = (bf16[128,512]{1,0:T(8,128)(2,1)S(1)}, bf16[128,512]{1,0:T(8,128)(2,1)S(1)}, u32[]{:S(2)}, u32[]{:S(2)}) collective-permute-start(bf16[128,512]{1,0:T(8,128)(2,1)S(1)} %collective-permute-done.36), channel_id=1, source_target_pairs={{0,8},{8,16},{16,24},{24,28},{28,20},{20,12},{12,4},{4,0},{1,9},{9... | collective-permute-start | bytes 393224 | tf_op jit(solution)/shard_map/ppermute | solution.py:77
  182.1 6.4 %collective-permute-start.59 = (bf16[128,512]{1,0:T(8,128)(2,1)S(1)}, bf16[128,512]{1,0:T(8,128)(2,1)S(1)}, u32[]{:S(2)}, u32[]{:S(2)}) collective-permute-start(bf16[128,512]{1,0:T(8,128)(2,1)S(1)} %collective-permute-done.58), channel_id=1, source_target_pairs={{8,0},{16,8},{24,16},{28,24},{20,28},{12,20},{4,12},{0,4},{9,1},{1... | collective-permute-start | bytes 393224 | tf_op jit(solution)/shard_map/ppermute | solution.py:77
  183.8 6.7 %collective-permute-start.52 = (bf16[128,512]{1,0:T(8,128)(2,1)S(1)}, bf16[128,512]{1,0:T(8,128)(2,1)S(1)}, u32[]{:S(2)}, u32[]{:S(2)}) collective-permute-start(bf16[128,512]{1,0:T(8,128)(2,1)S(1)} %collective-permute-done.51), channel_id=1, source_target_pairs={{8,0},{16,8},{24,16},{28,24},{20,28},{12,20},{4,12},{0,4},{9,1},{1... | collective-permute-start | bytes 393224 | tf_op jit(solution)/shard_map/ppermute | solution.py:77
  185.0 6.7 %collective-permute-start.45 = (bf16[128,512]{1,0:T(8,128)(2,1)S(1)}, bf16[128,512]{1,0:T(8,128)(2,1)S(1)}, u32[]{:S(2)}, u32[]{:S(2)}) collective-permute-start(bf16[128,512]{1,0:T(8,128)(2,1)S(1)} %collective-permute-done.44), channel_id=1, source_target_pairs={{0,8},{8,16},{16,24},{24,28},{28,20},{20,12},{12,4},{4,0},{1,9},{9... | collective-permute-start | bytes 393224 | tf_op jit(solution)/shard_map/ppermute | solution.py:77
  187.6 5.5 %collective-permute-start.38 = (bf16[128,512]{1,0:T(8,128)(2,1)S(1)}, bf16[128,512]{1,0:T(8,128)(2,1)S(1)}, u32[]{:S(2)}, u32[]{:S(2)}) collective-permute-start(bf16[128,512]{1,0:T(8,128)(2,1)S(1)} %collective-permute-done.37), channel_id=1, source_target_pairs={{0,8},{8,16},{16,24},{24,28},{28,20},{20,12},{12,4},{4,0},{1,9},{9... | collective-permute-start | bytes 393224 | tf_op jit(solution)/shard_map/ppermute | solution.py:77
  188.5 6.4 %collective-permute-start.60 = (bf16[128,512]{1,0:T(8,128)(2,1)S(1)}, bf16[128,512]{1,0:T(8,128)(2,1)S(1)}, u32[]{:S(2)}, u32[]{:S(2)}) collective-permute-start(bf16[128,512]{1,0:T(8,128)(2,1)S(1)} %collective-permute-done.59), channel_id=1, source_target_pairs={{8,0},{16,8},{24,16},{28,24},{20,28},{12,20},{4,12},{0,4},{9,1},{1... | collective-permute-start | bytes 393224 | tf_op jit(solution)/shard_map/ppermute | solution.py:77
  190.5 5.7 %collective-permute-start.53 = (bf16[128,512]{1,0:T(8,128)(2,1)S(1)}, bf16[128,512]{1,0:T(8,128)(2,1)S(1)}, u32[]{:S(2)}, u32[]{:S(2)}) collective-permute-start(bf16[128,512]{1,0:T(8,128)(2,1)S(1)} %collective-permute-done.52), channel_id=1, source_target_pairs={{8,0},{16,8},{24,16},{28,24},{20,28},{12,20},{4,12},{0,4},{9,1},{1... | collective-permute-start | bytes 393224 | tf_op jit(solution)/shard_map/ppermute | solution.py:77
  191.7 6.1 %collective-permute-start.46 = (bf16[128,512]{1,0:T(8,128)(2,1)S(1)}, bf16[128,512]{1,0:T(8,128)(2,1)S(1)}, u32[]{:S(2)}, u32[]{:S(2)}) collective-permute-start(bf16[128,512]{1,0:T(8,128)(2,1)S(1)} %collective-permute-done.45), channel_id=1, source_target_pairs={{0,8},{8,16},{16,24},{24,28},{28,20},{20,12},{12,4},{4,0},{1,9},{9... | collective-permute-start | bytes 393224 | tf_op jit(solution)/shard_map/ppermute | solution.py:77
  193.1 6.0 %collective-permute-start.39 = (bf16[128,512]{1,0:T(8,128)(2,1)S(1)}, bf16[128,512]{1,0:T(8,128)(2,1)S(1)}, u32[]{:S(2)}, u32[]{:S(2)}) collective-permute-start(bf16[128,512]{1,0:T(8,128)(2,1)S(1)} %collective-permute-done.38), channel_id=1, source_target_pairs={{0,8},{8,16},{16,24},{24,28},{28,20},{20,12},{12,4},{4,0},{1,9},{9... | collective-permute-start | bytes 393224 | tf_op jit(solution)/shard_map/ppermute | solution.py:77
  194.9 5.0 %collective-permute-start.61 = (bf16[128,512]{1,0:T(8,128)(2,1)S(1)}, bf16[128,512]{1,0:T(8,128)(2,1)S(1)}, u32[]{:S(2)}, u32[]{:S(2)}) collective-permute-start(bf16[128,512]{1,0:T(8,128)(2,1)S(1)} %collective-permute-done.60), channel_id=1, source_target_pairs={{8,0},{16,8},{24,16},{28,24},{20,28},{12,20},{4,12},{0,4},{9,1},{1... | collective-permute-start | bytes 393224 | tf_op jit(solution)/shard_map/ppermute | solution.py:77
  196.3 5.0 %collective-permute-start.54 = (bf16[128,512]{1,0:T(8,128)(2,1)S(1)}, bf16[128,512]{1,0:T(8,128)(2,1)S(1)}, u32[]{:S(2)}, u32[]{:S(2)}) collective-permute-start(bf16[128,512]{1,0:T(8,128)(2,1)S(1)} %collective-permute-done.53), channel_id=1, source_target_pairs={{8,0},{16,8},{24,16},{28,24},{20,28},{12,20},{4,12},{0,4},{9,1},{1... | collective-permute-start | bytes 393224 | tf_op jit(solution)/shard_map/ppermute | solution.py:77
  197.7 5.0 %collective-permute-start.47 = (bf16[128,512]{1,0:T(8,128)(2,1)S(1)}, bf16[128,512]{1,0:T(8,128)(2,1)S(1)}, u32[]{:S(2)}, u32[]{:S(2)}) collective-permute-start(bf16[128,512]{1,0:T(8,128)(2,1)S(1)} %collective-permute-done.46), channel_id=1, source_target_pairs={{0,8},{8,16},{16,24},{24,28},{28,20},{20,12},{12,4},{4,0},{1,9},{9... | collective-permute-start | bytes 393224 | tf_op jit(solution)/shard_map/ppermute | solution.py:77
  199.1 5.0 %collective-permute-start.40 = (bf16[128,512]{1,0:T(8,128)(2,1)S(1)}, bf16[128,512]{1,0:T(8,128)(2,1)S(1)}, u32[]{:S(2)}, u32[]{:S(2)}) collective-permute-start(bf16[128,512]{1,0:T(8,128)(2,1)S(1)} %collective-permute-done.39), channel_id=1, source_target_pairs={{0,8},{8,16},{16,24},{24,28},{28,20},{20,12},{12,4},{4,0},{1,9},{9... | collective-permute-start | bytes 393224 | tf_op jit(solution)/shard_map/ppermute | solution.py:77
  208.0 8.4 %collective-permute-start.63 = (bf16[256,512]{1,0:T(8,128)(2,1)S(1)}, bf16[256,512]{1,0:T(8,128)(2,1)S(1)}, u32[]{:S(2)}, u32[]{:S(2)}) collective-permute-start(bf16[256,512]{1,0:T(8,128)(2,1)S(1)} %bitcast_convert_fusion), channel_id=1, source_target_pairs={{0,2},{1,3},{2,0},{3,1},{4,6},{5,7},{6,4},{7,5},{8,10},{9,11},{10,... | collective-permute-start | bytes 786440 | tf_op jit(solution)/shard_map/ppermute | solution.py:139
  216.5 13.3 %collective-permute-start.64 = (bf16[128,512]{1,0:T(8,128)(2,1)S(1)}, bf16[128,512]{1,0:T(8,128)(2,1)S(1)}, u32[]{:S(2)}, u32[]{:S(2)}) collective-permute-start(bf16[128,512]{1,0:T(8,128)(2,1)S(1)} %get-tuple-element.89), channel_id=1, source_target_pairs={{0,4},{1,12},{2,20},{3,28},{4,0},{5,8},{6,16},{7,24},{8,5},{9,13},... | collective-permute-start | bytes 393224 | tf_op jit(solution)/shard_map/ppermute | solution.py:44
  218.3 14.1 %collective-permute-start.65 = (bf16[128,512]{1,0:T(8,128)(2,1)S(1)}, bf16[128,512]{1,0:T(8,128)(2,1)S(1)}, u32[]{:S(2)}, u32[]{:S(2)}) collective-permute-start(bf16[128,512]{1,0:T(8,128)(2,1)S(1)} %get-tuple-element.88), channel_id=1, source_target_pairs={{0,0},{1,8},{2,16},{3,24},{4,4},{5,12},{6,20},{7,28},{8,1},{9,9},{... | collective-permute-start | bytes 393224 | tf_op jit(solution)/shard_map/ppermute | solution.py:44
  (22 other events, 151.1 us)

commit v10 on v9

--- a/solution.py
+++ b/solution.py
@@ -174,6 +174,9 @@
     gate_value = gate_branch.astype(jnp.float32)
     gate_act = jax.nn.silu(gate_value)
     conv_act = jax.nn.silu(conv_sum)
+    conv_scale, gate_scale = lax.optimization_barrier(
+        (gate_act * silu_grad(conv_sum), conv_act * silu_grad(gate_value))
+    )
     mixed = (conv_act * gate_act).astype(jnp.bfloat16)
     partial_value = jnp.dot(mixed, out_weight, preferred_element_type=jnp.float32)
     columns = tokens.shape[1] // lax.axis_size("col")
@@ -191,8 +194,8 @@
     grad_mixed = lax.dot_general(
         residual_grad, out_weight, (((1,), (1,)), ((), ())), preferred_element_type=jnp.float32
     )
-    grad_conv = grad_mixed * gate_act * silu_grad(conv_sum)
-    grad_gate = (grad_mixed * conv_act * silu_grad(gate_value)).astype(jnp.bfloat16)
+    grad_conv = grad_mixed * conv_scale
+    grad_gate = (grad_mixed * gate_scale).astype(jnp.bfloat16)
     local_grad = conv_weight[0][None, :] * grad_conv
     spill_over = jnp.zeros((margin, inner_width), jnp.float32)
     for offset in range(1, CONV):

time: 234 us -> 236 us (level)
  other arithmetic: 13.5 us -> 18.1 us
    mul x0 -> x2, other arithmetic: none -> 3.76 us  [the longest x1 2.2 us: shards(): conv_act * silu_grad(gate_value)]
  transfers between devices with their start and end apart: 67 -> 67, of which waited for: 48 -> 50; matrix products, arithmetic and copies ran while one was open for 8% -> 8% of each run, Pallas kernels for 0% -> 0%
where the time goes in v10:
time: 236 us
  waiting for transfers between devices  90.4 us (38%)
  starting transfers between devices  76.4 us (32%)
  matrix products  32 us (14%)
  other arithmetic  18.1 us (8%)
  local copies, waits for them, and re-layouts  16.1 us (7%)
  between operations  2.8 us (1%)
    ppermute x28, starting transfers between devices, ring_gather(): part = lax.ppermute(part, axis, pairs)  30.2 us
    ppermute x28, starting transfers between devices, ring_reduce_scatter(): total = lax.ppermute(total, axis, pairs)  28.9 us
    ppermute x28, waiting for transfers between devices, ring_reduce_scatter(): total = lax.ppermute(total, axis, pairs)  25.7 us
    ppermute x28, waiting for transfers between devices, ring_gather(): part = lax.ppermute(part, axis, pairs)  17.1 us
    dot_general x1, matrix products, shards(): lax.dot_general(residual_grad, out_weight, (((1,), (1,)), ((), ())), pref...  13.5 us
    ppermute x1, waiting for transfers between devices, col_psum(): lax.ppermute(pair.astype(jnp.bfloat16), 'col', [(c, c ^ 2) for c in range...  13.4 us
    ppermute x2, waiting for transfers between devices, placed_blocks(): got.append(lax.ppermute(piece, ('row', 'col'), pairs))  8.57 us
    dot_general x1, matrix products, shards(): jnp.dot(mixed, out_weight, preferred_element_type=jnp.float32)  8.43 us
  transfers between devices with their start and end apart: 67, of which 50 were waited for; matrix products, arithmetic and copies ran while one was open for 8% of the time, Pallas kernels for 0%

profile of v10, /device:TPU:2, one launch (start us, length us, event | category | flops | bytes accessed | tf_op | source)
XLA Modules:
  0.0 235.9 jit_solution(15712264812183767157)
XLA Ops:
  0.7 1.6 copy.26
  3.4 5.8 %all-to-all-start = ((bf16[128,8,256]{2,0,1:T(8,128)(2,1)}), bf16[128,8,256]{2,0,1:T(8,128)(2,1)S(1)}, u32[]{:S(2)}, u32[]{:S(2)}) async-start(bf16[128,8,256]{2,0,1:T(8,128)(2,1)} %copy.28), calls=%async_computation | async-start | bytes 1048576 | tf_op jit(solution)/shard_map/all_to_all | solution.py:24
  16.0 7.7 %all-to-all-done = bf16[128,8,256]{2,0,1:T(8,128)(2,1)S(1)} async-done(((bf16[128,8,256]{2,0,1:T(8,128)(2,1)}), bf16[128,8,256]{2,0,1:T(8,128)(2,1)S(1)}, u32[]{:S(2)}, u32[]{:S(2)}) %all-to-all-start) | async-done | bytes 524320 | tf_op jit(solution)/shard_map/all_to_all | solution.py:24
  25.7 1.6 maximum_select_fusion.1
  27.3 1.6 gather_fusion.4
  28.9 4.5 %fusion.112 = (bf16[8,128,1024]{2,1,0:T(8,128)(2,1)S(1)}, f32[8,128,1024]{2,1,0:T(8,128)}) fusion(bf16[512,2048]{1,0:T(8,128)(2,1)S(1)} %copy-done.2, bf16[8,128,512]{2,1,0:T(8,128)(2,1)} %gather_fusion.4, pred[8]{0:T(512)(128)(4,1)S(1)} %get-tuple-element.111), kind=kOutput, calls=%fused_computation.252 | convolution fusion | flops 1075314688 | bytes 8389120 | tf_op jit(solution)/shard_map/dot_general | solution.py:95
  33.5 1.5 collective-permute-start.15
  35.1 1.7 gather_fusion.3
  36.8 2.7 %fusion.113 = (bf16[8,128,1024]{2,1,0:T(8,128)(2,1)S(1)}, f32[8,128,1024]{2,1,0:T(8,128)S(1)}) fusion(bf16[512,2048]{1,0:T(8,128)(2,1)S(1)} %copy-done.2, bf16[8,128,512]{2,1,0:T(8,128)(2,1)} %gather_fusion.3, pred[8]{0:T(512)(128)(4,1)} %compare_and_fusion.2), kind=kOutput, calls=%fused_computation.253 | convolution fusion | flops 1075314688 | bytes 8388616 | tf_op jit(solution)/shard_map/dot_general | solution.py:94
  39.5 2.0 collective-permute-start.1
  43.1 1.5 collective-permute-start.16
  45.9 1.7 collective-permute-done.8
  47.7 1.7 collective-permute-start.2
  50.6 1.5 collective-permute-start.17
  53.5 1.4 collective-permute-done.9
  55.0 1.4 collective-permute-start.3
  57.3 1.5 collective-permute-start.18
  60.0 1.7 collective-permute-done.10
  61.8 1.7 collective-permute-start.4
  64.7 1.3 collective-permute-start.19
  66.8 3.1 %collective-permute-done.11 = bf16[128,512]{1,0:T(8,128)(2,1)S(1)} collective-permute-done((bf16[128,512]{1,0:T(8,128)(2,1)S(1)}, bf16[128,512]{1,0:T(8,128)(2,1)S(1)}, u32[]{:S(2)}, u32[]{:S(2)}) %collective-permute-start.11) | collective-permute-done | bytes 131104 | tf_op jit(solution)/shard_map/ppermute | solution.py:104
  70.0 1.8 collective-permute-start.5
  74.3 1.7 collective-permute-done.5
  76.0 2.8 %collective-permute-done.12 = bf16[128,512]{1,0:T(8,128)(2,1)S(1)} collective-permute-done((bf16[128,512]{1,0:T(8,128)(2,1)S(1)}, bf16[128,512]{1,0:T(8,128)(2,1)S(1)}, u32[]{:S(2)}, u32[]{:S(2)}) %collective-permute-start.12) | collective-permute-done | bytes 131104 | tf_op jit(solution)/shard_map/ppermute | solution.py:104
  78.9 2.1 collective-permute-start.6
  83.2 2.0 collective-permute-done.6
  85.2 2.5 %collective-permute-done.13 = bf16[128,512]{1,0:T(8,128)(2,1)S(1)} collective-permute-done((bf16[128,512]{1,0:T(8,128)(2,1)S(1)}, bf16[128,512]{1,0:T(8,128)(2,1)S(1)}, u32[]{:S(2)}, u32[]{:S(2)}) %collective-permute-start.13) | collective-permute-done | bytes 131104 | tf_op jit(solution)/shard_map/ppermute | solution.py:104
  87.8 1.8 collective-permute-start.7
  90.3 2.6 %collective-permute-done.7 = bf16[128,512]{1,0:T(8,128)(2,1)S(1)} collective-permute-done((bf16[128,512]{1,0:T(8,128)(2,1)S(1)}, bf16[128,512]{1,0:T(8,128)(2,1)S(1)}, u32[]{:S(2)}, u32[]{:S(2)}) %collective-permute-start.7) | collective-permute-done | bytes 131104 | tf_op jit(solution)/shard_map/ppermute | solution.py:104
  92.8 1.8 collective-permute-done.14
  94.7 2.3 collective-permute-start.29
  97.1 1.2 collective-permute-done.29
  98.5 2.2 fusion.5
  100.7 8.4 %convolution_convert_fusion = bf16[128,4096]{1,0:T(8,128)(2,1)S(1)} fusion(bf16[2048,4096]{1,0:T(8,128)(2,1)} %param.23, bf16[128,2048]{1,0:T(8,128)(2,1)S(1)} %copy-done.9, f32[128,2048]{1,0:T(8,128)S(1)} %get-tuple-element.48), kind=kOutput, calls=%fused_computation.6 | convolution fusion | flops 2150891520 | bytes 19398656 | tf_op jit(solution)/shard_map/dot_general | solution.py:181
  109.2 1.9 collective-permute-done.30
  112.0 13.4 %collective-permute-done.31 = bf16[128,2048]{1,0:T(8,128)(2,1)S(1)} collective-permute-done((bf16[128,2048]{1,0:T(8,128)(2,1)S(1)}, bf16[128,2048]{1,0:T(8,128)(2,1)S(1)}, u32[]{:S(2)}, u32[]{:S(2)}) %collective-permute-start.31) | collective-permute-done | bytes 524320 | tf_op jit(solution)/shard_map/ppermute | solution.py:120
  126.0 1.6 multiply_multiply_fusion.3
  128.8 13.5 %multiply_multiply_fusion.2 = (f32[128,2048]{1,0:T(8,128)}, f32[128,2048]{1,0:T(8,128)S(1)}, bf16[128,2048]{1,0:T(8,128)(2,1)}) fusion(f32[128]{0:T(128)S(1)} %get-tuple-element.101, f32[2048]{0:T(1024)S(1)} %bitcast.324, f32[128,2048]{1,0:T(8,128)} %multiply_multiply_fusion.3, f32[128,2048]{1,0:T(8,128)} %get-tuple-element.11, ...), kind=kOutput, calls=%fused_computation.43 | convolution fusion | flops 2150891520 | bytes 24650752 | tf_op jit(solution)/shard_map/dot_general | solution.py:194
  143.8 1.3 collective-permute-start.33
  145.2 1.5 slice.317
  147.1 3.1 %collective-permute-done.33 = f32[3,2048]{1,0:T(4,128)S(1)} collective-permute-done((f32[3,2048]{1,0:T(4,128)S(1)}, f32[3,2048]{1,0:T(4,128)S(1)}, u32[]{:S(2)}, u32[]{:S(2)}) %collective-permute-start.33) | collective-permute-done | bytes 24608 | tf_op jit(solution)/shard_map/ppermute | solution.py:13
  150.6 3.2 %collective-permute-start.55 = (bf16[128,512]{1,0:T(8,128)(2,1)S(1)}, bf16[128,512]{1,0:T(8,128)(2,1)S(1)}, u32[]{:S(2)}, u32[]{:S(2)}) collective-permute-start(bf16[128,512]{1,0:T(8,128)(2,1)S(1)} %get-tuple-element.85), channel_id=1, source_target_pairs={{8,0},{16,8},{24,16},{28,24},{20,28},{12,20},{4,12},{0,4},{9,1},{1... | collective-permute-start | bytes 393224 | tf_op jit(solution)/shard_map/ppermute | solution.py:77
  154.7 1.2 collective-permute-start.41
  156.6 2.3 collective-permute-done.55
  158.9 1.5 collective-permute-start.56
  160.3 1.3 collective-permute-done.48
  161.7 1.5 collective-permute-start.49
  163.7 1.7 collective-permute-start.35
  166.0 2.1 collective-permute-done.49
  168.1 1.5 collective-permute-start.50
  170.2 1.9 collective-permute-done.35
  172.7 1.4 collective-permute-start.58
  176.4 1.9 collective-permute-done.36
  179.2 1.3 collective-permute-start.59
  181.1 1.4 collective-permute-start.52
  186.6 1.3 collective-permute-done.52
  201.6 1.6 gather_fusion.5
  203.2 1.4 broadcast_select_fusion
  205.4 2.2 collective-permute-done.62
  210.5 7.8 %collective-permute-done.63 = bf16[256,512]{1,0:T(8,128)(2,1)S(1)} collective-permute-done((bf16[256,512]{1,0:T(8,128)(2,1)S(1)}, bf16[256,512]{1,0:T(8,128)(2,1)S(1)}, u32[]{:S(2)}, u32[]{:S(2)}) %collective-permute-start.63) | collective-permute-done | bytes 262176 | tf_op jit(solution)/shard_map/ppermute | solution.py:139
  219.4 1.5 collective-permute-start.64
  220.9 4.9 %collective-permute-start.65 = (bf16[128,512]{1,0:T(8,128)(2,1)S(1)}, bf16[128,512]{1,0:T(8,128)(2,1)S(1)}, u32[]{:S(2)}, u32[]{:S(2)}) collective-permute-start(bf16[128,512]{1,0:T(8,128)(2,1)S(1)} %get-tuple-element.94), channel_id=1, source_target_pairs={{0,0},{1,8},{2,16},{3,24},{4,4},{5,12},{6,20},{7,28},{8,1},{9,9},{... | collective-permute-start | bytes 393224 | tf_op jit(solution)/shard_map/ppermute | solution.py:44
  226.6 6.6 %collective-permute-done.64 = bf16[128,512]{1,0:T(8,128)(2,1)S(1)} collective-permute-done((bf16[128,512]{1,0:T(8,128)(2,1)S(1)}, bf16[128,512]{1,0:T(8,128)(2,1)S(1)}, u32[]{:S(2)}, u32[]{:S(2)}) %collective-permute-start.64) | collective-permute-done | bytes 131104 | tf_op jit(solution)/shard_map/ppermute | solution.py:44
  233.1 2.0 collective-permute-done.65
  (220 shorter events, 60.8 us)
Async XLA Ops:
  3.4 20.3 %all-to-all-start = ((bf16[128,8,256]{2,0,1:T(8,128)(2,1)}), bf16[128,8,256]{2,0,1:T(8,128)(2,1)S(1)}, u32[]{:S(2)}, u32[]{:S(2)}) async-start(bf16[128,8,256]{2,0,1:T(8,128)(2,1)} %copy.28), calls=%async_computation | async-start | bytes 1048576 | tf_op jit(solution)/shard_map/all_to_all | solution.py:24
  33.5 8.6 %collective-permute-start.15 = (bf16[128,512]{1,0:T(8,128)(2,1)S(1)}, bf16[128,512]{1,0:T(8,128)(2,1)S(1)}, u32[]{:S(2)}, u32[]{:S(2)}) collective-permute-start(bf16[128,512]{1,0:T(8,128)(2,1)S(1)} %get-tuple-element.79), channel_id=1, source_target_pairs={{8,0},{16,8},{24,16},{28,24},{20,28},{12,20},{4,12},{0,4},{9,1},{1... | collective-permute-start | bytes 393224 | tf_op jit(solution)/shard_map/ppermute | solution.py:104
  35.0 7.1 %collective-permute-start.22 = (bf16[128,512]{1,0:T(8,128)(2,1)S(1)}, bf16[128,512]{1,0:T(8,128)(2,1)}, u32[]{:S(2)}, u32[]{:S(2)}) collective-permute-start(bf16[128,512]{1,0:T(8,128)(2,1)S(1)} %get-tuple-element.80), channel_id=1, source_target_pairs={{8,0},{16,8},{24,16},{28,24},{20,28},{12,20},{4,12},{0,4},{9,1},{1... | collective-permute-start | bytes 393224 | tf_op jit(solution)/shard_map/ppermute | solution.py:104
  39.5 6.4 %collective-permute-start.1 = (bf16[128,512]{1,0:T(8,128)(2,1)S(1)}, bf16[128,512]{1,0:T(8,128)(2,1)S(1)}, u32[]{:S(2)}, u32[]{:S(2)}) collective-permute-start(bf16[128,512]{1,0:T(8,128)(2,1)S(1)} %get-tuple-element.77), channel_id=1, source_target_pairs={{0,8},{8,16},{16,24},{24,28},{28,20},{20,12},{12,4},{4,0},{1,9},{9... | collective-permute-start | bytes 393224 | tf_op jit(solution)/shard_map/ppermute | solution.py:104
  41.5 6.1 %collective-permute-start.8 = (bf16[128,512]{1,0:T(8,128)(2,1)S(1)}, bf16[128,512]{1,0:T(8,128)(2,1)S(1)}, u32[]{:S(2)}, u32[]{:S(2)}) collective-permute-start(bf16[128,512]{1,0:T(8,128)(2,1)S(1)} %get-tuple-element.78), channel_id=1, source_target_pairs={{0,8},{8,16},{16,24},{24,28},{28,20},{20,12},{12,4},{4,0},{1,9},{9... | collective-permute-start | bytes 393224 | tf_op jit(solution)/shard_map/ppermute | solution.py:104
  43.1 6.9 %collective-permute-start.16 = (bf16[128,512]{1,0:T(8,128)(2,1)S(1)}, bf16[128,512]{1,0:T(8,128)(2,1)S(1)}, u32[]{:S(2)}, u32[]{:S(2)}) collective-permute-start(bf16[128,512]{1,0:T(8,128)(2,1)S(1)} %get-tuple-element.75), channel_id=1, source_target_pairs={{8,0},{16,8},{24,16},{28,24},{20,28},{12,20},{4,12},{0,4},{9,1},{1... | collective-permute-start | bytes 393224 | tf_op jit(solution)/shard_map/ppermute | solution.py:104
  44.6 6.0 %collective-permute-start.23 = (bf16[128,512]{1,0:T(8,128)(2,1)S(1)}, bf16[128,512]{1,0:T(8,128)(2,1)S(1)}, u32[]{:S(2)}, u32[]{:S(2)}) collective-permute-start(bf16[128,512]{1,0:T(8,128)(2,1)S(1)} %get-tuple-element.76), channel_id=1, source_target_pairs={{8,0},{16,8},{24,16},{28,24},{20,28},{12,20},{4,12},{0,4},{9,1},{1... | collective-permute-start | bytes 393224 | tf_op jit(solution)/shard_map/ppermute | solution.py:104
  47.7 5.8 %collective-permute-start.2 = (bf16[128,512]{1,0:T(8,128)(2,1)S(1)}, bf16[128,512]{1,0:T(8,128)(2,1)S(1)}, u32[]{:S(2)}, u32[]{:S(2)}) collective-permute-start(bf16[128,512]{1,0:T(8,128)(2,1)S(1)} %get-tuple-element.61), channel_id=1, source_target_pairs={{0,8},{8,16},{16,24},{24,28},{28,20},{20,12},{12,4},{4,0},{1,9},{9... | collective-permute-start | bytes 393224 | tf_op jit(solution)/shard_map/ppermute | solution.py:104
  49.4 5.5 %collective-permute-start.9 = (bf16[128,512]{1,0:T(8,128)(2,1)S(1)}, bf16[128,512]{1,0:T(8,128)(2,1)S(1)}, u32[]{:S(2)}, u32[]{:S(2)}) collective-permute-start(bf16[128,512]{1,0:T(8,128)(2,1)S(1)} %get-tuple-element.62), channel_id=1, source_target_pairs={{0,8},{8,16},{16,24},{24,28},{28,20},{20,12},{12,4},{4,0},{1,9},{9... | collective-permute-start | bytes 393224 | tf_op jit(solution)/shard_map/ppermute | solution.py:104
  50.6 6.4 %collective-permute-start.17 = (bf16[128,512]{1,0:T(8,128)(2,1)S(1)}, bf16[128,512]{1,0:T(8,128)(2,1)S(1)}, u32[]{:S(2)}, u32[]{:S(2)}) collective-permute-start(bf16[128,512]{1,0:T(8,128)(2,1)S(1)} %get-tuple-element.73), channel_id=1, source_target_pairs={{8,0},{16,8},{24,16},{28,24},{20,28},{12,20},{4,12},{0,4},{9,1},{1... | collective-permute-start | bytes 393224 | tf_op jit(solution)/shard_map/ppermute | solution.py:104
  52.1 5.0 %collective-permute-start.24 = (bf16[128,512]{1,0:T(8,128)(2,1)S(1)}, bf16[128,512]{1,0:T(8,128)(2,1)S(1)}, u32[]{:S(2)}, u32[]{:S(2)}) collective-permute-start(bf16[128,512]{1,0:T(8,128)(2,1)S(1)} %get-tuple-element.74), channel_id=1, source_target_pairs={{8,0},{16,8},{24,16},{28,24},{20,28},{12,20},{4,12},{0,4},{9,1},{1... | collective-permute-start | bytes 393224 | tf_op jit(solution)/shard_map/ppermute | solution.py:104
  55.0 5.0 %collective-permute-start.3 = (bf16[128,512]{1,0:T(8,128)(2,1)S(1)}, bf16[128,512]{1,0:T(8,128)(2,1)S(1)}, u32[]{:S(2)}, u32[]{:S(2)}) collective-permute-start(bf16[128,512]{1,0:T(8,128)(2,1)S(1)} %get-tuple-element.59), channel_id=1, source_target_pairs={{0,8},{8,16},{16,24},{24,28},{28,20},{20,12},{12,4},{4,0},{1,9},{9... | collective-permute-start | bytes 393224 | tf_op jit(solution)/shard_map/ppermute | solution.py:104
  56.4 5.3 %collective-permute-start.10 = (bf16[128,512]{1,0:T(8,128)(2,1)S(1)}, bf16[128,512]{1,0:T(8,128)(2,1)S(1)}, u32[]{:S(2)}, u32[]{:S(2)}) collective-permute-start(bf16[128,512]{1,0:T(8,128)(2,1)S(1)} %get-tuple-element.60), channel_id=1, source_target_pairs={{0,8},{8,16},{16,24},{24,28},{28,20},{20,12},{12,4},{4,0},{1,9},{9... | collective-permute-start | bytes 393224 | tf_op jit(solution)/shard_map/ppermute | solution.py:104
  57.3 6.9 %collective-permute-start.18 = (bf16[128,512]{1,0:T(8,128)(2,1)S(1)}, bf16[128,512]{1,0:T(8,128)(2,1)S(1)}, u32[]{:S(2)}, u32[]{:S(2)}) collective-permute-start(bf16[128,512]{1,0:T(8,128)(2,1)S(1)} %get-tuple-element.71), channel_id=1, source_target_pairs={{8,0},{16,8},{24,16},{28,24},{20,28},{12,20},{4,12},{0,4},{9,1},{1... | collective-permute-start | bytes 393224 | tf_op jit(solution)/shard_map/ppermute | solution.py:104
  58.8 5.8 %collective-permute-start.25 = (bf16[128,512]{1,0:T(8,128)(2,1)S(1)}, bf16[128,512]{1,0:T(8,128)(2,1)S(1)}, u32[]{:S(2)}, u32[]{:S(2)}) collective-permute-start(bf16[128,512]{1,0:T(8,128)(2,1)S(1)} %get-tuple-element.72), channel_id=1, source_target_pairs={{8,0},{16,8},{24,16},{28,24},{20,28},{12,20},{4,12},{0,4},{9,1},{1... | collective-permute-start | bytes 393224 | tf_op jit(solution)/shard_map/ppermute | solution.py:104
  61.8 5.0 %collective-permute-start.4 = (bf16[128,512]{1,0:T(8,128)(2,1)S(1)}, bf16[128,512]{1,0:T(8,128)(2,1)S(1)}, u32[]{:S(2)}, u32[]{:S(2)}) collective-permute-start(bf16[128,512]{1,0:T(8,128)(2,1)S(1)} %get-tuple-element.57), channel_id=1, source_target_pairs={{0,8},{8,16},{16,24},{24,28},{28,20},{20,12},{12,4},{4,0},{1,9},{9... | collective-permute-start | bytes 393224 | tf_op jit(solution)/shard_map/ppermute | solution.py:104
  63.6 6.4 %collective-permute-start.11 = (bf16[128,512]{1,0:T(8,128)(2,1)S(1)}, bf16[128,512]{1,0:T(8,128)(2,1)S(1)}, u32[]{:S(2)}, u32[]{:S(2)}) collective-permute-start(bf16[128,512]{1,0:T(8,128)(2,1)S(1)} %get-tuple-element.58), channel_id=1, source_target_pairs={{0,8},{8,16},{16,24},{24,28},{28,20},{20,12},{12,4},{4,0},{1,9},{9... | collective-permute-start | bytes 393224 | tf_op jit(solution)/shard_map/ppermute | solution.py:104
  64.7 7.7 %collective-permute-start.19 = (bf16[128,512]{1,0:T(8,128)(2,1)S(1)}, bf16[128,512]{1,0:T(8,128)(2,1)S(1)}, u32[]{:S(2)}, u32[]{:S(2)}) collective-permute-start(bf16[128,512]{1,0:T(8,128)(2,1)S(1)} %get-tuple-element.69), channel_id=1, source_target_pairs={{8,0},{16,8},{24,16},{28,24},{20,28},{12,20},{4,12},{0,4},{9,1},{1... | collective-permute-start | bytes 393224 | tf_op jit(solution)/shard_map/ppermute | solution.py:104
  66.0 6.8 %collective-permute-start.26 = (bf16[128,512]{1,0:T(8,128)(2,1)S(1)}, bf16[128,512]{1,0:T(8,128)(2,1)S(1)}, u32[]{:S(2)}, u32[]{:S(2)}) collective-permute-start(bf16[128,512]{1,0:T(8,128)(2,1)S(1)} %get-tuple-element.70), channel_id=1, source_target_pairs={{8,0},{16,8},{24,16},{28,24},{20,28},{12,20},{4,12},{0,4},{9,1},{1... | collective-permute-start | bytes 393224 | tf_op jit(solution)/shard_map/ppermute | solution.py:104
  70.0 6.0 %collective-permute-start.5 = (bf16[128,512]{1,0:T(8,128)(2,1)S(1)}, bf16[128,512]{1,0:T(8,128)(2,1)S(1)}, u32[]{:S(2)}, u32[]{:S(2)}) collective-permute-start(bf16[128,512]{1,0:T(8,128)(2,1)S(1)} %get-tuple-element.55), channel_id=1, source_target_pairs={{0,8},{8,16},{16,24},{24,28},{28,20},{20,12},{12,4},{4,0},{1,9},{9... | collective-permute-start | bytes 393224 | tf_op jit(solution)/shard_map/ppermute | solution.py:104
  71.8 6.9 %collective-permute-start.12 = (bf16[128,512]{1,0:T(8,128)(2,1)S(1)}, bf16[128,512]{1,0:T(8,128)(2,1)S(1)}, u32[]{:S(2)}, u32[]{:S(2)}) collective-permute-start(bf16[128,512]{1,0:T(8,128)(2,1)S(1)} %get-tuple-element.56), channel_id=1, source_target_pairs={{0,8},{8,16},{16,24},{24,28},{28,20},{20,12},{12,4},{4,0},{1,9},{9... | collective-permute-start | bytes 393224 | tf_op jit(solution)/shard_map/ppermute | solution.py:104
  72.9 8.6 %collective-permute-start.20 = (bf16[128,512]{1,0:T(8,128)(2,1)S(1)}, bf16[128,512]{1,0:T(8,128)(2,1)S(1)}, u32[]{:S(2)}, u32[]{:S(2)}) collective-permute-start(bf16[128,512]{1,0:T(8,128)(2,1)S(1)} %get-tuple-element.67), channel_id=1, source_target_pairs={{8,0},{16,8},{24,16},{28,24},{20,28},{12,20},{4,12},{0,4},{9,1},{1... | collective-permute-start | bytes 393224 | tf_op jit(solution)/shard_map/ppermute | solution.py:104
  74.0 7.9 %collective-permute-start.27 = (bf16[128,512]{1,0:T(8,128)(2,1)S(1)}, bf16[128,512]{1,0:T(8,128)(2,1)S(1)}, u32[]{:S(2)}, u32[]{:S(2)}) collective-permute-start(bf16[128,512]{1,0:T(8,128)(2,1)S(1)} %get-tuple-element.68), channel_id=1, source_target_pairs={{8,0},{16,8},{24,16},{28,24},{20,28},{12,20},{4,12},{0,4},{9,1},{1... | collective-permute-start | bytes 393224 | tf_op jit(solution)/shard_map/ppermute | solution.py:104
  78.9 6.3 %collective-permute-start.6 = (bf16[128,512]{1,0:T(8,128)(2,1)S(1)}, bf16[128,512]{1,0:T(8,128)(2,1)S(1)}, u32[]{:S(2)}, u32[]{:S(2)}) collective-permute-start(bf16[128,512]{1,0:T(8,128)(2,1)S(1)} %get-tuple-element.53), channel_id=1, source_target_pairs={{0,8},{8,16},{16,24},{24,28},{28,20},{20,12},{12,4},{4,0},{1,9},{9... | collective-permute-start | bytes 393224 | tf_op jit(solution)/shard_map/ppermute | solution.py:104
  80.9 6.8 %collective-permute-start.13 = (bf16[128,512]{1,0:T(8,128)(2,1)S(1)}, bf16[128,512]{1,0:T(8,128)(2,1)S(1)}, u32[]{:S(2)}, u32[]{:S(2)}) collective-permute-start(bf16[128,512]{1,0:T(8,128)(2,1)S(1)} %get-tuple-element.54), channel_id=1, source_target_pairs={{0,8},{8,16},{16,24},{24,28},{28,20},{20,12},{12,4},{4,0},{1,9},{9... | collective-permute-start | bytes 393224 | tf_op jit(solution)/shard_map/ppermute | solution.py:104
  82.0 8.2 %collective-permute-start.21 = (bf16[128,512]{1,0:T(8,128)(2,1)S(1)}, bf16[128,512]{1,0:T(8,128)(2,1)S(1)}, u32[]{:S(2)}, u32[]{:S(2)}) collective-permute-start(bf16[128,512]{1,0:T(8,128)(2,1)S(1)} %get-tuple-element.65), channel_id=1, source_target_pairs={{8,0},{16,8},{24,16},{28,24},{20,28},{12,20},{4,12},{0,4},{9,1},{1... | collective-permute-start | bytes 393224 | tf_op jit(solution)/shard_map/ppermute | solution.py:104
  83.1 7.0 %collective-permute-start.28 = (bf16[128,512]{1,0:T(8,128)(2,1)S(1)}, bf16[128,512]{1,0:T(8,128)(2,1)S(1)}, u32[]{:S(2)}, u32[]{:S(2)}) collective-permute-start(bf16[128,512]{1,0:T(8,128)(2,1)S(1)} %get-tuple-element.66), channel_id=1, source_target_pairs={{8,0},{16,8},{24,16},{28,24},{20,28},{12,20},{4,12},{0,4},{9,1},{1... | collective-permute-start | bytes 393224 | tf_op jit(solution)/shard_map/ppermute | solution.py:104
  87.8 5.0 %collective-permute-start.7 = (bf16[128,512]{1,0:T(8,128)(2,1)S(1)}, bf16[128,512]{1,0:T(8,128)(2,1)S(1)}, u32[]{:S(2)}, u32[]{:S(2)}) collective-permute-start(bf16[128,512]{1,0:T(8,128)(2,1)S(1)} %get-tuple-element.51), channel_id=1, source_target_pairs={{0,8},{8,16},{16,24},{24,28},{28,20},{20,12},{12,4},{4,0},{1,9},{9... | collective-permute-start | bytes 393224 | tf_op jit(solution)/shard_map/ppermute | solution.py:104
  89.6 5.0 %collective-permute-start.14 = (bf16[128,512]{1,0:T(8,128)(2,1)S(1)}, bf16[128,512]{1,0:T(8,128)(2,1)S(1)}, u32[]{:S(2)}, u32[]{:S(2)}) collective-permute-start(bf16[128,512]{1,0:T(8,128)(2,1)S(1)} %get-tuple-element.52), channel_id=1, source_target_pairs={{0,8},{8,16},{16,24},{24,28},{28,20},{20,12},{12,4},{4,0},{1,9},{9... | collective-permute-start | bytes 393224 | tf_op jit(solution)/shard_map/ppermute | solution.py:104
  94.7 3.6 %collective-permute-start.29 = (bf16[3,2048]{1,0:T(4,128)(2,1)S(1)}, bf16[3,2048]{1,0:T(4,128)(2,1)S(1)}, u32[]{:S(2)}, u32[]{:S(2)}) collective-permute-start(bf16[3,2048]{1,0:T(4,128)(2,1)S(1)} %pad_maximum_fusion.1), channel_id=1, source_target_pairs={{0,4},{4,8},{8,12},{12,16},{16,20},{20,24},{24,28},{1,5},{5,9},{9,... | collective-permute-start | bytes 36872 | tf_op jit(solution)/shard_map/ppermute | solution.py:13
  111.4 14.0 %collective-permute-start.31 = (bf16[128,2048]{1,0:T(8,128)(2,1)S(1)}, bf16[128,2048]{1,0:T(8,128)(2,1)S(1)}, u32[]{:S(2)}, u32[]{:S(2)}) collective-permute-start(bf16[128,2048]{1,0:T(8,128)(2,1)S(1)} %fusion.26), channel_id=1, source_target_pairs={{0,2},{1,3},{2,0},{3,1},{4,6},{5,7},{6,4},{7,5},{8,10},{9,11},{10,... | collective-permute-start | bytes 1572872 | tf_op jit(solution)/shard_map/ppermute | solution.py:120
  125.8 2.7 %collective-permute-start.32 = (f32[128,2048]{1,0:T(8,128)S(1)}, f32[128,2048]{1,0:T(8,128)S(1)}, u32[]{:S(2)}, u32[]{:S(2)}) collective-permute-start(f32[128,2048]{1,0:T(8,128)S(1)} %convert_add_fusion.1), channel_id=1, source_target_pairs={{0,1},{1,0},{2,3},{3,2},{4,5},{5,4},{6,7},{7,6},{8,9},{9,8},{10,11... | collective-permute-start | bytes 3145736 | tf_op jit(solution)/shard_map/ppermute | solution.py:123
  143.8 6.4 %collective-permute-start.33 = (f32[3,2048]{1,0:T(4,128)S(1)}, f32[3,2048]{1,0:T(4,128)S(1)}, u32[]{:S(2)}, u32[]{:S(2)}) collective-permute-start(f32[3,2048]{1,0:T(4,128)S(1)} %slice_add_fusion), channel_id=1, source_target_pairs={{4,0},{8,4},{12,8},{16,12},{20,16},{24,20},{28,24},{5,1},{9,5},{13... | collective-permute-start | bytes 73736 | tf_op jit(solution)/shard_map/ppermute | solution.py:13
  150.6 8.2 %collective-permute-start.55 = (bf16[128,512]{1,0:T(8,128)(2,1)S(1)}, bf16[128,512]{1,0:T(8,128)(2,1)S(1)}, u32[]{:S(2)}, u32[]{:S(2)}) collective-permute-start(bf16[128,512]{1,0:T(8,128)(2,1)S(1)} %get-tuple-element.85), channel_id=1, source_target_pairs={{8,0},{16,8},{24,16},{28,24},{20,28},{12,20},{4,12},{0,4},{9,1},{1... | collective-permute-start | bytes 393224 | tf_op jit(solution)/shard_map/ppermute | solution.py:77
  153.9 7.8 %collective-permute-start.48 = (bf16[128,512]{1,0:T(8,128)(2,1)S(1)}, bf16[128,512]{1,0:T(8,128)(2,1)S(1)}, u32[]{:S(2)}, u32[]{:S(2)}) collective-permute-start(bf16[128,512]{1,0:T(8,128)(2,1)S(1)} %get-tuple-element.86), channel_id=1, source_target_pairs={{8,0},{16,8},{24,16},{28,24},{20,28},{12,20},{4,12},{0,4},{9,1},{1... | collective-permute-start | bytes 393224 | tf_op jit(solution)/shard_map/ppermute | solution.py:77
  154.7 8.5 %collective-permute-start.41 = (bf16[128,512]{1,0:T(8,128)(2,1)S(1)}, bf16[128,512]{1,0:T(8,128)(2,1)S(1)}, u32[]{:S(2)}, u32[]{:S(2)}) collective-permute-start(bf16[128,512]{1,0:T(8,128)(2,1)S(1)} %get-tuple-element.87), channel_id=1, source_target_pairs={{0,8},{8,16},{16,24},{24,28},{28,20},{20,12},{12,4},{4,0},{1,9},{9... | collective-permute-start | bytes 393224 | tf_op jit(solution)/shard_map/ppermute | solution.py:77
  155.9 7.8 %collective-permute-start.34 = (bf16[128,512]{1,0:T(8,128)(2,1)S(1)}, bf16[128,512]{1,0:T(8,128)(2,1)S(1)}, u32[]{:S(2)}, u32[]{:S(2)}) collective-permute-start(bf16[128,512]{1,0:T(8,128)(2,1)S(1)} %get-tuple-element.84), channel_id=1, source_target_pairs={{0,8},{8,16},{16,24},{24,28},{28,20},{20,12},{12,4},{4,0},{1,9},{9... | collective-permute-start | bytes 393224 | tf_op jit(solution)/shard_map/ppermute | solution.py:77
  158.9 6.6 %collective-permute-start.56 = (bf16[128,512]{1,0:T(8,128)(2,1)S(1)}, bf16[128,512]{1,0:T(8,128)(2,1)S(1)}, u32[]{:S(2)}, u32[]{:S(2)}) collective-permute-start(bf16[128,512]{1,0:T(8,128)(2,1)S(1)} %collective-permute-done.55), channel_id=1, source_target_pairs={{8,0},{16,8},{24,16},{28,24},{20,28},{12,20},{4,12},{0,4},{9,1},{1... | collective-permute-start | bytes 393224 | tf_op jit(solution)/shard_map/ppermute | solution.py:77
  161.7 6.4 %collective-permute-start.49 = (bf16[128,512]{1,0:T(8,128)(2,1)S(1)}, bf16[128,512]{1,0:T(8,128)(2,1)S(1)}, u32[]{:S(2)}, u32[]{:S(2)}) collective-permute-start(bf16[128,512]{1,0:T(8,128)(2,1)S(1)} %collective-permute-done.48), channel_id=1, source_target_pairs={{8,0},{16,8},{24,16},{28,24},{20,28},{12,20},{4,12},{0,4},{9,1},{1... | collective-permute-start | bytes 393224 | tf_op jit(solution)/shard_map/ppermute | solution.py:77
  163.1 6.4 %collective-permute-start.42 = (bf16[128,512]{1,0:T(8,128)(2,1)S(1)}, bf16[128,512]{1,0:T(8,128)(2,1)S(1)}, u32[]{:S(2)}, u32[]{:S(2)}) collective-permute-start(bf16[128,512]{1,0:T(8,128)(2,1)S(1)} %collective-permute-done.41), channel_id=1, source_target_pairs={{0,8},{8,16},{16,24},{24,28},{28,20},{20,12},{12,4},{4,0},{1,9},{9... | collective-permute-start | bytes 393224 | tf_op jit(solution)/shard_map/ppermute | solution.py:77
  163.7 8.3 %collective-permute-start.35 = (bf16[128,512]{1,0:T(8,128)(2,1)S(1)}, bf16[128,512]{1,0:T(8,128)(2,1)S(1)}, u32[]{:S(2)}, u32[]{:S(2)}) collective-permute-start(bf16[128,512]{1,0:T(8,128)(2,1)S(1)} %collective-permute-done.34), channel_id=1, source_target_pairs={{0,8},{8,16},{16,24},{24,28},{28,20},{20,12},{12,4},{4,0},{1,9},{9... | collective-permute-start | bytes 393224 | tf_op jit(solution)/shard_map/ppermute | solution.py:77
  165.5 7.2 %collective-permute-start.57 = (bf16[128,512]{1,0:T(8,128)(2,1)S(1)}, bf16[128,512]{1,0:T(8,128)(2,1)S(1)}, u32[]{:S(2)}, u32[]{:S(2)}) collective-permute-start(bf16[128,512]{1,0:T(8,128)(2,1)S(1)} %collective-permute-done.56), channel_id=1, source_target_pairs={{8,0},{16,8},{24,16},{28,24},{20,28},{12,20},{4,12},{0,4},{9,1},{1... | collective-permute-start | bytes 393224 | tf_op jit(solution)/shard_map/ppermute | solution.py:77
  168.1 6.3 %collective-permute-start.50 = (bf16[128,512]{1,0:T(8,128)(2,1)S(1)}, bf16[128,512]{1,0:T(8,128)(2,1)S(1)}, u32[]{:S(2)}, u32[]{:S(2)}) collective-permute-start(bf16[128,512]{1,0:T(8,128)(2,1)S(1)} %collective-permute-done.49), channel_id=1, source_target_pairs={{8,0},{16,8},{24,16},{28,24},{20,28},{12,20},{4,12},{0,4},{9,1},{1... | collective-permute-start | bytes 393224 | tf_op jit(solution)/shard_map/ppermute | solution.py:77
  169.6 6.0 %collective-permute-start.43 = (bf16[128,512]{1,0:T(8,128)(2,1)S(1)}, bf16[128,512]{1,0:T(8,128)(2,1)S(1)}, u32[]{:S(2)}, u32[]{:S(2)}) collective-permute-start(bf16[128,512]{1,0:T(8,128)(2,1)S(1)} %collective-permute-done.42), channel_id=1, source_target_pairs={{0,8},{8,16},{16,24},{24,28},{28,20},{20,12},{12,4},{4,0},{1,9},{9... | collective-permute-start | bytes 393224 | tf_op jit(solution)/shard_map/ppermute | solution.py:77
  172.0 6.3 %collective-permute-start.36 = (bf16[128,512]{1,0:T(8,128)(2,1)S(1)}, bf16[128,512]{1,0:T(8,128)(2,1)S(1)}, u32[]{:S(2)}, u32[]{:S(2)}) collective-permute-start(bf16[128,512]{1,0:T(8,128)(2,1)S(1)} %collective-permute-done.35), channel_id=1, source_target_pairs={{0,8},{8,16},{16,24},{24,28},{28,20},{20,12},{12,4},{4,0},{1,9},{9... | collective-permute-start | bytes 393224 | tf_op jit(solution)/shard_map/ppermute | solution.py:77
  172.7 6.4 %collective-permute-start.58 = (bf16[128,512]{1,0:T(8,128)(2,1)S(1)}, bf16[128,512]{1,0:T(8,128)(2,1)S(1)}, u32[]{:S(2)}, u32[]{:S(2)}) collective-permute-start(bf16[128,512]{1,0:T(8,128)(2,1)S(1)} %collective-permute-done.57), channel_id=1, source_target_pairs={{8,0},{16,8},{24,16},{28,24},{20,28},{12,20},{4,12},{0,4},{9,1},{1... | collective-permute-start | bytes 393224 | tf_op jit(solution)/shard_map/ppermute | solution.py:77
  174.4 6.7 %collective-permute-start.51 = (bf16[128,512]{1,0:T(8,128)(2,1)S(1)}, bf16[128,512]{1,0:T(8,128)(2,1)S(1)}, u32[]{:S(2)}, u32[]{:S(2)}) collective-permute-start(bf16[128,512]{1,0:T(8,128)(2,1)S(1)} %collective-permute-done.50), channel_id=1, source_target_pairs={{8,0},{16,8},{24,16},{28,24},{20,28},{12,20},{4,12},{0,4},{9,1},{1... | collective-permute-start | bytes 393224 | tf_op jit(solution)/shard_map/ppermute | solution.py:77
  175.6 6.9 %collective-permute-start.44 = (bf16[128,512]{1,0:T(8,128)(2,1)S(1)}, bf16[128,512]{1,0:T(8,128)(2,1)S(1)}, u32[]{:S(2)}, u32[]{:S(2)}) collective-permute-start(bf16[128,512]{1,0:T(8,128)(2,1)S(1)} %collective-permute-done.43), channel_id=1, source_target_pairs={{0,8},{8,16},{16,24},{24,28},{28,20},{20,12},{12,4},{4,0},{1,9},{9... | collective-permute-start | bytes 393224 | tf_op jit(solution)/shard_map/ppermute | solution.py:77
  178.3 5.5 %collective-permute-start.37 = (bf16[128,512]{1,0:T(8,128)(2,1)S(1)}, bf16[128,512]{1,0:T(8,128)(2,1)S(1)}, u32[]{:S(2)}, u32[]{:S(2)}) collective-permute-start(bf16[128,512]{1,0:T(8,128)(2,1)S(1)} %collective-permute-done.36), channel_id=1, source_target_pairs={{0,8},{8,16},{16,24},{24,28},{28,20},{20,12},{12,4},{4,0},{1,9},{9... | collective-permute-start | bytes 393224 | tf_op jit(solution)/shard_map/ppermute | solution.py:77
  179.2 6.4 %collective-permute-start.59 = (bf16[128,512]{1,0:T(8,128)(2,1)S(1)}, bf16[128,512]{1,0:T(8,128)(2,1)S(1)}, u32[]{:S(2)}, u32[]{:S(2)}) collective-permute-start(bf16[128,512]{1,0:T(8,128)(2,1)S(1)} %collective-permute-done.58), channel_id=1, source_target_pairs={{8,0},{16,8},{24,16},{28,24},{20,28},{12,20},{4,12},{0,4},{9,1},{1... | collective-permute-start | bytes 393224 | tf_op jit(solution)/shard_map/ppermute | solution.py:77
  181.1 6.8 %collective-permute-start.52 = (bf16[128,512]{1,0:T(8,128)(2,1)S(1)}, bf16[128,512]{1,0:T(8,128)(2,1)S(1)}, u32[]{:S(2)}, u32[]{:S(2)}) collective-permute-start(bf16[128,512]{1,0:T(8,128)(2,1)S(1)} %collective-permute-done.51), channel_id=1, source_target_pairs={{8,0},{16,8},{24,16},{28,24},{20,28},{12,20},{4,12},{0,4},{9,1},{1... | collective-permute-start | bytes 393224 | tf_op jit(solution)/shard_map/ppermute | solution.py:77
  182.5 6.3 %collective-permute-start.45 = (bf16[128,512]{1,0:T(8,128)(2,1)S(1)}, bf16[128,512]{1,0:T(8,128)(2,1)S(1)}, u32[]{:S(2)}, u32[]{:S(2)}) collective-permute-start(bf16[128,512]{1,0:T(8,128)(2,1)S(1)} %collective-permute-done.44), channel_id=1, source_target_pairs={{0,8},{8,16},{16,24},{24,28},{28,20},{20,12},{12,4},{4,0},{1,9},{9... | collective-permute-start | bytes 393224 | tf_op jit(solution)/shard_map/ppermute | solution.py:77
  183.8 7.0 %collective-permute-start.38 = (bf16[128,512]{1,0:T(8,128)(2,1)S(1)}, bf16[128,512]{1,0:T(8,128)(2,1)S(1)}, u32[]{:S(2)}, u32[]{:S(2)}) collective-permute-start(bf16[128,512]{1,0:T(8,128)(2,1)S(1)} %collective-permute-done.37), channel_id=1, source_target_pairs={{0,8},{8,16},{16,24},{24,28},{28,20},{20,12},{12,4},{4,0},{1,9},{9... | collective-permute-start | bytes 393224 | tf_op jit(solution)/shard_map/ppermute | solution.py:77
  185.5 6.5 %collective-permute-start.60 = (bf16[128,512]{1,0:T(8,128)(2,1)S(1)}, bf16[128,512]{1,0:T(8,128)(2,1)S(1)}, u32[]{:S(2)}, u32[]{:S(2)}) collective-permute-start(bf16[128,512]{1,0:T(8,128)(2,1)S(1)} %collective-permute-done.59), channel_id=1, source_target_pairs={{8,0},{16,8},{24,16},{28,24},{20,28},{12,20},{4,12},{0,4},{9,1},{1... | collective-permute-start | bytes 393224 | tf_op jit(solution)/shard_map/ppermute | solution.py:77
  187.9 5.0 %collective-permute-start.53 = (bf16[128,512]{1,0:T(8,128)(2,1)S(1)}, bf16[128,512]{1,0:T(8,128)(2,1)S(1)}, u32[]{:S(2)}, u32[]{:S(2)}) collective-permute-start(bf16[128,512]{1,0:T(8,128)(2,1)S(1)} %collective-permute-done.52), channel_id=1, source_target_pairs={{8,0},{16,8},{24,16},{28,24},{20,28},{12,20},{4,12},{0,4},{9,1},{1... | collective-permute-start | bytes 393224 | tf_op jit(solution)/shard_map/ppermute | solution.py:77
  188.8 5.6 %collective-permute-start.46 = (bf16[128,512]{1,0:T(8,128)(2,1)S(1)}, bf16[128,512]{1,0:T(8,128)(2,1)S(1)}, u32[]{:S(2)}, u32[]{:S(2)}) collective-permute-start(bf16[128,512]{1,0:T(8,128)(2,1)S(1)} %collective-permute-done.45), channel_id=1, source_target_pairs={{0,8},{8,16},{16,24},{24,28},{28,20},{20,12},{12,4},{4,0},{1,9},{9... | collective-permute-start | bytes 393224 | tf_op jit(solution)/shard_map/ppermute | solution.py:77
  190.7 5.1 %collective-permute-start.39 = (bf16[128,512]{1,0:T(8,128)(2,1)S(1)}, bf16[128,512]{1,0:T(8,128)(2,1)S(1)}, u32[]{:S(2)}, u32[]{:S(2)}) collective-permute-start(bf16[128,512]{1,0:T(8,128)(2,1)S(1)} %collective-permute-done.38), channel_id=1, source_target_pairs={{0,8},{8,16},{16,24},{24,28},{28,20},{20,12},{12,4},{4,0},{1,9},{9... | collective-permute-start | bytes 393224 | tf_op jit(solution)/shard_map/ppermute | solution.py:77
  192.0 5.0 %collective-permute-start.61 = (bf16[128,512]{1,0:T(8,128)(2,1)S(1)}, bf16[128,512]{1,0:T(8,128)(2,1)S(1)}, u32[]{:S(2)}, u32[]{:S(2)}) collective-permute-start(bf16[128,512]{1,0:T(8,128)(2,1)S(1)} %collective-permute-done.60), channel_id=1, source_target_pairs={{8,0},{16,8},{24,16},{28,24},{20,28},{12,20},{4,12},{0,4},{9,1},{1... | collective-permute-start | bytes 393224 | tf_op jit(solution)/shard_map/ppermute | solution.py:77
  192.9 5.5 %collective-permute-start.54 = (bf16[128,512]{1,0:T(8,128)(2,1)S(1)}, bf16[128,512]{1,0:T(8,128)(2,1)S(1)}, u32[]{:S(2)}, u32[]{:S(2)}) collective-permute-start(bf16[128,512]{1,0:T(8,128)(2,1)S(1)} %collective-permute-done.53), channel_id=1, source_target_pairs={{8,0},{16,8},{24,16},{28,24},{20,28},{12,20},{4,12},{0,4},{9,1},{1... | collective-permute-start | bytes 393224 | tf_op jit(solution)/shard_map/ppermute | solution.py:77
  194.4 5.0 %collective-permute-start.47 = (bf16[128,512]{1,0:T(8,128)(2,1)S(1)}, bf16[128,512]{1,0:T(8,128)(2,1)S(1)}, u32[]{:S(2)}, u32[]{:S(2)}) collective-permute-start(bf16[128,512]{1,0:T(8,128)(2,1)S(1)} %collective-permute-done.46), channel_id=1, source_target_pairs={{0,8},{8,16},{16,24},{24,28},{28,20},{20,12},{12,4},{4,0},{1,9},{9... | collective-permute-start | bytes 393224 | tf_op jit(solution)/shard_map/ppermute | solution.py:77
  195.8 5.0 %collective-permute-start.40 = (bf16[128,512]{1,0:T(8,128)(2,1)S(1)}, bf16[128,512]{1,0:T(8,128)(2,1)S(1)}, u32[]{:S(2)}, u32[]{:S(2)}) collective-permute-start(bf16[128,512]{1,0:T(8,128)(2,1)S(1)} %collective-permute-done.39), channel_id=1, source_target_pairs={{0,8},{8,16},{16,24},{24,28},{28,20},{20,12},{12,4},{4,0},{1,9},{9... | collective-permute-start | bytes 393224 | tf_op jit(solution)/shard_map/ppermute | solution.py:77
  209.9 8.4 %collective-permute-start.63 = (bf16[256,512]{1,0:T(8,128)(2,1)S(1)}, bf16[256,512]{1,0:T(8,128)(2,1)S(1)}, u32[]{:S(2)}, u32[]{:S(2)}) collective-permute-start(bf16[256,512]{1,0:T(8,128)(2,1)S(1)} %bitcast_convert_fusion), channel_id=1, source_target_pairs={{0,2},{1,3},{2,0},{3,1},{4,6},{5,7},{6,4},{7,5},{8,10},{9,11},{10,... | collective-permute-start | bytes 786440 | tf_op jit(solution)/shard_map/ppermute | solution.py:139
  219.4 13.7 %collective-permute-start.64 = (bf16[128,512]{1,0:T(8,128)(2,1)S(1)}, bf16[128,512]{1,0:T(8,128)(2,1)S(1)}, u32[]{:S(2)}, u32[]{:S(2)}) collective-permute-start(bf16[128,512]{1,0:T(8,128)(2,1)S(1)} %get-tuple-element.95), channel_id=1, source_target_pairs={{0,4},{1,12},{2,20},{3,28},{4,0},{5,8},{6,16},{7,24},{8,5},{9,13},... | collective-permute-start | bytes 393224 | tf_op jit(solution)/shard_map/ppermute | solution.py:44
  220.9 14.2 %collective-permute-start.65 = (bf16[128,512]{1,0:T(8,128)(2,1)S(1)}, bf16[128,512]{1,0:T(8,128)(2,1)S(1)}, u32[]{:S(2)}, u32[]{:S(2)}) collective-permute-start(bf16[128,512]{1,0:T(8,128)(2,1)S(1)} %get-tuple-element.94), channel_id=1, source_target_pairs={{0,0},{1,8},{2,16},{3,24},{4,4},{5,12},{6,20},{7,28},{8,1},{9,9},{... | collective-permute-start | bytes 393224 | tf_op jit(solution)/shard_map/ppermute | solution.py:44
  (24 other events, 186.3 us)

commit v11 on v10

--- a/solution.py
+++ b/solution.py
@@ -111,19 +111,21 @@
     return jnp.where(upper, high, low), jnp.where(upper, low, high)
 
 
-def col_psum(value):
+def col_psum(value, alongside, work):
     core = lax.axis_index("col") % 2 == 1
     keep, give = halves_of(value, 1, core)
     count = lax.axis_size("col")
     got = lax.ppermute(give, "col", [(c, c ^ 1) for c in range(count)])
     pair = keep.astype(jnp.float32) + got.astype(jnp.float32)
-    total = pair + lax.ppermute(
-        pair.astype(jnp.bfloat16), "col", [(c, c ^ 2) for c in range(count)]
-    ).astype(jnp.float32)
+    sent, alongside = lax.optimization_barrier((pair.astype(jnp.bfloat16), alongside))
+    got, done = lax.optimization_barrier(
+        (lax.ppermute(sent, "col", [(c, c ^ 2) for c in range(count)]), work(*alongside))
+    )
+    total = pair + got.astype(jnp.float32)
     other = lax.ppermute(total, "col", [(c, c ^ 1) for c in range(count)])
     return jnp.where(
         core, jnp.concatenate([other, total], axis=1), jnp.concatenate([total, other], axis=1)
-    )
+    ), done
 
 
 def col_psum_scatter(value):
@@ -174,9 +176,6 @@
     gate_value = gate_branch.astype(jnp.float32)
     gate_act = jax.nn.silu(gate_value)
     conv_act = jax.nn.silu(conv_sum)
-    conv_scale, gate_scale = lax.optimization_barrier(
-        (gate_act * silu_grad(conv_sum), conv_act * silu_grad(gate_value))
-    )
     mixed = (conv_act * gate_act).astype(jnp.bfloat16)
     partial_value = jnp.dot(mixed, out_weight, preferred_element_type=jnp.float32)
     columns = tokens.shape[1] // lax.axis_size("col")
@@ -186,9 +185,15 @@
     )
     token_weight = jnp.sum(lang_table * lang_weight[None, :], axis=1)[:, None]
     if moves_tokens and lax.axis_size("col") == 4:
-        out_total = col_psum(partial_value.astype(jnp.bfloat16))
+        out_total, (conv_scale, gate_scale) = col_psum(
+            partial_value.astype(jnp.bfloat16),
+            (gate_value, conv_sum),
+            lambda gate, conv: (jax.nn.silu(gate) * silu_grad(conv), jax.nn.silu(conv) * silu_grad(gate)),
+        )
     else:
         out_total = lax.psum(partial_value.astype(jnp.bfloat16), "col").astype(jnp.float32)
+        conv_scale = gate_act * silu_grad(conv_sum)
+        gate_scale = conv_act * silu_grad(gate_value)
     out_block = lax.dynamic_slice_in_dim(out_total, col_start, columns, 1)
     residual_grad = (token_weight * (out_total - target.astype(jnp.float32))).astype(jnp.bfloat16)
     grad_mixed = lax.dot_general(

time: 236 us -> 235 us (level)
  transfers between devices with their start and end apart: 67 -> 67, of which waited for: 50 -> 49; matrix products, arithmetic and copies ran while one was open for 8% -> 9% of each run, Pallas kernels for 0% -> 0%
where the time goes in v11:
time: 235 us
  waiting for transfers between devices  88.6 us (38%)
  starting transfers between devices  77.6 us (33%)
  matrix products  32 us (14%)
  other arithmetic  17.3 us (7%)
  local copies, waits for them, and re-layouts  16.4 us (7%)
  between operations  2.79 us (1%)
    ppermute x28, starting transfers between devices, ring_gather(): part = lax.ppermute(part, axis, pairs)  31.2 us
    ppermute x28, starting transfers between devices, ring_reduce_scatter(): total = lax.ppermute(total, axis, pairs)  28.9 us
    ppermute x28, waiting for transfers between devices, ring_reduce_scatter(): total = lax.ppermute(total, axis, pairs)  25.7 us
    ppermute x28, waiting for transfers between devices, ring_gather(): part = lax.ppermute(part, axis, pairs)  16.1 us
    dot_general x1, matrix products, shards(): lax.dot_general(residual_grad, out_weight, (((1,), (1,)), ((), ())), pref...  13.4 us
    ppermute x1, waiting for transfers between devices, col_psum(): lax.ppermute(sent, 'col', [(c, c ^ 2) for c in range(count)])  11.3 us
    ppermute x2, waiting for transfers between devices, placed_blocks(): got.append(lax.ppermute(piece, ('row', 'col'), pairs))  8.57 us
    dot_general x1, matrix products, shards(): jnp.dot(mixed, out_weight, preferred_element_type=jnp.float32)  8.43 us
  transfers between devices with their start and end apart: 67, of which 49 were waited for; matrix products, arithmetic and copies ran while one was open for 9% of the time, Pallas kernels for 0%

profile of v11, /device:TPU:2, one launch (start us, length us, event | category | flops | bytes accessed | tf_op | source)
XLA Modules:
  0.0 234.8 jit_solution(10591822786634353830)
XLA Ops:
  0.7 1.6 copy.26
  3.4 5.8 %all-to-all-start = ((bf16[128,8,256]{2,0,1:T(8,128)(2,1)}), bf16[128,8,256]{2,0,1:T(8,128)(2,1)S(1)}, u32[]{:S(2)}, u32[]{:S(2)}) async-start(bf16[128,8,256]{2,0,1:T(8,128)(2,1)} %copy.28), calls=%async_computation | async-start | bytes 1048576 | tf_op jit(solution)/shard_map/all_to_all | solution.py:24
  16.0 7.7 %all-to-all-done = bf16[128,8,256]{2,0,1:T(8,128)(2,1)S(1)} async-done(((bf16[128,8,256]{2,0,1:T(8,128)(2,1)}), bf16[128,8,256]{2,0,1:T(8,128)(2,1)S(1)}, u32[]{:S(2)}, u32[]{:S(2)}) %all-to-all-start) | async-done | bytes 524320 | tf_op jit(solution)/shard_map/all_to_all | solution.py:24
  25.7 1.6 maximum_select_fusion.1
  27.3 1.6 gather_fusion.4
  28.9 4.5 %fusion.105 = (bf16[8,128,1024]{2,1,0:T(8,128)(2,1)S(1)}, f32[8,128,1024]{2,1,0:T(8,128)}) fusion(bf16[512,2048]{1,0:T(8,128)(2,1)S(1)} %copy-done.2, bf16[8,128,512]{2,1,0:T(8,128)(2,1)} %gather_fusion.4, pred[8]{0:T(512)(128)(4,1)S(1)} %get-tuple-element.119), kind=kOutput, calls=%fused_computation.246 | convolution fusion | flops 1075314688 | bytes 8389120 | tf_op jit(solution)/shard_map/dot_general | solution.py:95
  33.5 1.5 collective-permute-start.15
  35.1 1.7 gather_fusion.3
  36.8 2.7 %fusion.106 = (bf16[8,128,1024]{2,1,0:T(8,128)(2,1)S(1)}, f32[8,128,1024]{2,1,0:T(8,128)S(1)}) fusion(bf16[512,2048]{1,0:T(8,128)(2,1)S(1)} %copy-done.2, bf16[8,128,512]{2,1,0:T(8,128)(2,1)} %gather_fusion.3, pred[8]{0:T(512)(128)(4,1)} %compare_and_fusion.2), kind=kOutput, calls=%fused_computation.247 | convolution fusion | flops 1075314688 | bytes 8388616 | tf_op jit(solution)/shard_map/dot_general | solution.py:94
  39.5 2.0 collective-permute-start.1
  43.1 1.5 collective-permute-start.16
  45.9 1.7 collective-permute-done.8
  47.7 1.7 collective-permute-start.2
  50.6 1.5 collective-permute-start.17
  53.5 1.4 collective-permute-done.9
  55.0 1.4 collective-permute-start.3
  57.3 1.5 collective-permute-start.18
  60.0 1.7 collective-permute-done.10
  61.8 1.7 collective-permute-start.4
  64.7 1.3 collective-permute-start.19
  66.8 3.1 %collective-permute-done.11 = bf16[128,512]{1,0:T(8,128)(2,1)S(1)} collective-permute-done((bf16[128,512]{1,0:T(8,128)(2,1)S(1)}, bf16[128,512]{1,0:T(8,128)(2,1)S(1)}, u32[]{:S(2)}, u32[]{:S(2)}) %collective-permute-start.11) | collective-permute-done | bytes 131104 | tf_op jit(solution)/shard_map/ppermute | solution.py:104
  70.0 1.8 collective-permute-start.5
  74.3 1.7 collective-permute-done.5
  76.0 2.8 %collective-permute-done.12 = bf16[128,512]{1,0:T(8,128)(2,1)S(1)} collective-permute-done((bf16[128,512]{1,0:T(8,128)(2,1)S(1)}, bf16[128,512]{1,0:T(8,128)(2,1)S(1)}, u32[]{:S(2)}, u32[]{:S(2)}) %collective-permute-start.12) | collective-permute-done | bytes 131104 | tf_op jit(solution)/shard_map/ppermute | solution.py:104
  78.9 2.1 collective-permute-start.6
  83.2 2.0 collective-permute-done.6
  85.2 2.5 %collective-permute-done.13 = bf16[128,512]{1,0:T(8,128)(2,1)S(1)} collective-permute-done((bf16[128,512]{1,0:T(8,128)(2,1)S(1)}, bf16[128,512]{1,0:T(8,128)(2,1)S(1)}, u32[]{:S(2)}, u32[]{:S(2)}) %collective-permute-start.13) | collective-permute-done | bytes 131104 | tf_op jit(solution)/shard_map/ppermute | solution.py:104
  87.8 1.8 collective-permute-start.7
  90.3 2.6 %collective-permute-done.7 = bf16[128,512]{1,0:T(8,128)(2,1)S(1)} collective-permute-done((bf16[128,512]{1,0:T(8,128)(2,1)S(1)}, bf16[128,512]{1,0:T(8,128)(2,1)S(1)}, u32[]{:S(2)}, u32[]{:S(2)}) %collective-permute-start.7) | collective-permute-done | bytes 131104 | tf_op jit(solution)/shard_map/ppermute | solution.py:104
  92.8 1.8 collective-permute-done.14
  94.7 2.3 collective-permute-start.29
  99.5 8.4 %convolution_convert_fusion = bf16[128,4096]{1,0:T(8,128)(2,1)S(1)} fusion(bf16[2048,4096]{1,0:T(8,128)(2,1)} %param.23, f32[128,2048]{1,0:T(8,128)S(1)} %fusion.2, bf16[128,2048]{1,0:T(8,128)(2,1)S(1)} %copy-done.10), kind=kOutput, calls=%fused_computation.6 | convolution fusion | flops 2150891520 | bytes 19398656 | tf_op jit(solution)/shard_map/dot_general | solution.py:180
  108.2 1.8 collective-permute-done.30
  110.8 2.2 multiply_multiply_fusion.3
  113.0 11.3 %collective-permute-done.31 = bf16[128,2048]{1,0:T(8,128)(2,1)S(1)} collective-permute-done((bf16[128,2048]{1,0:T(8,128)(2,1)S(1)}, bf16[128,2048]{1,0:T(8,128)(2,1)S(1)}, u32[]{:S(2)}, u32[]{:S(2)}) %collective-permute-start.31) | collective-permute-done | bytes 524320 | tf_op jit(solution)/shard_map/ppermute | solution.py:122
  124.8 2.5 %collective-permute-done.32 = f32[128,2048]{1,0:T(8,128)S(1)} collective-permute-done((f32[128,2048]{1,0:T(8,128)S(1)}, f32[128,2048]{1,0:T(8,128)S(1)}, u32[]{:S(2)}, u32[]{:S(2)}) %collective-permute-start.32) | collective-permute-done | bytes 1048608 | tf_op jit(solution)/shard_map/ppermute | solution.py:125
  127.6 13.4 %multiply_multiply_fusion.2 = (f32[128,2048]{1,0:T(8,128)}, f32[128,2048]{1,0:T(8,128)S(1)}, bf16[128,2048]{1,0:T(8,128)(2,1)}) fusion(f32[128]{0:T(128)S(1)} %get-tuple-element.109, f32[2048]{0:T(1024)S(1)} %bitcast.324, f32[128,2048]{1,0:T(8,128)} %get-tuple-element.17, f32[128,2048]{1,0:T(8,128)} %get-tuple-element.19, bf16[2048,4096]{1,0:T(8,128)(2,1)} %param.23, ...), kind=kOutput, calls=%fused_computation.34 | convolution fusion | flops 2150891520 | bytes 24650752 | tf_op jit(solution)/shard_map/dot_general | solution.py:199
  142.6 1.3 collective-permute-start.33
  144.0 1.5 slice.317
  145.9 3.1 %collective-permute-done.33 = f32[3,2048]{1,0:T(4,128)S(1)} collective-permute-done((f32[3,2048]{1,0:T(4,128)S(1)}, f32[3,2048]{1,0:T(4,128)S(1)}, u32[]{:S(2)}, u32[]{:S(2)}) %collective-permute-start.33) | collective-permute-done | bytes 24608 | tf_op jit(solution)/shard_map/ppermute | solution.py:13
  149.4 3.2 %collective-permute-start.55 = (bf16[128,512]{1,0:T(8,128)(2,1)S(1)}, bf16[128,512]{1,0:T(8,128)(2,1)S(1)}, u32[]{:S(2)}, u32[]{:S(2)}) collective-permute-start(bf16[128,512]{1,0:T(8,128)(2,1)S(1)} %get-tuple-element.93), channel_id=1, source_target_pairs={{8,0},{16,8},{24,16},{28,24},{20,28},{12,20},{4,12},{0,4},{9,1},{1... | collective-permute-start | bytes 393224 | tf_op jit(solution)/shard_map/ppermute | solution.py:77
  155.4 2.3 collective-permute-done.55
  157.6 1.5 collective-permute-start.56
  159.1 1.3 collective-permute-done.48
  160.4 1.5 collective-permute-start.49
  162.5 1.8 collective-permute-start.35
  164.8 2.1 collective-permute-done.49
  166.9 1.5 collective-permute-start.50
  168.9 1.8 collective-permute-done.35
  171.5 1.6 collective-permute-start.58
  175.4 1.6 collective-permute-done.36
  177.9 1.5 collective-permute-start.59
  179.9 1.4 collective-permute-start.52
  184.2 1.5 collective-permute-start.60
  186.3 1.4 collective-permute-start.53
  191.5 1.4 collective-permute-start.54
  200.3 1.6 gather_fusion.5
  201.9 1.4 broadcast_select_fusion
  204.1 2.2 collective-permute-done.62
  209.3 7.7 %collective-permute-done.63 = bf16[256,512]{1,0:T(8,128)(2,1)S(1)} collective-permute-done((bf16[256,512]{1,0:T(8,128)(2,1)S(1)}, bf16[256,512]{1,0:T(8,128)(2,1)S(1)}, u32[]{:S(2)}, u32[]{:S(2)}) %collective-permute-start.63) | collective-permute-done | bytes 262176 | tf_op jit(solution)/shard_map/ppermute | solution.py:141
  218.2 1.5 collective-permute-start.64
  219.6 5.1 %collective-permute-start.65 = (bf16[128,512]{1,0:T(8,128)(2,1)S(1)}, bf16[128,512]{1,0:T(8,128)(2,1)S(1)}, u32[]{:S(2)}, u32[]{:S(2)}) collective-permute-start(bf16[128,512]{1,0:T(8,128)(2,1)S(1)} %get-tuple-element.102), channel_id=1, source_target_pairs={{0,0},{1,8},{2,16},{3,24},{4,4},{5,12},{6,20},{7,28},{8,1},{9,9},{... | collective-permute-start | bytes 393224 | tf_op jit(solution)/shard_map/ppermute | solution.py:44
  225.5 6.2 %collective-permute-done.64 = bf16[128,512]{1,0:T(8,128)(2,1)S(1)} collective-permute-done((bf16[128,512]{1,0:T(8,128)(2,1)S(1)}, bf16[128,512]{1,0:T(8,128)(2,1)S(1)}, u32[]{:S(2)}, u32[]{:S(2)}) %collective-permute-start.64) | collective-permute-done | bytes 131104 | tf_op jit(solution)/shard_map/ppermute | solution.py:44
  231.7 2.4 %collective-permute-done.65 = bf16[128,512]{1,0:T(8,128)(2,1)S(1)} collective-permute-done((bf16[128,512]{1,0:T(8,128)(2,1)S(1)}, bf16[128,512]{1,0:T(8,128)(2,1)S(1)}, u32[]{:S(2)}, u32[]{:S(2)}) %collective-permute-start.65) | collective-permute-done | bytes 131104 | tf_op jit(solution)/shard_map/ppermute | solution.py:44
  (221 shorter events, 60.2 us)
Async XLA Ops:
  3.4 20.3 %all-to-all-start = ((bf16[128,8,256]{2,0,1:T(8,128)(2,1)}), bf16[128,8,256]{2,0,1:T(8,128)(2,1)S(1)}, u32[]{:S(2)}, u32[]{:S(2)}) async-start(bf16[128,8,256]{2,0,1:T(8,128)(2,1)} %copy.28), calls=%async_computation | async-start | bytes 1048576 | tf_op jit(solution)/shard_map/all_to_all | solution.py:24
  33.5 8.6 %collective-permute-start.15 = (bf16[128,512]{1,0:T(8,128)(2,1)S(1)}, bf16[128,512]{1,0:T(8,128)(2,1)S(1)}, u32[]{:S(2)}, u32[]{:S(2)}) collective-permute-start(bf16[128,512]{1,0:T(8,128)(2,1)S(1)} %get-tuple-element.87), channel_id=1, source_target_pairs={{8,0},{16,8},{24,16},{28,24},{20,28},{12,20},{4,12},{0,4},{9,1},{1... | collective-permute-start | bytes 393224 | tf_op jit(solution)/shard_map/ppermute | solution.py:104
  35.0 7.1 %collective-permute-start.22 = (bf16[128,512]{1,0:T(8,128)(2,1)S(1)}, bf16[128,512]{1,0:T(8,128)(2,1)}, u32[]{:S(2)}, u32[]{:S(2)}) collective-permute-start(bf16[128,512]{1,0:T(8,128)(2,1)S(1)} %get-tuple-element.88), channel_id=1, source_target_pairs={{8,0},{16,8},{24,16},{28,24},{20,28},{12,20},{4,12},{0,4},{9,1},{1... | collective-permute-start | bytes 393224 | tf_op jit(solution)/shard_map/ppermute | solution.py:104
  39.5 6.4 %collective-permute-start.1 = (bf16[128,512]{1,0:T(8,128)(2,1)S(1)}, bf16[128,512]{1,0:T(8,128)(2,1)S(1)}, u32[]{:S(2)}, u32[]{:S(2)}) collective-permute-start(bf16[128,512]{1,0:T(8,128)(2,1)S(1)} %get-tuple-element.85), channel_id=1, source_target_pairs={{0,8},{8,16},{16,24},{24,28},{28,20},{20,12},{12,4},{4,0},{1,9},{9... | collective-permute-start | bytes 393224 | tf_op jit(solution)/shard_map/ppermute | solution.py:104
  41.5 6.1 %collective-permute-start.8 = (bf16[128,512]{1,0:T(8,128)(2,1)S(1)}, bf16[128,512]{1,0:T(8,128)(2,1)S(1)}, u32[]{:S(2)}, u32[]{:S(2)}) collective-permute-start(bf16[128,512]{1,0:T(8,128)(2,1)S(1)} %get-tuple-element.86), channel_id=1, source_target_pairs={{0,8},{8,16},{16,24},{24,28},{28,20},{20,12},{12,4},{4,0},{1,9},{9... | collective-permute-start | bytes 393224 | tf_op jit(solution)/shard_map/ppermute | solution.py:104
  43.1 6.9 %collective-permute-start.16 = (bf16[128,512]{1,0:T(8,128)(2,1)S(1)}, bf16[128,512]{1,0:T(8,128)(2,1)S(1)}, u32[]{:S(2)}, u32[]{:S(2)}) collective-permute-start(bf16[128,512]{1,0:T(8,128)(2,1)S(1)} %get-tuple-element.81), channel_id=1, source_target_pairs={{8,0},{16,8},{24,16},{28,24},{20,28},{12,20},{4,12},{0,4},{9,1},{1... | collective-permute-start | bytes 393224 | tf_op jit(solution)/shard_map/ppermute | solution.py:104
  44.6 6.0 %collective-permute-start.23 = (bf16[128,512]{1,0:T(8,128)(2,1)S(1)}, bf16[128,512]{1,0:T(8,128)(2,1)S(1)}, u32[]{:S(2)}, u32[]{:S(2)}) collective-permute-start(bf16[128,512]{1,0:T(8,128)(2,1)S(1)} %get-tuple-element.82), channel_id=1, source_target_pairs={{8,0},{16,8},{24,16},{28,24},{20,28},{12,20},{4,12},{0,4},{9,1},{1... | collective-permute-start | bytes 393224 | tf_op jit(solution)/shard_map/ppermute | solution.py:104
  47.7 5.8 %collective-permute-start.2 = (bf16[128,512]{1,0:T(8,128)(2,1)S(1)}, bf16[128,512]{1,0:T(8,128)(2,1)S(1)}, u32[]{:S(2)}, u32[]{:S(2)}) collective-permute-start(bf16[128,512]{1,0:T(8,128)(2,1)S(1)} %get-tuple-element.67), channel_id=1, source_target_pairs={{0,8},{8,16},{16,24},{24,28},{28,20},{20,12},{12,4},{4,0},{1,9},{9... | collective-permute-start | bytes 393224 | tf_op jit(solution)/shard_map/ppermute | solution.py:104
  49.4 5.5 %collective-permute-start.9 = (bf16[128,512]{1,0:T(8,128)(2,1)S(1)}, bf16[128,512]{1,0:T(8,128)(2,1)S(1)}, u32[]{:S(2)}, u32[]{:S(2)}) collective-permute-start(bf16[128,512]{1,0:T(8,128)(2,1)S(1)} %get-tuple-element.68), channel_id=1, source_target_pairs={{0,8},{8,16},{16,24},{24,28},{28,20},{20,12},{12,4},{4,0},{1,9},{9... | collective-permute-start | bytes 393224 | tf_op jit(solution)/shard_map/ppermute | solution.py:104
  50.6 6.4 %collective-permute-start.17 = (bf16[128,512]{1,0:T(8,128)(2,1)S(1)}, bf16[128,512]{1,0:T(8,128)(2,1)S(1)}, u32[]{:S(2)}, u32[]{:S(2)}) collective-permute-start(bf16[128,512]{1,0:T(8,128)(2,1)S(1)} %get-tuple-element.79), channel_id=1, source_target_pairs={{8,0},{16,8},{24,16},{28,24},{20,28},{12,20},{4,12},{0,4},{9,1},{1... | collective-permute-start | bytes 393224 | tf_op jit(solution)/shard_map/ppermute | solution.py:104
  52.1 5.0 %collective-permute-start.24 = (bf16[128,512]{1,0:T(8,128)(2,1)S(1)}, bf16[128,512]{1,0:T(8,128)(2,1)S(1)}, u32[]{:S(2)}, u32[]{:S(2)}) collective-permute-start(bf16[128,512]{1,0:T(8,128)(2,1)S(1)} %get-tuple-element.80), channel_id=1, source_target_pairs={{8,0},{16,8},{24,16},{28,24},{20,28},{12,20},{4,12},{0,4},{9,1},{1... | collective-permute-start | bytes 393224 | tf_op jit(solution)/shard_map/ppermute | solution.py:104
  55.0 5.0 %collective-permute-start.3 = (bf16[128,512]{1,0:T(8,128)(2,1)S(1)}, bf16[128,512]{1,0:T(8,128)(2,1)S(1)}, u32[]{:S(2)}, u32[]{:S(2)}) collective-permute-start(bf16[128,512]{1,0:T(8,128)(2,1)S(1)} %get-tuple-element.65), channel_id=1, source_target_pairs={{0,8},{8,16},{16,24},{24,28},{28,20},{20,12},{12,4},{4,0},{1,9},{9... | collective-permute-start | bytes 393224 | tf_op jit(solution)/shard_map/ppermute | solution.py:104
  56.4 5.3 %collective-permute-start.10 = (bf16[128,512]{1,0:T(8,128)(2,1)S(1)}, bf16[128,512]{1,0:T(8,128)(2,1)S(1)}, u32[]{:S(2)}, u32[]{:S(2)}) collective-permute-start(bf16[128,512]{1,0:T(8,128)(2,1)S(1)} %get-tuple-element.66), channel_id=1, source_target_pairs={{0,8},{8,16},{16,24},{24,28},{28,20},{20,12},{12,4},{4,0},{1,9},{9... | collective-permute-start | bytes 393224 | tf_op jit(solution)/shard_map/ppermute | solution.py:104
  57.3 6.9 %collective-permute-start.18 = (bf16[128,512]{1,0:T(8,128)(2,1)S(1)}, bf16[128,512]{1,0:T(8,128)(2,1)S(1)}, u32[]{:S(2)}, u32[]{:S(2)}) collective-permute-start(bf16[128,512]{1,0:T(8,128)(2,1)S(1)} %get-tuple-element.77), channel_id=1, source_target_pairs={{8,0},{16,8},{24,16},{28,24},{20,28},{12,20},{4,12},{0,4},{9,1},{1... | collective-permute-start | bytes 393224 | tf_op jit(solution)/shard_map/ppermute | solution.py:104
  58.8 5.8 %collective-permute-start.25 = (bf16[128,512]{1,0:T(8,128)(2,1)S(1)}, bf16[128,512]{1,0:T(8,128)(2,1)S(1)}, u32[]{:S(2)}, u32[]{:S(2)}) collective-permute-start(bf16[128,512]{1,0:T(8,128)(2,1)S(1)} %get-tuple-element.78), channel_id=1, source_target_pairs={{8,0},{16,8},{24,16},{28,24},{20,28},{12,20},{4,12},{0,4},{9,1},{1... | collective-permute-start | bytes 393224 | tf_op jit(solution)/shard_map/ppermute | solution.py:104
  61.8 5.0 %collective-permute-start.4 = (bf16[128,512]{1,0:T(8,128)(2,1)S(1)}, bf16[128,512]{1,0:T(8,128)(2,1)S(1)}, u32[]{:S(2)}, u32[]{:S(2)}) collective-permute-start(bf16[128,512]{1,0:T(8,128)(2,1)S(1)} %get-tuple-element.63), channel_id=1, source_target_pairs={{0,8},{8,16},{16,24},{24,28},{28,20},{20,12},{12,4},{4,0},{1,9},{9... | collective-permute-start | bytes 393224 | tf_op jit(solution)/shard_map/ppermute | solution.py:104
  63.6 6.4 %collective-permute-start.11 = (bf16[128,512]{1,0:T(8,128)(2,1)S(1)}, bf16[128,512]{1,0:T(8,128)(2,1)S(1)}, u32[]{:S(2)}, u32[]{:S(2)}) collective-permute-start(bf16[128,512]{1,0:T(8,128)(2,1)S(1)} %get-tuple-element.64), channel_id=1, source_target_pairs={{0,8},{8,16},{16,24},{24,28},{28,20},{20,12},{12,4},{4,0},{1,9},{9... | collective-permute-start | bytes 393224 | tf_op jit(solution)/shard_map/ppermute | solution.py:104
  64.7 7.7 %collective-permute-start.19 = (bf16[128,512]{1,0:T(8,128)(2,1)S(1)}, bf16[128,512]{1,0:T(8,128)(2,1)S(1)}, u32[]{:S(2)}, u32[]{:S(2)}) collective-permute-start(bf16[128,512]{1,0:T(8,128)(2,1)S(1)} %get-tuple-element.75), channel_id=1, source_target_pairs={{8,0},{16,8},{24,16},{28,24},{20,28},{12,20},{4,12},{0,4},{9,1},{1... | collective-permute-start | bytes 393224 | tf_op jit(solution)/shard_map/ppermute | solution.py:104
  66.0 6.8 %collective-permute-start.26 = (bf16[128,512]{1,0:T(8,128)(2,1)S(1)}, bf16[128,512]{1,0:T(8,128)(2,1)S(1)}, u32[]{:S(2)}, u32[]{:S(2)}) collective-permute-start(bf16[128,512]{1,0:T(8,128)(2,1)S(1)} %get-tuple-element.76), channel_id=1, source_target_pairs={{8,0},{16,8},{24,16},{28,24},{20,28},{12,20},{4,12},{0,4},{9,1},{1... | collective-permute-start | bytes 393224 | tf_op jit(solution)/shard_map/ppermute | solution.py:104
  70.0 6.0 %collective-permute-start.5 = (bf16[128,512]{1,0:T(8,128)(2,1)S(1)}, bf16[128,512]{1,0:T(8,128)(2,1)S(1)}, u32[]{:S(2)}, u32[]{:S(2)}) collective-permute-start(bf16[128,512]{1,0:T(8,128)(2,1)S(1)} %get-tuple-element.61), channel_id=1, source_target_pairs={{0,8},{8,16},{16,24},{24,28},{28,20},{20,12},{12,4},{4,0},{1,9},{9... | collective-permute-start | bytes 393224 | tf_op jit(solution)/shard_map/ppermute | solution.py:104
  71.8 6.9 %collective-permute-start.12 = (bf16[128,512]{1,0:T(8,128)(2,1)S(1)}, bf16[128,512]{1,0:T(8,128)(2,1)S(1)}, u32[]{:S(2)}, u32[]{:S(2)}) collective-permute-start(bf16[128,512]{1,0:T(8,128)(2,1)S(1)} %get-tuple-element.62), channel_id=1, source_target_pairs={{0,8},{8,16},{16,24},{24,28},{28,20},{20,12},{12,4},{4,0},{1,9},{9... | collective-permute-start | bytes 393224 | tf_op jit(solution)/shard_map/ppermute | solution.py:104
  72.9 8.6 %collective-permute-start.20 = (bf16[128,512]{1,0:T(8,128)(2,1)S(1)}, bf16[128,512]{1,0:T(8,128)(2,1)S(1)}, u32[]{:S(2)}, u32[]{:S(2)}) collective-permute-start(bf16[128,512]{1,0:T(8,128)(2,1)S(1)} %get-tuple-element.73), channel_id=1, source_target_pairs={{8,0},{16,8},{24,16},{28,24},{20,28},{12,20},{4,12},{0,4},{9,1},{1... | collective-permute-start | bytes 393224 | tf_op jit(solution)/shard_map/ppermute | solution.py:104
  74.0 7.9 %collective-permute-start.27 = (bf16[128,512]{1,0:T(8,128)(2,1)S(1)}, bf16[128,512]{1,0:T(8,128)(2,1)S(1)}, u32[]{:S(2)}, u32[]{:S(2)}) collective-permute-start(bf16[128,512]{1,0:T(8,128)(2,1)S(1)} %get-tuple-element.74), channel_id=1, source_target_pairs={{8,0},{16,8},{24,16},{28,24},{20,28},{12,20},{4,12},{0,4},{9,1},{1... | collective-permute-start | bytes 393224 | tf_op jit(solution)/shard_map/ppermute | solution.py:104
  78.9 6.3 %collective-permute-start.6 = (bf16[128,512]{1,0:T(8,128)(2,1)S(1)}, bf16[128,512]{1,0:T(8,128)(2,1)S(1)}, u32[]{:S(2)}, u32[]{:S(2)}) collective-permute-start(bf16[128,512]{1,0:T(8,128)(2,1)S(1)} %get-tuple-element.59), channel_id=1, source_target_pairs={{0,8},{8,16},{16,24},{24,28},{28,20},{20,12},{12,4},{4,0},{1,9},{9... | collective-permute-start | bytes 393224 | tf_op jit(solution)/shard_map/ppermute | solution.py:104
  80.9 6.8 %collective-permute-start.13 = (bf16[128,512]{1,0:T(8,128)(2,1)S(1)}, bf16[128,512]{1,0:T(8,128)(2,1)S(1)}, u32[]{:S(2)}, u32[]{:S(2)}) collective-permute-start(bf16[128,512]{1,0:T(8,128)(2,1)S(1)} %get-tuple-element.60), channel_id=1, source_target_pairs={{0,8},{8,16},{16,24},{24,28},{28,20},{20,12},{12,4},{4,0},{1,9},{9... | collective-permute-start | bytes 393224 | tf_op jit(solution)/shard_map/ppermute | solution.py:104
  82.0 8.2 %collective-permute-start.21 = (bf16[128,512]{1,0:T(8,128)(2,1)S(1)}, bf16[128,512]{1,0:T(8,128)(2,1)S(1)}, u32[]{:S(2)}, u32[]{:S(2)}) collective-permute-start(bf16[128,512]{1,0:T(8,128)(2,1)S(1)} %get-tuple-element.71), channel_id=1, source_target_pairs={{8,0},{16,8},{24,16},{28,24},{20,28},{12,20},{4,12},{0,4},{9,1},{1... | collective-permute-start | bytes 393224 | tf_op jit(solution)/shard_map/ppermute | solution.py:104
  83.1 7.0 %collective-permute-start.28 = (bf16[128,512]{1,0:T(8,128)(2,1)S(1)}, bf16[128,512]{1,0:T(8,128)(2,1)S(1)}, u32[]{:S(2)}, u32[]{:S(2)}) collective-permute-start(bf16[128,512]{1,0:T(8,128)(2,1)S(1)} %get-tuple-element.72), channel_id=1, source_target_pairs={{8,0},{16,8},{24,16},{28,24},{20,28},{12,20},{4,12},{0,4},{9,1},{1... | collective-permute-start | bytes 393224 | tf_op jit(solution)/shard_map/ppermute | solution.py:104
  87.8 5.0 %collective-permute-start.7 = (bf16[128,512]{1,0:T(8,128)(2,1)S(1)}, bf16[128,512]{1,0:T(8,128)(2,1)S(1)}, u32[]{:S(2)}, u32[]{:S(2)}) collective-permute-start(bf16[128,512]{1,0:T(8,128)(2,1)S(1)} %get-tuple-element.57), channel_id=1, source_target_pairs={{0,8},{8,16},{16,24},{24,28},{28,20},{20,12},{12,4},{4,0},{1,9},{9... | collective-permute-start | bytes 393224 | tf_op jit(solution)/shard_map/ppermute | solution.py:104
  89.6 5.0 %collective-permute-start.14 = (bf16[128,512]{1,0:T(8,128)(2,1)S(1)}, bf16[128,512]{1,0:T(8,128)(2,1)S(1)}, u32[]{:S(2)}, u32[]{:S(2)}) collective-permute-start(bf16[128,512]{1,0:T(8,128)(2,1)S(1)} %get-tuple-element.58), channel_id=1, source_target_pairs={{0,8},{8,16},{16,24},{24,28},{28,20},{20,12},{12,4},{4,0},{1,9},{9... | collective-permute-start | bytes 393224 | tf_op jit(solution)/shard_map/ppermute | solution.py:104
  94.7 3.6 %collective-permute-start.29 = (bf16[3,2048]{1,0:T(4,128)(2,1)S(1)}, bf16[3,2048]{1,0:T(4,128)(2,1)S(1)}, u32[]{:S(2)}, u32[]{:S(2)}) collective-permute-start(bf16[3,2048]{1,0:T(4,128)(2,1)S(1)} %pad_maximum_fusion.1), channel_id=1, source_target_pairs={{0,4},{4,8},{8,12},{12,16},{16,20},{20,24},{24,28},{1,5},{5,9},{9,... | collective-permute-start | bytes 36872 | tf_op jit(solution)/shard_map/ppermute | solution.py:13
  110.2 14.0 %collective-permute-start.31 = (bf16[128,2048]{1,0:T(8,128)(2,1)S(1)}, bf16[128,2048]{1,0:T(8,128)(2,1)S(1)}, u32[]{:S(2)}, u32[]{:S(2)}) collective-permute-start(bf16[128,2048]{1,0:T(8,128)(2,1)S(1)} %fusion.19), channel_id=1, source_target_pairs={{0,2},{1,3},{2,0},{3,1},{4,6},{5,7},{6,4},{7,5},{8,10},{9,11},{10,... | collective-permute-start | bytes 1572872 | tf_op jit(solution)/shard_map/ppermute | solution.py:122
  124.6 2.7 %collective-permute-start.32 = (f32[128,2048]{1,0:T(8,128)S(1)}, f32[128,2048]{1,0:T(8,128)S(1)}, u32[]{:S(2)}, u32[]{:S(2)}) collective-permute-start(f32[128,2048]{1,0:T(8,128)S(1)} %convert_add_fusion.1), channel_id=1, source_target_pairs={{0,1},{1,0},{2,3},{3,2},{4,5},{5,4},{6,7},{7,6},{8,9},{9,8},{10,11... | collective-permute-start | bytes 3145736 | tf_op jit(solution)/shard_map/ppermute | solution.py:125
  142.6 6.4 %collective-permute-start.33 = (f32[3,2048]{1,0:T(4,128)S(1)}, f32[3,2048]{1,0:T(4,128)S(1)}, u32[]{:S(2)}, u32[]{:S(2)}) collective-permute-start(f32[3,2048]{1,0:T(4,128)S(1)} %slice_add_fusion), channel_id=1, source_target_pairs={{4,0},{8,4},{12,8},{16,12},{20,16},{24,20},{28,24},{5,1},{9,5},{13... | collective-permute-start | bytes 73736 | tf_op jit(solution)/shard_map/ppermute | solution.py:13
  149.4 8.2 %collective-permute-start.55 = (bf16[128,512]{1,0:T(8,128)(2,1)S(1)}, bf16[128,512]{1,0:T(8,128)(2,1)S(1)}, u32[]{:S(2)}, u32[]{:S(2)}) collective-permute-start(bf16[128,512]{1,0:T(8,128)(2,1)S(1)} %get-tuple-element.93), channel_id=1, source_target_pairs={{8,0},{16,8},{24,16},{28,24},{20,28},{12,20},{4,12},{0,4},{9,1},{1... | collective-permute-start | bytes 393224 | tf_op jit(solution)/shard_map/ppermute | solution.py:77
  152.7 7.8 %collective-permute-start.48 = (bf16[128,512]{1,0:T(8,128)(2,1)S(1)}, bf16[128,512]{1,0:T(8,128)(2,1)S(1)}, u32[]{:S(2)}, u32[]{:S(2)}) collective-permute-start(bf16[128,512]{1,0:T(8,128)(2,1)S(1)} %get-tuple-element.94), channel_id=1, source_target_pairs={{8,0},{16,8},{24,16},{28,24},{20,28},{12,20},{4,12},{0,4},{9,1},{1... | collective-permute-start | bytes 393224 | tf_op jit(solution)/shard_map/ppermute | solution.py:77
  153.5 8.5 %collective-permute-start.41 = (bf16[128,512]{1,0:T(8,128)(2,1)S(1)}, bf16[128,512]{1,0:T(8,128)(2,1)S(1)}, u32[]{:S(2)}, u32[]{:S(2)}) collective-permute-start(bf16[128,512]{1,0:T(8,128)(2,1)S(1)} %get-tuple-element.95), channel_id=1, source_target_pairs={{0,8},{8,16},{16,24},{24,28},{28,20},{20,12},{12,4},{4,0},{1,9},{9... | collective-permute-start | bytes 393224 | tf_op jit(solution)/shard_map/ppermute | solution.py:77
  154.7 7.8 %collective-permute-start.34 = (bf16[128,512]{1,0:T(8,128)(2,1)S(1)}, bf16[128,512]{1,0:T(8,128)(2,1)S(1)}, u32[]{:S(2)}, u32[]{:S(2)}) collective-permute-start(bf16[128,512]{1,0:T(8,128)(2,1)S(1)} %get-tuple-element.92), channel_id=1, source_target_pairs={{0,8},{8,16},{16,24},{24,28},{28,20},{20,12},{12,4},{4,0},{1,9},{9... | collective-permute-start | bytes 393224 | tf_op jit(solution)/shard_map/ppermute | solution.py:77
  157.6 6.6 %collective-permute-start.56 = (bf16[128,512]{1,0:T(8,128)(2,1)S(1)}, bf16[128,512]{1,0:T(8,128)(2,1)S(1)}, u32[]{:S(2)}, u32[]{:S(2)}) collective-permute-start(bf16[128,512]{1,0:T(8,128)(2,1)S(1)} %collective-permute-done.55), channel_id=1, source_target_pairs={{8,0},{16,8},{24,16},{28,24},{20,28},{12,20},{4,12},{0,4},{9,1},{1... | collective-permute-start | bytes 393224 | tf_op jit(solution)/shard_map/ppermute | solution.py:77
  160.4 6.4 %collective-permute-start.49 = (bf16[128,512]{1,0:T(8,128)(2,1)S(1)}, bf16[128,512]{1,0:T(8,128)(2,1)S(1)}, u32[]{:S(2)}, u32[]{:S(2)}) collective-permute-start(bf16[128,512]{1,0:T(8,128)(2,1)S(1)} %collective-permute-done.48), channel_id=1, source_target_pairs={{8,0},{16,8},{24,16},{28,24},{20,28},{12,20},{4,12},{0,4},{9,1},{1... | collective-permute-start | bytes 393224 | tf_op jit(solution)/shard_map/ppermute | solution.py:77
  161.9 6.4 %collective-permute-start.42 = (bf16[128,512]{1,0:T(8,128)(2,1)S(1)}, bf16[128,512]{1,0:T(8,128)(2,1)S(1)}, u32[]{:S(2)}, u32[]{:S(2)}) collective-permute-start(bf16[128,512]{1,0:T(8,128)(2,1)S(1)} %collective-permute-done.41), channel_id=1, source_target_pairs={{0,8},{8,16},{16,24},{24,28},{28,20},{20,12},{12,4},{4,0},{1,9},{9... | collective-permute-start | bytes 393224 | tf_op jit(solution)/shard_map/ppermute | solution.py:77
  162.5 8.3 %collective-permute-start.35 = (bf16[128,512]{1,0:T(8,128)(2,1)S(1)}, bf16[128,512]{1,0:T(8,128)(2,1)S(1)}, u32[]{:S(2)}, u32[]{:S(2)}) collective-permute-start(bf16[128,512]{1,0:T(8,128)(2,1)S(1)} %collective-permute-done.34), channel_id=1, source_target_pairs={{0,8},{8,16},{16,24},{24,28},{28,20},{20,12},{12,4},{4,0},{1,9},{9... | collective-permute-start | bytes 393224 | tf_op jit(solution)/shard_map/ppermute | solution.py:77
  164.3 7.2 %collective-permute-start.57 = (bf16[128,512]{1,0:T(8,128)(2,1)S(1)}, bf16[128,512]{1,0:T(8,128)(2,1)S(1)}, u32[]{:S(2)}, u32[]{:S(2)}) collective-permute-start(bf16[128,512]{1,0:T(8,128)(2,1)S(1)} %collective-permute-done.56), channel_id=1, source_target_pairs={{8,0},{16,8},{24,16},{28,24},{20,28},{12,20},{4,12},{0,4},{9,1},{1... | collective-permute-start | bytes 393224 | tf_op jit(solution)/shard_map/ppermute | solution.py:77
  166.9 6.5 %collective-permute-start.50 = (bf16[128,512]{1,0:T(8,128)(2,1)S(1)}, bf16[128,512]{1,0:T(8,128)(2,1)S(1)}, u32[]{:S(2)}, u32[]{:S(2)}) collective-permute-start(bf16[128,512]{1,0:T(8,128)(2,1)S(1)} %collective-permute-done.49), channel_id=1, source_target_pairs={{8,0},{16,8},{24,16},{28,24},{20,28},{12,20},{4,12},{0,4},{9,1},{1... | collective-permute-start | bytes 393224 | tf_op jit(solution)/shard_map/ppermute | solution.py:77
  168.4 6.1 %collective-permute-start.43 = (bf16[128,512]{1,0:T(8,128)(2,1)S(1)}, bf16[128,512]{1,0:T(8,128)(2,1)S(1)}, u32[]{:S(2)}, u32[]{:S(2)}) collective-permute-start(bf16[128,512]{1,0:T(8,128)(2,1)S(1)} %collective-permute-done.42), channel_id=1, source_target_pairs={{0,8},{8,16},{16,24},{24,28},{28,20},{20,12},{12,4},{4,0},{1,9},{9... | collective-permute-start | bytes 393224 | tf_op jit(solution)/shard_map/ppermute | solution.py:77
  170.8 6.3 %collective-permute-start.36 = (bf16[128,512]{1,0:T(8,128)(2,1)S(1)}, bf16[128,512]{1,0:T(8,128)(2,1)S(1)}, u32[]{:S(2)}, u32[]{:S(2)}) collective-permute-start(bf16[128,512]{1,0:T(8,128)(2,1)S(1)} %collective-permute-done.35), channel_id=1, source_target_pairs={{0,8},{8,16},{16,24},{24,28},{28,20},{20,12},{12,4},{4,0},{1,9},{9... | collective-permute-start | bytes 393224 | tf_op jit(solution)/shard_map/ppermute | solution.py:77
  171.5 6.4 %collective-permute-start.58 = (bf16[128,512]{1,0:T(8,128)(2,1)S(1)}, bf16[128,512]{1,0:T(8,128)(2,1)S(1)}, u32[]{:S(2)}, u32[]{:S(2)}) collective-permute-start(bf16[128,512]{1,0:T(8,128)(2,1)S(1)} %collective-permute-done.57), channel_id=1, source_target_pairs={{8,0},{16,8},{24,16},{28,24},{20,28},{12,20},{4,12},{0,4},{9,1},{1... | collective-permute-start | bytes 393224 | tf_op jit(solution)/shard_map/ppermute | solution.py:77
  173.4 6.5 %collective-permute-start.51 = (bf16[128,512]{1,0:T(8,128)(2,1)S(1)}, bf16[128,512]{1,0:T(8,128)(2,1)S(1)}, u32[]{:S(2)}, u32[]{:S(2)}) collective-permute-start(bf16[128,512]{1,0:T(8,128)(2,1)S(1)} %collective-permute-done.50), channel_id=1, source_target_pairs={{8,0},{16,8},{24,16},{28,24},{20,28},{12,20},{4,12},{0,4},{9,1},{1... | collective-permute-start | bytes 393224 | tf_op jit(solution)/shard_map/ppermute | solution.py:77
  174.4 6.8 %collective-permute-start.44 = (bf16[128,512]{1,0:T(8,128)(2,1)S(1)}, bf16[128,512]{1,0:T(8,128)(2,1)S(1)}, u32[]{:S(2)}, u32[]{:S(2)}) collective-permute-start(bf16[128,512]{1,0:T(8,128)(2,1)S(1)} %collective-permute-done.43), channel_id=1, source_target_pairs={{0,8},{8,16},{16,24},{24,28},{28,20},{20,12},{12,4},{4,0},{1,9},{9... | collective-permute-start | bytes 393224 | tf_op jit(solution)/shard_map/ppermute | solution.py:77
  177.1 5.5 %collective-permute-start.37 = (bf16[128,512]{1,0:T(8,128)(2,1)S(1)}, bf16[128,512]{1,0:T(8,128)(2,1)S(1)}, u32[]{:S(2)}, u32[]{:S(2)}) collective-permute-start(bf16[128,512]{1,0:T(8,128)(2,1)S(1)} %collective-permute-done.36), channel_id=1, source_target_pairs={{0,8},{8,16},{16,24},{24,28},{28,20},{20,12},{12,4},{4,0},{1,9},{9... | collective-permute-start | bytes 393224 | tf_op jit(solution)/shard_map/ppermute | solution.py:77
  177.9 6.3 %collective-permute-start.59 = (bf16[128,512]{1,0:T(8,128)(2,1)S(1)}, bf16[128,512]{1,0:T(8,128)(2,1)S(1)}, u32[]{:S(2)}, u32[]{:S(2)}) collective-permute-start(bf16[128,512]{1,0:T(8,128)(2,1)S(1)} %collective-permute-done.58), channel_id=1, source_target_pairs={{8,0},{16,8},{24,16},{28,24},{20,28},{12,20},{4,12},{0,4},{9,1},{1... | collective-permute-start | bytes 393224 | tf_op jit(solution)/shard_map/ppermute | solution.py:77
  179.9 6.4 %collective-permute-start.52 = (bf16[128,512]{1,0:T(8,128)(2,1)S(1)}, bf16[128,512]{1,0:T(8,128)(2,1)S(1)}, u32[]{:S(2)}, u32[]{:S(2)}) collective-permute-start(bf16[128,512]{1,0:T(8,128)(2,1)S(1)} %collective-permute-done.51), channel_id=1, source_target_pairs={{8,0},{16,8},{24,16},{28,24},{20,28},{12,20},{4,12},{0,4},{9,1},{1... | collective-permute-start | bytes 393224 | tf_op jit(solution)/shard_map/ppermute | solution.py:77
  181.3 6.5 %collective-permute-start.45 = (bf16[128,512]{1,0:T(8,128)(2,1)S(1)}, bf16[128,512]{1,0:T(8,128)(2,1)S(1)}, u32[]{:S(2)}, u32[]{:S(2)}) collective-permute-start(bf16[128,512]{1,0:T(8,128)(2,1)S(1)} %collective-permute-done.44), channel_id=1, source_target_pairs={{0,8},{8,16},{16,24},{24,28},{28,20},{20,12},{12,4},{4,0},{1,9},{9... | collective-permute-start | bytes 393224 | tf_op jit(solution)/shard_map/ppermute | solution.py:77
  182.6 6.8 %collective-permute-start.38 = (bf16[128,512]{1,0:T(8,128)(2,1)S(1)}, bf16[128,512]{1,0:T(8,128)(2,1)S(1)}, u32[]{:S(2)}, u32[]{:S(2)}) collective-permute-start(bf16[128,512]{1,0:T(8,128)(2,1)S(1)} %collective-permute-done.37), channel_id=1, source_target_pairs={{0,8},{8,16},{16,24},{24,28},{28,20},{20,12},{12,4},{4,0},{1,9},{9... | collective-permute-start | bytes 393224 | tf_op jit(solution)/shard_map/ppermute | solution.py:77
  184.2 6.2 %collective-permute-start.60 = (bf16[128,512]{1,0:T(8,128)(2,1)S(1)}, bf16[128,512]{1,0:T(8,128)(2,1)S(1)}, u32[]{:S(2)}, u32[]{:S(2)}) collective-permute-start(bf16[128,512]{1,0:T(8,128)(2,1)S(1)} %collective-permute-done.59), channel_id=1, source_target_pairs={{8,0},{16,8},{24,16},{28,24},{20,28},{12,20},{4,12},{0,4},{9,1},{1... | collective-permute-start | bytes 393224 | tf_op jit(solution)/shard_map/ppermute | solution.py:77
  186.3 5.2 %collective-permute-start.53 = (bf16[128,512]{1,0:T(8,128)(2,1)S(1)}, bf16[128,512]{1,0:T(8,128)(2,1)S(1)}, u32[]{:S(2)}, u32[]{:S(2)}) collective-permute-start(bf16[128,512]{1,0:T(8,128)(2,1)S(1)} %collective-permute-done.52), channel_id=1, source_target_pairs={{8,0},{16,8},{24,16},{28,24},{20,28},{12,20},{4,12},{0,4},{9,1},{1... | collective-permute-start | bytes 393224 | tf_op jit(solution)/shard_map/ppermute | solution.py:77
  187.7 5.4 %collective-permute-start.46 = (bf16[128,512]{1,0:T(8,128)(2,1)S(1)}, bf16[128,512]{1,0:T(8,128)(2,1)S(1)}, u32[]{:S(2)}, u32[]{:S(2)}) collective-permute-start(bf16[128,512]{1,0:T(8,128)(2,1)S(1)} %collective-permute-done.45), channel_id=1, source_target_pairs={{0,8},{8,16},{16,24},{24,28},{28,20},{20,12},{12,4},{4,0},{1,9},{9... | collective-permute-start | bytes 393224 | tf_op jit(solution)/shard_map/ppermute | solution.py:77
  189.4 5.2 %collective-permute-start.39 = (bf16[128,512]{1,0:T(8,128)(2,1)S(1)}, bf16[128,512]{1,0:T(8,128)(2,1)S(1)}, u32[]{:S(2)}, u32[]{:S(2)}) collective-permute-start(bf16[128,512]{1,0:T(8,128)(2,1)S(1)} %collective-permute-done.38), channel_id=1, source_target_pairs={{0,8},{8,16},{16,24},{24,28},{28,20},{20,12},{12,4},{4,0},{1,9},{9... | collective-permute-start | bytes 393224 | tf_op jit(solution)/shard_map/ppermute | solution.py:77
  190.5 5.0 %collective-permute-start.61 = (bf16[128,512]{1,0:T(8,128)(2,1)S(1)}, bf16[128,512]{1,0:T(8,128)(2,1)S(1)}, u32[]{:S(2)}, u32[]{:S(2)}) collective-permute-start(bf16[128,512]{1,0:T(8,128)(2,1)S(1)} %collective-permute-done.60), channel_id=1, source_target_pairs={{8,0},{16,8},{24,16},{28,24},{20,28},{12,20},{4,12},{0,4},{9,1},{1... | collective-permute-start | bytes 393224 | tf_op jit(solution)/shard_map/ppermute | solution.py:77
  191.5 5.4 %collective-permute-start.54 = (bf16[128,512]{1,0:T(8,128)(2,1)S(1)}, bf16[128,512]{1,0:T(8,128)(2,1)S(1)}, u32[]{:S(2)}, u32[]{:S(2)}) collective-permute-start(bf16[128,512]{1,0:T(8,128)(2,1)S(1)} %collective-permute-done.53), channel_id=1, source_target_pairs={{8,0},{16,8},{24,16},{28,24},{20,28},{12,20},{4,12},{0,4},{9,1},{1... | collective-permute-start | bytes 393224 | tf_op jit(solution)/shard_map/ppermute | solution.py:77
  193.1 5.0 %collective-permute-start.47 = (bf16[128,512]{1,0:T(8,128)(2,1)S(1)}, bf16[128,512]{1,0:T(8,128)(2,1)S(1)}, u32[]{:S(2)}, u32[]{:S(2)}) collective-permute-start(bf16[128,512]{1,0:T(8,128)(2,1)S(1)} %collective-permute-done.46), channel_id=1, source_target_pairs={{0,8},{8,16},{16,24},{24,28},{28,20},{20,12},{12,4},{4,0},{1,9},{9... | collective-permute-start | bytes 393224 | tf_op jit(solution)/shard_map/ppermute | solution.py:77
  194.5 5.0 %collective-permute-start.40 = (bf16[128,512]{1,0:T(8,128)(2,1)S(1)}, bf16[128,512]{1,0:T(8,128)(2,1)S(1)}, u32[]{:S(2)}, u32[]{:S(2)}) collective-permute-start(bf16[128,512]{1,0:T(8,128)(2,1)S(1)} %collective-permute-done.39), channel_id=1, source_target_pairs={{0,8},{8,16},{16,24},{24,28},{28,20},{20,12},{12,4},{4,0},{1,9},{9... | collective-permute-start | bytes 393224 | tf_op jit(solution)/shard_map/ppermute | solution.py:77
  208.6 8.4 %collective-permute-start.63 = (bf16[256,512]{1,0:T(8,128)(2,1)S(1)}, bf16[256,512]{1,0:T(8,128)(2,1)S(1)}, u32[]{:S(2)}, u32[]{:S(2)}) collective-permute-start(bf16[256,512]{1,0:T(8,128)(2,1)S(1)} %bitcast_convert_fusion), channel_id=1, source_target_pairs={{0,2},{1,3},{2,0},{3,1},{4,6},{5,7},{6,4},{7,5},{8,10},{9,11},{10,... | collective-permute-start | bytes 786440 | tf_op jit(solution)/shard_map/ppermute | solution.py:141
  218.2 13.5 %collective-permute-start.64 = (bf16[128,512]{1,0:T(8,128)(2,1)S(1)}, bf16[128,512]{1,0:T(8,128)(2,1)S(1)}, u32[]{:S(2)}, u32[]{:S(2)}) collective-permute-start(bf16[128,512]{1,0:T(8,128)(2,1)S(1)} %get-tuple-element.103), channel_id=1, source_target_pairs={{0,4},{1,12},{2,20},{3,28},{4,0},{5,8},{6,16},{7,24},{8,5},{9,13},... | collective-permute-start | bytes 393224 | tf_op jit(solution)/shard_map/ppermute | solution.py:44
  219.6 14.4 %collective-permute-start.65 = (bf16[128,512]{1,0:T(8,128)(2,1)S(1)}, bf16[128,512]{1,0:T(8,128)(2,1)S(1)}, u32[]{:S(2)}, u32[]{:S(2)}) collective-permute-start(bf16[128,512]{1,0:T(8,128)(2,1)S(1)} %get-tuple-element.102), channel_id=1, source_target_pairs={{0,0},{1,8},{2,16},{3,24},{4,4},{5,12},{6,20},{7,28},{8,1},{9,9},{... | collective-permute-start | bytes 393224 | tf_op jit(solution)/shard_map/ppermute | solution.py:44
  (24 other events, 169.9 us)

commit v12 on v9

--- a/solution.py
+++ b/solution.py
@@ -207,15 +207,24 @@
         spill_over = spill_over + jnp.concatenate(
             [jnp.zeros((margin - offset, inner_width), jnp.float32), masked[:offset]], axis=0
         )
-    from_next = passed_along(spill_over, "row", -1)
-    grad_x = (
-        local_grad
-        + jnp.concatenate(
-            [jnp.zeros((row_count - margin, inner_width), jnp.float32), from_next], axis=0
-        )
-    ).astype(jnp.bfloat16)
     if moves_tokens:
-        stacks, sources = ring_gather(grad_x, "row")
+        carried = jnp.concatenate(
+            [local_grad.astype(jnp.bfloat16), spill_over.astype(jnp.bfloat16)], axis=0
+        )
+        carried_stacks, sources = ring_gather(carried, "row")
+        count = lax.axis_size("row")
+        position = jnp.argsort(sources)
+        after = jnp.where(sources + 1 < count, position[jnp.minimum(sources + 1, count - 1)], count)
+        stacks = []
+        for stack in carried_stacks:
+            spills = jnp.concatenate(
+                [stack[:, row_count:], jnp.zeros((1, margin, stack.shape[2]), jnp.bfloat16)], axis=0
+            )
+            last = (
+                stack[:, row_count - margin : row_count].astype(jnp.float32)
+                + jnp.take(spills, after, axis=0).astype(jnp.float32)
+            ).astype(jnp.bfloat16)
+            stacks.append(jnp.concatenate([stack[:, : row_count - margin], last], axis=1))
         contract = (((2,), (1,)), ((), ()))
         weight_parts = jnp.split(in_weight, len(stacks), axis=1)
         grad_cols = lax.dot_general(
@@ -233,6 +242,13 @@
             grad_sum = lax.psum_scatter(grad_cols, "col", scatter_dimension=0, tiled=True)
         grad_tokens = placed_blocks(grad_sum, row_count)
     else:
+        from_next = passed_along(spill_over, "row", -1)
+        grad_x = (
+            local_grad
+            + jnp.concatenate(
+                [jnp.zeros((row_count - margin, inner_width), jnp.float32), from_next], axis=0
+            )
+        ).astype(jnp.bfloat16)
         partial_grad = lax.dot_general(
             grad_x, full_in, (((1,), (1,)), ((), ())), preferred_element_type=jnp.float32
         )

time: 234 us -> 242 us (1.034)
  local copies, waits for them, and re-layouts: 15.9 us -> 31 us
  waiting for transfers between devices: 91.3 us -> 87.5 us
  other arithmetic: 13.5 us -> 10.5 us
    slice x0 -> x8, local copies, waits for them, and re-layouts: none -> 7.12 us  [the longest x4 6.23 us: shards(): stack[:, :row_count - margin]]
    unnamed x64 -> x57, local copies, waits for them, and re-layouts: 4.69 us -> 9.66 us
    ppermute x2 -> x1, waiting for transfers between devices: 4.65 us -> 1.22 us  [passed_along(): lax.ppermute(value, axis, [(source, source + steps) for source in range(f...]
    dot_general x1, matrix products: 4.51 us -> 1.29 us  [ring_reduce_scatter(): jnp.dot(second, weight[:, half:], preferred_element_type=jnp.float32)]
    ppermute x28, waiting for transfers between devices: 17.1 us -> 13.9 us  [ring_gather(): part = lax.ppermute(part, axis, pairs)]
    gather x0 -> x5, local copies, waits for them, and re-layouts: none -> 2.99 us  [the longest x4 2.35 us: shards(): jnp.take(spills, after, axis=0).astype(jnp.float32)]
  transfers between devices with their start and end apart: 67 -> 66, of which waited for: 48 -> 41; matrix products, arithmetic and copies ran while one was open for 8% -> 9% of each run, Pallas kernels for 0% -> 0%
where the time goes in v12:
time: 242 us; the launch traced here: 241 us
  waiting for transfers between devices  87.5 us (36%)
  starting transfers between devices  76 us (31%)
  matrix products  32.7 us (14%)
  local copies, waits for them, and re-layouts  31 us (13%)
  other arithmetic  10.5 us (4%)
  between operations  2.86 us (1%)
    ppermute x28, starting transfers between devices, ring_gather(): part = lax.ppermute(part, axis, pairs)  30.3 us
    ppermute x28, starting transfers between devices, ring_reduce_scatter(): total = lax.ppermute(total, axis, pairs)  28.7 us
    ppermute x28, waiting for transfers between devices, ring_reduce_scatter(): total = lax.ppermute(total, axis, pairs)  24.8 us
    dot_general x1, matrix products, shards(): lax.dot_general(residual_grad, out_weight, (((1,), (1,)), ((), ())), pref...  14.6 us
    ppermute x28, waiting for transfers between devices, ring_gather(): part = lax.ppermute(part, axis, pairs)  13.9 us
    ppermute x1, waiting for transfers between devices, col_psum(): lax.ppermute(pair.astype(jnp.bfloat16), 'col', [(c, c ^ 2) for c in range...  13.6 us
    unnamed x57, local copies, waits for them, and re-layouts  9.66 us
    ppermute x2, waiting for transfers between devices, placed_blocks(): got.append(lax.ppermute(piece, ('row', 'col'), pairs))  9.31 us
  transfers between devices with their start and end apart: 66, of which 41 were waited for; matrix products, arithmetic and copies ran while one was open for 9% of the time, Pallas kernels for 0%

profile of v12, /device:TPU:2, one launch (start us, length us, event | category | flops | bytes accessed | tf_op | source)
XLA Modules:
  0.0 240.6 jit_solution(8295330392993748724)
XLA Ops:
  0.7 1.6 copy.26
  3.4 6.0 %all-to-all-start = ((bf16[128,8,256]{2,0,1:T(8,128)(2,1)}), bf16[128,8,256]{2,0,1:T(8,128)(2,1)S(1)}, u32[]{:S(2)}, u32[]{:S(2)}) async-start(bf16[128,8,256]{2,0,1:T(8,128)(2,1)} %copy.28), calls=%async_computation | async-start | bytes 1048576 | tf_op jit(solution)/shard_map/all_to_all | solution.py:24
  14.9 8.9 %all-to-all-done = bf16[128,8,256]{2,0,1:T(8,128)(2,1)S(1)} async-done(((bf16[128,8,256]{2,0,1:T(8,128)(2,1)}), bf16[128,8,256]{2,0,1:T(8,128)(2,1)S(1)}, u32[]{:S(2)}, u32[]{:S(2)}) %all-to-all-start) | async-done | bytes 524320 | tf_op jit(solution)/shard_map/all_to_all | solution.py:24
  23.9 1.9 collective-permute-done
  27.3 2.7 %fusion.136 = (bf16[8,128,1024]{2,1,0:T(8,128)(2,1)S(1)}, f32[8,128,1024]{2,1,0:T(8,128)S(1)}) fusion(bf16[512,2048]{1,0:T(8,128)(2,1)} %param.22, bf16[8,128,512]{2,1,0:T(8,128)(2,1)S(1)} %gather_fusion.4, pred[8]{0:T(512)(128)(4,1)S(1)} %compare_and_fusion.3), kind=kOutput, calls=%fused_computation.295 | convolution fusion | flops 1075314688 | bytes 8388616 | tf_op jit(solution)/shard_map/dot_general | solution.py:94
  30.9 1.3 fusion.135
  32.2 2.0 collective-permute-start.15
  36.4 2.0 collective-permute-done.8
  40.4 1.7 collective-permute-start.16
  44.6 1.4 collective-permute-done.9
  47.7 1.4 collective-permute-start.17
  49.1 1.3 collective-permute-start.24
  51.4 1.4 collective-permute-done.10
  55.8 1.3 collective-permute-start.25
  57.9 2.3 collective-permute-done.11
  62.0 1.3 collective-permute-start.19
  63.3 1.5 collective-permute-start.26
  65.8 2.8 %collective-permute-done.12 = bf16[128,512]{1,0:T(8,128)(2,1)S(1)} collective-permute-done((bf16[128,512]{1,0:T(8,128)(2,1)S(1)}, bf16[128,512]{1,0:T(8,128)(2,1)S(1)}, u32[]{:S(2)}, u32[]{:S(2)}) %collective-permute-start.12) | collective-permute-done | bytes 131104 | tf_op jit(solution)/shard_map/ppermute | solution.py:104
  70.2 1.8 collective-permute-start.20
  72.0 1.4 collective-permute-start.27
  73.3 1.7 collective-permute-done.6
  75.0 2.8 %collective-permute-done.13 = bf16[128,512]{1,0:T(8,128)(2,1)S(1)} collective-permute-done((bf16[128,512]{1,0:T(8,128)(2,1)S(1)}, bf16[128,512]{1,0:T(8,128)(2,1)S(1)}, u32[]{:S(2)}, u32[]{:S(2)}) %collective-permute-start.13) | collective-permute-done | bytes 131104 | tf_op jit(solution)/shard_map/ppermute | solution.py:104
  79.5 1.3 collective-permute-start.21
  80.8 1.8 collective-permute-start.28
  82.9 1.4 collective-permute-done.14
  84.5 1.4 collective-permute-done.28
  86.0 3.7 %collective-permute-start.29 = (bf16[3,2048]{1,0:T(4,128)(2,1)S(1)}, bf16[3,2048]{1,0:T(4,128)(2,1)S(1)}, u32[]{:S(2)}, u32[]{:S(2)}) collective-permute-start(bf16[3,2048]{1,0:T(4,128)(2,1)S(1)} %pad_maximum_fusion.2), channel_id=1, source_target_pairs={{0,4},{4,8},{8,12},{12,16},{16,20},{20,24},{24,28},{1,5},{5,9},{9,... | collective-permute-start | bytes 36872 | tf_op jit(solution)/shard_map/ppermute | solution.py:13
  92.2 8.8 %convolution_convert_fusion = bf16[128,4096]{1,0:T(8,128)(2,1)S(1)} fusion(bf16[2048,4096]{1,0:T(8,128)(2,1)} %param.25, bf16[128,2048]{1,0:T(8,128)(2,1)S(1)} %copy-done.12, f32[128,2048]{1,0:T(8,128)S(1)} %fusion.9), kind=kOutput, calls=%fused_computation.11 | convolution fusion | flops 2150891520 | bytes 19398656 | tf_op jit(solution)/shard_map/dot_general | solution.py:178
  101.2 1.9 collective-permute-done.30
  103.7 13.6 %collective-permute-done.31 = bf16[128,2048]{1,0:T(8,128)(2,1)S(1)} collective-permute-done((bf16[128,2048]{1,0:T(8,128)(2,1)S(1)}, bf16[128,2048]{1,0:T(8,128)(2,1)S(1)}, u32[]{:S(2)}, u32[]{:S(2)}) %collective-permute-start.31) | collective-permute-done | bytes 524320 | tf_op jit(solution)/shard_map/ppermute | solution.py:120
  118.6 2.0 collective-permute-done.32
  120.6 1.8 maximum_select_fusion
  122.4 14.6 %multiply_multiply_fusion.2 = (f32[128,2048]{1,0:T(8,128)}, f32[128,2048]{1,0:T(8,128)S(1)}, bf16[128,2048]{1,0:T(8,128)(2,1)}) fusion(f32[128]{0:T(128)S(1)} %get-tuple-element.108, f32[2048]{0:T(1024)S(1)} %bitcast.324, f32[128,2048]{1,0:T(8,128)} %copy-done.7, bf16[128,2048]{1,0:T(8,128)(2,1)} %param.23, bf16[2048,4096]{1,0:T(8,128)(2,1)} %param.25, ...), kind=kOutput, calls=%fused_computation.63 | convolution fusion | flops 2155872256 | bytes 24126464 | tf_op jit(solution)/shard_map/dot_general | solution.py:191
  137.8 1.3 slice.373
  140.8 2.3 collective-permute-start.54
  143.9 2.0 collective-permute-start.40
  146.0 2.3 collective-permute-done.54
  148.3 1.7 collective-permute-start.55
  150.7 1.9 collective-permute-done.40
  153.2 1.6 bitcast_dynamic-update-slice_fusion.30
  154.8 1.3 collective-permute-start.48
  157.1 1.6 collective-permute-start.56
  160.7 1.7 collective-permute-start.49
  163.5 1.9 collective-permute-start.57
  168.0 1.4 collective-permute-start.50
  170.0 1.9 collective-permute-start.58
  172.0 2.3 collective-permute-done.43
  175.0 2.0 collective-permute-start.51
  177.1 1.4 collective-permute-start.59
  179.1 1.9 collective-permute-done.44
  181.9 1.9 collective-permute-start.52
  184.2 1.7 collective-permute-start.60
  188.6 1.4 collective-permute-start.53
  192.5 2.3 slice.379
  199.8 1.5 slice.388
  204.8 2.1 fusion.19
  208.9 1.8 add_convert_fusion
  211.7 1.9 collective-permute-done.61
  214.1 8.1 %collective-permute-done.62 = bf16[256,512]{1,0:T(8,128)(2,1)S(1)} collective-permute-done((bf16[256,512]{1,0:T(8,128)(2,1)S(1)}, bf16[256,512]{1,0:T(8,128)(2,1)S(1)}, u32[]{:S(2)}, u32[]{:S(2)}) %collective-permute-start.62) | collective-permute-done | bytes 262176 | tf_op jit(solution)/shard_map/ppermute | solution.py:139
  222.3 3.0 %collective-permute-start.64 = (bf16[128,512]{1,0:T(8,128)(2,1)S(1)}, bf16[128,512]{1,0:T(8,128)(2,1)S(1)}, u32[]{:S(2)}, u32[]{:S(2)}) collective-permute-start(bf16[128,512]{1,0:T(8,128)(2,1)S(1)} %get-tuple-element.97), channel_id=1, source_target_pairs={{0,0},{1,8},{2,16},{3,24},{4,4},{5,12},{6,20},{7,28},{8,1},{9,9},{... | collective-permute-start | bytes 393224 | tf_op jit(solution)/shard_map/ppermute | solution.py:44
  225.4 3.4 %collective-permute-start.63 = (bf16[128,512]{1,0:T(8,128)(2,1)S(1)}, bf16[128,512]{1,0:T(8,128)(2,1)S(1)}, u32[]{:S(2)}, u32[]{:S(2)}) collective-permute-start(bf16[128,512]{1,0:T(8,128)(2,1)S(1)} %get-tuple-element.98), channel_id=1, source_target_pairs={{0,4},{1,12},{2,20},{3,28},{4,0},{5,8},{6,16},{7,24},{8,5},{9,13},... | collective-permute-start | bytes 393224 | tf_op jit(solution)/shard_map/ppermute | solution.py:44
  228.8 1.8 dynamic-slice_convert_fusion
  230.5 5.9 %collective-permute-done.64 = bf16[128,512]{1,0:T(8,128)(2,1)S(1)} collective-permute-done((bf16[128,512]{1,0:T(8,128)(2,1)S(1)}, bf16[128,512]{1,0:T(8,128)(2,1)S(1)}, u32[]{:S(2)}, u32[]{:S(2)}) %collective-permute-start.64) | collective-permute-done | bytes 131104 | tf_op jit(solution)/shard_map/ppermute | solution.py:44
  236.5 3.4 %collective-permute-done.63 = bf16[128,512]{1,0:T(8,128)(2,1)S(1)} collective-permute-done((bf16[128,512]{1,0:T(8,128)(2,1)S(1)}, bf16[128,512]{1,0:T(8,128)(2,1)S(1)}, u32[]{:S(2)}, u32[]{:S(2)}) %collective-permute-start.63) | collective-permute-done | bytes 131104 | tf_op jit(solution)/shard_map/ppermute | solution.py:44
  (227 shorter events, 64.2 us)
Async XLA Ops:
  3.4 20.5 %all-to-all-start = ((bf16[128,8,256]{2,0,1:T(8,128)(2,1)}), bf16[128,8,256]{2,0,1:T(8,128)(2,1)S(1)}, u32[]{:S(2)}, u32[]{:S(2)}) async-start(bf16[128,8,256]{2,0,1:T(8,128)(2,1)} %copy.28), calls=%async_computation | async-start | bytes 1048576 | tf_op jit(solution)/shard_map/all_to_all | solution.py:24
  30.0 6.4 %collective-permute-start.1 = (bf16[128,512]{1,0:T(8,128)(2,1)S(1)}, bf16[128,512]{1,0:T(8,128)(2,1)S(1)}, u32[]{:S(2)}, u32[]{:S(2)}) collective-permute-start(bf16[128,512]{1,0:T(8,128)(2,1)S(1)} %get-tuple-element.83), channel_id=1, source_target_pairs={{0,8},{8,16},{16,24},{24,28},{28,20},{20,12},{12,4},{4,0},{1,9},{9... | collective-permute-start | bytes 393224 | tf_op jit(solution)/shard_map/ppermute | solution.py:104
  30.8 7.6 %collective-permute-start.8 = (bf16[128,512]{1,0:T(8,128)(2,1)S(1)}, bf16[128,512]{1,0:T(8,128)(2,1)S(1)}, u32[]{:S(2)}, u32[]{:S(2)}) collective-permute-start(bf16[128,512]{1,0:T(8,128)(2,1)S(1)} %get-tuple-element.84), channel_id=1, source_target_pairs={{0,8},{8,16},{16,24},{24,28},{28,20},{20,12},{12,4},{4,0},{1,9},{9... | collective-permute-start | bytes 393224 | tf_op jit(solution)/shard_map/ppermute | solution.py:104
  32.2 7.4 %collective-permute-start.15 = (bf16[128,512]{1,0:T(8,128)(2,1)S(1)}, bf16[128,512]{1,0:T(8,128)(2,1)S(1)}, u32[]{:S(2)}, u32[]{:S(2)}) collective-permute-start(bf16[128,512]{1,0:T(8,128)(2,1)S(1)} %get-tuple-element.85), channel_id=1, source_target_pairs={{8,0},{16,8},{24,16},{28,24},{20,28},{12,20},{4,12},{0,4},{9,1},{1... | collective-permute-start | bytes 393224 | tf_op jit(solution)/shard_map/ppermute | solution.py:104
  34.2 6.1 %collective-permute-start.22 = (bf16[128,512]{1,0:T(8,128)(2,1)S(1)}, bf16[128,512]{1,0:T(8,128)(2,1)S(1)}, u32[]{:S(2)}, u32[]{:S(2)}) collective-permute-start(bf16[128,512]{1,0:T(8,128)(2,1)S(1)} %get-tuple-element.86), channel_id=1, source_target_pairs={{8,0},{16,8},{24,16},{28,24},{20,28},{12,20},{4,12},{0,4},{9,1},{1... | collective-permute-start | bytes 393224 | tf_op jit(solution)/shard_map/ppermute | solution.py:104
  38.5 6.2 %collective-permute-start.2 = (bf16[128,512]{1,0:T(8,128)(2,1)S(1)}, bf16[128,512]{1,0:T(8,128)(2,1)S(1)}, u32[]{:S(2)}, u32[]{:S(2)}) collective-permute-start(bf16[128,512]{1,0:T(8,128)(2,1)S(1)} %get-tuple-element.66), channel_id=1, source_target_pairs={{0,8},{8,16},{16,24},{24,28},{28,20},{20,12},{12,4},{4,0},{1,9},{9... | collective-permute-start | bytes 393224 | tf_op jit(solution)/shard_map/ppermute | solution.py:104
  39.3 6.8 %collective-permute-start.9 = (bf16[128,512]{1,0:T(8,128)(2,1)S(1)}, bf16[128,512]{1,0:T(8,128)(2,1)S(1)}, u32[]{:S(2)}, u32[]{:S(2)}) collective-permute-start(bf16[128,512]{1,0:T(8,128)(2,1)S(1)} %get-tuple-element.67), channel_id=1, source_target_pairs={{0,8},{8,16},{16,24},{24,28},{28,20},{20,12},{12,4},{4,0},{1,9},{9... | collective-permute-start | bytes 393224 | tf_op jit(solution)/shard_map/ppermute | solution.py:104
  40.4 7.1 %collective-permute-start.16 = (bf16[128,512]{1,0:T(8,128)(2,1)S(1)}, bf16[128,512]{1,0:T(8,128)(2,1)S(1)}, u32[]{:S(2)}, u32[]{:S(2)}) collective-permute-start(bf16[128,512]{1,0:T(8,128)(2,1)S(1)} %get-tuple-element.80), channel_id=1, source_target_pairs={{8,0},{16,8},{24,16},{28,24},{20,28},{12,20},{4,12},{0,4},{9,1},{1... | collective-permute-start | bytes 393224 | tf_op jit(solution)/shard_map/ppermute | solution.py:104
  42.1 5.5 %collective-permute-start.23 = (bf16[128,512]{1,0:T(8,128)(2,1)S(1)}, bf16[128,512]{1,0:T(8,128)(2,1)S(1)}, u32[]{:S(2)}, u32[]{:S(2)}) collective-permute-start(bf16[128,512]{1,0:T(8,128)(2,1)S(1)} %get-tuple-element.81), channel_id=1, source_target_pairs={{8,0},{16,8},{24,16},{28,24},{20,28},{12,20},{4,12},{0,4},{9,1},{1... | collective-permute-start | bytes 393224 | tf_op jit(solution)/shard_map/ppermute | solution.py:104
  46.1 5.2 %collective-permute-start.3 = (bf16[128,512]{1,0:T(8,128)(2,1)S(1)}, bf16[128,512]{1,0:T(8,128)(2,1)S(1)}, u32[]{:S(2)}, u32[]{:S(2)}) collective-permute-start(bf16[128,512]{1,0:T(8,128)(2,1)S(1)} %get-tuple-element.64), channel_id=1, source_target_pairs={{0,8},{8,16},{16,24},{24,28},{28,20},{20,12},{12,4},{4,0},{1,9},{9... | collective-permute-start | bytes 393224 | tf_op jit(solution)/shard_map/ppermute | solution.py:104
  46.9 5.8 %collective-permute-start.10 = (bf16[128,512]{1,0:T(8,128)(2,1)S(1)}, bf16[128,512]{1,0:T(8,128)(2,1)S(1)}, u32[]{:S(2)}, u32[]{:S(2)}) collective-permute-start(bf16[128,512]{1,0:T(8,128)(2,1)S(1)} %get-tuple-element.65), channel_id=1, source_target_pairs={{0,8},{8,16},{16,24},{24,28},{28,20},{20,12},{12,4},{4,0},{1,9},{9... | collective-permute-start | bytes 393224 | tf_op jit(solution)/shard_map/ppermute | solution.py:104
  47.7 6.9 %collective-permute-start.17 = (bf16[128,512]{1,0:T(8,128)(2,1)S(1)}, bf16[128,512]{1,0:T(8,128)(2,1)S(1)}, u32[]{:S(2)}, u32[]{:S(2)}) collective-permute-start(bf16[128,512]{1,0:T(8,128)(2,1)S(1)} %get-tuple-element.78), channel_id=1, source_target_pairs={{8,0},{16,8},{24,16},{28,24},{20,28},{12,20},{4,12},{0,4},{9,1},{1... | collective-permute-start | bytes 393224 | tf_op jit(solution)/shard_map/ppermute | solution.py:104
  49.1 5.5 %collective-permute-start.24 = (bf16[128,512]{1,0:T(8,128)(2,1)S(1)}, bf16[128,512]{1,0:T(8,128)(2,1)S(1)}, u32[]{:S(2)}, u32[]{:S(2)}) collective-permute-start(bf16[128,512]{1,0:T(8,128)(2,1)S(1)} %get-tuple-element.79), channel_id=1, source_target_pairs={{8,0},{16,8},{24,16},{28,24},{20,28},{12,20},{4,12},{0,4},{9,1},{1... | collective-permute-start | bytes 393224 | tf_op jit(solution)/shard_map/ppermute | solution.py:104
  52.9 5.0 %collective-permute-start.4 = (bf16[128,512]{1,0:T(8,128)(2,1)S(1)}, bf16[128,512]{1,0:T(8,128)(2,1)S(1)}, u32[]{:S(2)}, u32[]{:S(2)}) collective-permute-start(bf16[128,512]{1,0:T(8,128)(2,1)S(1)} %get-tuple-element.62), channel_id=1, source_target_pairs={{0,8},{8,16},{16,24},{24,28},{28,20},{20,12},{12,4},{4,0},{1,9},{9... | collective-permute-start | bytes 393224 | tf_op jit(solution)/shard_map/ppermute | solution.py:104
  53.7 6.5 %collective-permute-start.11 = (bf16[128,512]{1,0:T(8,128)(2,1)S(1)}, bf16[128,512]{1,0:T(8,128)(2,1)S(1)}, u32[]{:S(2)}, u32[]{:S(2)}) collective-permute-start(bf16[128,512]{1,0:T(8,128)(2,1)S(1)} %get-tuple-element.63), channel_id=1, source_target_pairs={{0,8},{8,16},{16,24},{24,28},{28,20},{20,12},{12,4},{4,0},{1,9},{9... | collective-permute-start | bytes 393224 | tf_op jit(solution)/shard_map/ppermute | solution.py:104
  54.7 7.0 %collective-permute-start.18 = (bf16[128,512]{1,0:T(8,128)(2,1)S(1)}, bf16[128,512]{1,0:T(8,128)(2,1)S(1)}, u32[]{:S(2)}, u32[]{:S(2)}) collective-permute-start(bf16[128,512]{1,0:T(8,128)(2,1)S(1)} %get-tuple-element.76), channel_id=1, source_target_pairs={{8,0},{16,8},{24,16},{28,24},{20,28},{12,20},{4,12},{0,4},{9,1},{1... | collective-permute-start | bytes 393224 | tf_op jit(solution)/shard_map/ppermute | solution.py:104
  55.8 6.1 %collective-permute-start.25 = (bf16[128,512]{1,0:T(8,128)(2,1)S(1)}, bf16[128,512]{1,0:T(8,128)(2,1)S(1)}, u32[]{:S(2)}, u32[]{:S(2)}) collective-permute-start(bf16[128,512]{1,0:T(8,128)(2,1)S(1)} %get-tuple-element.77), channel_id=1, source_target_pairs={{8,0},{16,8},{24,16},{28,24},{20,28},{12,20},{4,12},{0,4},{9,1},{1... | collective-permute-start | bytes 393224 | tf_op jit(solution)/shard_map/ppermute | solution.py:104
  60.2 5.5 %collective-permute-start.5 = (bf16[128,512]{1,0:T(8,128)(2,1)S(1)}, bf16[128,512]{1,0:T(8,128)(2,1)S(1)}, u32[]{:S(2)}, u32[]{:S(2)}) collective-permute-start(bf16[128,512]{1,0:T(8,128)(2,1)S(1)} %get-tuple-element.60), channel_id=1, source_target_pairs={{0,8},{8,16},{16,24},{24,28},{28,20},{20,12},{12,4},{4,0},{1,9},{9... | collective-permute-start | bytes 393224 | tf_op jit(solution)/shard_map/ppermute | solution.py:104
  61.1 7.5 %collective-permute-start.12 = (bf16[128,512]{1,0:T(8,128)(2,1)S(1)}, bf16[128,512]{1,0:T(8,128)(2,1)S(1)}, u32[]{:S(2)}, u32[]{:S(2)}) collective-permute-start(bf16[128,512]{1,0:T(8,128)(2,1)S(1)} %get-tuple-element.61), channel_id=1, source_target_pairs={{0,8},{8,16},{16,24},{24,28},{28,20},{20,12},{12,4},{4,0},{1,9},{9... | collective-permute-start | bytes 393224 | tf_op jit(solution)/shard_map/ppermute | solution.py:104
  62.0 7.6 %collective-permute-start.19 = (bf16[128,512]{1,0:T(8,128)(2,1)S(1)}, bf16[128,512]{1,0:T(8,128)(2,1)S(1)}, u32[]{:S(2)}, u32[]{:S(2)}) collective-permute-start(bf16[128,512]{1,0:T(8,128)(2,1)S(1)} %get-tuple-element.74), channel_id=1, source_target_pairs={{8,0},{16,8},{24,16},{28,24},{20,28},{12,20},{4,12},{0,4},{9,1},{1... | collective-permute-start | bytes 393224 | tf_op jit(solution)/shard_map/ppermute | solution.py:104
  63.3 6.8 %collective-permute-start.26 = (bf16[128,512]{1,0:T(8,128)(2,1)S(1)}, bf16[128,512]{1,0:T(8,128)(2,1)S(1)}, u32[]{:S(2)}, u32[]{:S(2)}) collective-permute-start(bf16[128,512]{1,0:T(8,128)(2,1)S(1)} %get-tuple-element.75), channel_id=1, source_target_pairs={{8,0},{16,8},{24,16},{28,24},{20,28},{12,20},{4,12},{0,4},{9,1},{1... | collective-permute-start | bytes 393224 | tf_op jit(solution)/shard_map/ppermute | solution.py:104
  68.7 6.4 %collective-permute-start.6 = (bf16[128,512]{1,0:T(8,128)(2,1)S(1)}, bf16[128,512]{1,0:T(8,128)(2,1)S(1)}, u32[]{:S(2)}, u32[]{:S(2)}) collective-permute-start(bf16[128,512]{1,0:T(8,128)(2,1)S(1)} %get-tuple-element.58), channel_id=1, source_target_pairs={{0,8},{8,16},{16,24},{24,28},{28,20},{20,12},{12,4},{4,0},{1,9},{9... | collective-permute-start | bytes 393224 | tf_op jit(solution)/shard_map/ppermute | solution.py:104
  69.3 8.5 %collective-permute-start.13 = (bf16[128,512]{1,0:T(8,128)(2,1)S(1)}, bf16[128,512]{1,0:T(8,128)(2,1)S(1)}, u32[]{:S(2)}, u32[]{:S(2)}) collective-permute-start(bf16[128,512]{1,0:T(8,128)(2,1)S(1)} %get-tuple-element.59), channel_id=1, source_target_pairs={{0,8},{8,16},{16,24},{24,28},{28,20},{20,12},{12,4},{4,0},{1,9},{9... | collective-permute-start | bytes 393224 | tf_op jit(solution)/shard_map/ppermute | solution.py:104
  70.2 8.4 %collective-permute-start.20 = (bf16[128,512]{1,0:T(8,128)(2,1)S(1)}, bf16[128,512]{1,0:T(8,128)(2,1)S(1)}, u32[]{:S(2)}, u32[]{:S(2)}) collective-permute-start(bf16[128,512]{1,0:T(8,128)(2,1)S(1)} %get-tuple-element.72), channel_id=1, source_target_pairs={{8,0},{16,8},{24,16},{28,24},{20,28},{12,20},{4,12},{0,4},{9,1},{1... | collective-permute-start | bytes 393224 | tf_op jit(solution)/shard_map/ppermute | solution.py:104
  72.0 7.4 %collective-permute-start.27 = (bf16[128,512]{1,0:T(8,128)(2,1)S(1)}, bf16[128,512]{1,0:T(8,128)(2,1)S(1)}, u32[]{:S(2)}, u32[]{:S(2)}) collective-permute-start(bf16[128,512]{1,0:T(8,128)(2,1)S(1)} %get-tuple-element.73), channel_id=1, source_target_pairs={{8,0},{16,8},{24,16},{28,24},{20,28},{12,20},{4,12},{0,4},{9,1},{1... | collective-permute-start | bytes 393224 | tf_op jit(solution)/shard_map/ppermute | solution.py:104
  77.9 5.0 %collective-permute-start.7 = (bf16[128,512]{1,0:T(8,128)(2,1)S(1)}, bf16[128,512]{1,0:T(8,128)(2,1)S(1)}, u32[]{:S(2)}, u32[]{:S(2)}) collective-permute-start(bf16[128,512]{1,0:T(8,128)(2,1)S(1)} %get-tuple-element.56), channel_id=1, source_target_pairs={{0,8},{8,16},{16,24},{24,28},{28,20},{20,12},{12,4},{4,0},{1,9},{9... | collective-permute-start | bytes 393224 | tf_op jit(solution)/shard_map/ppermute | solution.py:104
  78.4 5.9 %collective-permute-start.14 = (bf16[128,512]{1,0:T(8,128)(2,1)S(1)}, bf16[128,512]{1,0:T(8,128)(2,1)S(1)}, u32[]{:S(2)}, u32[]{:S(2)}) collective-permute-start(bf16[128,512]{1,0:T(8,128)(2,1)S(1)} %get-tuple-element.57), channel_id=1, source_target_pairs={{0,8},{8,16},{16,24},{24,28},{28,20},{20,12},{12,4},{4,0},{1,9},{9... | collective-permute-start | bytes 393224 | tf_op jit(solution)/shard_map/ppermute | solution.py:104
  79.5 5.0 %collective-permute-start.21 = (bf16[128,512]{1,0:T(8,128)(2,1)S(1)}, bf16[128,512]{1,0:T(8,128)(2,1)S(1)}, u32[]{:S(2)}, u32[]{:S(2)}) collective-permute-start(bf16[128,512]{1,0:T(8,128)(2,1)S(1)} %get-tuple-element.70), channel_id=1, source_target_pairs={{8,0},{16,8},{24,16},{28,24},{20,28},{12,20},{4,12},{0,4},{9,1},{1... | collective-permute-start | bytes 393224 | tf_op jit(solution)/shard_map/ppermute | solution.py:104
  80.8 5.1 %collective-permute-start.28 = (bf16[128,512]{1,0:T(8,128)(2,1)S(1)}, bf16[128,512]{1,0:T(8,128)(2,1)S(1)}, u32[]{:S(2)}, u32[]{:S(2)}) collective-permute-start(bf16[128,512]{1,0:T(8,128)(2,1)S(1)} %get-tuple-element.71), channel_id=1, source_target_pairs={{8,0},{16,8},{24,16},{28,24},{20,28},{12,20},{4,12},{0,4},{9,1},{1... | collective-permute-start | bytes 393224 | tf_op jit(solution)/shard_map/ppermute | solution.py:104
  86.0 5.0 %collective-permute-start.29 = (bf16[3,2048]{1,0:T(4,128)(2,1)S(1)}, bf16[3,2048]{1,0:T(4,128)(2,1)S(1)}, u32[]{:S(2)}, u32[]{:S(2)}) collective-permute-start(bf16[3,2048]{1,0:T(4,128)(2,1)S(1)} %pad_maximum_fusion.2), channel_id=1, source_target_pairs={{0,4},{4,8},{8,12},{12,16},{16,20},{20,24},{24,28},{1,5},{5,9},{9,... | collective-permute-start | bytes 36872 | tf_op jit(solution)/shard_map/ppermute | solution.py:13
  101.1 2.0 collective-permute-start.30
  103.4 14.0 %collective-permute-start.31 = (bf16[128,2048]{1,0:T(8,128)(2,1)S(1)}, bf16[128,2048]{1,0:T(8,128)(2,1)S(1)}, u32[]{:S(2)}, u32[]{:S(2)}) collective-permute-start(bf16[128,2048]{1,0:T(8,128)(2,1)S(1)} %fusion.42), channel_id=1, source_target_pairs={{0,2},{1,3},{2,0},{3,1},{4,6},{5,7},{6,4},{7,5},{8,10},{9,11},{10,... | collective-permute-start | bytes 1572872 | tf_op jit(solution)/shard_map/ppermute | solution.py:120
  117.7 2.9 %collective-permute-start.32 = (f32[128,2048]{1,0:T(8,128)S(1)}, f32[128,2048]{1,0:T(8,128)}, u32[]{:S(2)}, u32[]{:S(2)}) collective-permute-start(f32[128,2048]{1,0:T(8,128)S(1)} %convert_add_fusion.1), channel_id=1, source_target_pairs={{0,1},{1,0},{2,3},{3,2},{4,5},{5,4},{6,7},{7,6},{8,9},{9,8},{10,11... | collective-permute-start | bytes 3145736 | tf_op jit(solution)/shard_map/ppermute | solution.py:123
  140.8 7.4 %collective-permute-start.54 = (bf16[131,512]{1,0:T(8,128)(2,1)}, bf16[131,512]{1,0:T(8,128)(2,1)}, u32[]{:S(2)}, u32[]{:S(2)}) collective-permute-start(bf16[131,512]{1,0:T(8,128)(2,1)} %get-tuple-element.43), channel_id=1, source_target_pairs={{8,0},{16,8},{24,16},{28,24},{20,28},{12,20},{4,12},{0,4},{9,1},{1... | collective-permute-start | bytes 402440 | tf_op jit(solution)/shard_map/ppermute | solution.py:77
  143.1 6.9 %collective-permute-start.33 = (bf16[131,512]{1,0:T(8,128)(2,1)}, bf16[131,512]{1,0:T(8,128)(2,1)}, u32[]{:S(2)}, u32[]{:S(2)}) collective-permute-start(bf16[131,512]{1,0:T(8,128)(2,1)} %get-tuple-element.90), channel_id=1, source_target_pairs={{0,8},{8,16},{16,24},{24,28},{28,20},{20,12},{12,4},{4,0},{1,9},{9... | collective-permute-start | bytes 402440 | tf_op jit(solution)/shard_map/ppermute | solution.py:77
  143.9 8.7 %collective-permute-start.40 = (bf16[131,512]{1,0:T(8,128)(2,1)}, bf16[131,512]{1,0:T(8,128)(2,1)}, u32[]{:S(2)}, u32[]{:S(2)}) collective-permute-start(bf16[131,512]{1,0:T(8,128)(2,1)} %get-tuple-element.92), channel_id=1, source_target_pairs={{0,8},{8,16},{16,24},{24,28},{28,20},{20,12},{12,4},{4,0},{1,9},{9... | collective-permute-start | bytes 402440 | tf_op jit(solution)/shard_map/ppermute | solution.py:77
  145.9 8.9 %collective-permute-start.47 = (bf16[131,512]{1,0:T(8,128)(2,1)S(1)}, bf16[131,512]{1,0:T(8,128)(2,1)S(1)}, u32[]{:S(2)}, u32[]{:S(2)}) collective-permute-start(bf16[131,512]{1,0:T(8,128)(2,1)S(1)} %get-tuple-element.94), channel_id=1, source_target_pairs={{8,0},{16,8},{24,16},{28,24},{20,28},{12,20},{4,12},{0,4},{9,1},{1... | collective-permute-start | bytes 402440 | tf_op jit(solution)/shard_map/ppermute | solution.py:77
  148.3 8.8 %collective-permute-start.55 = (bf16[131,512]{1,0:T(8,128)(2,1)}, bf16[131,512]{1,0:T(8,128)(2,1)S(1)}, u32[]{:S(2)}, u32[]{:S(2)}) collective-permute-start(bf16[131,512]{1,0:T(8,128)(2,1)} %collective-permute-done.54), channel_id=1, source_target_pairs={{8,0},{16,8},{24,16},{28,24},{20,28},{12,20},{4,12},{0,4},{9,1},{1... | collective-permute-start | bytes 402440 | tf_op jit(solution)/shard_map/ppermute | solution.py:77
  150.0 8.7 %collective-permute-start.34 = (bf16[131,512]{1,0:T(8,128)(2,1)}, bf16[131,512]{1,0:T(8,128)(2,1)S(1)}, u32[]{:S(2)}, u32[]{:S(2)}) collective-permute-start(bf16[131,512]{1,0:T(8,128)(2,1)} %collective-permute-done.33), channel_id=1, source_target_pairs={{0,8},{8,16},{16,24},{24,28},{28,20},{20,12},{12,4},{4,0},{1,9},{9... | collective-permute-start | bytes 402440 | tf_op jit(solution)/shard_map/ppermute | solution.py:77
  152.6 6.6 %collective-permute-start.41 = (bf16[131,512]{1,0:T(8,128)(2,1)}, bf16[131,512]{1,0:T(8,128)(2,1)S(1)}, u32[]{:S(2)}, u32[]{:S(2)}) collective-permute-start(bf16[131,512]{1,0:T(8,128)(2,1)} %collective-permute-done.40), channel_id=1, source_target_pairs={{0,8},{8,16},{16,24},{24,28},{28,20},{20,12},{12,4},{4,0},{1,9},{9... | collective-permute-start | bytes 402440 | tf_op jit(solution)/shard_map/ppermute | solution.py:77
  154.8 5.8 %collective-permute-start.48 = (bf16[131,512]{1,0:T(8,128)(2,1)S(1)}, bf16[131,512]{1,0:T(8,128)(2,1)S(1)}, u32[]{:S(2)}, u32[]{:S(2)}) collective-permute-start(bf16[131,512]{1,0:T(8,128)(2,1)S(1)} %collective-permute-done.47), channel_id=1, source_target_pairs={{8,0},{16,8},{24,16},{28,24},{20,28},{12,20},{4,12},{0,4},{9,1},{1... | collective-permute-start | bytes 402440 | tf_op jit(solution)/shard_map/ppermute | solution.py:77
  157.1 6.4 %collective-permute-start.56 = (bf16[131,512]{1,0:T(8,128)(2,1)S(1)}, bf16[131,512]{1,0:T(8,128)(2,1)S(1)}, u32[]{:S(2)}, u32[]{:S(2)}) collective-permute-start(bf16[131,512]{1,0:T(8,128)(2,1)S(1)} %collective-permute-done.55), channel_id=1, source_target_pairs={{8,0},{16,8},{24,16},{28,24},{20,28},{12,20},{4,12},{0,4},{9,1},{1... | collective-permute-start | bytes 402440 | tf_op jit(solution)/shard_map/ppermute | solution.py:77
  158.7 6.6 %collective-permute-start.35 = (bf16[131,512]{1,0:T(8,128)(2,1)S(1)}, bf16[131,512]{1,0:T(8,128)(2,1)S(1)}, u32[]{:S(2)}, u32[]{:S(2)}) collective-permute-start(bf16[131,512]{1,0:T(8,128)(2,1)S(1)} %collective-permute-done.34), channel_id=1, source_target_pairs={{0,8},{8,16},{16,24},{24,28},{28,20},{20,12},{12,4},{4,0},{1,9},{9... | collective-permute-start | bytes 402440 | tf_op jit(solution)/shard_map/ppermute | solution.py:77
  159.2 7.5 %collective-permute-start.42 = (bf16[131,512]{1,0:T(8,128)(2,1)S(1)}, bf16[131,512]{1,0:T(8,128)(2,1)S(1)}, u32[]{:S(2)}, u32[]{:S(2)}) collective-permute-start(bf16[131,512]{1,0:T(8,128)(2,1)S(1)} %collective-permute-done.41), channel_id=1, source_target_pairs={{0,8},{8,16},{16,24},{24,28},{28,20},{20,12},{12,4},{4,0},{1,9},{9... | collective-permute-start | bytes 402440 | tf_op jit(solution)/shard_map/ppermute | solution.py:77
  160.7 7.3 %collective-permute-start.49 = (bf16[131,512]{1,0:T(8,128)(2,1)S(1)}, bf16[131,512]{1,0:T(8,128)(2,1)S(1)}, u32[]{:S(2)}, u32[]{:S(2)}) collective-permute-start(bf16[131,512]{1,0:T(8,128)(2,1)S(1)} %collective-permute-done.48), channel_id=1, source_target_pairs={{8,0},{16,8},{24,16},{28,24},{20,28},{12,20},{4,12},{0,4},{9,1},{1... | collective-permute-start | bytes 402440 | tf_op jit(solution)/shard_map/ppermute | solution.py:77
  163.5 6.5 %collective-permute-start.57 = (bf16[131,512]{1,0:T(8,128)(2,1)S(1)}, bf16[131,512]{1,0:T(8,128)(2,1)S(1)}, u32[]{:S(2)}, u32[]{:S(2)}) collective-permute-start(bf16[131,512]{1,0:T(8,128)(2,1)S(1)} %collective-permute-done.56), channel_id=1, source_target_pairs={{8,0},{16,8},{24,16},{28,24},{20,28},{12,20},{4,12},{0,4},{9,1},{1... | collective-permute-start | bytes 402440 | tf_op jit(solution)/shard_map/ppermute | solution.py:77
  165.3 6.6 %collective-permute-start.36 = (bf16[131,512]{1,0:T(8,128)(2,1)S(1)}, bf16[131,512]{1,0:T(8,128)(2,1)S(1)}, u32[]{:S(2)}, u32[]{:S(2)}) collective-permute-start(bf16[131,512]{1,0:T(8,128)(2,1)S(1)} %collective-permute-done.35), channel_id=1, source_target_pairs={{0,8},{8,16},{16,24},{24,28},{28,20},{20,12},{12,4},{4,0},{1,9},{9... | collective-permute-start | bytes 402440 | tf_op jit(solution)/shard_map/ppermute | solution.py:77
  166.7 7.6 %collective-permute-start.43 = (bf16[131,512]{1,0:T(8,128)(2,1)S(1)}, bf16[131,512]{1,0:T(8,128)(2,1)S(1)}, u32[]{:S(2)}, u32[]{:S(2)}) collective-permute-start(bf16[131,512]{1,0:T(8,128)(2,1)S(1)} %collective-permute-done.42), channel_id=1, source_target_pairs={{0,8},{8,16},{16,24},{24,28},{28,20},{20,12},{12,4},{4,0},{1,9},{9... | collective-permute-start | bytes 402440 | tf_op jit(solution)/shard_map/ppermute | solution.py:77
  168.0 7.0 %collective-permute-start.50 = (bf16[131,512]{1,0:T(8,128)(2,1)S(1)}, bf16[131,512]{1,0:T(8,128)(2,1)S(1)}, u32[]{:S(2)}, u32[]{:S(2)}) collective-permute-start(bf16[131,512]{1,0:T(8,128)(2,1)S(1)} %collective-permute-done.49), channel_id=1, source_target_pairs={{8,0},{16,8},{24,16},{28,24},{20,28},{12,20},{4,12},{0,4},{9,1},{1... | collective-permute-start | bytes 402440 | tf_op jit(solution)/shard_map/ppermute | solution.py:77
  170.0 7.1 %collective-permute-start.58 = (bf16[131,512]{1,0:T(8,128)(2,1)S(1)}, bf16[131,512]{1,0:T(8,128)(2,1)S(1)}, u32[]{:S(2)}, u32[]{:S(2)}) collective-permute-start(bf16[131,512]{1,0:T(8,128)(2,1)S(1)} %collective-permute-done.57), channel_id=1, source_target_pairs={{8,0},{16,8},{24,16},{28,24},{20,28},{12,20},{4,12},{0,4},{9,1},{1... | collective-permute-start | bytes 402440 | tf_op jit(solution)/shard_map/ppermute | solution.py:77
  171.9 6.6 %collective-permute-start.37 = (bf16[131,512]{1,0:T(8,128)(2,1)S(1)}, bf16[131,512]{1,0:T(8,128)(2,1)S(1)}, u32[]{:S(2)}, u32[]{:S(2)}) collective-permute-start(bf16[131,512]{1,0:T(8,128)(2,1)S(1)} %collective-permute-done.36), channel_id=1, source_target_pairs={{0,8},{8,16},{16,24},{24,28},{28,20},{20,12},{12,4},{4,0},{1,9},{9... | collective-permute-start | bytes 402440 | tf_op jit(solution)/shard_map/ppermute | solution.py:77
  174.3 6.8 %collective-permute-start.44 = (bf16[131,512]{1,0:T(8,128)(2,1)S(1)}, bf16[131,512]{1,0:T(8,128)(2,1)S(1)}, u32[]{:S(2)}, u32[]{:S(2)}) collective-permute-start(bf16[131,512]{1,0:T(8,128)(2,1)S(1)} %collective-permute-done.43), channel_id=1, source_target_pairs={{0,8},{8,16},{16,24},{24,28},{28,20},{20,12},{12,4},{4,0},{1,9},{9... | collective-permute-start | bytes 402440 | tf_op jit(solution)/shard_map/ppermute | solution.py:77
  175.0 6.9 %collective-permute-start.51 = (bf16[131,512]{1,0:T(8,128)(2,1)S(1)}, bf16[131,512]{1,0:T(8,128)(2,1)S(1)}, u32[]{:S(2)}, u32[]{:S(2)}) collective-permute-start(bf16[131,512]{1,0:T(8,128)(2,1)S(1)} %collective-permute-done.50), channel_id=1, source_target_pairs={{8,0},{16,8},{24,16},{28,24},{20,28},{12,20},{4,12},{0,4},{9,1},{1... | collective-permute-start | bytes 402440 | tf_op jit(solution)/shard_map/ppermute | solution.py:77
  177.1 7.1 %collective-permute-start.59 = (bf16[131,512]{1,0:T(8,128)(2,1)S(1)}, bf16[131,512]{1,0:T(8,128)(2,1)S(1)}, u32[]{:S(2)}, u32[]{:S(2)}) collective-permute-start(bf16[131,512]{1,0:T(8,128)(2,1)S(1)} %collective-permute-done.58), channel_id=1, source_target_pairs={{8,0},{16,8},{24,16},{28,24},{20,28},{12,20},{4,12},{0,4},{9,1},{1... | collective-permute-start | bytes 402440 | tf_op jit(solution)/shard_map/ppermute | solution.py:77
  178.5 7.4 %collective-permute-start.38 = (bf16[131,512]{1,0:T(8,128)(2,1)S(1)}, bf16[131,512]{1,0:T(8,128)(2,1)S(1)}, u32[]{:S(2)}, u32[]{:S(2)}) collective-permute-start(bf16[131,512]{1,0:T(8,128)(2,1)S(1)} %collective-permute-done.37), channel_id=1, source_target_pairs={{0,8},{8,16},{16,24},{24,28},{28,20},{20,12},{12,4},{4,0},{1,9},{9... | collective-permute-start | bytes 402440 | tf_op jit(solution)/shard_map/ppermute | solution.py:77
  181.1 6.2 %collective-permute-start.45 = (bf16[131,512]{1,0:T(8,128)(2,1)S(1)}, bf16[131,512]{1,0:T(8,128)(2,1)S(1)}, u32[]{:S(2)}, u32[]{:S(2)}) collective-permute-start(bf16[131,512]{1,0:T(8,128)(2,1)S(1)} %collective-permute-done.44), channel_id=1, source_target_pairs={{0,8},{8,16},{16,24},{24,28},{28,20},{20,12},{12,4},{4,0},{1,9},{9... | collective-permute-start | bytes 402440 | tf_op jit(solution)/shard_map/ppermute | solution.py:77
  181.9 6.7 %collective-permute-start.52 = (bf16[131,512]{1,0:T(8,128)(2,1)S(1)}, bf16[131,512]{1,0:T(8,128)(2,1)S(1)}, u32[]{:S(2)}, u32[]{:S(2)}) collective-permute-start(bf16[131,512]{1,0:T(8,128)(2,1)S(1)} %collective-permute-done.51), channel_id=1, source_target_pairs={{8,0},{16,8},{24,16},{28,24},{20,28},{12,20},{4,12},{0,4},{9,1},{1... | collective-permute-start | bytes 402440 | tf_op jit(solution)/shard_map/ppermute | solution.py:77
  184.2 13.4 %collective-permute-start.60 = (bf16[131,512]{1,0:T(8,128)(2,1)S(1)}, bf16[131,512]{1,0:T(8,128)(2,1)S(1)}, u32[]{:S(2)}, u32[]{:S(2)}) collective-permute-start(bf16[131,512]{1,0:T(8,128)(2,1)S(1)} %collective-permute-done.59), channel_id=1, source_target_pairs={{8,0},{16,8},{24,16},{28,24},{20,28},{12,20},{4,12},{0,4},{9,1},{1... | collective-permute-start | bytes 402440 | tf_op jit(solution)/shard_map/ppermute | solution.py:77
  185.9 5.1 %collective-permute-start.39 = (bf16[131,512]{1,0:T(8,128)(2,1)S(1)}, bf16[131,512]{1,0:T(8,128)(2,1)S(1)}, u32[]{:S(2)}, u32[]{:S(2)}) collective-permute-start(bf16[131,512]{1,0:T(8,128)(2,1)S(1)} %collective-permute-done.38), channel_id=1, source_target_pairs={{0,8},{8,16},{16,24},{24,28},{28,20},{20,12},{12,4},{4,0},{1,9},{9... | collective-permute-start | bytes 402440 | tf_op jit(solution)/shard_map/ppermute | solution.py:77
  187.3 8.9 %collective-permute-start.46 = (bf16[131,512]{1,0:T(8,128)(2,1)S(1)}, bf16[131,512]{1,0:T(8,128)(2,1)S(1)}, u32[]{:S(2)}, u32[]{:S(2)}) collective-permute-start(bf16[131,512]{1,0:T(8,128)(2,1)S(1)} %collective-permute-done.45), channel_id=1, source_target_pairs={{0,8},{8,16},{16,24},{24,28},{28,20},{20,12},{12,4},{4,0},{1,9},{9... | collective-permute-start | bytes 402440 | tf_op jit(solution)/shard_map/ppermute | solution.py:77
  188.6 6.3 %collective-permute-start.53 = (bf16[131,512]{1,0:T(8,128)(2,1)S(1)}, bf16[131,512]{1,0:T(8,128)(2,1)S(1)}, u32[]{:S(2)}, u32[]{:S(2)}) collective-permute-start(bf16[131,512]{1,0:T(8,128)(2,1)S(1)} %collective-permute-done.52), channel_id=1, source_target_pairs={{8,0},{16,8},{24,16},{28,24},{20,28},{12,20},{4,12},{0,4},{9,1},{1... | collective-permute-start | bytes 402440 | tf_op jit(solution)/shard_map/ppermute | solution.py:77
  213.8 8.4 %collective-permute-start.62 = (bf16[256,512]{1,0:T(8,128)(2,1)S(1)}, bf16[256,512]{1,0:T(8,128)(2,1)S(1)}, u32[]{:S(2)}, u32[]{:S(2)}) collective-permute-start(bf16[256,512]{1,0:T(8,128)(2,1)S(1)} %bitcast_convert_fusion), channel_id=1, source_target_pairs={{0,2},{1,3},{2,0},{3,1},{4,6},{5,7},{6,4},{7,5},{8,10},{9,11},{10,... | collective-permute-start | bytes 786440 | tf_op jit(solution)/shard_map/ppermute | solution.py:139
  222.3 14.2 %collective-permute-start.64 = (bf16[128,512]{1,0:T(8,128)(2,1)S(1)}, bf16[128,512]{1,0:T(8,128)(2,1)S(1)}, u32[]{:S(2)}, u32[]{:S(2)}) collective-permute-start(bf16[128,512]{1,0:T(8,128)(2,1)S(1)} %get-tuple-element.97), channel_id=1, source_target_pairs={{0,0},{1,8},{2,16},{3,24},{4,4},{5,12},{6,20},{7,28},{8,1},{9,9},{... | collective-permute-start | bytes 393224 | tf_op jit(solution)/shard_map/ppermute | solution.py:44
  225.4 14.5 %collective-permute-start.63 = (bf16[128,512]{1,0:T(8,128)(2,1)S(1)}, bf16[128,512]{1,0:T(8,128)(2,1)S(1)}, u32[]{:S(2)}, u32[]{:S(2)}) collective-permute-start(bf16[128,512]{1,0:T(8,128)(2,1)S(1)} %get-tuple-element.98), channel_id=1, source_target_pairs={{0,4},{1,12},{2,20},{3,28},{4,0},{5,8},{6,16},{7,24},{8,5},{9,13},... | collective-permute-start | bytes 393224 | tf_op jit(solution)/shard_map/ppermute | solution.py:44
  (18 other events, 120.3 us)

commit v13 on v9

--- a/solution.py
+++ b/solution.py
@@ -88,21 +88,27 @@
     rows = token_cols.shape[0] // count
     blocks = token_cols.reshape(count, rows, token_cols.shape[1])
     half = weight.shape[1] // 2
-    steps = jnp.arange(count)
-    first = jnp.take(blocks, order[(place - 1 - steps) % count], axis=0).reshape(token_cols.shape)
-    second = jnp.take(blocks, order[(place + 1 + steps) % count], axis=0).reshape(token_cols.shape)
+    steps = jnp.arange(1, count)
+    later = (count - 1) * rows
+    first_0 = jnp.take(blocks, order[(place - 1) % count], axis=0)
+    second_0 = jnp.take(blocks, order[(place + 1) % count], axis=0)
+    start_a = jnp.dot(first_0, weight[:, :half], preferred_element_type=jnp.float32)
+    start_b = jnp.dot(second_0, weight[:, half:], preferred_element_type=jnp.float32)
+    first = jnp.take(blocks, order[(place - 1 - steps) % count], axis=0).reshape(later, -1)
+    second = jnp.take(blocks, order[(place + 1 + steps) % count], axis=0).reshape(later, -1)
     own_a = jnp.dot(first, weight[:, :half], preferred_element_type=jnp.float32)
     own_b = jnp.dot(second, weight[:, half:], preferred_element_type=jnp.float32)
-    owns = jnp.split(own_a.reshape(count, rows, half), chains, axis=2) + jnp.split(
-        own_b.reshape(count, rows, weight.shape[1] - half), chains, axis=2
-    )
+    own_a = own_a.reshape(count - 1, rows, half)
+    own_b = own_b.reshape(count - 1, rows, weight.shape[1] - half)
+    starts = jnp.split(start_a, chains, axis=1) + jnp.split(start_b, chains, axis=1)
+    owns = jnp.split(own_a, chains, axis=2) + jnp.split(own_b, chains, axis=2)
     sums = []
-    for number, own in enumerate(owns):
+    for number, (start, own) in enumerate(zip(starts, owns)):
         pairs = ahead if number < chains else behind
-        total = own[0].astype(jnp.bfloat16)
+        total = start.astype(jnp.bfloat16)
         for s in range(1, count):
             total = lax.ppermute(total, axis, pairs)
-            total = (total.astype(jnp.float32) + own[s]).astype(jnp.bfloat16)
+            total = (total.astype(jnp.float32) + own[s - 1]).astype(jnp.bfloat16)
         sums.append(total)
     return jnp.concatenate(sums, axis=1)
 

time: 234 us -> 230 us (0.983)
  waiting for transfers between devices: 91.3 us -> 85.9 us
  between operations: 2.83 us -> 6.92 us
  matrix products: 33 us -> 30.1 us
    dot_general x1, matrix products: 4.51 us -> 1.75 us  [ring_reduce_scatter(): jnp.dot(second, weight[:, half:], preferred_element_type=jnp.float32)]
    all_to_all x1, waiting for transfers between devices: 7.81 us -> 5.39 us  [fetched_columns(): mine = lax.all_to_all(mine, 'row', 1, 0, tiled=True)]
    unnamed x64 -> x66, local copies, waits for them, and re-layouts: 4.69 us -> 4.58 us
  transfers between devices with their start and end apart: 67 -> 67, of which waited for: 48 -> 47; matrix products, arithmetic and copies ran while one was open for 8% -> 8% of each run, Pallas kernels for 0% -> 0%
where the time goes in v13:
time: 230 us; the launch traced here: 229 us
  waiting for transfers between devices  85.9 us (37%)
  starting transfers between devices  75.2 us (33%)
  matrix products  30.1 us (13%)
  local copies, waits for them, and re-layouts  16.4 us (7%)
  other arithmetic  14.5 us (6%)
  between operations  6.92 us (3%)
    ppermute x28, starting transfers between devices, ring_gather(): part = lax.ppermute(part, axis, pairs)  31.2 us
    ppermute x28, starting transfers between devices, ring_reduce_scatter(): total = lax.ppermute(total, axis, pairs)  26.6 us
    ppermute x28, waiting for transfers between devices, ring_reduce_scatter(): total = lax.ppermute(total, axis, pairs)  25.1 us
    ppermute x28, waiting for transfers between devices, ring_gather(): part = lax.ppermute(part, axis, pairs)  16.7 us
    dot_general x1, matrix products, shards(): lax.dot_general(residual_grad, out_weight, (((1,), (1,)), ((), ())), pref...  14.7 us
    ppermute x1, waiting for transfers between devices, col_psum(): lax.ppermute(pair.astype(jnp.bfloat16), 'col', [(c, c ^ 2) for c in range...  13.4 us
    dot_general x1, matrix products, shards(): jnp.dot(mixed, out_weight, preferred_element_type=jnp.float32)  8.81 us
    ppermute x2, waiting for transfers between devices, placed_blocks(): got.append(lax.ppermute(piece, ('row', 'col'), pairs))  7.85 us
  transfers between devices with their start and end apart: 67, of which 47 were waited for; matrix products, arithmetic and copies ran while one was open for 8% of the time, Pallas kernels for 0%

profile of v13, /device:TPU:2, one launch (start us, length us, event | category | flops | bytes accessed | tf_op | source)
XLA Modules:
  0.0 229.1 jit_solution(4382823125218212139)
XLA Ops:
  0.7 1.6 copy.26
  3.4 5.8 %all-to-all-start = ((bf16[128,8,256]{2,0,1:T(8,128)(2,1)}), bf16[128,8,256]{2,0,1:T(8,128)(2,1)S(1)}, u32[]{:S(2)}, u32[]{:S(2)}) async-start(bf16[128,8,256]{2,0,1:T(8,128)(2,1)} %copy.28), calls=%async_computation | async-start | bytes 1048576 | tf_op jit(solution)/shard_map/all_to_all | solution.py:24
  18.3 5.4 %all-to-all-done = bf16[128,8,256]{2,0,1:T(8,128)(2,1)S(1)} async-done(((bf16[128,8,256]{2,0,1:T(8,128)(2,1)}), bf16[128,8,256]{2,0,1:T(8,128)(2,1)S(1)}, u32[]{:S(2)}, u32[]{:S(2)}) %all-to-all-start) | async-done | bytes 524320 | tf_op jit(solution)/shard_map/all_to_all | solution.py:24
  25.6 1.5 maximum_select_fusion.1
  27.1 1.5 gather_fusion.5
  29.0 1.5 collective-permute-start.15
  30.6 1.6 gather_fusion.4
  32.5 2.0 collective-permute-start.1
  35.1 1.8 fusion.15
  39.0 1.5 collective-permute-start.16
  40.7 2.0 collective-permute-start.2
  43.3 1.6 collective-permute-done.16
  44.9 1.4 collective-permute-done.23
  46.4 1.5 collective-permute-start.17
  48.4 1.7 collective-permute-start.3
  51.4 1.8 collective-permute-done.24
  53.4 1.3 collective-permute-start.18
  55.5 1.6 collective-permute-start.4
  58.5 2.8 %collective-permute-done.25 = bf16[128,512]{1,0:T(8,128)(2,1)S(1)} collective-permute-done((bf16[128,512]{1,0:T(8,128)(2,1)S(1)}, bf16[128,512]{1,0:T(8,128)(2,1)S(1)}, u32[]{:S(2)}, u32[]{:S(2)}) %collective-permute-start.25) | collective-permute-done | bytes 131104 | tf_op jit(solution)/shard_map/ppermute | solution.py:110
  61.4 1.2 collective-permute-start.19
  63.5 1.4 collective-permute-start.5
  65.6 1.8 collective-permute-done.19
  67.4 2.8 %collective-permute-done.26 = bf16[128,512]{1,0:T(8,128)(2,1)S(1)} collective-permute-done((bf16[128,512]{1,0:T(8,128)(2,1)S(1)}, bf16[128,512]{1,0:T(8,128)(2,1)S(1)}, u32[]{:S(2)}, u32[]{:S(2)}) %collective-permute-start.26) | collective-permute-done | bytes 131104 | tf_op jit(solution)/shard_map/ppermute | solution.py:110
  74.6 2.0 collective-permute-done.20
  76.6 2.4 %collective-permute-done.27 = bf16[128,512]{1,0:T(8,128)(2,1)S(1)} collective-permute-done((bf16[128,512]{1,0:T(8,128)(2,1)S(1)}, bf16[128,512]{1,0:T(8,128)(2,1)S(1)}, u32[]{:S(2)}, u32[]{:S(2)}) %collective-permute-start.27) | collective-permute-done | bytes 131104 | tf_op jit(solution)/shard_map/ppermute | solution.py:110
  79.2 1.2 collective-permute-start.21
  81.0 1.7 collective-permute-start.7
  84.2 1.4 collective-permute-done.28
  86.1 1.6 collective-permute-done.14
  87.8 2.5 %collective-permute-start.29 = (bf16[3,2048]{1,0:T(4,128)(2,1)S(1)}, bf16[3,2048]{1,0:T(4,128)(2,1)S(1)}, u32[]{:S(2)}, u32[]{:S(2)}) collective-permute-start(bf16[3,2048]{1,0:T(4,128)(2,1)S(1)} %pad_maximum_fusion.1), channel_id=1, source_target_pairs={{0,4},{4,8},{8,12},{12,16},{16,20},{20,24},{24,28},{1,5},{5,9},{9,... | collective-permute-start | bytes 36872 | tf_op jit(solution)/shard_map/ppermute | solution.py:13
  90.3 1.2 collective-permute-done.29
  92.8 8.8 %convolution_convert_fusion = bf16[128,4096]{1,0:T(8,128)(2,1)S(1)} fusion(bf16[2048,4096]{1,0:T(8,128)(2,1)} %param.25, bf16[128,2048]{1,0:T(8,128)(2,1)S(1)} %copy-done.16, f32[128,2048]{1,0:T(8,128)S(1)} %fusion.9), kind=kOutput, calls=%fused_computation.6 | convolution fusion | flops 2150891520 | bytes 19398656 | tf_op jit(solution)/shard_map/dot_general | solution.py:184
  101.7 1.9 collective-permute-done.30
  104.5 13.4 %collective-permute-done.31 = bf16[128,2048]{1,0:T(8,128)(2,1)S(1)} collective-permute-done((bf16[128,2048]{1,0:T(8,128)(2,1)S(1)}, bf16[128,2048]{1,0:T(8,128)(2,1)S(1)}, u32[]{:S(2)}, u32[]{:S(2)}) %collective-permute-start.31) | collective-permute-done | bytes 524320 | tf_op jit(solution)/shard_map/ppermute | solution.py:126
  121.1 3.2 %maximum_select_fusion = f32[128,4096]{1,0:T(8,128)} fusion(f32[128,2048]{1,0:T(8,128)S(1)} %convert_add_fusion.1, f32[128,2048]{1,0:T(8,128)} %collective-permute-done.32, pred[]{:T(512)S(6)} %eq.45), kind=kLoop, calls=%fused_computation.7 | loop fusion | flops 1572864 | bytes 4194305 | tf_op jit(solution)/shard_map/jit(_where)/select_n | solution.py:130
  124.3 14.7 %multiply_multiply_fusion.2 = (f32[128,2048]{1,0:T(8,128)}, f32[128,2048]{1,0:T(8,128)}, bf16[128,2048]{1,0:T(8,128)(2,1)}) fusion(f32[128]{0:T(128)S(1)} %get-tuple-element.107, f32[2048]{0:T(1024)S(1)} %bitcast.309, f32[128,2048]{1,0:T(8,128)} %copy-done.9, bf16[128,2048]{1,0:T(8,128)(2,1)} %param.23, bf16[2048,4096]{1,0:T(8,128)(2,1)} %param.25, ...), kind=kOutput, calls=%fused_computation.44 | convolution fusion | flops 2155872256 | bytes 24126464 | tf_op jit(solution)/shard_map/dot_general | solution.py:197
  139.0 1.5 multiply_multiply_fusion.1
  142.4 1.3 collective-permute-start.33
  145.6 3.1 %collective-permute-done.33 = f32[3,2048]{1,0:T(4,128)S(1)} collective-permute-done((f32[3,2048]{1,0:T(4,128)S(1)}, f32[3,2048]{1,0:T(4,128)S(1)}, u32[]{:S(2)}, u32[]{:S(2)}) %collective-permute-start.33) | collective-permute-done | bytes 24608 | tf_op jit(solution)/shard_map/ppermute | solution.py:13
  149.1 3.2 %collective-permute-start.55 = (bf16[128,512]{1,0:T(8,128)(2,1)S(1)}, bf16[128,512]{1,0:T(8,128)(2,1)S(1)}, u32[]{:S(2)}, u32[]{:S(2)}) collective-permute-start(bf16[128,512]{1,0:T(8,128)(2,1)S(1)} %get-tuple-element.87), channel_id=1, source_target_pairs={{8,0},{16,8},{24,16},{28,24},{20,28},{12,20},{4,12},{0,4},{9,1},{1... | collective-permute-start | bytes 393224 | tf_op jit(solution)/shard_map/ppermute | solution.py:77
  152.4 1.4 collective-permute-start.48
  155.1 2.3 collective-permute-done.55
  157.3 1.3 collective-permute-start.56
  158.7 1.5 collective-permute-done.48
  160.1 1.3 collective-permute-start.49
  162.2 1.8 collective-permute-start.35
  164.4 2.2 collective-permute-done.49
  166.6 1.3 collective-permute-start.50
  168.9 2.0 collective-permute-start.36
  171.2 1.9 collective-permute-done.50
  173.8 1.3 collective-permute-start.44
  175.2 1.3 collective-permute-done.36
  176.5 1.2 collective-permute-start.37
  181.5 1.5 collective-permute-done.37
  185.9 1.2 collective-permute-start.53
  188.6 1.6 collective-permute-start.39
  191.8 1.4 collective-permute-start.54
  201.6 1.9 collective-permute-done.62
  204.3 7.8 %collective-permute-done.63 = bf16[256,512]{1,0:T(8,128)(2,1)S(1)} collective-permute-done((bf16[256,512]{1,0:T(8,128)(2,1)S(1)}, bf16[256,512]{1,0:T(8,128)(2,1)S(1)}, u32[]{:S(2)}, u32[]{:S(2)}) %collective-permute-start.63) | collective-permute-done | bytes 262176 | tf_op jit(solution)/shard_map/ppermute | solution.py:145
  212.2 2.0 collective-permute-start.64
  214.2 4.4 %collective-permute-start.65 = (bf16[128,512]{1,0:T(8,128)(2,1)S(1)}, bf16[128,512]{1,0:T(8,128)(2,1)S(1)}, u32[]{:S(2)}, u32[]{:S(2)}) collective-permute-start(bf16[128,512]{1,0:T(8,128)(2,1)S(1)} %get-tuple-element.96), channel_id=1, source_target_pairs={{0,0},{1,8},{2,16},{3,24},{4,4},{5,12},{6,20},{7,28},{8,1},{9,9},{... | collective-permute-start | bytes 393224 | tf_op jit(solution)/shard_map/ppermute | solution.py:44
  218.7 1.8 dynamic-slice_convert_fusion
  220.5 5.2 %collective-permute-done.64 = bf16[128,512]{1,0:T(8,128)(2,1)S(1)} collective-permute-done((bf16[128,512]{1,0:T(8,128)(2,1)S(1)}, bf16[128,512]{1,0:T(8,128)(2,1)S(1)}, u32[]{:S(2)}, u32[]{:S(2)}) %collective-permute-start.64) | collective-permute-done | bytes 131104 | tf_op jit(solution)/shard_map/ppermute | solution.py:44
  225.7 2.7 %collective-permute-done.65 = bf16[128,512]{1,0:T(8,128)(2,1)S(1)} collective-permute-done((bf16[128,512]{1,0:T(8,128)(2,1)S(1)}, bf16[128,512]{1,0:T(8,128)(2,1)S(1)}, u32[]{:S(2)}, u32[]{:S(2)}) %collective-permute-start.65) | collective-permute-done | bytes 131104 | tf_op jit(solution)/shard_map/ppermute | solution.py:44
  (225 shorter events, 57.4 us)
Async XLA Ops:
  3.4 20.3 %all-to-all-start = ((bf16[128,8,256]{2,0,1:T(8,128)(2,1)}), bf16[128,8,256]{2,0,1:T(8,128)(2,1)S(1)}, u32[]{:S(2)}, u32[]{:S(2)}) async-start(bf16[128,8,256]{2,0,1:T(8,128)(2,1)} %copy.28), calls=%async_computation | async-start | bytes 1048576 | tf_op jit(solution)/shard_map/all_to_all | solution.py:24
  29.0 9.0 %collective-permute-start.15 = (bf16[128,512]{1,0:T(8,128)(2,1)S(1)}, bf16[128,512]{1,0:T(8,128)(2,1)S(1)}, u32[]{:S(2)}, u32[]{:S(2)}) collective-permute-start(bf16[128,512]{1,0:T(8,128)(2,1)S(1)} %get-tuple-element.100), channel_id=1, source_target_pairs={{8,0},{16,8},{24,16},{28,24},{20,28},{12,20},{4,12},{0,4},{9,1},{1... | collective-permute-start | bytes 393224 | tf_op jit(solution)/shard_map/ppermute | solution.py:110
  30.5 7.5 %collective-permute-start.22 = (bf16[128,512]{1,0:T(8,128)(2,1)S(1)}, bf16[128,512]{1,0:T(8,128)(2,1)}, u32[]{:S(2)}, u32[]{:S(2)}) collective-permute-start(bf16[128,512]{1,0:T(8,128)(2,1)S(1)} %get-tuple-element.101), channel_id=1, source_target_pairs={{8,0},{16,8},{24,16},{28,24},{20,28},{12,20},{4,12},{0,4},{9,1},{1... | collective-permute-start | bytes 393224 | tf_op jit(solution)/shard_map/ppermute | solution.py:110
  32.5 8.1 %collective-permute-start.1 = (bf16[128,512]{1,0:T(8,128)(2,1)S(1)}, bf16[128,512]{1,0:T(8,128)(2,1)S(1)}, u32[]{:S(2)}, u32[]{:S(2)}) collective-permute-start(bf16[128,512]{1,0:T(8,128)(2,1)S(1)} %get-tuple-element.98), channel_id=1, source_target_pairs={{0,8},{8,16},{16,24},{24,28},{28,20},{20,12},{12,4},{4,0},{1,9},{9... | collective-permute-start | bytes 393224 | tf_op jit(solution)/shard_map/ppermute | solution.py:110
  34.5 6.1 %collective-permute-start.8 = (bf16[128,512]{1,0:T(8,128)(2,1)S(1)}, bf16[128,512]{1,0:T(8,128)(2,1)S(1)}, u32[]{:S(2)}, u32[]{:S(2)}) collective-permute-start(bf16[128,512]{1,0:T(8,128)(2,1)S(1)} %get-tuple-element.99), channel_id=1, source_target_pairs={{0,8},{8,16},{16,24},{24,28},{28,20},{20,12},{12,4},{4,0},{1,9},{9... | collective-permute-start | bytes 393224 | tf_op jit(solution)/shard_map/ppermute | solution.py:110
  39.0 5.9 %collective-permute-start.16 = (bf16[128,512]{1,0:T(8,128)(2,1)S(1)}, bf16[128,512]{1,0:T(8,128)(2,1)S(1)}, u32[]{:S(2)}, u32[]{:S(2)}) collective-permute-start(bf16[128,512]{1,0:T(8,128)(2,1)S(1)} %get-tuple-element.81), channel_id=1, source_target_pairs={{8,0},{16,8},{24,16},{28,24},{20,28},{12,20},{4,12},{0,4},{9,1},{1... | collective-permute-start | bytes 393224 | tf_op jit(solution)/shard_map/ppermute | solution.py:110
  40.6 5.8 %collective-permute-start.23 = (bf16[128,512]{1,0:T(8,128)(2,1)S(1)}, bf16[128,512]{1,0:T(8,128)(2,1)S(1)}, u32[]{:S(2)}, u32[]{:S(2)}) collective-permute-start(bf16[128,512]{1,0:T(8,128)(2,1)S(1)} %get-tuple-element.82), channel_id=1, source_target_pairs={{8,0},{16,8},{24,16},{28,24},{20,28},{12,20},{4,12},{0,4},{9,1},{1... | collective-permute-start | bytes 393224 | tf_op jit(solution)/shard_map/ppermute | solution.py:110
  40.7 7.6 %collective-permute-start.2 = (bf16[128,512]{1,0:T(8,128)(2,1)S(1)}, bf16[128,512]{1,0:T(8,128)(2,1)S(1)}, u32[]{:S(2)}, u32[]{:S(2)}) collective-permute-start(bf16[128,512]{1,0:T(8,128)(2,1)S(1)} %get-tuple-element.67), channel_id=1, source_target_pairs={{0,8},{8,16},{16,24},{24,28},{28,20},{20,12},{12,4},{4,0},{1,9},{9... | collective-permute-start | bytes 393224 | tf_op jit(solution)/shard_map/ppermute | solution.py:110
  42.7 5.6 %collective-permute-start.9 = (bf16[128,512]{1,0:T(8,128)(2,1)S(1)}, bf16[128,512]{1,0:T(8,128)(2,1)S(1)}, u32[]{:S(2)}, u32[]{:S(2)}) collective-permute-start(bf16[128,512]{1,0:T(8,128)(2,1)S(1)} %get-tuple-element.68), channel_id=1, source_target_pairs={{0,8},{8,16},{16,24},{24,28},{28,20},{20,12},{12,4},{4,0},{1,9},{9... | collective-permute-start | bytes 393224 | tf_op jit(solution)/shard_map/ppermute | solution.py:110
  46.4 5.0 %collective-permute-start.17 = (bf16[128,512]{1,0:T(8,128)(2,1)S(1)}, bf16[128,512]{1,0:T(8,128)(2,1)S(1)}, u32[]{:S(2)}, u32[]{:S(2)}) collective-permute-start(bf16[128,512]{1,0:T(8,128)(2,1)S(1)} %get-tuple-element.79), channel_id=1, source_target_pairs={{8,0},{16,8},{24,16},{28,24},{20,28},{12,20},{4,12},{0,4},{9,1},{1... | collective-permute-start | bytes 393224 | tf_op jit(solution)/shard_map/ppermute | solution.py:110
  47.9 5.4 %collective-permute-start.24 = (bf16[128,512]{1,0:T(8,128)(2,1)S(1)}, bf16[128,512]{1,0:T(8,128)(2,1)S(1)}, u32[]{:S(2)}, u32[]{:S(2)}) collective-permute-start(bf16[128,512]{1,0:T(8,128)(2,1)S(1)} %get-tuple-element.80), channel_id=1, source_target_pairs={{8,0},{16,8},{24,16},{28,24},{20,28},{12,20},{4,12},{0,4},{9,1},{1... | collective-permute-start | bytes 393224 | tf_op jit(solution)/shard_map/ppermute | solution.py:110
  48.4 6.7 %collective-permute-start.3 = (bf16[128,512]{1,0:T(8,128)(2,1)S(1)}, bf16[128,512]{1,0:T(8,128)(2,1)S(1)}, u32[]{:S(2)}, u32[]{:S(2)}) collective-permute-start(bf16[128,512]{1,0:T(8,128)(2,1)S(1)} %get-tuple-element.65), channel_id=1, source_target_pairs={{0,8},{8,16},{16,24},{24,28},{28,20},{20,12},{12,4},{4,0},{1,9},{9... | collective-permute-start | bytes 393224 | tf_op jit(solution)/shard_map/ppermute | solution.py:110
  50.1 5.3 %collective-permute-start.10 = (bf16[128,512]{1,0:T(8,128)(2,1)S(1)}, bf16[128,512]{1,0:T(8,128)(2,1)S(1)}, u32[]{:S(2)}, u32[]{:S(2)}) collective-permute-start(bf16[128,512]{1,0:T(8,128)(2,1)S(1)} %get-tuple-element.66), channel_id=1, source_target_pairs={{0,8},{8,16},{16,24},{24,28},{28,20},{20,12},{12,4},{4,0},{1,9},{9... | collective-permute-start | bytes 393224 | tf_op jit(solution)/shard_map/ppermute | solution.py:110
  53.4 5.1 %collective-permute-start.18 = (bf16[128,512]{1,0:T(8,128)(2,1)S(1)}, bf16[128,512]{1,0:T(8,128)(2,1)S(1)}, u32[]{:S(2)}, u32[]{:S(2)}) collective-permute-start(bf16[128,512]{1,0:T(8,128)(2,1)S(1)} %get-tuple-element.77), channel_id=1, source_target_pairs={{8,0},{16,8},{24,16},{28,24},{20,28},{12,20},{4,12},{0,4},{9,1},{1... | collective-permute-start | bytes 393224 | tf_op jit(solution)/shard_map/ppermute | solution.py:110
  54.7 6.6 %collective-permute-start.25 = (bf16[128,512]{1,0:T(8,128)(2,1)S(1)}, bf16[128,512]{1,0:T(8,128)(2,1)S(1)}, u32[]{:S(2)}, u32[]{:S(2)}) collective-permute-start(bf16[128,512]{1,0:T(8,128)(2,1)S(1)} %get-tuple-element.78), channel_id=1, source_target_pairs={{8,0},{16,8},{24,16},{28,24},{20,28},{12,20},{4,12},{0,4},{9,1},{1... | collective-permute-start | bytes 393224 | tf_op jit(solution)/shard_map/ppermute | solution.py:110
  55.5 7.1 %collective-permute-start.4 = (bf16[128,512]{1,0:T(8,128)(2,1)S(1)}, bf16[128,512]{1,0:T(8,128)(2,1)S(1)}, u32[]{:S(2)}, u32[]{:S(2)}) collective-permute-start(bf16[128,512]{1,0:T(8,128)(2,1)S(1)} %get-tuple-element.63), channel_id=1, source_target_pairs={{0,8},{8,16},{16,24},{24,28},{28,20},{20,12},{12,4},{4,0},{1,9},{9... | collective-permute-start | bytes 393224 | tf_op jit(solution)/shard_map/ppermute | solution.py:110
  57.1 6.3 %collective-permute-start.11 = (bf16[128,512]{1,0:T(8,128)(2,1)S(1)}, bf16[128,512]{1,0:T(8,128)(2,1)S(1)}, u32[]{:S(2)}, u32[]{:S(2)}) collective-permute-start(bf16[128,512]{1,0:T(8,128)(2,1)S(1)} %get-tuple-element.64), channel_id=1, source_target_pairs={{0,8},{8,16},{16,24},{24,28},{28,20},{20,12},{12,4},{4,0},{1,9},{9... | collective-permute-start | bytes 393224 | tf_op jit(solution)/shard_map/ppermute | solution.py:110
  61.4 6.0 %collective-permute-start.19 = (bf16[128,512]{1,0:T(8,128)(2,1)S(1)}, bf16[128,512]{1,0:T(8,128)(2,1)S(1)}, u32[]{:S(2)}, u32[]{:S(2)}) collective-permute-start(bf16[128,512]{1,0:T(8,128)(2,1)S(1)} %get-tuple-element.75), channel_id=1, source_target_pairs={{8,0},{16,8},{24,16},{28,24},{20,28},{12,20},{4,12},{0,4},{9,1},{1... | collective-permute-start | bytes 393224 | tf_op jit(solution)/shard_map/ppermute | solution.py:110
  62.5 7.7 %collective-permute-start.26 = (bf16[128,512]{1,0:T(8,128)(2,1)S(1)}, bf16[128,512]{1,0:T(8,128)(2,1)S(1)}, u32[]{:S(2)}, u32[]{:S(2)}) collective-permute-start(bf16[128,512]{1,0:T(8,128)(2,1)S(1)} %get-tuple-element.76), channel_id=1, source_target_pairs={{8,0},{16,8},{24,16},{28,24},{20,28},{12,20},{4,12},{0,4},{9,1},{1... | collective-permute-start | bytes 393224 | tf_op jit(solution)/shard_map/ppermute | solution.py:110
  63.5 7.8 %collective-permute-start.5 = (bf16[128,512]{1,0:T(8,128)(2,1)S(1)}, bf16[128,512]{1,0:T(8,128)(2,1)S(1)}, u32[]{:S(2)}, u32[]{:S(2)}) collective-permute-start(bf16[128,512]{1,0:T(8,128)(2,1)S(1)} %get-tuple-element.61), channel_id=1, source_target_pairs={{0,8},{8,16},{16,24},{24,28},{28,20},{20,12},{12,4},{4,0},{1,9},{9... | collective-permute-start | bytes 393224 | tf_op jit(solution)/shard_map/ppermute | solution.py:110
  64.9 7.5 %collective-permute-start.12 = (bf16[128,512]{1,0:T(8,128)(2,1)S(1)}, bf16[128,512]{1,0:T(8,128)(2,1)S(1)}, u32[]{:S(2)}, u32[]{:S(2)}) collective-permute-start(bf16[128,512]{1,0:T(8,128)(2,1)S(1)} %get-tuple-element.62), channel_id=1, source_target_pairs={{0,8},{8,16},{16,24},{24,28},{28,20},{20,12},{12,4},{4,0},{1,9},{9... | collective-permute-start | bytes 393224 | tf_op jit(solution)/shard_map/ppermute | solution.py:110
  70.3 6.3 %collective-permute-start.20 = (bf16[128,512]{1,0:T(8,128)(2,1)S(1)}, bf16[128,512]{1,0:T(8,128)(2,1)S(1)}, u32[]{:S(2)}, u32[]{:S(2)}) collective-permute-start(bf16[128,512]{1,0:T(8,128)(2,1)S(1)} %get-tuple-element.73), channel_id=1, source_target_pairs={{8,0},{16,8},{24,16},{28,24},{20,28},{12,20},{4,12},{0,4},{9,1},{1... | collective-permute-start | bytes 393224 | tf_op jit(solution)/shard_map/ppermute | solution.py:110
  71.3 7.8 %collective-permute-start.27 = (bf16[128,512]{1,0:T(8,128)(2,1)S(1)}, bf16[128,512]{1,0:T(8,128)(2,1)S(1)}, u32[]{:S(2)}, u32[]{:S(2)}) collective-permute-start(bf16[128,512]{1,0:T(8,128)(2,1)S(1)} %get-tuple-element.74), channel_id=1, source_target_pairs={{8,0},{16,8},{24,16},{28,24},{20,28},{12,20},{4,12},{0,4},{9,1},{1... | collective-permute-start | bytes 393224 | tf_op jit(solution)/shard_map/ppermute | solution.py:110
  72.6 8.1 %collective-permute-start.6 = (bf16[128,512]{1,0:T(8,128)(2,1)S(1)}, bf16[128,512]{1,0:T(8,128)(2,1)S(1)}, u32[]{:S(2)}, u32[]{:S(2)}) collective-permute-start(bf16[128,512]{1,0:T(8,128)(2,1)S(1)} %get-tuple-element.59), channel_id=1, source_target_pairs={{0,8},{8,16},{16,24},{24,28},{28,20},{20,12},{12,4},{4,0},{1,9},{9... | collective-permute-start | bytes 393224 | tf_op jit(solution)/shard_map/ppermute | solution.py:110
  73.7 7.3 %collective-permute-start.13 = (bf16[128,512]{1,0:T(8,128)(2,1)S(1)}, bf16[128,512]{1,0:T(8,128)(2,1)S(1)}, u32[]{:S(2)}, u32[]{:S(2)}) collective-permute-start(bf16[128,512]{1,0:T(8,128)(2,1)S(1)} %get-tuple-element.60), channel_id=1, source_target_pairs={{0,8},{8,16},{16,24},{24,28},{28,20},{20,12},{12,4},{4,0},{1,9},{9... | collective-permute-start | bytes 393224 | tf_op jit(solution)/shard_map/ppermute | solution.py:110
  79.2 5.0 %collective-permute-start.21 = (bf16[128,512]{1,0:T(8,128)(2,1)S(1)}, bf16[128,512]{1,0:T(8,128)(2,1)S(1)}, u32[]{:S(2)}, u32[]{:S(2)}) collective-permute-start(bf16[128,512]{1,0:T(8,128)(2,1)S(1)} %get-tuple-element.71), channel_id=1, source_target_pairs={{8,0},{16,8},{24,16},{28,24},{20,28},{12,20},{4,12},{0,4},{9,1},{1... | collective-permute-start | bytes 393224 | tf_op jit(solution)/shard_map/ppermute | solution.py:110
  80.4 5.2 %collective-permute-start.28 = (bf16[128,512]{1,0:T(8,128)(2,1)S(1)}, bf16[128,512]{1,0:T(8,128)(2,1)S(1)}, u32[]{:S(2)}, u32[]{:S(2)}) collective-permute-start(bf16[128,512]{1,0:T(8,128)(2,1)S(1)} %get-tuple-element.72), channel_id=1, source_target_pairs={{8,0},{16,8},{24,16},{28,24},{20,28},{12,20},{4,12},{0,4},{9,1},{1... | collective-permute-start | bytes 393224 | tf_op jit(solution)/shard_map/ppermute | solution.py:110
  81.0 5.0 %collective-permute-start.7 = (bf16[128,512]{1,0:T(8,128)(2,1)S(1)}, bf16[128,512]{1,0:T(8,128)(2,1)S(1)}, u32[]{:S(2)}, u32[]{:S(2)}) collective-permute-start(bf16[128,512]{1,0:T(8,128)(2,1)S(1)} %get-tuple-element.57), channel_id=1, source_target_pairs={{0,8},{8,16},{16,24},{24,28},{28,20},{20,12},{12,4},{4,0},{1,9},{9... | collective-permute-start | bytes 393224 | tf_op jit(solution)/shard_map/ppermute | solution.py:110
  82.7 5.0 %collective-permute-start.14 = (bf16[128,512]{1,0:T(8,128)(2,1)S(1)}, bf16[128,512]{1,0:T(8,128)(2,1)S(1)}, u32[]{:S(2)}, u32[]{:S(2)}) collective-permute-start(bf16[128,512]{1,0:T(8,128)(2,1)S(1)} %get-tuple-element.58), channel_id=1, source_target_pairs={{0,8},{8,16},{16,24},{24,28},{28,20},{20,12},{12,4},{4,0},{1,9},{9... | collective-permute-start | bytes 393224 | tf_op jit(solution)/shard_map/ppermute | solution.py:110
  87.8 3.7 %collective-permute-start.29 = (bf16[3,2048]{1,0:T(4,128)(2,1)S(1)}, bf16[3,2048]{1,0:T(4,128)(2,1)S(1)}, u32[]{:S(2)}, u32[]{:S(2)}) collective-permute-start(bf16[3,2048]{1,0:T(4,128)(2,1)S(1)} %pad_maximum_fusion.1), channel_id=1, source_target_pairs={{0,4},{4,8},{8,12},{12,16},{16,20},{20,24},{24,28},{1,5},{5,9},{9,... | collective-permute-start | bytes 36872 | tf_op jit(solution)/shard_map/ppermute | solution.py:13
  103.9 14.0 %collective-permute-start.31 = (bf16[128,2048]{1,0:T(8,128)(2,1)S(1)}, bf16[128,2048]{1,0:T(8,128)(2,1)S(1)}, u32[]{:S(2)}, u32[]{:S(2)}) collective-permute-start(bf16[128,2048]{1,0:T(8,128)(2,1)S(1)} %fusion.21), channel_id=1, source_target_pairs={{0,2},{1,3},{2,0},{3,1},{4,6},{5,7},{6,4},{7,5},{8,10},{9,11},{10,... | collective-permute-start | bytes 1572872 | tf_op jit(solution)/shard_map/ppermute | solution.py:126
  118.3 2.9 %collective-permute-start.32 = (f32[128,2048]{1,0:T(8,128)S(1)}, f32[128,2048]{1,0:T(8,128)}, u32[]{:S(2)}, u32[]{:S(2)}) collective-permute-start(f32[128,2048]{1,0:T(8,128)S(1)} %convert_add_fusion.1), channel_id=1, source_target_pairs={{0,1},{1,0},{2,3},{3,2},{4,5},{5,4},{6,7},{7,6},{8,9},{9,8},{10,11... | collective-permute-start | bytes 3145736 | tf_op jit(solution)/shard_map/ppermute | solution.py:129
  142.4 6.3 %collective-permute-start.33 = (f32[3,2048]{1,0:T(4,128)S(1)}, f32[3,2048]{1,0:T(4,128)S(1)}, u32[]{:S(2)}, u32[]{:S(2)}) collective-permute-start(f32[3,2048]{1,0:T(4,128)S(1)} %slice_add_fusion), channel_id=1, source_target_pairs={{4,0},{8,4},{12,8},{16,12},{20,16},{24,20},{28,24},{5,1},{9,5},{13... | collective-permute-start | bytes 73736 | tf_op jit(solution)/shard_map/ppermute | solution.py:13
  149.1 8.2 %collective-permute-start.55 = (bf16[128,512]{1,0:T(8,128)(2,1)S(1)}, bf16[128,512]{1,0:T(8,128)(2,1)S(1)}, u32[]{:S(2)}, u32[]{:S(2)}) collective-permute-start(bf16[128,512]{1,0:T(8,128)(2,1)S(1)} %get-tuple-element.87), channel_id=1, source_target_pairs={{8,0},{16,8},{24,16},{28,24},{20,28},{12,20},{4,12},{0,4},{9,1},{1... | collective-permute-start | bytes 393224 | tf_op jit(solution)/shard_map/ppermute | solution.py:77
  152.4 7.8 %collective-permute-start.48 = (bf16[128,512]{1,0:T(8,128)(2,1)S(1)}, bf16[128,512]{1,0:T(8,128)(2,1)S(1)}, u32[]{:S(2)}, u32[]{:S(2)}) collective-permute-start(bf16[128,512]{1,0:T(8,128)(2,1)S(1)} %get-tuple-element.88), channel_id=1, source_target_pairs={{8,0},{16,8},{24,16},{28,24},{20,28},{12,20},{4,12},{0,4},{9,1},{1... | collective-permute-start | bytes 393224 | tf_op jit(solution)/shard_map/ppermute | solution.py:77
  153.8 7.7 %collective-permute-start.41 = (bf16[128,512]{1,0:T(8,128)(2,1)S(1)}, bf16[128,512]{1,0:T(8,128)(2,1)S(1)}, u32[]{:S(2)}, u32[]{:S(2)}) collective-permute-start(bf16[128,512]{1,0:T(8,128)(2,1)S(1)} %get-tuple-element.89), channel_id=1, source_target_pairs={{0,8},{8,16},{16,24},{24,28},{28,20},{20,12},{12,4},{4,0},{1,9},{9... | collective-permute-start | bytes 393224 | tf_op jit(solution)/shard_map/ppermute | solution.py:77
  154.4 7.8 %collective-permute-start.34 = (bf16[128,512]{1,0:T(8,128)(2,1)S(1)}, bf16[128,512]{1,0:T(8,128)(2,1)S(1)}, u32[]{:S(2)}, u32[]{:S(2)}) collective-permute-start(bf16[128,512]{1,0:T(8,128)(2,1)S(1)} %get-tuple-element.86), channel_id=1, source_target_pairs={{0,8},{8,16},{16,24},{24,28},{28,20},{20,12},{12,4},{4,0},{1,9},{9... | collective-permute-start | bytes 393224 | tf_op jit(solution)/shard_map/ppermute | solution.py:77
  157.3 6.7 %collective-permute-start.56 = (bf16[128,512]{1,0:T(8,128)(2,1)S(1)}, bf16[128,512]{1,0:T(8,128)(2,1)S(1)}, u32[]{:S(2)}, u32[]{:S(2)}) collective-permute-start(bf16[128,512]{1,0:T(8,128)(2,1)S(1)} %collective-permute-done.55), channel_id=1, source_target_pairs={{8,0},{16,8},{24,16},{28,24},{20,28},{12,20},{4,12},{0,4},{9,1},{1... | collective-permute-start | bytes 393224 | tf_op jit(solution)/shard_map/ppermute | solution.py:77
  160.1 6.4 %collective-permute-start.49 = (bf16[128,512]{1,0:T(8,128)(2,1)S(1)}, bf16[128,512]{1,0:T(8,128)(2,1)S(1)}, u32[]{:S(2)}, u32[]{:S(2)}) collective-permute-start(bf16[128,512]{1,0:T(8,128)(2,1)S(1)} %collective-permute-done.48), channel_id=1, source_target_pairs={{8,0},{16,8},{24,16},{28,24},{20,28},{12,20},{4,12},{0,4},{9,1},{1... | collective-permute-start | bytes 393224 | tf_op jit(solution)/shard_map/ppermute | solution.py:77
  161.5 6.3 %collective-permute-start.42 = (bf16[128,512]{1,0:T(8,128)(2,1)S(1)}, bf16[128,512]{1,0:T(8,128)(2,1)S(1)}, u32[]{:S(2)}, u32[]{:S(2)}) collective-permute-start(bf16[128,512]{1,0:T(8,128)(2,1)S(1)} %collective-permute-done.41), channel_id=1, source_target_pairs={{0,8},{8,16},{16,24},{24,28},{28,20},{20,12},{12,4},{4,0},{1,9},{9... | collective-permute-start | bytes 393224 | tf_op jit(solution)/shard_map/ppermute | solution.py:77
  162.2 6.7 %collective-permute-start.35 = (bf16[128,512]{1,0:T(8,128)(2,1)S(1)}, bf16[128,512]{1,0:T(8,128)(2,1)S(1)}, u32[]{:S(2)}, u32[]{:S(2)}) collective-permute-start(bf16[128,512]{1,0:T(8,128)(2,1)S(1)} %collective-permute-done.34), channel_id=1, source_target_pairs={{0,8},{8,16},{16,24},{24,28},{28,20},{20,12},{12,4},{4,0},{1,9},{9... | collective-permute-start | bytes 393224 | tf_op jit(solution)/shard_map/ppermute | solution.py:77
  164.0 6.8 %collective-permute-start.57 = (bf16[128,512]{1,0:T(8,128)(2,1)S(1)}, bf16[128,512]{1,0:T(8,128)(2,1)S(1)}, u32[]{:S(2)}, u32[]{:S(2)}) collective-permute-start(bf16[128,512]{1,0:T(8,128)(2,1)S(1)} %collective-permute-done.56), channel_id=1, source_target_pairs={{8,0},{16,8},{24,16},{28,24},{20,28},{12,20},{4,12},{0,4},{9,1},{1... | collective-permute-start | bytes 393224 | tf_op jit(solution)/shard_map/ppermute | solution.py:77
  166.6 6.6 %collective-permute-start.50 = (bf16[128,512]{1,0:T(8,128)(2,1)S(1)}, bf16[128,512]{1,0:T(8,128)(2,1)S(1)}, u32[]{:S(2)}, u32[]{:S(2)}) collective-permute-start(bf16[128,512]{1,0:T(8,128)(2,1)S(1)} %collective-permute-done.49), channel_id=1, source_target_pairs={{8,0},{16,8},{24,16},{28,24},{20,28},{12,20},{4,12},{0,4},{9,1},{1... | collective-permute-start | bytes 393224 | tf_op jit(solution)/shard_map/ppermute | solution.py:77
  167.8 6.0 %collective-permute-start.43 = (bf16[128,512]{1,0:T(8,128)(2,1)S(1)}, bf16[128,512]{1,0:T(8,128)(2,1)S(1)}, u32[]{:S(2)}, u32[]{:S(2)}) collective-permute-start(bf16[128,512]{1,0:T(8,128)(2,1)S(1)} %collective-permute-done.42), channel_id=1, source_target_pairs={{0,8},{8,16},{16,24},{24,28},{28,20},{20,12},{12,4},{4,0},{1,9},{9... | collective-permute-start | bytes 393224 | tf_op jit(solution)/shard_map/ppermute | solution.py:77
  168.9 7.6 %collective-permute-start.36 = (bf16[128,512]{1,0:T(8,128)(2,1)S(1)}, bf16[128,512]{1,0:T(8,128)(2,1)S(1)}, u32[]{:S(2)}, u32[]{:S(2)}) collective-permute-start(bf16[128,512]{1,0:T(8,128)(2,1)S(1)} %collective-permute-done.35), channel_id=1, source_target_pairs={{0,8},{8,16},{16,24},{24,28},{28,20},{20,12},{12,4},{4,0},{1,9},{9... | collective-permute-start | bytes 393224 | tf_op jit(solution)/shard_map/ppermute | solution.py:77
  170.8 6.8 %collective-permute-start.58 = (bf16[128,512]{1,0:T(8,128)(2,1)S(1)}, bf16[128,512]{1,0:T(8,128)(2,1)S(1)}, u32[]{:S(2)}, u32[]{:S(2)}) collective-permute-start(bf16[128,512]{1,0:T(8,128)(2,1)S(1)} %collective-permute-done.57), channel_id=1, source_target_pairs={{8,0},{16,8},{24,16},{28,24},{20,28},{12,20},{4,12},{0,4},{9,1},{1... | collective-permute-start | bytes 393224 | tf_op jit(solution)/shard_map/ppermute | solution.py:77
  173.1 6.4 %collective-permute-start.51 = (bf16[128,512]{1,0:T(8,128)(2,1)S(1)}, bf16[128,512]{1,0:T(8,128)(2,1)S(1)}, u32[]{:S(2)}, u32[]{:S(2)}) collective-permute-start(bf16[128,512]{1,0:T(8,128)(2,1)S(1)} %collective-permute-done.50), channel_id=1, source_target_pairs={{8,0},{16,8},{24,16},{28,24},{20,28},{12,20},{4,12},{0,4},{9,1},{1... | collective-permute-start | bytes 393224 | tf_op jit(solution)/shard_map/ppermute | solution.py:77
  173.8 6.6 %collective-permute-start.44 = (bf16[128,512]{1,0:T(8,128)(2,1)S(1)}, bf16[128,512]{1,0:T(8,128)(2,1)S(1)}, u32[]{:S(2)}, u32[]{:S(2)}) collective-permute-start(bf16[128,512]{1,0:T(8,128)(2,1)S(1)} %collective-permute-done.43), channel_id=1, source_target_pairs={{0,8},{8,16},{16,24},{24,28},{28,20},{20,12},{12,4},{4,0},{1,9},{9... | collective-permute-start | bytes 393224 | tf_op jit(solution)/shard_map/ppermute | solution.py:77
  176.5 6.5 %collective-permute-start.37 = (bf16[128,512]{1,0:T(8,128)(2,1)S(1)}, bf16[128,512]{1,0:T(8,128)(2,1)S(1)}, u32[]{:S(2)}, u32[]{:S(2)}) collective-permute-start(bf16[128,512]{1,0:T(8,128)(2,1)S(1)} %collective-permute-done.36), channel_id=1, source_target_pairs={{0,8},{8,16},{16,24},{24,28},{28,20},{20,12},{12,4},{4,0},{1,9},{9... | collective-permute-start | bytes 393224 | tf_op jit(solution)/shard_map/ppermute | solution.py:77
  177.7 6.4 %collective-permute-start.59 = (bf16[128,512]{1,0:T(8,128)(2,1)S(1)}, bf16[128,512]{1,0:T(8,128)(2,1)S(1)}, u32[]{:S(2)}, u32[]{:S(2)}) collective-permute-start(bf16[128,512]{1,0:T(8,128)(2,1)S(1)} %collective-permute-done.58), channel_id=1, source_target_pairs={{8,0},{16,8},{24,16},{28,24},{20,28},{12,20},{4,12},{0,4},{9,1},{1... | collective-permute-start | bytes 393224 | tf_op jit(solution)/shard_map/ppermute | solution.py:77
  179.5 6.4 %collective-permute-start.52 = (bf16[128,512]{1,0:T(8,128)(2,1)S(1)}, bf16[128,512]{1,0:T(8,128)(2,1)S(1)}, u32[]{:S(2)}, u32[]{:S(2)}) collective-permute-start(bf16[128,512]{1,0:T(8,128)(2,1)S(1)} %collective-permute-done.51), channel_id=1, source_target_pairs={{8,0},{16,8},{24,16},{28,24},{20,28},{12,20},{4,12},{0,4},{9,1},{1... | collective-permute-start | bytes 393224 | tf_op jit(solution)/shard_map/ppermute | solution.py:77
  180.4 6.7 %collective-permute-start.45 = (bf16[128,512]{1,0:T(8,128)(2,1)S(1)}, bf16[128,512]{1,0:T(8,128)(2,1)S(1)}, u32[]{:S(2)}, u32[]{:S(2)}) collective-permute-start(bf16[128,512]{1,0:T(8,128)(2,1)S(1)} %collective-permute-done.44), channel_id=1, source_target_pairs={{0,8},{8,16},{16,24},{24,28},{28,20},{20,12},{12,4},{4,0},{1,9},{9... | collective-permute-start | bytes 393224 | tf_op jit(solution)/shard_map/ppermute | solution.py:77
  183.0 5.6 %collective-permute-start.38 = (bf16[128,512]{1,0:T(8,128)(2,1)S(1)}, bf16[128,512]{1,0:T(8,128)(2,1)S(1)}, u32[]{:S(2)}, u32[]{:S(2)}) collective-permute-start(bf16[128,512]{1,0:T(8,128)(2,1)S(1)} %collective-permute-done.37), channel_id=1, source_target_pairs={{0,8},{8,16},{16,24},{24,28},{28,20},{20,12},{12,4},{4,0},{1,9},{9... | collective-permute-start | bytes 393224 | tf_op jit(solution)/shard_map/ppermute | solution.py:77
  184.1 6.3 %collective-permute-start.60 = (bf16[128,512]{1,0:T(8,128)(2,1)S(1)}, bf16[128,512]{1,0:T(8,128)(2,1)S(1)}, u32[]{:S(2)}, u32[]{:S(2)}) collective-permute-start(bf16[128,512]{1,0:T(8,128)(2,1)S(1)} %collective-permute-done.59), channel_id=1, source_target_pairs={{8,0},{16,8},{24,16},{28,24},{20,28},{12,20},{4,12},{0,4},{9,1},{1... | collective-permute-start | bytes 393224 | tf_op jit(solution)/shard_map/ppermute | solution.py:77
  185.9 5.9 %collective-permute-start.53 = (bf16[128,512]{1,0:T(8,128)(2,1)S(1)}, bf16[128,512]{1,0:T(8,128)(2,1)S(1)}, u32[]{:S(2)}, u32[]{:S(2)}) collective-permute-start(bf16[128,512]{1,0:T(8,128)(2,1)S(1)} %collective-permute-done.52), channel_id=1, source_target_pairs={{8,0},{16,8},{24,16},{28,24},{20,28},{12,20},{4,12},{0,4},{9,1},{1... | collective-permute-start | bytes 393224 | tf_op jit(solution)/shard_map/ppermute | solution.py:77
  187.1 6.3 %collective-permute-start.46 = (bf16[128,512]{1,0:T(8,128)(2,1)S(1)}, bf16[128,512]{1,0:T(8,128)(2,1)S(1)}, u32[]{:S(2)}, u32[]{:S(2)}) collective-permute-start(bf16[128,512]{1,0:T(8,128)(2,1)S(1)} %collective-permute-done.45), channel_id=1, source_target_pairs={{0,8},{8,16},{16,24},{24,28},{28,20},{20,12},{12,4},{4,0},{1,9},{9... | collective-permute-start | bytes 393224 | tf_op jit(solution)/shard_map/ppermute | solution.py:77
  188.6 6.2 %collective-permute-start.39 = (bf16[128,512]{1,0:T(8,128)(2,1)S(1)}, bf16[128,512]{1,0:T(8,128)(2,1)S(1)}, u32[]{:S(2)}, u32[]{:S(2)}) collective-permute-start(bf16[128,512]{1,0:T(8,128)(2,1)S(1)} %collective-permute-done.38), channel_id=1, source_target_pairs={{0,8},{8,16},{16,24},{24,28},{28,20},{20,12},{12,4},{4,0},{1,9},{9... | collective-permute-start | bytes 393224 | tf_op jit(solution)/shard_map/ppermute | solution.py:77
  190.4 5.3 %collective-permute-start.61 = (bf16[128,512]{1,0:T(8,128)(2,1)S(1)}, bf16[128,512]{1,0:T(8,128)(2,1)S(1)}, u32[]{:S(2)}, u32[]{:S(2)}) collective-permute-start(bf16[128,512]{1,0:T(8,128)(2,1)S(1)} %collective-permute-done.60), channel_id=1, source_target_pairs={{8,0},{16,8},{24,16},{28,24},{20,28},{12,20},{4,12},{0,4},{9,1},{1... | collective-permute-start | bytes 393224 | tf_op jit(solution)/shard_map/ppermute | solution.py:77
  191.8 5.0 %collective-permute-start.54 = (bf16[128,512]{1,0:T(8,128)(2,1)S(1)}, bf16[128,512]{1,0:T(8,128)(2,1)S(1)}, u32[]{:S(2)}, u32[]{:S(2)}) collective-permute-start(bf16[128,512]{1,0:T(8,128)(2,1)S(1)} %collective-permute-done.53), channel_id=1, source_target_pairs={{8,0},{16,8},{24,16},{28,24},{20,28},{12,20},{4,12},{0,4},{9,1},{1... | collective-permute-start | bytes 393224 | tf_op jit(solution)/shard_map/ppermute | solution.py:77
  193.4 5.0 %collective-permute-start.47 = (bf16[128,512]{1,0:T(8,128)(2,1)S(1)}, bf16[128,512]{1,0:T(8,128)(2,1)S(1)}, u32[]{:S(2)}, u32[]{:S(2)}) collective-permute-start(bf16[128,512]{1,0:T(8,128)(2,1)S(1)} %collective-permute-done.46), channel_id=1, source_target_pairs={{0,8},{8,16},{16,24},{24,28},{28,20},{20,12},{12,4},{4,0},{1,9},{9... | collective-permute-start | bytes 393224 | tf_op jit(solution)/shard_map/ppermute | solution.py:77
  194.8 5.0 %collective-permute-start.40 = (bf16[128,512]{1,0:T(8,128)(2,1)S(1)}, bf16[128,512]{1,0:T(8,128)(2,1)S(1)}, u32[]{:S(2)}, u32[]{:S(2)}) collective-permute-start(bf16[128,512]{1,0:T(8,128)(2,1)S(1)} %collective-permute-done.39), channel_id=1, source_target_pairs={{0,8},{8,16},{16,24},{24,28},{28,20},{20,12},{12,4},{4,0},{1,9},{9... | collective-permute-start | bytes 393224 | tf_op jit(solution)/shard_map/ppermute | solution.py:77
  203.7 8.4 %collective-permute-start.63 = (bf16[256,512]{1,0:T(8,128)(2,1)S(1)}, bf16[256,512]{1,0:T(8,128)(2,1)S(1)}, u32[]{:S(2)}, u32[]{:S(2)}) collective-permute-start(bf16[256,512]{1,0:T(8,128)(2,1)S(1)} %bitcast_convert_fusion), channel_id=1, source_target_pairs={{0,2},{1,3},{2,0},{3,1},{4,6},{5,7},{6,4},{7,5},{8,10},{9,11},{10,... | collective-permute-start | bytes 786440 | tf_op jit(solution)/shard_map/ppermute | solution.py:145
  212.2 13.4 %collective-permute-start.64 = (bf16[128,512]{1,0:T(8,128)(2,1)S(1)}, bf16[128,512]{1,0:T(8,128)(2,1)S(1)}, u32[]{:S(2)}, u32[]{:S(2)}) collective-permute-start(bf16[128,512]{1,0:T(8,128)(2,1)S(1)} %get-tuple-element.97), channel_id=1, source_target_pairs={{0,4},{1,12},{2,20},{3,28},{4,0},{5,8},{6,16},{7,24},{8,5},{9,13},... | collective-permute-start | bytes 393224 | tf_op jit(solution)/shard_map/ppermute | solution.py:44
  214.2 14.1 %collective-permute-start.65 = (bf16[128,512]{1,0:T(8,128)(2,1)S(1)}, bf16[128,512]{1,0:T(8,128)(2,1)S(1)}, u32[]{:S(2)}, u32[]{:S(2)}) collective-permute-start(bf16[128,512]{1,0:T(8,128)(2,1)S(1)} %get-tuple-element.96), channel_id=1, source_target_pairs={{0,0},{1,8},{2,16},{3,24},{4,4},{5,12},{6,20},{7,28},{8,1},{9,9},{... | collective-permute-start | bytes 393224 | tf_op jit(solution)/shard_map/ppermute | solution.py:44
  (23 other events, 153.1 us)

commit v14 on v13

--- a/solution.py
+++ b/solution.py
@@ -50,6 +50,32 @@
             piece = jnp.where(want == m, got[m], piece)
         pieces.append(piece)
     return jnp.concatenate(pieces, axis=1)
+
+def placed_sums(grad_cols, row_count):
+    n_row, n_col = lax.axis_size("row"), lax.axis_size("col")
+    row, col = lax.axis_index("row"), lax.axis_index("col")
+    core, chip = col % 2, col // 2
+    quarters = grad_cols.reshape(2, 2, grad_cols.shape[0] // 4, grad_cols.shape[1])
+    keep = jnp.take(quarters, core, axis=1)
+    give = jnp.take(quarters, 1 - core, axis=1)
+    got = lax.ppermute(give, "col", [(c, c ^ 1) for c in range(n_col)])
+    pair = (keep.astype(jnp.float32) + got.astype(jnp.float32)).astype(jnp.bfloat16)
+    pieces = pair.reshape(2, 2, row_count, grad_cols.shape[1])
+    arrived = {}
+    for a in range(2):
+        for b in range(2):
+            pairs = [
+                (r * n_col + c, (2 * (((c // 2) ^ b) * 2 + c % 2) + ((r % 2) ^ a)) * n_col + r // 2)
+                for r in range(n_row)
+                for c in range(n_col)
+            ]
+            piece = jnp.take(jnp.take(pieces, chip ^ b, axis=0), (row % 2) ^ a, axis=0)
+            arrived[a, b] = lax.ppermute(piece, ("row", "col"), pairs).astype(jnp.float32)
+    sums = [arrived[a, 0] + arrived[a, 1] for a in range(2)]
+    return jnp.concatenate(
+        [jnp.where((row % 2) ^ j == 0, sums[0], sums[1]).astype(jnp.bfloat16) for j in range(2)], axis=1
+    )
+
 
 def ring_order(count):
     if count % 2:
@@ -233,11 +259,11 @@
             )
         grad_cols = jnp.take(grad_cols.astype(jnp.bfloat16), jnp.argsort(sources), axis=0)
         grad_cols = grad_cols.reshape(-1, grad_cols.shape[2])
-        if lax.axis_size("col") == 4:
-            grad_sum = col_psum_scatter(grad_cols)
+        if lax.axis_size("col") == 4 and lax.axis_size("row") == 8:
+            grad_tokens = placed_sums(grad_cols, row_count)
         else:
             grad_sum = lax.psum_scatter(grad_cols, "col", scatter_dimension=0, tiled=True)
-        grad_tokens = placed_blocks(grad_sum, row_count)
+            grad_tokens = placed_blocks(grad_sum, row_count)
     else:
         partial_grad = lax.dot_general(
             grad_x, full_in, (((1,), (1,)), ((), ())), preferred_element_type=jnp.float32

time: 230 us -> 224 us (0.974)
  waiting for transfers between devices: 85.9 us -> 80.8 us
    ppermute x4 -> x5, waiting for transfers between devices: 17.5 us -> 11.8 us  [the longest x4 10 us: placed_sums(): lax.ppermute(piece, ('row', 'col'), pairs).astype(jnp.float32)]
    ppermute x4 -> x5, starting transfers between devices: 7.08 us -> 7.18 us  [the longest x4 7.11 us: placed_sums(): lax.ppermute(piece, ('row', 'col'), pairs).astype(jnp.float32)]
  transfers between devices with their start and end apart: 67 -> 68, of which waited for: 47 -> 48; matrix products, arithmetic and copies ran while one was open for 8% -> 8% of each run, Pallas kernels for 0% -> 0%
where the time goes in v14:
time: 224 us
  waiting for transfers between devices  80.8 us (36%)
  starting transfers between devices  75.1 us (34%)
  matrix products  30 us (13%)
  local copies, waits for them, and re-layouts  16.4 us (7%)
  other arithmetic  14.4 us (6%)
  between operations  6.8 us (3%)
    ppermute x28, starting transfers between devices, ring_gather(): part = lax.ppermute(part, axis, pairs)  30.7 us
    ppermute x28, starting transfers between devices, ring_reduce_scatter(): total = lax.ppermute(total, axis, pairs)  26.9 us
    ppermute x28, waiting for transfers between devices, ring_reduce_scatter(): total = lax.ppermute(total, axis, pairs)  24.9 us
    ppermute x28, waiting for transfers between devices, ring_gather(): part = lax.ppermute(part, axis, pairs)  17.3 us
    dot_general x1, matrix products, shards(): lax.dot_general(residual_grad, out_weight, (((1,), (1,)), ((), ())), pref...  14.7 us
    ppermute x1, waiting for transfers between devices, col_psum(): lax.ppermute(pair.astype(jnp.bfloat16), 'col', [(c, c ^ 2) for c in range...  13.4 us
    ppermute x4, waiting for transfers between devices, placed_sums(): lax.ppermute(piece, ('row', 'col'), pairs).astype(jnp.float32)  10 us
    dot_general x1, matrix products, shards(): jnp.dot(mixed, out_weight, preferred_element_type=jnp.float32)  8.81 us
  transfers between devices with their start and end apart: 68, of which 48 were waited for; matrix products, arithmetic and copies ran while one was open for 8% of the time, Pallas kernels for 0%

profile of v14, /device:TPU:2, one launch (start us, length us, event | category | flops | bytes accessed | tf_op | source)
XLA Modules:
  0.0 223.5 jit_solution(376132395394569589)
XLA Ops:
  0.7 1.6 copy.23
  3.4 5.8 %all-to-all-start = ((bf16[128,8,256]{2,0,1:T(8,128)(2,1)}), bf16[128,8,256]{2,0,1:T(8,128)(2,1)S(1)}, u32[]{:S(2)}, u32[]{:S(2)}) async-start(bf16[128,8,256]{2,0,1:T(8,128)(2,1)} %copy.25), calls=%async_computation | async-start | bytes 1048576 | tf_op jit(solution)/shard_map/all_to_all | solution.py:24
  18.2 5.6 %all-to-all-done = bf16[128,8,256]{2,0,1:T(8,128)(2,1)S(1)} async-done(((bf16[128,8,256]{2,0,1:T(8,128)(2,1)}), bf16[128,8,256]{2,0,1:T(8,128)(2,1)S(1)}, u32[]{:S(2)}, u32[]{:S(2)}) %all-to-all-start) | async-done | bytes 524320 | tf_op jit(solution)/shard_map/all_to_all | solution.py:24
  24.5 1.2 collective-permute-done
  25.6 1.5 maximum_select_fusion.1
  27.1 1.5 gather_fusion.5
  29.0 1.5 collective-permute-start.15
  30.6 1.6 gather_fusion.4
  32.5 2.0 collective-permute-start.1
  35.1 1.7 fusion.15
  39.0 1.5 collective-permute-start.16
  40.7 2.0 collective-permute-start.2
  43.3 1.6 collective-permute-done.16
  44.9 1.4 collective-permute-done.23
  46.4 1.5 collective-permute-start.17
  48.4 1.7 collective-permute-start.3
  51.4 1.8 collective-permute-done.24
  53.3 1.3 collective-permute-start.18
  55.4 1.7 collective-permute-start.4
  58.4 2.8 %collective-permute-done.25 = bf16[128,512]{1,0:T(8,128)(2,1)S(1)} collective-permute-done((bf16[128,512]{1,0:T(8,128)(2,1)S(1)}, bf16[128,512]{1,0:T(8,128)(2,1)S(1)}, u32[]{:S(2)}, u32[]{:S(2)}) %collective-permute-start.25) | collective-permute-done | bytes 131104 | tf_op jit(solution)/shard_map/ppermute | solution.py:136
  61.3 1.2 collective-permute-start.19
  63.5 1.4 collective-permute-start.5
  65.6 1.8 collective-permute-done.19
  67.4 2.8 %collective-permute-done.26 = bf16[128,512]{1,0:T(8,128)(2,1)S(1)} collective-permute-done((bf16[128,512]{1,0:T(8,128)(2,1)S(1)}, bf16[128,512]{1,0:T(8,128)(2,1)S(1)}, u32[]{:S(2)}, u32[]{:S(2)}) %collective-permute-start.26) | collective-permute-done | bytes 131104 | tf_op jit(solution)/shard_map/ppermute | solution.py:136
  74.6 2.0 collective-permute-done.20
  76.6 2.4 %collective-permute-done.27 = bf16[128,512]{1,0:T(8,128)(2,1)S(1)} collective-permute-done((bf16[128,512]{1,0:T(8,128)(2,1)S(1)}, bf16[128,512]{1,0:T(8,128)(2,1)S(1)}, u32[]{:S(2)}, u32[]{:S(2)}) %collective-permute-start.27) | collective-permute-done | bytes 131104 | tf_op jit(solution)/shard_map/ppermute | solution.py:136
  79.1 1.2 collective-permute-start.21
  81.0 1.7 collective-permute-start.7
  84.2 1.4 collective-permute-done.28
  86.0 1.6 collective-permute-done.14
  87.8 2.5 %collective-permute-start.29 = (bf16[3,2048]{1,0:T(4,128)(2,1)S(1)}, bf16[3,2048]{1,0:T(4,128)(2,1)S(1)}, u32[]{:S(2)}, u32[]{:S(2)}) collective-permute-start(bf16[3,2048]{1,0:T(4,128)(2,1)S(1)} %pad_maximum_fusion.1), channel_id=1, source_target_pairs={{0,4},{4,8},{8,12},{12,16},{16,20},{20,24},{24,28},{1,5},{5,9},{9,... | collective-permute-start | bytes 36872 | tf_op jit(solution)/shard_map/ppermute | solution.py:13
  90.3 1.2 collective-permute-done.29
  92.7 8.8 %convolution_convert_fusion = bf16[128,4096]{1,0:T(8,128)(2,1)S(1)} fusion(bf16[2048,4096]{1,0:T(8,128)(2,1)} %param.27, bf16[128,2048]{1,0:T(8,128)(2,1)S(1)} %copy-done.16, f32[128,2048]{1,0:T(8,128)S(1)} %fusion.9), kind=kOutput, calls=%fused_computation.6 | convolution fusion | flops 2150891520 | bytes 19398656 | tf_op jit(solution)/shard_map/dot_general | solution.py:210
  101.7 1.9 collective-permute-done.30
  104.5 13.4 %collective-permute-done.31 = bf16[128,2048]{1,0:T(8,128)(2,1)S(1)} collective-permute-done((bf16[128,2048]{1,0:T(8,128)(2,1)S(1)}, bf16[128,2048]{1,0:T(8,128)(2,1)S(1)}, u32[]{:S(2)}, u32[]{:S(2)}) %collective-permute-start.31) | collective-permute-done | bytes 524320 | tf_op jit(solution)/shard_map/ppermute | solution.py:152
  121.1 3.2 %maximum_select_fusion = f32[128,4096]{1,0:T(8,128)} fusion(f32[128,2048]{1,0:T(8,128)S(1)} %convert_add_fusion, f32[128,2048]{1,0:T(8,128)} %collective-permute-done.32, pred[]{:T(512)S(6)} %eq.42), kind=kLoop, calls=%fused_computation.7 | loop fusion | flops 1572864 | bytes 4194305 | tf_op jit(solution)/shard_map/jit(_where)/select_n | solution.py:156
  124.3 14.7 %multiply_multiply_fusion.2 = (f32[128,2048]{1,0:T(8,128)}, f32[128,2048]{1,0:T(8,128)}, bf16[128,2048]{1,0:T(8,128)(2,1)}) fusion(f32[128]{0:T(128)S(1)} %get-tuple-element.123, f32[2048]{0:T(1024)S(1)} %bitcast.323, f32[128,2048]{1,0:T(8,128)} %copy-done.9, bf16[128,2048]{1,0:T(8,128)(2,1)} %param.25, bf16[2048,4096]{1,0:T(8,128)(2,1)} %param.27, ...), kind=kOutput, calls=%fused_computation.43 | convolution fusion | flops 2155872256 | bytes 24126464 | tf_op jit(solution)/shard_map/dot_general | solution.py:223
  139.0 1.5 multiply_multiply_fusion.1
  142.4 1.3 collective-permute-start.33
  145.6 3.1 %collective-permute-done.33 = f32[3,2048]{1,0:T(4,128)S(1)} collective-permute-done((f32[3,2048]{1,0:T(4,128)S(1)}, f32[3,2048]{1,0:T(4,128)S(1)}, u32[]{:S(2)}, u32[]{:S(2)}) %collective-permute-start.33) | collective-permute-done | bytes 24608 | tf_op jit(solution)/shard_map/ppermute | solution.py:13
  149.1 3.2 %collective-permute-start.55 = (bf16[128,512]{1,0:T(8,128)(2,1)S(1)}, bf16[128,512]{1,0:T(8,128)(2,1)S(1)}, u32[]{:S(2)}, u32[]{:S(2)}) collective-permute-start(bf16[128,512]{1,0:T(8,128)(2,1)S(1)} %get-tuple-element.103), channel_id=1, source_target_pairs={{8,0},{16,8},{24,16},{28,24},{20,28},{12,20},{4,12},{0,4},{9,1},{1... | collective-permute-start | bytes 393224 | tf_op jit(solution)/shard_map/ppermute | solution.py:103
  152.4 1.4 collective-permute-start.48
  155.1 2.3 %collective-permute-done.55 = bf16[128,512]{1,0:T(8,128)(2,1)S(1)} collective-permute-done((bf16[128,512]{1,0:T(8,128)(2,1)S(1)}, bf16[128,512]{1,0:T(8,128)(2,1)S(1)}, u32[]{:S(2)}, u32[]{:S(2)}) %collective-permute-start.55) | collective-permute-done | bytes 131104 | tf_op jit(solution)/shard_map/ppermute | solution.py:103
  157.3 1.4 collective-permute-start.56
  158.7 1.4 collective-permute-done.48
  160.1 1.4 collective-permute-start.49
  162.2 1.8 collective-permute-start.35
  164.4 2.2 collective-permute-done.49
  166.6 1.3 collective-permute-start.50
  169.0 1.8 collective-permute-start.36
  171.4 1.7 collective-permute-done.50
  173.9 1.2 collective-permute-start.44
  175.1 1.4 collective-permute-done.36
  181.5 1.6 collective-permute-done.37
  185.9 1.3 collective-permute-start.53
  188.7 1.3 collective-permute-start.39
  191.8 1.4 collective-permute-start.54
  201.7 1.8 collective-permute-done.62
  204.4 3.7 %collective-permute-start.63 = (bf16[128,512]{1,0:T(8,128)(2,1)S(1)}, bf16[128,512]{1,0:T(8,128)(2,1)S(1)}, u32[]{:S(2)}, u32[]{:S(2)}) collective-permute-start(bf16[128,512]{1,0:T(8,128)(2,1)S(1)} %get-tuple-element.111), channel_id=1, source_target_pairs={{0,0},{1,8},{2,16},{3,24},{4,4},{5,12},{6,20},{7,28},{8,1},{9,9},{... | collective-permute-start | bytes 393224 | tf_op jit(solution)/shard_map/ppermute | solution.py:73
  208.2 2.7 %collective-permute-start.65 = (bf16[128,512]{1,0:T(8,128)(2,1)S(1)}, bf16[128,512]{1,0:T(8,128)(2,1)S(1)}, u32[]{:S(2)}, u32[]{:S(2)}) collective-permute-start(bf16[128,512]{1,0:T(8,128)(2,1)S(1)} %get-tuple-element.110), channel_id=1, source_target_pairs={{0,4},{1,12},{2,20},{3,28},{4,0},{5,8},{6,16},{7,24},{8,5},{9,13},... | collective-permute-start | bytes 393224 | tf_op jit(solution)/shard_map/ppermute | solution.py:73
  210.9 1.8 dynamic-slice_convert_fusion
  212.7 1.7 collective-permute-done.64
  214.4 4.8 %collective-permute-done.63 = bf16[128,512]{1,0:T(8,128)(2,1)S(1)} collective-permute-done((bf16[128,512]{1,0:T(8,128)(2,1)S(1)}, bf16[128,512]{1,0:T(8,128)(2,1)S(1)}, u32[]{:S(2)}, u32[]{:S(2)}) %collective-permute-start.63) | collective-permute-done | bytes 131104 | tf_op jit(solution)/shard_map/ppermute | solution.py:73
  220.2 2.5 %collective-permute-done.65 = bf16[128,512]{1,0:T(8,128)(2,1)S(1)} collective-permute-done((bf16[128,512]{1,0:T(8,128)(2,1)S(1)}, bf16[128,512]{1,0:T(8,128)(2,1)S(1)}, u32[]{:S(2)}, u32[]{:S(2)}) %collective-permute-start.65) | collective-permute-done | bytes 131104 | tf_op jit(solution)/shard_map/ppermute | solution.py:73
  (226 shorter events, 58.8 us)
Async XLA Ops:
  3.4 20.3 %all-to-all-start = ((bf16[128,8,256]{2,0,1:T(8,128)(2,1)}), bf16[128,8,256]{2,0,1:T(8,128)(2,1)S(1)}, u32[]{:S(2)}, u32[]{:S(2)}) async-start(bf16[128,8,256]{2,0,1:T(8,128)(2,1)} %copy.25), calls=%async_computation | async-start | bytes 1048576 | tf_op jit(solution)/shard_map/all_to_all | solution.py:24
  29.0 9.0 %collective-permute-start.15 = (bf16[128,512]{1,0:T(8,128)(2,1)S(1)}, bf16[128,512]{1,0:T(8,128)(2,1)S(1)}, u32[]{:S(2)}, u32[]{:S(2)}) collective-permute-start(bf16[128,512]{1,0:T(8,128)(2,1)S(1)} %get-tuple-element.116), channel_id=1, source_target_pairs={{8,0},{16,8},{24,16},{28,24},{20,28},{12,20},{4,12},{0,4},{9,1},{1... | collective-permute-start | bytes 393224 | tf_op jit(solution)/shard_map/ppermute | solution.py:136
  30.5 7.5 %collective-permute-start.22 = (bf16[128,512]{1,0:T(8,128)(2,1)S(1)}, bf16[128,512]{1,0:T(8,128)(2,1)}, u32[]{:S(2)}, u32[]{:S(2)}) collective-permute-start(bf16[128,512]{1,0:T(8,128)(2,1)S(1)} %get-tuple-element.117), channel_id=1, source_target_pairs={{8,0},{16,8},{24,16},{28,24},{20,28},{12,20},{4,12},{0,4},{9,1},{1... | collective-permute-start | bytes 393224 | tf_op jit(solution)/shard_map/ppermute | solution.py:136
  32.5 8.1 %collective-permute-start.1 = (bf16[128,512]{1,0:T(8,128)(2,1)S(1)}, bf16[128,512]{1,0:T(8,128)(2,1)S(1)}, u32[]{:S(2)}, u32[]{:S(2)}) collective-permute-start(bf16[128,512]{1,0:T(8,128)(2,1)S(1)} %get-tuple-element.114), channel_id=1, source_target_pairs={{0,8},{8,16},{16,24},{24,28},{28,20},{20,12},{12,4},{4,0},{1,9},{9... | collective-permute-start | bytes 393224 | tf_op jit(solution)/shard_map/ppermute | solution.py:136
  34.5 6.1 %collective-permute-start.8 = (bf16[128,512]{1,0:T(8,128)(2,1)S(1)}, bf16[128,512]{1,0:T(8,128)(2,1)S(1)}, u32[]{:S(2)}, u32[]{:S(2)}) collective-permute-start(bf16[128,512]{1,0:T(8,128)(2,1)S(1)} %get-tuple-element.115), channel_id=1, source_target_pairs={{0,8},{8,16},{16,24},{24,28},{28,20},{20,12},{12,4},{4,0},{1,9},{9... | collective-permute-start | bytes 393224 | tf_op jit(solution)/shard_map/ppermute | solution.py:136
  39.0 5.9 %collective-permute-start.16 = (bf16[128,512]{1,0:T(8,128)(2,1)S(1)}, bf16[128,512]{1,0:T(8,128)(2,1)S(1)}, u32[]{:S(2)}, u32[]{:S(2)}) collective-permute-start(bf16[128,512]{1,0:T(8,128)(2,1)S(1)} %get-tuple-element.93), channel_id=1, source_target_pairs={{8,0},{16,8},{24,16},{28,24},{20,28},{12,20},{4,12},{0,4},{9,1},{1... | collective-permute-start | bytes 393224 | tf_op jit(solution)/shard_map/ppermute | solution.py:136
  40.5 5.8 %collective-permute-start.23 = (bf16[128,512]{1,0:T(8,128)(2,1)S(1)}, bf16[128,512]{1,0:T(8,128)(2,1)S(1)}, u32[]{:S(2)}, u32[]{:S(2)}) collective-permute-start(bf16[128,512]{1,0:T(8,128)(2,1)S(1)} %get-tuple-element.94), channel_id=1, source_target_pairs={{8,0},{16,8},{24,16},{28,24},{20,28},{12,20},{4,12},{0,4},{9,1},{1... | collective-permute-start | bytes 393224 | tf_op jit(solution)/shard_map/ppermute | solution.py:136
  40.7 7.6 %collective-permute-start.2 = (bf16[128,512]{1,0:T(8,128)(2,1)S(1)}, bf16[128,512]{1,0:T(8,128)(2,1)S(1)}, u32[]{:S(2)}, u32[]{:S(2)}) collective-permute-start(bf16[128,512]{1,0:T(8,128)(2,1)S(1)} %get-tuple-element.79), channel_id=1, source_target_pairs={{0,8},{8,16},{16,24},{24,28},{28,20},{20,12},{12,4},{4,0},{1,9},{9... | collective-permute-start | bytes 393224 | tf_op jit(solution)/shard_map/ppermute | solution.py:136
  42.7 5.6 %collective-permute-start.9 = (bf16[128,512]{1,0:T(8,128)(2,1)S(1)}, bf16[128,512]{1,0:T(8,128)(2,1)S(1)}, u32[]{:S(2)}, u32[]{:S(2)}) collective-permute-start(bf16[128,512]{1,0:T(8,128)(2,1)S(1)} %get-tuple-element.80), channel_id=1, source_target_pairs={{0,8},{8,16},{16,24},{24,28},{28,20},{20,12},{12,4},{4,0},{1,9},{9... | collective-permute-start | bytes 393224 | tf_op jit(solution)/shard_map/ppermute | solution.py:136
  46.4 5.0 %collective-permute-start.17 = (bf16[128,512]{1,0:T(8,128)(2,1)S(1)}, bf16[128,512]{1,0:T(8,128)(2,1)S(1)}, u32[]{:S(2)}, u32[]{:S(2)}) collective-permute-start(bf16[128,512]{1,0:T(8,128)(2,1)S(1)} %get-tuple-element.91), channel_id=1, source_target_pairs={{8,0},{16,8},{24,16},{28,24},{20,28},{12,20},{4,12},{0,4},{9,1},{1... | collective-permute-start | bytes 393224 | tf_op jit(solution)/shard_map/ppermute | solution.py:136
  47.9 5.4 %collective-permute-start.24 = (bf16[128,512]{1,0:T(8,128)(2,1)S(1)}, bf16[128,512]{1,0:T(8,128)(2,1)S(1)}, u32[]{:S(2)}, u32[]{:S(2)}) collective-permute-start(bf16[128,512]{1,0:T(8,128)(2,1)S(1)} %get-tuple-element.92), channel_id=1, source_target_pairs={{8,0},{16,8},{24,16},{28,24},{20,28},{12,20},{4,12},{0,4},{9,1},{1... | collective-permute-start | bytes 393224 | tf_op jit(solution)/shard_map/ppermute | solution.py:136
  48.4 6.7 %collective-permute-start.3 = (bf16[128,512]{1,0:T(8,128)(2,1)S(1)}, bf16[128,512]{1,0:T(8,128)(2,1)S(1)}, u32[]{:S(2)}, u32[]{:S(2)}) collective-permute-start(bf16[128,512]{1,0:T(8,128)(2,1)S(1)} %get-tuple-element.77), channel_id=1, source_target_pairs={{0,8},{8,16},{16,24},{24,28},{28,20},{20,12},{12,4},{4,0},{1,9},{9... | collective-permute-start | bytes 393224 | tf_op jit(solution)/shard_map/ppermute | solution.py:136
  50.1 5.2 %collective-permute-start.10 = (bf16[128,512]{1,0:T(8,128)(2,1)S(1)}, bf16[128,512]{1,0:T(8,128)(2,1)S(1)}, u32[]{:S(2)}, u32[]{:S(2)}) collective-permute-start(bf16[128,512]{1,0:T(8,128)(2,1)S(1)} %get-tuple-element.78), channel_id=1, source_target_pairs={{0,8},{8,16},{16,24},{24,28},{28,20},{20,12},{12,4},{4,0},{1,9},{9... | collective-permute-start | bytes 393224 | tf_op jit(solution)/shard_map/ppermute | solution.py:136
  53.3 5.1 %collective-permute-start.18 = (bf16[128,512]{1,0:T(8,128)(2,1)S(1)}, bf16[128,512]{1,0:T(8,128)(2,1)S(1)}, u32[]{:S(2)}, u32[]{:S(2)}) collective-permute-start(bf16[128,512]{1,0:T(8,128)(2,1)S(1)} %get-tuple-element.89), channel_id=1, source_target_pairs={{8,0},{16,8},{24,16},{28,24},{20,28},{12,20},{4,12},{0,4},{9,1},{1... | collective-permute-start | bytes 393224 | tf_op jit(solution)/shard_map/ppermute | solution.py:136
  54.7 6.6 %collective-permute-start.25 = (bf16[128,512]{1,0:T(8,128)(2,1)S(1)}, bf16[128,512]{1,0:T(8,128)(2,1)S(1)}, u32[]{:S(2)}, u32[]{:S(2)}) collective-permute-start(bf16[128,512]{1,0:T(8,128)(2,1)S(1)} %get-tuple-element.90), channel_id=1, source_target_pairs={{8,0},{16,8},{24,16},{28,24},{20,28},{12,20},{4,12},{0,4},{9,1},{1... | collective-permute-start | bytes 393224 | tf_op jit(solution)/shard_map/ppermute | solution.py:136
  55.4 7.2 %collective-permute-start.4 = (bf16[128,512]{1,0:T(8,128)(2,1)S(1)}, bf16[128,512]{1,0:T(8,128)(2,1)S(1)}, u32[]{:S(2)}, u32[]{:S(2)}) collective-permute-start(bf16[128,512]{1,0:T(8,128)(2,1)S(1)} %get-tuple-element.75), channel_id=1, source_target_pairs={{0,8},{8,16},{16,24},{24,28},{28,20},{20,12},{12,4},{4,0},{1,9},{9... | collective-permute-start | bytes 393224 | tf_op jit(solution)/shard_map/ppermute | solution.py:136
  57.1 6.3 %collective-permute-start.11 = (bf16[128,512]{1,0:T(8,128)(2,1)S(1)}, bf16[128,512]{1,0:T(8,128)(2,1)S(1)}, u32[]{:S(2)}, u32[]{:S(2)}) collective-permute-start(bf16[128,512]{1,0:T(8,128)(2,1)S(1)} %get-tuple-element.76), channel_id=1, source_target_pairs={{0,8},{8,16},{16,24},{24,28},{28,20},{20,12},{12,4},{4,0},{1,9},{9... | collective-permute-start | bytes 393224 | tf_op jit(solution)/shard_map/ppermute | solution.py:136
  61.3 6.0 %collective-permute-start.19 = (bf16[128,512]{1,0:T(8,128)(2,1)S(1)}, bf16[128,512]{1,0:T(8,128)(2,1)S(1)}, u32[]{:S(2)}, u32[]{:S(2)}) collective-permute-start(bf16[128,512]{1,0:T(8,128)(2,1)S(1)} %get-tuple-element.87), channel_id=1, source_target_pairs={{8,0},{16,8},{24,16},{28,24},{20,28},{12,20},{4,12},{0,4},{9,1},{1... | collective-permute-start | bytes 393224 | tf_op jit(solution)/shard_map/ppermute | solution.py:136
  62.5 7.7 %collective-permute-start.26 = (bf16[128,512]{1,0:T(8,128)(2,1)S(1)}, bf16[128,512]{1,0:T(8,128)(2,1)S(1)}, u32[]{:S(2)}, u32[]{:S(2)}) collective-permute-start(bf16[128,512]{1,0:T(8,128)(2,1)S(1)} %get-tuple-element.88), channel_id=1, source_target_pairs={{8,0},{16,8},{24,16},{28,24},{20,28},{12,20},{4,12},{0,4},{9,1},{1... | collective-permute-start | bytes 393224 | tf_op jit(solution)/shard_map/ppermute | solution.py:136
  63.5 8.0 %collective-permute-start.5 = (bf16[128,512]{1,0:T(8,128)(2,1)S(1)}, bf16[128,512]{1,0:T(8,128)(2,1)S(1)}, u32[]{:S(2)}, u32[]{:S(2)}) collective-permute-start(bf16[128,512]{1,0:T(8,128)(2,1)S(1)} %get-tuple-element.73), channel_id=1, source_target_pairs={{0,8},{8,16},{16,24},{24,28},{28,20},{20,12},{12,4},{4,0},{1,9},{9... | collective-permute-start | bytes 393224 | tf_op jit(solution)/shard_map/ppermute | solution.py:136
  64.9 7.5 %collective-permute-start.12 = (bf16[128,512]{1,0:T(8,128)(2,1)S(1)}, bf16[128,512]{1,0:T(8,128)(2,1)S(1)}, u32[]{:S(2)}, u32[]{:S(2)}) collective-permute-start(bf16[128,512]{1,0:T(8,128)(2,1)S(1)} %get-tuple-element.74), channel_id=1, source_target_pairs={{0,8},{8,16},{16,24},{24,28},{28,20},{20,12},{12,4},{4,0},{1,9},{9... | collective-permute-start | bytes 393224 | tf_op jit(solution)/shard_map/ppermute | solution.py:136
  70.3 6.3 %collective-permute-start.20 = (bf16[128,512]{1,0:T(8,128)(2,1)S(1)}, bf16[128,512]{1,0:T(8,128)(2,1)S(1)}, u32[]{:S(2)}, u32[]{:S(2)}) collective-permute-start(bf16[128,512]{1,0:T(8,128)(2,1)S(1)} %get-tuple-element.85), channel_id=1, source_target_pairs={{8,0},{16,8},{24,16},{28,24},{20,28},{12,20},{4,12},{0,4},{9,1},{1... | collective-permute-start | bytes 393224 | tf_op jit(solution)/shard_map/ppermute | solution.py:136
  71.4 7.6 %collective-permute-start.27 = (bf16[128,512]{1,0:T(8,128)(2,1)S(1)}, bf16[128,512]{1,0:T(8,128)(2,1)S(1)}, u32[]{:S(2)}, u32[]{:S(2)}) collective-permute-start(bf16[128,512]{1,0:T(8,128)(2,1)S(1)} %get-tuple-element.86), channel_id=1, source_target_pairs={{8,0},{16,8},{24,16},{28,24},{20,28},{12,20},{4,12},{0,4},{9,1},{1... | collective-permute-start | bytes 393224 | tf_op jit(solution)/shard_map/ppermute | solution.py:136
  72.6 8.1 %collective-permute-start.6 = (bf16[128,512]{1,0:T(8,128)(2,1)S(1)}, bf16[128,512]{1,0:T(8,128)(2,1)S(1)}, u32[]{:S(2)}, u32[]{:S(2)}) collective-permute-start(bf16[128,512]{1,0:T(8,128)(2,1)S(1)} %get-tuple-element.71), channel_id=1, source_target_pairs={{0,8},{8,16},{16,24},{24,28},{28,20},{20,12},{12,4},{4,0},{1,9},{9... | collective-permute-start | bytes 393224 | tf_op jit(solution)/shard_map/ppermute | solution.py:136
  73.7 7.3 %collective-permute-start.13 = (bf16[128,512]{1,0:T(8,128)(2,1)S(1)}, bf16[128,512]{1,0:T(8,128)(2,1)S(1)}, u32[]{:S(2)}, u32[]{:S(2)}) collective-permute-start(bf16[128,512]{1,0:T(8,128)(2,1)S(1)} %get-tuple-element.72), channel_id=1, source_target_pairs={{0,8},{8,16},{16,24},{24,28},{28,20},{20,12},{12,4},{4,0},{1,9},{9... | collective-permute-start | bytes 393224 | tf_op jit(solution)/shard_map/ppermute | solution.py:136
  79.1 5.0 %collective-permute-start.21 = (bf16[128,512]{1,0:T(8,128)(2,1)S(1)}, bf16[128,512]{1,0:T(8,128)(2,1)S(1)}, u32[]{:S(2)}, u32[]{:S(2)}) collective-permute-start(bf16[128,512]{1,0:T(8,128)(2,1)S(1)} %get-tuple-element.83), channel_id=1, source_target_pairs={{8,0},{16,8},{24,16},{28,24},{20,28},{12,20},{4,12},{0,4},{9,1},{1... | collective-permute-start | bytes 393224 | tf_op jit(solution)/shard_map/ppermute | solution.py:136
  80.3 5.2 %collective-permute-start.28 = (bf16[128,512]{1,0:T(8,128)(2,1)S(1)}, bf16[128,512]{1,0:T(8,128)(2,1)S(1)}, u32[]{:S(2)}, u32[]{:S(2)}) collective-permute-start(bf16[128,512]{1,0:T(8,128)(2,1)S(1)} %get-tuple-element.84), channel_id=1, source_target_pairs={{8,0},{16,8},{24,16},{28,24},{20,28},{12,20},{4,12},{0,4},{9,1},{1... | collective-permute-start | bytes 393224 | tf_op jit(solution)/shard_map/ppermute | solution.py:136
  81.0 5.0 %collective-permute-start.7 = (bf16[128,512]{1,0:T(8,128)(2,1)S(1)}, bf16[128,512]{1,0:T(8,128)(2,1)S(1)}, u32[]{:S(2)}, u32[]{:S(2)}) collective-permute-start(bf16[128,512]{1,0:T(8,128)(2,1)S(1)} %get-tuple-element.69), channel_id=1, source_target_pairs={{0,8},{8,16},{16,24},{24,28},{28,20},{20,12},{12,4},{4,0},{1,9},{9... | collective-permute-start | bytes 393224 | tf_op jit(solution)/shard_map/ppermute | solution.py:136
  82.7 5.0 %collective-permute-start.14 = (bf16[128,512]{1,0:T(8,128)(2,1)S(1)}, bf16[128,512]{1,0:T(8,128)(2,1)S(1)}, u32[]{:S(2)}, u32[]{:S(2)}) collective-permute-start(bf16[128,512]{1,0:T(8,128)(2,1)S(1)} %get-tuple-element.70), channel_id=1, source_target_pairs={{0,8},{8,16},{16,24},{24,28},{28,20},{20,12},{12,4},{4,0},{1,9},{9... | collective-permute-start | bytes 393224 | tf_op jit(solution)/shard_map/ppermute | solution.py:136
  87.8 3.7 %collective-permute-start.29 = (bf16[3,2048]{1,0:T(4,128)(2,1)S(1)}, bf16[3,2048]{1,0:T(4,128)(2,1)S(1)}, u32[]{:S(2)}, u32[]{:S(2)}) collective-permute-start(bf16[3,2048]{1,0:T(4,128)(2,1)S(1)} %pad_maximum_fusion.1), channel_id=1, source_target_pairs={{0,4},{4,8},{8,12},{12,16},{16,20},{20,24},{24,28},{1,5},{5,9},{9,... | collective-permute-start | bytes 36872 | tf_op jit(solution)/shard_map/ppermute | solution.py:13
  103.9 14.0 %collective-permute-start.31 = (bf16[128,2048]{1,0:T(8,128)(2,1)S(1)}, bf16[128,2048]{1,0:T(8,128)(2,1)S(1)}, u32[]{:S(2)}, u32[]{:S(2)}) collective-permute-start(bf16[128,2048]{1,0:T(8,128)(2,1)S(1)} %fusion.21), channel_id=1, source_target_pairs={{0,2},{1,3},{2,0},{3,1},{4,6},{5,7},{6,4},{7,5},{8,10},{9,11},{10,... | collective-permute-start | bytes 1572872 | tf_op jit(solution)/shard_map/ppermute | solution.py:152
  142.4 6.3 %collective-permute-start.33 = (f32[3,2048]{1,0:T(4,128)S(1)}, f32[3,2048]{1,0:T(4,128)S(1)}, u32[]{:S(2)}, u32[]{:S(2)}) collective-permute-start(f32[3,2048]{1,0:T(4,128)S(1)} %slice_add_fusion), channel_id=1, source_target_pairs={{4,0},{8,4},{12,8},{16,12},{20,16},{24,20},{28,24},{5,1},{9,5},{13... | collective-permute-start | bytes 73736 | tf_op jit(solution)/shard_map/ppermute | solution.py:13
  149.1 8.2 %collective-permute-start.55 = (bf16[128,512]{1,0:T(8,128)(2,1)S(1)}, bf16[128,512]{1,0:T(8,128)(2,1)S(1)}, u32[]{:S(2)}, u32[]{:S(2)}) collective-permute-start(bf16[128,512]{1,0:T(8,128)(2,1)S(1)} %get-tuple-element.103), channel_id=1, source_target_pairs={{8,0},{16,8},{24,16},{28,24},{20,28},{12,20},{4,12},{0,4},{9,1},{1... | collective-permute-start | bytes 393224 | tf_op jit(solution)/shard_map/ppermute | solution.py:103
  152.4 7.8 %collective-permute-start.48 = (bf16[128,512]{1,0:T(8,128)(2,1)S(1)}, bf16[128,512]{1,0:T(8,128)(2,1)S(1)}, u32[]{:S(2)}, u32[]{:S(2)}) collective-permute-start(bf16[128,512]{1,0:T(8,128)(2,1)S(1)} %get-tuple-element.104), channel_id=1, source_target_pairs={{8,0},{16,8},{24,16},{28,24},{20,28},{12,20},{4,12},{0,4},{9,1},{1... | collective-permute-start | bytes 393224 | tf_op jit(solution)/shard_map/ppermute | solution.py:103
  153.8 7.7 %collective-permute-start.41 = (bf16[128,512]{1,0:T(8,128)(2,1)S(1)}, bf16[128,512]{1,0:T(8,128)(2,1)S(1)}, u32[]{:S(2)}, u32[]{:S(2)}) collective-permute-start(bf16[128,512]{1,0:T(8,128)(2,1)S(1)} %get-tuple-element.105), channel_id=1, source_target_pairs={{0,8},{8,16},{16,24},{24,28},{28,20},{20,12},{12,4},{4,0},{1,9},{9... | collective-permute-start | bytes 393224 | tf_op jit(solution)/shard_map/ppermute | solution.py:103
  154.4 7.8 %collective-permute-start.34 = (bf16[128,512]{1,0:T(8,128)(2,1)S(1)}, bf16[128,512]{1,0:T(8,128)(2,1)S(1)}, u32[]{:S(2)}, u32[]{:S(2)}) collective-permute-start(bf16[128,512]{1,0:T(8,128)(2,1)S(1)} %get-tuple-element.102), channel_id=1, source_target_pairs={{0,8},{8,16},{16,24},{24,28},{28,20},{20,12},{12,4},{4,0},{1,9},{9... | collective-permute-start | bytes 393224 | tf_op jit(solution)/shard_map/ppermute | solution.py:103
  157.3 6.6 %collective-permute-start.56 = (bf16[128,512]{1,0:T(8,128)(2,1)S(1)}, bf16[128,512]{1,0:T(8,128)(2,1)S(1)}, u32[]{:S(2)}, u32[]{:S(2)}) collective-permute-start(bf16[128,512]{1,0:T(8,128)(2,1)S(1)} %collective-permute-done.55), channel_id=1, source_target_pairs={{8,0},{16,8},{24,16},{28,24},{20,28},{12,20},{4,12},{0,4},{9,1},{1... | collective-permute-start | bytes 393224 | tf_op jit(solution)/shard_map/ppermute | solution.py:103
  160.1 6.4 %collective-permute-start.49 = (bf16[128,512]{1,0:T(8,128)(2,1)S(1)}, bf16[128,512]{1,0:T(8,128)(2,1)S(1)}, u32[]{:S(2)}, u32[]{:S(2)}) collective-permute-start(bf16[128,512]{1,0:T(8,128)(2,1)S(1)} %collective-permute-done.48), channel_id=1, source_target_pairs={{8,0},{16,8},{24,16},{28,24},{20,28},{12,20},{4,12},{0,4},{9,1},{1... | collective-permute-start | bytes 393224 | tf_op jit(solution)/shard_map/ppermute | solution.py:103
  161.5 6.3 %collective-permute-start.42 = (bf16[128,512]{1,0:T(8,128)(2,1)S(1)}, bf16[128,512]{1,0:T(8,128)(2,1)S(1)}, u32[]{:S(2)}, u32[]{:S(2)}) collective-permute-start(bf16[128,512]{1,0:T(8,128)(2,1)S(1)} %collective-permute-done.41), channel_id=1, source_target_pairs={{0,8},{8,16},{16,24},{24,28},{28,20},{20,12},{12,4},{4,0},{1,9},{9... | collective-permute-start | bytes 393224 | tf_op jit(solution)/shard_map/ppermute | solution.py:103
  162.2 6.9 %collective-permute-start.35 = (bf16[128,512]{1,0:T(8,128)(2,1)S(1)}, bf16[128,512]{1,0:T(8,128)(2,1)S(1)}, u32[]{:S(2)}, u32[]{:S(2)}) collective-permute-start(bf16[128,512]{1,0:T(8,128)(2,1)S(1)} %collective-permute-done.34), channel_id=1, source_target_pairs={{0,8},{8,16},{16,24},{24,28},{28,20},{20,12},{12,4},{4,0},{1,9},{9... | collective-permute-start | bytes 393224 | tf_op jit(solution)/shard_map/ppermute | solution.py:103
  164.0 6.9 %collective-permute-start.57 = (bf16[128,512]{1,0:T(8,128)(2,1)S(1)}, bf16[128,512]{1,0:T(8,128)(2,1)S(1)}, u32[]{:S(2)}, u32[]{:S(2)}) collective-permute-start(bf16[128,512]{1,0:T(8,128)(2,1)S(1)} %collective-permute-done.56), channel_id=1, source_target_pairs={{8,0},{16,8},{24,16},{28,24},{20,28},{12,20},{4,12},{0,4},{9,1},{1... | collective-permute-start | bytes 393224 | tf_op jit(solution)/shard_map/ppermute | solution.py:103
  166.6 6.5 %collective-permute-start.50 = (bf16[128,512]{1,0:T(8,128)(2,1)S(1)}, bf16[128,512]{1,0:T(8,128)(2,1)S(1)}, u32[]{:S(2)}, u32[]{:S(2)}) collective-permute-start(bf16[128,512]{1,0:T(8,128)(2,1)S(1)} %collective-permute-done.49), channel_id=1, source_target_pairs={{8,0},{16,8},{24,16},{28,24},{20,28},{12,20},{4,12},{0,4},{9,1},{1... | collective-permute-start | bytes 393224 | tf_op jit(solution)/shard_map/ppermute | solution.py:103
  167.9 6.0 %collective-permute-start.43 = (bf16[128,512]{1,0:T(8,128)(2,1)S(1)}, bf16[128,512]{1,0:T(8,128)(2,1)S(1)}, u32[]{:S(2)}, u32[]{:S(2)}) collective-permute-start(bf16[128,512]{1,0:T(8,128)(2,1)S(1)} %collective-permute-done.42), channel_id=1, source_target_pairs={{0,8},{8,16},{16,24},{24,28},{28,20},{20,12},{12,4},{4,0},{1,9},{9... | collective-permute-start | bytes 393224 | tf_op jit(solution)/shard_map/ppermute | solution.py:103
  169.0 7.5 %collective-permute-start.36 = (bf16[128,512]{1,0:T(8,128)(2,1)S(1)}, bf16[128,512]{1,0:T(8,128)(2,1)S(1)}, u32[]{:S(2)}, u32[]{:S(2)}) collective-permute-start(bf16[128,512]{1,0:T(8,128)(2,1)S(1)} %collective-permute-done.35), channel_id=1, source_target_pairs={{0,8},{8,16},{16,24},{24,28},{28,20},{20,12},{12,4},{4,0},{1,9},{9... | collective-permute-start | bytes 393224 | tf_op jit(solution)/shard_map/ppermute | solution.py:103
  170.9 6.8 %collective-permute-start.58 = (bf16[128,512]{1,0:T(8,128)(2,1)S(1)}, bf16[128,512]{1,0:T(8,128)(2,1)S(1)}, u32[]{:S(2)}, u32[]{:S(2)}) collective-permute-start(bf16[128,512]{1,0:T(8,128)(2,1)S(1)} %collective-permute-done.57), channel_id=1, source_target_pairs={{8,0},{16,8},{24,16},{28,24},{20,28},{12,20},{4,12},{0,4},{9,1},{1... | collective-permute-start | bytes 393224 | tf_op jit(solution)/shard_map/ppermute | solution.py:103
  173.1 6.4 %collective-permute-start.51 = (bf16[128,512]{1,0:T(8,128)(2,1)S(1)}, bf16[128,512]{1,0:T(8,128)(2,1)S(1)}, u32[]{:S(2)}, u32[]{:S(2)}) collective-permute-start(bf16[128,512]{1,0:T(8,128)(2,1)S(1)} %collective-permute-done.50), channel_id=1, source_target_pairs={{8,0},{16,8},{24,16},{28,24},{20,28},{12,20},{4,12},{0,4},{9,1},{1... | collective-permute-start | bytes 393224 | tf_op jit(solution)/shard_map/ppermute | solution.py:103
  173.9 6.4 %collective-permute-start.44 = (bf16[128,512]{1,0:T(8,128)(2,1)S(1)}, bf16[128,512]{1,0:T(8,128)(2,1)S(1)}, u32[]{:S(2)}, u32[]{:S(2)}) collective-permute-start(bf16[128,512]{1,0:T(8,128)(2,1)S(1)} %collective-permute-done.43), channel_id=1, source_target_pairs={{0,8},{8,16},{16,24},{24,28},{28,20},{20,12},{12,4},{4,0},{1,9},{9... | collective-permute-start | bytes 393224 | tf_op jit(solution)/shard_map/ppermute | solution.py:103
  176.5 6.6 %collective-permute-start.37 = (bf16[128,512]{1,0:T(8,128)(2,1)S(1)}, bf16[128,512]{1,0:T(8,128)(2,1)S(1)}, u32[]{:S(2)}, u32[]{:S(2)}) collective-permute-start(bf16[128,512]{1,0:T(8,128)(2,1)S(1)} %collective-permute-done.36), channel_id=1, source_target_pairs={{0,8},{8,16},{16,24},{24,28},{28,20},{20,12},{12,4},{4,0},{1,9},{9... | collective-permute-start | bytes 393224 | tf_op jit(solution)/shard_map/ppermute | solution.py:103
  177.7 6.4 %collective-permute-start.59 = (bf16[128,512]{1,0:T(8,128)(2,1)S(1)}, bf16[128,512]{1,0:T(8,128)(2,1)S(1)}, u32[]{:S(2)}, u32[]{:S(2)}) collective-permute-start(bf16[128,512]{1,0:T(8,128)(2,1)S(1)} %collective-permute-done.58), channel_id=1, source_target_pairs={{8,0},{16,8},{24,16},{28,24},{20,28},{12,20},{4,12},{0,4},{9,1},{1... | collective-permute-start | bytes 393224 | tf_op jit(solution)/shard_map/ppermute | solution.py:103
  179.4 6.5 %collective-permute-start.52 = (bf16[128,512]{1,0:T(8,128)(2,1)S(1)}, bf16[128,512]{1,0:T(8,128)(2,1)S(1)}, u32[]{:S(2)}, u32[]{:S(2)}) collective-permute-start(bf16[128,512]{1,0:T(8,128)(2,1)S(1)} %collective-permute-done.51), channel_id=1, source_target_pairs={{8,0},{16,8},{24,16},{28,24},{20,28},{12,20},{4,12},{0,4},{9,1},{1... | collective-permute-start | bytes 393224 | tf_op jit(solution)/shard_map/ppermute | solution.py:103
  180.3 6.9 %collective-permute-start.45 = (bf16[128,512]{1,0:T(8,128)(2,1)S(1)}, bf16[128,512]{1,0:T(8,128)(2,1)S(1)}, u32[]{:S(2)}, u32[]{:S(2)}) collective-permute-start(bf16[128,512]{1,0:T(8,128)(2,1)S(1)} %collective-permute-done.44), channel_id=1, source_target_pairs={{0,8},{8,16},{16,24},{24,28},{28,20},{20,12},{12,4},{4,0},{1,9},{9... | collective-permute-start | bytes 393224 | tf_op jit(solution)/shard_map/ppermute | solution.py:103
  183.1 5.6 %collective-permute-start.38 = (bf16[128,512]{1,0:T(8,128)(2,1)S(1)}, bf16[128,512]{1,0:T(8,128)(2,1)S(1)}, u32[]{:S(2)}, u32[]{:S(2)}) collective-permute-start(bf16[128,512]{1,0:T(8,128)(2,1)S(1)} %collective-permute-done.37), channel_id=1, source_target_pairs={{0,8},{8,16},{16,24},{24,28},{28,20},{20,12},{12,4},{4,0},{1,9},{9... | collective-permute-start | bytes 393224 | tf_op jit(solution)/shard_map/ppermute | solution.py:103
  184.1 6.3 %collective-permute-start.60 = (bf16[128,512]{1,0:T(8,128)(2,1)S(1)}, bf16[128,512]{1,0:T(8,128)(2,1)S(1)}, u32[]{:S(2)}, u32[]{:S(2)}) collective-permute-start(bf16[128,512]{1,0:T(8,128)(2,1)S(1)} %collective-permute-done.59), channel_id=1, source_target_pairs={{8,0},{16,8},{24,16},{28,24},{20,28},{12,20},{4,12},{0,4},{9,1},{1... | collective-permute-start | bytes 393224 | tf_op jit(solution)/shard_map/ppermute | solution.py:103
  185.9 5.9 %collective-permute-start.53 = (bf16[128,512]{1,0:T(8,128)(2,1)S(1)}, bf16[128,512]{1,0:T(8,128)(2,1)S(1)}, u32[]{:S(2)}, u32[]{:S(2)}) collective-permute-start(bf16[128,512]{1,0:T(8,128)(2,1)S(1)} %collective-permute-done.52), channel_id=1, source_target_pairs={{8,0},{16,8},{24,16},{28,24},{20,28},{12,20},{4,12},{0,4},{9,1},{1... | collective-permute-start | bytes 393224 | tf_op jit(solution)/shard_map/ppermute | solution.py:103
  187.2 6.3 %collective-permute-start.46 = (bf16[128,512]{1,0:T(8,128)(2,1)S(1)}, bf16[128,512]{1,0:T(8,128)(2,1)S(1)}, u32[]{:S(2)}, u32[]{:S(2)}) collective-permute-start(bf16[128,512]{1,0:T(8,128)(2,1)S(1)} %collective-permute-done.45), channel_id=1, source_target_pairs={{0,8},{8,16},{16,24},{24,28},{28,20},{20,12},{12,4},{4,0},{1,9},{9... | collective-permute-start | bytes 393224 | tf_op jit(solution)/shard_map/ppermute | solution.py:103
  188.7 6.2 %collective-permute-start.39 = (bf16[128,512]{1,0:T(8,128)(2,1)S(1)}, bf16[128,512]{1,0:T(8,128)(2,1)S(1)}, u32[]{:S(2)}, u32[]{:S(2)}) collective-permute-start(bf16[128,512]{1,0:T(8,128)(2,1)S(1)} %collective-permute-done.38), channel_id=1, source_target_pairs={{0,8},{8,16},{16,24},{24,28},{28,20},{20,12},{12,4},{4,0},{1,9},{9... | collective-permute-start | bytes 393224 | tf_op jit(solution)/shard_map/ppermute | solution.py:103
  190.4 5.2 %collective-permute-start.61 = (bf16[128,512]{1,0:T(8,128)(2,1)S(1)}, bf16[128,512]{1,0:T(8,128)(2,1)S(1)}, u32[]{:S(2)}, u32[]{:S(2)}) collective-permute-start(bf16[128,512]{1,0:T(8,128)(2,1)S(1)} %collective-permute-done.60), channel_id=1, source_target_pairs={{8,0},{16,8},{24,16},{28,24},{20,28},{12,20},{4,12},{0,4},{9,1},{1... | collective-permute-start | bytes 393224 | tf_op jit(solution)/shard_map/ppermute | solution.py:103
  191.8 5.0 %collective-permute-start.54 = (bf16[128,512]{1,0:T(8,128)(2,1)S(1)}, bf16[128,512]{1,0:T(8,128)(2,1)S(1)}, u32[]{:S(2)}, u32[]{:S(2)}) collective-permute-start(bf16[128,512]{1,0:T(8,128)(2,1)S(1)} %collective-permute-done.53), channel_id=1, source_target_pairs={{8,0},{16,8},{24,16},{28,24},{20,28},{12,20},{4,12},{0,4},{9,1},{1... | collective-permute-start | bytes 393224 | tf_op jit(solution)/shard_map/ppermute | solution.py:103
  193.5 5.0 %collective-permute-start.47 = (bf16[128,512]{1,0:T(8,128)(2,1)S(1)}, bf16[128,512]{1,0:T(8,128)(2,1)S(1)}, u32[]{:S(2)}, u32[]{:S(2)}) collective-permute-start(bf16[128,512]{1,0:T(8,128)(2,1)S(1)} %collective-permute-done.46), channel_id=1, source_target_pairs={{0,8},{8,16},{16,24},{24,28},{28,20},{20,12},{12,4},{4,0},{1,9},{9... | collective-permute-start | bytes 393224 | tf_op jit(solution)/shard_map/ppermute | solution.py:103
  194.9 5.0 %collective-permute-start.40 = (bf16[128,512]{1,0:T(8,128)(2,1)S(1)}, bf16[128,512]{1,0:T(8,128)(2,1)S(1)}, u32[]{:S(2)}, u32[]{:S(2)}) collective-permute-start(bf16[128,512]{1,0:T(8,128)(2,1)S(1)} %collective-permute-done.39), channel_id=1, source_target_pairs={{0,8},{8,16},{16,24},{24,28},{28,20},{20,12},{12,4},{4,0},{1,9},{9... | collective-permute-start | bytes 393224 | tf_op jit(solution)/shard_map/ppermute | solution.py:103
  203.8 10.7 %collective-permute-start.64 = (bf16[128,512]{1,0:T(8,128)(2,1)S(1)}, bf16[128,512]{1,0:T(8,128)(2,1)S(1)}, u32[]{:S(2)}, u32[]{:S(2)}) collective-permute-start(bf16[128,512]{1,0:T(8,128)(2,1)S(1)} %get-tuple-element.113), channel_id=1, source_target_pairs={{0,16},{1,24},{2,0},{3,8},{4,20},{5,28},{6,4},{7,12},{8,17},{9,25}... | collective-permute-start | bytes 393224 | tf_op jit(solution)/shard_map/ppermute | solution.py:73
  204.4 14.8 %collective-permute-start.63 = (bf16[128,512]{1,0:T(8,128)(2,1)S(1)}, bf16[128,512]{1,0:T(8,128)(2,1)S(1)}, u32[]{:S(2)}, u32[]{:S(2)}) collective-permute-start(bf16[128,512]{1,0:T(8,128)(2,1)S(1)} %get-tuple-element.111), channel_id=1, source_target_pairs={{0,0},{1,8},{2,16},{3,24},{4,4},{5,12},{6,20},{7,28},{8,1},{9,9},{... | collective-permute-start | bytes 393224 | tf_op jit(solution)/shard_map/ppermute | solution.py:73
  208.1 12.1 %collective-permute-start.66 = (bf16[128,512]{1,0:T(8,128)(2,1)S(1)}, bf16[128,512]{1,0:T(8,128)(2,1)S(1)}, u32[]{:S(2)}, u32[]{:S(2)}) collective-permute-start(bf16[128,512]{1,0:T(8,128)(2,1)S(1)} %get-tuple-element.112), channel_id=1, source_target_pairs={{0,20},{1,28},{2,4},{3,12},{4,16},{5,24},{6,0},{7,8},{8,21},{9,29}... | collective-permute-start | bytes 393224 | tf_op jit(solution)/shard_map/ppermute | solution.py:73
  208.2 14.5 %collective-permute-start.65 = (bf16[128,512]{1,0:T(8,128)(2,1)S(1)}, bf16[128,512]{1,0:T(8,128)(2,1)S(1)}, u32[]{:S(2)}, u32[]{:S(2)}) collective-permute-start(bf16[128,512]{1,0:T(8,128)(2,1)S(1)} %get-tuple-element.110), channel_id=1, source_target_pairs={{0,4},{1,12},{2,20},{3,28},{4,0},{5,8},{6,16},{7,24},{8,5},{9,13},... | collective-permute-start | bytes 393224 | tf_op jit(solution)/shard_map/ppermute | solution.py:73
  (24 other events, 155.8 us)

commit v15 on v14

--- a/solution.py
+++ b/solution.py
@@ -149,10 +149,14 @@
     count = lax.axis_size("col")
     got = lax.ppermute(give, "col", [(c, c ^ 1) for c in range(count)])
     pair = keep.astype(jnp.float32) + got.astype(jnp.float32)
-    total = pair + lax.ppermute(
-        pair.astype(jnp.bfloat16), "col", [(c, c ^ 2) for c in range(count)]
-    ).astype(jnp.float32)
-    other = lax.ppermute(total, "col", [(c, c ^ 1) for c in range(count)])
+    totals, others = [], []
+    for chunk in jnp.split(pair, 2, axis=1):
+        total = chunk + lax.ppermute(
+            chunk.astype(jnp.bfloat16), "col", [(c, c ^ 2) for c in range(count)]
+        ).astype(jnp.float32)
+        totals.append(total)
+        others.append(lax.ppermute(total, "col", [(c, c ^ 1) for c in range(count)]))
+    total, other = jnp.concatenate(totals, axis=1), jnp.concatenate(others, axis=1)
     return jnp.where(
         core, jnp.concatenate([other, total], axis=1), jnp.concatenate([total, other], axis=1)
     )

time: 224 us -> 224 us (level)
    ppermute x2 -> x4, waiting for transfers between devices: 13.8 us -> 12 us  [the longest x2 10 us: col_psum(): lax.ppermute(chunk.astype(jnp.bfloat16), 'col', [(c, c ^ 2) for c in rang...]
    unnamed x66 -> x68, local copies, waits for them, and re-layouts: 4.58 us -> 4.57 us
  transfers between devices with their start and end apart: 68 -> 70, of which waited for: 48 -> 50; matrix products, arithmetic and copies ran while one was open for 8% -> 8% of each run, Pallas kernels for 0% -> 0%
where the time goes in v15:
time: 224 us; the launch traced here: 223 us
  waiting for transfers between devices  79.2 us (35%)
  starting transfers between devices  76.9 us (34%)
  matrix products  29.8 us (13%)
  local copies, waits for them, and re-layouts  17.2 us (8%)
  other arithmetic  13.5 us (6%)
  between operations  6.8 us (3%)
    ppermute x28, starting transfers between devices, ring_gather(): part = lax.ppermute(part, axis, pairs)  30.9 us
    ppermute x28, starting transfers between devices, ring_reduce_scatter(): total = lax.ppermute(total, axis, pairs)  26.5 us
    ppermute x28, waiting for transfers between devices, ring_reduce_scatter(): total = lax.ppermute(total, axis, pairs)  25.2 us
    ppermute x28, waiting for transfers between devices, ring_gather(): part = lax.ppermute(part, axis, pairs)  17.1 us
    dot_general x1, matrix products, shards(): lax.dot_general(residual_grad, out_weight, (((1,), (1,)), ((), ())), pref...  14.4 us
    ppermute x4, waiting for transfers between devices, placed_sums(): lax.ppermute(piece, ('row', 'col'), pairs).astype(jnp.float32)  10 us
    ppermute x2, waiting for transfers between devices, col_psum(): lax.ppermute(chunk.astype(jnp.bfloat16), 'col', [(c, c ^ 2) for c in rang...  10 us
    dot_general x1, matrix products, shards(): jnp.dot(mixed, out_weight, preferred_element_type=jnp.float32)  8.8 us
  transfers between devices with their start and end apart: 70, of which 50 were waited for; matrix products, arithmetic and copies ran while one was open for 8% of the time, Pallas kernels for 0%

profile of v15, /device:TPU:2, one launch (start us, length us, event | category | flops | bytes accessed | tf_op | source)
XLA Modules:
  0.0 223.3 jit_solution(13396426598474908007)
XLA Ops:
  0.7 1.6 copy.23
  3.4 5.8 %all-to-all-start = ((bf16[128,8,256]{2,0,1:T(8,128)(2,1)}), bf16[128,8,256]{2,0,1:T(8,128)(2,1)S(1)}, u32[]{:S(2)}, u32[]{:S(2)}) async-start(bf16[128,8,256]{2,0,1:T(8,128)(2,1)} %copy.25), calls=%async_computation | async-start | bytes 1048576 | tf_op jit(solution)/shard_map/all_to_all | solution.py:24
  18.1 5.6 %all-to-all-done = bf16[128,8,256]{2,0,1:T(8,128)(2,1)S(1)} async-done(((bf16[128,8,256]{2,0,1:T(8,128)(2,1)}), bf16[128,8,256]{2,0,1:T(8,128)(2,1)S(1)}, u32[]{:S(2)}, u32[]{:S(2)}) %all-to-all-start) | async-done | bytes 524320 | tf_op jit(solution)/shard_map/all_to_all | solution.py:24
  25.6 1.5 maximum_select_fusion.1
  27.1 1.5 gather_fusion.5
  29.0 1.5 collective-permute-start.15
  30.6 1.6 gather_fusion.4
  32.5 2.0 collective-permute-start.1
  35.1 1.8 fusion.15
  39.0 1.5 collective-permute-start.16
  40.7 2.0 collective-permute-start.2
  43.3 1.6 collective-permute-done.16
  44.9 1.4 collective-permute-done.23
  46.4 1.5 collective-permute-start.17
  48.4 1.7 collective-permute-start.3
  51.4 1.9 collective-permute-done.24
  53.3 1.3 collective-permute-start.18
  55.5 1.6 collective-permute-start.4
  58.4 2.8 %collective-permute-done.25 = bf16[128,512]{1,0:T(8,128)(2,1)S(1)} collective-permute-done((bf16[128,512]{1,0:T(8,128)(2,1)S(1)}, bf16[128,512]{1,0:T(8,128)(2,1)S(1)}, u32[]{:S(2)}, u32[]{:S(2)}) %collective-permute-start.25) | collective-permute-done | bytes 131104 | tf_op jit(solution)/shard_map/ppermute | solution.py:136
  63.5 1.4 collective-permute-start.5
  65.6 1.8 collective-permute-done.19
  67.3 2.8 %collective-permute-done.26 = bf16[128,512]{1,0:T(8,128)(2,1)S(1)} collective-permute-done((bf16[128,512]{1,0:T(8,128)(2,1)S(1)}, bf16[128,512]{1,0:T(8,128)(2,1)S(1)}, u32[]{:S(2)}, u32[]{:S(2)}) %collective-permute-start.26) | collective-permute-done | bytes 131104 | tf_op jit(solution)/shard_map/ppermute | solution.py:136
  74.6 2.0 collective-permute-done.20
  76.6 2.5 %collective-permute-done.27 = bf16[128,512]{1,0:T(8,128)(2,1)S(1)} collective-permute-done((bf16[128,512]{1,0:T(8,128)(2,1)S(1)}, bf16[128,512]{1,0:T(8,128)(2,1)S(1)}, u32[]{:S(2)}, u32[]{:S(2)}) %collective-permute-start.27) | collective-permute-done | bytes 131104 | tf_op jit(solution)/shard_map/ppermute | solution.py:136
  81.0 1.7 collective-permute-start.7
  84.2 1.4 collective-permute-done.28
  86.0 1.6 collective-permute-done.14
  87.8 2.5 %collective-permute-start.29 = (bf16[3,2048]{1,0:T(4,128)(2,1)S(1)}, bf16[3,2048]{1,0:T(4,128)(2,1)S(1)}, u32[]{:S(2)}, u32[]{:S(2)}) collective-permute-start(bf16[3,2048]{1,0:T(4,128)(2,1)S(1)} %pad_maximum_fusion.1), channel_id=1, source_target_pairs={{0,4},{4,8},{8,12},{12,16},{16,20},{20,24},{24,28},{1,5},{5,9},{9,... | collective-permute-start | bytes 36872 | tf_op jit(solution)/shard_map/ppermute | solution.py:13
  90.3 1.2 collective-permute-done.29
  92.7 8.8 %convolution_convert_fusion = bf16[128,4096]{1,0:T(8,128)(2,1)S(1)} fusion(bf16[2048,4096]{1,0:T(8,128)(2,1)} %param.27, bf16[128,2048]{1,0:T(8,128)(2,1)S(1)} %copy-done.17, f32[128,2048]{1,0:T(8,128)S(1)} %fusion.9), kind=kOutput, calls=%fused_computation.6 | convolution fusion | flops 2150891520 | bytes 19398656 | tf_op jit(solution)/shard_map/dot_general | solution.py:214
  101.7 1.9 collective-permute-done.30
  105.3 1.5 collective-permute-start.33
  109.0 5.1 %collective-permute-done.31 = bf16[128,1024]{1,0:T(8,128)(2,1)S(1)} collective-permute-done((bf16[128,1024]{1,0:T(8,128)(2,1)}, bf16[128,1024]{1,0:T(8,128)(2,1)S(1)}, u32[]{:S(2)}, u32[]{:S(2)}) %collective-permute-start.31) | collective-permute-done | bytes 262176 | tf_op jit(solution)/shard_map/ppermute | solution.py:154
  114.1 4.9 %collective-permute-done.33 = bf16[128,1024]{1,0:T(8,128)(2,1)} collective-permute-done((bf16[128,1024]{1,0:T(8,128)(2,1)}, bf16[128,1024]{1,0:T(8,128)(2,1)}, u32[]{:S(2)}, u32[]{:S(2)}) %collective-permute-start.33) | collective-permute-done | bytes 262176 | tf_op jit(solution)/shard_map/ppermute | solution.py:154
  120.8 1.3 collective-permute-done.34
  122.8 1.5 maximum_select_fusion
  124.4 14.4 %multiply_multiply_fusion.2 = (f32[128,2048]{1,0:T(8,128)}, f32[128,2048]{1,0:T(8,128)}, bf16[128,2048]{1,0:T(8,128)(2,1)}) fusion(f32[128]{0:T(128)S(1)} %get-tuple-element.127, f32[2048]{0:T(1024)S(1)} %bitcast.323, f32[128,2048]{1,0:T(8,128)S(1)} %copy-done.10, bf16[128,2048]{1,0:T(8,128)(2,1)} %param.25, bf16[2048,4096]{1,0:T(8,128)(2,1)} %param.27, ...), kind=kOutput, calls=%fused_computation.43 | convolution fusion | flops 2155872256 | bytes 24126464 | tf_op jit(solution)/shard_map/dot_general | solution.py:227
  138.8 1.5 multiply_multiply_fusion.1
  142.2 1.3 collective-permute-start.35
  145.3 3.1 %collective-permute-done.35 = f32[3,2048]{1,0:T(4,128)S(1)} collective-permute-done((f32[3,2048]{1,0:T(4,128)S(1)}, f32[3,2048]{1,0:T(4,128)S(1)}, u32[]{:S(2)}, u32[]{:S(2)}) %collective-permute-start.35) | collective-permute-done | bytes 24608 | tf_op jit(solution)/shard_map/ppermute | solution.py:13
  148.9 3.2 %collective-permute-start.57 = (bf16[128,512]{1,0:T(8,128)(2,1)S(1)}, bf16[128,512]{1,0:T(8,128)(2,1)S(1)}, u32[]{:S(2)}, u32[]{:S(2)}) collective-permute-start(bf16[128,512]{1,0:T(8,128)(2,1)S(1)} %get-tuple-element.107), channel_id=1, source_target_pairs={{8,0},{16,8},{24,16},{28,24},{20,28},{12,20},{4,12},{0,4},{9,1},{1... | collective-permute-start | bytes 393224 | tf_op jit(solution)/shard_map/ppermute | solution.py:103
  152.1 1.4 collective-permute-start.50
  154.8 2.3 %collective-permute-done.57 = bf16[128,512]{1,0:T(8,128)(2,1)S(1)} collective-permute-done((bf16[128,512]{1,0:T(8,128)(2,1)S(1)}, bf16[128,512]{1,0:T(8,128)(2,1)S(1)}, u32[]{:S(2)}, u32[]{:S(2)}) %collective-permute-start.57) | collective-permute-done | bytes 131104 | tf_op jit(solution)/shard_map/ppermute | solution.py:103
  157.1 1.4 collective-permute-start.58
  158.4 1.4 collective-permute-done.50
  159.9 1.4 collective-permute-start.51
  161.9 1.8 collective-permute-start.37
  164.1 2.2 collective-permute-done.51
  166.3 1.3 collective-permute-start.52
  168.8 1.8 collective-permute-start.38
  171.1 1.7 collective-permute-done.52
  173.6 1.2 collective-permute-start.46
  174.9 1.4 collective-permute-done.38
  181.2 1.6 collective-permute-done.39
  185.6 1.3 collective-permute-start.55
  188.4 1.4 collective-permute-start.41
  191.5 1.4 collective-permute-start.56
  201.4 1.8 collective-permute-done.64
  204.1 3.8 %collective-permute-start.65 = (bf16[128,512]{1,0:T(8,128)(2,1)S(1)}, bf16[128,512]{1,0:T(8,128)(2,1)S(1)}, u32[]{:S(2)}, u32[]{:S(2)}) collective-permute-start(bf16[128,512]{1,0:T(8,128)(2,1)S(1)} %get-tuple-element.115), channel_id=1, source_target_pairs={{0,0},{1,8},{2,16},{3,24},{4,4},{5,12},{6,20},{7,28},{8,1},{9,9},{... | collective-permute-start | bytes 393224 | tf_op jit(solution)/shard_map/ppermute | solution.py:73
  208.0 2.6 %collective-permute-start.67 = (bf16[128,512]{1,0:T(8,128)(2,1)S(1)}, bf16[128,512]{1,0:T(8,128)(2,1)S(1)}, u32[]{:S(2)}, u32[]{:S(2)}) collective-permute-start(bf16[128,512]{1,0:T(8,128)(2,1)S(1)} %get-tuple-element.114), channel_id=1, source_target_pairs={{0,4},{1,12},{2,20},{3,28},{4,0},{5,8},{6,16},{7,24},{8,5},{9,13},... | collective-permute-start | bytes 393224 | tf_op jit(solution)/shard_map/ppermute | solution.py:73
  210.7 1.8 dynamic-slice_convert_fusion
  212.5 1.7 collective-permute-done.66
  214.2 4.8 %collective-permute-done.65 = bf16[128,512]{1,0:T(8,128)(2,1)S(1)} collective-permute-done((bf16[128,512]{1,0:T(8,128)(2,1)S(1)}, bf16[128,512]{1,0:T(8,128)(2,1)S(1)}, u32[]{:S(2)}, u32[]{:S(2)}) %collective-permute-start.65) | collective-permute-done | bytes 131104 | tf_op jit(solution)/shard_map/ppermute | solution.py:73
  219.9 2.6 %collective-permute-done.67 = bf16[128,512]{1,0:T(8,128)(2,1)S(1)} collective-permute-done((bf16[128,512]{1,0:T(8,128)(2,1)S(1)}, bf16[128,512]{1,0:T(8,128)(2,1)S(1)}, u32[]{:S(2)}, u32[]{:S(2)}) %collective-permute-start.67) | collective-permute-done | bytes 131104 | tf_op jit(solution)/shard_map/ppermute | solution.py:73
  (233 shorter events, 64.7 us)
Async XLA Ops:
  3.4 20.3 %all-to-all-start = ((bf16[128,8,256]{2,0,1:T(8,128)(2,1)}), bf16[128,8,256]{2,0,1:T(8,128)(2,1)S(1)}, u32[]{:S(2)}, u32[]{:S(2)}) async-start(bf16[128,8,256]{2,0,1:T(8,128)(2,1)} %copy.25), calls=%async_computation | async-start | bytes 1048576 | tf_op jit(solution)/shard_map/all_to_all | solution.py:24
  29.0 9.0 %collective-permute-start.15 = (bf16[128,512]{1,0:T(8,128)(2,1)S(1)}, bf16[128,512]{1,0:T(8,128)(2,1)S(1)}, u32[]{:S(2)}, u32[]{:S(2)}) collective-permute-start(bf16[128,512]{1,0:T(8,128)(2,1)S(1)} %get-tuple-element.120), channel_id=1, source_target_pairs={{8,0},{16,8},{24,16},{28,24},{20,28},{12,20},{4,12},{0,4},{9,1},{1... | collective-permute-start | bytes 393224 | tf_op jit(solution)/shard_map/ppermute | solution.py:136
  30.5 7.5 %collective-permute-start.22 = (bf16[128,512]{1,0:T(8,128)(2,1)S(1)}, bf16[128,512]{1,0:T(8,128)(2,1)}, u32[]{:S(2)}, u32[]{:S(2)}) collective-permute-start(bf16[128,512]{1,0:T(8,128)(2,1)S(1)} %get-tuple-element.121), channel_id=1, source_target_pairs={{8,0},{16,8},{24,16},{28,24},{20,28},{12,20},{4,12},{0,4},{9,1},{1... | collective-permute-start | bytes 393224 | tf_op jit(solution)/shard_map/ppermute | solution.py:136
  32.5 8.1 %collective-permute-start.1 = (bf16[128,512]{1,0:T(8,128)(2,1)S(1)}, bf16[128,512]{1,0:T(8,128)(2,1)S(1)}, u32[]{:S(2)}, u32[]{:S(2)}) collective-permute-start(bf16[128,512]{1,0:T(8,128)(2,1)S(1)} %get-tuple-element.118), channel_id=1, source_target_pairs={{0,8},{8,16},{16,24},{24,28},{28,20},{20,12},{12,4},{4,0},{1,9},{9... | collective-permute-start | bytes 393224 | tf_op jit(solution)/shard_map/ppermute | solution.py:136
  34.5 6.1 %collective-permute-start.8 = (bf16[128,512]{1,0:T(8,128)(2,1)S(1)}, bf16[128,512]{1,0:T(8,128)(2,1)S(1)}, u32[]{:S(2)}, u32[]{:S(2)}) collective-permute-start(bf16[128,512]{1,0:T(8,128)(2,1)S(1)} %get-tuple-element.119), channel_id=1, source_target_pairs={{0,8},{8,16},{16,24},{24,28},{28,20},{20,12},{12,4},{4,0},{1,9},{9... | collective-permute-start | bytes 393224 | tf_op jit(solution)/shard_map/ppermute | solution.py:136
  39.0 5.9 %collective-permute-start.16 = (bf16[128,512]{1,0:T(8,128)(2,1)S(1)}, bf16[128,512]{1,0:T(8,128)(2,1)S(1)}, u32[]{:S(2)}, u32[]{:S(2)}) collective-permute-start(bf16[128,512]{1,0:T(8,128)(2,1)S(1)} %get-tuple-element.93), channel_id=1, source_target_pairs={{8,0},{16,8},{24,16},{28,24},{20,28},{12,20},{4,12},{0,4},{9,1},{1... | collective-permute-start | bytes 393224 | tf_op jit(solution)/shard_map/ppermute | solution.py:136
  40.5 5.8 %collective-permute-start.23 = (bf16[128,512]{1,0:T(8,128)(2,1)S(1)}, bf16[128,512]{1,0:T(8,128)(2,1)S(1)}, u32[]{:S(2)}, u32[]{:S(2)}) collective-permute-start(bf16[128,512]{1,0:T(8,128)(2,1)S(1)} %get-tuple-element.94), channel_id=1, source_target_pairs={{8,0},{16,8},{24,16},{28,24},{20,28},{12,20},{4,12},{0,4},{9,1},{1... | collective-permute-start | bytes 393224 | tf_op jit(solution)/shard_map/ppermute | solution.py:136
  40.7 7.6 %collective-permute-start.2 = (bf16[128,512]{1,0:T(8,128)(2,1)S(1)}, bf16[128,512]{1,0:T(8,128)(2,1)S(1)}, u32[]{:S(2)}, u32[]{:S(2)}) collective-permute-start(bf16[128,512]{1,0:T(8,128)(2,1)S(1)} %get-tuple-element.79), channel_id=1, source_target_pairs={{0,8},{8,16},{16,24},{24,28},{28,20},{20,12},{12,4},{4,0},{1,9},{9... | collective-permute-start | bytes 393224 | tf_op jit(solution)/shard_map/ppermute | solution.py:136
  42.7 5.6 %collective-permute-start.9 = (bf16[128,512]{1,0:T(8,128)(2,1)S(1)}, bf16[128,512]{1,0:T(8,128)(2,1)S(1)}, u32[]{:S(2)}, u32[]{:S(2)}) collective-permute-start(bf16[128,512]{1,0:T(8,128)(2,1)S(1)} %get-tuple-element.80), channel_id=1, source_target_pairs={{0,8},{8,16},{16,24},{24,28},{28,20},{20,12},{12,4},{4,0},{1,9},{9... | collective-permute-start | bytes 393224 | tf_op jit(solution)/shard_map/ppermute | solution.py:136
  46.4 5.0 %collective-permute-start.17 = (bf16[128,512]{1,0:T(8,128)(2,1)S(1)}, bf16[128,512]{1,0:T(8,128)(2,1)S(1)}, u32[]{:S(2)}, u32[]{:S(2)}) collective-permute-start(bf16[128,512]{1,0:T(8,128)(2,1)S(1)} %get-tuple-element.91), channel_id=1, source_target_pairs={{8,0},{16,8},{24,16},{28,24},{20,28},{12,20},{4,12},{0,4},{9,1},{1... | collective-permute-start | bytes 393224 | tf_op jit(solution)/shard_map/ppermute | solution.py:136
  47.9 5.4 %collective-permute-start.24 = (bf16[128,512]{1,0:T(8,128)(2,1)S(1)}, bf16[128,512]{1,0:T(8,128)(2,1)S(1)}, u32[]{:S(2)}, u32[]{:S(2)}) collective-permute-start(bf16[128,512]{1,0:T(8,128)(2,1)S(1)} %get-tuple-element.92), channel_id=1, source_target_pairs={{8,0},{16,8},{24,16},{28,24},{20,28},{12,20},{4,12},{0,4},{9,1},{1... | collective-permute-start | bytes 393224 | tf_op jit(solution)/shard_map/ppermute | solution.py:136
  48.4 6.6 %collective-permute-start.3 = (bf16[128,512]{1,0:T(8,128)(2,1)S(1)}, bf16[128,512]{1,0:T(8,128)(2,1)S(1)}, u32[]{:S(2)}, u32[]{:S(2)}) collective-permute-start(bf16[128,512]{1,0:T(8,128)(2,1)S(1)} %get-tuple-element.77), channel_id=1, source_target_pairs={{0,8},{8,16},{16,24},{24,28},{28,20},{20,12},{12,4},{4,0},{1,9},{9... | collective-permute-start | bytes 393224 | tf_op jit(solution)/shard_map/ppermute | solution.py:136
  50.1 5.3 %collective-permute-start.10 = (bf16[128,512]{1,0:T(8,128)(2,1)S(1)}, bf16[128,512]{1,0:T(8,128)(2,1)S(1)}, u32[]{:S(2)}, u32[]{:S(2)}) collective-permute-start(bf16[128,512]{1,0:T(8,128)(2,1)S(1)} %get-tuple-element.78), channel_id=1, source_target_pairs={{0,8},{8,16},{16,24},{24,28},{28,20},{20,12},{12,4},{4,0},{1,9},{9... | collective-permute-start | bytes 393224 | tf_op jit(solution)/shard_map/ppermute | solution.py:136
  53.3 5.1 %collective-permute-start.18 = (bf16[128,512]{1,0:T(8,128)(2,1)S(1)}, bf16[128,512]{1,0:T(8,128)(2,1)S(1)}, u32[]{:S(2)}, u32[]{:S(2)}) collective-permute-start(bf16[128,512]{1,0:T(8,128)(2,1)S(1)} %get-tuple-element.89), channel_id=1, source_target_pairs={{8,0},{16,8},{24,16},{28,24},{20,28},{12,20},{4,12},{0,4},{9,1},{1... | collective-permute-start | bytes 393224 | tf_op jit(solution)/shard_map/ppermute | solution.py:136
  54.7 6.6 %collective-permute-start.25 = (bf16[128,512]{1,0:T(8,128)(2,1)S(1)}, bf16[128,512]{1,0:T(8,128)(2,1)S(1)}, u32[]{:S(2)}, u32[]{:S(2)}) collective-permute-start(bf16[128,512]{1,0:T(8,128)(2,1)S(1)} %get-tuple-element.90), channel_id=1, source_target_pairs={{8,0},{16,8},{24,16},{28,24},{20,28},{12,20},{4,12},{0,4},{9,1},{1... | collective-permute-start | bytes 393224 | tf_op jit(solution)/shard_map/ppermute | solution.py:136
  55.5 7.1 %collective-permute-start.4 = (bf16[128,512]{1,0:T(8,128)(2,1)S(1)}, bf16[128,512]{1,0:T(8,128)(2,1)S(1)}, u32[]{:S(2)}, u32[]{:S(2)}) collective-permute-start(bf16[128,512]{1,0:T(8,128)(2,1)S(1)} %get-tuple-element.75), channel_id=1, source_target_pairs={{0,8},{8,16},{16,24},{24,28},{28,20},{20,12},{12,4},{4,0},{1,9},{9... | collective-permute-start | bytes 393224 | tf_op jit(solution)/shard_map/ppermute | solution.py:136
  57.1 6.3 %collective-permute-start.11 = (bf16[128,512]{1,0:T(8,128)(2,1)S(1)}, bf16[128,512]{1,0:T(8,128)(2,1)S(1)}, u32[]{:S(2)}, u32[]{:S(2)}) collective-permute-start(bf16[128,512]{1,0:T(8,128)(2,1)S(1)} %get-tuple-element.76), channel_id=1, source_target_pairs={{0,8},{8,16},{16,24},{24,28},{28,20},{20,12},{12,4},{4,0},{1,9},{9... | collective-permute-start | bytes 393224 | tf_op jit(solution)/shard_map/ppermute | solution.py:136
  61.3 6.0 %collective-permute-start.19 = (bf16[128,512]{1,0:T(8,128)(2,1)S(1)}, bf16[128,512]{1,0:T(8,128)(2,1)S(1)}, u32[]{:S(2)}, u32[]{:S(2)}) collective-permute-start(bf16[128,512]{1,0:T(8,128)(2,1)S(1)} %get-tuple-element.87), channel_id=1, source_target_pairs={{8,0},{16,8},{24,16},{28,24},{20,28},{12,20},{4,12},{0,4},{9,1},{1... | collective-permute-start | bytes 393224 | tf_op jit(solution)/shard_map/ppermute | solution.py:136
  62.5 7.6 %collective-permute-start.26 = (bf16[128,512]{1,0:T(8,128)(2,1)S(1)}, bf16[128,512]{1,0:T(8,128)(2,1)S(1)}, u32[]{:S(2)}, u32[]{:S(2)}) collective-permute-start(bf16[128,512]{1,0:T(8,128)(2,1)S(1)} %get-tuple-element.88), channel_id=1, source_target_pairs={{8,0},{16,8},{24,16},{28,24},{20,28},{12,20},{4,12},{0,4},{9,1},{1... | collective-permute-start | bytes 393224 | tf_op jit(solution)/shard_map/ppermute | solution.py:136
  63.5 7.8 %collective-permute-start.5 = (bf16[128,512]{1,0:T(8,128)(2,1)S(1)}, bf16[128,512]{1,0:T(8,128)(2,1)S(1)}, u32[]{:S(2)}, u32[]{:S(2)}) collective-permute-start(bf16[128,512]{1,0:T(8,128)(2,1)S(1)} %get-tuple-element.73), channel_id=1, source_target_pairs={{0,8},{8,16},{16,24},{24,28},{28,20},{20,12},{12,4},{4,0},{1,9},{9... | collective-permute-start | bytes 393224 | tf_op jit(solution)/shard_map/ppermute | solution.py:136
  64.9 7.5 %collective-permute-start.12 = (bf16[128,512]{1,0:T(8,128)(2,1)S(1)}, bf16[128,512]{1,0:T(8,128)(2,1)S(1)}, u32[]{:S(2)}, u32[]{:S(2)}) collective-permute-start(bf16[128,512]{1,0:T(8,128)(2,1)S(1)} %get-tuple-element.74), channel_id=1, source_target_pairs={{0,8},{8,16},{16,24},{24,28},{28,20},{20,12},{12,4},{4,0},{1,9},{9... | collective-permute-start | bytes 393224 | tf_op jit(solution)/shard_map/ppermute | solution.py:136
  70.2 6.3 %collective-permute-start.20 = (bf16[128,512]{1,0:T(8,128)(2,1)S(1)}, bf16[128,512]{1,0:T(8,128)(2,1)S(1)}, u32[]{:S(2)}, u32[]{:S(2)}) collective-permute-start(bf16[128,512]{1,0:T(8,128)(2,1)S(1)} %get-tuple-element.85), channel_id=1, source_target_pairs={{8,0},{16,8},{24,16},{28,24},{20,28},{12,20},{4,12},{0,4},{9,1},{1... | collective-permute-start | bytes 393224 | tf_op jit(solution)/shard_map/ppermute | solution.py:136
  71.3 7.8 %collective-permute-start.27 = (bf16[128,512]{1,0:T(8,128)(2,1)S(1)}, bf16[128,512]{1,0:T(8,128)(2,1)S(1)}, u32[]{:S(2)}, u32[]{:S(2)}) collective-permute-start(bf16[128,512]{1,0:T(8,128)(2,1)S(1)} %get-tuple-element.86), channel_id=1, source_target_pairs={{8,0},{16,8},{24,16},{28,24},{20,28},{12,20},{4,12},{0,4},{9,1},{1... | collective-permute-start | bytes 393224 | tf_op jit(solution)/shard_map/ppermute | solution.py:136
  72.6 8.1 %collective-permute-start.6 = (bf16[128,512]{1,0:T(8,128)(2,1)S(1)}, bf16[128,512]{1,0:T(8,128)(2,1)S(1)}, u32[]{:S(2)}, u32[]{:S(2)}) collective-permute-start(bf16[128,512]{1,0:T(8,128)(2,1)S(1)} %get-tuple-element.71), channel_id=1, source_target_pairs={{0,8},{8,16},{16,24},{24,28},{28,20},{20,12},{12,4},{4,0},{1,9},{9... | collective-permute-start | bytes 393224 | tf_op jit(solution)/shard_map/ppermute | solution.py:136
  73.7 7.3 %collective-permute-start.13 = (bf16[128,512]{1,0:T(8,128)(2,1)S(1)}, bf16[128,512]{1,0:T(8,128)(2,1)S(1)}, u32[]{:S(2)}, u32[]{:S(2)}) collective-permute-start(bf16[128,512]{1,0:T(8,128)(2,1)S(1)} %get-tuple-element.72), channel_id=1, source_target_pairs={{0,8},{8,16},{16,24},{24,28},{28,20},{20,12},{12,4},{4,0},{1,9},{9... | collective-permute-start | bytes 393224 | tf_op jit(solution)/shard_map/ppermute | solution.py:136
  79.1 5.0 %collective-permute-start.21 = (bf16[128,512]{1,0:T(8,128)(2,1)S(1)}, bf16[128,512]{1,0:T(8,128)(2,1)S(1)}, u32[]{:S(2)}, u32[]{:S(2)}) collective-permute-start(bf16[128,512]{1,0:T(8,128)(2,1)S(1)} %get-tuple-element.83), channel_id=1, source_target_pairs={{8,0},{16,8},{24,16},{28,24},{20,28},{12,20},{4,12},{0,4},{9,1},{1... | collective-permute-start | bytes 393224 | tf_op jit(solution)/shard_map/ppermute | solution.py:136
  80.3 5.2 %collective-permute-start.28 = (bf16[128,512]{1,0:T(8,128)(2,1)S(1)}, bf16[128,512]{1,0:T(8,128)(2,1)S(1)}, u32[]{:S(2)}, u32[]{:S(2)}) collective-permute-start(bf16[128,512]{1,0:T(8,128)(2,1)S(1)} %get-tuple-element.84), channel_id=1, source_target_pairs={{8,0},{16,8},{24,16},{28,24},{20,28},{12,20},{4,12},{0,4},{9,1},{1... | collective-permute-start | bytes 393224 | tf_op jit(solution)/shard_map/ppermute | solution.py:136
  81.0 5.0 %collective-permute-start.7 = (bf16[128,512]{1,0:T(8,128)(2,1)S(1)}, bf16[128,512]{1,0:T(8,128)(2,1)S(1)}, u32[]{:S(2)}, u32[]{:S(2)}) collective-permute-start(bf16[128,512]{1,0:T(8,128)(2,1)S(1)} %get-tuple-element.69), channel_id=1, source_target_pairs={{0,8},{8,16},{16,24},{24,28},{28,20},{20,12},{12,4},{4,0},{1,9},{9... | collective-permute-start | bytes 393224 | tf_op jit(solution)/shard_map/ppermute | solution.py:136
  82.7 5.0 %collective-permute-start.14 = (bf16[128,512]{1,0:T(8,128)(2,1)S(1)}, bf16[128,512]{1,0:T(8,128)(2,1)S(1)}, u32[]{:S(2)}, u32[]{:S(2)}) collective-permute-start(bf16[128,512]{1,0:T(8,128)(2,1)S(1)} %get-tuple-element.70), channel_id=1, source_target_pairs={{0,8},{8,16},{16,24},{24,28},{28,20},{20,12},{12,4},{4,0},{1,9},{9... | collective-permute-start | bytes 393224 | tf_op jit(solution)/shard_map/ppermute | solution.py:136
  104.7 9.4 %collective-permute-start.31 = (bf16[128,1024]{1,0:T(8,128)(2,1)}, bf16[128,1024]{1,0:T(8,128)(2,1)S(1)}, u32[]{:S(2)}, u32[]{:S(2)}) collective-permute-start(bf16[128,1024]{1,0:T(8,128)(2,1)} %get-tuple-element.100), channel_id=1, source_target_pairs={{0,2},{1,3},{2,0},{3,1},{4,6},{5,7},{6,4},{7,5},{8,10},{9,11},{10,... | collective-permute-start | bytes 786440 | tf_op jit(solution)/shard_map/ppermute | solution.py:154
  105.3 13.7 %collective-permute-start.33 = (bf16[128,1024]{1,0:T(8,128)(2,1)}, bf16[128,1024]{1,0:T(8,128)(2,1)}, u32[]{:S(2)}, u32[]{:S(2)}) collective-permute-start(bf16[128,1024]{1,0:T(8,128)(2,1)} %get-tuple-element.101), channel_id=1, source_target_pairs={{0,2},{1,3},{2,0},{3,1},{4,6},{5,7},{6,4},{7,5},{8,10},{9,11},{10,... | collective-permute-start | bytes 786440 | tf_op jit(solution)/shard_map/ppermute | solution.py:154
  142.2 6.3 %collective-permute-start.35 = (f32[3,2048]{1,0:T(4,128)S(1)}, f32[3,2048]{1,0:T(4,128)S(1)}, u32[]{:S(2)}, u32[]{:S(2)}) collective-permute-start(f32[3,2048]{1,0:T(4,128)S(1)} %slice_add_fusion), channel_id=1, source_target_pairs={{4,0},{8,4},{12,8},{16,12},{20,16},{24,20},{28,24},{5,1},{9,5},{13... | collective-permute-start | bytes 73736 | tf_op jit(solution)/shard_map/ppermute | solution.py:13
  148.9 8.2 %collective-permute-start.57 = (bf16[128,512]{1,0:T(8,128)(2,1)S(1)}, bf16[128,512]{1,0:T(8,128)(2,1)S(1)}, u32[]{:S(2)}, u32[]{:S(2)}) collective-permute-start(bf16[128,512]{1,0:T(8,128)(2,1)S(1)} %get-tuple-element.107), channel_id=1, source_target_pairs={{8,0},{16,8},{24,16},{28,24},{20,28},{12,20},{4,12},{0,4},{9,1},{1... | collective-permute-start | bytes 393224 | tf_op jit(solution)/shard_map/ppermute | solution.py:103
  152.1 7.8 %collective-permute-start.50 = (bf16[128,512]{1,0:T(8,128)(2,1)S(1)}, bf16[128,512]{1,0:T(8,128)(2,1)S(1)}, u32[]{:S(2)}, u32[]{:S(2)}) collective-permute-start(bf16[128,512]{1,0:T(8,128)(2,1)S(1)} %get-tuple-element.108), channel_id=1, source_target_pairs={{8,0},{16,8},{24,16},{28,24},{20,28},{12,20},{4,12},{0,4},{9,1},{1... | collective-permute-start | bytes 393224 | tf_op jit(solution)/shard_map/ppermute | solution.py:103
  153.5 7.7 %collective-permute-start.43 = (bf16[128,512]{1,0:T(8,128)(2,1)S(1)}, bf16[128,512]{1,0:T(8,128)(2,1)S(1)}, u32[]{:S(2)}, u32[]{:S(2)}) collective-permute-start(bf16[128,512]{1,0:T(8,128)(2,1)S(1)} %get-tuple-element.109), channel_id=1, source_target_pairs={{0,8},{8,16},{16,24},{24,28},{28,20},{20,12},{12,4},{4,0},{1,9},{9... | collective-permute-start | bytes 393224 | tf_op jit(solution)/shard_map/ppermute | solution.py:103
  154.1 7.8 %collective-permute-start.36 = (bf16[128,512]{1,0:T(8,128)(2,1)S(1)}, bf16[128,512]{1,0:T(8,128)(2,1)S(1)}, u32[]{:S(2)}, u32[]{:S(2)}) collective-permute-start(bf16[128,512]{1,0:T(8,128)(2,1)S(1)} %get-tuple-element.106), channel_id=1, source_target_pairs={{0,8},{8,16},{16,24},{24,28},{28,20},{20,12},{12,4},{4,0},{1,9},{9... | collective-permute-start | bytes 393224 | tf_op jit(solution)/shard_map/ppermute | solution.py:103
  157.1 6.6 %collective-permute-start.58 = (bf16[128,512]{1,0:T(8,128)(2,1)S(1)}, bf16[128,512]{1,0:T(8,128)(2,1)S(1)}, u32[]{:S(2)}, u32[]{:S(2)}) collective-permute-start(bf16[128,512]{1,0:T(8,128)(2,1)S(1)} %collective-permute-done.57), channel_id=1, source_target_pairs={{8,0},{16,8},{24,16},{28,24},{20,28},{12,20},{4,12},{0,4},{9,1},{1... | collective-permute-start | bytes 393224 | tf_op jit(solution)/shard_map/ppermute | solution.py:103
  159.9 6.4 %collective-permute-start.51 = (bf16[128,512]{1,0:T(8,128)(2,1)S(1)}, bf16[128,512]{1,0:T(8,128)(2,1)S(1)}, u32[]{:S(2)}, u32[]{:S(2)}) collective-permute-start(bf16[128,512]{1,0:T(8,128)(2,1)S(1)} %collective-permute-done.50), channel_id=1, source_target_pairs={{8,0},{16,8},{24,16},{28,24},{20,28},{12,20},{4,12},{0,4},{9,1},{1... | collective-permute-start | bytes 393224 | tf_op jit(solution)/shard_map/ppermute | solution.py:103
  161.2 6.3 %collective-permute-start.44 = (bf16[128,512]{1,0:T(8,128)(2,1)S(1)}, bf16[128,512]{1,0:T(8,128)(2,1)S(1)}, u32[]{:S(2)}, u32[]{:S(2)}) collective-permute-start(bf16[128,512]{1,0:T(8,128)(2,1)S(1)} %collective-permute-done.43), channel_id=1, source_target_pairs={{0,8},{8,16},{16,24},{24,28},{28,20},{20,12},{12,4},{4,0},{1,9},{9... | collective-permute-start | bytes 393224 | tf_op jit(solution)/shard_map/ppermute | solution.py:103
  161.9 6.9 %collective-permute-start.37 = (bf16[128,512]{1,0:T(8,128)(2,1)S(1)}, bf16[128,512]{1,0:T(8,128)(2,1)S(1)}, u32[]{:S(2)}, u32[]{:S(2)}) collective-permute-start(bf16[128,512]{1,0:T(8,128)(2,1)S(1)} %collective-permute-done.36), channel_id=1, source_target_pairs={{0,8},{8,16},{16,24},{24,28},{28,20},{20,12},{12,4},{4,0},{1,9},{9... | collective-permute-start | bytes 393224 | tf_op jit(solution)/shard_map/ppermute | solution.py:103
  163.7 6.9 %collective-permute-start.59 = (bf16[128,512]{1,0:T(8,128)(2,1)S(1)}, bf16[128,512]{1,0:T(8,128)(2,1)S(1)}, u32[]{:S(2)}, u32[]{:S(2)}) collective-permute-start(bf16[128,512]{1,0:T(8,128)(2,1)S(1)} %collective-permute-done.58), channel_id=1, source_target_pairs={{8,0},{16,8},{24,16},{28,24},{20,28},{12,20},{4,12},{0,4},{9,1},{1... | collective-permute-start | bytes 393224 | tf_op jit(solution)/shard_map/ppermute | solution.py:103
  166.3 6.5 %collective-permute-start.52 = (bf16[128,512]{1,0:T(8,128)(2,1)S(1)}, bf16[128,512]{1,0:T(8,128)(2,1)S(1)}, u32[]{:S(2)}, u32[]{:S(2)}) collective-permute-start(bf16[128,512]{1,0:T(8,128)(2,1)S(1)} %collective-permute-done.51), channel_id=1, source_target_pairs={{8,0},{16,8},{24,16},{28,24},{20,28},{12,20},{4,12},{0,4},{9,1},{1... | collective-permute-start | bytes 393224 | tf_op jit(solution)/shard_map/ppermute | solution.py:103
  167.6 6.0 %collective-permute-start.45 = (bf16[128,512]{1,0:T(8,128)(2,1)S(1)}, bf16[128,512]{1,0:T(8,128)(2,1)S(1)}, u32[]{:S(2)}, u32[]{:S(2)}) collective-permute-start(bf16[128,512]{1,0:T(8,128)(2,1)S(1)} %collective-permute-done.44), channel_id=1, source_target_pairs={{0,8},{8,16},{16,24},{24,28},{28,20},{20,12},{12,4},{4,0},{1,9},{9... | collective-permute-start | bytes 393224 | tf_op jit(solution)/shard_map/ppermute | solution.py:103
  168.8 7.5 %collective-permute-start.38 = (bf16[128,512]{1,0:T(8,128)(2,1)S(1)}, bf16[128,512]{1,0:T(8,128)(2,1)S(1)}, u32[]{:S(2)}, u32[]{:S(2)}) collective-permute-start(bf16[128,512]{1,0:T(8,128)(2,1)S(1)} %collective-permute-done.37), channel_id=1, source_target_pairs={{0,8},{8,16},{16,24},{24,28},{28,20},{20,12},{12,4},{4,0},{1,9},{9... | collective-permute-start | bytes 393224 | tf_op jit(solution)/shard_map/ppermute | solution.py:103
  170.6 6.8 %collective-permute-start.60 = (bf16[128,512]{1,0:T(8,128)(2,1)S(1)}, bf16[128,512]{1,0:T(8,128)(2,1)S(1)}, u32[]{:S(2)}, u32[]{:S(2)}) collective-permute-start(bf16[128,512]{1,0:T(8,128)(2,1)S(1)} %collective-permute-done.59), channel_id=1, source_target_pairs={{8,0},{16,8},{24,16},{28,24},{20,28},{12,20},{4,12},{0,4},{9,1},{1... | collective-permute-start | bytes 393224 | tf_op jit(solution)/shard_map/ppermute | solution.py:103
  172.8 6.4 %collective-permute-start.53 = (bf16[128,512]{1,0:T(8,128)(2,1)S(1)}, bf16[128,512]{1,0:T(8,128)(2,1)S(1)}, u32[]{:S(2)}, u32[]{:S(2)}) collective-permute-start(bf16[128,512]{1,0:T(8,128)(2,1)S(1)} %collective-permute-done.52), channel_id=1, source_target_pairs={{8,0},{16,8},{24,16},{28,24},{20,28},{12,20},{4,12},{0,4},{9,1},{1... | collective-permute-start | bytes 393224 | tf_op jit(solution)/shard_map/ppermute | solution.py:103
  173.6 6.4 %collective-permute-start.46 = (bf16[128,512]{1,0:T(8,128)(2,1)S(1)}, bf16[128,512]{1,0:T(8,128)(2,1)S(1)}, u32[]{:S(2)}, u32[]{:S(2)}) collective-permute-start(bf16[128,512]{1,0:T(8,128)(2,1)S(1)} %collective-permute-done.45), channel_id=1, source_target_pairs={{0,8},{8,16},{16,24},{24,28},{28,20},{20,12},{12,4},{4,0},{1,9},{9... | collective-permute-start | bytes 393224 | tf_op jit(solution)/shard_map/ppermute | solution.py:103
  176.3 6.6 %collective-permute-start.39 = (bf16[128,512]{1,0:T(8,128)(2,1)S(1)}, bf16[128,512]{1,0:T(8,128)(2,1)S(1)}, u32[]{:S(2)}, u32[]{:S(2)}) collective-permute-start(bf16[128,512]{1,0:T(8,128)(2,1)S(1)} %collective-permute-done.38), channel_id=1, source_target_pairs={{0,8},{8,16},{16,24},{24,28},{28,20},{20,12},{12,4},{4,0},{1,9},{9... | collective-permute-start | bytes 393224 | tf_op jit(solution)/shard_map/ppermute | solution.py:103
  177.4 6.4 %collective-permute-start.61 = (bf16[128,512]{1,0:T(8,128)(2,1)S(1)}, bf16[128,512]{1,0:T(8,128)(2,1)S(1)}, u32[]{:S(2)}, u32[]{:S(2)}) collective-permute-start(bf16[128,512]{1,0:T(8,128)(2,1)S(1)} %collective-permute-done.60), channel_id=1, source_target_pairs={{8,0},{16,8},{24,16},{28,24},{20,28},{12,20},{4,12},{0,4},{9,1},{1... | collective-permute-start | bytes 393224 | tf_op jit(solution)/shard_map/ppermute | solution.py:103
  179.2 6.5 %collective-permute-start.54 = (bf16[128,512]{1,0:T(8,128)(2,1)S(1)}, bf16[128,512]{1,0:T(8,128)(2,1)S(1)}, u32[]{:S(2)}, u32[]{:S(2)}) collective-permute-start(bf16[128,512]{1,0:T(8,128)(2,1)S(1)} %collective-permute-done.53), channel_id=1, source_target_pairs={{8,0},{16,8},{24,16},{28,24},{20,28},{12,20},{4,12},{0,4},{9,1},{1... | collective-permute-start | bytes 393224 | tf_op jit(solution)/shard_map/ppermute | solution.py:103
  180.1 6.9 %collective-permute-start.47 = (bf16[128,512]{1,0:T(8,128)(2,1)S(1)}, bf16[128,512]{1,0:T(8,128)(2,1)S(1)}, u32[]{:S(2)}, u32[]{:S(2)}) collective-permute-start(bf16[128,512]{1,0:T(8,128)(2,1)S(1)} %collective-permute-done.46), channel_id=1, source_target_pairs={{0,8},{8,16},{16,24},{24,28},{28,20},{20,12},{12,4},{4,0},{1,9},{9... | collective-permute-start | bytes 393224 | tf_op jit(solution)/shard_map/ppermute | solution.py:103
  182.8 5.6 %collective-permute-start.40 = (bf16[128,512]{1,0:T(8,128)(2,1)S(1)}, bf16[128,512]{1,0:T(8,128)(2,1)S(1)}, u32[]{:S(2)}, u32[]{:S(2)}) collective-permute-start(bf16[128,512]{1,0:T(8,128)(2,1)S(1)} %collective-permute-done.39), channel_id=1, source_target_pairs={{0,8},{8,16},{16,24},{24,28},{28,20},{20,12},{12,4},{4,0},{1,9},{9... | collective-permute-start | bytes 393224 | tf_op jit(solution)/shard_map/ppermute | solution.py:103
  183.9 6.3 %collective-permute-start.62 = (bf16[128,512]{1,0:T(8,128)(2,1)S(1)}, bf16[128,512]{1,0:T(8,128)(2,1)S(1)}, u32[]{:S(2)}, u32[]{:S(2)}) collective-permute-start(bf16[128,512]{1,0:T(8,128)(2,1)S(1)} %collective-permute-done.61), channel_id=1, source_target_pairs={{8,0},{16,8},{24,16},{28,24},{20,28},{12,20},{4,12},{0,4},{9,1},{1... | collective-permute-start | bytes 393224 | tf_op jit(solution)/shard_map/ppermute | solution.py:103
  185.6 5.9 %collective-permute-start.55 = (bf16[128,512]{1,0:T(8,128)(2,1)S(1)}, bf16[128,512]{1,0:T(8,128)(2,1)S(1)}, u32[]{:S(2)}, u32[]{:S(2)}) collective-permute-start(bf16[128,512]{1,0:T(8,128)(2,1)S(1)} %collective-permute-done.54), channel_id=1, source_target_pairs={{8,0},{16,8},{24,16},{28,24},{20,28},{12,20},{4,12},{0,4},{9,1},{1... | collective-permute-start | bytes 393224 | tf_op jit(solution)/shard_map/ppermute | solution.py:103
  186.9 6.3 %collective-permute-start.48 = (bf16[128,512]{1,0:T(8,128)(2,1)S(1)}, bf16[128,512]{1,0:T(8,128)(2,1)S(1)}, u32[]{:S(2)}, u32[]{:S(2)}) collective-permute-start(bf16[128,512]{1,0:T(8,128)(2,1)S(1)} %collective-permute-done.47), channel_id=1, source_target_pairs={{0,8},{8,16},{16,24},{24,28},{28,20},{20,12},{12,4},{4,0},{1,9},{9... | collective-permute-start | bytes 393224 | tf_op jit(solution)/shard_map/ppermute | solution.py:103
  188.4 6.2 %collective-permute-start.41 = (bf16[128,512]{1,0:T(8,128)(2,1)S(1)}, bf16[128,512]{1,0:T(8,128)(2,1)S(1)}, u32[]{:S(2)}, u32[]{:S(2)}) collective-permute-start(bf16[128,512]{1,0:T(8,128)(2,1)S(1)} %collective-permute-done.40), channel_id=1, source_target_pairs={{0,8},{8,16},{16,24},{24,28},{28,20},{20,12},{12,4},{4,0},{1,9},{9... | collective-permute-start | bytes 393224 | tf_op jit(solution)/shard_map/ppermute | solution.py:103
  190.1 5.2 %collective-permute-start.63 = (bf16[128,512]{1,0:T(8,128)(2,1)S(1)}, bf16[128,512]{1,0:T(8,128)(2,1)S(1)}, u32[]{:S(2)}, u32[]{:S(2)}) collective-permute-start(bf16[128,512]{1,0:T(8,128)(2,1)S(1)} %collective-permute-done.62), channel_id=1, source_target_pairs={{8,0},{16,8},{24,16},{28,24},{20,28},{12,20},{4,12},{0,4},{9,1},{1... | collective-permute-start | bytes 393224 | tf_op jit(solution)/shard_map/ppermute | solution.py:103
  191.5 5.0 %collective-permute-start.56 = (bf16[128,512]{1,0:T(8,128)(2,1)S(1)}, bf16[128,512]{1,0:T(8,128)(2,1)S(1)}, u32[]{:S(2)}, u32[]{:S(2)}) collective-permute-start(bf16[128,512]{1,0:T(8,128)(2,1)S(1)} %collective-permute-done.55), channel_id=1, source_target_pairs={{8,0},{16,8},{24,16},{28,24},{20,28},{12,20},{4,12},{0,4},{9,1},{1... | collective-permute-start | bytes 393224 | tf_op jit(solution)/shard_map/ppermute | solution.py:103
  193.2 5.0 %collective-permute-start.49 = (bf16[128,512]{1,0:T(8,128)(2,1)S(1)}, bf16[128,512]{1,0:T(8,128)(2,1)S(1)}, u32[]{:S(2)}, u32[]{:S(2)}) collective-permute-start(bf16[128,512]{1,0:T(8,128)(2,1)S(1)} %collective-permute-done.48), channel_id=1, source_target_pairs={{0,8},{8,16},{16,24},{24,28},{28,20},{20,12},{12,4},{4,0},{1,9},{9... | collective-permute-start | bytes 393224 | tf_op jit(solution)/shard_map/ppermute | solution.py:103
  194.6 5.0 %collective-permute-start.42 = (bf16[128,512]{1,0:T(8,128)(2,1)S(1)}, bf16[128,512]{1,0:T(8,128)(2,1)S(1)}, u32[]{:S(2)}, u32[]{:S(2)}) collective-permute-start(bf16[128,512]{1,0:T(8,128)(2,1)S(1)} %collective-permute-done.41), channel_id=1, source_target_pairs={{0,8},{8,16},{16,24},{24,28},{28,20},{20,12},{12,4},{4,0},{1,9},{9... | collective-permute-start | bytes 393224 | tf_op jit(solution)/shard_map/ppermute | solution.py:103
  203.5 10.6 %collective-permute-start.66 = (bf16[128,512]{1,0:T(8,128)(2,1)S(1)}, bf16[128,512]{1,0:T(8,128)(2,1)S(1)}, u32[]{:S(2)}, u32[]{:S(2)}) collective-permute-start(bf16[128,512]{1,0:T(8,128)(2,1)S(1)} %get-tuple-element.117), channel_id=1, source_target_pairs={{0,16},{1,24},{2,0},{3,8},{4,20},{5,28},{6,4},{7,12},{8,17},{9,25}... | collective-permute-start | bytes 393224 | tf_op jit(solution)/shard_map/ppermute | solution.py:73
  204.1 14.8 %collective-permute-start.65 = (bf16[128,512]{1,0:T(8,128)(2,1)S(1)}, bf16[128,512]{1,0:T(8,128)(2,1)S(1)}, u32[]{:S(2)}, u32[]{:S(2)}) collective-permute-start(bf16[128,512]{1,0:T(8,128)(2,1)S(1)} %get-tuple-element.115), channel_id=1, source_target_pairs={{0,0},{1,8},{2,16},{3,24},{4,4},{5,12},{6,20},{7,28},{8,1},{9,9},{... | collective-permute-start | bytes 393224 | tf_op jit(solution)/shard_map/ppermute | solution.py:73
  208.0 11.9 %collective-permute-start.68 = (bf16[128,512]{1,0:T(8,128)(2,1)S(1)}, bf16[128,512]{1,0:T(8,128)(2,1)S(1)}, u32[]{:S(2)}, u32[]{:S(2)}) collective-permute-start(bf16[128,512]{1,0:T(8,128)(2,1)S(1)} %get-tuple-element.116), channel_id=1, source_target_pairs={{0,20},{1,28},{2,4},{3,12},{4,16},{5,24},{6,0},{7,8},{8,21},{9,29}... | collective-permute-start | bytes 393224 | tf_op jit(solution)/shard_map/ppermute | solution.py:73
  208.0 14.4 %collective-permute-start.67 = (bf16[128,512]{1,0:T(8,128)(2,1)S(1)}, bf16[128,512]{1,0:T(8,128)(2,1)S(1)}, u32[]{:S(2)}, u32[]{:S(2)}) collective-permute-start(bf16[128,512]{1,0:T(8,128)(2,1)S(1)} %get-tuple-element.114), channel_id=1, source_target_pairs={{0,4},{1,12},{2,20},{3,28},{4,0},{5,8},{6,16},{7,24},{8,5},{9,13},... | collective-permute-start | bytes 393224 | tf_op jit(solution)/shard_map/ppermute | solution.py:73
  (27 other events, 165.2 us)

commit v16 on v14

--- a/solution.py
+++ b/solution.py
@@ -17,7 +17,7 @@
     n_row, n_col = lax.axis_size("row"), lax.axis_size("col")
     width = tokens.shape[1] // n_row
     if n_col % 2:
-        return lax.all_to_all(tokens, "row", 1, 0, tiled=True)
+        return lax.all_to_all(tokens, "row", 1, 0, tiled=True), None
     core = lax.axis_index("col") % 2
     halves = tokens.reshape(tokens.shape[0], n_row, 2, width // 2)
     mine = jnp.take(halves, core, axis=2).reshape(tokens.shape[0], n_row * (width // 2))
@@ -25,7 +25,7 @@
     other = lax.ppermute(mine, "col", [(c, c ^ 1) for c in range(n_col)])
     return jnp.where(
         core == 0, jnp.concatenate([mine, other], axis=1), jnp.concatenate([other, mine], axis=1)
-    )
+    ), (mine, other, core)
 
 
 def placed_blocks(grad_sum, row_count):
@@ -109,15 +109,27 @@
     return stacks, sources
 
 
-def ring_reduce_scatter(token_cols, weight, axis, chains=2):
+def ring_reduce_scatter(token_cols, weight, axis, chains=2, halves=None):
     count, order, place, ahead, behind = ring_place(axis)
     rows = token_cols.shape[0] // count
     blocks = token_cols.reshape(count, rows, token_cols.shape[1])
     half = weight.shape[1] // 2
     steps = jnp.arange(1, count)
     later = (count - 1) * rows
-    first_0 = jnp.take(blocks, order[(place - 1) % count], axis=0)
-    second_0 = jnp.take(blocks, order[(place + 1) % count], axis=0)
+    def block_at(index):
+        if halves is None:
+            return jnp.take(blocks, index, axis=0)
+        mine, other, core = halves
+        own = lax.dynamic_slice_in_dim(mine, index * rows, rows, 0)
+        swapped = lax.dynamic_slice_in_dim(other, index * rows, rows, 0)
+        return jnp.where(
+            core == 0,
+            jnp.concatenate([own, swapped], axis=1),
+            jnp.concatenate([swapped, own], axis=1),
+        )
+
+    first_0 = block_at(order[(place - 1) % count])
+    second_0 = block_at(order[(place + 1) % count])
     start_a = jnp.dot(first_0, weight[:, :half], preferred_element_type=jnp.float32)
     start_b = jnp.dot(second_0, weight[:, half:], preferred_element_type=jnp.float32)
     first = jnp.take(blocks, order[(place - 1 - steps) % count], axis=0).reshape(later, -1)
@@ -188,7 +200,8 @@
         and lax.axis_size("row") % lax.axis_size("col") == 0
     )
     if moves_tokens:
-        inner_x = ring_reduce_scatter(fetched_columns(tokens), in_weight, "row")
+        token_cols, halves = fetched_columns(tokens)
+        inner_x = ring_reduce_scatter(token_cols, in_weight, "row", halves=halves)
     else:
         full_in = lax.all_gather(in_weight, "row", axis=0, tiled=True)
         inner_x = jnp.dot(tokens, full_in, preferred_element_type=jnp.float32).astype(jnp.bfloat16)

time: 224 us -> 225 us (level)
  between operations: 6.8 us -> 4.34 us
    unnamed x66 -> x68, local copies, waits for them, and re-layouts: 4.58 us -> 4.57 us
  transfers between devices with their start and end apart: 68 -> 68, of which waited for: 48 -> 49; matrix products, arithmetic and copies ran while one was open for 8% -> 10% of each run, Pallas kernels for 0% -> 0%
where the time goes in v16:
time: 225 us
  waiting for transfers between devices  80.5 us (36%)
  starting transfers between devices  76.3 us (34%)
  matrix products  30.5 us (14%)
  local copies, waits for them, and re-layouts  17.9 us (8%)
  other arithmetic  15 us (7%)
  between operations  4.34 us (2%)
    ppermute x28, starting transfers between devices, ring_gather(): part = lax.ppermute(part, axis, pairs)  31.2 us
    ppermute x28, starting transfers between devices, ring_reduce_scatter(): total = lax.ppermute(total, axis, pairs)  27.6 us
    ppermute x28, waiting for transfers between devices, ring_reduce_scatter(): total = lax.ppermute(total, axis, pairs)  23.9 us
    ppermute x28, waiting for transfers between devices, ring_gather(): part = lax.ppermute(part, axis, pairs)  16.8 us
    dot_general x1, matrix products, shards(): lax.dot_general(residual_grad, out_weight, (((1,), (1,)), ((), ())), pref...  14.7 us
    ppermute x1, waiting for transfers between devices, col_psum(): lax.ppermute(pair.astype(jnp.bfloat16), 'col', [(c, c ^ 2) for c in range...  13.4 us
    ppermute x4, waiting for transfers between devices, placed_sums(): lax.ppermute(piece, ('row', 'col'), pairs).astype(jnp.float32)  10 us
    dot_general x1, matrix products, shards(): jnp.dot(mixed, out_weight, preferred_element_type=jnp.float32)  8.81 us
  transfers between devices with their start and end apart: 68, of which 49 were waited for; matrix products, arithmetic and copies ran while one was open for 10% of the time, Pallas kernels for 0%

profile of v16, /device:TPU:2, one launch (start us, length us, event | category | flops | bytes accessed | tf_op | source)
XLA Modules:
  0.0 224.6 jit_solution(13954286514799171342)
XLA Ops:
  0.7 1.6 copy.23
  3.4 5.8 %all-to-all-start = ((bf16[128,8,256]{2,0,1:T(8,128)(2,1)}), bf16[128,8,256]{2,0,1:T(8,128)(2,1)S(1)}, u32[]{:S(2)}, u32[]{:S(2)}) async-start(bf16[128,8,256]{2,0,1:T(8,128)(2,1)} %copy.25), calls=%async_computation | async-start | bytes 1048576 | tf_op jit(solution)/shard_map/all_to_all | solution.py:24
  16.3 7.4 %all-to-all-done = bf16[128,8,256]{2,0,1:T(8,128)(2,1)S(1)} async-done(((bf16[128,8,256]{2,0,1:T(8,128)(2,1)}), bf16[128,8,256]{2,0,1:T(8,128)(2,1)S(1)}, u32[]{:S(2)}, u32[]{:S(2)}) %all-to-all-start) | async-done | bytes 524320 | tf_op jit(solution)/shard_map/all_to_all | solution.py:24
  26.6 1.5 collective-permute-start.15
  28.2 1.5 maximum_select_fusion.1
  29.7 1.5 gather_fusion.5
  31.3 1.8 gather_fusion.4
  33.1 1.3 convolution_convert_fusion.2
  34.4 2.0 collective-permute-start.1
  40.4 1.5 collective-permute-start.16
  42.6 1.7 collective-permute-start.2
  44.9 1.3 collective-permute-done.16
  46.2 1.4 collective-permute-done.23
  47.7 1.5 collective-permute-start.17
  50.0 1.4 collective-permute-start.3
  52.7 1.8 collective-permute-done.24
  54.7 1.3 collective-permute-start.18
  56.5 1.8 collective-permute-start.4
  59.8 2.8 %collective-permute-done.25 = bf16[128,512]{1,0:T(8,128)(2,1)S(1)} collective-permute-done((bf16[128,512]{1,0:T(8,128)(2,1)S(1)}, bf16[128,512]{1,0:T(8,128)(2,1)S(1)}, u32[]{:S(2)}, u32[]{:S(2)}) %collective-permute-start.25) | collective-permute-done | bytes 131104 | tf_op jit(solution)/shard_map/ppermute | solution.py:148
  64.5 1.6 collective-permute-start.5
  66.9 1.8 collective-permute-done.19
  68.7 2.8 %collective-permute-done.26 = bf16[128,512]{1,0:T(8,128)(2,1)S(1)} collective-permute-done((bf16[128,512]{1,0:T(8,128)(2,1)S(1)}, bf16[128,512]{1,0:T(8,128)(2,1)S(1)}, u32[]{:S(2)}, u32[]{:S(2)}) %collective-permute-start.26) | collective-permute-done | bytes 131104 | tf_op jit(solution)/shard_map/ppermute | solution.py:148
  71.6 1.3 collective-permute-start.20
  73.4 1.7 collective-permute-start.6
  75.9 2.1 collective-permute-done.20
  78.0 2.4 %collective-permute-done.27 = bf16[128,512]{1,0:T(8,128)(2,1)S(1)} collective-permute-done((bf16[128,512]{1,0:T(8,128)(2,1)S(1)}, bf16[128,512]{1,0:T(8,128)(2,1)S(1)}, u32[]{:S(2)}, u32[]{:S(2)}) %collective-permute-start.27) | collective-permute-done | bytes 131104 | tf_op jit(solution)/shard_map/ppermute | solution.py:148
  82.1 1.8 collective-permute-start.7
  85.5 1.4 collective-permute-done.28
  87.1 1.7 collective-permute-done.14
  88.9 2.5 %collective-permute-start.29 = (bf16[3,2048]{1,0:T(4,128)(2,1)S(1)}, bf16[3,2048]{1,0:T(4,128)(2,1)S(1)}, u32[]{:S(2)}, u32[]{:S(2)}) collective-permute-start(bf16[3,2048]{1,0:T(4,128)(2,1)S(1)} %pad_maximum_fusion.1), channel_id=1, source_target_pairs={{0,4},{4,8},{8,12},{12,16},{16,20},{20,24},{24,28},{1,5},{5,9},{9,... | collective-permute-start | bytes 36872 | tf_op jit(solution)/shard_map/ppermute | solution.py:13
  91.5 1.2 collective-permute-done.29
  93.9 8.8 %convolution_convert_fusion = bf16[128,4096]{1,0:T(8,128)(2,1)S(1)} fusion(bf16[2048,4096]{1,0:T(8,128)(2,1)} %param.25, bf16[128,2048]{1,0:T(8,128)(2,1)S(1)} %copy-done.17, f32[128,2048]{1,0:T(8,128)S(1)} %fusion.9), kind=kOutput, calls=%fused_computation.6 | convolution fusion | flops 2150891520 | bytes 19398656 | tf_op jit(solution)/shard_map/dot_general | solution.py:223
  102.9 1.9 collective-permute-done.30
  105.7 13.4 %collective-permute-done.31 = bf16[128,2048]{1,0:T(8,128)(2,1)S(1)} collective-permute-done((bf16[128,2048]{1,0:T(8,128)(2,1)S(1)}, bf16[128,2048]{1,0:T(8,128)(2,1)S(1)}, u32[]{:S(2)}, u32[]{:S(2)}) %collective-permute-start.31) | collective-permute-done | bytes 524320 | tf_op jit(solution)/shard_map/ppermute | solution.py:164
  122.3 3.2 %maximum_select_fusion = f32[128,4096]{1,0:T(8,128)} fusion(f32[128,2048]{1,0:T(8,128)S(1)} %convert_add_fusion, f32[128,2048]{1,0:T(8,128)} %collective-permute-done.32, pred[]{:T(512)S(6)} %eq.44), kind=kLoop, calls=%fused_computation.7 | loop fusion | flops 1572864 | bytes 4194305 | tf_op jit(solution)/shard_map/jit(_where)/select_n | solution.py:168
  125.4 14.7 %multiply_multiply_fusion.2 = (f32[128,2048]{1,0:T(8,128)}, f32[128,2048]{1,0:T(8,128)}, bf16[128,2048]{1,0:T(8,128)(2,1)}) fusion(f32[128]{0:T(128)S(1)} %get-tuple-element.115, f32[2048]{0:T(1024)S(1)} %bitcast.318, f32[128,2048]{1,0:T(8,128)} %copy-done.9, bf16[128,2048]{1,0:T(8,128)(2,1)} %param.23, bf16[2048,4096]{1,0:T(8,128)(2,1)} %param.25, ...), kind=kOutput, calls=%fused_computation.43 | convolution fusion | flops 2155872256 | bytes 24126464 | tf_op jit(solution)/shard_map/dot_general | solution.py:236
  140.2 1.5 multiply_multiply_fusion.1
  143.5 1.3 collective-permute-start.33
  146.7 3.1 %collective-permute-done.33 = f32[3,2048]{1,0:T(4,128)S(1)} collective-permute-done((f32[3,2048]{1,0:T(4,128)S(1)}, f32[3,2048]{1,0:T(4,128)S(1)}, u32[]{:S(2)}, u32[]{:S(2)}) %collective-permute-start.33) | collective-permute-done | bytes 24608 | tf_op jit(solution)/shard_map/ppermute | solution.py:13
  150.2 3.2 %collective-permute-start.55 = (bf16[128,512]{1,0:T(8,128)(2,1)S(1)}, bf16[128,512]{1,0:T(8,128)(2,1)S(1)}, u32[]{:S(2)}, u32[]{:S(2)}) collective-permute-start(bf16[128,512]{1,0:T(8,128)(2,1)S(1)} %get-tuple-element.91), channel_id=1, source_target_pairs={{8,0},{16,8},{24,16},{28,24},{20,28},{12,20},{4,12},{0,4},{9,1},{1... | collective-permute-start | bytes 393224 | tf_op jit(solution)/shard_map/ppermute | solution.py:103
  153.4 1.4 collective-permute-start.48
  156.1 2.3 %collective-permute-done.55 = bf16[128,512]{1,0:T(8,128)(2,1)S(1)} collective-permute-done((bf16[128,512]{1,0:T(8,128)(2,1)S(1)}, bf16[128,512]{1,0:T(8,128)(2,1)S(1)}, u32[]{:S(2)}, u32[]{:S(2)}) %collective-permute-start.55) | collective-permute-done | bytes 131104 | tf_op jit(solution)/shard_map/ppermute | solution.py:103
  158.4 1.3 collective-permute-start.56
  159.7 1.5 collective-permute-done.48
  161.2 1.3 collective-permute-start.49
  163.3 1.8 collective-permute-start.35
  165.5 2.2 collective-permute-done.49
  167.6 1.3 collective-permute-start.50
  169.9 2.0 collective-permute-start.36
  172.3 1.9 collective-permute-done.50
  174.9 1.3 collective-permute-start.44
  176.2 1.3 collective-permute-done.36
  177.6 1.2 collective-permute-start.37
  182.6 1.4 collective-permute-done.37
  187.0 1.2 collective-permute-start.53
  189.7 1.6 collective-permute-start.39
  192.9 1.4 collective-permute-start.54
  202.7 1.8 collective-permute-done.62
  205.4 4.0 %collective-permute-start.63 = (bf16[128,512]{1,0:T(8,128)(2,1)S(1)}, bf16[128,512]{1,0:T(8,128)(2,1)S(1)}, u32[]{:S(2)}, u32[]{:S(2)}) collective-permute-start(bf16[128,512]{1,0:T(8,128)(2,1)S(1)} %get-tuple-element.103), channel_id=1, source_target_pairs={{0,0},{1,8},{2,16},{3,24},{4,4},{5,12},{6,20},{7,28},{8,1},{9,9},{... | collective-permute-start | bytes 393224 | tf_op jit(solution)/shard_map/ppermute | solution.py:73
  209.5 2.5 %collective-permute-start.65 = (bf16[128,512]{1,0:T(8,128)(2,1)S(1)}, bf16[128,512]{1,0:T(8,128)(2,1)S(1)}, u32[]{:S(2)}, u32[]{:S(2)}) collective-permute-start(bf16[128,512]{1,0:T(8,128)(2,1)S(1)} %get-tuple-element.102), channel_id=1, source_target_pairs={{0,4},{1,12},{2,20},{3,28},{4,0},{5,8},{6,16},{7,24},{8,5},{9,13},... | collective-permute-start | bytes 393224 | tf_op jit(solution)/shard_map/ppermute | solution.py:73
  212.0 1.8 dynamic-slice_convert_fusion
  213.8 1.8 collective-permute-done.64
  215.6 4.7 %collective-permute-done.63 = bf16[128,512]{1,0:T(8,128)(2,1)S(1)} collective-permute-done((bf16[128,512]{1,0:T(8,128)(2,1)S(1)}, bf16[128,512]{1,0:T(8,128)(2,1)S(1)}, u32[]{:S(2)}, u32[]{:S(2)}) %collective-permute-start.63) | collective-permute-done | bytes 131104 | tf_op jit(solution)/shard_map/ppermute | solution.py:73
  221.3 2.5 %collective-permute-done.65 = bf16[128,512]{1,0:T(8,128)(2,1)S(1)} collective-permute-done((bf16[128,512]{1,0:T(8,128)(2,1)S(1)}, bf16[128,512]{1,0:T(8,128)(2,1)S(1)}, u32[]{:S(2)}, u32[]{:S(2)}) %collective-permute-start.65) | collective-permute-done | bytes 131104 | tf_op jit(solution)/shard_map/ppermute | solution.py:73
  (230 shorter events, 60.1 us)
Async XLA Ops:
  3.4 20.3 %all-to-all-start = ((bf16[128,8,256]{2,0,1:T(8,128)(2,1)}), bf16[128,8,256]{2,0,1:T(8,128)(2,1)S(1)}, u32[]{:S(2)}, u32[]{:S(2)}) async-start(bf16[128,8,256]{2,0,1:T(8,128)(2,1)} %copy.25), calls=%async_computation | async-start | bytes 1048576 | tf_op jit(solution)/shard_map/all_to_all | solution.py:24
  26.6 12.7 %collective-permute-start.15 = (bf16[128,512]{1,0:T(8,128)(2,1)S(1)}, bf16[128,512]{1,0:T(8,128)(2,1)S(1)}, u32[]{:S(2)}, u32[]{:S(2)}) collective-permute-start(bf16[128,512]{1,0:T(8,128)(2,1)S(1)} %get-tuple-element.108), channel_id=1, source_target_pairs={{8,0},{16,8},{24,16},{28,24},{20,28},{12,20},{4,12},{0,4},{9,1},{1... | collective-permute-start | bytes 393224 | tf_op jit(solution)/shard_map/ppermute | solution.py:148
  28.2 11.2 %collective-permute-start.22 = (bf16[128,512]{1,0:T(8,128)(2,1)S(1)}, bf16[128,512]{1,0:T(8,128)(2,1)}, u32[]{:S(2)}, u32[]{:S(2)}) collective-permute-start(bf16[128,512]{1,0:T(8,128)(2,1)S(1)} %get-tuple-element.109), channel_id=1, source_target_pairs={{8,0},{16,8},{24,16},{28,24},{20,28},{12,20},{4,12},{0,4},{9,1},{1... | collective-permute-start | bytes 393224 | tf_op jit(solution)/shard_map/ppermute | solution.py:148
  34.4 7.5 %collective-permute-start.1 = (bf16[128,512]{1,0:T(8,128)(2,1)S(1)}, bf16[128,512]{1,0:T(8,128)(2,1)S(1)}, u32[]{:S(2)}, u32[]{:S(2)}) collective-permute-start(bf16[128,512]{1,0:T(8,128)(2,1)S(1)} %get-tuple-element.106), channel_id=1, source_target_pairs={{0,8},{8,16},{16,24},{24,28},{28,20},{20,12},{12,4},{4,0},{1,9},{9... | collective-permute-start | bytes 393224 | tf_op jit(solution)/shard_map/ppermute | solution.py:148
  36.5 6.1 %collective-permute-start.8 = (bf16[128,512]{1,0:T(8,128)(2,1)S(1)}, bf16[128,512]{1,0:T(8,128)(2,1)S(1)}, u32[]{:S(2)}, u32[]{:S(2)}) collective-permute-start(bf16[128,512]{1,0:T(8,128)(2,1)S(1)} %get-tuple-element.107), channel_id=1, source_target_pairs={{0,8},{8,16},{16,24},{24,28},{28,20},{20,12},{12,4},{4,0},{1,9},{9... | collective-permute-start | bytes 393224 | tf_op jit(solution)/shard_map/ppermute | solution.py:148
  40.4 5.9 %collective-permute-start.16 = (bf16[128,512]{1,0:T(8,128)(2,1)S(1)}, bf16[128,512]{1,0:T(8,128)(2,1)S(1)}, u32[]{:S(2)}, u32[]{:S(2)}) collective-permute-start(bf16[128,512]{1,0:T(8,128)(2,1)S(1)} %get-tuple-element.81), channel_id=1, source_target_pairs={{8,0},{16,8},{24,16},{28,24},{20,28},{12,20},{4,12},{0,4},{9,1},{1... | collective-permute-start | bytes 393224 | tf_op jit(solution)/shard_map/ppermute | solution.py:148
  41.9 5.8 %collective-permute-start.23 = (bf16[128,512]{1,0:T(8,128)(2,1)S(1)}, bf16[128,512]{1,0:T(8,128)(2,1)S(1)}, u32[]{:S(2)}, u32[]{:S(2)}) collective-permute-start(bf16[128,512]{1,0:T(8,128)(2,1)S(1)} %get-tuple-element.82), channel_id=1, source_target_pairs={{8,0},{16,8},{24,16},{28,24},{20,28},{12,20},{4,12},{0,4},{9,1},{1... | collective-permute-start | bytes 393224 | tf_op jit(solution)/shard_map/ppermute | solution.py:148
  42.6 6.9 %collective-permute-start.2 = (bf16[128,512]{1,0:T(8,128)(2,1)S(1)}, bf16[128,512]{1,0:T(8,128)(2,1)S(1)}, u32[]{:S(2)}, u32[]{:S(2)}) collective-permute-start(bf16[128,512]{1,0:T(8,128)(2,1)S(1)} %get-tuple-element.67), channel_id=1, source_target_pairs={{0,8},{8,16},{16,24},{24,28},{28,20},{20,12},{12,4},{4,0},{1,9},{9... | collective-permute-start | bytes 393224 | tf_op jit(solution)/shard_map/ppermute | solution.py:148
  44.4 5.5 %collective-permute-start.9 = (bf16[128,512]{1,0:T(8,128)(2,1)S(1)}, bf16[128,512]{1,0:T(8,128)(2,1)S(1)}, u32[]{:S(2)}, u32[]{:S(2)}) collective-permute-start(bf16[128,512]{1,0:T(8,128)(2,1)S(1)} %get-tuple-element.68), channel_id=1, source_target_pairs={{0,8},{8,16},{16,24},{24,28},{28,20},{20,12},{12,4},{4,0},{1,9},{9... | collective-permute-start | bytes 393224 | tf_op jit(solution)/shard_map/ppermute | solution.py:148
  47.7 5.0 %collective-permute-start.17 = (bf16[128,512]{1,0:T(8,128)(2,1)S(1)}, bf16[128,512]{1,0:T(8,128)(2,1)S(1)}, u32[]{:S(2)}, u32[]{:S(2)}) collective-permute-start(bf16[128,512]{1,0:T(8,128)(2,1)S(1)} %get-tuple-element.79), channel_id=1, source_target_pairs={{8,0},{16,8},{24,16},{28,24},{20,28},{12,20},{4,12},{0,4},{9,1},{1... | collective-permute-start | bytes 393224 | tf_op jit(solution)/shard_map/ppermute | solution.py:148
  49.2 5.4 %collective-permute-start.24 = (bf16[128,512]{1,0:T(8,128)(2,1)S(1)}, bf16[128,512]{1,0:T(8,128)(2,1)S(1)}, u32[]{:S(2)}, u32[]{:S(2)}) collective-permute-start(bf16[128,512]{1,0:T(8,128)(2,1)S(1)} %get-tuple-element.80), channel_id=1, source_target_pairs={{8,0},{16,8},{24,16},{28,24},{20,28},{12,20},{4,12},{0,4},{9,1},{1... | collective-permute-start | bytes 393224 | tf_op jit(solution)/shard_map/ppermute | solution.py:148
  50.0 6.3 %collective-permute-start.3 = (bf16[128,512]{1,0:T(8,128)(2,1)S(1)}, bf16[128,512]{1,0:T(8,128)(2,1)S(1)}, u32[]{:S(2)}, u32[]{:S(2)}) collective-permute-start(bf16[128,512]{1,0:T(8,128)(2,1)S(1)} %get-tuple-element.65), channel_id=1, source_target_pairs={{0,8},{8,16},{16,24},{24,28},{28,20},{20,12},{12,4},{4,0},{1,9},{9... | collective-permute-start | bytes 393224 | tf_op jit(solution)/shard_map/ppermute | solution.py:148
  51.4 5.0 %collective-permute-start.10 = (bf16[128,512]{1,0:T(8,128)(2,1)S(1)}, bf16[128,512]{1,0:T(8,128)(2,1)S(1)}, u32[]{:S(2)}, u32[]{:S(2)}) collective-permute-start(bf16[128,512]{1,0:T(8,128)(2,1)S(1)} %get-tuple-element.66), channel_id=1, source_target_pairs={{0,8},{8,16},{16,24},{24,28},{28,20},{20,12},{12,4},{4,0},{1,9},{9... | collective-permute-start | bytes 393224 | tf_op jit(solution)/shard_map/ppermute | solution.py:148
  54.7 5.1 %collective-permute-start.18 = (bf16[128,512]{1,0:T(8,128)(2,1)S(1)}, bf16[128,512]{1,0:T(8,128)(2,1)S(1)}, u32[]{:S(2)}, u32[]{:S(2)}) collective-permute-start(bf16[128,512]{1,0:T(8,128)(2,1)S(1)} %get-tuple-element.77), channel_id=1, source_target_pairs={{8,0},{16,8},{24,16},{28,24},{20,28},{12,20},{4,12},{0,4},{9,1},{1... | collective-permute-start | bytes 393224 | tf_op jit(solution)/shard_map/ppermute | solution.py:148
  56.0 6.6 %collective-permute-start.25 = (bf16[128,512]{1,0:T(8,128)(2,1)S(1)}, bf16[128,512]{1,0:T(8,128)(2,1)S(1)}, u32[]{:S(2)}, u32[]{:S(2)}) collective-permute-start(bf16[128,512]{1,0:T(8,128)(2,1)S(1)} %get-tuple-element.78), channel_id=1, source_target_pairs={{8,0},{16,8},{24,16},{28,24},{20,28},{12,20},{4,12},{0,4},{9,1},{1... | collective-permute-start | bytes 393224 | tf_op jit(solution)/shard_map/ppermute | solution.py:148
  56.5 7.4 %collective-permute-start.4 = (bf16[128,512]{1,0:T(8,128)(2,1)S(1)}, bf16[128,512]{1,0:T(8,128)(2,1)S(1)}, u32[]{:S(2)}, u32[]{:S(2)}) collective-permute-start(bf16[128,512]{1,0:T(8,128)(2,1)S(1)} %get-tuple-element.63), channel_id=1, source_target_pairs={{0,8},{8,16},{16,24},{24,28},{28,20},{20,12},{12,4},{4,0},{1,9},{9... | collective-permute-start | bytes 393224 | tf_op jit(solution)/shard_map/ppermute | solution.py:148
  58.3 6.1 %collective-permute-start.11 = (bf16[128,512]{1,0:T(8,128)(2,1)S(1)}, bf16[128,512]{1,0:T(8,128)(2,1)S(1)}, u32[]{:S(2)}, u32[]{:S(2)}) collective-permute-start(bf16[128,512]{1,0:T(8,128)(2,1)S(1)} %get-tuple-element.64), channel_id=1, source_target_pairs={{0,8},{8,16},{16,24},{24,28},{28,20},{20,12},{12,4},{4,0},{1,9},{9... | collective-permute-start | bytes 393224 | tf_op jit(solution)/shard_map/ppermute | solution.py:148
  62.7 6.0 %collective-permute-start.19 = (bf16[128,512]{1,0:T(8,128)(2,1)S(1)}, bf16[128,512]{1,0:T(8,128)(2,1)S(1)}, u32[]{:S(2)}, u32[]{:S(2)}) collective-permute-start(bf16[128,512]{1,0:T(8,128)(2,1)S(1)} %get-tuple-element.75), channel_id=1, source_target_pairs={{8,0},{16,8},{24,16},{28,24},{20,28},{12,20},{4,12},{0,4},{9,1},{1... | collective-permute-start | bytes 393224 | tf_op jit(solution)/shard_map/ppermute | solution.py:148
  63.9 7.7 %collective-permute-start.26 = (bf16[128,512]{1,0:T(8,128)(2,1)S(1)}, bf16[128,512]{1,0:T(8,128)(2,1)S(1)}, u32[]{:S(2)}, u32[]{:S(2)}) collective-permute-start(bf16[128,512]{1,0:T(8,128)(2,1)S(1)} %get-tuple-element.76), channel_id=1, source_target_pairs={{8,0},{16,8},{24,16},{28,24},{20,28},{12,20},{4,12},{0,4},{9,1},{1... | collective-permute-start | bytes 393224 | tf_op jit(solution)/shard_map/ppermute | solution.py:148
  64.5 8.5 %collective-permute-start.5 = (bf16[128,512]{1,0:T(8,128)(2,1)S(1)}, bf16[128,512]{1,0:T(8,128)(2,1)S(1)}, u32[]{:S(2)}, u32[]{:S(2)}) collective-permute-start(bf16[128,512]{1,0:T(8,128)(2,1)S(1)} %get-tuple-element.61), channel_id=1, source_target_pairs={{0,8},{8,16},{16,24},{24,28},{28,20},{20,12},{12,4},{4,0},{1,9},{9... | collective-permute-start | bytes 393224 | tf_op jit(solution)/shard_map/ppermute | solution.py:148
  66.0 7.3 %collective-permute-start.12 = (bf16[128,512]{1,0:T(8,128)(2,1)S(1)}, bf16[128,512]{1,0:T(8,128)(2,1)S(1)}, u32[]{:S(2)}, u32[]{:S(2)}) collective-permute-start(bf16[128,512]{1,0:T(8,128)(2,1)S(1)} %get-tuple-element.62), channel_id=1, source_target_pairs={{0,8},{8,16},{16,24},{24,28},{28,20},{20,12},{12,4},{4,0},{1,9},{9... | collective-permute-start | bytes 393224 | tf_op jit(solution)/shard_map/ppermute | solution.py:148
  71.6 6.3 %collective-permute-start.20 = (bf16[128,512]{1,0:T(8,128)(2,1)S(1)}, bf16[128,512]{1,0:T(8,128)(2,1)S(1)}, u32[]{:S(2)}, u32[]{:S(2)}) collective-permute-start(bf16[128,512]{1,0:T(8,128)(2,1)S(1)} %get-tuple-element.73), channel_id=1, source_target_pairs={{8,0},{16,8},{24,16},{28,24},{20,28},{12,20},{4,12},{0,4},{9,1},{1... | collective-permute-start | bytes 393224 | tf_op jit(solution)/shard_map/ppermute | solution.py:148
  72.9 7.5 %collective-permute-start.27 = (bf16[128,512]{1,0:T(8,128)(2,1)S(1)}, bf16[128,512]{1,0:T(8,128)(2,1)S(1)}, u32[]{:S(2)}, u32[]{:S(2)}) collective-permute-start(bf16[128,512]{1,0:T(8,128)(2,1)S(1)} %get-tuple-element.74), channel_id=1, source_target_pairs={{8,0},{16,8},{24,16},{28,24},{20,28},{12,20},{4,12},{0,4},{9,1},{1... | collective-permute-start | bytes 393224 | tf_op jit(solution)/shard_map/ppermute | solution.py:148
  73.4 8.6 %collective-permute-start.6 = (bf16[128,512]{1,0:T(8,128)(2,1)S(1)}, bf16[128,512]{1,0:T(8,128)(2,1)S(1)}, u32[]{:S(2)}, u32[]{:S(2)}) collective-permute-start(bf16[128,512]{1,0:T(8,128)(2,1)S(1)} %get-tuple-element.59), channel_id=1, source_target_pairs={{0,8},{8,16},{16,24},{24,28},{28,20},{20,12},{12,4},{4,0},{1,9},{9... | collective-permute-start | bytes 393224 | tf_op jit(solution)/shard_map/ppermute | solution.py:148
  75.1 6.9 %collective-permute-start.13 = (bf16[128,512]{1,0:T(8,128)(2,1)S(1)}, bf16[128,512]{1,0:T(8,128)(2,1)S(1)}, u32[]{:S(2)}, u32[]{:S(2)}) collective-permute-start(bf16[128,512]{1,0:T(8,128)(2,1)S(1)} %get-tuple-element.60), channel_id=1, source_target_pairs={{0,8},{8,16},{16,24},{24,28},{28,20},{20,12},{12,4},{4,0},{1,9},{9... | collective-permute-start | bytes 393224 | tf_op jit(solution)/shard_map/ppermute | solution.py:148
  80.5 5.0 %collective-permute-start.21 = (bf16[128,512]{1,0:T(8,128)(2,1)S(1)}, bf16[128,512]{1,0:T(8,128)(2,1)S(1)}, u32[]{:S(2)}, u32[]{:S(2)}) collective-permute-start(bf16[128,512]{1,0:T(8,128)(2,1)S(1)} %get-tuple-element.71), channel_id=1, source_target_pairs={{8,0},{16,8},{24,16},{28,24},{20,28},{12,20},{4,12},{0,4},{9,1},{1... | collective-permute-start | bytes 393224 | tf_op jit(solution)/shard_map/ppermute | solution.py:148
  81.7 5.2 %collective-permute-start.28 = (bf16[128,512]{1,0:T(8,128)(2,1)S(1)}, bf16[128,512]{1,0:T(8,128)(2,1)S(1)}, u32[]{:S(2)}, u32[]{:S(2)}) collective-permute-start(bf16[128,512]{1,0:T(8,128)(2,1)S(1)} %get-tuple-element.72), channel_id=1, source_target_pairs={{8,0},{16,8},{24,16},{28,24},{20,28},{12,20},{4,12},{0,4},{9,1},{1... | collective-permute-start | bytes 393224 | tf_op jit(solution)/shard_map/ppermute | solution.py:148
  82.1 5.0 %collective-permute-start.7 = (bf16[128,512]{1,0:T(8,128)(2,1)S(1)}, bf16[128,512]{1,0:T(8,128)(2,1)S(1)}, u32[]{:S(2)}, u32[]{:S(2)}) collective-permute-start(bf16[128,512]{1,0:T(8,128)(2,1)S(1)} %get-tuple-element.57), channel_id=1, source_target_pairs={{0,8},{8,16},{16,24},{24,28},{28,20},{20,12},{12,4},{4,0},{1,9},{9... | collective-permute-start | bytes 393224 | tf_op jit(solution)/shard_map/ppermute | solution.py:148
  83.9 5.0 %collective-permute-start.14 = (bf16[128,512]{1,0:T(8,128)(2,1)S(1)}, bf16[128,512]{1,0:T(8,128)(2,1)S(1)}, u32[]{:S(2)}, u32[]{:S(2)}) collective-permute-start(bf16[128,512]{1,0:T(8,128)(2,1)S(1)} %get-tuple-element.58), channel_id=1, source_target_pairs={{0,8},{8,16},{16,24},{24,28},{28,20},{20,12},{12,4},{4,0},{1,9},{9... | collective-permute-start | bytes 393224 | tf_op jit(solution)/shard_map/ppermute | solution.py:148
  88.9 3.7 %collective-permute-start.29 = (bf16[3,2048]{1,0:T(4,128)(2,1)S(1)}, bf16[3,2048]{1,0:T(4,128)(2,1)S(1)}, u32[]{:S(2)}, u32[]{:S(2)}) collective-permute-start(bf16[3,2048]{1,0:T(4,128)(2,1)S(1)} %pad_maximum_fusion.1), channel_id=1, source_target_pairs={{0,4},{4,8},{8,12},{12,16},{16,20},{20,24},{24,28},{1,5},{5,9},{9,... | collective-permute-start | bytes 36872 | tf_op jit(solution)/shard_map/ppermute | solution.py:13
  105.0 14.0 %collective-permute-start.31 = (bf16[128,2048]{1,0:T(8,128)(2,1)S(1)}, bf16[128,2048]{1,0:T(8,128)(2,1)S(1)}, u32[]{:S(2)}, u32[]{:S(2)}) collective-permute-start(bf16[128,2048]{1,0:T(8,128)(2,1)S(1)} %fusion.21), channel_id=1, source_target_pairs={{0,2},{1,3},{2,0},{3,1},{4,6},{5,7},{6,4},{7,5},{8,10},{9,11},{10,... | collective-permute-start | bytes 1572872 | tf_op jit(solution)/shard_map/ppermute | solution.py:164
  143.5 6.3 %collective-permute-start.33 = (f32[3,2048]{1,0:T(4,128)S(1)}, f32[3,2048]{1,0:T(4,128)S(1)}, u32[]{:S(2)}, u32[]{:S(2)}) collective-permute-start(f32[3,2048]{1,0:T(4,128)S(1)} %slice_add_fusion), channel_id=1, source_target_pairs={{4,0},{8,4},{12,8},{16,12},{20,16},{24,20},{28,24},{5,1},{9,5},{13... | collective-permute-start | bytes 73736 | tf_op jit(solution)/shard_map/ppermute | solution.py:13
  150.2 8.2 %collective-permute-start.55 = (bf16[128,512]{1,0:T(8,128)(2,1)S(1)}, bf16[128,512]{1,0:T(8,128)(2,1)S(1)}, u32[]{:S(2)}, u32[]{:S(2)}) collective-permute-start(bf16[128,512]{1,0:T(8,128)(2,1)S(1)} %get-tuple-element.91), channel_id=1, source_target_pairs={{8,0},{16,8},{24,16},{28,24},{20,28},{12,20},{4,12},{0,4},{9,1},{1... | collective-permute-start | bytes 393224 | tf_op jit(solution)/shard_map/ppermute | solution.py:103
  153.4 7.8 %collective-permute-start.48 = (bf16[128,512]{1,0:T(8,128)(2,1)S(1)}, bf16[128,512]{1,0:T(8,128)(2,1)S(1)}, u32[]{:S(2)}, u32[]{:S(2)}) collective-permute-start(bf16[128,512]{1,0:T(8,128)(2,1)S(1)} %get-tuple-element.92), channel_id=1, source_target_pairs={{8,0},{16,8},{24,16},{28,24},{20,28},{12,20},{4,12},{0,4},{9,1},{1... | collective-permute-start | bytes 393224 | tf_op jit(solution)/shard_map/ppermute | solution.py:103
  154.9 7.7 %collective-permute-start.41 = (bf16[128,512]{1,0:T(8,128)(2,1)S(1)}, bf16[128,512]{1,0:T(8,128)(2,1)S(1)}, u32[]{:S(2)}, u32[]{:S(2)}) collective-permute-start(bf16[128,512]{1,0:T(8,128)(2,1)S(1)} %get-tuple-element.93), channel_id=1, source_target_pairs={{0,8},{8,16},{16,24},{24,28},{28,20},{20,12},{12,4},{4,0},{1,9},{9... | collective-permute-start | bytes 393224 | tf_op jit(solution)/shard_map/ppermute | solution.py:103
  155.5 7.8 %collective-permute-start.34 = (bf16[128,512]{1,0:T(8,128)(2,1)S(1)}, bf16[128,512]{1,0:T(8,128)(2,1)S(1)}, u32[]{:S(2)}, u32[]{:S(2)}) collective-permute-start(bf16[128,512]{1,0:T(8,128)(2,1)S(1)} %get-tuple-element.90), channel_id=1, source_target_pairs={{0,8},{8,16},{16,24},{24,28},{28,20},{20,12},{12,4},{4,0},{1,9},{9... | collective-permute-start | bytes 393224 | tf_op jit(solution)/shard_map/ppermute | solution.py:103
  158.4 6.7 %collective-permute-start.56 = (bf16[128,512]{1,0:T(8,128)(2,1)S(1)}, bf16[128,512]{1,0:T(8,128)(2,1)S(1)}, u32[]{:S(2)}, u32[]{:S(2)}) collective-permute-start(bf16[128,512]{1,0:T(8,128)(2,1)S(1)} %collective-permute-done.55), channel_id=1, source_target_pairs={{8,0},{16,8},{24,16},{28,24},{20,28},{12,20},{4,12},{0,4},{9,1},{1... | collective-permute-start | bytes 393224 | tf_op jit(solution)/shard_map/ppermute | solution.py:103
  161.2 6.4 %collective-permute-start.49 = (bf16[128,512]{1,0:T(8,128)(2,1)S(1)}, bf16[128,512]{1,0:T(8,128)(2,1)S(1)}, u32[]{:S(2)}, u32[]{:S(2)}) collective-permute-start(bf16[128,512]{1,0:T(8,128)(2,1)S(1)} %collective-permute-done.48), channel_id=1, source_target_pairs={{8,0},{16,8},{24,16},{28,24},{20,28},{12,20},{4,12},{0,4},{9,1},{1... | collective-permute-start | bytes 393224 | tf_op jit(solution)/shard_map/ppermute | solution.py:103
  162.6 6.3 %collective-permute-start.42 = (bf16[128,512]{1,0:T(8,128)(2,1)S(1)}, bf16[128,512]{1,0:T(8,128)(2,1)S(1)}, u32[]{:S(2)}, u32[]{:S(2)}) collective-permute-start(bf16[128,512]{1,0:T(8,128)(2,1)S(1)} %collective-permute-done.41), channel_id=1, source_target_pairs={{0,8},{8,16},{16,24},{24,28},{28,20},{20,12},{12,4},{4,0},{1,9},{9... | collective-permute-start | bytes 393224 | tf_op jit(solution)/shard_map/ppermute | solution.py:103
  163.3 6.7 %collective-permute-start.35 = (bf16[128,512]{1,0:T(8,128)(2,1)S(1)}, bf16[128,512]{1,0:T(8,128)(2,1)S(1)}, u32[]{:S(2)}, u32[]{:S(2)}) collective-permute-start(bf16[128,512]{1,0:T(8,128)(2,1)S(1)} %collective-permute-done.34), channel_id=1, source_target_pairs={{0,8},{8,16},{16,24},{24,28},{28,20},{20,12},{12,4},{4,0},{1,9},{9... | collective-permute-start | bytes 393224 | tf_op jit(solution)/shard_map/ppermute | solution.py:103
  165.1 6.8 %collective-permute-start.57 = (bf16[128,512]{1,0:T(8,128)(2,1)S(1)}, bf16[128,512]{1,0:T(8,128)(2,1)S(1)}, u32[]{:S(2)}, u32[]{:S(2)}) collective-permute-start(bf16[128,512]{1,0:T(8,128)(2,1)S(1)} %collective-permute-done.56), channel_id=1, source_target_pairs={{8,0},{16,8},{24,16},{28,24},{20,28},{12,20},{4,12},{0,4},{9,1},{1... | collective-permute-start | bytes 393224 | tf_op jit(solution)/shard_map/ppermute | solution.py:103
  167.6 6.6 %collective-permute-start.50 = (bf16[128,512]{1,0:T(8,128)(2,1)S(1)}, bf16[128,512]{1,0:T(8,128)(2,1)S(1)}, u32[]{:S(2)}, u32[]{:S(2)}) collective-permute-start(bf16[128,512]{1,0:T(8,128)(2,1)S(1)} %collective-permute-done.49), channel_id=1, source_target_pairs={{8,0},{16,8},{24,16},{28,24},{20,28},{12,20},{4,12},{0,4},{9,1},{1... | collective-permute-start | bytes 393224 | tf_op jit(solution)/shard_map/ppermute | solution.py:103
  168.9 6.0 %collective-permute-start.43 = (bf16[128,512]{1,0:T(8,128)(2,1)S(1)}, bf16[128,512]{1,0:T(8,128)(2,1)S(1)}, u32[]{:S(2)}, u32[]{:S(2)}) collective-permute-start(bf16[128,512]{1,0:T(8,128)(2,1)S(1)} %collective-permute-done.42), channel_id=1, source_target_pairs={{0,8},{8,16},{16,24},{24,28},{28,20},{20,12},{12,4},{4,0},{1,9},{9... | collective-permute-start | bytes 393224 | tf_op jit(solution)/shard_map/ppermute | solution.py:103
  169.9 7.6 %collective-permute-start.36 = (bf16[128,512]{1,0:T(8,128)(2,1)S(1)}, bf16[128,512]{1,0:T(8,128)(2,1)S(1)}, u32[]{:S(2)}, u32[]{:S(2)}) collective-permute-start(bf16[128,512]{1,0:T(8,128)(2,1)S(1)} %collective-permute-done.35), channel_id=1, source_target_pairs={{0,8},{8,16},{16,24},{24,28},{28,20},{20,12},{12,4},{4,0},{1,9},{9... | collective-permute-start | bytes 393224 | tf_op jit(solution)/shard_map/ppermute | solution.py:103
  171.9 6.8 %collective-permute-start.58 = (bf16[128,512]{1,0:T(8,128)(2,1)S(1)}, bf16[128,512]{1,0:T(8,128)(2,1)S(1)}, u32[]{:S(2)}, u32[]{:S(2)}) collective-permute-start(bf16[128,512]{1,0:T(8,128)(2,1)S(1)} %collective-permute-done.57), channel_id=1, source_target_pairs={{8,0},{16,8},{24,16},{28,24},{20,28},{12,20},{4,12},{0,4},{9,1},{1... | collective-permute-start | bytes 393224 | tf_op jit(solution)/shard_map/ppermute | solution.py:103
  174.2 6.4 %collective-permute-start.51 = (bf16[128,512]{1,0:T(8,128)(2,1)S(1)}, bf16[128,512]{1,0:T(8,128)(2,1)S(1)}, u32[]{:S(2)}, u32[]{:S(2)}) collective-permute-start(bf16[128,512]{1,0:T(8,128)(2,1)S(1)} %collective-permute-done.50), channel_id=1, source_target_pairs={{8,0},{16,8},{24,16},{28,24},{20,28},{12,20},{4,12},{0,4},{9,1},{1... | collective-permute-start | bytes 393224 | tf_op jit(solution)/shard_map/ppermute | solution.py:103
  174.9 6.6 %collective-permute-start.44 = (bf16[128,512]{1,0:T(8,128)(2,1)S(1)}, bf16[128,512]{1,0:T(8,128)(2,1)S(1)}, u32[]{:S(2)}, u32[]{:S(2)}) collective-permute-start(bf16[128,512]{1,0:T(8,128)(2,1)S(1)} %collective-permute-done.43), channel_id=1, source_target_pairs={{0,8},{8,16},{16,24},{24,28},{28,20},{20,12},{12,4},{4,0},{1,9},{9... | collective-permute-start | bytes 393224 | tf_op jit(solution)/shard_map/ppermute | solution.py:103
  177.6 6.5 %collective-permute-start.37 = (bf16[128,512]{1,0:T(8,128)(2,1)S(1)}, bf16[128,512]{1,0:T(8,128)(2,1)S(1)}, u32[]{:S(2)}, u32[]{:S(2)}) collective-permute-start(bf16[128,512]{1,0:T(8,128)(2,1)S(1)} %collective-permute-done.36), channel_id=1, source_target_pairs={{0,8},{8,16},{16,24},{24,28},{28,20},{20,12},{12,4},{4,0},{1,9},{9... | collective-permute-start | bytes 393224 | tf_op jit(solution)/shard_map/ppermute | solution.py:103
  178.8 6.4 %collective-permute-start.59 = (bf16[128,512]{1,0:T(8,128)(2,1)S(1)}, bf16[128,512]{1,0:T(8,128)(2,1)S(1)}, u32[]{:S(2)}, u32[]{:S(2)}) collective-permute-start(bf16[128,512]{1,0:T(8,128)(2,1)S(1)} %collective-permute-done.58), channel_id=1, source_target_pairs={{8,0},{16,8},{24,16},{28,24},{20,28},{12,20},{4,12},{0,4},{9,1},{1... | collective-permute-start | bytes 393224 | tf_op jit(solution)/shard_map/ppermute | solution.py:103
  180.6 6.4 %collective-permute-start.52 = (bf16[128,512]{1,0:T(8,128)(2,1)S(1)}, bf16[128,512]{1,0:T(8,128)(2,1)S(1)}, u32[]{:S(2)}, u32[]{:S(2)}) collective-permute-start(bf16[128,512]{1,0:T(8,128)(2,1)S(1)} %collective-permute-done.51), channel_id=1, source_target_pairs={{8,0},{16,8},{24,16},{28,24},{20,28},{12,20},{4,12},{0,4},{9,1},{1... | collective-permute-start | bytes 393224 | tf_op jit(solution)/shard_map/ppermute | solution.py:103
  181.4 6.8 %collective-permute-start.45 = (bf16[128,512]{1,0:T(8,128)(2,1)S(1)}, bf16[128,512]{1,0:T(8,128)(2,1)S(1)}, u32[]{:S(2)}, u32[]{:S(2)}) collective-permute-start(bf16[128,512]{1,0:T(8,128)(2,1)S(1)} %collective-permute-done.44), channel_id=1, source_target_pairs={{0,8},{8,16},{16,24},{24,28},{28,20},{20,12},{12,4},{4,0},{1,9},{9... | collective-permute-start | bytes 393224 | tf_op jit(solution)/shard_map/ppermute | solution.py:103
  184.1 5.7 %collective-permute-start.38 = (bf16[128,512]{1,0:T(8,128)(2,1)S(1)}, bf16[128,512]{1,0:T(8,128)(2,1)S(1)}, u32[]{:S(2)}, u32[]{:S(2)}) collective-permute-start(bf16[128,512]{1,0:T(8,128)(2,1)S(1)} %collective-permute-done.37), channel_id=1, source_target_pairs={{0,8},{8,16},{16,24},{24,28},{28,20},{20,12},{12,4},{4,0},{1,9},{9... | collective-permute-start | bytes 393224 | tf_op jit(solution)/shard_map/ppermute | solution.py:103
  185.2 6.3 %collective-permute-start.60 = (bf16[128,512]{1,0:T(8,128)(2,1)S(1)}, bf16[128,512]{1,0:T(8,128)(2,1)S(1)}, u32[]{:S(2)}, u32[]{:S(2)}) collective-permute-start(bf16[128,512]{1,0:T(8,128)(2,1)S(1)} %collective-permute-done.59), channel_id=1, source_target_pairs={{8,0},{16,8},{24,16},{28,24},{20,28},{12,20},{4,12},{0,4},{9,1},{1... | collective-permute-start | bytes 393224 | tf_op jit(solution)/shard_map/ppermute | solution.py:103
  187.0 5.9 %collective-permute-start.53 = (bf16[128,512]{1,0:T(8,128)(2,1)S(1)}, bf16[128,512]{1,0:T(8,128)(2,1)S(1)}, u32[]{:S(2)}, u32[]{:S(2)}) collective-permute-start(bf16[128,512]{1,0:T(8,128)(2,1)S(1)} %collective-permute-done.52), channel_id=1, source_target_pairs={{8,0},{16,8},{24,16},{28,24},{20,28},{12,20},{4,12},{0,4},{9,1},{1... | collective-permute-start | bytes 393224 | tf_op jit(solution)/shard_map/ppermute | solution.py:103
  188.2 6.3 %collective-permute-start.46 = (bf16[128,512]{1,0:T(8,128)(2,1)S(1)}, bf16[128,512]{1,0:T(8,128)(2,1)S(1)}, u32[]{:S(2)}, u32[]{:S(2)}) collective-permute-start(bf16[128,512]{1,0:T(8,128)(2,1)S(1)} %collective-permute-done.45), channel_id=1, source_target_pairs={{0,8},{8,16},{16,24},{24,28},{28,20},{20,12},{12,4},{4,0},{1,9},{9... | collective-permute-start | bytes 393224 | tf_op jit(solution)/shard_map/ppermute | solution.py:103
  189.7 6.2 %collective-permute-start.39 = (bf16[128,512]{1,0:T(8,128)(2,1)S(1)}, bf16[128,512]{1,0:T(8,128)(2,1)S(1)}, u32[]{:S(2)}, u32[]{:S(2)}) collective-permute-start(bf16[128,512]{1,0:T(8,128)(2,1)S(1)} %collective-permute-done.38), channel_id=1, source_target_pairs={{0,8},{8,16},{16,24},{24,28},{28,20},{20,12},{12,4},{4,0},{1,9},{9... | collective-permute-start | bytes 393224 | tf_op jit(solution)/shard_map/ppermute | solution.py:103
  191.5 5.2 %collective-permute-start.61 = (bf16[128,512]{1,0:T(8,128)(2,1)S(1)}, bf16[128,512]{1,0:T(8,128)(2,1)S(1)}, u32[]{:S(2)}, u32[]{:S(2)}) collective-permute-start(bf16[128,512]{1,0:T(8,128)(2,1)S(1)} %collective-permute-done.60), channel_id=1, source_target_pairs={{8,0},{16,8},{24,16},{28,24},{20,28},{12,20},{4,12},{0,4},{9,1},{1... | collective-permute-start | bytes 393224 | tf_op jit(solution)/shard_map/ppermute | solution.py:103
  192.9 5.0 %collective-permute-start.54 = (bf16[128,512]{1,0:T(8,128)(2,1)S(1)}, bf16[128,512]{1,0:T(8,128)(2,1)S(1)}, u32[]{:S(2)}, u32[]{:S(2)}) collective-permute-start(bf16[128,512]{1,0:T(8,128)(2,1)S(1)} %collective-permute-done.53), channel_id=1, source_target_pairs={{8,0},{16,8},{24,16},{28,24},{20,28},{12,20},{4,12},{0,4},{9,1},{1... | collective-permute-start | bytes 393224 | tf_op jit(solution)/shard_map/ppermute | solution.py:103
  194.5 5.0 %collective-permute-start.47 = (bf16[128,512]{1,0:T(8,128)(2,1)S(1)}, bf16[128,512]{1,0:T(8,128)(2,1)S(1)}, u32[]{:S(2)}, u32[]{:S(2)}) collective-permute-start(bf16[128,512]{1,0:T(8,128)(2,1)S(1)} %collective-permute-done.46), channel_id=1, source_target_pairs={{0,8},{8,16},{16,24},{24,28},{28,20},{20,12},{12,4},{4,0},{1,9},{9... | collective-permute-start | bytes 393224 | tf_op jit(solution)/shard_map/ppermute | solution.py:103
  195.9 5.0 %collective-permute-start.40 = (bf16[128,512]{1,0:T(8,128)(2,1)S(1)}, bf16[128,512]{1,0:T(8,128)(2,1)S(1)}, u32[]{:S(2)}, u32[]{:S(2)}) collective-permute-start(bf16[128,512]{1,0:T(8,128)(2,1)S(1)} %collective-permute-done.39), channel_id=1, source_target_pairs={{0,8},{8,16},{16,24},{24,28},{28,20},{20,12},{12,4},{4,0},{1,9},{9... | collective-permute-start | bytes 393224 | tf_op jit(solution)/shard_map/ppermute | solution.py:103
  204.8 10.7 %collective-permute-start.64 = (bf16[128,512]{1,0:T(8,128)(2,1)S(1)}, bf16[128,512]{1,0:T(8,128)(2,1)S(1)}, u32[]{:S(2)}, u32[]{:S(2)}) collective-permute-start(bf16[128,512]{1,0:T(8,128)(2,1)S(1)} %get-tuple-element.105), channel_id=1, source_target_pairs={{0,16},{1,24},{2,0},{3,8},{4,20},{5,28},{6,4},{7,12},{8,17},{9,25}... | collective-permute-start | bytes 393224 | tf_op jit(solution)/shard_map/ppermute | solution.py:73
  205.4 14.8 %collective-permute-start.63 = (bf16[128,512]{1,0:T(8,128)(2,1)S(1)}, bf16[128,512]{1,0:T(8,128)(2,1)S(1)}, u32[]{:S(2)}, u32[]{:S(2)}) collective-permute-start(bf16[128,512]{1,0:T(8,128)(2,1)S(1)} %get-tuple-element.103), channel_id=1, source_target_pairs={{0,0},{1,8},{2,16},{3,24},{4,4},{5,12},{6,20},{7,28},{8,1},{9,9},{... | collective-permute-start | bytes 393224 | tf_op jit(solution)/shard_map/ppermute | solution.py:73
  209.4 11.9 %collective-permute-start.66 = (bf16[128,512]{1,0:T(8,128)(2,1)S(1)}, bf16[128,512]{1,0:T(8,128)(2,1)S(1)}, u32[]{:S(2)}, u32[]{:S(2)}) collective-permute-start(bf16[128,512]{1,0:T(8,128)(2,1)S(1)} %get-tuple-element.104), channel_id=1, source_target_pairs={{0,20},{1,28},{2,4},{3,12},{4,16},{5,24},{6,0},{7,8},{8,21},{9,29}... | collective-permute-start | bytes 393224 | tf_op jit(solution)/shard_map/ppermute | solution.py:73
  209.5 14.3 %collective-permute-start.65 = (bf16[128,512]{1,0:T(8,128)(2,1)S(1)}, bf16[128,512]{1,0:T(8,128)(2,1)S(1)}, u32[]{:S(2)}, u32[]{:S(2)}) collective-permute-start(bf16[128,512]{1,0:T(8,128)(2,1)S(1)} %get-tuple-element.102), channel_id=1, source_target_pairs={{0,4},{1,12},{2,20},{3,28},{4,0},{5,8},{6,16},{7,24},{8,5},{9,13},... | collective-permute-start | bytes 393224 | tf_op jit(solution)/shard_map/ppermute | solution.py:73
  (25 other events, 176.4 us)

commit v17 on v14

--- a/solution.py
+++ b/solution.py
@@ -152,7 +152,9 @@
     total = pair + lax.ppermute(
         pair.astype(jnp.bfloat16), "col", [(c, c ^ 2) for c in range(count)]
     ).astype(jnp.float32)
-    other = lax.ppermute(total, "col", [(c, c ^ 1) for c in range(count)])
+    other = lax.ppermute(
+        total.astype(jnp.bfloat16), "col", [(c, c ^ 1) for c in range(count)]
+    ).astype(jnp.float32)
     return jnp.where(
         core, jnp.concatenate([other, total], axis=1), jnp.concatenate([total, other], axis=1)
     )

time: 224 us -> 225 us (level)
    unnamed x66 -> x70, local copies, waits for them, and re-layouts: 4.58 us -> 5.37 us
  transfers between devices with their start and end apart: 68 -> 68, of which waited for: 48 -> 47; matrix products, arithmetic and copies ran while one was open for 8% -> 8% of each run, Pallas kernels for 0% -> 0%
where the time goes in v17:
time: 225 us; the launch traced here: 224 us
  waiting for transfers between devices  80.2 us (36%)
  starting transfers between devices  75.2 us (33%)
  matrix products  29.7 us (13%)
  local copies, waits for them, and re-layouts  17.1 us (8%)
  other arithmetic  14.9 us (7%)
  between operations  6.73 us (3%)
    ppermute x28, starting transfers between devices, ring_gather(): part = lax.ppermute(part, axis, pairs)  31.1 us
    ppermute x28, starting transfers between devices, ring_reduce_scatter(): total = lax.ppermute(total, axis, pairs)  26.7 us
    ppermute x28, waiting for transfers between devices, ring_reduce_scatter(): total = lax.ppermute(total, axis, pairs)  25.1 us
    ppermute x28, waiting for transfers between devices, ring_gather(): part = lax.ppermute(part, axis, pairs)  16.8 us
    dot_general x1, matrix products, shards(): lax.dot_general(residual_grad, out_weight, (((1,), (1,)), ((), ())), pref...  14.4 us
    ppermute x1, waiting for transfers between devices, col_psum(): lax.ppermute(pair.astype(jnp.bfloat16), 'col', [(c, c ^ 2) for c in range...  11.5 us
    ppermute x4, waiting for transfers between devices, placed_sums(): lax.ppermute(piece, ('row', 'col'), pairs).astype(jnp.float32)  10 us
    dot_general x1, matrix products, shards(): jnp.dot(mixed, out_weight, preferred_element_type=jnp.float32)  8.81 us
  transfers between devices with their start and end apart: 68, of which 47 were waited for; matrix products, arithmetic and copies ran while one was open for 8% of the time, Pallas kernels for 0%

profile of v17, /device:TPU:2, one launch (start us, length us, event | category | flops | bytes accessed | tf_op | source)
XLA Modules:
  0.0 223.9 jit_solution(15977172196300500136)
XLA Ops:
  0.7 1.6 copy.23
  3.4 5.8 %all-to-all-start = ((bf16[128,8,256]{2,0,1:T(8,128)(2,1)}), bf16[128,8,256]{2,0,1:T(8,128)(2,1)S(1)}, u32[]{:S(2)}, u32[]{:S(2)}) async-start(bf16[128,8,256]{2,0,1:T(8,128)(2,1)} %copy.25), calls=%async_computation | async-start | bytes 1048576 | tf_op jit(solution)/shard_map/all_to_all | solution.py:24
  18.0 5.7 %all-to-all-done = bf16[128,8,256]{2,0,1:T(8,128)(2,1)S(1)} async-done(((bf16[128,8,256]{2,0,1:T(8,128)(2,1)}), bf16[128,8,256]{2,0,1:T(8,128)(2,1)S(1)}, u32[]{:S(2)}, u32[]{:S(2)}) %all-to-all-start) | async-done | bytes 524320 | tf_op jit(solution)/shard_map/all_to_all | solution.py:24
  25.6 1.5 maximum_select_fusion.1
  27.1 1.5 gather_fusion.5
  29.0 1.5 collective-permute-start.15
  30.6 1.6 gather_fusion.4
  32.5 2.0 collective-permute-start.1
  35.1 1.8 fusion.15
  39.0 1.5 collective-permute-start.16
  40.7 2.0 collective-permute-start.2
  43.3 1.6 collective-permute-done.16
  44.9 1.4 collective-permute-done.23
  46.4 1.5 collective-permute-start.17
  48.4 1.7 collective-permute-start.3
  51.4 1.8 collective-permute-done.24
  53.4 1.3 collective-permute-start.18
  55.5 1.6 collective-permute-start.4
  58.4 2.8 %collective-permute-done.25 = bf16[128,512]{1,0:T(8,128)(2,1)S(1)} collective-permute-done((bf16[128,512]{1,0:T(8,128)(2,1)S(1)}, bf16[128,512]{1,0:T(8,128)(2,1)S(1)}, u32[]{:S(2)}, u32[]{:S(2)}) %collective-permute-start.25) | collective-permute-done | bytes 131104 | tf_op jit(solution)/shard_map/ppermute | solution.py:136
  61.3 1.2 collective-permute-start.19
  63.6 1.4 collective-permute-start.5
  65.6 1.7 collective-permute-done.19
  67.3 2.8 %collective-permute-done.26 = bf16[128,512]{1,0:T(8,128)(2,1)S(1)} collective-permute-done((bf16[128,512]{1,0:T(8,128)(2,1)S(1)}, bf16[128,512]{1,0:T(8,128)(2,1)S(1)}, u32[]{:S(2)}, u32[]{:S(2)}) %collective-permute-start.26) | collective-permute-done | bytes 131104 | tf_op jit(solution)/shard_map/ppermute | solution.py:136
  74.6 1.9 collective-permute-done.20
  76.5 2.5 %collective-permute-done.27 = bf16[128,512]{1,0:T(8,128)(2,1)S(1)} collective-permute-done((bf16[128,512]{1,0:T(8,128)(2,1)S(1)}, bf16[128,512]{1,0:T(8,128)(2,1)S(1)}, u32[]{:S(2)}, u32[]{:S(2)}) %collective-permute-start.27) | collective-permute-done | bytes 131104 | tf_op jit(solution)/shard_map/ppermute | solution.py:136
  79.1 1.2 collective-permute-start.21
  81.1 1.7 collective-permute-start.7
  84.2 1.4 collective-permute-done.28
  86.1 1.6 collective-permute-done.14
  87.8 2.5 %collective-permute-start.29 = (bf16[3,2048]{1,0:T(4,128)(2,1)S(1)}, bf16[3,2048]{1,0:T(4,128)(2,1)S(1)}, u32[]{:S(2)}, u32[]{:S(2)}) collective-permute-start(bf16[3,2048]{1,0:T(4,128)(2,1)S(1)} %pad_maximum_fusion.1), channel_id=1, source_target_pairs={{0,4},{4,8},{8,12},{12,16},{16,20},{20,24},{24,28},{1,5},{5,9},{9,... | collective-permute-start | bytes 36872 | tf_op jit(solution)/shard_map/ppermute | solution.py:13
  90.3 1.2 collective-permute-done.29
  92.8 8.8 %convolution_convert_fusion = bf16[128,4096]{1,0:T(8,128)(2,1)S(1)} fusion(bf16[2048,4096]{1,0:T(8,128)(2,1)} %param.27, bf16[128,2048]{1,0:T(8,128)(2,1)S(1)} %copy-done.18, f32[128,2048]{1,0:T(8,128)S(1)} %fusion.9), kind=kOutput, calls=%fused_computation.6 | convolution fusion | flops 2150891520 | bytes 19398656 | tf_op jit(solution)/shard_map/dot_general | solution.py:212
  101.7 1.9 collective-permute-done.30
  108.3 11.5 %collective-permute-done.31 = bf16[128,2048]{1,0:T(8,128)(2,1)} collective-permute-done((bf16[128,2048]{1,0:T(8,128)(2,1)}, bf16[128,2048]{1,0:T(8,128)(2,1)}, u32[]{:S(2)}, u32[]{:S(2)}) %collective-permute-start.31) | collective-permute-done | bytes 524320 | tf_op jit(solution)/shard_map/ppermute | solution.py:152
  119.8 1.5 fusion.124
  121.5 1.8 collective-permute-done.32
  123.4 1.5 maximum_select_fusion
  125.0 14.4 %multiply_multiply_fusion.2 = (f32[128,2048]{1,0:T(8,128)}, f32[128,2048]{1,0:T(8,128)}, bf16[128,2048]{1,0:T(8,128)(2,1)}) fusion(f32[128]{0:T(128)S(1)} %get-tuple-element.125, f32[2048]{0:T(1024)S(1)} %bitcast.323, f32[128,2048]{1,0:T(8,128)S(1)} %copy-done.11, bf16[128,2048]{1,0:T(8,128)(2,1)} %param.25, bf16[2048,4096]{1,0:T(8,128)(2,1)} %param.27, ...), kind=kOutput, calls=%fused_computation.43 | convolution fusion | flops 2155872256 | bytes 24126464 | tf_op jit(solution)/shard_map/dot_general | solution.py:225
  139.4 1.5 multiply_multiply_fusion.1
  142.8 1.3 collective-permute-start.33
  145.9 3.1 %collective-permute-done.33 = f32[3,2048]{1,0:T(4,128)S(1)} collective-permute-done((f32[3,2048]{1,0:T(4,128)S(1)}, f32[3,2048]{1,0:T(4,128)S(1)}, u32[]{:S(2)}, u32[]{:S(2)}) %collective-permute-start.33) | collective-permute-done | bytes 24608 | tf_op jit(solution)/shard_map/ppermute | solution.py:13
  149.5 3.2 %collective-permute-start.55 = (bf16[128,512]{1,0:T(8,128)(2,1)S(1)}, bf16[128,512]{1,0:T(8,128)(2,1)S(1)}, u32[]{:S(2)}, u32[]{:S(2)}) collective-permute-start(bf16[128,512]{1,0:T(8,128)(2,1)S(1)} %get-tuple-element.105), channel_id=1, source_target_pairs={{8,0},{16,8},{24,16},{28,24},{20,28},{12,20},{4,12},{0,4},{9,1},{1... | collective-permute-start | bytes 393224 | tf_op jit(solution)/shard_map/ppermute | solution.py:103
  152.7 1.4 collective-permute-start.48
  155.4 2.3 %collective-permute-done.55 = bf16[128,512]{1,0:T(8,128)(2,1)S(1)} collective-permute-done((bf16[128,512]{1,0:T(8,128)(2,1)S(1)}, bf16[128,512]{1,0:T(8,128)(2,1)S(1)}, u32[]{:S(2)}, u32[]{:S(2)}) %collective-permute-start.55) | collective-permute-done | bytes 131104 | tf_op jit(solution)/shard_map/ppermute | solution.py:103
  157.7 1.4 collective-permute-start.56
  159.0 1.4 collective-permute-done.48
  160.5 1.4 collective-permute-start.49
  162.5 1.8 collective-permute-start.35
  164.7 2.2 collective-permute-done.49
  166.9 1.3 collective-permute-start.50
  169.4 1.8 collective-permute-start.36
  171.5 1.9 collective-permute-done.50
  175.5 1.4 collective-permute-done.36
  181.8 1.6 collective-permute-done.37
  186.2 1.3 collective-permute-start.53
  189.0 1.7 collective-permute-start.39
  192.2 1.4 collective-permute-start.54
  202.0 1.8 collective-permute-done.62
  204.7 4.1 %collective-permute-start.63 = (bf16[128,512]{1,0:T(8,128)(2,1)S(1)}, bf16[128,512]{1,0:T(8,128)(2,1)S(1)}, u32[]{:S(2)}, u32[]{:S(2)}) collective-permute-start(bf16[128,512]{1,0:T(8,128)(2,1)S(1)} %get-tuple-element.113), channel_id=1, source_target_pairs={{0,0},{1,8},{2,16},{3,24},{4,4},{5,12},{6,20},{7,28},{8,1},{9,9},{... | collective-permute-start | bytes 393224 | tf_op jit(solution)/shard_map/ppermute | solution.py:73
  208.9 2.3 %collective-permute-start.65 = (bf16[128,512]{1,0:T(8,128)(2,1)S(1)}, bf16[128,512]{1,0:T(8,128)(2,1)S(1)}, u32[]{:S(2)}, u32[]{:S(2)}) collective-permute-start(bf16[128,512]{1,0:T(8,128)(2,1)S(1)} %get-tuple-element.112), channel_id=1, source_target_pairs={{0,4},{1,12},{2,20},{3,28},{4,0},{5,8},{6,16},{7,24},{8,5},{9,13},... | collective-permute-start | bytes 393224 | tf_op jit(solution)/shard_map/ppermute | solution.py:73
  211.3 1.8 dynamic-slice_convert_fusion
  213.0 1.6 collective-permute-done.64
  214.6 4.9 %collective-permute-done.63 = bf16[128,512]{1,0:T(8,128)(2,1)S(1)} collective-permute-done((bf16[128,512]{1,0:T(8,128)(2,1)S(1)}, bf16[128,512]{1,0:T(8,128)(2,1)S(1)}, u32[]{:S(2)}, u32[]{:S(2)}) %collective-permute-start.63) | collective-permute-done | bytes 131104 | tf_op jit(solution)/shard_map/ppermute | solution.py:73
  220.6 2.4 %collective-permute-done.65 = bf16[128,512]{1,0:T(8,128)(2,1)S(1)} collective-permute-done((bf16[128,512]{1,0:T(8,128)(2,1)S(1)}, bf16[128,512]{1,0:T(8,128)(2,1)S(1)}, u32[]{:S(2)}, u32[]{:S(2)}) %collective-permute-start.65) | collective-permute-done | bytes 131104 | tf_op jit(solution)/shard_map/ppermute | solution.py:73
  (231 shorter events, 61.7 us)
Async XLA Ops:
  3.4 20.3 %all-to-all-start = ((bf16[128,8,256]{2,0,1:T(8,128)(2,1)}), bf16[128,8,256]{2,0,1:T(8,128)(2,1)S(1)}, u32[]{:S(2)}, u32[]{:S(2)}) async-start(bf16[128,8,256]{2,0,1:T(8,128)(2,1)} %copy.25), calls=%async_computation | async-start | bytes 1048576 | tf_op jit(solution)/shard_map/all_to_all | solution.py:24
  29.0 9.0 %collective-permute-start.15 = (bf16[128,512]{1,0:T(8,128)(2,1)S(1)}, bf16[128,512]{1,0:T(8,128)(2,1)S(1)}, u32[]{:S(2)}, u32[]{:S(2)}) collective-permute-start(bf16[128,512]{1,0:T(8,128)(2,1)S(1)} %get-tuple-element.118), channel_id=1, source_target_pairs={{8,0},{16,8},{24,16},{28,24},{20,28},{12,20},{4,12},{0,4},{9,1},{1... | collective-permute-start | bytes 393224 | tf_op jit(solution)/shard_map/ppermute | solution.py:136
  30.5 7.5 %collective-permute-start.22 = (bf16[128,512]{1,0:T(8,128)(2,1)S(1)}, bf16[128,512]{1,0:T(8,128)(2,1)}, u32[]{:S(2)}, u32[]{:S(2)}) collective-permute-start(bf16[128,512]{1,0:T(8,128)(2,1)S(1)} %get-tuple-element.119), channel_id=1, source_target_pairs={{8,0},{16,8},{24,16},{28,24},{20,28},{12,20},{4,12},{0,4},{9,1},{1... | collective-permute-start | bytes 393224 | tf_op jit(solution)/shard_map/ppermute | solution.py:136
  32.5 8.1 %collective-permute-start.1 = (bf16[128,512]{1,0:T(8,128)(2,1)S(1)}, bf16[128,512]{1,0:T(8,128)(2,1)S(1)}, u32[]{:S(2)}, u32[]{:S(2)}) collective-permute-start(bf16[128,512]{1,0:T(8,128)(2,1)S(1)} %get-tuple-element.116), channel_id=1, source_target_pairs={{0,8},{8,16},{16,24},{24,28},{28,20},{20,12},{12,4},{4,0},{1,9},{9... | collective-permute-start | bytes 393224 | tf_op jit(solution)/shard_map/ppermute | solution.py:136
  34.5 6.1 %collective-permute-start.8 = (bf16[128,512]{1,0:T(8,128)(2,1)S(1)}, bf16[128,512]{1,0:T(8,128)(2,1)S(1)}, u32[]{:S(2)}, u32[]{:S(2)}) collective-permute-start(bf16[128,512]{1,0:T(8,128)(2,1)S(1)} %get-tuple-element.117), channel_id=1, source_target_pairs={{0,8},{8,16},{16,24},{24,28},{28,20},{20,12},{12,4},{4,0},{1,9},{9... | collective-permute-start | bytes 393224 | tf_op jit(solution)/shard_map/ppermute | solution.py:136
  39.0 5.9 %collective-permute-start.16 = (bf16[128,512]{1,0:T(8,128)(2,1)S(1)}, bf16[128,512]{1,0:T(8,128)(2,1)S(1)}, u32[]{:S(2)}, u32[]{:S(2)}) collective-permute-start(bf16[128,512]{1,0:T(8,128)(2,1)S(1)} %get-tuple-element.95), channel_id=1, source_target_pairs={{8,0},{16,8},{24,16},{28,24},{20,28},{12,20},{4,12},{0,4},{9,1},{1... | collective-permute-start | bytes 393224 | tf_op jit(solution)/shard_map/ppermute | solution.py:136
  40.6 5.8 %collective-permute-start.23 = (bf16[128,512]{1,0:T(8,128)(2,1)S(1)}, bf16[128,512]{1,0:T(8,128)(2,1)S(1)}, u32[]{:S(2)}, u32[]{:S(2)}) collective-permute-start(bf16[128,512]{1,0:T(8,128)(2,1)S(1)} %get-tuple-element.96), channel_id=1, source_target_pairs={{8,0},{16,8},{24,16},{28,24},{20,28},{12,20},{4,12},{0,4},{9,1},{1... | collective-permute-start | bytes 393224 | tf_op jit(solution)/shard_map/ppermute | solution.py:136
  40.7 7.6 %collective-permute-start.2 = (bf16[128,512]{1,0:T(8,128)(2,1)S(1)}, bf16[128,512]{1,0:T(8,128)(2,1)S(1)}, u32[]{:S(2)}, u32[]{:S(2)}) collective-permute-start(bf16[128,512]{1,0:T(8,128)(2,1)S(1)} %get-tuple-element.81), channel_id=1, source_target_pairs={{0,8},{8,16},{16,24},{24,28},{28,20},{20,12},{12,4},{4,0},{1,9},{9... | collective-permute-start | bytes 393224 | tf_op jit(solution)/shard_map/ppermute | solution.py:136
  42.7 5.6 %collective-permute-start.9 = (bf16[128,512]{1,0:T(8,128)(2,1)S(1)}, bf16[128,512]{1,0:T(8,128)(2,1)S(1)}, u32[]{:S(2)}, u32[]{:S(2)}) collective-permute-start(bf16[128,512]{1,0:T(8,128)(2,1)S(1)} %get-tuple-element.82), channel_id=1, source_target_pairs={{0,8},{8,16},{16,24},{24,28},{28,20},{20,12},{12,4},{4,0},{1,9},{9... | collective-permute-start | bytes 393224 | tf_op jit(solution)/shard_map/ppermute | solution.py:136
  46.4 5.0 %collective-permute-start.17 = (bf16[128,512]{1,0:T(8,128)(2,1)S(1)}, bf16[128,512]{1,0:T(8,128)(2,1)S(1)}, u32[]{:S(2)}, u32[]{:S(2)}) collective-permute-start(bf16[128,512]{1,0:T(8,128)(2,1)S(1)} %get-tuple-element.93), channel_id=1, source_target_pairs={{8,0},{16,8},{24,16},{28,24},{20,28},{12,20},{4,12},{0,4},{9,1},{1... | collective-permute-start | bytes 393224 | tf_op jit(solution)/shard_map/ppermute | solution.py:136
  47.9 5.4 %collective-permute-start.24 = (bf16[128,512]{1,0:T(8,128)(2,1)S(1)}, bf16[128,512]{1,0:T(8,128)(2,1)S(1)}, u32[]{:S(2)}, u32[]{:S(2)}) collective-permute-start(bf16[128,512]{1,0:T(8,128)(2,1)S(1)} %get-tuple-element.94), channel_id=1, source_target_pairs={{8,0},{16,8},{24,16},{28,24},{20,28},{12,20},{4,12},{0,4},{9,1},{1... | collective-permute-start | bytes 393224 | tf_op jit(solution)/shard_map/ppermute | solution.py:136
  48.4 6.7 %collective-permute-start.3 = (bf16[128,512]{1,0:T(8,128)(2,1)S(1)}, bf16[128,512]{1,0:T(8,128)(2,1)S(1)}, u32[]{:S(2)}, u32[]{:S(2)}) collective-permute-start(bf16[128,512]{1,0:T(8,128)(2,1)S(1)} %get-tuple-element.79), channel_id=1, source_target_pairs={{0,8},{8,16},{16,24},{24,28},{28,20},{20,12},{12,4},{4,0},{1,9},{9... | collective-permute-start | bytes 393224 | tf_op jit(solution)/shard_map/ppermute | solution.py:136
  50.1 5.3 %collective-permute-start.10 = (bf16[128,512]{1,0:T(8,128)(2,1)S(1)}, bf16[128,512]{1,0:T(8,128)(2,1)S(1)}, u32[]{:S(2)}, u32[]{:S(2)}) collective-permute-start(bf16[128,512]{1,0:T(8,128)(2,1)S(1)} %get-tuple-element.80), channel_id=1, source_target_pairs={{0,8},{8,16},{16,24},{24,28},{28,20},{20,12},{12,4},{4,0},{1,9},{9... | collective-permute-start | bytes 393224 | tf_op jit(solution)/shard_map/ppermute | solution.py:136
  53.4 5.1 %collective-permute-start.18 = (bf16[128,512]{1,0:T(8,128)(2,1)S(1)}, bf16[128,512]{1,0:T(8,128)(2,1)S(1)}, u32[]{:S(2)}, u32[]{:S(2)}) collective-permute-start(bf16[128,512]{1,0:T(8,128)(2,1)S(1)} %get-tuple-element.91), channel_id=1, source_target_pairs={{8,0},{16,8},{24,16},{28,24},{20,28},{12,20},{4,12},{0,4},{9,1},{1... | collective-permute-start | bytes 393224 | tf_op jit(solution)/shard_map/ppermute | solution.py:136
  54.7 6.5 %collective-permute-start.25 = (bf16[128,512]{1,0:T(8,128)(2,1)S(1)}, bf16[128,512]{1,0:T(8,128)(2,1)S(1)}, u32[]{:S(2)}, u32[]{:S(2)}) collective-permute-start(bf16[128,512]{1,0:T(8,128)(2,1)S(1)} %get-tuple-element.92), channel_id=1, source_target_pairs={{8,0},{16,8},{24,16},{28,24},{20,28},{12,20},{4,12},{0,4},{9,1},{1... | collective-permute-start | bytes 393224 | tf_op jit(solution)/shard_map/ppermute | solution.py:136
  55.5 7.1 %collective-permute-start.4 = (bf16[128,512]{1,0:T(8,128)(2,1)S(1)}, bf16[128,512]{1,0:T(8,128)(2,1)S(1)}, u32[]{:S(2)}, u32[]{:S(2)}) collective-permute-start(bf16[128,512]{1,0:T(8,128)(2,1)S(1)} %get-tuple-element.77), channel_id=1, source_target_pairs={{0,8},{8,16},{16,24},{24,28},{28,20},{20,12},{12,4},{4,0},{1,9},{9... | collective-permute-start | bytes 393224 | tf_op jit(solution)/shard_map/ppermute | solution.py:136
  57.1 6.3 %collective-permute-start.11 = (bf16[128,512]{1,0:T(8,128)(2,1)S(1)}, bf16[128,512]{1,0:T(8,128)(2,1)S(1)}, u32[]{:S(2)}, u32[]{:S(2)}) collective-permute-start(bf16[128,512]{1,0:T(8,128)(2,1)S(1)} %get-tuple-element.78), channel_id=1, source_target_pairs={{0,8},{8,16},{16,24},{24,28},{28,20},{20,12},{12,4},{4,0},{1,9},{9... | collective-permute-start | bytes 393224 | tf_op jit(solution)/shard_map/ppermute | solution.py:136
  61.3 6.0 %collective-permute-start.19 = (bf16[128,512]{1,0:T(8,128)(2,1)S(1)}, bf16[128,512]{1,0:T(8,128)(2,1)S(1)}, u32[]{:S(2)}, u32[]{:S(2)}) collective-permute-start(bf16[128,512]{1,0:T(8,128)(2,1)S(1)} %get-tuple-element.89), channel_id=1, source_target_pairs={{8,0},{16,8},{24,16},{28,24},{20,28},{12,20},{4,12},{0,4},{9,1},{1... | collective-permute-start | bytes 393224 | tf_op jit(solution)/shard_map/ppermute | solution.py:136
  62.6 7.6 %collective-permute-start.26 = (bf16[128,512]{1,0:T(8,128)(2,1)S(1)}, bf16[128,512]{1,0:T(8,128)(2,1)S(1)}, u32[]{:S(2)}, u32[]{:S(2)}) collective-permute-start(bf16[128,512]{1,0:T(8,128)(2,1)S(1)} %get-tuple-element.90), channel_id=1, source_target_pairs={{8,0},{16,8},{24,16},{28,24},{20,28},{12,20},{4,12},{0,4},{9,1},{1... | collective-permute-start | bytes 393224 | tf_op jit(solution)/shard_map/ppermute | solution.py:136
  63.6 7.8 %collective-permute-start.5 = (bf16[128,512]{1,0:T(8,128)(2,1)S(1)}, bf16[128,512]{1,0:T(8,128)(2,1)S(1)}, u32[]{:S(2)}, u32[]{:S(2)}) collective-permute-start(bf16[128,512]{1,0:T(8,128)(2,1)S(1)} %get-tuple-element.75), channel_id=1, source_target_pairs={{0,8},{8,16},{16,24},{24,28},{28,20},{20,12},{12,4},{4,0},{1,9},{9... | collective-permute-start | bytes 393224 | tf_op jit(solution)/shard_map/ppermute | solution.py:136
  65.0 7.5 %collective-permute-start.12 = (bf16[128,512]{1,0:T(8,128)(2,1)S(1)}, bf16[128,512]{1,0:T(8,128)(2,1)S(1)}, u32[]{:S(2)}, u32[]{:S(2)}) collective-permute-start(bf16[128,512]{1,0:T(8,128)(2,1)S(1)} %get-tuple-element.76), channel_id=1, source_target_pairs={{0,8},{8,16},{16,24},{24,28},{28,20},{20,12},{12,4},{4,0},{1,9},{9... | collective-permute-start | bytes 393224 | tf_op jit(solution)/shard_map/ppermute | solution.py:136
  70.2 6.3 %collective-permute-start.20 = (bf16[128,512]{1,0:T(8,128)(2,1)S(1)}, bf16[128,512]{1,0:T(8,128)(2,1)S(1)}, u32[]{:S(2)}, u32[]{:S(2)}) collective-permute-start(bf16[128,512]{1,0:T(8,128)(2,1)S(1)} %get-tuple-element.87), channel_id=1, source_target_pairs={{8,0},{16,8},{24,16},{28,24},{20,28},{12,20},{4,12},{0,4},{9,1},{1... | collective-permute-start | bytes 393224 | tf_op jit(solution)/shard_map/ppermute | solution.py:136
  71.3 7.7 %collective-permute-start.27 = (bf16[128,512]{1,0:T(8,128)(2,1)S(1)}, bf16[128,512]{1,0:T(8,128)(2,1)S(1)}, u32[]{:S(2)}, u32[]{:S(2)}) collective-permute-start(bf16[128,512]{1,0:T(8,128)(2,1)S(1)} %get-tuple-element.88), channel_id=1, source_target_pairs={{8,0},{16,8},{24,16},{28,24},{20,28},{12,20},{4,12},{0,4},{9,1},{1... | collective-permute-start | bytes 393224 | tf_op jit(solution)/shard_map/ppermute | solution.py:136
  72.6 8.1 %collective-permute-start.6 = (bf16[128,512]{1,0:T(8,128)(2,1)S(1)}, bf16[128,512]{1,0:T(8,128)(2,1)S(1)}, u32[]{:S(2)}, u32[]{:S(2)}) collective-permute-start(bf16[128,512]{1,0:T(8,128)(2,1)S(1)} %get-tuple-element.73), channel_id=1, source_target_pairs={{0,8},{8,16},{16,24},{24,28},{28,20},{20,12},{12,4},{4,0},{1,9},{9... | collective-permute-start | bytes 393224 | tf_op jit(solution)/shard_map/ppermute | solution.py:136
  73.7 7.3 %collective-permute-start.13 = (bf16[128,512]{1,0:T(8,128)(2,1)S(1)}, bf16[128,512]{1,0:T(8,128)(2,1)S(1)}, u32[]{:S(2)}, u32[]{:S(2)}) collective-permute-start(bf16[128,512]{1,0:T(8,128)(2,1)S(1)} %get-tuple-element.74), channel_id=1, source_target_pairs={{0,8},{8,16},{16,24},{24,28},{28,20},{20,12},{12,4},{4,0},{1,9},{9... | collective-permute-start | bytes 393224 | tf_op jit(solution)/shard_map/ppermute | solution.py:136
  79.1 5.0 %collective-permute-start.21 = (bf16[128,512]{1,0:T(8,128)(2,1)S(1)}, bf16[128,512]{1,0:T(8,128)(2,1)S(1)}, u32[]{:S(2)}, u32[]{:S(2)}) collective-permute-start(bf16[128,512]{1,0:T(8,128)(2,1)S(1)} %get-tuple-element.85), channel_id=1, source_target_pairs={{8,0},{16,8},{24,16},{28,24},{20,28},{12,20},{4,12},{0,4},{9,1},{1... | collective-permute-start | bytes 393224 | tf_op jit(solution)/shard_map/ppermute | solution.py:136
  80.4 5.2 %collective-permute-start.28 = (bf16[128,512]{1,0:T(8,128)(2,1)S(1)}, bf16[128,512]{1,0:T(8,128)(2,1)S(1)}, u32[]{:S(2)}, u32[]{:S(2)}) collective-permute-start(bf16[128,512]{1,0:T(8,128)(2,1)S(1)} %get-tuple-element.86), channel_id=1, source_target_pairs={{8,0},{16,8},{24,16},{28,24},{20,28},{12,20},{4,12},{0,4},{9,1},{1... | collective-permute-start | bytes 393224 | tf_op jit(solution)/shard_map/ppermute | solution.py:136
  81.1 5.0 %collective-permute-start.7 = (bf16[128,512]{1,0:T(8,128)(2,1)S(1)}, bf16[128,512]{1,0:T(8,128)(2,1)S(1)}, u32[]{:S(2)}, u32[]{:S(2)}) collective-permute-start(bf16[128,512]{1,0:T(8,128)(2,1)S(1)} %get-tuple-element.71), channel_id=1, source_target_pairs={{0,8},{8,16},{16,24},{24,28},{28,20},{20,12},{12,4},{4,0},{1,9},{9... | collective-permute-start | bytes 393224 | tf_op jit(solution)/shard_map/ppermute | solution.py:136
  82.7 5.0 %collective-permute-start.14 = (bf16[128,512]{1,0:T(8,128)(2,1)S(1)}, bf16[128,512]{1,0:T(8,128)(2,1)S(1)}, u32[]{:S(2)}, u32[]{:S(2)}) collective-permute-start(bf16[128,512]{1,0:T(8,128)(2,1)S(1)} %get-tuple-element.72), channel_id=1, source_target_pairs={{0,8},{8,16},{16,24},{24,28},{28,20},{20,12},{12,4},{4,0},{1,9},{9... | collective-permute-start | bytes 393224 | tf_op jit(solution)/shard_map/ppermute | solution.py:136
  87.8 3.7 %collective-permute-start.29 = (bf16[3,2048]{1,0:T(4,128)(2,1)S(1)}, bf16[3,2048]{1,0:T(4,128)(2,1)S(1)}, u32[]{:S(2)}, u32[]{:S(2)}) collective-permute-start(bf16[3,2048]{1,0:T(4,128)(2,1)S(1)} %pad_maximum_fusion.1), channel_id=1, source_target_pairs={{0,4},{4,8},{8,12},{12,16},{16,20},{20,24},{24,28},{1,5},{5,9},{9,... | collective-permute-start | bytes 36872 | tf_op jit(solution)/shard_map/ppermute | solution.py:13
  105.5 14.3 %collective-permute-start.31 = (bf16[128,2048]{1,0:T(8,128)(2,1)}, bf16[128,2048]{1,0:T(8,128)(2,1)}, u32[]{:S(2)}, u32[]{:S(2)}) collective-permute-start(bf16[128,2048]{1,0:T(8,128)(2,1)} %fusion.21), channel_id=1, source_target_pairs={{0,2},{1,3},{2,0},{3,1},{4,6},{5,7},{6,4},{7,5},{8,10},{9,11},{10,... | collective-permute-start | bytes 1572872 | tf_op jit(solution)/shard_map/ppermute | solution.py:152
  142.8 6.3 %collective-permute-start.33 = (f32[3,2048]{1,0:T(4,128)S(1)}, f32[3,2048]{1,0:T(4,128)S(1)}, u32[]{:S(2)}, u32[]{:S(2)}) collective-permute-start(f32[3,2048]{1,0:T(4,128)S(1)} %slice_add_fusion), channel_id=1, source_target_pairs={{4,0},{8,4},{12,8},{16,12},{20,16},{24,20},{28,24},{5,1},{9,5},{13... | collective-permute-start | bytes 73736 | tf_op jit(solution)/shard_map/ppermute | solution.py:13
  149.5 8.2 %collective-permute-start.55 = (bf16[128,512]{1,0:T(8,128)(2,1)S(1)}, bf16[128,512]{1,0:T(8,128)(2,1)S(1)}, u32[]{:S(2)}, u32[]{:S(2)}) collective-permute-start(bf16[128,512]{1,0:T(8,128)(2,1)S(1)} %get-tuple-element.105), channel_id=1, source_target_pairs={{8,0},{16,8},{24,16},{28,24},{20,28},{12,20},{4,12},{0,4},{9,1},{1... | collective-permute-start | bytes 393224 | tf_op jit(solution)/shard_map/ppermute | solution.py:103
  152.7 7.8 %collective-permute-start.48 = (bf16[128,512]{1,0:T(8,128)(2,1)S(1)}, bf16[128,512]{1,0:T(8,128)(2,1)S(1)}, u32[]{:S(2)}, u32[]{:S(2)}) collective-permute-start(bf16[128,512]{1,0:T(8,128)(2,1)S(1)} %get-tuple-element.106), channel_id=1, source_target_pairs={{8,0},{16,8},{24,16},{28,24},{20,28},{12,20},{4,12},{0,4},{9,1},{1... | collective-permute-start | bytes 393224 | tf_op jit(solution)/shard_map/ppermute | solution.py:103
  154.1 7.7 %collective-permute-start.41 = (bf16[128,512]{1,0:T(8,128)(2,1)S(1)}, bf16[128,512]{1,0:T(8,128)(2,1)S(1)}, u32[]{:S(2)}, u32[]{:S(2)}) collective-permute-start(bf16[128,512]{1,0:T(8,128)(2,1)S(1)} %get-tuple-element.107), channel_id=1, source_target_pairs={{0,8},{8,16},{16,24},{24,28},{28,20},{20,12},{12,4},{4,0},{1,9},{9... | collective-permute-start | bytes 393224 | tf_op jit(solution)/shard_map/ppermute | solution.py:103
  154.7 7.8 %collective-permute-start.34 = (bf16[128,512]{1,0:T(8,128)(2,1)S(1)}, bf16[128,512]{1,0:T(8,128)(2,1)S(1)}, u32[]{:S(2)}, u32[]{:S(2)}) collective-permute-start(bf16[128,512]{1,0:T(8,128)(2,1)S(1)} %get-tuple-element.104), channel_id=1, source_target_pairs={{0,8},{8,16},{16,24},{24,28},{28,20},{20,12},{12,4},{4,0},{1,9},{9... | collective-permute-start | bytes 393224 | tf_op jit(solution)/shard_map/ppermute | solution.py:103
  157.7 6.6 %collective-permute-start.56 = (bf16[128,512]{1,0:T(8,128)(2,1)S(1)}, bf16[128,512]{1,0:T(8,128)(2,1)S(1)}, u32[]{:S(2)}, u32[]{:S(2)}) collective-permute-start(bf16[128,512]{1,0:T(8,128)(2,1)S(1)} %collective-permute-done.55), channel_id=1, source_target_pairs={{8,0},{16,8},{24,16},{28,24},{20,28},{12,20},{4,12},{0,4},{9,1},{1... | collective-permute-start | bytes 393224 | tf_op jit(solution)/shard_map/ppermute | solution.py:103
  160.5 6.4 %collective-permute-start.49 = (bf16[128,512]{1,0:T(8,128)(2,1)S(1)}, bf16[128,512]{1,0:T(8,128)(2,1)S(1)}, u32[]{:S(2)}, u32[]{:S(2)}) collective-permute-start(bf16[128,512]{1,0:T(8,128)(2,1)S(1)} %collective-permute-done.48), channel_id=1, source_target_pairs={{8,0},{16,8},{24,16},{28,24},{20,28},{12,20},{4,12},{0,4},{9,1},{1... | collective-permute-start | bytes 393224 | tf_op jit(solution)/shard_map/ppermute | solution.py:103
  161.9 6.3 %collective-permute-start.42 = (bf16[128,512]{1,0:T(8,128)(2,1)S(1)}, bf16[128,512]{1,0:T(8,128)(2,1)S(1)}, u32[]{:S(2)}, u32[]{:S(2)}) collective-permute-start(bf16[128,512]{1,0:T(8,128)(2,1)S(1)} %collective-permute-done.41), channel_id=1, source_target_pairs={{0,8},{8,16},{16,24},{24,28},{28,20},{20,12},{12,4},{4,0},{1,9},{9... | collective-permute-start | bytes 393224 | tf_op jit(solution)/shard_map/ppermute | solution.py:103
  162.5 6.9 %collective-permute-start.35 = (bf16[128,512]{1,0:T(8,128)(2,1)S(1)}, bf16[128,512]{1,0:T(8,128)(2,1)S(1)}, u32[]{:S(2)}, u32[]{:S(2)}) collective-permute-start(bf16[128,512]{1,0:T(8,128)(2,1)S(1)} %collective-permute-done.34), channel_id=1, source_target_pairs={{0,8},{8,16},{16,24},{24,28},{28,20},{20,12},{12,4},{4,0},{1,9},{9... | collective-permute-start | bytes 393224 | tf_op jit(solution)/shard_map/ppermute | solution.py:103
  164.3 6.9 %collective-permute-start.57 = (bf16[128,512]{1,0:T(8,128)(2,1)S(1)}, bf16[128,512]{1,0:T(8,128)(2,1)S(1)}, u32[]{:S(2)}, u32[]{:S(2)}) collective-permute-start(bf16[128,512]{1,0:T(8,128)(2,1)S(1)} %collective-permute-done.56), channel_id=1, source_target_pairs={{8,0},{16,8},{24,16},{28,24},{20,28},{12,20},{4,12},{0,4},{9,1},{1... | collective-permute-start | bytes 393224 | tf_op jit(solution)/shard_map/ppermute | solution.py:103
  166.9 6.5 %collective-permute-start.50 = (bf16[128,512]{1,0:T(8,128)(2,1)S(1)}, bf16[128,512]{1,0:T(8,128)(2,1)S(1)}, u32[]{:S(2)}, u32[]{:S(2)}) collective-permute-start(bf16[128,512]{1,0:T(8,128)(2,1)S(1)} %collective-permute-done.49), channel_id=1, source_target_pairs={{8,0},{16,8},{24,16},{28,24},{20,28},{12,20},{4,12},{0,4},{9,1},{1... | collective-permute-start | bytes 393224 | tf_op jit(solution)/shard_map/ppermute | solution.py:103
  168.2 6.1 %collective-permute-start.43 = (bf16[128,512]{1,0:T(8,128)(2,1)S(1)}, bf16[128,512]{1,0:T(8,128)(2,1)S(1)}, u32[]{:S(2)}, u32[]{:S(2)}) collective-permute-start(bf16[128,512]{1,0:T(8,128)(2,1)S(1)} %collective-permute-done.42), channel_id=1, source_target_pairs={{0,8},{8,16},{16,24},{24,28},{28,20},{20,12},{12,4},{4,0},{1,9},{9... | collective-permute-start | bytes 393224 | tf_op jit(solution)/shard_map/ppermute | solution.py:103
  169.4 7.4 %collective-permute-start.36 = (bf16[128,512]{1,0:T(8,128)(2,1)S(1)}, bf16[128,512]{1,0:T(8,128)(2,1)S(1)}, u32[]{:S(2)}, u32[]{:S(2)}) collective-permute-start(bf16[128,512]{1,0:T(8,128)(2,1)S(1)} %collective-permute-done.35), channel_id=1, source_target_pairs={{0,8},{8,16},{16,24},{24,28},{28,20},{20,12},{12,4},{4,0},{1,9},{9... | collective-permute-start | bytes 393224 | tf_op jit(solution)/shard_map/ppermute | solution.py:103
  171.2 6.8 %collective-permute-start.58 = (bf16[128,512]{1,0:T(8,128)(2,1)S(1)}, bf16[128,512]{1,0:T(8,128)(2,1)S(1)}, u32[]{:S(2)}, u32[]{:S(2)}) collective-permute-start(bf16[128,512]{1,0:T(8,128)(2,1)S(1)} %collective-permute-done.57), channel_id=1, source_target_pairs={{8,0},{16,8},{24,16},{28,24},{20,28},{12,20},{4,12},{0,4},{9,1},{1... | collective-permute-start | bytes 393224 | tf_op jit(solution)/shard_map/ppermute | solution.py:103
  173.4 6.4 %collective-permute-start.51 = (bf16[128,512]{1,0:T(8,128)(2,1)S(1)}, bf16[128,512]{1,0:T(8,128)(2,1)S(1)}, u32[]{:S(2)}, u32[]{:S(2)}) collective-permute-start(bf16[128,512]{1,0:T(8,128)(2,1)S(1)} %collective-permute-done.50), channel_id=1, source_target_pairs={{8,0},{16,8},{24,16},{28,24},{20,28},{12,20},{4,12},{0,4},{9,1},{1... | collective-permute-start | bytes 393224 | tf_op jit(solution)/shard_map/ppermute | solution.py:103
  174.3 6.4 %collective-permute-start.44 = (bf16[128,512]{1,0:T(8,128)(2,1)S(1)}, bf16[128,512]{1,0:T(8,128)(2,1)S(1)}, u32[]{:S(2)}, u32[]{:S(2)}) collective-permute-start(bf16[128,512]{1,0:T(8,128)(2,1)S(1)} %collective-permute-done.43), channel_id=1, source_target_pairs={{0,8},{8,16},{16,24},{24,28},{28,20},{20,12},{12,4},{4,0},{1,9},{9... | collective-permute-start | bytes 393224 | tf_op jit(solution)/shard_map/ppermute | solution.py:103
  176.9 6.6 %collective-permute-start.37 = (bf16[128,512]{1,0:T(8,128)(2,1)S(1)}, bf16[128,512]{1,0:T(8,128)(2,1)S(1)}, u32[]{:S(2)}, u32[]{:S(2)}) collective-permute-start(bf16[128,512]{1,0:T(8,128)(2,1)S(1)} %collective-permute-done.36), channel_id=1, source_target_pairs={{0,8},{8,16},{16,24},{24,28},{28,20},{20,12},{12,4},{4,0},{1,9},{9... | collective-permute-start | bytes 393224 | tf_op jit(solution)/shard_map/ppermute | solution.py:103
  178.0 6.4 %collective-permute-start.59 = (bf16[128,512]{1,0:T(8,128)(2,1)S(1)}, bf16[128,512]{1,0:T(8,128)(2,1)S(1)}, u32[]{:S(2)}, u32[]{:S(2)}) collective-permute-start(bf16[128,512]{1,0:T(8,128)(2,1)S(1)} %collective-permute-done.58), channel_id=1, source_target_pairs={{8,0},{16,8},{24,16},{28,24},{20,28},{12,20},{4,12},{0,4},{9,1},{1... | collective-permute-start | bytes 393224 | tf_op jit(solution)/shard_map/ppermute | solution.py:103
  179.8 6.5 %collective-permute-start.52 = (bf16[128,512]{1,0:T(8,128)(2,1)S(1)}, bf16[128,512]{1,0:T(8,128)(2,1)S(1)}, u32[]{:S(2)}, u32[]{:S(2)}) collective-permute-start(bf16[128,512]{1,0:T(8,128)(2,1)S(1)} %collective-permute-done.51), channel_id=1, source_target_pairs={{8,0},{16,8},{24,16},{28,24},{20,28},{12,20},{4,12},{0,4},{9,1},{1... | collective-permute-start | bytes 393224 | tf_op jit(solution)/shard_map/ppermute | solution.py:103
  180.7 6.8 %collective-permute-start.45 = (bf16[128,512]{1,0:T(8,128)(2,1)S(1)}, bf16[128,512]{1,0:T(8,128)(2,1)S(1)}, u32[]{:S(2)}, u32[]{:S(2)}) collective-permute-start(bf16[128,512]{1,0:T(8,128)(2,1)S(1)} %collective-permute-done.44), channel_id=1, source_target_pairs={{0,8},{8,16},{16,24},{24,28},{28,20},{20,12},{12,4},{4,0},{1,9},{9... | collective-permute-start | bytes 393224 | tf_op jit(solution)/shard_map/ppermute | solution.py:103
  183.4 5.6 %collective-permute-start.38 = (bf16[128,512]{1,0:T(8,128)(2,1)S(1)}, bf16[128,512]{1,0:T(8,128)(2,1)S(1)}, u32[]{:S(2)}, u32[]{:S(2)}) collective-permute-start(bf16[128,512]{1,0:T(8,128)(2,1)S(1)} %collective-permute-done.37), channel_id=1, source_target_pairs={{0,8},{8,16},{16,24},{24,28},{28,20},{20,12},{12,4},{4,0},{1,9},{9... | collective-permute-start | bytes 393224 | tf_op jit(solution)/shard_map/ppermute | solution.py:103
  184.4 6.4 %collective-permute-start.60 = (bf16[128,512]{1,0:T(8,128)(2,1)S(1)}, bf16[128,512]{1,0:T(8,128)(2,1)S(1)}, u32[]{:S(2)}, u32[]{:S(2)}) collective-permute-start(bf16[128,512]{1,0:T(8,128)(2,1)S(1)} %collective-permute-done.59), channel_id=1, source_target_pairs={{8,0},{16,8},{24,16},{28,24},{20,28},{12,20},{4,12},{0,4},{9,1},{1... | collective-permute-start | bytes 393224 | tf_op jit(solution)/shard_map/ppermute | solution.py:103
  186.2 5.9 %collective-permute-start.53 = (bf16[128,512]{1,0:T(8,128)(2,1)S(1)}, bf16[128,512]{1,0:T(8,128)(2,1)S(1)}, u32[]{:S(2)}, u32[]{:S(2)}) collective-permute-start(bf16[128,512]{1,0:T(8,128)(2,1)S(1)} %collective-permute-done.52), channel_id=1, source_target_pairs={{8,0},{16,8},{24,16},{28,24},{20,28},{12,20},{4,12},{0,4},{9,1},{1... | collective-permute-start | bytes 393224 | tf_op jit(solution)/shard_map/ppermute | solution.py:103
  187.5 6.3 %collective-permute-start.46 = (bf16[128,512]{1,0:T(8,128)(2,1)S(1)}, bf16[128,512]{1,0:T(8,128)(2,1)S(1)}, u32[]{:S(2)}, u32[]{:S(2)}) collective-permute-start(bf16[128,512]{1,0:T(8,128)(2,1)S(1)} %collective-permute-done.45), channel_id=1, source_target_pairs={{0,8},{8,16},{16,24},{24,28},{28,20},{20,12},{12,4},{4,0},{1,9},{9... | collective-permute-start | bytes 393224 | tf_op jit(solution)/shard_map/ppermute | solution.py:103
  189.0 6.2 %collective-permute-start.39 = (bf16[128,512]{1,0:T(8,128)(2,1)S(1)}, bf16[128,512]{1,0:T(8,128)(2,1)S(1)}, u32[]{:S(2)}, u32[]{:S(2)}) collective-permute-start(bf16[128,512]{1,0:T(8,128)(2,1)S(1)} %collective-permute-done.38), channel_id=1, source_target_pairs={{0,8},{8,16},{16,24},{24,28},{28,20},{20,12},{12,4},{4,0},{1,9},{9... | collective-permute-start | bytes 393224 | tf_op jit(solution)/shard_map/ppermute | solution.py:103
  190.8 5.1 %collective-permute-start.61 = (bf16[128,512]{1,0:T(8,128)(2,1)S(1)}, bf16[128,512]{1,0:T(8,128)(2,1)S(1)}, u32[]{:S(2)}, u32[]{:S(2)}) collective-permute-start(bf16[128,512]{1,0:T(8,128)(2,1)S(1)} %collective-permute-done.60), channel_id=1, source_target_pairs={{8,0},{16,8},{24,16},{28,24},{20,28},{12,20},{4,12},{0,4},{9,1},{1... | collective-permute-start | bytes 393224 | tf_op jit(solution)/shard_map/ppermute | solution.py:103
  192.2 5.1 %collective-permute-start.54 = (bf16[128,512]{1,0:T(8,128)(2,1)S(1)}, bf16[128,512]{1,0:T(8,128)(2,1)S(1)}, u32[]{:S(2)}, u32[]{:S(2)}) collective-permute-start(bf16[128,512]{1,0:T(8,128)(2,1)S(1)} %collective-permute-done.53), channel_id=1, source_target_pairs={{8,0},{16,8},{24,16},{28,24},{20,28},{12,20},{4,12},{0,4},{9,1},{1... | collective-permute-start | bytes 393224 | tf_op jit(solution)/shard_map/ppermute | solution.py:103
  193.8 5.0 %collective-permute-start.47 = (bf16[128,512]{1,0:T(8,128)(2,1)S(1)}, bf16[128,512]{1,0:T(8,128)(2,1)S(1)}, u32[]{:S(2)}, u32[]{:S(2)}) collective-permute-start(bf16[128,512]{1,0:T(8,128)(2,1)S(1)} %collective-permute-done.46), channel_id=1, source_target_pairs={{0,8},{8,16},{16,24},{24,28},{28,20},{20,12},{12,4},{4,0},{1,9},{9... | collective-permute-start | bytes 393224 | tf_op jit(solution)/shard_map/ppermute | solution.py:103
  195.2 5.0 %collective-permute-start.40 = (bf16[128,512]{1,0:T(8,128)(2,1)S(1)}, bf16[128,512]{1,0:T(8,128)(2,1)S(1)}, u32[]{:S(2)}, u32[]{:S(2)}) collective-permute-start(bf16[128,512]{1,0:T(8,128)(2,1)S(1)} %collective-permute-done.39), channel_id=1, source_target_pairs={{0,8},{8,16},{16,24},{24,28},{28,20},{20,12},{12,4},{4,0},{1,9},{9... | collective-permute-start | bytes 393224 | tf_op jit(solution)/shard_map/ppermute | solution.py:103
  204.1 10.5 %collective-permute-start.64 = (bf16[128,512]{1,0:T(8,128)(2,1)S(1)}, bf16[128,512]{1,0:T(8,128)(2,1)S(1)}, u32[]{:S(2)}, u32[]{:S(2)}) collective-permute-start(bf16[128,512]{1,0:T(8,128)(2,1)S(1)} %get-tuple-element.115), channel_id=1, source_target_pairs={{0,16},{1,24},{2,0},{3,8},{4,20},{5,28},{6,4},{7,12},{8,17},{9,25}... | collective-permute-start | bytes 393224 | tf_op jit(solution)/shard_map/ppermute | solution.py:73
  204.7 14.8 %collective-permute-start.63 = (bf16[128,512]{1,0:T(8,128)(2,1)S(1)}, bf16[128,512]{1,0:T(8,128)(2,1)S(1)}, u32[]{:S(2)}, u32[]{:S(2)}) collective-permute-start(bf16[128,512]{1,0:T(8,128)(2,1)S(1)} %get-tuple-element.113), channel_id=1, source_target_pairs={{0,0},{1,8},{2,16},{3,24},{4,4},{5,12},{6,20},{7,28},{8,1},{9,9},{... | collective-permute-start | bytes 393224 | tf_op jit(solution)/shard_map/ppermute | solution.py:73
  208.9 11.8 %collective-permute-start.66 = (bf16[128,512]{1,0:T(8,128)(2,1)S(1)}, bf16[128,512]{1,0:T(8,128)(2,1)S(1)}, u32[]{:S(2)}, u32[]{:S(2)}) collective-permute-start(bf16[128,512]{1,0:T(8,128)(2,1)S(1)} %get-tuple-element.114), channel_id=1, source_target_pairs={{0,20},{1,28},{2,4},{3,12},{4,16},{5,24},{6,0},{7,8},{8,21},{9,29}... | collective-permute-start | bytes 393224 | tf_op jit(solution)/shard_map/ppermute | solution.py:73
  208.9 14.1 %collective-permute-start.65 = (bf16[128,512]{1,0:T(8,128)(2,1)S(1)}, bf16[128,512]{1,0:T(8,128)(2,1)S(1)}, u32[]{:S(2)}, u32[]{:S(2)}) collective-permute-start(bf16[128,512]{1,0:T(8,128)(2,1)S(1)} %get-tuple-element.112), channel_id=1, source_target_pairs={{0,4},{1,12},{2,20},{3,28},{4,0},{5,8},{6,16},{7,24},{8,5},{9,13},... | collective-permute-start | bytes 393224 | tf_op jit(solution)/shard_map/ppermute | solution.py:73
  (26 other events, 153.5 us)

commit v18 on v14

--- a/solution.py
+++ b/solution.py
@@ -247,7 +247,7 @@
         )
     ).astype(jnp.bfloat16)
     if moves_tokens:
-        stacks, sources = ring_gather(grad_x, "row")
+        stacks, sources = ring_gather(grad_x, "row", chains=1)
         contract = (((2,), (1,)), ((), ()))
         weight_parts = jnp.split(in_weight, len(stacks), axis=1)
         grad_cols = lax.dot_general(

time: 224 us -> 224 us (level)
  waiting for transfers between devices: 80.8 us -> 106 us
  starting transfers between devices: 75.1 us -> 61.3 us
  other arithmetic: 14.4 us -> 8.44 us
  local copies, waits for them, and re-layouts: 16.4 us -> 10.6 us
    ppermute x28 -> x14, waiting for transfers between devices: 17.3 us -> 36.8 us  [ring_gather(): part = lax.ppermute(part, axis, pairs)]
    ppermute x28 -> x14, starting transfers between devices: 30.7 us -> 16.1 us  [ring_gather(): part = lax.ppermute(part, axis, pairs)]
    unnamed x66 -> x34, local copies, waits for them, and re-layouts: 4.58 us -> 2.25 us
  transfers between devices with their start and end apart: 68 -> 54, of which waited for: 48 -> 40; matrix products, arithmetic and copies ran while one was open for 8% -> 6% of each run, Pallas kernels for 0% -> 0%
where the time goes in v18:
time: 224 us
  waiting for transfers between devices  106 us (47%)
  starting transfers between devices  61.3 us (27%)
  matrix products  30.9 us (14%)
  local copies, waits for them, and re-layouts  10.6 us (5%)
  other arithmetic  8.44 us (4%)
  between operations  6.48 us (3%)
    ppermute x14, waiting for transfers between devices, ring_gather(): part = lax.ppermute(part, axis, pairs)  36.8 us
    ppermute x28, starting transfers between devices, ring_reduce_scatter(): total = lax.ppermute(total, axis, pairs)  27.7 us
    ppermute x28, waiting for transfers between devices, ring_reduce_scatter(): total = lax.ppermute(total, axis, pairs)  25.1 us
    ppermute x14, starting transfers between devices, ring_gather(): part = lax.ppermute(part, axis, pairs)  16.1 us
    dot_general x1, matrix products, shards(): lax.dot_general(residual_grad, out_weight, (((1,), (1,)), ((), ())), pref...  13.9 us
    ppermute x1, waiting for transfers between devices, col_psum(): lax.ppermute(pair.astype(jnp.bfloat16), 'col', [(c, c ^ 2) for c in range...  13.4 us
    ppermute x4, waiting for transfers between devices, placed_sums(): lax.ppermute(piece, ('row', 'col'), pairs).astype(jnp.float32)  10 us
    dot_general x1, matrix products, shards(): jnp.dot(mixed, out_weight, preferred_element_type=jnp.float32)  8.81 us
  transfers between devices with their start and end apart: 54, of which 40 were waited for; matrix products, arithmetic and copies ran while one was open for 6% of the time, Pallas kernels for 0%

profile of v18, /device:TPU:2, one launch (start us, length us, event | category | flops | bytes accessed | tf_op | source)
XLA Modules:
  0.0 223.8 jit_solution(14923429756974680105)
XLA Ops:
  0.7 1.6 copy.23
  3.4 5.8 %all-to-all-start = ((bf16[128,8,256]{2,0,1:T(8,128)(2,1)}), bf16[128,8,256]{2,0,1:T(8,128)(2,1)S(1)}, u32[]{:S(2)}, u32[]{:S(2)}) async-start(bf16[128,8,256]{2,0,1:T(8,128)(2,1)} %copy.25), calls=%async_computation | async-start | bytes 1048576 | tf_op jit(solution)/shard_map/all_to_all | solution.py:24
  16.9 6.9 %all-to-all-done = bf16[128,8,256]{2,0,1:T(8,128)(2,1)S(1)} async-done(((bf16[128,8,256]{2,0,1:T(8,128)(2,1)}), bf16[128,8,256]{2,0,1:T(8,128)(2,1)S(1)}, u32[]{:S(2)}, u32[]{:S(2)}) %all-to-all-start) | async-done | bytes 524320 | tf_op jit(solution)/shard_map/all_to_all | solution.py:24
  23.8 1.9 collective-permute-done
  26.6 1.5 convolution_convert_fusion.1
  28.2 1.5 collective-permute-start.15
  30.4 1.7 convolution_convert_fusion.2
  32.1 2.0 collective-permute-start.1
  34.7 1.1 fusion.17
  35.8 1.2 fusion.20
  37.1 1.5 collective-permute-start.16
  38.7 1.5 collective-permute-done.8
  40.3 1.7 collective-permute-start.2
  43.0 1.4 collective-permute-done.23
  44.5 1.5 collective-permute-start.17
  47.6 1.4 collective-permute-start.3
  49.6 1.7 collective-permute-done.24
  51.4 1.3 collective-permute-start.18
  54.1 2.0 collective-permute-start.4
  56.7 2.3 %collective-permute-done.25 = bf16[128,512]{1,0:T(8,128)(2,1)S(1)} collective-permute-done((bf16[128,512]{1,0:T(8,128)(2,1)S(1)}, bf16[128,512]{1,0:T(8,128)(2,1)S(1)}, u32[]{:S(2)}, u32[]{:S(2)}) %collective-permute-start.25) | collective-permute-done | bytes 131104 | tf_op jit(solution)/shard_map/ppermute | solution.py:136
  59.1 1.5 collective-permute-start.19
  60.7 1.9 collective-permute-done.11
  62.6 1.5 collective-permute-start.5
  64.7 2.8 %collective-permute-done.26 = bf16[128,512]{1,0:T(8,128)(2,1)S(1)} collective-permute-done((bf16[128,512]{1,0:T(8,128)(2,1)S(1)}, bf16[128,512]{1,0:T(8,128)(2,1)S(1)}, u32[]{:S(2)}, u32[]{:S(2)}) %collective-permute-start.26) | collective-permute-done | bytes 131104 | tf_op jit(solution)/shard_map/ppermute | solution.py:136
  67.6 1.7 collective-permute-start.20
  69.4 1.9 collective-permute-done.12
  71.5 1.5 collective-permute-start.6
  74.1 2.7 %collective-permute-done.27 = bf16[128,512]{1,0:T(8,128)(2,1)S(1)} collective-permute-done((bf16[128,512]{1,0:T(8,128)(2,1)S(1)}, bf16[128,512]{1,0:T(8,128)(2,1)S(1)}, u32[]{:S(2)}, u32[]{:S(2)}) %collective-permute-start.27) | collective-permute-done | bytes 131104 | tf_op jit(solution)/shard_map/ppermute | solution.py:136
  76.9 1.5 collective-permute-start.21
  78.7 1.6 collective-permute-done.13
  80.4 1.5 collective-permute-start.7
  83.5 2.0 collective-permute-done.7
  85.4 1.4 collective-permute-done.14
  86.9 2.7 %collective-permute-start.29 = (bf16[3,2048]{1,0:T(4,128)(2,1)S(1)}, bf16[3,2048]{1,0:T(4,128)(2,1)S(1)}, u32[]{:S(2)}, u32[]{:S(2)}) collective-permute-start(bf16[3,2048]{1,0:T(4,128)(2,1)S(1)} %pad_maximum_fusion.1), channel_id=1, source_target_pairs={{0,4},{4,8},{8,12},{12,16},{16,20},{20,24},{24,28},{1,5},{5,9},{9,... | collective-permute-start | bytes 36872 | tf_op jit(solution)/shard_map/ppermute | solution.py:13
  89.7 1.2 collective-permute-done.29
  92.1 8.8 %convolution_convert_fusion = bf16[128,4096]{1,0:T(8,128)(2,1)S(1)} fusion(bf16[2048,4096]{1,0:T(8,128)(2,1)} %param.27, bf16[128,2048]{1,0:T(8,128)(2,1)S(1)} %copy-done.6, f32[128,2048]{1,0:T(8,128)S(1)} %fusion.9), kind=kOutput, calls=%fused_computation.6 | convolution fusion | flops 2150891520 | bytes 19398656 | tf_op jit(solution)/shard_map/dot_general | solution.py:210
  101.1 1.9 collective-permute-done.30
  103.8 13.4 %collective-permute-done.31 = bf16[128,2048]{1,0:T(8,128)(2,1)S(1)} collective-permute-done((bf16[128,2048]{1,0:T(8,128)(2,1)S(1)}, bf16[128,2048]{1,0:T(8,128)(2,1)S(1)}, u32[]{:S(2)}, u32[]{:S(2)}) %collective-permute-start.31) | collective-permute-done | bytes 524320 | tf_op jit(solution)/shard_map/ppermute | solution.py:152
  117.8 2.5 %collective-permute-done.32 = f32[128,2048]{1,0:T(8,128)S(1)} collective-permute-done((f32[128,2048]{1,0:T(8,128)S(1)}, f32[128,2048]{1,0:T(8,128)S(1)}, u32[]{:S(2)}, u32[]{:S(2)}) %collective-permute-start.32) | collective-permute-done | bytes 1048608 | tf_op jit(solution)/shard_map/ppermute | solution.py:155
  120.3 1.5 maximum_select_fusion
  121.8 13.9 %multiply_multiply_fusion.2 = (f32[128,2048]{1,0:T(8,128)S(1)}, f32[128,2048]{1,0:T(8,128)S(1)}, bf16[128,2048]{1,0:T(8,128)(2,1)}) fusion(f32[128]{0:T(128)S(1)} %get-tuple-element.119, f32[2048]{0:T(1024)S(1)} %bitcast.281, f32[128,2048]{1,0:T(8,128)} %copy-done.3, bf16[128,2048]{1,0:T(8,128)(2,1)S(1)} %copy-done.6, bf16[2048,4096]{1,0:T(8,128)(2,1)} %param.27, ...), kind=kOutput, calls=%fused_computation.46 | convolution fusion | flops 2155872256 | bytes 24126464 | tf_op jit(solution)/shard_map/dot_general | solution.py:223
  136.1 1.3 collective-permute-start.33
  137.7 4.5 %collective-permute-done.33 = f32[3,2048]{1,0:T(4,128)S(1)} collective-permute-done((f32[3,2048]{1,0:T(4,128)S(1)}, f32[3,2048]{1,0:T(4,128)S(1)}, u32[]{:S(2)}, u32[]{:S(2)}) %collective-permute-start.33) | collective-permute-done | bytes 24608 | tf_op jit(solution)/shard_map/ppermute | solution.py:13
  142.7 3.2 %collective-permute-start.41 = (bf16[128,1024]{1,0:T(8,128)(2,1)S(1)}, bf16[128,1024]{1,0:T(8,128)(2,1)S(1)}, u32[]{:S(2)}, u32[]{:S(2)}) collective-permute-start(bf16[128,1024]{1,0:T(8,128)(2,1)S(1)} %get-tuple-element.103), channel_id=1, source_target_pairs={{8,0},{16,8},{24,16},{28,24},{20,28},{12,20},{4,12},{0,4},{9,1},{1... | collective-permute-start | bytes 786440 | tf_op jit(solution)/shard_map/ppermute | solution.py:103
  146.5 5.4 %collective-permute-done.41 = bf16[128,1024]{1,0:T(8,128)(2,1)S(1)} collective-permute-done((bf16[128,1024]{1,0:T(8,128)(2,1)S(1)}, bf16[128,1024]{1,0:T(8,128)(2,1)S(1)}, u32[]{:S(2)}, u32[]{:S(2)}) %collective-permute-start.41) | collective-permute-done | bytes 262176 | tf_op jit(solution)/shard_map/ppermute | solution.py:103
  151.9 1.5 collective-permute-start.42
  156.2 2.2 collective-permute-done.42
  158.4 1.5 collective-permute-start.43
  161.1 4.7 %collective-permute-done.43 = bf16[128,1024]{1,0:T(8,128)(2,1)S(1)} collective-permute-done((bf16[128,1024]{1,0:T(8,128)(2,1)S(1)}, bf16[128,1024]{1,0:T(8,128)(2,1)S(1)}, u32[]{:S(2)}, u32[]{:S(2)}) %collective-permute-start.43) | collective-permute-done | bytes 262176 | tf_op jit(solution)/shard_map/ppermute | solution.py:103
  165.9 1.5 collective-permute-start.44
  168.7 6.4 %collective-permute-done.44 = bf16[128,1024]{1,0:T(8,128)(2,1)S(1)} collective-permute-done((bf16[128,1024]{1,0:T(8,128)(2,1)S(1)}, bf16[128,1024]{1,0:T(8,128)(2,1)S(1)}, u32[]{:S(2)}, u32[]{:S(2)}) %collective-permute-start.44) | collective-permute-done | bytes 262176 | tf_op jit(solution)/shard_map/ppermute | solution.py:103
  176.3 1.1 collective-permute-start.38
  177.5 6.6 %collective-permute-done.45 = bf16[128,1024]{1,0:T(8,128)(2,1)S(1)} collective-permute-done((bf16[128,1024]{1,0:T(8,128)(2,1)S(1)}, bf16[128,1024]{1,0:T(8,128)(2,1)S(1)}, u32[]{:S(2)}, u32[]{:S(2)}) %collective-permute-start.45) | collective-permute-done | bytes 262176 | tf_op jit(solution)/shard_map/ppermute | solution.py:103
  186.2 5.8 %collective-permute-done.46 = bf16[128,1024]{1,0:T(8,128)(2,1)S(1)} collective-permute-done((bf16[128,1024]{1,0:T(8,128)(2,1)S(1)}, bf16[128,1024]{1,0:T(8,128)(2,1)S(1)}, u32[]{:S(2)}, u32[]{:S(2)}) %collective-permute-start.46) | collective-permute-done | bytes 262176 | tf_op jit(solution)/shard_map/ppermute | solution.py:103
  194.1 4.2 %collective-permute-done.47 = bf16[128,1024]{1,0:T(8,128)(2,1)S(1)} collective-permute-done((bf16[128,1024]{1,0:T(8,128)(2,1)S(1)}, bf16[128,1024]{1,0:T(8,128)(2,1)S(1)}, u32[]{:S(2)}, u32[]{:S(2)}) %collective-permute-start.47) | collective-permute-done | bytes 262176 | tf_op jit(solution)/shard_map/ppermute | solution.py:103
  198.5 1.3 fusion.15
  199.9 1.3 add_convert_fusion
  202.2 1.8 collective-permute-done.48
  205.0 4.6 %collective-permute-start.49 = (bf16[128,512]{1,0:T(8,128)(2,1)S(1)}, bf16[128,512]{1,0:T(8,128)(2,1)S(1)}, u32[]{:S(2)}, u32[]{:S(2)}) collective-permute-start(bf16[128,512]{1,0:T(8,128)(2,1)S(1)} %get-tuple-element.107), channel_id=1, source_target_pairs={{0,0},{1,8},{2,16},{3,24},{4,4},{5,12},{6,20},{7,28},{8,1},{9,9},{... | collective-permute-start | bytes 393224 | tf_op jit(solution)/shard_map/ppermute | solution.py:73
  209.6 1.5 collective-permute-start.51
  211.1 1.8 dynamic-slice_convert_fusion
  212.9 4.3 %collective-permute-done.50 = bf16[128,512]{1,0:T(8,128)(2,1)S(1)} collective-permute-done((bf16[128,512]{1,0:T(8,128)(2,1)S(1)}, bf16[128,512]{1,0:T(8,128)(2,1)S(1)}, u32[]{:S(2)}, u32[]{:S(2)}) %collective-permute-start.50) | collective-permute-done | bytes 131104 | tf_op jit(solution)/shard_map/ppermute | solution.py:73
  217.2 3.3 %collective-permute-done.49 = bf16[128,512]{1,0:T(8,128)(2,1)S(1)} collective-permute-done((bf16[128,512]{1,0:T(8,128)(2,1)S(1)}, bf16[128,512]{1,0:T(8,128)(2,1)S(1)}, u32[]{:S(2)}, u32[]{:S(2)}) %collective-permute-start.49) | collective-permute-done | bytes 131104 | tf_op jit(solution)/shard_map/ppermute | solution.py:73
  220.5 2.5 %collective-permute-done.51 = bf16[128,512]{1,0:T(8,128)(2,1)S(1)} collective-permute-done((bf16[128,512]{1,0:T(8,128)(2,1)S(1)}, bf16[128,512]{1,0:T(8,128)(2,1)S(1)}, u32[]{:S(2)}, u32[]{:S(2)}) %collective-permute-start.51) | collective-permute-done | bytes 131104 | tf_op jit(solution)/shard_map/ppermute | solution.py:73
  (162 shorter events, 33.9 us)
Async XLA Ops:
  2.3 7.0 %copy-start.9 = (s32[8]{0:T(128)S(1)}, s32[8]{0:T(128)}, u32[]{:S(2)}) copy-start(s32[8]{0:T(128)} %constant.203.clone) | copy-start | bytes 100
  2.3 8.9 %copy-start = (s32[8]{0:T(128)S(1)}, s32[8]{0:T(128)}, u32[]{:S(2)}) copy-start(s32[8]{0:T(128)} %constant.204.clone) | copy-start | bytes 100
  2.3 21.4 %copy-start.4 = (f32[4,2048]{1,0:T(4,128)S(1)}, f32[4,2048]{1,0:T(4,128)}, u32[]{:S(2)}) copy-start(f32[4,2048]{1,0:T(4,128)} %param.26) | copy-start | bytes 98308
  3.4 20.3 %all-to-all-start = ((bf16[128,8,256]{2,0,1:T(8,128)(2,1)}), bf16[128,8,256]{2,0,1:T(8,128)(2,1)S(1)}, u32[]{:S(2)}, u32[]{:S(2)}) async-start(bf16[128,8,256]{2,0,1:T(8,128)(2,1)} %copy.25), calls=%async_computation | async-start | bytes 1048576 | tf_op jit(solution)/shard_map/all_to_all | solution.py:24
  23.8 1.9 collective-permute-start
  28.2 8.8 %collective-permute-start.15 = (bf16[128,512]{1,0:T(8,128)(2,1)S(1)}, bf16[128,512]{1,0:T(8,128)(2,1)S(1)}, u32[]{:S(2)}, u32[]{:S(2)}) collective-permute-start(bf16[128,512]{1,0:T(8,128)(2,1)S(1)} %get-tuple-element.112), channel_id=1, source_target_pairs={{8,0},{16,8},{24,16},{28,24},{20,28},{12,20},{4,12},{0,4},{9,1},{1... | collective-permute-start | bytes 393224 | tf_op jit(solution)/shard_map/ppermute | solution.py:136
  29.7 7.3 %collective-permute-start.22 = (bf16[128,512]{1,0:T(8,128)(2,1)S(1)}, bf16[128,512]{1,0:T(8,128)(2,1)S(1)}, u32[]{:S(2)}, u32[]{:S(2)}) collective-permute-start(bf16[128,512]{1,0:T(8,128)(2,1)S(1)} %get-tuple-element.113), channel_id=1, source_target_pairs={{8,0},{16,8},{24,16},{28,24},{20,28},{12,20},{4,12},{0,4},{9,1},{1... | collective-permute-start | bytes 393224 | tf_op jit(solution)/shard_map/ppermute | solution.py:136
  30.4 4.3 %copy-start.1 = (bf16[512,2048]{1,0:T(8,128)(2,1)S(1)}, bf16[512,2048]{1,0:T(8,128)(2,1)}, u32[]{:S(2)}) copy-start(bf16[512,2048]{1,0:T(8,128)(2,1)} %param.24) | copy-start | bytes 6291460
  32.1 6.6 %collective-permute-start.1 = (bf16[128,512]{1,0:T(8,128)(2,1)S(1)}, bf16[128,512]{1,0:T(8,128)(2,1)S(1)}, u32[]{:S(2)}, u32[]{:S(2)}) collective-permute-start(bf16[128,512]{1,0:T(8,128)(2,1)S(1)} %get-tuple-element.110), channel_id=1, source_target_pairs={{0,8},{8,16},{16,24},{24,28},{28,20},{20,12},{12,4},{4,0},{1,9},{9... | collective-permute-start | bytes 393224 | tf_op jit(solution)/shard_map/ppermute | solution.py:136
  34.1 6.1 %collective-permute-start.8 = (bf16[128,512]{1,0:T(8,128)(2,1)S(1)}, bf16[128,512]{1,0:T(8,128)(2,1)S(1)}, u32[]{:S(2)}, u32[]{:S(2)}) collective-permute-start(bf16[128,512]{1,0:T(8,128)(2,1)S(1)} %get-tuple-element.111), channel_id=1, source_target_pairs={{0,8},{8,16},{16,24},{24,28},{28,20},{20,12},{12,4},{4,0},{1,9},{9... | collective-permute-start | bytes 393224 | tf_op jit(solution)/shard_map/ppermute | solution.py:136
  37.1 5.9 %collective-permute-start.16 = (bf16[128,512]{1,0:T(8,128)(2,1)S(1)}, bf16[128,512]{1,0:T(8,128)(2,1)S(1)}, u32[]{:S(2)}, u32[]{:S(2)}) collective-permute-start(bf16[128,512]{1,0:T(8,128)(2,1)S(1)} %get-tuple-element.93), channel_id=1, source_target_pairs={{8,0},{16,8},{24,16},{28,24},{20,28},{12,20},{4,12},{0,4},{9,1},{1... | collective-permute-start | bytes 393224 | tf_op jit(solution)/shard_map/ppermute | solution.py:136
  38.6 5.8 %collective-permute-start.23 = (bf16[128,512]{1,0:T(8,128)(2,1)S(1)}, bf16[128,512]{1,0:T(8,128)(2,1)S(1)}, u32[]{:S(2)}, u32[]{:S(2)}) collective-permute-start(bf16[128,512]{1,0:T(8,128)(2,1)S(1)} %get-tuple-element.94), channel_id=1, source_target_pairs={{8,0},{16,8},{24,16},{28,24},{20,28},{12,20},{4,12},{0,4},{9,1},{1... | collective-permute-start | bytes 393224 | tf_op jit(solution)/shard_map/ppermute | solution.py:136
  40.3 6.1 %collective-permute-start.2 = (bf16[128,512]{1,0:T(8,128)(2,1)S(1)}, bf16[128,512]{1,0:T(8,128)(2,1)S(1)}, u32[]{:S(2)}, u32[]{:S(2)}) collective-permute-start(bf16[128,512]{1,0:T(8,128)(2,1)S(1)} %get-tuple-element.79), channel_id=1, source_target_pairs={{0,8},{8,16},{16,24},{24,28},{28,20},{20,12},{12,4},{4,0},{1,9},{9... | collective-permute-start | bytes 393224 | tf_op jit(solution)/shard_map/ppermute | solution.py:136
  42.0 5.5 %collective-permute-start.9 = (bf16[128,512]{1,0:T(8,128)(2,1)S(1)}, bf16[128,512]{1,0:T(8,128)(2,1)S(1)}, u32[]{:S(2)}, u32[]{:S(2)}) collective-permute-start(bf16[128,512]{1,0:T(8,128)(2,1)S(1)} %get-tuple-element.80), channel_id=1, source_target_pairs={{0,8},{8,16},{16,24},{24,28},{28,20},{20,12},{12,4},{4,0},{1,9},{9... | collective-permute-start | bytes 393224 | tf_op jit(solution)/shard_map/ppermute | solution.py:136
  44.5 5.2 %collective-permute-start.17 = (bf16[128,512]{1,0:T(8,128)(2,1)S(1)}, bf16[128,512]{1,0:T(8,128)(2,1)S(1)}, u32[]{:S(2)}, u32[]{:S(2)}) collective-permute-start(bf16[128,512]{1,0:T(8,128)(2,1)S(1)} %get-tuple-element.91), channel_id=1, source_target_pairs={{8,0},{16,8},{24,16},{28,24},{20,28},{12,20},{4,12},{0,4},{9,1},{1... | collective-permute-start | bytes 393224 | tf_op jit(solution)/shard_map/ppermute | solution.py:136
  46.0 5.3 %collective-permute-start.24 = (bf16[128,512]{1,0:T(8,128)(2,1)S(1)}, bf16[128,512]{1,0:T(8,128)(2,1)S(1)}, u32[]{:S(2)}, u32[]{:S(2)}) collective-permute-start(bf16[128,512]{1,0:T(8,128)(2,1)S(1)} %get-tuple-element.92), channel_id=1, source_target_pairs={{8,0},{16,8},{24,16},{28,24},{20,28},{12,20},{4,12},{0,4},{9,1},{1... | collective-permute-start | bytes 393224 | tf_op jit(solution)/shard_map/ppermute | solution.py:136
  47.6 5.6 %collective-permute-start.3 = (bf16[128,512]{1,0:T(8,128)(2,1)S(1)}, bf16[128,512]{1,0:T(8,128)(2,1)S(1)}, u32[]{:S(2)}, u32[]{:S(2)}) collective-permute-start(bf16[128,512]{1,0:T(8,128)(2,1)S(1)} %get-tuple-element.77), channel_id=1, source_target_pairs={{0,8},{8,16},{16,24},{24,28},{28,20},{20,12},{12,4},{4,0},{1,9},{9... | collective-permute-start | bytes 393224 | tf_op jit(solution)/shard_map/ppermute | solution.py:136
  49.0 5.0 %collective-permute-start.10 = (bf16[128,512]{1,0:T(8,128)(2,1)S(1)}, bf16[128,512]{1,0:T(8,128)(2,1)S(1)}, u32[]{:S(2)}, u32[]{:S(2)}) collective-permute-start(bf16[128,512]{1,0:T(8,128)(2,1)S(1)} %get-tuple-element.78), channel_id=1, source_target_pairs={{0,8},{8,16},{16,24},{24,28},{28,20},{20,12},{12,4},{4,0},{1,9},{9... | collective-permute-start | bytes 393224 | tf_op jit(solution)/shard_map/ppermute | solution.py:136
  51.4 5.3 %collective-permute-start.18 = (bf16[128,512]{1,0:T(8,128)(2,1)S(1)}, bf16[128,512]{1,0:T(8,128)(2,1)S(1)}, u32[]{:S(2)}, u32[]{:S(2)}) collective-permute-start(bf16[128,512]{1,0:T(8,128)(2,1)S(1)} %get-tuple-element.89), channel_id=1, source_target_pairs={{8,0},{16,8},{24,16},{28,24},{20,28},{12,20},{4,12},{0,4},{9,1},{1... | collective-permute-start | bytes 393224 | tf_op jit(solution)/shard_map/ppermute | solution.py:136
  52.7 6.3 %collective-permute-start.25 = (bf16[128,512]{1,0:T(8,128)(2,1)S(1)}, bf16[128,512]{1,0:T(8,128)(2,1)S(1)}, u32[]{:S(2)}, u32[]{:S(2)}) collective-permute-start(bf16[128,512]{1,0:T(8,128)(2,1)S(1)} %get-tuple-element.90), channel_id=1, source_target_pairs={{8,0},{16,8},{24,16},{28,24},{20,28},{12,20},{4,12},{0,4},{9,1},{1... | collective-permute-start | bytes 393224 | tf_op jit(solution)/shard_map/ppermute | solution.py:136
  54.1 6.5 %collective-permute-start.4 = (bf16[128,512]{1,0:T(8,128)(2,1)S(1)}, bf16[128,512]{1,0:T(8,128)(2,1)S(1)}, u32[]{:S(2)}, u32[]{:S(2)}) collective-permute-start(bf16[128,512]{1,0:T(8,128)(2,1)S(1)} %get-tuple-element.75), channel_id=1, source_target_pairs={{0,8},{8,16},{16,24},{24,28},{28,20},{20,12},{12,4},{4,0},{1,9},{9... | collective-permute-start | bytes 393224 | tf_op jit(solution)/shard_map/ppermute | solution.py:136
  56.2 6.4 %collective-permute-start.11 = (bf16[128,512]{1,0:T(8,128)(2,1)S(1)}, bf16[128,512]{1,0:T(8,128)(2,1)S(1)}, u32[]{:S(2)}, u32[]{:S(2)}) collective-permute-start(bf16[128,512]{1,0:T(8,128)(2,1)S(1)} %get-tuple-element.76), channel_id=1, source_target_pairs={{0,8},{8,16},{16,24},{24,28},{28,20},{20,12},{12,4},{4,0},{1,9},{9... | collective-permute-start | bytes 393224 | tf_op jit(solution)/shard_map/ppermute | solution.py:136
  59.1 5.7 %collective-permute-start.19 = (bf16[128,512]{1,0:T(8,128)(2,1)S(1)}, bf16[128,512]{1,0:T(8,128)(2,1)S(1)}, u32[]{:S(2)}, u32[]{:S(2)}) collective-permute-start(bf16[128,512]{1,0:T(8,128)(2,1)S(1)} %get-tuple-element.87), channel_id=1, source_target_pairs={{8,0},{16,8},{24,16},{28,24},{20,28},{12,20},{4,12},{0,4},{9,1},{1... | collective-permute-start | bytes 393224 | tf_op jit(solution)/shard_map/ppermute | solution.py:136
  60.6 6.9 %collective-permute-start.26 = (bf16[128,512]{1,0:T(8,128)(2,1)S(1)}, bf16[128,512]{1,0:T(8,128)(2,1)S(1)}, u32[]{:S(2)}, u32[]{:S(2)}) collective-permute-start(bf16[128,512]{1,0:T(8,128)(2,1)S(1)} %get-tuple-element.88), channel_id=1, source_target_pairs={{8,0},{16,8},{24,16},{28,24},{20,28},{12,20},{4,12},{0,4},{9,1},{1... | collective-permute-start | bytes 393224 | tf_op jit(solution)/shard_map/ppermute | solution.py:136
  62.6 6.8 %collective-permute-start.5 = (bf16[128,512]{1,0:T(8,128)(2,1)S(1)}, bf16[128,512]{1,0:T(8,128)(2,1)S(1)}, u32[]{:S(2)}, u32[]{:S(2)}) collective-permute-start(bf16[128,512]{1,0:T(8,128)(2,1)S(1)} %get-tuple-element.73), channel_id=1, source_target_pairs={{0,8},{8,16},{16,24},{24,28},{28,20},{20,12},{12,4},{4,0},{1,9},{9... | collective-permute-start | bytes 393224 | tf_op jit(solution)/shard_map/ppermute | solution.py:136
  64.1 7.3 %collective-permute-start.12 = (bf16[128,512]{1,0:T(8,128)(2,1)S(1)}, bf16[128,512]{1,0:T(8,128)(2,1)S(1)}, u32[]{:S(2)}, u32[]{:S(2)}) collective-permute-start(bf16[128,512]{1,0:T(8,128)(2,1)S(1)} %get-tuple-element.74), channel_id=1, source_target_pairs={{0,8},{8,16},{16,24},{24,28},{28,20},{20,12},{12,4},{4,0},{1,9},{9... | collective-permute-start | bytes 393224 | tf_op jit(solution)/shard_map/ppermute | solution.py:136
  67.6 6.4 %collective-permute-start.20 = (bf16[128,512]{1,0:T(8,128)(2,1)S(1)}, bf16[128,512]{1,0:T(8,128)(2,1)S(1)}, u32[]{:S(2)}, u32[]{:S(2)}) collective-permute-start(bf16[128,512]{1,0:T(8,128)(2,1)S(1)} %get-tuple-element.85), channel_id=1, source_target_pairs={{8,0},{16,8},{24,16},{28,24},{20,28},{12,20},{4,12},{0,4},{9,1},{1... | collective-permute-start | bytes 393224 | tf_op jit(solution)/shard_map/ppermute | solution.py:136
  69.4 7.4 %collective-permute-start.27 = (bf16[128,512]{1,0:T(8,128)(2,1)S(1)}, bf16[128,512]{1,0:T(8,128)(2,1)S(1)}, u32[]{:S(2)}, u32[]{:S(2)}) collective-permute-start(bf16[128,512]{1,0:T(8,128)(2,1)S(1)} %get-tuple-element.86), channel_id=1, source_target_pairs={{8,0},{16,8},{24,16},{28,24},{20,28},{12,20},{4,12},{0,4},{9,1},{1... | collective-permute-start | bytes 393224 | tf_op jit(solution)/shard_map/ppermute | solution.py:136
  71.5 7.2 %collective-permute-start.6 = (bf16[128,512]{1,0:T(8,128)(2,1)S(1)}, bf16[128,512]{1,0:T(8,128)(2,1)S(1)}, u32[]{:S(2)}, u32[]{:S(2)}) collective-permute-start(bf16[128,512]{1,0:T(8,128)(2,1)S(1)} %get-tuple-element.71), channel_id=1, source_target_pairs={{0,8},{8,16},{16,24},{24,28},{28,20},{20,12},{12,4},{4,0},{1,9},{9... | collective-permute-start | bytes 393224 | tf_op jit(solution)/shard_map/ppermute | solution.py:136
  72.9 7.4 %collective-permute-start.13 = (bf16[128,512]{1,0:T(8,128)(2,1)S(1)}, bf16[128,512]{1,0:T(8,128)(2,1)S(1)}, u32[]{:S(2)}, u32[]{:S(2)}) collective-permute-start(bf16[128,512]{1,0:T(8,128)(2,1)S(1)} %get-tuple-element.72), channel_id=1, source_target_pairs={{0,8},{8,16},{16,24},{24,28},{28,20},{20,12},{12,4},{4,0},{1,9},{9... | collective-permute-start | bytes 393224 | tf_op jit(solution)/shard_map/ppermute | solution.py:136
  76.9 12.8 %copy-start.5 = (s32[128]{0:T(128)S(1)}, s32[128]{0:T(128)}, u32[]{:S(2)}) copy-start(s32[128]{0:T(128)} %param.31) | copy-start | bytes 1540
  76.9 5.6 %collective-permute-start.21 = (bf16[128,512]{1,0:T(8,128)(2,1)S(1)}, bf16[128,512]{1,0:T(8,128)(2,1)S(1)}, u32[]{:S(2)}, u32[]{:S(2)}) collective-permute-start(bf16[128,512]{1,0:T(8,128)(2,1)S(1)} %get-tuple-element.83), channel_id=1, source_target_pairs={{8,0},{16,8},{24,16},{28,24},{20,28},{12,20},{4,12},{0,4},{9,1},{1... | collective-permute-start | bytes 393224 | tf_op jit(solution)/shard_map/ppermute | solution.py:136
  78.4 5.0 %collective-permute-start.28 = (bf16[128,512]{1,0:T(8,128)(2,1)S(1)}, bf16[128,512]{1,0:T(8,128)(2,1)S(1)}, u32[]{:S(2)}, u32[]{:S(2)}) collective-permute-start(bf16[128,512]{1,0:T(8,128)(2,1)S(1)} %get-tuple-element.84), channel_id=1, source_target_pairs={{8,0},{16,8},{24,16},{28,24},{20,28},{12,20},{4,12},{0,4},{9,1},{1... | collective-permute-start | bytes 393224 | tf_op jit(solution)/shard_map/ppermute | solution.py:136
  80.4 5.0 %collective-permute-start.7 = (bf16[128,512]{1,0:T(8,128)(2,1)S(1)}, bf16[128,512]{1,0:T(8,128)(2,1)S(1)}, u32[]{:S(2)}, u32[]{:S(2)}) collective-permute-start(bf16[128,512]{1,0:T(8,128)(2,1)S(1)} %get-tuple-element.69), channel_id=1, source_target_pairs={{0,8},{8,16},{16,24},{24,28},{28,20},{20,12},{12,4},{4,0},{1,9},{9... | collective-permute-start | bytes 393224 | tf_op jit(solution)/shard_map/ppermute | solution.py:136
  81.9 5.0 %collective-permute-start.14 = (bf16[128,512]{1,0:T(8,128)(2,1)S(1)}, bf16[128,512]{1,0:T(8,128)(2,1)S(1)}, u32[]{:S(2)}, u32[]{:S(2)}) collective-permute-start(bf16[128,512]{1,0:T(8,128)(2,1)S(1)} %get-tuple-element.70), channel_id=1, source_target_pairs={{0,8},{8,16},{16,24},{24,28},{28,20},{20,12},{12,4},{4,0},{1,9},{9... | collective-permute-start | bytes 393224 | tf_op jit(solution)/shard_map/ppermute | solution.py:136
  86.9 3.9 %collective-permute-start.29 = (bf16[3,2048]{1,0:T(4,128)(2,1)S(1)}, bf16[3,2048]{1,0:T(4,128)(2,1)S(1)}, u32[]{:S(2)}, u32[]{:S(2)}) collective-permute-start(bf16[3,2048]{1,0:T(4,128)(2,1)S(1)} %pad_maximum_fusion.1), channel_id=1, source_target_pairs={{0,4},{4,8},{8,12},{12,16},{16,20},{20,24},{24,28},{1,5},{5,9},{9,... | collective-permute-start | bytes 36872 | tf_op jit(solution)/shard_map/ppermute | solution.py:13
  91.0 1.0 copy-start.6
  92.1 8.8 %copy-start.3 = (f32[128,2048]{1,0:T(8,128)}, f32[128,2048]{1,0:T(8,128)S(1)}, u32[]{:S(2)}) copy-start(f32[128,2048]{1,0:T(8,128)S(1)} %fusion.9) | copy-start | bytes 3145732
  101.0 2.0 collective-permute-start.30
  103.2 14.5 %copy-start.7 = (f32[32]{0:T(128)S(1)}, f32[32]{0:T(128)}, u32[]{:S(2)}) copy-start(f32[32]{0:T(128)} %param.30) | copy-start | bytes 388
  103.2 14.4 %copy-start.8 = (s32[128]{0:T(128)S(1)}, s32[128]{0:T(128)}, u32[]{:S(2)}) copy-start(s32[128]{0:T(128)} %param.29) | copy-start | bytes 1540
  103.2 14.0 %collective-permute-start.31 = (bf16[128,2048]{1,0:T(8,128)(2,1)S(1)}, bf16[128,2048]{1,0:T(8,128)(2,1)S(1)}, u32[]{:S(2)}, u32[]{:S(2)}) collective-permute-start(bf16[128,2048]{1,0:T(8,128)(2,1)S(1)} %fusion.24), channel_id=1, source_target_pairs={{0,2},{1,3},{2,0},{3,1},{4,6},{5,7},{6,4},{7,5},{8,10},{9,11},{10,... | collective-permute-start | bytes 1572872 | tf_op jit(solution)/shard_map/ppermute | solution.py:152
  117.6 2.7 %collective-permute-start.32 = (f32[128,2048]{1,0:T(8,128)S(1)}, f32[128,2048]{1,0:T(8,128)S(1)}, u32[]{:S(2)}, u32[]{:S(2)}) collective-permute-start(f32[128,2048]{1,0:T(8,128)S(1)} %convert_add_fusion), channel_id=1, source_target_pairs={{0,1},{1,0},{2,3},{3,2},{4,5},{5,4},{6,7},{7,6},{8,9},{9,8},{10,11... | collective-permute-start | bytes 3145736 | tf_op jit(solution)/shard_map/ppermute | solution.py:155
  136.1 6.1 %collective-permute-start.33 = (f32[3,2048]{1,0:T(4,128)S(1)}, f32[3,2048]{1,0:T(4,128)S(1)}, u32[]{:S(2)}, u32[]{:S(2)}) collective-permute-start(f32[3,2048]{1,0:T(4,128)S(1)} %slice_add_fusion), channel_id=1, source_target_pairs={{4,0},{8,4},{12,8},{16,12},{20,16},{24,20},{28,24},{5,1},{9,5},{13... | collective-permute-start | bytes 73736 | tf_op jit(solution)/shard_map/ppermute | solution.py:13
  142.7 9.2 %collective-permute-start.41 = (bf16[128,1024]{1,0:T(8,128)(2,1)S(1)}, bf16[128,1024]{1,0:T(8,128)(2,1)S(1)}, u32[]{:S(2)}, u32[]{:S(2)}) collective-permute-start(bf16[128,1024]{1,0:T(8,128)(2,1)S(1)} %get-tuple-element.103), channel_id=1, source_target_pairs={{8,0},{16,8},{24,16},{28,24},{20,28},{12,20},{4,12},{0,4},{9,1},{1... | collective-permute-start | bytes 786440 | tf_op jit(solution)/shard_map/ppermute | solution.py:103
  145.9 8.1 %collective-permute-start.34 = (bf16[128,1024]{1,0:T(8,128)(2,1)S(1)}, bf16[128,1024]{1,0:T(8,128)(2,1)S(1)}, u32[]{:S(2)}, u32[]{:S(2)}) collective-permute-start(bf16[128,1024]{1,0:T(8,128)(2,1)S(1)} %get-tuple-element.102), channel_id=1, source_target_pairs={{0,8},{8,16},{16,24},{24,28},{28,20},{20,12},{12,4},{4,0},{1,9},{9... | collective-permute-start | bytes 786440 | tf_op jit(solution)/shard_map/ppermute | solution.py:103
  151.9 6.6 %collective-permute-start.42 = (bf16[128,1024]{1,0:T(8,128)(2,1)S(1)}, bf16[128,1024]{1,0:T(8,128)(2,1)S(1)}, u32[]{:S(2)}, u32[]{:S(2)}) collective-permute-start(bf16[128,1024]{1,0:T(8,128)(2,1)S(1)} %collective-permute-done.41), channel_id=1, source_target_pairs={{8,0},{16,8},{24,16},{28,24},{20,28},{12,20},{4,12},{0,4},{9,1},{1... | collective-permute-start | bytes 786440 | tf_op jit(solution)/shard_map/ppermute | solution.py:103
  154.0 6.5 %collective-permute-start.35 = (bf16[128,1024]{1,0:T(8,128)(2,1)S(1)}, bf16[128,1024]{1,0:T(8,128)(2,1)S(1)}, u32[]{:S(2)}, u32[]{:S(2)}) collective-permute-start(bf16[128,1024]{1,0:T(8,128)(2,1)S(1)} %collective-permute-done.34), channel_id=1, source_target_pairs={{0,8},{8,16},{16,24},{24,28},{28,20},{20,12},{12,4},{4,0},{1,9},{9... | collective-permute-start | bytes 786440 | tf_op jit(solution)/shard_map/ppermute | solution.py:103
  158.4 7.4 %collective-permute-start.43 = (bf16[128,1024]{1,0:T(8,128)(2,1)S(1)}, bf16[128,1024]{1,0:T(8,128)(2,1)S(1)}, u32[]{:S(2)}, u32[]{:S(2)}) collective-permute-start(bf16[128,1024]{1,0:T(8,128)(2,1)S(1)} %collective-permute-done.42), channel_id=1, source_target_pairs={{8,0},{16,8},{24,16},{28,24},{20,28},{12,20},{4,12},{0,4},{9,1},{1... | collective-permute-start | bytes 786440 | tf_op jit(solution)/shard_map/ppermute | solution.py:103
  160.6 7.3 %collective-permute-start.36 = (bf16[128,1024]{1,0:T(8,128)(2,1)S(1)}, bf16[128,1024]{1,0:T(8,128)(2,1)S(1)}, u32[]{:S(2)}, u32[]{:S(2)}) collective-permute-start(bf16[128,1024]{1,0:T(8,128)(2,1)S(1)} %collective-permute-done.35), channel_id=1, source_target_pairs={{0,8},{8,16},{16,24},{24,28},{28,20},{20,12},{12,4},{4,0},{1,9},{9... | collective-permute-start | bytes 786440 | tf_op jit(solution)/shard_map/ppermute | solution.py:103
  165.9 9.2 %collective-permute-start.44 = (bf16[128,1024]{1,0:T(8,128)(2,1)S(1)}, bf16[128,1024]{1,0:T(8,128)(2,1)S(1)}, u32[]{:S(2)}, u32[]{:S(2)}) collective-permute-start(bf16[128,1024]{1,0:T(8,128)(2,1)S(1)} %collective-permute-done.43), channel_id=1, source_target_pairs={{8,0},{16,8},{24,16},{28,24},{20,28},{12,20},{4,12},{0,4},{9,1},{1... | collective-permute-start | bytes 786440 | tf_op jit(solution)/shard_map/ppermute | solution.py:103
  167.8 8.5 %collective-permute-start.37 = (bf16[128,1024]{1,0:T(8,128)(2,1)S(1)}, bf16[128,1024]{1,0:T(8,128)(2,1)S(1)}, u32[]{:S(2)}, u32[]{:S(2)}) collective-permute-start(bf16[128,1024]{1,0:T(8,128)(2,1)S(1)} %collective-permute-done.36), channel_id=1, source_target_pairs={{0,8},{8,16},{16,24},{24,28},{28,20},{20,12},{12,4},{4,0},{1,9},{9... | collective-permute-start | bytes 786440 | tf_op jit(solution)/shard_map/ppermute | solution.py:103
  175.1 9.0 %collective-permute-start.45 = (bf16[128,1024]{1,0:T(8,128)(2,1)S(1)}, bf16[128,1024]{1,0:T(8,128)(2,1)S(1)}, u32[]{:S(2)}, u32[]{:S(2)}) collective-permute-start(bf16[128,1024]{1,0:T(8,128)(2,1)S(1)} %collective-permute-done.44), channel_id=1, source_target_pairs={{8,0},{16,8},{24,16},{28,24},{20,28},{12,20},{4,12},{0,4},{9,1},{1... | collective-permute-start | bytes 786440 | tf_op jit(solution)/shard_map/ppermute | solution.py:103
  176.3 8.8 %collective-permute-start.38 = (bf16[128,1024]{1,0:T(8,128)(2,1)S(1)}, bf16[128,1024]{1,0:T(8,128)(2,1)S(1)}, u32[]{:S(2)}, u32[]{:S(2)}) collective-permute-start(bf16[128,1024]{1,0:T(8,128)(2,1)S(1)} %collective-permute-done.37), channel_id=1, source_target_pairs={{0,8},{8,16},{16,24},{24,28},{28,20},{20,12},{12,4},{4,0},{1,9},{9... | collective-permute-start | bytes 786440 | tf_op jit(solution)/shard_map/ppermute | solution.py:103
  184.0 7.9 %collective-permute-start.46 = (bf16[128,1024]{1,0:T(8,128)(2,1)S(1)}, bf16[128,1024]{1,0:T(8,128)(2,1)S(1)}, u32[]{:S(2)}, u32[]{:S(2)}) collective-permute-start(bf16[128,1024]{1,0:T(8,128)(2,1)S(1)} %collective-permute-done.45), channel_id=1, source_target_pairs={{8,0},{16,8},{24,16},{28,24},{20,28},{12,20},{4,12},{0,4},{9,1},{1... | collective-permute-start | bytes 786440 | tf_op jit(solution)/shard_map/ppermute | solution.py:103
  185.1 8.0 %collective-permute-start.39 = (bf16[128,1024]{1,0:T(8,128)(2,1)S(1)}, bf16[128,1024]{1,0:T(8,128)(2,1)S(1)}, u32[]{:S(2)}, u32[]{:S(2)}) collective-permute-start(bf16[128,1024]{1,0:T(8,128)(2,1)S(1)} %collective-permute-done.38), channel_id=1, source_target_pairs={{0,8},{8,16},{16,24},{24,28},{28,20},{20,12},{12,4},{4,0},{1,9},{9... | collective-permute-start | bytes 786440 | tf_op jit(solution)/shard_map/ppermute | solution.py:103
  191.9 6.4 %collective-permute-start.47 = (bf16[128,1024]{1,0:T(8,128)(2,1)S(1)}, bf16[128,1024]{1,0:T(8,128)(2,1)S(1)}, u32[]{:S(2)}, u32[]{:S(2)}) collective-permute-start(bf16[128,1024]{1,0:T(8,128)(2,1)S(1)} %collective-permute-done.46), channel_id=1, source_target_pairs={{8,0},{16,8},{24,16},{28,24},{20,28},{12,20},{4,12},{0,4},{9,1},{1... | collective-permute-start | bytes 786440 | tf_op jit(solution)/shard_map/ppermute | solution.py:103
  192.9 5.6 %copy-start.2 = (bf16[512,2048]{1,0:T(8,128)(2,1)S(1)}, bf16[512,2048]{1,0:T(8,128)(2,1)}, u32[]{:S(2)}) copy-start(bf16[512,2048]{1,0:T(8,128)(2,1)} %param.24) | copy-start | bytes 6291460
  193.0 6.8 %collective-permute-start.40 = (bf16[128,1024]{1,0:T(8,128)(2,1)S(1)}, bf16[128,1024]{1,0:T(8,128)(2,1)S(1)}, u32[]{:S(2)}, u32[]{:S(2)}) collective-permute-start(bf16[128,1024]{1,0:T(8,128)(2,1)S(1)} %collective-permute-done.39), channel_id=1, source_target_pairs={{0,8},{8,16},{16,24},{24,28},{28,20},{20,12},{12,4},{4,0},{1,9},{9... | collective-permute-start | bytes 786440 | tf_op jit(solution)/shard_map/ppermute | solution.py:103
  202.1 2.0 collective-permute-start.48
  204.3 12.9 %collective-permute-start.50 = (bf16[128,512]{1,0:T(8,128)(2,1)S(1)}, bf16[128,512]{1,0:T(8,128)(2,1)S(1)}, u32[]{:S(2)}, u32[]{:S(2)}) collective-permute-start(bf16[128,512]{1,0:T(8,128)(2,1)S(1)} %get-tuple-element.109), channel_id=1, source_target_pairs={{0,16},{1,24},{2,0},{3,8},{4,20},{5,28},{6,4},{7,12},{8,17},{9,25}... | collective-permute-start | bytes 393224 | tf_op jit(solution)/shard_map/ppermute | solution.py:73
  205.0 15.5 %collective-permute-start.49 = (bf16[128,512]{1,0:T(8,128)(2,1)S(1)}, bf16[128,512]{1,0:T(8,128)(2,1)S(1)}, u32[]{:S(2)}, u32[]{:S(2)}) collective-permute-start(bf16[128,512]{1,0:T(8,128)(2,1)S(1)} %get-tuple-element.107), channel_id=1, source_target_pairs={{0,0},{1,8},{2,16},{3,24},{4,4},{5,12},{6,20},{7,28},{8,1},{9,9},{... | collective-permute-start | bytes 393224 | tf_op jit(solution)/shard_map/ppermute | solution.py:73
  209.6 10.9 %collective-permute-start.52 = (bf16[128,512]{1,0:T(8,128)(2,1)S(1)}, bf16[128,512]{1,0:T(8,128)(2,1)S(1)}, u32[]{:S(2)}, u32[]{:S(2)}) collective-permute-start(bf16[128,512]{1,0:T(8,128)(2,1)S(1)} %get-tuple-element.108), channel_id=1, source_target_pairs={{0,20},{1,28},{2,4},{3,12},{4,16},{5,24},{6,0},{7,8},{8,21},{9,29}... | collective-permute-start | bytes 393224 | tf_op jit(solution)/shard_map/ppermute | solution.py:73
  209.6 13.3 %collective-permute-start.51 = (bf16[128,512]{1,0:T(8,128)(2,1)S(1)}, bf16[128,512]{1,0:T(8,128)(2,1)S(1)}, u32[]{:S(2)}, u32[]{:S(2)}) collective-permute-start(bf16[128,512]{1,0:T(8,128)(2,1)S(1)} %get-tuple-element.106), channel_id=1, source_target_pairs={{0,4},{1,12},{2,20},{3,28},{4,0},{5,8},{6,16},{7,24},{8,5},{9,13},... | collective-permute-start | bytes 393224 | tf_op jit(solution)/shard_map/ppermute | solution.py:73

commit v19 on v14

--- a/solution.py
+++ b/solution.py
@@ -188,7 +188,7 @@
         and lax.axis_size("row") % lax.axis_size("col") == 0
     )
     if moves_tokens:
-        inner_x = ring_reduce_scatter(fetched_columns(tokens), in_weight, "row")
+        inner_x = ring_reduce_scatter(fetched_columns(tokens), in_weight, "row", chains=4)
     else:
         full_in = lax.all_gather(in_weight, "row", axis=0, tiled=True)
         inner_x = jnp.dot(tokens, full_in, preferred_element_type=jnp.float32).astype(jnp.bfloat16)

time: 224 us -> 233 us (1.040)
  starting transfers between devices: 75.1 us -> 110 us
  waiting for transfers between devices: 80.8 us -> 57.3 us
    ppermute x28 -> x56, starting transfers between devices: 26.9 us -> 58.2 us  [ring_reduce_scatter(): total = lax.ppermute(total, axis, pairs)]
    ppermute x28 -> x56, waiting for transfers between devices: 24.9 us -> 3.85 us  [ring_reduce_scatter(): total = lax.ppermute(total, axis, pairs)]
    ppermute x28, waiting for transfers between devices: 17.3 us -> 13.1 us  [ring_gather(): part = lax.ppermute(part, axis, pairs)]
    ppermute x28, starting transfers between devices: 30.7 us -> 33.5 us  [ring_gather(): part = lax.ppermute(part, axis, pairs)]
    unnamed x66 -> x58, local copies, waits for them, and re-layouts: 4.58 us -> 5.03 us
  transfers between devices with their start and end apart: 68 -> 96, of which waited for: 48 -> 35; matrix products, arithmetic and copies ran while one was open for 8% -> 6% of each run, Pallas kernels for 0% -> 0%
where the time goes in v19:
time: 233 us
  starting transfers between devices  110 us (47%)
  waiting for transfers between devices  57.3 us (25%)
  matrix products  29.5 us (13%)
  local copies, waits for them, and re-layouts  16.8 us (7%)
  other arithmetic  12.3 us (5%)
  between operations  6.81 us (3%)
    ppermute x56, starting transfers between devices, ring_reduce_scatter(): total = lax.ppermute(total, axis, pairs)  58.2 us
    ppermute x28, starting transfers between devices, ring_gather(): part = lax.ppermute(part, axis, pairs)  33.5 us
    dot_general x1, matrix products, shards(): lax.dot_general(residual_grad, out_weight, (((1,), (1,)), ((), ())), pref...  14.7 us
    ppermute x1, waiting for transfers between devices, col_psum(): lax.ppermute(pair.astype(jnp.bfloat16), 'col', [(c, c ^ 2) for c in range...  13.4 us
    ppermute x28, waiting for transfers between devices, ring_gather(): part = lax.ppermute(part, axis, pairs)  13.1 us
    ppermute x4, waiting for transfers between devices, placed_sums(): lax.ppermute(piece, ('row', 'col'), pairs).astype(jnp.float32)  10 us
    dot_general x1, matrix products, shards(): jnp.dot(mixed, out_weight, preferred_element_type=jnp.float32)  8.8 us
    ppermute x4, starting transfers between devices, placed_sums(): lax.ppermute(piece, ('row', 'col'), pairs).astype(jnp.float32)  7.01 us
  transfers between devices with their start and end apart: 96, of which 35 were waited for; matrix products, arithmetic and copies ran while one was open for 6% of the time, Pallas kernels for 0%

profile of v19, /device:TPU:2, one launch (start us, length us, event | category | flops | bytes accessed | tf_op | source)
XLA Modules:
  0.0 232.6 jit_solution(13488426169212513951)
XLA Ops:
  0.7 1.6 copy.23
  3.4 5.8 %all-to-all-start = ((bf16[128,8,256]{2,0,1:T(8,128)(2,1)}), bf16[128,8,256]{2,0,1:T(8,128)(2,1)S(1)}, u32[]{:S(2)}, u32[]{:S(2)}) async-start(bf16[128,8,256]{2,0,1:T(8,128)(2,1)} %copy.25), calls=%async_computation | async-start | bytes 1048576 | tf_op jit(solution)/shard_map/all_to_all | solution.py:24
  17.0 6.7 %all-to-all-done = bf16[128,8,256]{2,0,1:T(8,128)(2,1)S(1)} async-done(((bf16[128,8,256]{2,0,1:T(8,128)(2,1)}), bf16[128,8,256]{2,0,1:T(8,128)(2,1)S(1)}, u32[]{:S(2)}, u32[]{:S(2)}) %all-to-all-start) | async-done | bytes 524320 | tf_op jit(solution)/shard_map/all_to_all | solution.py:24
  23.8 1.9 collective-permute-done
  25.6 1.5 maximum_select_fusion.1
  27.1 1.6 gather_fusion.4
  30.5 1.5 collective-permute-start.8
  32.0 1.7 collective-permute-start.1
  33.7 1.6 gather_fusion.5
  39.1 1.7 collective-permute-start.36
  40.9 1.3 collective-permute-start.29
  43.3 1.7 collective-permute-start.9
  45.1 1.3 collective-permute-start.2
  48.0 1.3 collective-permute-start.37
  49.3 1.3 collective-permute-start.30
  52.2 1.2 collective-permute-start.10
  53.4 1.5 collective-permute-start.3
  55.6 1.5 collective-permute-start.45
  57.1 1.4 collective-permute-start.38
  59.3 1.3 collective-permute-start.25
  64.8 1.5 collective-permute-start.46
  66.3 1.2 collective-permute-start.39
  72.8 1.2 collective-permute-start.54
  75.0 1.3 collective-permute-start.40
  76.3 1.2 collective-permute-start.33
  79.3 1.2 collective-permute-start.13
  80.5 1.2 collective-permute-start.6
  84.7 1.2 collective-permute-start.34
  92.0 1.2 collective-permute-start.49
  93.2 1.3 collective-permute-start.56
  96.4 1.2 collective-permute-done.56
  97.6 3.3 %collective-permute-start.57 = (bf16[3,2048]{1,0:T(4,128)(2,1)S(1)}, bf16[3,2048]{1,0:T(4,128)(2,1)S(1)}, u32[]{:S(2)}, u32[]{:S(2)}) collective-permute-start(bf16[3,2048]{1,0:T(4,128)(2,1)S(1)} %slice.473), channel_id=1, source_target_pairs={{0,4},{4,8},{8,12},{12,16},{16,20},{20,24},{24,28},{1,5},{5,9},{9,... | collective-permute-start | bytes 36872 | tf_op jit(solution)/shard_map/ppermute | solution.py:13
  100.9 1.2 collective-permute-done.57
  103.3 8.8 %convolution_convert_fusion = bf16[128,4096]{1,0:T(8,128)(2,1)S(1)} fusion(bf16[2048,4096]{1,0:T(8,128)(2,1)} %param.27, bf16[128,2048]{1,0:T(8,128)(2,1)S(1)} %copy-done.12, f32[128,2048]{1,0:T(8,128)S(1)} %fusion.9), kind=kOutput, calls=%fused_computation.6 | convolution fusion | flops 2150891520 | bytes 19398656 | tf_op jit(solution)/shard_map/dot_general | solution.py:210
  112.3 1.9 collective-permute-done.58
  115.1 13.4 %collective-permute-done.59 = bf16[128,2048]{1,0:T(8,128)(2,1)S(1)} collective-permute-done((bf16[128,2048]{1,0:T(8,128)(2,1)S(1)}, bf16[128,2048]{1,0:T(8,128)(2,1)S(1)}, u32[]{:S(2)}, u32[]{:S(2)}) %collective-permute-start.59) | collective-permute-done | bytes 524320 | tf_op jit(solution)/shard_map/ppermute | solution.py:152
  131.7 3.2 %maximum_select_fusion = f32[128,4096]{1,0:T(8,128)} fusion(f32[128,2048]{1,0:T(8,128)S(1)} %convert_add_fusion, f32[128,2048]{1,0:T(8,128)} %collective-permute-done.60, pred[]{:T(512)S(6)} %eq.42), kind=kLoop, calls=%fused_computation.7 | loop fusion | flops 1572864 | bytes 4194305 | tf_op jit(solution)/shard_map/jit(_where)/select_n | solution.py:156
  134.9 14.7 %multiply_multiply_fusion.2 = (f32[128,2048]{1,0:T(8,128)}, f32[128,2048]{1,0:T(8,128)}, bf16[128,2048]{1,0:T(8,128)(2,1)}) fusion(f32[128]{0:T(128)S(1)} %get-tuple-element.147, f32[2048]{0:T(1024)S(1)} %bitcast.507, f32[128,2048]{1,0:T(8,128)} %copy-done.9, bf16[128,2048]{1,0:T(8,128)(2,1)} %param.25, bf16[2048,4096]{1,0:T(8,128)(2,1)} %param.27, ...), kind=kOutput, calls=%fused_computation.43 | convolution fusion | flops 2155872256 | bytes 24126464 | tf_op jit(solution)/shard_map/dot_general | solution.py:223
  149.7 1.5 multiply_multiply_fusion.1
  153.0 1.3 collective-permute-start.61
  156.2 2.9 %collective-permute-done.61 = f32[3,2048]{1,0:T(4,128)S(1)} collective-permute-done((f32[3,2048]{1,0:T(4,128)S(1)}, f32[3,2048]{1,0:T(4,128)S(1)}, u32[]{:S(2)}, u32[]{:S(2)}) %collective-permute-start.61) | collective-permute-done | bytes 24608 | tf_op jit(solution)/shard_map/ppermute | solution.py:13
  159.5 3.0 %collective-permute-start.83 = (bf16[128,512]{1,0:T(8,128)(2,1)S(1)}, bf16[128,512]{1,0:T(8,128)(2,1)S(1)}, u32[]{:S(2)}, u32[]{:S(2)}) collective-permute-start(bf16[128,512]{1,0:T(8,128)(2,1)S(1)} %get-tuple-element.123), channel_id=1, source_target_pairs={{8,0},{16,8},{24,16},{28,24},{20,28},{12,20},{4,12},{0,4},{9,1},{1... | collective-permute-start | bytes 393224 | tf_op jit(solution)/shard_map/ppermute | solution.py:103
  164.6 1.9 collective-permute-done.83
  166.5 2.1 collective-permute-start.84
  169.3 2.1 collective-permute-start.77
  171.5 2.1 collective-permute-start.63
  174.3 1.5 collective-permute-done.77
  175.8 2.1 collective-permute-start.78
  177.9 2.5 %collective-permute-done.63 = bf16[128,512]{1,0:T(8,128)(2,1)S(1)} collective-permute-done((bf16[128,512]{1,0:T(8,128)(2,1)S(1)}, bf16[128,512]{1,0:T(8,128)(2,1)S(1)}, u32[]{:S(2)}, u32[]{:S(2)}) %collective-permute-start.63) | collective-permute-done | bytes 131104 | tf_op jit(solution)/shard_map/ppermute | solution.py:103
  180.4 2.3 collective-permute-start.86
  182.7 1.2 collective-permute-start.79
  184.8 2.0 collective-permute-done.64
  186.9 2.2 collective-permute-start.87
  189.1 1.8 collective-permute-start.80
  193.4 1.7 collective-permute-start.88
  195.4 2.2 collective-permute-start.81
  198.1 1.6 collective-permute-start.67
  201.2 1.4 collective-permute-start.82
  210.8 1.8 collective-permute-done.90
  213.5 4.5 %collective-permute-start.91 = (bf16[128,512]{1,0:T(8,128)(2,1)S(1)}, bf16[128,512]{1,0:T(8,128)(2,1)S(1)}, u32[]{:S(2)}, u32[]{:S(2)}) collective-permute-start(bf16[128,512]{1,0:T(8,128)(2,1)S(1)} %get-tuple-element.131), channel_id=1, source_target_pairs={{0,0},{1,8},{2,16},{3,24},{4,4},{5,12},{6,20},{7,28},{8,1},{9,9},{... | collective-permute-start | bytes 393224 | tf_op jit(solution)/shard_map/ppermute | solution.py:73
  218.1 1.9 collective-permute-start.93
  220.0 1.8 dynamic-slice_convert_fusion
  222.0 6.6 %collective-permute-done.91 = bf16[128,512]{1,0:T(8,128)(2,1)S(1)} collective-permute-done((bf16[128,512]{1,0:T(8,128)(2,1)S(1)}, bf16[128,512]{1,0:T(8,128)(2,1)S(1)}, u32[]{:S(2)}, u32[]{:S(2)}) %collective-permute-start.91) | collective-permute-done | bytes 131104 | tf_op jit(solution)/shard_map/ppermute | solution.py:73
  229.5 2.3 collective-permute-done.93
  (280 shorter events, 67.7 us)
Async XLA Ops:
  3.4 20.3 %all-to-all-start = ((bf16[128,8,256]{2,0,1:T(8,128)(2,1)}), bf16[128,8,256]{2,0,1:T(8,128)(2,1)S(1)}, u32[]{:S(2)}, u32[]{:S(2)}) async-start(bf16[128,8,256]{2,0,1:T(8,128)(2,1)} %copy.25), calls=%async_computation | async-start | bytes 1048576 | tf_op jit(solution)/shard_map/all_to_all | solution.py:24
  29.7 9.1 %collective-permute-start.22 = (bf16[128,256]{1,0:T(8,128)(2,1)}, bf16[128,256]{1,0:T(8,128)(2,1)S(1)}, u32[]{:S(2)}, u32[]{:S(2)}) collective-permute-start(bf16[128,256]{1,0:T(8,128)(2,1)} %get-tuple-element.138), channel_id=1, source_target_pairs={{0,8},{8,16},{16,24},{24,28},{28,20},{20,12},{12,4},{4,0},{1,9},{9... | collective-permute-start | bytes 196616 | tf_op jit(solution)/shard_map/ppermute | solution.py:136
  30.4 8.7 %collective-permute-start.15 = (bf16[128,256]{1,0:T(8,128)(2,1)}, bf16[128,256]{1,0:T(8,128)(2,1)S(1)}, u32[]{:S(2)}, u32[]{:S(2)}) collective-permute-start(bf16[128,256]{1,0:T(8,128)(2,1)} %get-tuple-element.139), channel_id=1, source_target_pairs={{0,8},{8,16},{16,24},{24,28},{28,20},{20,12},{12,4},{4,0},{1,9},{9... | collective-permute-start | bytes 196616 | tf_op jit(solution)/shard_map/ppermute | solution.py:136
  30.5 10.4 %collective-permute-start.8 = (bf16[128,256]{1,0:T(8,128)(2,1)}, bf16[128,256]{1,0:T(8,128)(2,1)S(1)}, u32[]{:S(2)}, u32[]{:S(2)}) collective-permute-start(bf16[128,256]{1,0:T(8,128)(2,1)} %get-tuple-element.140), channel_id=1, source_target_pairs={{0,8},{8,16},{16,24},{24,28},{28,20},{20,12},{12,4},{4,0},{1,9},{9... | collective-permute-start | bytes 196616 | tf_op jit(solution)/shard_map/ppermute | solution.py:136
  32.0 10.2 %collective-permute-start.1 = (bf16[128,256]{1,0:T(8,128)(2,1)S(1)}, bf16[128,256]{1,0:T(8,128)(2,1)S(1)}, u32[]{:S(2)}, u32[]{:S(2)}) collective-permute-start(bf16[128,256]{1,0:T(8,128)(2,1)S(1)} %get-tuple-element.141), channel_id=1, source_target_pairs={{0,8},{8,16},{16,24},{24,28},{28,20},{20,12},{12,4},{4,0},{1,9},{9... | collective-permute-start | bytes 196616 | tf_op jit(solution)/shard_map/ppermute | solution.py:136
  35.7 7.4 %collective-permute-start.50 = (bf16[128,256]{1,0:T(8,128)(2,1)S(1)}, bf16[128,256]{1,0:T(8,128)(2,1)S(1)}, u32[]{:S(2)}, u32[]{:S(2)}) collective-permute-start(bf16[128,256]{1,0:T(8,128)(2,1)S(1)} %get-tuple-element.134), channel_id=1, source_target_pairs={{8,0},{16,8},{24,16},{28,24},{20,28},{12,20},{4,12},{0,4},{9,1},{1... | collective-permute-start | bytes 196616 | tf_op jit(solution)/shard_map/ppermute | solution.py:136
  39.1 5.9 %collective-permute-start.36 = (bf16[128,256]{1,0:T(8,128)(2,1)S(1)}, bf16[128,256]{1,0:T(8,128)(2,1)S(1)}, u32[]{:S(2)}, u32[]{:S(2)}) collective-permute-start(bf16[128,256]{1,0:T(8,128)(2,1)S(1)} %get-tuple-element.136), channel_id=1, source_target_pairs={{8,0},{16,8},{24,16},{28,24},{20,28},{12,20},{4,12},{0,4},{9,1},{1... | collective-permute-start | bytes 196616 | tf_op jit(solution)/shard_map/ppermute | solution.py:136
  40.9 5.5 %collective-permute-start.29 = (bf16[128,256]{1,0:T(8,128)(2,1)S(1)}, bf16[128,256]{1,0:T(8,128)(2,1)S(1)}, u32[]{:S(2)}, u32[]{:S(2)}) collective-permute-start(bf16[128,256]{1,0:T(8,128)(2,1)S(1)} %get-tuple-element.137), channel_id=1, source_target_pairs={{8,0},{16,8},{24,16},{28,24},{20,28},{12,20},{4,12},{0,4},{9,1},{1... | collective-permute-start | bytes 196616 | tf_op jit(solution)/shard_map/ppermute | solution.py:136
  43.3 5.9 %collective-permute-start.9 = (bf16[128,256]{1,0:T(8,128)(2,1)S(1)}, bf16[128,256]{1,0:T(8,128)(2,1)S(1)}, u32[]{:S(2)}, u32[]{:S(2)}) collective-permute-start(bf16[128,256]{1,0:T(8,128)(2,1)S(1)} %get-tuple-element.113), channel_id=1, source_target_pairs={{0,8},{8,16},{16,24},{24,28},{28,20},{20,12},{12,4},{4,0},{1,9},{9... | collective-permute-start | bytes 196616 | tf_op jit(solution)/shard_map/ppermute | solution.py:136
  45.1 5.5 %collective-permute-start.2 = (bf16[128,256]{1,0:T(8,128)(2,1)S(1)}, bf16[128,256]{1,0:T(8,128)(2,1)S(1)}, u32[]{:S(2)}, u32[]{:S(2)}) collective-permute-start(bf16[128,256]{1,0:T(8,128)(2,1)S(1)} %get-tuple-element.114), channel_id=1, source_target_pairs={{0,8},{8,16},{16,24},{24,28},{28,20},{20,12},{12,4},{4,0},{1,9},{9... | collective-permute-start | bytes 196616 | tf_op jit(solution)/shard_map/ppermute | solution.py:136
  48.0 5.4 %collective-permute-start.37 = (bf16[128,256]{1,0:T(8,128)(2,1)S(1)}, bf16[128,256]{1,0:T(8,128)(2,1)S(1)}, u32[]{:S(2)}, u32[]{:S(2)}) collective-permute-start(bf16[128,256]{1,0:T(8,128)(2,1)S(1)} %get-tuple-element.89), channel_id=1, source_target_pairs={{8,0},{16,8},{24,16},{28,24},{20,28},{12,20},{4,12},{0,4},{9,1},{1... | collective-permute-start | bytes 196616 | tf_op jit(solution)/shard_map/ppermute | solution.py:136
  49.3 5.7 %collective-permute-start.30 = (bf16[128,256]{1,0:T(8,128)(2,1)S(1)}, bf16[128,256]{1,0:T(8,128)(2,1)S(1)}, u32[]{:S(2)}, u32[]{:S(2)}) collective-permute-start(bf16[128,256]{1,0:T(8,128)(2,1)S(1)} %get-tuple-element.90), channel_id=1, source_target_pairs={{8,0},{16,8},{24,16},{28,24},{20,28},{12,20},{4,12},{0,4},{9,1},{1... | collective-permute-start | bytes 196616 | tf_op jit(solution)/shard_map/ppermute | solution.py:136
  51.4 5.6 %collective-permute-start.17 = (bf16[128,256]{1,0:T(8,128)(2,1)S(1)}, bf16[128,256]{1,0:T(8,128)(2,1)S(1)}, u32[]{:S(2)}, u32[]{:S(2)}) collective-permute-start(bf16[128,256]{1,0:T(8,128)(2,1)S(1)} %get-tuple-element.108), channel_id=1, source_target_pairs={{0,8},{8,16},{16,24},{24,28},{28,20},{20,12},{12,4},{4,0},{1,9},{9... | collective-permute-start | bytes 196616 | tf_op jit(solution)/shard_map/ppermute | solution.py:136
  52.2 6.3 %collective-permute-start.10 = (bf16[128,256]{1,0:T(8,128)(2,1)S(1)}, bf16[128,256]{1,0:T(8,128)(2,1)S(1)}, u32[]{:S(2)}, u32[]{:S(2)}) collective-permute-start(bf16[128,256]{1,0:T(8,128)(2,1)S(1)} %get-tuple-element.109), channel_id=1, source_target_pairs={{0,8},{8,16},{16,24},{24,28},{28,20},{20,12},{12,4},{4,0},{1,9},{9... | collective-permute-start | bytes 196616 | tf_op jit(solution)/shard_map/ppermute | solution.py:136
  53.4 5.8 %collective-permute-start.3 = (bf16[128,256]{1,0:T(8,128)(2,1)S(1)}, bf16[128,256]{1,0:T(8,128)(2,1)S(1)}, u32[]{:S(2)}, u32[]{:S(2)}) collective-permute-start(bf16[128,256]{1,0:T(8,128)(2,1)S(1)} %get-tuple-element.110), channel_id=1, source_target_pairs={{0,8},{8,16},{16,24},{24,28},{28,20},{20,12},{12,4},{4,0},{1,9},{9... | collective-permute-start | bytes 196616 | tf_op jit(solution)/shard_map/ppermute | solution.py:136
  55.0 5.7 %collective-permute-start.52 = (bf16[128,256]{1,0:T(8,128)(2,1)S(1)}, bf16[128,256]{1,0:T(8,128)(2,1)S(1)}, u32[]{:S(2)}, u32[]{:S(2)}) collective-permute-start(bf16[128,256]{1,0:T(8,128)(2,1)S(1)} %get-tuple-element.83), channel_id=1, source_target_pairs={{8,0},{16,8},{24,16},{28,24},{20,28},{12,20},{4,12},{0,4},{9,1},{1... | collective-permute-start | bytes 196616 | tf_op jit(solution)/shard_map/ppermute | solution.py:136
  55.6 5.8 %collective-permute-start.45 = (bf16[128,256]{1,0:T(8,128)(2,1)S(1)}, bf16[128,256]{1,0:T(8,128)(2,1)S(1)}, u32[]{:S(2)}, u32[]{:S(2)}) collective-permute-start(bf16[128,256]{1,0:T(8,128)(2,1)S(1)} %get-tuple-element.84), channel_id=1, source_target_pairs={{8,0},{16,8},{24,16},{28,24},{20,28},{12,20},{4,12},{0,4},{9,1},{1... | collective-permute-start | bytes 196616 | tf_op jit(solution)/shard_map/ppermute | solution.py:136
  57.1 5.5 %collective-permute-start.38 = (bf16[128,256]{1,0:T(8,128)(2,1)S(1)}, bf16[128,256]{1,0:T(8,128)(2,1)S(1)}, u32[]{:S(2)}, u32[]{:S(2)}) collective-permute-start(bf16[128,256]{1,0:T(8,128)(2,1)S(1)} %get-tuple-element.85), channel_id=1, source_target_pairs={{8,0},{16,8},{24,16},{28,24},{20,28},{12,20},{4,12},{0,4},{9,1},{1... | collective-permute-start | bytes 196616 | tf_op jit(solution)/shard_map/ppermute | solution.py:136
  58.5 5.5 %collective-permute-start.31 = (bf16[128,256]{1,0:T(8,128)(2,1)S(1)}, bf16[128,256]{1,0:T(8,128)(2,1)S(1)}, u32[]{:S(2)}, u32[]{:S(2)}) collective-permute-start(bf16[128,256]{1,0:T(8,128)(2,1)S(1)} %get-tuple-element.86), channel_id=1, source_target_pairs={{8,0},{16,8},{24,16},{28,24},{20,28},{12,20},{4,12},{0,4},{9,1},{1... | collective-permute-start | bytes 196616 | tf_op jit(solution)/shard_map/ppermute | solution.py:136
  59.3 5.5 %collective-permute-start.25 = (bf16[128,256]{1,0:T(8,128)(2,1)S(1)}, bf16[128,256]{1,0:T(8,128)(2,1)S(1)}, u32[]{:S(2)}, u32[]{:S(2)}) collective-permute-start(bf16[128,256]{1,0:T(8,128)(2,1)S(1)} %get-tuple-element.103), channel_id=1, source_target_pairs={{0,8},{8,16},{16,24},{24,28},{28,20},{20,12},{12,4},{4,0},{1,9},{9... | collective-permute-start | bytes 196616 | tf_op jit(solution)/shard_map/ppermute | solution.py:136
  60.7 5.6 %collective-permute-start.18 = (bf16[128,256]{1,0:T(8,128)(2,1)S(1)}, bf16[128,256]{1,0:T(8,128)(2,1)S(1)}, u32[]{:S(2)}, u32[]{:S(2)}) collective-permute-start(bf16[128,256]{1,0:T(8,128)(2,1)S(1)} %get-tuple-element.104), channel_id=1, source_target_pairs={{0,8},{8,16},{16,24},{24,28},{28,20},{20,12},{12,4},{4,0},{1,9},{9... | collective-permute-start | bytes 196616 | tf_op jit(solution)/shard_map/ppermute | solution.py:136
  61.4 6.1 %collective-permute-start.11 = (bf16[128,256]{1,0:T(8,128)(2,1)S(1)}, bf16[128,256]{1,0:T(8,128)(2,1)S(1)}, u32[]{:S(2)}, u32[]{:S(2)}) collective-permute-start(bf16[128,256]{1,0:T(8,128)(2,1)S(1)} %get-tuple-element.105), channel_id=1, source_target_pairs={{0,8},{8,16},{16,24},{24,28},{28,20},{20,12},{12,4},{4,0},{1,9},{9... | collective-permute-start | bytes 196616 | tf_op jit(solution)/shard_map/ppermute | solution.py:136
  62.6 5.9 %collective-permute-start.4 = (bf16[128,256]{1,0:T(8,128)(2,1)S(1)}, bf16[128,256]{1,0:T(8,128)(2,1)S(1)}, u32[]{:S(2)}, u32[]{:S(2)}) collective-permute-start(bf16[128,256]{1,0:T(8,128)(2,1)S(1)} %get-tuple-element.106), channel_id=1, source_target_pairs={{0,8},{8,16},{16,24},{24,28},{28,20},{20,12},{12,4},{4,0},{1,9},{9... | collective-permute-start | bytes 196616 | tf_op jit(solution)/shard_map/ppermute | solution.py:136
  64.0 5.7 %collective-permute-start.53 = (bf16[128,256]{1,0:T(8,128)(2,1)S(1)}, bf16[128,256]{1,0:T(8,128)(2,1)S(1)}, u32[]{:S(2)}, u32[]{:S(2)}) collective-permute-start(bf16[128,256]{1,0:T(8,128)(2,1)S(1)} %get-tuple-element.79), channel_id=1, source_target_pairs={{8,0},{16,8},{24,16},{28,24},{20,28},{12,20},{4,12},{0,4},{9,1},{1... | collective-permute-start | bytes 196616 | tf_op jit(solution)/shard_map/ppermute | solution.py:136
  64.8 5.8 %collective-permute-start.46 = (bf16[128,256]{1,0:T(8,128)(2,1)S(1)}, bf16[128,256]{1,0:T(8,128)(2,1)S(1)}, u32[]{:S(2)}, u32[]{:S(2)}) collective-permute-start(bf16[128,256]{1,0:T(8,128)(2,1)S(1)} %get-tuple-element.80), channel_id=1, source_target_pairs={{8,0},{16,8},{24,16},{28,24},{20,28},{12,20},{4,12},{0,4},{9,1},{1... | collective-permute-start | bytes 196616 | tf_op jit(solution)/shard_map/ppermute | solution.py:136
  66.3 5.5 %collective-permute-start.39 = (bf16[128,256]{1,0:T(8,128)(2,1)S(1)}, bf16[128,256]{1,0:T(8,128)(2,1)S(1)}, u32[]{:S(2)}, u32[]{:S(2)}) collective-permute-start(bf16[128,256]{1,0:T(8,128)(2,1)S(1)} %get-tuple-element.81), channel_id=1, source_target_pairs={{8,0},{16,8},{24,16},{28,24},{20,28},{12,20},{4,12},{0,4},{9,1},{1... | collective-permute-start | bytes 196616 | tf_op jit(solution)/shard_map/ppermute | solution.py:136
  68.6 5.4 %collective-permute-start.26 = (bf16[128,256]{1,0:T(8,128)(2,1)S(1)}, bf16[128,256]{1,0:T(8,128)(2,1)S(1)}, u32[]{:S(2)}, u32[]{:S(2)}) collective-permute-start(bf16[128,256]{1,0:T(8,128)(2,1)S(1)} %get-tuple-element.99), channel_id=1, source_target_pairs={{0,8},{8,16},{16,24},{24,28},{28,20},{20,12},{12,4},{4,0},{1,9},{9... | collective-permute-start | bytes 196616 | tf_op jit(solution)/shard_map/ppermute | solution.py:136
  70.6 5.7 %collective-permute-start.12 = (bf16[128,256]{1,0:T(8,128)(2,1)S(1)}, bf16[128,256]{1,0:T(8,128)(2,1)S(1)}, u32[]{:S(2)}, u32[]{:S(2)}) collective-permute-start(bf16[128,256]{1,0:T(8,128)(2,1)S(1)} %get-tuple-element.101), channel_id=1, source_target_pairs={{0,8},{8,16},{16,24},{24,28},{28,20},{20,12},{12,4},{4,0},{1,9},{9... | collective-permute-start | bytes 196616 | tf_op jit(solution)/shard_map/ppermute | solution.py:136
  71.8 5.7 %collective-permute-start.5 = (bf16[128,256]{1,0:T(8,128)(2,1)S(1)}, bf16[128,256]{1,0:T(8,128)(2,1)S(1)}, u32[]{:S(2)}, u32[]{:S(2)}) collective-permute-start(bf16[128,256]{1,0:T(8,128)(2,1)S(1)} %get-tuple-element.102), channel_id=1, source_target_pairs={{0,8},{8,16},{16,24},{24,28},{28,20},{20,12},{12,4},{4,0},{1,9},{9... | collective-permute-start | bytes 196616 | tf_op jit(solution)/shard_map/ppermute | solution.py:136
  72.8 5.7 %collective-permute-start.54 = (bf16[128,256]{1,0:T(8,128)(2,1)S(1)}, bf16[128,256]{1,0:T(8,128)(2,1)S(1)}, u32[]{:S(2)}, u32[]{:S(2)}) collective-permute-start(bf16[128,256]{1,0:T(8,128)(2,1)S(1)} %get-tuple-element.75), channel_id=1, source_target_pairs={{8,0},{16,8},{24,16},{28,24},{20,28},{12,20},{4,12},{0,4},{9,1},{1... | collective-permute-start | bytes 196616 | tf_op jit(solution)/shard_map/ppermute | solution.py:136
  75.0 5.5 %collective-permute-start.40 = (bf16[128,256]{1,0:T(8,128)(2,1)S(1)}, bf16[128,256]{1,0:T(8,128)(2,1)S(1)}, u32[]{:S(2)}, u32[]{:S(2)}) collective-permute-start(bf16[128,256]{1,0:T(8,128)(2,1)S(1)} %get-tuple-element.77), channel_id=1, source_target_pairs={{8,0},{16,8},{24,16},{28,24},{20,28},{12,20},{4,12},{0,4},{9,1},{1... | collective-permute-start | bytes 196616 | tf_op jit(solution)/shard_map/ppermute | solution.py:136
  76.3 5.3 %collective-permute-start.33 = (bf16[128,256]{1,0:T(8,128)(2,1)S(1)}, bf16[128,256]{1,0:T(8,128)(2,1)S(1)}, u32[]{:S(2)}, u32[]{:S(2)}) collective-permute-start(bf16[128,256]{1,0:T(8,128)(2,1)S(1)} %get-tuple-element.78), channel_id=1, source_target_pairs={{8,0},{16,8},{24,16},{28,24},{20,28},{12,20},{4,12},{0,4},{9,1},{1... | collective-permute-start | bytes 196616 | tf_op jit(solution)/shard_map/ppermute | solution.py:136
  79.3 5.5 %collective-permute-start.13 = (bf16[128,256]{1,0:T(8,128)(2,1)S(1)}, bf16[128,256]{1,0:T(8,128)(2,1)S(1)}, u32[]{:S(2)}, u32[]{:S(2)}) collective-permute-start(bf16[128,256]{1,0:T(8,128)(2,1)S(1)} %get-tuple-element.97), channel_id=1, source_target_pairs={{0,8},{8,16},{16,24},{24,28},{28,20},{20,12},{12,4},{4,0},{1,9},{9... | collective-permute-start | bytes 196616 | tf_op jit(solution)/shard_map/ppermute | solution.py:136
  80.5 5.5 %collective-permute-start.6 = (bf16[128,256]{1,0:T(8,128)(2,1)S(1)}, bf16[128,256]{1,0:T(8,128)(2,1)S(1)}, u32[]{:S(2)}, u32[]{:S(2)}) collective-permute-start(bf16[128,256]{1,0:T(8,128)(2,1)S(1)} %get-tuple-element.98), channel_id=1, source_target_pairs={{0,8},{8,16},{16,24},{24,28},{28,20},{20,12},{12,4},{4,0},{1,9},{9... | collective-permute-start | bytes 196616 | tf_op jit(solution)/shard_map/ppermute | solution.py:136
  87.8 5.4 %collective-permute-start.21 = (bf16[128,256]{1,0:T(8,128)(2,1)S(1)}, bf16[128,256]{1,0:T(8,128)(2,1)S(1)}, u32[]{:S(2)}, u32[]{:S(2)}) collective-permute-start(bf16[128,256]{1,0:T(8,128)(2,1)S(1)} %get-tuple-element.92), channel_id=1, source_target_pairs={{0,8},{8,16},{16,24},{24,28},{28,20},{20,12},{12,4},{4,0},{1,9},{9... | collective-permute-start | bytes 196616 | tf_op jit(solution)/shard_map/ppermute | solution.py:136
  88.9 5.6 %collective-permute-start.28 = (bf16[128,256]{1,0:T(8,128)(2,1)S(1)}, bf16[128,256]{1,0:T(8,128)(2,1)S(1)}, u32[]{:S(2)}, u32[]{:S(2)}) collective-permute-start(bf16[128,256]{1,0:T(8,128)(2,1)S(1)} %get-tuple-element.91), channel_id=1, source_target_pairs={{0,8},{8,16},{16,24},{24,28},{28,20},{20,12},{12,4},{4,0},{1,9},{9... | collective-permute-start | bytes 196616 | tf_op jit(solution)/shard_map/ppermute | solution.py:136
  114.5 14.0 %collective-permute-start.59 = (bf16[128,2048]{1,0:T(8,128)(2,1)S(1)}, bf16[128,2048]{1,0:T(8,128)(2,1)S(1)}, u32[]{:S(2)}, u32[]{:S(2)}) collective-permute-start(bf16[128,2048]{1,0:T(8,128)(2,1)S(1)} %fusion.21), channel_id=1, source_target_pairs={{0,2},{1,3},{2,0},{3,1},{4,6},{5,7},{6,4},{7,5},{8,10},{9,11},{10,... | collective-permute-start | bytes 1572872 | tf_op jit(solution)/shard_map/ppermute | solution.py:152
  153.0 6.1 %collective-permute-start.61 = (f32[3,2048]{1,0:T(4,128)S(1)}, f32[3,2048]{1,0:T(4,128)S(1)}, u32[]{:S(2)}, u32[]{:S(2)}) collective-permute-start(f32[3,2048]{1,0:T(4,128)S(1)} %slice_add_fusion), channel_id=1, source_target_pairs={{4,0},{8,4},{12,8},{16,12},{20,16},{24,20},{28,24},{5,1},{9,5},{13... | collective-permute-start | bytes 73736 | tf_op jit(solution)/shard_map/ppermute | solution.py:13
  159.5 7.0 %collective-permute-start.83 = (bf16[128,512]{1,0:T(8,128)(2,1)S(1)}, bf16[128,512]{1,0:T(8,128)(2,1)S(1)}, u32[]{:S(2)}, u32[]{:S(2)}) collective-permute-start(bf16[128,512]{1,0:T(8,128)(2,1)S(1)} %get-tuple-element.123), channel_id=1, source_target_pairs={{8,0},{16,8},{24,16},{28,24},{20,28},{12,20},{4,12},{0,4},{9,1},{1... | collective-permute-start | bytes 393224 | tf_op jit(solution)/shard_map/ppermute | solution.py:103
  162.5 6.8 %collective-permute-start.76 = (bf16[128,512]{1,0:T(8,128)(2,1)S(1)}, bf16[128,512]{1,0:T(8,128)(2,1)S(1)}, u32[]{:S(2)}, u32[]{:S(2)}) collective-permute-start(bf16[128,512]{1,0:T(8,128)(2,1)S(1)} %get-tuple-element.124), channel_id=1, source_target_pairs={{8,0},{16,8},{24,16},{28,24},{20,28},{12,20},{4,12},{0,4},{9,1},{1... | collective-permute-start | bytes 393224 | tf_op jit(solution)/shard_map/ppermute | solution.py:103
  163.5 7.9 %collective-permute-start.69 = (bf16[128,512]{1,0:T(8,128)(2,1)S(1)}, bf16[128,512]{1,0:T(8,128)(2,1)S(1)}, u32[]{:S(2)}, u32[]{:S(2)}) collective-permute-start(bf16[128,512]{1,0:T(8,128)(2,1)S(1)} %get-tuple-element.125), channel_id=1, source_target_pairs={{0,8},{8,16},{16,24},{24,28},{28,20},{20,12},{12,4},{4,0},{1,9},{9... | collective-permute-start | bytes 393224 | tf_op jit(solution)/shard_map/ppermute | solution.py:103
  164.5 6.9 %collective-permute-start.62 = (bf16[128,512]{1,0:T(8,128)(2,1)S(1)}, bf16[128,512]{1,0:T(8,128)(2,1)S(1)}, u32[]{:S(2)}, u32[]{:S(2)}) collective-permute-start(bf16[128,512]{1,0:T(8,128)(2,1)S(1)} %get-tuple-element.122), channel_id=1, source_target_pairs={{0,8},{8,16},{16,24},{24,28},{28,20},{20,12},{12,4},{4,0},{1,9},{9... | collective-permute-start | bytes 393224 | tf_op jit(solution)/shard_map/ppermute | solution.py:103
  166.5 7.0 %collective-permute-start.84 = (bf16[128,512]{1,0:T(8,128)(2,1)S(1)}, bf16[128,512]{1,0:T(8,128)(2,1)S(1)}, u32[]{:S(2)}, u32[]{:S(2)}) collective-permute-start(bf16[128,512]{1,0:T(8,128)(2,1)S(1)} %collective-permute-done.83), channel_id=1, source_target_pairs={{8,0},{16,8},{24,16},{28,24},{20,28},{12,20},{4,12},{0,4},{9,1},{1... | collective-permute-start | bytes 393224 | tf_op jit(solution)/shard_map/ppermute | solution.py:103
  169.3 6.4 %collective-permute-start.77 = (bf16[128,512]{1,0:T(8,128)(2,1)S(1)}, bf16[128,512]{1,0:T(8,128)(2,1)S(1)}, u32[]{:S(2)}, u32[]{:S(2)}) collective-permute-start(bf16[128,512]{1,0:T(8,128)(2,1)S(1)} %collective-permute-done.76), channel_id=1, source_target_pairs={{8,0},{16,8},{24,16},{28,24},{20,28},{12,20},{4,12},{0,4},{9,1},{1... | collective-permute-start | bytes 393224 | tf_op jit(solution)/shard_map/ppermute | solution.py:103
  171.4 6.4 %collective-permute-start.70 = (bf16[128,512]{1,0:T(8,128)(2,1)S(1)}, bf16[128,512]{1,0:T(8,128)(2,1)S(1)}, u32[]{:S(2)}, u32[]{:S(2)}) collective-permute-start(bf16[128,512]{1,0:T(8,128)(2,1)S(1)} %collective-permute-done.69), channel_id=1, source_target_pairs={{0,8},{8,16},{16,24},{24,28},{28,20},{20,12},{12,4},{4,0},{1,9},{9... | collective-permute-start | bytes 393224 | tf_op jit(solution)/shard_map/ppermute | solution.py:103
  171.5 8.9 %collective-permute-start.63 = (bf16[128,512]{1,0:T(8,128)(2,1)S(1)}, bf16[128,512]{1,0:T(8,128)(2,1)S(1)}, u32[]{:S(2)}, u32[]{:S(2)}) collective-permute-start(bf16[128,512]{1,0:T(8,128)(2,1)S(1)} %collective-permute-done.62), channel_id=1, source_target_pairs={{0,8},{8,16},{16,24},{24,28},{28,20},{20,12},{12,4},{4,0},{1,9},{9... | collective-permute-start | bytes 393224 | tf_op jit(solution)/shard_map/ppermute | solution.py:103
  173.5 6.9 %collective-permute-start.85 = (bf16[128,512]{1,0:T(8,128)(2,1)S(1)}, bf16[128,512]{1,0:T(8,128)(2,1)S(1)}, u32[]{:S(2)}, u32[]{:S(2)}) collective-permute-start(bf16[128,512]{1,0:T(8,128)(2,1)S(1)} %collective-permute-done.84), channel_id=1, source_target_pairs={{8,0},{16,8},{24,16},{28,24},{20,28},{12,20},{4,12},{0,4},{9,1},{1... | collective-permute-start | bytes 393224 | tf_op jit(solution)/shard_map/ppermute | solution.py:103
  175.8 7.0 %collective-permute-start.78 = (bf16[128,512]{1,0:T(8,128)(2,1)S(1)}, bf16[128,512]{1,0:T(8,128)(2,1)S(1)}, u32[]{:S(2)}, u32[]{:S(2)}) collective-permute-start(bf16[128,512]{1,0:T(8,128)(2,1)S(1)} %collective-permute-done.77), channel_id=1, source_target_pairs={{8,0},{16,8},{24,16},{28,24},{20,28},{12,20},{4,12},{0,4},{9,1},{1... | collective-permute-start | bytes 393224 | tf_op jit(solution)/shard_map/ppermute | solution.py:103
  177.9 6.1 %collective-permute-start.71 = (bf16[128,512]{1,0:T(8,128)(2,1)S(1)}, bf16[128,512]{1,0:T(8,128)(2,1)S(1)}, u32[]{:S(2)}, u32[]{:S(2)}) collective-permute-start(bf16[128,512]{1,0:T(8,128)(2,1)S(1)} %collective-permute-done.70), channel_id=1, source_target_pairs={{0,8},{8,16},{16,24},{24,28},{28,20},{20,12},{12,4},{4,0},{1,9},{9... | collective-permute-start | bytes 393224 | tf_op jit(solution)/shard_map/ppermute | solution.py:103
  180.4 6.3 %collective-permute-start.64 = (bf16[128,512]{1,0:T(8,128)(2,1)S(1)}, bf16[128,512]{1,0:T(8,128)(2,1)S(1)}, u32[]{:S(2)}, u32[]{:S(2)}) collective-permute-start(bf16[128,512]{1,0:T(8,128)(2,1)S(1)} %collective-permute-done.63), channel_id=1, source_target_pairs={{0,8},{8,16},{16,24},{24,28},{28,20},{20,12},{12,4},{4,0},{1,9},{9... | collective-permute-start | bytes 393224 | tf_op jit(solution)/shard_map/ppermute | solution.py:103
  180.4 6.5 %collective-permute-start.86 = (bf16[128,512]{1,0:T(8,128)(2,1)S(1)}, bf16[128,512]{1,0:T(8,128)(2,1)S(1)}, u32[]{:S(2)}, u32[]{:S(2)}) collective-permute-start(bf16[128,512]{1,0:T(8,128)(2,1)S(1)} %collective-permute-done.85), channel_id=1, source_target_pairs={{8,0},{16,8},{24,16},{28,24},{20,28},{12,20},{4,12},{0,4},{9,1},{1... | collective-permute-start | bytes 393224 | tf_op jit(solution)/shard_map/ppermute | solution.py:103
  182.7 6.4 %collective-permute-start.79 = (bf16[128,512]{1,0:T(8,128)(2,1)S(1)}, bf16[128,512]{1,0:T(8,128)(2,1)S(1)}, u32[]{:S(2)}, u32[]{:S(2)}) collective-permute-start(bf16[128,512]{1,0:T(8,128)(2,1)S(1)} %collective-permute-done.78), channel_id=1, source_target_pairs={{8,0},{16,8},{24,16},{28,24},{20,28},{12,20},{4,12},{0,4},{9,1},{1... | collective-permute-start | bytes 393224 | tf_op jit(solution)/shard_map/ppermute | solution.py:103
  184.0 7.0 %collective-permute-start.72 = (bf16[128,512]{1,0:T(8,128)(2,1)S(1)}, bf16[128,512]{1,0:T(8,128)(2,1)S(1)}, u32[]{:S(2)}, u32[]{:S(2)}) collective-permute-start(bf16[128,512]{1,0:T(8,128)(2,1)S(1)} %collective-permute-done.71), channel_id=1, source_target_pairs={{0,8},{8,16},{16,24},{24,28},{28,20},{20,12},{12,4},{4,0},{1,9},{9... | collective-permute-start | bytes 393224 | tf_op jit(solution)/shard_map/ppermute | solution.py:103
  186.9 6.5 %collective-permute-start.87 = (bf16[128,512]{1,0:T(8,128)(2,1)S(1)}, bf16[128,512]{1,0:T(8,128)(2,1)S(1)}, u32[]{:S(2)}, u32[]{:S(2)}) collective-permute-start(bf16[128,512]{1,0:T(8,128)(2,1)S(1)} %collective-permute-done.86), channel_id=1, source_target_pairs={{8,0},{16,8},{24,16},{28,24},{20,28},{12,20},{4,12},{0,4},{9,1},{1... | collective-permute-start | bytes 393224 | tf_op jit(solution)/shard_map/ppermute | solution.py:103
  189.1 6.3 %collective-permute-start.80 = (bf16[128,512]{1,0:T(8,128)(2,1)S(1)}, bf16[128,512]{1,0:T(8,128)(2,1)S(1)}, u32[]{:S(2)}, u32[]{:S(2)}) collective-permute-start(bf16[128,512]{1,0:T(8,128)(2,1)S(1)} %collective-permute-done.79), channel_id=1, source_target_pairs={{8,0},{16,8},{24,16},{28,24},{20,28},{12,20},{4,12},{0,4},{9,1},{1... | collective-permute-start | bytes 393224 | tf_op jit(solution)/shard_map/ppermute | solution.py:103
  190.9 6.7 %collective-permute-start.73 = (bf16[128,512]{1,0:T(8,128)(2,1)S(1)}, bf16[128,512]{1,0:T(8,128)(2,1)S(1)}, u32[]{:S(2)}, u32[]{:S(2)}) collective-permute-start(bf16[128,512]{1,0:T(8,128)(2,1)S(1)} %collective-permute-done.72), channel_id=1, source_target_pairs={{0,8},{8,16},{16,24},{24,28},{28,20},{20,12},{12,4},{4,0},{1,9},{9... | collective-permute-start | bytes 393224 | tf_op jit(solution)/shard_map/ppermute | solution.py:103
  192.0 6.1 %collective-permute-start.66 = (bf16[128,512]{1,0:T(8,128)(2,1)S(1)}, bf16[128,512]{1,0:T(8,128)(2,1)S(1)}, u32[]{:S(2)}, u32[]{:S(2)}) collective-permute-start(bf16[128,512]{1,0:T(8,128)(2,1)S(1)} %collective-permute-done.65), channel_id=1, source_target_pairs={{0,8},{8,16},{16,24},{24,28},{28,20},{20,12},{12,4},{4,0},{1,9},{9... | collective-permute-start | bytes 393224 | tf_op jit(solution)/shard_map/ppermute | solution.py:103
  193.4 6.4 %collective-permute-start.88 = (bf16[128,512]{1,0:T(8,128)(2,1)S(1)}, bf16[128,512]{1,0:T(8,128)(2,1)S(1)}, u32[]{:S(2)}, u32[]{:S(2)}) collective-permute-start(bf16[128,512]{1,0:T(8,128)(2,1)S(1)} %collective-permute-done.87), channel_id=1, source_target_pairs={{8,0},{16,8},{24,16},{28,24},{20,28},{12,20},{4,12},{0,4},{9,1},{1... | collective-permute-start | bytes 393224 | tf_op jit(solution)/shard_map/ppermute | solution.py:103
  195.4 5.8 %collective-permute-start.81 = (bf16[128,512]{1,0:T(8,128)(2,1)S(1)}, bf16[128,512]{1,0:T(8,128)(2,1)S(1)}, u32[]{:S(2)}, u32[]{:S(2)}) collective-permute-start(bf16[128,512]{1,0:T(8,128)(2,1)S(1)} %collective-permute-done.80), channel_id=1, source_target_pairs={{8,0},{16,8},{24,16},{28,24},{20,28},{12,20},{4,12},{0,4},{9,1},{1... | collective-permute-start | bytes 393224 | tf_op jit(solution)/shard_map/ppermute | solution.py:103
  198.1 5.9 %collective-permute-start.67 = (bf16[128,512]{1,0:T(8,128)(2,1)S(1)}, bf16[128,512]{1,0:T(8,128)(2,1)S(1)}, u32[]{:S(2)}, u32[]{:S(2)}) collective-permute-start(bf16[128,512]{1,0:T(8,128)(2,1)S(1)} %collective-permute-done.66), channel_id=1, source_target_pairs={{0,8},{8,16},{16,24},{24,28},{28,20},{20,12},{12,4},{4,0},{1,9},{9... | collective-permute-start | bytes 393224 | tf_op jit(solution)/shard_map/ppermute | solution.py:103
  212.9 9.1 %collective-permute-start.92 = (bf16[128,512]{1,0:T(8,128)(2,1)S(1)}, bf16[128,512]{1,0:T(8,128)(2,1)S(1)}, u32[]{:S(2)}, u32[]{:S(2)}) collective-permute-start(bf16[128,512]{1,0:T(8,128)(2,1)S(1)} %get-tuple-element.133), channel_id=1, source_target_pairs={{0,16},{1,24},{2,0},{3,8},{4,20},{5,28},{6,4},{7,12},{8,17},{9,25}... | collective-permute-start | bytes 393224 | tf_op jit(solution)/shard_map/ppermute | solution.py:73
  213.5 15.1 %collective-permute-start.91 = (bf16[128,512]{1,0:T(8,128)(2,1)S(1)}, bf16[128,512]{1,0:T(8,128)(2,1)S(1)}, u32[]{:S(2)}, u32[]{:S(2)}) collective-permute-start(bf16[128,512]{1,0:T(8,128)(2,1)S(1)} %get-tuple-element.131), channel_id=1, source_target_pairs={{0,0},{1,8},{2,16},{3,24},{4,4},{5,12},{6,20},{7,28},{8,1},{9,9},{... | collective-permute-start | bytes 393224 | tf_op jit(solution)/shard_map/ppermute | solution.py:73
  218.0 11.5 %collective-permute-start.94 = (bf16[128,512]{1,0:T(8,128)(2,1)S(1)}, bf16[128,512]{1,0:T(8,128)(2,1)S(1)}, u32[]{:S(2)}, u32[]{:S(2)}) collective-permute-start(bf16[128,512]{1,0:T(8,128)(2,1)S(1)} %get-tuple-element.132), channel_id=1, source_target_pairs={{0,20},{1,28},{2,4},{3,12},{4,16},{5,24},{6,0},{7,8},{8,21},{9,29}... | collective-permute-start | bytes 393224 | tf_op jit(solution)/shard_map/ppermute | solution.py:73
  218.1 13.7 %collective-permute-start.93 = (bf16[128,512]{1,0:T(8,128)(2,1)S(1)}, bf16[128,512]{1,0:T(8,128)(2,1)S(1)}, u32[]{:S(2)}, u32[]{:S(2)}) collective-permute-start(bf16[128,512]{1,0:T(8,128)(2,1)S(1)} %get-tuple-element.130), channel_id=1, source_target_pairs={{0,4},{1,12},{2,20},{3,28},{4,0},{5,8},{6,16},{7,24},{8,5},{9,13},... | collective-permute-start | bytes 393224 | tf_op jit(solution)/shard_map/ppermute | solution.py:73
  (48 other events, 267.8 us)
